TPU v7x, 32 devices: a whole 2x2x4 slice. The times are simulated.
32 devices in a mesh: dp: 2 (over x), ctx: 16 (over z, y, core).
Axes of the slice: x: 2, y: 2, z: 4, core: 2. Of those that a mesh axis runs over, the one named last changes fastest.
Arguments:
- token_values: bfloat16 [2, 2048, 2560], P('dp', 'ctx'), may hold values from -0.3125 to 0.3125
- cotangent: bfloat16 [2, 2048, 2560], P('dp', 'ctx'), may hold values from -0.5 to 0.5
- write_coeffs: bfloat16 [2, 2048, 128], P('dp', 'ctx'), may hold values from -1.5 to 1.5
- read_coeffs: bfloat16 [2, 2048, 128], P('dp', 'ctx'), may hold values from -1.5 to 1.5
- decay_codes: int32 [2, 2048, 40], P('dp', 'ctx'), may hold values from 0 to 3276, as said below
- skip_gain: float32 [40], replicated, may hold values from 0.5 to 2
Outputs:
- grad_values: bfloat16 [2, 2048, 2560], P('dp', 'ctx')
- grad_write: bfloat16 [2, 2048, 128], P('dp', 'ctx')
- grad_read: bfloat16 [2, 2048, 128], P('dp', 'ctx')
- grad_skip: float32 [40], replicated
Inputs may be any that keep to these rules, and one draw needn't show every extreme that they name: `decay_codes`: one code per sequence, token and head; larger codes mean faster forgetting.
All inputs are finite; a program needn't handle non-finite values.
Results may differ from a plain program's by a relative error of at most 0.0059.
Values sent between devices are 32-bit elements; how exact they have to be, the bound alone decides.
No kernel may reach another device: no remote copies, remote signals or barrier semaphores. Data moves between devices by JAX's collectives and lax.ppermute only.
A program may use at most 128 MiB of HBM per device.

v0:
```python
import functools

import jax
import jax.numpy as jnp
from jax import lax
from jax.sharding import PartitionSpec as P


def from_partner(array, axis, bit):
    return lax.ppermute(array, axis, [(i, i ^ 1 << bit) for i in range(lax.axis_size(axis))])


def block_states(values, cotan, write_map, read_map, codes, factor):
    token_count = values.shape[0]
    head_count = codes.shape[1]
    head_width = values.shape[1] // head_count
    log_decay = -codes.astype(jnp.float32) * factor
    within = jnp.cumsum(log_decay, axis=0)
    totals = within[-1]
    vals_three = values.reshape(token_count, head_count, head_width)
    cot_three = cotan.reshape(token_count, head_count, head_width)
    decayed_vals = (vals_three * jnp.exp(totals - within)[:, :, None]).astype(jnp.bfloat16)
    decayed_cot = (cot_three * jnp.exp(within)[:, :, None]).astype(jnp.bfloat16)
    fwd_state = jnp.einsum(
        "jn,jhp->hnp", write_map, decayed_vals, preferred_element_type=jnp.float32
    )
    adj_state = jnp.einsum("in,ihp->hnp", read_map, decayed_cot, preferred_element_type=jnp.float32)
    return (within, totals, decayed_vals, decayed_cot, fwd_state, adj_state)


def block_grads(
    values,
    cotan,
    write_map,
    read_map,
    within,
    totals,
    decayed_vals,
    decayed_cot,
    carried_state,
    carried_adjoint,
    skip_gain,
):
    token_count = values.shape[0]
    head_count = skip_gain.shape[0]
    head_width = values.shape[1] // head_count
    vals_three = values.reshape(token_count, head_count, head_width)
    cot_three = cotan.reshape(token_count, head_count, head_width)
    rows = jnp.arange(token_count)
    causal = (rows[:, None] >= rows[None, :])[None]
    lead = within.T
    spread = lead[:, :, None] - lead[:, None, :]
    decay_matrix = jnp.where(causal, jnp.exp(jnp.where(causal, spread, 0.0)), 0.0)
    products = jnp.einsum("ihp,jhp->hij", cot_three, vals_three, preferred_element_type=jnp.float32)
    read_weights = (products * decay_matrix).astype(jnp.bfloat16)
    gram = jnp.einsum("in,jn->ij", read_map, write_map, preferred_element_type=jnp.float32)
    value_weights = (gram[None] * decay_matrix).astype(jnp.bfloat16)
    state_rounded = carried_state.astype(jnp.bfloat16)
    adjoint_rounded = carried_adjoint.astype(jnp.bfloat16)
    grad_read = jnp.einsum(
        "hij,jn->in", read_weights, write_map, preferred_element_type=jnp.float32
    ) + jnp.einsum("ihp,hnp->in", decayed_cot, state_rounded, preferred_element_type=jnp.float32)
    grad_write = jnp.einsum(
        "hij,in->jn", read_weights, read_map, preferred_element_type=jnp.float32
    ) + jnp.einsum("jhp,hnp->jn", decayed_vals, adjoint_rounded, preferred_element_type=jnp.float32)
    carried_term = jnp.einsum(
        "jn,hnp->jhp", write_map, adjoint_rounded, preferred_element_type=jnp.float32
    )
    grad_values = (
        jnp.einsum("hij,ihp->jhp", value_weights, cot_three, preferred_element_type=jnp.float32)
        + jnp.exp(totals - within)[:, :, None] * carried_term
        + skip_gain[None, :, None] * cot_three
    )
    skip_part = jnp.einsum("ihp,ihp->h", cot_three, vals_three, preferred_element_type=jnp.float32)
    return (
        grad_values.reshape(token_count, head_count * head_width).astype(jnp.bfloat16),
        grad_write.astype(jnp.bfloat16),
        grad_read.astype(jnp.bfloat16),
        skip_part,
    )


def chain_pair(earlier, later):
    return (earlier[0] * later[0], later[0][..., None, None] * earlier[1] + later[1])


def pick_tree(flag, first_tree, second_tree):
    return jax.tree.map(
        lambda first_leaf, other_leaf: jnp.where(flag, first_leaf, other_leaf),
        first_tree,
        second_tree,
    )


def local(token_values, cotangent, write_coeffs, read_coeffs, decay_codes, skip_gain):
    seq_len = token_values.shape[1] * lax.axis_size("ctx")
    factor = 0.25 / seq_len
    prepare = jax.vmap(functools.partial(block_states, factor=factor))
    within, totals, decayed_vals, decayed_cot, fwd_state, adj_state = prepare(
        token_values, cotangent, write_coeffs, read_coeffs, decay_codes
    )
    block_gains = jnp.exp(totals)
    identity = (jnp.ones_like(block_gains), jnp.zeros_like(fwd_state))
    position = lax.axis_index("ctx")
    level_count = lax.axis_size("ctx").bit_length() - 1
    fwd_total = (block_gains, fwd_state)
    rev_total = (block_gains, adj_state)
    fwd_prefix = identity
    rev_prefix = identity
    for level in range(level_count):
        partner = from_partner(
            (fwd_total[0], fwd_total[1], rev_total[0], rev_total[1]), "ctx", level
        )
        upper = position >> level & 1 == 1
        other_fwd = (partner[0], partner[1])
        other_rev = (partner[2], partner[3])
        fwd_prefix = pick_tree(upper, chain_pair(other_fwd, fwd_prefix), fwd_prefix)
        fwd_total = pick_tree(
            upper, chain_pair(other_fwd, fwd_total), chain_pair(fwd_total, other_fwd)
        )
        rev_prefix = pick_tree(upper, rev_prefix, chain_pair(other_rev, rev_prefix))
        rev_total = pick_tree(
            upper, chain_pair(rev_total, other_rev), chain_pair(other_rev, rev_total)
        )
    carried_state = fwd_prefix[1]
    carried_adjoint = rev_prefix[1]
    finish = jax.vmap(block_grads, (0, 0, 0, 0, 0, 0, 0, 0, 0, 0, None))
    grad_values, grad_write, grad_read, skip_parts = finish(
        token_values,
        cotangent,
        write_coeffs,
        read_coeffs,
        within,
        totals,
        decayed_vals,
        decayed_cot,
        carried_state,
        carried_adjoint,
        skip_gain,
    )
    grad_skip = lax.psum(jnp.sum(skip_parts, axis=0), ("dp", "ctx"))
    return (grad_values, grad_write, grad_read, grad_skip)


def solution(mesh):
    in_specs = (
        P("dp", "ctx", None),
        P("dp", "ctx", None),
        P("dp", "ctx", None),
        P("dp", "ctx", None),
        P("dp", "ctx", None),
        P(),
    )
    out_specs = (P("dp", "ctx", None), P("dp", "ctx", None), P("dp", "ctx", None), P())
    return jax.shard_map(local, mesh=mesh, in_specs=in_specs, out_specs=out_specs, check_vma=False)
```

profile of v0, /device:TPU:1, one launch (start us, length us, event | category | flops | bytes accessed | tf_op | source)
XLA Modules:
  0.0 289.7 jit_solution(18061633513673262370)
XLA Ops:
  0.6 0.7 negate_multiply_fusion
  1.5 0.2 reduce_window_sum.13
  1.7 1.4 copy.37
  3.4 1.4 convolution_bitcast_fusion.3
  4.8 0.3 copy.40
  5.3 1.4 convolution_bitcast_fusion.1
  6.7 0.5 collective-permute-start.7
  7.2 2.5 collective-permute-done.1
  9.7 0.5 collective-permute-done.7
  10.1 4.5 %add_select_fusion.8 = (f32[1,40,128,64]{2,3,1,0:T(8,128)}, f32[1,40,128,64]{2,3,1,0:T(8,128)}) fusion(f32[1,40,128,64]{2,3,1,0:T(8,128)} %collective-permute-done.7, f32[1,40,128,64]{2,3,1,0:T(8,128)} %convolution_bitcast_fusion.1, f32[40]{0:T(128)S(1)} %fusion.42, f32[40]{0:T(128)S(1)} %bitcast.148, pred[]{:T(512)S(6)} %eq.15, ...), kind=kLoop, calls=%fused_computation.29 | loop fusion | flops 3276800 | bytes 7864641 | tf_op jit(solution)/shard_map/jit(_where)/select_n | solution.py:89
  14.6 2.6 collective-permute-start.8
  17.3 1.4 collective-permute-start.3
  18.7 55.9 %collective-permute-done.3 = f32[1,40]{1,0:T(1,128)S(1)} collective-permute-done((f32[1,40]{1,0:T(1,128)S(1)}, f32[1,40]{1,0:T(1,128)S(1)}, u32[]{:S(2)}, u32[]{:S(2)}) %collective-permute-start.3) | collective-permute-done | bytes 192 | tf_op jit(solution)/shard_map/ppermute | solution.py:10
  74.7 4.5 %add_select_fusion.7 = (f32[1,40,128,64]{2,3,1,0:T(8,128)}, f32[1,40,128,64]{2,3,1,0:T(8,128)}) fusion(f32[1,40,128,64]{2,3,1,0:T(8,128)} %collective-permute-done.8, f32[1,40,128,64]{2,3,1,0:T(8,128)} %get-tuple-element.30, f32[40]{0:T(128)S(1)} %bitcast.153, f32[40]{0:T(128)S(1)} %bitcast.149, pred[]{:T(512)S(6)} %eq.14, ...), kind=kLoop, calls=%fused_computation.28 | loop fusion | flops 3276800 | bytes 7864641 | tf_op jit(solution)/shard_map/jit(_where)/select_n | solution.py:89
  79.2 1.3 collective-permute-start.9
  80.5 0.2 collective-permute-start.4
  80.6 1.3 collective-permute-start.5
  81.9 55.3 %collective-permute-done.5 = f32[1,40]{1,0:T(1,128)S(1)} collective-permute-done((f32[1,40]{1,0:T(1,128)S(1)}, f32[1,40]{1,0:T(1,128)S(1)}, u32[]{:S(2)}, u32[]{:S(2)}) %collective-permute-start.5) | collective-permute-done | bytes 192 | tf_op jit(solution)/shard_map/ppermute | solution.py:10
  137.2 4.5 %add_select_fusion.6 = (f32[1,40,128,64]{2,3,1,0:T(8,128)}, f32[1,40,128,64]{2,3,1,0:T(8,128)}) fusion(f32[1,40,128,64]{2,3,1,0:T(8,128)} %collective-permute-done.9, f32[1,40,128,64]{2,3,1,0:T(8,128)} %get-tuple-element.28, f32[40]{0:T(128)S(1)} %bitcast.154, f32[40]{0:T(128)S(1)} %bitcast.150, pred[]{:T(512)S(6)} %eq.13, ...), kind=kLoop, calls=%fused_computation.27 | loop fusion | flops 3276800 | bytes 7864641 | tf_op jit(solution)/shard_map/jit(_where)/select_n | solution.py:89
  141.7 2.0 collective-permute-start.6
  144.0 1.3 convert_reduce_fusion
  145.4 0.2 fusion.32
  145.6 0.4 collective-permute-start.10
  146.0 0.4 fusion.7
  146.4 132.6 %psum.7 = f32[40]{0:T(128)} all-reduce(f32[40]{0:T(128)S(1)} %fusion.7), channel_id=1, replica_groups=mesh['dp'=2,'ctx'=16] {'dp','ctx'}, use_global_device_ids=true, to_apply=%region_2.3 | all-reduce | flops 40 | bytes 320 | tf_op jit(solution)/shard_map/psum | solution.py:141
  279.1 2.7 fusion.5
  281.8 0.3 fusion.3
  282.1 0.3 copy-done.3
  282.4 1.3 fusion.4
  283.8 1.1 copy.42
  284.9 1.0 fusion.19
  285.8 3.9 %fusion.20 = bf16[1,128,128]{2,1,0:T(8,128)(2,1)} fusion(f32[128,128]{1,0:T(8,128)S(1)} %fusion.28, bf16[128,40,64]{0,2,1:T(8,128)(2,1)S(1)} %bitcast.137, f32[1,40,128,64]{2,3,1,0:T(8,128)} %collective-permute-done.7, f32[1,40,128,64]{2,3,1,0:T(8,128)} %collective-permute-done.8, f32[1,40,128,64]{2,3,1,0:T(8,128)} %collective-permute-done.9, ...), kind=kOutput, calls=%fused_computation.45 | convolution fusion | flops 87523328 | bytes 5997028 | tf_op jit(solution)/shard_map/vmap(ihp,hnp->in)/dot_general | solution.py:62
  (31 shorter events, 1.1 us)
Async XLA Ops:
  0.6 4.7 %copy-start = (bf16[1,128,128]{2,1,0:T(8,128)(2,1)S(1)}, bf16[1,128,128]{2,1,0:T(8,128)(2,1)}, u32[]{:S(2)}) copy-start(bf16[1,128,128]{2,1,0:T(8,128)(2,1)} %param.8) | copy-start | bytes 98308
  1.7 1.7 copy-start.2
  3.4 1.4 copy-start.1
  4.8 4.9 %collective-permute-start = (f32[1,40,128,64]{2,3,1,0:T(8,128)}, f32[1,40,128,64]{2,3,1,0:T(8,128)}, u32[]{:S(2)}, u32[]{:S(2)}) collective-permute-start(f32[1,40,128,64]{2,3,1,0:T(8,128)} %convolution_bitcast_fusion.3), channel_id=1, source_target_pairs={{0,1},{1,0},{2,3},{3,2},{4,5},{5,4},{6,7},{7,6},{8,9},{9,8},{10,11... | collective-permute-start | bytes 3932168 | tf_op jit(solution)/shard_map/ppermute | solution.py:10
  6.7 3.5 %collective-permute-start.7 = (f32[1,40,128,64]{2,3,1,0:T(8,128)}, f32[1,40,128,64]{2,3,1,0:T(8,128)}, u32[]{:S(2)}, u32[]{:S(2)}) collective-permute-start(f32[1,40,128,64]{2,3,1,0:T(8,128)} %convolution_bitcast_fusion.1), channel_id=1, source_target_pairs={{0,1},{1,0},{2,3},{3,2},{4,5},{5,4},{6,7},{7,6},{8,9},{9,8},{10,11... | collective-permute-start | bytes 3932168 | tf_op jit(solution)/shard_map/ppermute | solution.py:10
  7.1 2.5 collective-permute-start.1
  14.6 60.0 %collective-permute-start.8 = (f32[1,40,128,64]{2,3,1,0:T(8,128)}, f32[1,40,128,64]{2,3,1,0:T(8,128)}, u32[]{:S(2)}, u32[]{:S(2)}) collective-permute-start(f32[1,40,128,64]{2,3,1,0:T(8,128)} %get-tuple-element.30), channel_id=1, source_target_pairs={{0,2},{1,3},{2,0},{3,1},{4,6},{5,7},{6,4},{7,5},{8,10},{9,11},{10,... | collective-permute-start | bytes 3932168 | tf_op jit(solution)/shard_map/ppermute | solution.py:10
  17.2 57.4 %collective-permute-start.2 = (f32[1,40,128,64]{2,3,1,0:T(8,128)}, f32[1,40,128,64]{2,3,1,0:T(8,128)}, u32[]{:S(2)}, u32[]{:S(2)}) collective-permute-start(f32[1,40,128,64]{2,3,1,0:T(8,128)} %get-tuple-element.31), channel_id=1, source_target_pairs={{0,2},{1,3},{2,0},{3,1},{4,6},{5,7},{6,4},{7,5},{8,10},{9,11},{10,... | collective-permute-start | bytes 3932168 | tf_op jit(solution)/shard_map/ppermute | solution.py:10
  17.3 57.4 %collective-permute-start.3 = (f32[1,40]{1,0:T(1,128)S(1)}, f32[1,40]{1,0:T(1,128)S(1)}, u32[]{:S(2)}, u32[]{:S(2)}) collective-permute-start(f32[1,40]{1,0:T(1,128)S(1)} %fusion.43), channel_id=1, source_target_pairs={{0,2},{1,3},{2,0},{3,1},{4,6},{5,7},{6,4},{7,5},{8,10},{9,11},{10,... | collective-permute-start | bytes 488 | tf_op jit(solution)/shard_map/ppermute | solution.py:10
  79.2 58.0 %collective-permute-start.9 = (f32[1,40,128,64]{2,3,1,0:T(8,128)}, f32[1,40,128,64]{2,3,1,0:T(8,128)}, u32[]{:S(2)}, u32[]{:S(2)}) collective-permute-start(f32[1,40,128,64]{2,3,1,0:T(8,128)} %get-tuple-element.28), channel_id=1, source_target_pairs={{0,4},{1,5},{2,6},{3,7},{4,0},{5,1},{6,2},{7,3},{8,12},{9,13},{10,... | collective-permute-start | bytes 3932168 | tf_op jit(solution)/shard_map/ppermute | solution.py:10
  80.5 56.7 %collective-permute-start.4 = (f32[1,40,128,64]{2,3,1,0:T(8,128)}, f32[1,40,128,64]{2,3,1,0:T(8,128)}, u32[]{:S(2)}, u32[]{:S(2)}) collective-permute-start(f32[1,40,128,64]{2,3,1,0:T(8,128)} %get-tuple-element.29), channel_id=1, source_target_pairs={{0,4},{1,5},{2,6},{3,7},{4,0},{5,1},{6,2},{7,3},{8,12},{9,13},{10,... | collective-permute-start | bytes 3932168 | tf_op jit(solution)/shard_map/ppermute | solution.py:10
  80.6 56.5 %collective-permute-start.5 = (f32[1,40]{1,0:T(1,128)S(1)}, f32[1,40]{1,0:T(1,128)S(1)}, u32[]{:S(2)}, u32[]{:S(2)}) collective-permute-start(f32[1,40]{1,0:T(1,128)S(1)} %mul.283), channel_id=1, source_target_pairs={{0,4},{1,5},{2,6},{3,7},{4,0},{5,1},{6,2},{7,3},{8,12},{9,13},{10,... | collective-permute-start | bytes 488 | tf_op jit(solution)/shard_map/ppermute | solution.py:10
  141.7 137.4 %collective-permute-start.6 = (f32[1,40,128,64]{2,3,1,0:T(8,128)}, f32[1,40,128,64]{2,3,1,0:T(8,128)}, u32[]{:S(2)}, u32[]{:S(2)}) collective-permute-start(f32[1,40,128,64]{2,3,1,0:T(8,128)} %get-tuple-element.27), channel_id=1, source_target_pairs={{0,8},{1,9},{2,10},{3,11},{4,12},{5,13},{6,14},{7,15},{8,0},{9,1},... | collective-permute-start | bytes 3932168 | tf_op jit(solution)/shard_map/ppermute | solution.py:10
  145.6 140.2 %collective-permute-start.10 = (f32[1,40,128,64]{2,3,1,0:T(8,128)}, f32[1,40,128,64]{2,3,1,0:T(8,128)}, u32[]{:S(2)}, u32[]{:S(2)}) collective-permute-start(f32[1,40,128,64]{2,3,1,0:T(8,128)} %get-tuple-element.26), channel_id=1, source_target_pairs={{0,8},{1,9},{2,10},{3,11},{4,12},{5,13},{6,14},{7,15},{8,0},{9,1},... | collective-permute-start | bytes 3932168 | tf_op jit(solution)/shard_map/ppermute | solution.py:10
  281.8 0.7 copy-start.3
where the time goes:
time: 291 us; the launch traced here: 290 us
  blocking collectives  133 us (46%)
  waiting for transfers between devices  114 us (39%)
  other arithmetic  17.9 us (6%)
  matrix products  10.9 us (4%)
  starting transfers between devices  9.83 us (3%)
  local copies, waits for them, and re-layouts  3.43 us (1%)
    psum x1, blocking collectives, local(): grad_skip = lax.psum(jnp.sum(skip_parts, axis=0), ('dp', 'ctx'))  133 us
    ppermute x11, waiting for transfers between devices, from_partner(): lax.ppermute(array, axis, [(i, i ^ 1 << bit) for i in range(lax.axis_size...  114 us
    select_n x3, other arithmetic, pick_tree(): jnp.where(flag, first_leaf, other_leaf)  13.6 us
    ppermute x11, starting transfers between devices, from_partner(): lax.ppermute(array, axis, [(i, i ^ 1 << bit) for i in range(lax.axis_size...  9.83 us
  transfers between devices with their start and end apart: 11, of which 4 were waited for; matrix products, arithmetic and copies ran while one was open for 4% of the time, Pallas kernels for 0%

commit v1 on v0

--- a/solution.py
+++ b/solution.py
@@ -4,10 +4,6 @@
 import jax.numpy as jnp
 from jax import lax
 from jax.sharding import PartitionSpec as P
-
-
-def from_partner(array, axis, bit):
-    return lax.ppermute(array, axis, [(i, i ^ 1 << bit) for i in range(lax.axis_size(axis))])
 
 
 def block_states(values, cotan, write_map, read_map, codes, factor):
@@ -92,6 +88,38 @@
     )
 
 
+def sweep_scan(gains, state, position, count, reverse):
+    level_count = count.bit_length() - 1
+    index = count - 1 - position if reverse else position
+
+    def mapped(pairs):
+        if reverse:
+            return [(count - 1 - a, count - 1 - b) for a, b in pairs]
+        return pairs
+
+    total = (gains, state)
+    lowers = []
+    for level in range(level_count):
+        span = 1 << level
+        pairs = [(i, i + span) for i in range(count) if i % (2 * span) == span - 1]
+        lower = lax.ppermute(total, "ctx", mapped(pairs))
+        lowers.append(lower)
+        if level < level_count - 1:
+            receives = index % (2 * span) == 2 * span - 1
+            total = pick_tree(receives, chain_pair(lower, total), total)
+    prefix = jnp.zeros_like(state)
+    for level in reversed(range(level_count)):
+        span = 1 << level
+        if level < level_count - 1:
+            pairs = [(i, i - span) for i in range(count) if i % (2 * span) == 2 * span - 1]
+            sent = lax.ppermute(prefix, "ctx", mapped(pairs))
+            prefix = jnp.where(index % (2 * span) == span - 1, sent, prefix)
+        lower_gain, lower_state = lowers[level]
+        grown = lower_gain[..., None, None] * prefix + lower_state
+        prefix = jnp.where(index % (2 * span) == 2 * span - 1, grown, prefix)
+    return prefix
+
+
 def local(token_values, cotangent, write_coeffs, read_coeffs, decay_codes, skip_gain):
     seq_len = token_values.shape[1] * lax.axis_size("ctx")
     factor = 0.25 / seq_len
@@ -100,30 +128,10 @@
         token_values, cotangent, write_coeffs, read_coeffs, decay_codes
     )
     block_gains = jnp.exp(totals)
-    identity = (jnp.ones_like(block_gains), jnp.zeros_like(fwd_state))
     position = lax.axis_index("ctx")
-    level_count = lax.axis_size("ctx").bit_length() - 1
-    fwd_total = (block_gains, fwd_state)
-    rev_total = (block_gains, adj_state)
-    fwd_prefix = identity
-    rev_prefix = identity
-    for level in range(level_count):
-        partner = from_partner(
-            (fwd_total[0], fwd_total[1], rev_total[0], rev_total[1]), "ctx", level
-        )
-        upper = position >> level & 1 == 1
-        other_fwd = (partner[0], partner[1])
-        other_rev = (partner[2], partner[3])
-        fwd_prefix = pick_tree(upper, chain_pair(other_fwd, fwd_prefix), fwd_prefix)
-        fwd_total = pick_tree(
-            upper, chain_pair(other_fwd, fwd_total), chain_pair(fwd_total, other_fwd)
-        )
-        rev_prefix = pick_tree(upper, rev_prefix, chain_pair(other_rev, rev_prefix))
-        rev_total = pick_tree(
-            upper, chain_pair(rev_total, other_rev), chain_pair(other_rev, rev_total)
-        )
-    carried_state = fwd_prefix[1]
-    carried_adjoint = rev_prefix[1]
+    count = lax.axis_size("ctx")
+    carried_state = sweep_scan(block_gains, fwd_state, position, count, False)
+    carried_adjoint = sweep_scan(block_gains, adj_state, position, count, True)
     finish = jax.vmap(block_grads, (0, 0, 0, 0, 0, 0, 0, 0, 0, 0, None))
     grad_values, grad_write, grad_read, skip_parts = finish(
         token_values,

time: 291 us -> 191 us (0.66)
  blocking collectives: 133 us -> 40.8 us
  waiting for transfers between devices: 114 us -> 46.8 us
  starting transfers between devices: 9.83 us -> 48.9 us
  other arithmetic: 17.9 us -> 37.5 us
    psum x1, blocking collectives: 133 us -> 40.8 us  [local(): grad_skip = lax.psum(jnp.sum(skip_parts, axis=0), ('dp', 'ctx'))]
    ppermute x11 -> x22, waiting for transfers between devices: 114 us -> 46.8 us  [the longest x6 38.1 us: sweep_scan(): sent = lax.ppermute(prefix, 'ctx', mapped(pairs))]
    ppermute x11 -> x22, starting transfers between devices: 9.83 us -> 48.9 us  [the longest x16 32.6 us: sweep_scan(): lower = lax.ppermute(total, 'ctx', mapped(pairs))]
    select_n x0 -> x6, other arithmetic: none -> 17.4 us  [sweep_scan(): prefix = jnp.where(index % (2 * span) == 2 * span - 1, grown, prefix)]
    select_n x3 -> x10, other arithmetic: 13.6 us -> 16.5 us  [pick_tree(): jnp.where(flag, first_leaf, other_leaf)]
  transfers between devices with their start and end apart: 11 -> 22, of which waited for: 4 -> 4; matrix products, arithmetic and copies ran while one was open for 4% -> 21% of each run, Pallas kernels for 0% -> 0%
where the time goes in v1:
time: 191 us; the launch traced here: 189 us
  starting transfers between devices  48.9 us (26%)
  waiting for transfers between devices  46.8 us (25%)
  blocking collectives  40.8 us (21%)
  other arithmetic  37.5 us (20%)
  matrix products  10.1 us (5%)
  local copies, waits for them, and re-layouts  3.41 us (2%)
    psum x1, blocking collectives, local(): grad_skip = lax.psum(jnp.sum(skip_parts, axis=0), ('dp', 'ctx'))  40.8 us
    ppermute x6, waiting for transfers between devices, sweep_scan(): sent = lax.ppermute(prefix, 'ctx', mapped(pairs))  38.1 us
    ppermute x16, starting transfers between devices, sweep_scan(): lower = lax.ppermute(total, 'ctx', mapped(pairs))  32.6 us
    select_n x6, other arithmetic, sweep_scan(): prefix = jnp.where(index % (2 * span) == 2 * span - 1, grown, prefix)  17.4 us
    select_n x10, other arithmetic, pick_tree(): jnp.where(flag, first_leaf, other_leaf)  16.5 us
    ppermute x6, starting transfers between devices, sweep_scan(): sent = lax.ppermute(prefix, 'ctx', mapped(pairs))  16.3 us
    ppermute x16, waiting for transfers between devices, sweep_scan(): lower = lax.ppermute(total, 'ctx', mapped(pairs))  8.68 us
  transfers between devices with their start and end apart: 22, of which 4 were waited for; matrix products, arithmetic and copies ran while one was open for 21% of the time, Pallas kernels for 0%

profile of v1, /device:TPU:1, one launch (start us, length us, event | category | flops | bytes accessed | tf_op | source)
XLA Modules:
  0.0 188.6 jit_solution(6923856736481318662)
XLA Ops:
  1.7 1.4 copy.37
  3.4 1.4 convolution_bitcast_fusion.3
  4.8 3.0 %collective-permute-start.4 = (f32[1,40,128,64]{2,3,1,0:T(8,128)}, f32[1,40,128,64]{2,3,1,0:T(8,128)}, u32[]{:S(2)}, u32[]{:S(2)}) collective-permute-start(f32[1,40,128,64]{2,3,1,0:T(8,128)} %convolution_bitcast_fusion.3), channel_id=1, source_target_pairs={{15,14},{13,12},{11,10},{9,8},{7,6},{5,4},{3,2},{1,0},{31,30},{29,... | collective-permute-start | bytes 3932168 | tf_op jit(solution)/shard_map/ppermute | solution.py:105
  11.1 3.9 %collective-permute-done.15 = f32[1,40,128,64]{2,3,1,0:T(8,128)} collective-permute-done((f32[1,40,128,64]{2,3,1,0:T(8,128)}, f32[1,40,128,64]{2,3,1,0:T(8,128)}, u32[]{:S(2)}, u32[]{:S(2)}) %collective-permute-start.15) | collective-permute-done | bytes 1310752 | tf_op jit(solution)/shard_map/ppermute | solution.py:105
  15.0 4.3 %add_select_fusion.2 = (f32[1,40,128,64]{2,3,1,0:T(8,128)}, f32[1,40,128,64]{2,3,1,0:T(8,128)}) fusion(f32[1,40,128,64]{2,3,1,0:T(8,128)} %convolution_bitcast_fusion.1, f32[1,40,128,64]{2,3,1,0:T(8,128)} %collective-permute-done.15, f32[40]{0:T(128)S(1)} %fusion.37, pred[]{:T(512)S(6)} %eq.76, f32[1,40,128,64]{2,3,1,0:T(8,128)} %convolution_bitcast_fusion.3, ...), kind=kLoop, calls=%fused_computation.6 | loop fusion | flops 1966080 | bytes 7864482 | tf_op jit(solution)/shard_map/jit(_where)/select_n | solution.py:85
  19.4 1.7 collective-permute-start.5
  21.1 5.7 %collective-permute-start.16 = (f32[1,40,128,64]{2,3,1,0:T(8,128)}, f32[1,40,128,64]{2,3,1,0:T(8,128)}, u32[]{:S(2)}, u32[]{:S(2)}) collective-permute-start(f32[1,40,128,64]{2,3,1,0:T(8,128)} %get-tuple-element.22), channel_id=1, source_target_pairs={{1,3},{5,7},{9,11},{13,15},{17,19},{21,23},{25,27},{29,31}} | collective-permute-start | bytes 3932168 | tf_op jit(solution)/shard_map/ppermute | solution.py:105
  28.0 3.0 %collective-permute-start = (f32[1,40]{1,0:T(1,128)S(1)}, f32[1,40]{1,0:T(1,128)S(1)}, u32[]{:S(2)}, u32[]{:S(2)}) collective-permute-start(f32[1,40]{1,0:T(1,128)S(1)} %get-tuple-element.19), channel_id=1, source_target_pairs={{15,14},{13,12},{11,10},{9,8},{7,6},{5,4},{3,2},{1,0},{31,30},{29,... | collective-permute-start | bytes 488 | tf_op jit(solution)/shard_map/ppermute | solution.py:105
  31.9 3.0 %add_select_fusion.4 = f32[1,40,128,64]{2,3,1,0:T(8,128)} fusion(f32[1,40,128,64]{2,3,1,0:T(8,128)} %get-tuple-element.23, f32[1,40,128,64]{2,3,1,0:T(8,128)} %collective-permute-done.5, f32[40]{0:T(128)S(1)} %bitcast.149, pred[]{:T(512)S(6)} %eq.71), kind=kLoop, calls=%fused_computation.8 | loop fusion | flops 983040 | bytes 3932321 | tf_op jit(solution)/shard_map/jit(_where)/select_n | solution.py:85
  34.9 1.7 collective-permute-start.6
  36.6 3.9 %collective-permute-done.16 = f32[1,40,128,64]{2,3,1,0:T(8,128)} collective-permute-done((f32[1,40,128,64]{2,3,1,0:T(8,128)}, f32[1,40,128,64]{2,3,1,0:T(8,128)}, u32[]{:S(2)}, u32[]{:S(2)}) %collective-permute-start.16) | collective-permute-done | bytes 1310752 | tf_op jit(solution)/shard_map/ppermute | solution.py:105
  40.5 3.1 %add_select_fusion.1 = f32[1,40,128,64]{2,3,1,0:T(8,128)} fusion(f32[1,40,128,64]{2,3,1,0:T(8,128)} %get-tuple-element.22, f32[1,40,128,64]{2,3,1,0:T(8,128)} %collective-permute-done.16, f32[40]{0:T(128)S(1)} %bitcast.148, pred[]{:T(512)S(6)} %eq.78), kind=kLoop, calls=%fused_computation.5 | loop fusion | flops 983040 | bytes 3932321 | tf_op jit(solution)/shard_map/jit(_where)/select_n | solution.py:85
  43.6 1.8 collective-permute-start.17
  46.0 3.0 %add_select_fusion.3 = f32[1,40,128,64]{2,3,1,0:T(8,128)} fusion(f32[1,40,128,64]{2,3,1,0:T(8,128)} %add_select_fusion.4, f32[1,40,128,64]{2,3,1,0:T(8,128)} %collective-permute-done.6, f32[40]{0:T(128)S(1)} %bitcast.150, pred[]{:T(512)S(6)} %eq.73), kind=kLoop, calls=%fused_computation.7 | loop fusion | flops 983040 | bytes 3932321 | tf_op jit(solution)/shard_map/jit(_where)/select_n | solution.py:85
  49.0 1.7 collective-permute-start.7
  50.7 6.3 %collective-permute-start.12 = (f32[1,40]{1,0:T(1,128)S(1)}, f32[1,40]{1,0:T(1,128)S(1)}, u32[]{:S(2)}, u32[]{:S(2)}) collective-permute-start(f32[1,40]{1,0:T(1,128)S(1)} %get-tuple-element.16), channel_id=1, source_target_pairs={{1,3},{5,7},{9,11},{13,15},{17,19},{21,23},{25,27},{29,31}} | collective-permute-start | bytes 488 | tf_op jit(solution)/shard_map/ppermute | solution.py:105
  57.8 3.1 %add_select_fusion = f32[1,40,128,64]{2,3,1,0:T(8,128)} fusion(f32[1,40,128,64]{2,3,1,0:T(8,128)} %add_select_fusion.1, f32[1,40,128,64]{2,3,1,0:T(8,128)} %collective-permute-done.17, f32[40]{0:T(128)S(1)} %bitcast.151, pred[]{:T(512)S(6)} %eq.80), kind=kLoop, calls=%fused_computation.4 | loop fusion | flops 983040 | bytes 3932321 | tf_op jit(solution)/shard_map/jit(_where)/select_n | solution.py:85
  60.9 1.8 collective-permute-start.18
  63.4 2.5 %add_select_fusion.11 = f32[1,40,128,64]{2,3,1,0:T(8,128)} fusion(f32[1,40,128,64]{2,3,1,0:T(8,128)} %collective-permute-done.7, f32[40]{0:T(128)S(1)} %multiply_bitcast_fusion.1, pred[]{:T(512)S(6)} %eq.75), kind=kLoop, calls=%fused_computation.32 | loop fusion | flops 655360 | bytes 2621601 | tf_op jit(solution)/shard_map/jit(_where)/select_n | solution.py:119
  65.9 1.7 collective-permute-start.8
  69.1 2.5 %add_select_fusion.8 = f32[1,40,128,64]{2,3,1,0:T(8,128)} fusion(f32[1,40,128,64]{2,3,1,0:T(8,128)} %collective-permute-done.18, f32[40]{0:T(128)S(1)} %multiply_bitcast_fusion, pred[]{:T(512)S(6)} %eq.82), kind=kLoop, calls=%fused_computation.28 | loop fusion | flops 655360 | bytes 2621601 | tf_op jit(solution)/shard_map/jit(_where)/select_n | solution.py:119
  71.6 1.8 collective-permute-start.19
  73.4 3.1 %add_select_fusion.10 = f32[1,40,128,64]{2,3,1,0:T(8,128)} fusion(f32[1,40,128,64]{2,3,1,0:T(8,128)} %collective-permute-done.6, f32[1,40,128,64]{2,3,1,0:T(8,128)} %collective-permute-done.8, f32[40]{0:T(128)S(1)} %bitcast.154, pred[]{:T(512)S(6)} %eq.74, pred[]{:T(512)S(6)} %eq.73, f32[1,40,128,64]{2,3,1,0:T(8,128)} %collective-permute-done.7, ...), kind=kLoop, calls=%fused_computation.31 | loop fusion | flops 1966080 | bytes 5243203 | tf_op jit(solution)/shard_map/jit(_where)/select_n | solution.py:119
  76.5 1.7 collective-permute-start.9
  78.3 3.1 %add_select_fusion.7 = f32[1,40,128,64]{2,3,1,0:T(8,128)} fusion(f32[1,40,128,64]{2,3,1,0:T(8,128)} %collective-permute-done.17, f32[1,40,128,64]{2,3,1,0:T(8,128)} %collective-permute-done.19, f32[40]{0:T(128)S(1)} %bitcast.155, pred[]{:T(512)S(6)} %eq.81, pred[]{:T(512)S(6)} %eq.80, f32[1,40,128,64]{2,3,1,0:T(8,128)} %collective-permute-done.18, ...), kind=kLoop, calls=%fused_computation.27 | loop fusion | flops 1966080 | bytes 5243203 | tf_op jit(solution)/shard_map/jit(_where)/select_n | solution.py:119
  82.8 3.0 %add_select_fusion.9 = f32[1,40,128,64]{2,3,1,0:T(8,128)} fusion(f32[1,40,128,64]{2,3,1,0:T(8,128)} %collective-permute-done.5, f32[1,40,128,64]{2,3,1,0:T(8,128)} %collective-permute-done.9, f32[1,40,128,64]{2,3,1,0:T(8,128)} %add_select_fusion.10, f32[40]{0:T(128)S(1)} %bitcast.152, pred[]{:T(512)S(6)} %eq.72, pred[]{:T(512)S(6)} %eq.71), kind=kLoop, calls=%fused_computation.30 | loop fusion | flops 1310720 | bytes 5243042 | tf_op jit(solution)/shard_map/jit(_where)/select_n | solution.py:119
  88.7 38.1 %collective-permute-done.20 = f32[1,40,128,64]{2,3,1,0:T(8,128)} collective-permute-done((f32[1,40,128,64]{2,3,1,0:T(8,128)}, f32[1,40,128,64]{2,3,1,0:T(8,128)}, u32[]{:S(2)}, u32[]{:S(2)}) %collective-permute-start.20) | collective-permute-done | bytes 1310752 | tf_op jit(solution)/shard_map/ppermute | solution.py:115
  126.8 3.0 %add_select_fusion.6 = f32[1,40,128,64]{2,3,1,0:T(8,128)} fusion(f32[1,40,128,64]{2,3,1,0:T(8,128)} %collective-permute-done.16, f32[1,40,128,64]{2,3,1,0:T(8,128)} %collective-permute-done.20, f32[1,40,128,64]{2,3,1,0:T(8,128)} %add_select_fusion.7, f32[40]{0:T(128)S(1)} %bitcast.153, pred[]{:T(512)S(6)} %eq.79, pred[]{:T(512)S(6)} %eq.78), kind=kLoop, calls=%fused_computation.26 | loop fusion | flops 1310720 | bytes 5243042 | tf_op jit(solution)/shard_map/jit(_where)/select_n | solution.py:119
  129.8 8.5 %collective-permute-start.21 = (f32[1,40,128,64]{2,3,1,0:T(8,128)}, f32[1,40,128,64]{2,3,1,0:T(8,128)}, u32[]{:S(2)}, u32[]{:S(2)}) collective-permute-start(f32[1,40,128,64]{2,3,1,0:T(8,128)} %add_select_fusion.6), channel_id=1, source_target_pairs={{1,0},{3,2},{5,4},{7,6},{9,8},{11,10},{13,12},{15,14},{17,16},{19,... | collective-permute-start | bytes 3932168 | tf_op jit(solution)/shard_map/ppermute | solution.py:115
  138.7 40.8 %psum.7 = f32[40]{0:T(128)} all-reduce(f32[40]{0:T(128)S(1)} %fusion.5), channel_id=1, replica_groups=mesh['dp'=2,'ctx'=16] {'dp','ctx'}, use_global_device_ids=true, to_apply=%region_2.3 | all-reduce | flops 40 | bytes 320 | tf_op jit(solution)/shard_map/psum | solution.py:149
  179.6 2.0 %fusion.19 = bf16[40,128,64]{1,2,0:T(8,128)(2,1)S(1)} fusion(f32[1,40,128,64]{2,3,1,0:T(8,128)} %collective-permute-done.4, f32[1,40,128,64]{2,3,1,0:T(8,128)} %collective-permute-done.10, f32[1,40,128,64]{2,3,1,0:T(8,128)} %add_select_fusion.9, f32[40]{0:T(128)S(1)} %bitcast.157, pred[]{:T(512)S(6)} %eq.70, pred[]{:T(512)S(6)} %eq.69), kind=kLoop, calls=%fused_computation.46 | loop fusion | flops 1638400 | bytes 4587682 | tf_op jit(solution)/shard_map/reshape.32
  185.7 2.9 %fusion.18 = bf16[1,128,128]{2,1,0:T(8,128)(2,1)} fusion(f32[128,128]{1,0:T(8,128)S(1)} %fusion.28, bf16[128,40,64]{0,2,1:T(8,128)(2,1)S(1)} %bitcast.145, f32[1,40,128,64]{2,3,1,0:T(8,128)} %collective-permute-done.15, f32[1,40,128,64]{2,3,1,0:T(8,128)} %collective-permute-done.21, f32[1,40,128,64]{2,3,1,0:T(8,128)} %add_select_fusion.6, ...), kind=kOutput, calls=%fused_computation.45 | convolution fusion | flops 85557248 | bytes 4685986 | tf_op jit(solution)/shard_map/vmap(ihp,hnp->in)/dot_general | solution.py:58
  (65 shorter events, 18.7 us)
Async XLA Ops:
  0.6 7.7 %copy-start = (bf16[1,128,128]{2,1,0:T(8,128)(2,1)S(1)}, bf16[1,128,128]{2,1,0:T(8,128)(2,1)}, u32[]{:S(2)}) copy-start(bf16[1,128,128]{2,1,0:T(8,128)(2,1)} %param.8) | copy-start | bytes 98308
  1.7 1.7 copy-start.2
  3.4 4.5 %copy-start.1 = (bf16[1,128,2560]{2,1,0:T(8,128)(2,1)S(1)}, bf16[1,128,2560]{2,1,0:T(8,128)(2,1)}, u32[]{:S(2)}) copy-start(bf16[1,128,2560]{2,1,0:T(8,128)(2,1)} %param.6) | copy-start | bytes 1966084
  4.8 6.2 %collective-permute-start.4 = (f32[1,40,128,64]{2,3,1,0:T(8,128)}, f32[1,40,128,64]{2,3,1,0:T(8,128)}, u32[]{:S(2)}, u32[]{:S(2)}) collective-permute-start(f32[1,40,128,64]{2,3,1,0:T(8,128)} %convolution_bitcast_fusion.3), channel_id=1, source_target_pairs={{15,14},{13,12},{11,10},{9,8},{7,6},{5,4},{3,2},{1,0},{31,30},{29,... | collective-permute-start | bytes 3932168 | tf_op jit(solution)/shard_map/ppermute | solution.py:105
  9.8 5.3 %collective-permute-start.15 = (f32[1,40,128,64]{2,3,1,0:T(8,128)}, f32[1,40,128,64]{2,3,1,0:T(8,128)}, u32[]{:S(2)}, u32[]{:S(2)}) collective-permute-start(f32[1,40,128,64]{2,3,1,0:T(8,128)} %convolution_bitcast_fusion.1), channel_id=1, source_target_pairs={{0,1},{2,3},{4,5},{6,7},{8,9},{10,11},{12,13},{14,15},{16,17},{18,... | collective-permute-start | bytes 3932168 | tf_op jit(solution)/shard_map/ppermute | solution.py:105
  19.4 12.5 %collective-permute-start.5 = (f32[1,40,128,64]{2,3,1,0:T(8,128)}, f32[1,40,128,64]{2,3,1,0:T(8,128)}, u32[]{:S(2)}, u32[]{:S(2)}) collective-permute-start(f32[1,40,128,64]{2,3,1,0:T(8,128)} %get-tuple-element.23), channel_id=1, source_target_pairs={{14,12},{10,8},{6,4},{2,0},{30,28},{26,24},{22,20},{18,16}} | collective-permute-start | bytes 3932168 | tf_op jit(solution)/shard_map/ppermute | solution.py:105
  21.1 19.4 %collective-permute-start.16 = (f32[1,40,128,64]{2,3,1,0:T(8,128)}, f32[1,40,128,64]{2,3,1,0:T(8,128)}, u32[]{:S(2)}, u32[]{:S(2)}) collective-permute-start(f32[1,40,128,64]{2,3,1,0:T(8,128)} %get-tuple-element.22), channel_id=1, source_target_pairs={{1,3},{5,7},{9,11},{13,15},{17,19},{21,23},{25,27},{29,31}} | collective-permute-start | bytes 3932168 | tf_op jit(solution)/shard_map/ppermute | solution.py:105
  26.7 4.3 %collective-permute-start.11 = (f32[1,40]{1,0:T(1,128)S(1)}, f32[1,40]{1,0:T(1,128)S(1)}, u32[]{:S(2)}, u32[]{:S(2)}) collective-permute-start(f32[1,40]{1,0:T(1,128)S(1)} %get-tuple-element.19), channel_id=1, source_target_pairs={{0,1},{2,3},{4,5},{6,7},{8,9},{10,11},{12,13},{14,15},{16,17},{18,... | collective-permute-start | bytes 488 | tf_op jit(solution)/shard_map/ppermute | solution.py:105
  28.0 3.8 %collective-permute-start = (f32[1,40]{1,0:T(1,128)S(1)}, f32[1,40]{1,0:T(1,128)S(1)}, u32[]{:S(2)}, u32[]{:S(2)}) collective-permute-start(f32[1,40]{1,0:T(1,128)S(1)} %get-tuple-element.19), channel_id=1, source_target_pairs={{15,14},{13,12},{11,10},{9,8},{7,6},{5,4},{3,2},{1,0},{31,30},{29,... | collective-permute-start | bytes 488 | tf_op jit(solution)/shard_map/ppermute | solution.py:105
  34.9 11.2 %collective-permute-start.6 = (f32[1,40,128,64]{2,3,1,0:T(8,128)}, f32[1,40,128,64]{2,3,1,0:T(8,128)}, u32[]{:S(2)}, u32[]{:S(2)}) collective-permute-start(f32[1,40,128,64]{2,3,1,0:T(8,128)} %add_select_fusion.4), channel_id=1, source_target_pairs={{12,8},{4,0},{28,24},{20,16}} | collective-permute-start | bytes 3932168 | tf_op jit(solution)/shard_map/ppermute | solution.py:105
  43.6 14.2 %collective-permute-start.17 = (f32[1,40,128,64]{2,3,1,0:T(8,128)}, f32[1,40,128,64]{2,3,1,0:T(8,128)}, u32[]{:S(2)}, u32[]{:S(2)}) collective-permute-start(f32[1,40,128,64]{2,3,1,0:T(8,128)} %add_select_fusion.1), channel_id=1, source_target_pairs={{3,7},{11,15},{19,23},{27,31}} | collective-permute-start | bytes 3932168 | tf_op jit(solution)/shard_map/ppermute | solution.py:105
  45.3 0.7 collective-permute-start.1
  49.0 14.4 %collective-permute-start.7 = (f32[1,40,128,64]{2,3,1,0:T(8,128)}, f32[1,40,128,64]{2,3,1,0:T(8,128)}, u32[]{:S(2)}, u32[]{:S(2)}) collective-permute-start(f32[1,40,128,64]{2,3,1,0:T(8,128)} %add_select_fusion.3), channel_id=1, source_target_pairs={{8,0},{24,16}} | collective-permute-start | bytes 3932168 | tf_op jit(solution)/shard_map/ppermute | solution.py:105
  50.7 7.0 %collective-permute-start.12 = (f32[1,40]{1,0:T(1,128)S(1)}, f32[1,40]{1,0:T(1,128)S(1)}, u32[]{:S(2)}, u32[]{:S(2)}) collective-permute-start(f32[1,40]{1,0:T(1,128)S(1)} %get-tuple-element.16), channel_id=1, source_target_pairs={{1,3},{5,7},{9,11},{13,15},{17,19},{21,23},{25,27},{29,31}} | collective-permute-start | bytes 488 | tf_op jit(solution)/shard_map/ppermute | solution.py:105
  57.1 5.6 %collective-permute-start.2 = (f32[1,40]{1,0:T(1,128)S(1)}, f32[1,40]{1,0:T(1,128)S(1)}, u32[]{:S(2)}, u32[]{:S(2)}) collective-permute-start(f32[1,40]{1,0:T(1,128)S(1)} %broadcast_select_fusion.4), channel_id=1, source_target_pairs={{12,8},{4,0},{28,24},{20,16}} | collective-permute-start | bytes 488 | tf_op jit(solution)/shard_map/ppermute | solution.py:105
  60.9 8.2 %collective-permute-start.18 = (f32[1,40,128,64]{2,3,1,0:T(8,128)}, f32[1,40,128,64]{2,3,1,0:T(8,128)}, u32[]{:S(2)}, u32[]{:S(2)}) collective-permute-start(f32[1,40,128,64]{2,3,1,0:T(8,128)} %add_select_fusion), channel_id=1, source_target_pairs={{7,15},{23,31}} | collective-permute-start | bytes 3932168 | tf_op jit(solution)/shard_map/ppermute | solution.py:105
  62.7 0.7 collective-permute-start.3
  65.9 7.5 %collective-permute-start.8 = (f32[1,40,128,64]{2,3,1,0:T(8,128)}, f32[1,40,128,64]{2,3,1,0:T(8,128)}, u32[]{:S(2)}, u32[]{:S(2)}) collective-permute-start(f32[1,40,128,64]{2,3,1,0:T(8,128)} %add_select_fusion.11), channel_id=1, source_target_pairs={{8,12},{0,4},{24,28},{16,20}} | collective-permute-start | bytes 3932168 | tf_op jit(solution)/shard_map/ppermute | solution.py:115
  67.7 0.7 collective-permute-start.13
  68.3 0.7 collective-permute-start.14
  71.6 6.7 %collective-permute-start.19 = (f32[1,40,128,64]{2,3,1,0:T(8,128)}, f32[1,40,128,64]{2,3,1,0:T(8,128)}, u32[]{:S(2)}, u32[]{:S(2)}) collective-permute-start(f32[1,40,128,64]{2,3,1,0:T(8,128)} %add_select_fusion.8), channel_id=1, source_target_pairs={{7,3},{15,11},{23,19},{31,27}} | collective-permute-start | bytes 3932168 | tf_op jit(solution)/shard_map/ppermute | solution.py:115
  76.5 6.3 %collective-permute-start.9 = (f32[1,40,128,64]{2,3,1,0:T(8,128)}, f32[1,40,128,64]{2,3,1,0:T(8,128)}, u32[]{:S(2)}, u32[]{:S(2)}) collective-permute-start(f32[1,40,128,64]{2,3,1,0:T(8,128)} %add_select_fusion.10), channel_id=1, source_target_pairs={{12,14},{8,10},{4,6},{0,2},{28,30},{24,26},{20,22},{16,18}} | collective-permute-start | bytes 3932168 | tf_op jit(solution)/shard_map/ppermute | solution.py:115
  81.4 45.4 %collective-permute-start.20 = (f32[1,40,128,64]{2,3,1,0:T(8,128)}, f32[1,40,128,64]{2,3,1,0:T(8,128)}, u32[]{:S(2)}, u32[]{:S(2)}) collective-permute-start(f32[1,40,128,64]{2,3,1,0:T(8,128)} %add_select_fusion.7), channel_id=1, source_target_pairs={{3,1},{7,5},{11,9},{15,13},{19,17},{23,21},{27,25},{31,29}} | collective-permute-start | bytes 3932168 | tf_op jit(solution)/shard_map/ppermute | solution.py:115
  85.9 93.8 %collective-permute-start.10 = (f32[1,40,128,64]{2,3,1,0:T(8,128)}, f32[1,40,128,64]{2,3,1,0:T(8,128)}, u32[]{:S(2)}, u32[]{:S(2)}) collective-permute-start(f32[1,40,128,64]{2,3,1,0:T(8,128)} %add_select_fusion.9), channel_id=1, source_target_pairs={{14,15},{12,13},{10,11},{8,9},{6,7},{4,5},{2,3},{0,1},{30,31},{28,... | collective-permute-start | bytes 3932168 | tf_op jit(solution)/shard_map/ppermute | solution.py:115
  129.8 55.9 %collective-permute-start.21 = (f32[1,40,128,64]{2,3,1,0:T(8,128)}, f32[1,40,128,64]{2,3,1,0:T(8,128)}, u32[]{:S(2)}, u32[]{:S(2)}) collective-permute-start(f32[1,40,128,64]{2,3,1,0:T(8,128)} %add_select_fusion.6), channel_id=1, source_target_pairs={{1,0},{3,2},{5,4},{7,6},{9,8},{11,10},{13,12},{15,14},{17,16},{19,... | collective-permute-start | bytes 3932168 | tf_op jit(solution)/shard_map/ppermute | solution.py:115
  181.6 0.7 copy-start.3

commit v2 on v1

v2 whole, which is shorter than its diff:
```python
import functools

import jax
import jax.numpy as jnp
from jax import lax
from jax.sharding import PartitionSpec as P


def spread_heads(per_head, width):
    return jnp.repeat(per_head, width, axis=-1)


def block_states(values, cotan, write_map, read_map, codes, factor):
    head_count = codes.shape[1]
    head_width = values.shape[1] // head_count
    log_decay = -codes.astype(jnp.float32) * factor
    within = jnp.cumsum(log_decay, axis=0)
    totals = within[-1]
    value_scale = spread_heads(jnp.exp(totals - within), head_width)
    cot_scale = spread_heads(jnp.exp(within), head_width)
    decayed_vals = (values.astype(jnp.float32) * value_scale).astype(jnp.bfloat16)
    decayed_cot = (cotan.astype(jnp.float32) * cot_scale).astype(jnp.bfloat16)
    fwd_state = jnp.einsum("jn,jq->nq", write_map, decayed_vals, preferred_element_type=jnp.float32)
    adj_state = jnp.einsum("in,iq->nq", read_map, decayed_cot, preferred_element_type=jnp.float32)
    skip_part = jnp.sum(
        (values.astype(jnp.float32) * cotan.astype(jnp.float32)).reshape(
            values.shape[0], head_count, head_width
        ),
        axis=(0, 2),
    )
    return within, totals, value_scale, decayed_vals, decayed_cot, fwd_state, adj_state, skip_part


def block_local_grads(values, cotan, write_map, read_map, within, skip_gain):
    token_count = values.shape[0]
    head_count = skip_gain.shape[0]
    head_width = values.shape[1] // head_count
    vals_three = values.reshape(token_count, head_count, head_width)
    cot_three = cotan.reshape(token_count, head_count, head_width)
    rows = jnp.arange(token_count)
    causal = (rows[:, None] >= rows[None, :])[None]
    lead = within.T
    spread = lead[:, :, None] - lead[:, None, :]
    decay_matrix = jnp.where(causal, jnp.exp(jnp.where(causal, spread, 0.0)), 0.0)
    products = jnp.einsum("ihp,jhp->hij", cot_three, vals_three, preferred_element_type=jnp.float32)
    read_weights = (products * decay_matrix).astype(jnp.bfloat16)
    gram = jnp.einsum("in,jn->ij", read_map, write_map, preferred_element_type=jnp.float32)
    value_weights = (gram[None] * decay_matrix).astype(jnp.bfloat16)
    grad_read = jnp.einsum("hij,jn->in", read_weights, write_map, preferred_element_type=jnp.float32)
    grad_write = jnp.einsum("hij,in->jn", read_weights, read_map, preferred_element_type=jnp.float32)
    grad_values = jnp.einsum(
        "hij,ihp->jhp", value_weights, cot_three, preferred_element_type=jnp.float32
    ) + skip_gain[None, :, None] * cot_three.astype(jnp.float32)
    return grad_values.reshape(token_count, head_count * head_width), grad_write, grad_read


def block_carried_grads(
    write_map, value_scale, decayed_vals, decayed_cot, carried_state, carried_adjoint, local_grads
):
    local_values, local_write, local_read = local_grads
    state_rounded = carried_state.astype(jnp.bfloat16)
    adjoint_rounded = carried_adjoint.astype(jnp.bfloat16)
    grad_read = local_read + jnp.einsum(
        "iq,nq->in", decayed_cot, state_rounded, preferred_element_type=jnp.float32
    )
    grad_write = local_write + jnp.einsum(
        "jq,nq->jn", decayed_vals, adjoint_rounded, preferred_element_type=jnp.float32
    )
    carried_term = jnp.einsum("jn,nq->jq", write_map, adjoint_rounded, preferred_element_type=jnp.float32)
    grad_values = local_values + value_scale * carried_term
    return (
        grad_values.astype(jnp.bfloat16),
        grad_write.astype(jnp.bfloat16),
        grad_read.astype(jnp.bfloat16),
    )


def sweep_scan(gains, state, position, count, reverse):
    head_width = state.shape[-1] // gains.shape[-1]
    level_count = count.bit_length() - 1
    index = count - 1 - position if reverse else position

    def mapped(pairs):
        if reverse:
            return [(count - 1 - a, count - 1 - b) for a, b in pairs]
        return pairs

    def grow(gain, earlier, later):
        return spread_heads(gain, head_width)[..., None, :] * earlier + later

    total_gain, total_state = gains, state
    lowers = []
    for level in range(level_count):
        span = 1 << level
        pairs = [(i, i + span) for i in range(count) if i % (2 * span) == span - 1]
        lower = lax.ppermute((total_gain, total_state), "ctx", mapped(pairs))
        lowers.append(lower)
        if level < level_count - 1:
            receives = index % (2 * span) == 2 * span - 1
            total_state = jnp.where(receives, grow(total_gain, lower[1], total_state), total_state)
            total_gain = jnp.where(receives, lower[0] * total_gain, total_gain)
    prefix = jnp.zeros_like(state)
    for level in reversed(range(level_count)):
        span = 1 << level
        if level < level_count - 1:
            pairs = [(i, i - span) for i in range(count) if i % (2 * span) == 2 * span - 1]
            sent = lax.ppermute(prefix, "ctx", mapped(pairs))
            prefix = jnp.where(index % (2 * span) == span - 1, sent, prefix)
        lower_gain, lower_state = lowers[level]
        prefix = jnp.where(
            index % (2 * span) == 2 * span - 1, grow(lower_gain, prefix, lower_state), prefix
        )
    return prefix


def local(token_values, cotangent, write_coeffs, read_coeffs, decay_codes, skip_gain):
    seq_len = token_values.shape[1] * lax.axis_size("ctx")
    factor = 0.25 / seq_len
    prepare = jax.vmap(functools.partial(block_states, factor=factor))
    within, totals, value_scale, decayed_vals, decayed_cot, fwd_state, adj_state, skip_parts = prepare(
        token_values, cotangent, write_coeffs, read_coeffs, decay_codes
    )
    grad_skip = lax.psum(jnp.sum(skip_parts, axis=0), ("dp", "ctx"))
    grad_skip, fwd_state, adj_state = lax.optimization_barrier((grad_skip, fwd_state, adj_state))
    block_gains = jnp.exp(totals)
    position = lax.axis_index("ctx")
    count = lax.axis_size("ctx")
    carried_state = sweep_scan(block_gains, fwd_state, position, count, False)
    carried_adjoint = sweep_scan(block_gains, adj_state, position, count, True)
    local_grads = jax.vmap(block_local_grads, (0, 0, 0, 0, 0, None))(
        token_values, cotangent, write_coeffs, read_coeffs, within, skip_gain
    )
    grad_values, grad_write, grad_read = jax.vmap(block_carried_grads)(
        write_coeffs, value_scale, decayed_vals, decayed_cot, carried_state, carried_adjoint, local_grads
    )
    return (grad_values, grad_write, grad_read, grad_skip)


def solution(mesh):
    in_specs = (
        P("dp", "ctx", None),
        P("dp", "ctx", None),
        P("dp", "ctx", None),
        P("dp", "ctx", None),
        P("dp", "ctx", None),
        P(),
    )
    out_specs = (P("dp", "ctx", None), P("dp", "ctx", None), P("dp", "ctx", None), P())
    return jax.shard_map(local, mesh=mesh, in_specs=in_specs, out_specs=out_specs, check_vma=False)
```

time: 191 us -> 195 us (1.021)
  starting transfers between devices: 48.9 us -> 40.4 us
  waiting for transfers between devices: 46.8 us -> 53 us
  local copies, waits for them, and re-layouts: 3.41 us -> 8.98 us
    ppermute x6, waiting for transfers between devices: 38.1 us -> 43.7 us  [sweep_scan(): sent = lax.ppermute(prefix, 'ctx', mapped(pairs))]
    ppermute x16, starting transfers between devices: 32.6 us -> 27.5 us  [sweep_scan(): lower = lax.ppermute((total_gain, total_state), 'ctx', mapped(pairs))]
    unnamed x11 -> x31, local copies, waits for them, and re-layouts: 3.18 us -> 6.71 us
    ppermute x6, starting transfers between devices: 16.3 us -> 12.9 us  [sweep_scan(): sent = lax.ppermute(prefix, 'ctx', mapped(pairs))]
where the time goes in v2:
time: 195 us; the launch traced here: 192 us
  waiting for transfers between devices  53 us (27%)
  blocking collectives  40.8 us (21%)
  starting transfers between devices  40.4 us (21%)
  other arithmetic  36.3 us (19%)
  matrix products  11.6 us (6%)
  local copies, waits for them, and re-layouts  8.98 us (5%)
    ppermute x6, waiting for transfers between devices, sweep_scan(): sent = lax.ppermute(prefix, 'ctx', mapped(pairs))  43.7 us
    psum x1, blocking collectives, local(): grad_skip = lax.psum(jnp.sum(skip_parts, axis=0), ('dp', 'ctx'))  40.8 us
    ppermute x16, starting transfers between devices, sweep_scan(): lower = lax.ppermute((total_gain, total_state), 'ctx', mapped(pairs))  27.5 us
    select_n x6, other arithmetic, sweep_scan(): jnp.where(index % (2 * span) == 2 * span - 1, grow(lower_gain, prefix, lo...  17.2 us
    select_n x5, other arithmetic, sweep_scan(): jnp.where(receives, grow(total_gain, lower[1], total_state), total_state)  15.3 us
    ppermute x6, starting transfers between devices, sweep_scan(): sent = lax.ppermute(prefix, 'ctx', mapped(pairs))  12.9 us
    ppermute x16, waiting for transfers between devices, sweep_scan(): lower = lax.ppermute((total_gain, total_state), 'ctx', mapped(pairs))  9.38 us
    unnamed x31, local copies, waits for them, and re-layouts  6.71 us
  transfers between devices with their start and end apart: 22, of which 4 were waited for; matrix products, arithmetic and copies ran while one was open for 21% of the time, Pallas kernels for 0%

profile of v2, /device:TPU:1, one launch (start us, length us, event | category | flops | bytes accessed | tf_op | source)
XLA Modules:
  0.0 192.1 jit_solution(5991380124199949358)
XLA Ops:
  1.8 1.4 copy.43
  4.6 40.8 %psum.7 = f32[40]{0:T(128)} all-reduce(f32[40]{0:T(128)S(1)} %reduce_sum.35), channel_id=1, replica_groups=mesh['dp'=2,'ctx'=16] {'dp','ctx'}, use_global_device_ids=true, to_apply=%region_3.4 | all-reduce | flops 40 | bytes 320 | tf_op jit(solution)/shard_map/psum | solution.py:123
  49.5 4.3 %collective-permute-start.4 = (f32[1,128,2560]{1,2,0:T(8,128)}, f32[1,128,2560]{1,2,0:T(8,128)}, u32[]{:S(2)}, u32[]{:S(2)}) collective-permute-start(f32[1,128,2560]{1,2,0:T(8,128)} %convolution_bitcast_fusion.1), channel_id=1, source_target_pairs={{15,14},{13,12},{11,10},{9,8},{7,6},{5,4},{3,2},{1,0},{31,30},{29,... | collective-permute-start | bytes 3932168 | tf_op jit(solution)/shard_map/ppermute | solution.py:96
  55.7 4.0 %add_select_fusion.2 = (f32[1,128,2560]{1,2,0:T(8,128)}, f32[1,128,2560]{1,2,0:T(8,128)S(1)}) fusion(f32[1,128,2560]{1,2,0:T(8,128)} %convolution_bitcast_fusion.2, f32[1,128,2560]{1,2,0:T(8,128)} %copy-done.2, f32[2560]{0:T(1024)S(1)} %broadcast_in_dim.115, pred[]{:T(512)S(6)} %eq.76, f32[1,128,2560]{1,2,0:T(8,128)} %convolution_bitcast_fusion.1, ...), kind=kLoop, calls=%fused_computation.13 | loop fusion | flops 1966080 | bytes 7874562 | tf_op jit(solution)/shard_map/jit(_where)/select_n | solution.py:100
  59.7 1.7 collective-permute-start.5
  61.5 1.8 collective-permute-start
  64.6 1.7 collective-permute-done.11
  66.5 6.4 %collective-permute-start.16 = (f32[1,128,2560]{1,2,0:T(8,128)}, f32[1,128,2560]{1,2,0:T(8,128)}, u32[]{:S(2)}, u32[]{:S(2)}) collective-permute-start(f32[1,128,2560]{1,2,0:T(8,128)} %get-tuple-element.35), channel_id=1, source_target_pairs={{1,3},{5,7},{9,11},{13,15},{17,19},{21,23},{25,27},{29,31}} | collective-permute-start | bytes 3932168 | tf_op jit(solution)/shard_map/ppermute | solution.py:96
  72.9 2.1 %add_select_fusion.4 = f32[1,128,2560]{1,2,0:T(8,128)S(1)} fusion(f32[1,128,2560]{1,2,0:T(8,128)} %copy-done.1, f32[1,128,2560]{1,2,0:T(8,128)} %collective-permute-done.5, f32[2560]{0:T(1024)S(1)} %broadcast_in_dim.113, pred[]{:T(512)S(6)} %eq.71), kind=kLoop, calls=%fused_computation.15 | loop fusion | flops 983040 | bytes 3942401 | tf_op jit(solution)/shard_map/jit(_where)/select_n | solution.py:100
  75.0 1.7 collective-permute-start.6
  79.7 7.0 %collective-permute-done.16 = f32[1,128,2560]{1,2,0:T(8,128)} collective-permute-done((f32[1,128,2560]{1,2,0:T(8,128)}, f32[1,128,2560]{1,2,0:T(8,128)}, u32[]{:S(2)}, u32[]{:S(2)}) %collective-permute-start.16) | collective-permute-done | bytes 1310752 | tf_op jit(solution)/shard_map/ppermute | solution.py:96
  86.7 3.2 %add_select_fusion.1 = f32[1,128,2560]{1,2,0:T(8,128)} fusion(f32[1,128,2560]{1,2,0:T(8,128)} %get-tuple-element.35, f32[1,128,2560]{1,2,0:T(8,128)} %collective-permute-done.16, f32[2560]{0:T(1024)S(1)} %broadcast_in_dim.129, pred[]{:T(512)S(6)} %eq.78), kind=kLoop, calls=%fused_computation.12 | loop fusion | flops 983040 | bytes 3942401 | tf_op jit(solution)/shard_map/jit(_where)/select_n | solution.py:100
  89.8 1.7 collective-permute-start.17
  91.6 2.8 %add_select_fusion.3 = f32[1,128,2560]{1,2,0:T(8,128)} fusion(f32[1,128,2560]{1,2,0:T(8,128)S(1)} %add_select_fusion.4, f32[1,128,2560]{1,2,0:T(8,128)} %collective-permute-done.6, f32[2560]{0:T(1024)S(1)} %broadcast_in_dim.111, pred[]{:T(512)S(6)} %eq.73), kind=kLoop, calls=%fused_computation.14 | loop fusion | flops 983040 | bytes 3942401 | tf_op jit(solution)/shard_map/jit(_where)/select_n | solution.py:100
  96.1 3.2 %add_select_fusion = f32[1,128,2560]{1,2,0:T(8,128)} fusion(f32[1,128,2560]{1,2,0:T(8,128)} %add_select_fusion.1, f32[1,128,2560]{1,2,0:T(8,128)} %collective-permute-done.17, f32[2560]{0:T(1024)S(1)} %broadcast_in_dim.127, pred[]{:T(512)S(6)} %eq.80), kind=kLoop, calls=%fused_computation.11 | loop fusion | flops 983040 | bytes 3942401 | tf_op jit(solution)/shard_map/jit(_where)/select_n | solution.py:100
  99.3 1.8 collective-permute-start.18
  101.2 1.5 add_select_fusion.11
  102.6 1.8 collective-permute-start.8
  106.2 2.8 %add_select_fusion.8 = f32[1,128,2560]{1,2,0:T(8,128)} fusion(f32[1,128,2560]{1,2,0:T(8,128)} %collective-permute-done.18, f32[2560]{0:T(1024)S(1)} %mul.242, pred[]{:T(512)S(6)} %eq.82), kind=kLoop, calls=%fused_computation.28 | loop fusion | flops 655360 | bytes 2631681 | tf_op jit(solution)/shard_map/jit(_where)/select_n | solution.py:110
  109.0 1.8 collective-permute-start.19
  110.8 3.7 %add_select_fusion.10 = f32[1,128,2560]{1,2,0:T(8,128)} fusion(f32[1,128,2560]{1,2,0:T(8,128)} %collective-permute-done.6, f32[1,128,2560]{1,2,0:T(8,128)} %collective-permute-done.8, f32[2560]{0:T(1024)S(1)} %broadcast_in_dim.108, pred[]{:T(512)S(6)} %eq.74, pred[]{:T(512)S(6)} %eq.73, f32[1,128,2560]{1,2,0:T(8,128)S(1)} %collective-permute-done.7, ...), kind=kLoop, calls=%fused_computation.31 | loop fusion | flops 1966080 | bytes 5263363 | tf_op jit(solution)/shard_map/jit(_where)/select_n | solution.py:110
  114.6 1.8 collective-permute-start.9
  116.5 2.2 %fusion.4 = f32[1,128,40,64]{1,3,2,0:T(8,128)} fusion(bf16[128,40,64]{0,2,1:T(8,128)(2,1)S(1)} %bitcast.115, f32[40,128]{1,0:T(8,128)S(1)} %copy.41, f32[128,128]{1,0:T(8,128)S(1)} %fusion.31, pred[128,128]{1,0:T(8,128)(4,1)S(1)} %iota_compare_fusion, f32[40]{0:T(128)S(1)} %copy-done.13, bf16[1,128,40,64]{1,3,2,0:T(8,128)(2,1)S(1)} %bitcast.116), kind=kOutput, calls=%fused_computation.20 | convolution fusion | flops 88145920 | bytes 2724000 | tf_op jit(solution)/shard_map/vmap(hij,ihp->jhp)/dot_general | solution.py:51
  119.0 3.9 %add_select_fusion.7 = f32[1,128,2560]{1,2,0:T(8,128)} fusion(f32[1,128,2560]{1,2,0:T(8,128)} %collective-permute-done.17, f32[1,128,2560]{1,2,0:T(8,128)} %collective-permute-done.19, f32[2560]{0:T(1024)S(1)} %broadcast_in_dim.124, pred[]{:T(512)S(6)} %eq.81, pred[]{:T(512)S(6)} %eq.80, f32[1,128,2560]{1,2,0:T(8,128)} %collective-permute-done.18, ...), kind=kLoop, calls=%fused_computation.27 | loop fusion | flops 1966080 | bytes 5263363 | tf_op jit(solution)/shard_map/jit(_where)/select_n | solution.py:110
  122.9 1.4 collective-permute-start.20
  124.3 2.1 %add_select_fusion.9 = f32[1,128,2560]{1,2,0:T(8,128)S(1)} fusion(f32[1,128,2560]{1,2,0:T(8,128)} %collective-permute-done.5, f32[1,128,2560]{1,2,0:T(8,128)} %collective-permute-done.9, f32[1,128,2560]{1,2,0:T(8,128)} %add_select_fusion.10, f32[2560]{0:T(1024)S(1)} %broadcast_in_dim.106, pred[]{:T(512)S(6)} %eq.72, pred[]{:T(512)S(6)} %eq.71), kind=kLoop, calls=%fused_computation.30 | loop fusion | flops 1310720 | bytes 5253122 | tf_op jit(solution)/shard_map/jit(_where)/select_n | solution.py:110
  129.4 43.7 %collective-permute-done.20 = f32[1,128,2560]{1,2,0:T(8,128)} collective-permute-done((f32[1,128,2560]{1,2,0:T(8,128)}, f32[1,128,2560]{1,2,0:T(8,128)}, u32[]{:S(2)}, u32[]{:S(2)}) %collective-permute-start.20) | collective-permute-done | bytes 1310752 | tf_op jit(solution)/shard_map/ppermute | solution.py:107
  173.0 3.2 %add_select_fusion.6 = f32[1,128,2560]{1,2,0:T(8,128)} fusion(f32[1,128,2560]{1,2,0:T(8,128)} %collective-permute-done.16, f32[1,128,2560]{1,2,0:T(8,128)} %collective-permute-done.20, f32[1,128,2560]{1,2,0:T(8,128)} %add_select_fusion.7, f32[2560]{0:T(1024)S(1)} %broadcast_in_dim.122, pred[]{:T(512)S(6)} %eq.79, pred[]{:T(512)S(6)} %eq.78), kind=kLoop, calls=%fused_computation.26 | loop fusion | flops 1310720 | bytes 5253122 | tf_op jit(solution)/shard_map/jit(_where)/select_n | solution.py:110
  176.2 4.7 %collective-permute-start.21 = (f32[1,128,2560]{1,2,0:T(8,128)}, f32[1,128,2560]{1,2,0:T(8,128)}, u32[]{:S(2)}, u32[]{:S(2)}) collective-permute-start(f32[1,128,2560]{1,2,0:T(8,128)} %add_select_fusion.6), channel_id=1, source_target_pairs={{1,0},{3,2},{5,4},{7,6},{9,8},{11,10},{13,12},{15,14},{17,16},{19,... | collective-permute-start | bytes 3932168 | tf_op jit(solution)/shard_map/ppermute | solution.py:107
  181.5 2.1 %fusion.17 = bf16[128,2560]{0,1:T(8,128)(2,1)S(1)} fusion(f32[1,128,2560]{1,2,0:T(8,128)} %collective-permute-done.4, f32[1,128,2560]{1,2,0:T(8,128)} %collective-permute-done.10, f32[1,128,2560]{1,2,0:T(8,128)S(1)} %add_select_fusion.9, f32[2560]{0:T(1024)S(1)} %broadcast_in_dim.104, pred[]{:T(512)S(6)} %eq.70, pred[]{:T(512)S(6)} %eq.69), kind=kLoop, calls=%fused_computation.44 | loop fusion | flops 1638400 | bytes 4597762 | tf_op jit(solution)/shard_map/reshape.45
  186.1 2.3 %copy.48 = bf16[1,128,2560]{2,1,0:T(8,128)(2,1)} copy(bf16[1,128,2560]{1,2,0:T(8,128)(2,1)} %fusion.3) | data formatting | bytes 1310720
  189.4 2.7 %fusion.15 = bf16[1,128,128]{2,1,0:T(8,128)(2,1)} fusion(f32[128,128]{1,0:T(8,128)S(1)} %fusion.27, f32[1,128,2560]{1,2,0:T(8,128)S(1)} %copy-done.3, f32[1,128,2560]{1,2,0:T(8,128)} %collective-permute-done.21, f32[1,128,2560]{1,2,0:T(8,128)} %add_select_fusion.6, bf16[1,128,2560]{1,2,0:T(8,128)(2,1)S(1)} %get-tuple-element.26, ...), kind=kOutput, calls=%fused_computation.42 | convolution fusion | flops 85557248 | bytes 4696066 | tf_op jit(solution)/shard_map/vmap(iq,nq->in)/dot_general | solution.py:63
  (112 shorter events, 23.6 us)
Async XLA Ops:
  0.6 46.2 %copy-start = (bf16[1,128,128]{2,1,0:T(8,128)(2,1)S(1)}, bf16[1,128,128]{2,1,0:T(8,128)(2,1)}, u32[]{:S(2)}) copy-start(bf16[1,128,128]{2,1,0:T(8,128)(2,1)} %param.8) | copy-start | bytes 98308
  3.2 113.2 %copy-start.4 = (bf16[1,128,2560]{1,2,0:T(8,128)(2,1)}, bf16[1,128,2560]{1,2,0:T(8,128)(2,1)S(1)}, u32[]{:S(2)}) copy-start(bf16[1,128,2560]{1,2,0:T(8,128)(2,1)S(1)} %copy.43) | copy-start | bytes 1966084
  3.7 41.7 %copy-start.10 = (bf16[1,128,128]{2,1,0:T(8,128)(2,1)S(1)}, bf16[1,128,128]{2,1,0:T(8,128)(2,1)}, u32[]{:S(2)}) copy-start(bf16[1,128,128]{2,1,0:T(8,128)(2,1)} %param.9) | copy-start | bytes 98308
  48.2 5.8 %collective-permute-start.15 = (f32[1,128,2560]{1,2,0:T(8,128)}, f32[1,128,2560]{1,2,0:T(8,128)S(1)}, u32[]{:S(2)}, u32[]{:S(2)}) collective-permute-start(f32[1,128,2560]{1,2,0:T(8,128)} %convolution_bitcast_fusion.2), channel_id=1, source_target_pairs={{0,1},{2,3},{4,5},{6,7},{8,9},{10,11},{12,13},{14,15},{16,17},{18,... | collective-permute-start | bytes 3932168 | tf_op jit(solution)/shard_map/ppermute | solution.py:96
  49.5 6.3 %collective-permute-start.4 = (f32[1,128,2560]{1,2,0:T(8,128)}, f32[1,128,2560]{1,2,0:T(8,128)}, u32[]{:S(2)}, u32[]{:S(2)}) collective-permute-start(f32[1,128,2560]{1,2,0:T(8,128)} %convolution_bitcast_fusion.1), channel_id=1, source_target_pairs={{15,14},{13,12},{11,10},{9,8},{7,6},{5,4},{3,2},{1,0},{31,30},{29,... | collective-permute-start | bytes 3932168 | tf_op jit(solution)/shard_map/ppermute | solution.py:96
  59.7 13.2 %copy-start.1 = (f32[1,128,2560]{1,2,0:T(8,128)}, f32[1,128,2560]{1,2,0:T(8,128)S(1)}, u32[]{:S(2)}) copy-start(f32[1,128,2560]{1,2,0:T(8,128)S(1)} %get-tuple-element.36) | copy-start | bytes 3932164
  59.7 13.2 %collective-permute-start.5 = (f32[1,128,2560]{1,2,0:T(8,128)S(1)}, f32[1,128,2560]{1,2,0:T(8,128)}, u32[]{:S(2)}, u32[]{:S(2)}) collective-permute-start(f32[1,128,2560]{1,2,0:T(8,128)S(1)} %get-tuple-element.36), channel_id=1, source_target_pairs={{14,12},{10,8},{6,4},{2,0},{30,28},{26,24},{22,20},{18,16}} | collective-permute-start | bytes 3932168 | tf_op jit(solution)/shard_map/ppermute | solution.py:96
  61.5 3.2 %collective-permute-start = (f32[1,40]{1,0:T(1,128)S(1)}, f32[1,40]{1,0:T(1,128)S(1)}, u32[]{:S(2)}, u32[]{:S(2)}) collective-permute-start(f32[1,40]{1,0:T(1,128)S(1)} %get-tuple-element.31), channel_id=1, source_target_pairs={{15,14},{13,12},{11,10},{9,8},{7,6},{5,4},{3,2},{1,0},{31,30},{29,... | collective-permute-start | bytes 488 | tf_op jit(solution)/shard_map/ppermute | solution.py:96
  63.3 3.0 %collective-permute-start.11 = (f32[1,40]{1,0:T(1,128)S(1)}, f32[1,40]{1,0:T(1,128)S(1)}, u32[]{:S(2)}, u32[]{:S(2)}) collective-permute-start(f32[1,40]{1,0:T(1,128)S(1)} %get-tuple-element.31), channel_id=1, source_target_pairs={{0,1},{2,3},{4,5},{6,7},{8,9},{10,11},{12,13},{14,15},{16,17},{18,... | collective-permute-start | bytes 488 | tf_op jit(solution)/shard_map/ppermute | solution.py:96
  66.5 20.2 %collective-permute-start.16 = (f32[1,128,2560]{1,2,0:T(8,128)}, f32[1,128,2560]{1,2,0:T(8,128)}, u32[]{:S(2)}, u32[]{:S(2)}) collective-permute-start(f32[1,128,2560]{1,2,0:T(8,128)} %get-tuple-element.35), channel_id=1, source_target_pairs={{1,3},{5,7},{9,11},{13,15},{17,19},{21,23},{25,27},{29,31}} | collective-permute-start | bytes 3932168 | tf_op jit(solution)/shard_map/ppermute | solution.py:96
  75.0 16.5 %collective-permute-start.6 = (f32[1,128,2560]{1,2,0:T(8,128)S(1)}, f32[1,128,2560]{1,2,0:T(8,128)}, u32[]{:S(2)}, u32[]{:S(2)}) collective-permute-start(f32[1,128,2560]{1,2,0:T(8,128)S(1)} %add_select_fusion.4), channel_id=1, source_target_pairs={{12,8},{4,0},{28,24},{20,16}} | collective-permute-start | bytes 3932168 | tf_op jit(solution)/shard_map/ppermute | solution.py:96
  76.8 2.1 %collective-permute-start.1 = (f32[1,40]{1,0:T(1,128)S(1)}, f32[1,40]{1,0:T(1,128)S(1)}, u32[]{:S(2)}, u32[]{:S(2)}) collective-permute-start(f32[1,40]{1,0:T(1,128)S(1)} %get-tuple-element.30), channel_id=1, source_target_pairs={{14,12},{10,8},{6,4},{2,0},{30,28},{26,24},{22,20},{18,16}} | collective-permute-start | bytes 488 | tf_op jit(solution)/shard_map/ppermute | solution.py:96
  77.4 17.7 %collective-permute-start.12 = (f32[1,40]{1,0:T(1,128)S(1)}, f32[1,40]{1,0:T(1,128)S(1)}, u32[]{:S(2)}, u32[]{:S(2)}) collective-permute-start(f32[1,40]{1,0:T(1,128)S(1)} %get-tuple-element.29), channel_id=1, source_target_pairs={{1,3},{5,7},{9,11},{13,15},{17,19},{21,23},{25,27},{29,31}} | collective-permute-start | bytes 488 | tf_op jit(solution)/shard_map/ppermute | solution.py:96
  78.9 16.3 %collective-permute-start.2 = (f32[1,40]{1,0:T(1,128)S(1)}, f32[1,40]{1,0:T(1,128)S(1)}, u32[]{:S(2)}, u32[]{:S(2)}) collective-permute-start(f32[1,40]{1,0:T(1,128)S(1)} %broadcast_select_fusion.4), channel_id=1, source_target_pairs={{12,8},{4,0},{28,24},{20,16}} | collective-permute-start | bytes 488 | tf_op jit(solution)/shard_map/ppermute | solution.py:96
  89.8 6.3 %collective-permute-start.17 = (f32[1,128,2560]{1,2,0:T(8,128)}, f32[1,128,2560]{1,2,0:T(8,128)}, u32[]{:S(2)}, u32[]{:S(2)}) collective-permute-start(f32[1,128,2560]{1,2,0:T(8,128)} %add_select_fusion.1), channel_id=1, source_target_pairs={{3,7},{11,15},{19,23},{27,31}} | collective-permute-start | bytes 3932168 | tf_op jit(solution)/shard_map/ppermute | solution.py:96
  94.4 6.8 %collective-permute-start.7 = (f32[1,128,2560]{1,2,0:T(8,128)}, f32[1,128,2560]{1,2,0:T(8,128)S(1)}, u32[]{:S(2)}, u32[]{:S(2)}) collective-permute-start(f32[1,128,2560]{1,2,0:T(8,128)} %add_select_fusion.3), channel_id=1, source_target_pairs={{8,0},{24,16}} | collective-permute-start | bytes 3932168 | tf_op jit(solution)/shard_map/ppermute | solution.py:96
  95.2 0.8 collective-permute-start.3
  99.3 6.9 %collective-permute-start.18 = (f32[1,128,2560]{1,2,0:T(8,128)}, f32[1,128,2560]{1,2,0:T(8,128)}, u32[]{:S(2)}, u32[]{:S(2)}) collective-permute-start(f32[1,128,2560]{1,2,0:T(8,128)} %add_select_fusion), channel_id=1, source_target_pairs={{7,15},{23,31}} | collective-permute-start | bytes 3932168 | tf_op jit(solution)/shard_map/ppermute | solution.py:96
  102.6 8.2 %collective-permute-start.8 = (f32[1,128,2560]{1,2,0:T(8,128)}, f32[1,128,2560]{1,2,0:T(8,128)}, u32[]{:S(2)}, u32[]{:S(2)}) collective-permute-start(f32[1,128,2560]{1,2,0:T(8,128)} %add_select_fusion.11), channel_id=1, source_target_pairs={{8,12},{0,4},{24,28},{16,20}} | collective-permute-start | bytes 3932168 | tf_op jit(solution)/shard_map/ppermute | solution.py:107
  104.4 12.0 %copy-start.11 = (pred[128,128]{1,0:T(8,128)(4,1)}, pred[128,128]{1,0:T(8,128)(4,1)S(1)}, u32[]{:S(2)}) copy-start(pred[128,128]{1,0:T(8,128)(4,1)S(1)} %iota_compare_fusion) | copy-start | bytes 49156
  104.5 0.7 collective-permute-start.13
  105.2 0.8 collective-permute-start.14
  109.0 7.5 %copy-start.13 = (f32[40]{0:T(128)S(1)}, f32[40]{0:T(128)}, u32[]{:S(2)}) copy-start(f32[40]{0:T(128)} %param.11) | copy-start | bytes 484
  109.0 10.0 %collective-permute-start.19 = (f32[1,128,2560]{1,2,0:T(8,128)}, f32[1,128,2560]{1,2,0:T(8,128)}, u32[]{:S(2)}, u32[]{:S(2)}) collective-permute-start(f32[1,128,2560]{1,2,0:T(8,128)} %add_select_fusion.8), channel_id=1, source_target_pairs={{7,3},{15,11},{23,19},{31,27}} | collective-permute-start | bytes 3932168 | tf_op jit(solution)/shard_map/ppermute | solution.py:107
  114.6 9.8 %collective-permute-start.9 = (f32[1,128,2560]{1,2,0:T(8,128)}, f32[1,128,2560]{1,2,0:T(8,128)}, u32[]{:S(2)}, u32[]{:S(2)}) collective-permute-start(f32[1,128,2560]{1,2,0:T(8,128)} %add_select_fusion.10), channel_id=1, source_target_pairs={{12,14},{8,10},{4,6},{0,2},{28,30},{24,26},{20,22},{16,18}} | collective-permute-start | bytes 3932168 | tf_op jit(solution)/shard_map/ppermute | solution.py:107
  122.9 4.9 %copy-start.5 = (bf16[1,128,2560]{1,2,0:T(8,128)(2,1)S(1)}, bf16[1,128,2560]{1,2,0:T(8,128)(2,1)}, u32[]{:S(2)}) copy-start(bf16[1,128,2560]{1,2,0:T(8,128)(2,1)} %copy-done.4) | copy-start | bytes 1966084
  122.9 4.9 %copy-start.7 = (bf16[1,128,2560]{1,2,0:T(8,128)(2,1)S(1)}, bf16[1,128,2560]{1,2,0:T(8,128)(2,1)}, u32[]{:S(2)}) copy-start(bf16[1,128,2560]{1,2,0:T(8,128)(2,1)} %copy-done.6) | copy-start | bytes 1966084
  122.9 4.9 %copy-start.12 = (pred[128,128]{1,0:T(8,128)(4,1)S(1)}, pred[128,128]{1,0:T(8,128)(4,1)}, u32[]{:S(2)}) copy-start(pred[128,128]{1,0:T(8,128)(4,1)} %copy-done.11) | copy-start | bytes 49156
  122.9 50.2 %collective-permute-start.20 = (f32[1,128,2560]{1,2,0:T(8,128)}, f32[1,128,2560]{1,2,0:T(8,128)}, u32[]{:S(2)}, u32[]{:S(2)}) collective-permute-start(f32[1,128,2560]{1,2,0:T(8,128)} %add_select_fusion.7), channel_id=1, source_target_pairs={{3,1},{7,5},{11,9},{15,13},{19,17},{23,21},{27,25},{31,29}} | collective-permute-start | bytes 3932168 | tf_op jit(solution)/shard_map/ppermute | solution.py:107
  126.5 55.0 %collective-permute-start.10 = (f32[1,128,2560]{1,2,0:T(8,128)S(1)}, f32[1,128,2560]{1,2,0:T(8,128)}, u32[]{:S(2)}, u32[]{:S(2)}) collective-permute-start(f32[1,128,2560]{1,2,0:T(8,128)S(1)} %add_select_fusion.9), channel_id=1, source_target_pairs={{14,15},{12,13},{10,11},{8,9},{6,7},{4,5},{2,3},{0,1},{30,31},{28,... | collective-permute-start | bytes 3932168 | tf_op jit(solution)/shard_map/ppermute | solution.py:107
  176.2 13.1 %collective-permute-start.21 = (f32[1,128,2560]{1,2,0:T(8,128)}, f32[1,128,2560]{1,2,0:T(8,128)}, u32[]{:S(2)}, u32[]{:S(2)}) collective-permute-start(f32[1,128,2560]{1,2,0:T(8,128)} %add_select_fusion.6), channel_id=1, source_target_pairs={{1,0},{3,2},{5,4},{7,6},{9,8},{11,10},{13,12},{15,14},{17,16},{19,... | collective-permute-start | bytes 3932168 | tf_op jit(solution)/shard_map/ppermute | solution.py:107
  186.1 3.3 %copy-start.3 = (f32[1,128,2560]{1,2,0:T(8,128)S(1)}, f32[1,128,2560]{1,2,0:T(8,128)}, u32[]{:S(2)}) copy-start(f32[1,128,2560]{1,2,0:T(8,128)} %copy-done.2) | copy-start | bytes 3932164
  (4 other events, 5.8 us)

commit v3 on v2

--- a/solution.py
+++ b/solution.py
@@ -75,8 +75,29 @@
     )
 
 
-def sweep_scan(gains, state, position, count, reverse):
-    head_width = state.shape[-1] // gains.shape[-1]
+def xor_pairs(count, bit):
+    return [(i, i ^ (1 << bit)) for i in range(count)]
+
+
+def gather_totals(totals, skip_part, position, count):
+    rows = jnp.arange(count)[:, None]
+    table = jnp.concatenate([jnp.where(rows == position, totals[None, :], 0.0), skip_part[None, :]], 0)
+    tables = [table]
+    for bit in range(count.bit_length() - 1):
+        table = table + lax.ppermute(table, "ctx", xor_pairs(count, bit))
+        tables.append(table)
+    return tables
+
+
+def range_gain(table, count, low, high, reverse):
+    rows = jnp.arange(count)
+    virtual = count - 1 - rows if reverse else rows
+    inside = (virtual >= low) & (virtual <= high)
+    return jnp.exp(jnp.sum(jnp.where(inside[:, None], table[:count], 0.0), axis=0))
+
+
+def sweep_scan(tables, state, position, count, reverse):
+    head_width = state.shape[-1] // tables[0].shape[-1]
     level_count = count.bit_length() - 1
     index = count - 1 - position if reverse else position
 
@@ -85,31 +106,28 @@
             return [(count - 1 - a, count - 1 - b) for a, b in pairs]
         return pairs
 
-    def grow(gain, earlier, later):
-        return spread_heads(gain, head_width)[..., None, :] * earlier + later
+    def spread(gain):
+        return spread_heads(gain, head_width)[..., None, :]
 
-    total_gain, total_state = gains, state
+    total = state
     lowers = []
     for level in range(level_count):
         span = 1 << level
         pairs = [(i, i + span) for i in range(count) if i % (2 * span) == span - 1]
-        lower = lax.ppermute((total_gain, total_state), "ctx", mapped(pairs))
+        lower = lax.ppermute(total, "ctx", mapped(pairs))
         lowers.append(lower)
         if level < level_count - 1:
-            receives = index % (2 * span) == 2 * span - 1
-            total_state = jnp.where(receives, grow(total_gain, lower[1], total_state), total_state)
-            total_gain = jnp.where(receives, lower[0] * total_gain, total_gain)
+            upper_gain = range_gain(tables[level], count, index - span + 1, index, reverse)
+            total = spread(upper_gain) * lower + total
     prefix = jnp.zeros_like(state)
     for level in reversed(range(level_count)):
         span = 1 << level
         if level < level_count - 1:
             pairs = [(i, i - span) for i in range(count) if i % (2 * span) == 2 * span - 1]
-            sent = lax.ppermute(prefix, "ctx", mapped(pairs))
-            prefix = jnp.where(index % (2 * span) == span - 1, sent, prefix)
-        lower_gain, lower_state = lowers[level]
-        prefix = jnp.where(
-            index % (2 * span) == 2 * span - 1, grow(lower_gain, prefix, lower_state), prefix
-        )
+            prefix = prefix + lax.ppermute(prefix, "ctx", mapped(pairs))
+        lower_gain = range_gain(tables[-1], count, index - 2 * span + 1, index - span, reverse)
+        lower_gain = jnp.where(index % (2 * span) == 2 * span - 1, lower_gain, 1.0)
+        prefix = spread(lower_gain) * prefix + lowers[level]
     return prefix
 
 
@@ -120,13 +138,15 @@
     within, totals, value_scale, decayed_vals, decayed_cot, fwd_state, adj_state, skip_parts = prepare(
         token_values, cotangent, write_coeffs, read_coeffs, decay_codes
     )
-    grad_skip = lax.psum(jnp.sum(skip_parts, axis=0), ("dp", "ctx"))
-    grad_skip, fwd_state, adj_state = lax.optimization_barrier((grad_skip, fwd_state, adj_state))
-    block_gains = jnp.exp(totals)
     position = lax.axis_index("ctx")
     count = lax.axis_size("ctx")
-    carried_state = sweep_scan(block_gains, fwd_state, position, count, False)
-    carried_adjoint = sweep_scan(block_gains, adj_state, position, count, True)
+    tables = jax.vmap(gather_totals, (0, 0, None, None))(totals, skip_parts, position, count)
+    grad_skip = jnp.sum(tables[-1][:, count], axis=0)
+    for bit in range(lax.axis_size("dp").bit_length() - 1):
+        grad_skip = grad_skip + lax.ppermute(grad_skip, "dp", xor_pairs(lax.axis_size("dp"), bit))
+    scan = jax.vmap(sweep_scan, (0, 0, None, None, None))
+    carried_state = scan(tables, fwd_state, position, count, False)
+    carried_adjoint = scan(tables, adj_state, position, count, True)
     local_grads = jax.vmap(block_local_grads, (0, 0, 0, 0, 0, None))(
         token_values, cotangent, write_coeffs, read_coeffs, within, skip_gain
     )

time: 195 us -> 161 us (0.83)
  blocking collectives: 40.8 us -> 0 us
  other arithmetic: 36.3 us -> 45.1 us
  starting transfers between devices: 40.4 us -> 42.4 us
    psum x1 -> x0, blocking collectives: 40.8 us -> none  [local(): grad_skip = lax.psum(jnp.sum(skip_parts, axis=0), ('dp', 'ctx'))]
    add x0 -> x17, other arithmetic: none -> 38.8 us  [the longest x6 19 us: sweep_scan(): prefix = spread(lower_gain) * prefix + lowers[level]]
    select_n x16 -> x6, other arithmetic: 32.5 us -> 0.03 us  [sweep_scan(): lower_gain = jnp.where(index % (2 * span) == 2 * span - 1, lower_gain, 1.0)]
    ppermute x22 -> x19, starting transfers between devices: 40.4 us -> 42.4 us  [the longest x6 19.9 us: sweep_scan(): prefix = prefix + lax.ppermute(prefix, 'ctx', mapped(pairs))]
    unnamed x31 -> x27, local copies, waits for them, and re-layouts: 6.71 us -> 4.99 us
    ppermute x22 -> x19, waiting for transfers between devices: 53 us -> 51.4 us  [the longest x6 42.1 us: sweep_scan(): prefix = prefix + lax.ppermute(prefix, 'ctx', mapped(pairs))]
  transfers between devices with their start and end apart: 22 -> 19, of which waited for: 4 -> 4; matrix products, arithmetic and copies ran while one was open for 21% -> 34% of each run, Pallas kernels for 0% -> 0%
where the time goes in v3:
time: 161 us; the launch traced here: 159 us
  waiting for transfers between devices  51.4 us (32%)
  other arithmetic  45.1 us (28%)
  starting transfers between devices  42.4 us (26%)
  matrix products  12 us (7%)
  local copies, waits for them, and re-layouts  7.45 us (5%)
    ppermute x6, waiting for transfers between devices, sweep_scan(): prefix = prefix + lax.ppermute(prefix, 'ctx', mapped(pairs))  42.1 us
    ppermute x6, starting transfers between devices, sweep_scan(): prefix = prefix + lax.ppermute(prefix, 'ctx', mapped(pairs))  19.9 us
    add x6, other arithmetic, sweep_scan(): prefix = spread(lower_gain) * prefix + lowers[level]  19 us
    add x6, other arithmetic, sweep_scan(): total = spread(upper_gain) * lower + total  18.5 us
    ppermute x8, starting transfers between devices, sweep_scan(): lower = lax.ppermute(total, 'ctx', mapped(pairs))  17.7 us
    ppermute x8, waiting for transfers between devices, sweep_scan(): lower = lax.ppermute(total, 'ctx', mapped(pairs))  6.46 us
    unnamed x27, local copies, waits for them, and re-layouts  4.99 us
    ppermute x4, starting transfers between devices, gather_totals(): table = table + lax.ppermute(table, 'ctx', xor_pairs(count, bit))  3.65 us
  transfers between devices with their start and end apart: 19, of which 4 were waited for; matrix products, arithmetic and copies ran while one was open for 34% of the time, Pallas kernels for 0%

profile of v3, /device:TPU:1, one launch (start us, length us, event | category | flops | bytes accessed | tf_op | source)
XLA Modules:
  0.0 159.5 jit_solution(16592049618640317734)
XLA Ops:
  1.8 1.4 copy.43
  5.4 1.4 convolution_bitcast_fusion.2
  6.8 3.4 %collective-permute-start.4 = (f32[1,128,2560]{1,2,0:T(8,128)}, f32[1,128,2560]{1,2,0:T(8,128)}, u32[]{:S(2)}, u32[]{:S(2)}) collective-permute-start(f32[1,128,2560]{1,2,0:T(8,128)} %convolution_bitcast_fusion.2), channel_id=1, source_target_pairs={{15,14},{13,12},{11,10},{9,8},{7,6},{5,4},{3,2},{1,0},{31,30},{29,... | collective-permute-start | bytes 3932168 | tf_op jit(solution)/shard_map/vmap()/ppermute | solution.py:117
  13.4 2.2 %convert_reduce_fusion = bf16[128,128]{1,0:T(8,128)(2,1)S(1)} fusion(f32[40,128]{1,0:T(8,128)S(1)} %copy.41, pred[128,128]{1,0:T(8,128)(4,1)S(1)} %iota_compare_fusion, bf16[128,40,64]{0,2,1:T(8,128)(2,1)S(1)} %bitcast.98, bf16[128,40,64]{0,2,1:T(8,128)(2,1)} %bitcast.101), kind=kOutput, calls=%fused_computation.7 | convolution fusion | flops 88457216 | bytes 1380352 | tf_op jit(solution)/shard_map/vmap(ihp,jhp->hij)/dot_general | solution.py:45
  16.6 3.2 %multiply_add_fusion.9 = f32[1,128,2560]{1,2,0:T(8,128)} fusion(f32[1,128,2560]{1,2,0:T(8,128)} %convolution_bitcast_fusion.2, f32[1,128,2560]{1,2,0:T(8,128)} %collective-permute-done.4, f32[2560]{0:T(1024)S(1)} %broadcast_in_dim.268), kind=kLoop, calls=%fused_computation.30 | loop fusion | flops 655360 | bytes 3942400 | tf_op jit(solution)/shard_map/vmap()/add | solution.py:121
  19.8 1.8 %collective-permute-start.5 = (f32[1,128,2560]{1,2,0:T(8,128)}, f32[1,128,2560]{1,2,0:T(8,128)}, u32[]{:S(2)}, u32[]{:S(2)}) collective-permute-start(f32[1,128,2560]{1,2,0:T(8,128)} %multiply_add_fusion.9), channel_id=1, source_target_pairs={{14,12},{10,8},{6,4},{2,0},{30,28},{26,24},{22,20},{18,16}} | collective-permute-start | bytes 3932168 | tf_op jit(solution)/shard_map/vmap()/ppermute | solution.py:117
  22.3 2.8 %multiply_add_fusion.4 = f32[1,128,2560]{1,2,0:T(8,128)} fusion(f32[1,128,2560]{1,2,0:T(8,128)S(1)} %convolution_bitcast_fusion, f32[1,128,2560]{1,2,0:T(8,128)} %collective-permute-done.11, f32[2560]{0:T(1024)S(1)} %broadcast_in_dim.291), kind=kLoop, calls=%fused_computation.24 | loop fusion | flops 655360 | bytes 3942400 | tf_op jit(solution)/shard_map/vmap()/add | solution.py:121
  25.1 5.2 %collective-permute-start.12 = (f32[1,128,2560]{1,2,0:T(8,128)}, f32[1,128,2560]{1,2,0:T(8,128)}, u32[]{:S(2)}, u32[]{:S(2)}) collective-permute-start(f32[1,128,2560]{1,2,0:T(8,128)} %multiply_add_fusion.4), channel_id=1, source_target_pairs={{1,3},{5,7},{9,11},{13,15},{17,19},{21,23},{25,27},{29,31}} | collective-permute-start | bytes 3932168 | tf_op jit(solution)/shard_map/vmap()/ppermute | solution.py:117
  31.4 3.3 %multiply_add_fusion.8 = f32[1,128,2560]{1,2,0:T(8,128)} fusion(f32[1,128,2560]{1,2,0:T(8,128)} %multiply_add_fusion.9, f32[1,128,2560]{1,2,0:T(8,128)} %collective-permute-done.5, f32[2560]{0:T(1024)S(1)} %broadcast_in_dim.265), kind=kLoop, calls=%fused_computation.29 | loop fusion | flops 655360 | bytes 3942400 | tf_op jit(solution)/shard_map/vmap()/add | solution.py:121
  35.4 2.2 %fusion.4 = f32[1,128,40,64]{1,3,2,0:T(8,128)} fusion(bf16[128,40,64]{0,2,1:T(8,128)(2,1)S(1)} %bitcast.99, f32[40,128]{1,0:T(8,128)S(1)} %copy.41, f32[128,128]{1,0:T(8,128)S(1)} %copy-done.5, pred[128,128]{1,0:T(8,128)(4,1)S(1)} %copy-done.7, f32[40]{0:T(128)S(1)} %copy-done.11, bf16[1,128,40,64]{1,3,2,0:T(8,128)(2,1)S(1)} %bitcast.100), kind=kOutput, calls=%fused_computation.14 | convolution fusion | flops 88145920 | bytes 2724000 | tf_op jit(solution)/shard_map/vmap(hij,ihp->jhp)/dot_general | solution.py:51
  37.7 6.4 %collective-permute-done.12 = f32[1,128,2560]{1,2,0:T(8,128)} collective-permute-done((f32[1,128,2560]{1,2,0:T(8,128)}, f32[1,128,2560]{1,2,0:T(8,128)}, u32[]{:S(2)}, u32[]{:S(2)}) %collective-permute-start.12) | collective-permute-done | bytes 1310752 | tf_op jit(solution)/shard_map/vmap()/ppermute | solution.py:117
  44.1 3.2 %multiply_add_fusion.3 = f32[1,128,2560]{1,2,0:T(8,128)} fusion(f32[1,128,2560]{1,2,0:T(8,128)} %multiply_add_fusion.4, f32[1,128,2560]{1,2,0:T(8,128)} %collective-permute-done.12, f32[2560]{0:T(1024)S(1)} %broadcast_in_dim.288), kind=kLoop, calls=%fused_computation.23 | loop fusion | flops 655360 | bytes 3942400 | tf_op jit(solution)/shard_map/vmap()/add | solution.py:121
  47.3 1.7 %collective-permute-start.13 = (f32[1,128,2560]{1,2,0:T(8,128)}, f32[1,128,2560]{1,2,0:T(8,128)}, u32[]{:S(2)}, u32[]{:S(2)}) collective-permute-start(f32[1,128,2560]{1,2,0:T(8,128)} %multiply_add_fusion.3), channel_id=1, source_target_pairs={{3,7},{11,15},{19,23},{27,31}} | collective-permute-start | bytes 3932168 | tf_op jit(solution)/shard_map/vmap()/ppermute | solution.py:117
  49.3 2.8 %multiply_add_fusion.7 = f32[1,128,2560]{1,2,0:T(8,128)} fusion(f32[1,128,2560]{1,2,0:T(8,128)} %multiply_add_fusion.8, f32[1,128,2560]{1,2,0:T(8,128)S(1)} %collective-permute-done.6, f32[2560]{0:T(1024)S(1)} %broadcast_in_dim.262), kind=kLoop, calls=%fused_computation.28 | loop fusion | flops 655360 | bytes 3942400 | tf_op jit(solution)/shard_map/vmap()/add | solution.py:121
  52.2 1.7 %collective-permute-start.7 = (f32[1,128,2560]{1,2,0:T(8,128)}, f32[1,128,2560]{1,2,0:T(8,128)}, u32[]{:S(2)}, u32[]{:S(2)}) collective-permute-start(f32[1,128,2560]{1,2,0:T(8,128)} %multiply_add_fusion.7), channel_id=1, source_target_pairs={{8,0},{24,16}} | collective-permute-start | bytes 3932168 | tf_op jit(solution)/shard_map/vmap()/ppermute | solution.py:117
  55.2 1.7 %collective-permute-done.2 = f32[1,17,40]{2,1,0:T(8,128)S(1)} collective-permute-done((f32[1,17,40]{2,1,0:T(8,128)S(1)}, f32[1,17,40]{2,1,0:T(8,128)S(1)}, u32[]{:S(2)}, u32[]{:S(2)}) %collective-permute-start.2) | collective-permute-done | bytes 2752 | tf_op jit(solution)/shard_map/vmap()/ppermute | solution.py:87
  56.9 2.3 %collective-permute-start.3 = (f32[1,17,40]{2,1,0:T(8,128)S(1)}, f32[1,17,40]{2,1,0:T(8,128)S(1)}, u32[]{:S(2)}, u32[]{:S(2)}) collective-permute-start(f32[1,17,40]{2,1,0:T(8,128)S(1)} %add.180), channel_id=1, source_target_pairs={{0,8},{1,9},{2,10},{3,11},{4,12},{5,13},{6,14},{7,15},{8,0},{9,1},... | collective-permute-start | bytes 8168 | tf_op jit(solution)/shard_map/vmap()/ppermute | solution.py:87
  60.6 3.2 %multiply_add_fusion.2 = f32[1,128,2560]{1,2,0:T(8,128)} fusion(f32[1,128,2560]{1,2,0:T(8,128)} %multiply_add_fusion.3, f32[1,128,2560]{1,2,0:T(8,128)} %collective-permute-done.13, f32[2560]{0:T(1024)S(1)} %broadcast_in_dim.285), kind=kLoop, calls=%fused_computation.22 | loop fusion | flops 655360 | bytes 3942400 | tf_op jit(solution)/shard_map/vmap()/add | solution.py:121
  63.8 1.8 %collective-permute-start.14 = (f32[1,128,2560]{1,2,0:T(8,128)}, f32[1,128,2560]{1,2,0:T(8,128)}, u32[]{:S(2)}, u32[]{:S(2)}) collective-permute-start(f32[1,128,2560]{1,2,0:T(8,128)} %multiply_add_fusion.2), channel_id=1, source_target_pairs={{7,15},{23,31}} | collective-permute-start | bytes 3932168 | tf_op jit(solution)/shard_map/vmap()/ppermute | solution.py:117
  65.8 2.8 %broadcast_add_fusion.1 = f32[1,128,2560]{1,2,0:T(8,128)} fusion(f32[1,128,2560]{1,2,0:T(8,128)} %collective-permute-done.7, f32[2560]{0:T(1024)S(1)} %mul.193), kind=kLoop, calls=%fused_computation.50 | loop fusion | flops 327680 | bytes 2631680 | tf_op jit(solution)/shard_map/vmap()/add | solution.py:130
  68.6 1.7 %collective-permute-start.8 = (f32[1,128,2560]{1,2,0:T(8,128)}, f32[1,128,2560]{1,2,0:T(8,128)}, u32[]{:S(2)}, u32[]{:S(2)}) collective-permute-start(f32[1,128,2560]{1,2,0:T(8,128)} %broadcast_add_fusion.1), channel_id=1, source_target_pairs={{8,12},{0,4},{24,28},{16,20}} | collective-permute-start | bytes 3932168 | tf_op jit(solution)/shard_map/vmap()/ppermute | solution.py:127
  70.5 2.8 %broadcast_add_fusion = f32[1,128,2560]{1,2,0:T(8,128)} fusion(f32[1,128,2560]{1,2,0:T(8,128)} %collective-permute-done.14, f32[2560]{0:T(1024)S(1)} %mul.212), kind=kLoop, calls=%fused_computation.48 | loop fusion | flops 327680 | bytes 2631680 | tf_op jit(solution)/shard_map/vmap()/add | solution.py:130
  73.3 1.8 %collective-permute-start.15 = (f32[1,128,2560]{1,2,0:T(8,128)}, f32[1,128,2560]{1,2,0:T(8,128)}, u32[]{:S(2)}, u32[]{:S(2)}) collective-permute-start(f32[1,128,2560]{1,2,0:T(8,128)} %broadcast_add_fusion), channel_id=1, source_target_pairs={{7,3},{15,11},{23,19},{31,27}} | collective-permute-start | bytes 3932168 | tf_op jit(solution)/shard_map/vmap()/ppermute | solution.py:127
  75.2 3.7 %multiply_add_fusion.6 = f32[1,128,2560]{1,2,0:T(8,128)} fusion(f32[1,128,2560]{1,2,0:T(8,128)S(1)} %collective-permute-done.6, f32[1,128,2560]{1,2,0:T(8,128)} %collective-permute-done.8, f32[2560]{0:T(1024)S(1)} %broadcast_in_dim.257, f32[1,128,2560]{1,2,0:T(8,128)} %collective-permute-done.7, f32[2560]{0:T(1024)S(1)} %mul.193), kind=kLoop, calls=%fused_computation.27 | loop fusion | flops 1310720 | bytes 5263360 | tf_op jit(solution)/shard_map/vmap()/add | solution.py:130
  78.9 1.7 %collective-permute-start.9 = (f32[1,128,2560]{1,2,0:T(8,128)}, f32[1,128,2560]{1,2,0:T(8,128)}, u32[]{:S(2)}, u32[]{:S(2)}) collective-permute-start(f32[1,128,2560]{1,2,0:T(8,128)} %multiply_add_fusion.6), channel_id=1, source_target_pairs={{12,14},{8,10},{4,6},{0,2},{28,30},{24,26},{20,22},{16,18}} | collective-permute-start | bytes 3932168 | tf_op jit(solution)/shard_map/vmap()/ppermute | solution.py:127
  80.7 3.0 %multiply_add_fusion.1 = f32[1,128,2560]{1,2,0:T(8,128)S(1)} fusion(f32[1,128,2560]{1,2,0:T(8,128)} %collective-permute-done.13, f32[1,128,2560]{1,2,0:T(8,128)} %collective-permute-done.15, f32[2560]{0:T(1024)S(1)} %broadcast_in_dim.280, f32[1,128,2560]{1,2,0:T(8,128)} %collective-permute-done.14, f32[2560]{0:T(1024)S(1)} %mul.212), kind=kLoop, calls=%fused_computation.21 | loop fusion | flops 1310720 | bytes 5263360 | tf_op jit(solution)/shard_map/vmap()/add | solution.py:130
  85.2 3.6 %multiply_add_fusion.5 = f32[1,128,2560]{1,2,0:T(8,128)} fusion(f32[1,128,2560]{1,2,0:T(8,128)} %collective-permute-done.5, f32[1,128,2560]{1,2,0:T(8,128)} %multiply_add_fusion.6, f32[1,128,2560]{1,2,0:T(8,128)} %collective-permute-done.9, f32[2560]{0:T(1024)S(1)} %broadcast_in_dim.254), kind=kLoop, calls=%fused_computation.26 | loop fusion | flops 983040 | bytes 5253120 | tf_op jit(solution)/shard_map/vmap()/add | solution.py:130
  91.8 42.1 %collective-permute-done.16 = f32[1,128,2560]{1,2,0:T(8,128)} collective-permute-done((f32[1,128,2560]{1,2,0:T(8,128)S(1)}, f32[1,128,2560]{1,2,0:T(8,128)}, u32[]{:S(2)}, u32[]{:S(2)}) %collective-permute-start.16) | collective-permute-done | bytes 1310752 | tf_op jit(solution)/shard_map/vmap()/ppermute | solution.py:127
  133.9 3.2 %multiply_add_fusion = f32[1,128,2560]{1,2,0:T(8,128)} fusion(f32[1,128,2560]{1,2,0:T(8,128)} %collective-permute-done.12, f32[1,128,2560]{1,2,0:T(8,128)S(1)} %multiply_add_fusion.1, f32[1,128,2560]{1,2,0:T(8,128)} %collective-permute-done.16, f32[2560]{0:T(1024)S(1)} %broadcast_in_dim.277), kind=kLoop, calls=%fused_computation.20 | loop fusion | flops 983040 | bytes 5253120 | tf_op jit(solution)/shard_map/vmap()/add | solution.py:130
  137.1 12.1 %collective-permute-start.17 = (f32[1,128,2560]{1,2,0:T(8,128)}, f32[1,128,2560]{1,2,0:T(8,128)}, u32[]{:S(2)}, u32[]{:S(2)}) collective-permute-start(f32[1,128,2560]{1,2,0:T(8,128)} %multiply_add_fusion), channel_id=1, source_target_pairs={{1,0},{3,2},{5,4},{7,6},{9,8},{11,10},{13,12},{15,14},{17,16},{19,... | collective-permute-start | bytes 3932168 | tf_op jit(solution)/shard_map/vmap()/ppermute | solution.py:127
  149.7 2.5 %fusion.17 = bf16[128,2560]{0,1:T(8,128)(2,1)S(1)} fusion(f32[1,128,2560]{1,2,0:T(8,128)} %collective-permute-done.4, f32[1,128,2560]{1,2,0:T(8,128)} %multiply_add_fusion.5, f32[1,128,2560]{1,2,0:T(8,128)} %collective-permute-done.10, f32[2560]{0:T(1024)S(1)} %broadcast_in_dim.251), kind=kLoop, calls=%fused_computation.42 | loop fusion | flops 1310720 | bytes 4597760 | tf_op jit(solution)/shard_map/reshape.59
  156.0 3.5 %fusion.15 = bf16[1,128,128]{2,1,0:T(8,128)(2,1)} fusion(f32[128,128]{1,0:T(8,128)S(1)} %fusion.26, f32[1,128,2560]{1,2,0:T(8,128)} %collective-permute-done.11, f32[1,128,2560]{1,2,0:T(8,128)} %multiply_add_fusion, f32[1,128,2560]{1,2,0:T(8,128)} %collective-permute-done.17, bf16[1,128,2560]{1,2,0:T(8,128)(2,1)S(1)} %get-tuple-element.36, ...), kind=kOutput, calls=%fused_computation.40 | convolution fusion | flops 85229568 | bytes 4696064 | tf_op jit(solution)/shard_map/vmap(iq,nq->in)/dot_general | solution.py:63
  (129 shorter events, 22.2 us)
Async XLA Ops:
  0.6 9.6 %copy-start = (bf16[1,128,128]{2,1,0:T(8,128)(2,1)S(1)}, bf16[1,128,128]{2,1,0:T(8,128)(2,1)}, u32[]{:S(2)}) copy-start(bf16[1,128,128]{2,1,0:T(8,128)(2,1)} %param.8) | copy-start | bytes 98308
  0.6 2.6 %copy-start.3 = (bf16[1,128,2560]{2,1,0:T(8,128)(2,1)S(1)}, bf16[1,128,2560]{2,1,0:T(8,128)(2,1)}, u32[]{:S(2)}) copy-start(bf16[1,128,2560]{2,1,0:T(8,128)(2,1)} %param.6) | copy-start | bytes 1966084
  3.6 0.8 copy-start.1
  3.7 1.7 %copy-start.4 = (bf16[1,128,128]{2,1,0:T(8,128)(2,1)S(1)}, bf16[1,128,128]{2,1,0:T(8,128)(2,1)}, u32[]{:S(2)}) copy-start(bf16[1,128,128]{2,1,0:T(8,128)(2,1)} %param.9) | copy-start | bytes 98308
  5.3 25.0 %collective-permute-start = (f32[1,17,40]{2,1,0:T(8,128)}, f32[1,17,40]{2,1,0:T(8,128)}, u32[]{:S(2)}, u32[]{:S(2)}) collective-permute-start(f32[1,17,40]{2,1,0:T(8,128)} %pad_maximum_fusion), channel_id=1, source_target_pairs={{0,1},{1,0},{2,3},{3,2},{4,5},{5,4},{6,7},{7,6},{8,9},{9,8},{10,11... | collective-permute-start | bytes 8168 | tf_op jit(solution)/shard_map/vmap()/ppermute | solution.py:87
  6.8 9.8 %collective-permute-start.4 = (f32[1,128,2560]{1,2,0:T(8,128)}, f32[1,128,2560]{1,2,0:T(8,128)}, u32[]{:S(2)}, u32[]{:S(2)}) collective-permute-start(f32[1,128,2560]{1,2,0:T(8,128)} %convolution_bitcast_fusion.2), channel_id=1, source_target_pairs={{15,14},{13,12},{11,10},{9,8},{7,6},{5,4},{3,2},{1,0},{31,30},{29,... | collective-permute-start | bytes 3932168 | tf_op jit(solution)/shard_map/vmap()/ppermute | solution.py:117
  10.6 11.8 %collective-permute-start.11 = (f32[1,128,2560]{1,2,0:T(8,128)S(1)}, f32[1,128,2560]{1,2,0:T(8,128)}, u32[]{:S(2)}, u32[]{:S(2)}) collective-permute-start(f32[1,128,2560]{1,2,0:T(8,128)S(1)} %convolution_bitcast_fusion), channel_id=1, source_target_pairs={{0,1},{2,3},{4,5},{6,7},{8,9},{10,11},{12,13},{14,15},{16,17},{18,... | collective-permute-start | bytes 3932168 | tf_op jit(solution)/shard_map/vmap()/ppermute | solution.py:117
  12.8 0.6 copy-start.6
  19.8 11.5 %collective-permute-start.5 = (f32[1,128,2560]{1,2,0:T(8,128)}, f32[1,128,2560]{1,2,0:T(8,128)}, u32[]{:S(2)}, u32[]{:S(2)}) collective-permute-start(f32[1,128,2560]{1,2,0:T(8,128)} %multiply_add_fusion.9), channel_id=1, source_target_pairs={{14,12},{10,8},{6,4},{2,0},{30,28},{26,24},{22,20},{18,16}} | collective-permute-start | bytes 3932168 | tf_op jit(solution)/shard_map/vmap()/ppermute | solution.py:117
  25.1 19.0 %collective-permute-start.12 = (f32[1,128,2560]{1,2,0:T(8,128)}, f32[1,128,2560]{1,2,0:T(8,128)}, u32[]{:S(2)}, u32[]{:S(2)}) collective-permute-start(f32[1,128,2560]{1,2,0:T(8,128)} %multiply_add_fusion.4), channel_id=1, source_target_pairs={{1,3},{5,7},{9,11},{13,15},{17,19},{21,23},{25,27},{29,31}} | collective-permute-start | bytes 3932168 | tf_op jit(solution)/shard_map/vmap()/ppermute | solution.py:117
  31.3 4.0 %copy-start.5 = (f32[128,128]{1,0:T(8,128)S(1)}, f32[128,128]{1,0:T(8,128)}, u32[]{:S(2)}) copy-start(f32[128,128]{1,0:T(8,128)} %fusion.29) | copy-start | bytes 196612
  31.3 4.0 %copy-start.7 = (pred[128,128]{1,0:T(8,128)(4,1)S(1)}, pred[128,128]{1,0:T(8,128)(4,1)}, u32[]{:S(2)}) copy-start(pred[128,128]{1,0:T(8,128)(4,1)} %copy-done.6) | copy-start | bytes 49156
  31.3 4.0 %copy-start.11 = (f32[40]{0:T(128)S(1)}, f32[40]{0:T(128)}, u32[]{:S(2)}) copy-start(f32[40]{0:T(128)} %param.11) | copy-start | bytes 484
  34.6 14.7 %collective-permute-start.6 = (f32[1,128,2560]{1,2,0:T(8,128)}, f32[1,128,2560]{1,2,0:T(8,128)S(1)}, u32[]{:S(2)}, u32[]{:S(2)}) collective-permute-start(f32[1,128,2560]{1,2,0:T(8,128)} %multiply_add_fusion.8), channel_id=1, source_target_pairs={{12,8},{4,0},{28,24},{20,16}} | collective-permute-start | bytes 3932168 | tf_op jit(solution)/shard_map/vmap()/ppermute | solution.py:117
  37.5 11.5 %collective-permute-start.1 = (f32[1,17,40]{2,1,0:T(8,128)S(1)}, f32[1,17,40]{2,1,0:T(8,128)S(1)}, u32[]{:S(2)}, u32[]{:S(2)}) collective-permute-start(f32[1,17,40]{2,1,0:T(8,128)S(1)} %fusion.41), channel_id=1, source_target_pairs={{0,2},{1,3},{2,0},{3,1},{4,6},{5,7},{6,4},{7,5},{8,10},{9,11},{10,... | collective-permute-start | bytes 8168 | tf_op jit(solution)/shard_map/vmap()/ppermute | solution.py:87
  37.7 11.4 %copy-start.9 = (pred[16]{0:T(512)(128)(4,1)S(1)}, pred[16]{0:T(512)(128)(4,1)}, u32[]{:S(2)}) copy-start(pred[16]{0:T(512)(128)(4,1)} %get-tuple-element.44) | copy-start | bytes 52
  37.7 11.4 %copy-start.10 = (pred[16]{0:T(512)(128)(4,1)S(1)}, pred[16]{0:T(512)(128)(4,1)}, u32[]{:S(2)}) copy-start(pred[16]{0:T(512)(128)(4,1)} %get-tuple-element.45) | copy-start | bytes 52
  47.3 13.3 %collective-permute-start.13 = (f32[1,128,2560]{1,2,0:T(8,128)}, f32[1,128,2560]{1,2,0:T(8,128)}, u32[]{:S(2)}, u32[]{:S(2)}) collective-permute-start(f32[1,128,2560]{1,2,0:T(8,128)} %multiply_add_fusion.3), channel_id=1, source_target_pairs={{3,7},{11,15},{19,23},{27,31}} | collective-permute-start | bytes 3932168 | tf_op jit(solution)/shard_map/vmap()/ppermute | solution.py:117
  49.3 11.2 %copy-start.8 = (pred[16]{0:T(512)(128)(4,1)S(1)}, pred[16]{0:T(512)(128)(4,1)}, u32[]{:S(2)}) copy-start(pred[16]{0:T(512)(128)(4,1)} %get-tuple-element.49) | copy-start | bytes 52
  52.2 13.6 %collective-permute-start.7 = (f32[1,128,2560]{1,2,0:T(8,128)}, f32[1,128,2560]{1,2,0:T(8,128)}, u32[]{:S(2)}, u32[]{:S(2)}) collective-permute-start(f32[1,128,2560]{1,2,0:T(8,128)} %multiply_add_fusion.7), channel_id=1, source_target_pairs={{8,0},{24,16}} | collective-permute-start | bytes 3932168 | tf_op jit(solution)/shard_map/vmap()/ppermute | solution.py:117
  53.9 3.0 %collective-permute-start.2 = (f32[1,17,40]{2,1,0:T(8,128)S(1)}, f32[1,17,40]{2,1,0:T(8,128)S(1)}, u32[]{:S(2)}, u32[]{:S(2)}) collective-permute-start(f32[1,17,40]{2,1,0:T(8,128)S(1)} %add.179), channel_id=1, source_target_pairs={{0,4},{1,5},{2,6},{3,7},{4,0},{5,1},{6,2},{7,3},{8,12},{9,13},{10,... | collective-permute-start | bytes 8168 | tf_op jit(solution)/shard_map/vmap()/ppermute | solution.py:87
  56.9 3.6 %collective-permute-start.3 = (f32[1,17,40]{2,1,0:T(8,128)S(1)}, f32[1,17,40]{2,1,0:T(8,128)S(1)}, u32[]{:S(2)}, u32[]{:S(2)}) collective-permute-start(f32[1,17,40]{2,1,0:T(8,128)S(1)} %add.180), channel_id=1, source_target_pairs={{0,8},{1,9},{2,10},{3,11},{4,12},{5,13},{6,14},{7,15},{8,0},{9,1},... | collective-permute-start | bytes 8168 | tf_op jit(solution)/shard_map/vmap()/ppermute | solution.py:87
  63.8 6.7 %collective-permute-start.14 = (f32[1,128,2560]{1,2,0:T(8,128)}, f32[1,128,2560]{1,2,0:T(8,128)}, u32[]{:S(2)}, u32[]{:S(2)}) collective-permute-start(f32[1,128,2560]{1,2,0:T(8,128)} %multiply_add_fusion.2), channel_id=1, source_target_pairs={{7,15},{23,31}} | collective-permute-start | bytes 3932168 | tf_op jit(solution)/shard_map/vmap()/ppermute | solution.py:117
  68.6 6.6 %collective-permute-start.8 = (f32[1,128,2560]{1,2,0:T(8,128)}, f32[1,128,2560]{1,2,0:T(8,128)}, u32[]{:S(2)}, u32[]{:S(2)}) collective-permute-start(f32[1,128,2560]{1,2,0:T(8,128)} %broadcast_add_fusion.1), channel_id=1, source_target_pairs={{8,12},{0,4},{24,28},{16,20}} | collective-permute-start | bytes 3932168 | tf_op jit(solution)/shard_map/vmap()/ppermute | solution.py:127
  73.3 7.5 %collective-permute-start.15 = (f32[1,128,2560]{1,2,0:T(8,128)}, f32[1,128,2560]{1,2,0:T(8,128)}, u32[]{:S(2)}, u32[]{:S(2)}) collective-permute-start(f32[1,128,2560]{1,2,0:T(8,128)} %broadcast_add_fusion), channel_id=1, source_target_pairs={{7,3},{15,11},{23,19},{31,27}} | collective-permute-start | bytes 3932168 | tf_op jit(solution)/shard_map/vmap()/ppermute | solution.py:127
  78.9 6.3 %collective-permute-start.9 = (f32[1,128,2560]{1,2,0:T(8,128)}, f32[1,128,2560]{1,2,0:T(8,128)}, u32[]{:S(2)}, u32[]{:S(2)}) collective-permute-start(f32[1,128,2560]{1,2,0:T(8,128)} %multiply_add_fusion.6), channel_id=1, source_target_pairs={{12,14},{8,10},{4,6},{0,2},{28,30},{24,26},{20,22},{16,18}} | collective-permute-start | bytes 3932168 | tf_op jit(solution)/shard_map/vmap()/ppermute | solution.py:127
  83.7 50.1 %collective-permute-start.16 = (f32[1,128,2560]{1,2,0:T(8,128)S(1)}, f32[1,128,2560]{1,2,0:T(8,128)}, u32[]{:S(2)}, u32[]{:S(2)}) collective-permute-start(f32[1,128,2560]{1,2,0:T(8,128)S(1)} %multiply_add_fusion.1), channel_id=1, source_target_pairs={{3,1},{7,5},{11,9},{15,13},{19,17},{23,21},{27,25},{31,29}} | collective-permute-start | bytes 3932168 | tf_op jit(solution)/shard_map/vmap()/ppermute | solution.py:127
  88.8 60.9 %collective-permute-start.10 = (f32[1,128,2560]{1,2,0:T(8,128)}, f32[1,128,2560]{1,2,0:T(8,128)}, u32[]{:S(2)}, u32[]{:S(2)}) collective-permute-start(f32[1,128,2560]{1,2,0:T(8,128)} %multiply_add_fusion.5), channel_id=1, source_target_pairs={{14,15},{12,13},{10,11},{8,9},{6,7},{4,5},{2,3},{0,1},{30,31},{28,... | collective-permute-start | bytes 3932168 | tf_op jit(solution)/shard_map/vmap()/ppermute | solution.py:127
  90.4 58.8 %collective-permute-start.18 = (f32[40]{0:T(128)S(1)}, f32[40]{0:T(128)S(1)}, u32[]{:S(2)}, u32[]{:S(2)}) collective-permute-start(f32[40]{0:T(128)S(1)} %slice_bitcast_fusion), channel_id=1, source_target_pairs={{0,16},{16,0},{1,17},{17,1},{2,18},{18,2},{3,19},{19,3},{4,20},{20... | collective-permute-start | bytes 488 | tf_op jit(solution)/shard_map/ppermute | solution.py:146
  137.1 18.9 %collective-permute-start.17 = (f32[1,128,2560]{1,2,0:T(8,128)}, f32[1,128,2560]{1,2,0:T(8,128)}, u32[]{:S(2)}, u32[]{:S(2)}) collective-permute-start(f32[1,128,2560]{1,2,0:T(8,128)} %multiply_add_fusion), channel_id=1, source_target_pairs={{1,0},{3,2},{5,4},{7,6},{9,8},{11,10},{13,12},{15,14},{17,16},{19,... | collective-permute-start | bytes 3932168 | tf_op jit(solution)/shard_map/vmap()/ppermute | solution.py:127
  152.2 1.3 copy-start.2

commit v4 on v3

--- a/solution.py
+++ b/solution.py
@@ -96,39 +96,90 @@
     return jnp.exp(jnp.sum(jnp.where(inside[:, None], table[:count], 0.0), axis=0))
 
 
-def sweep_scan(tables, state, position, count, reverse):
-    head_width = state.shape[-1] // tables[0].shape[-1]
-    level_count = count.bit_length() - 1
-    index = count - 1 - position if reverse else position
-
-    def mapped(pairs):
-        if reverse:
-            return [(count - 1 - a, count - 1 - b) for a, b in pairs]
+def take_half(array, upper):
+    half = array.shape[-1] // 2
+    return jnp.where(upper, array[..., half:], array[..., :half])
+
+
+def join_halves(mine, other, upper):
+    return jnp.where(upper, jnp.concatenate([other, mine], -1), jnp.concatenate([mine, other], -1))
+
+
+class Direction:
+    def __init__(self, tables, position, count, reverse, head_width):
+        self.tables = tables
+        self.count = count
+        self.reverse = reverse
+        self.head_width = head_width
+        self.index = count - 1 - position if reverse else position
+        self.upper = self.index % 2 == 1
+        self.pair = self.index // 2
+
+    def actual(self, pairs):
+        if self.reverse:
+            return [(self.count - 1 - a, self.count - 1 - b) for a, b in pairs]
         return pairs
 
-    def spread(gain):
-        return spread_heads(gain, head_width)[..., None, :]
-
-    total = state
+    def pair_pairs(self, pairs):
+        return self.actual([(2 * a + j, 2 * b + j) for a, b in pairs for j in (0, 1)])
+
+    def gain(self, table_index, low_block, high_block):
+        full = range_gain(self.tables[table_index], self.count, low_block, high_block, self.reverse)
+        return spread_heads(take_half(full, self.upper), self.head_width)[..., None, :]
+
+
+def pair_scan(way, pair_total):
+    pair_count = way.count // 2
+    level_count = pair_count.bit_length() - 1
+    low_tables = lambda level: min(level + 1, len(way.tables) - 1)
+    total = pair_total
     lowers = []
     for level in range(level_count):
         span = 1 << level
-        pairs = [(i, i + span) for i in range(count) if i % (2 * span) == span - 1]
-        lower = lax.ppermute(total, "ctx", mapped(pairs))
+        pairs = [(a, a + span) for a in range(pair_count) if a % (2 * span) == span - 1]
+        lower = lax.ppermute(total, "ctx", way.pair_pairs(pairs))
         lowers.append(lower)
         if level < level_count - 1:
-            upper_gain = range_gain(tables[level], count, index - span + 1, index, reverse)
-            total = spread(upper_gain) * lower + total
-    prefix = jnp.zeros_like(state)
+            first = 2 * (way.pair - span + 1)
+            total = way.gain(low_tables(level), first, 2 * way.pair + 1) * lower + total
+    prefix = jnp.zeros_like(pair_total)
     for level in reversed(range(level_count)):
         span = 1 << level
         if level < level_count - 1:
-            pairs = [(i, i - span) for i in range(count) if i % (2 * span) == 2 * span - 1]
-            prefix = prefix + lax.ppermute(prefix, "ctx", mapped(pairs))
-        lower_gain = range_gain(tables[-1], count, index - 2 * span + 1, index - span, reverse)
-        lower_gain = jnp.where(index % (2 * span) == 2 * span - 1, lower_gain, 1.0)
-        prefix = spread(lower_gain) * prefix + lowers[level]
+            pairs = [(a, a - span) for a in range(pair_count) if a % (2 * span) == 2 * span - 1]
+            prefix = prefix + lax.ppermute(prefix, "ctx", way.pair_pairs(pairs))
+        first = 2 * (way.pair - 2 * span + 1)
+        lower_gain = way.gain(-1, first, 2 * (way.pair - span) + 1)
+        lower_gain = jnp.where(way.pair % (2 * span) == 2 * span - 1, lower_gain, 1.0)
+        prefix = lower_gain * prefix + lowers[level]
     return prefix
+
+
+def carried_pair(tables, fwd_state, adj_state, position, count, head_width):
+    ways = [Direction(tables, position, count, reverse, head_width) for reverse in (False, True)]
+    states = [fwd_state, adj_state]
+    sent = jnp.concatenate([take_half(s, ~w.upper) for s, w in zip(states, ways)], -1)
+    got = lax.ppermute(sent, "ctx", [(i, i ^ 1) for i in range(count)])
+    got = [got[..., : got.shape[-1] // 2], got[..., got.shape[-1] // 2 :]]
+    lifted_parts = []
+    keep_parts = []
+    for way, state, other in zip(ways, states, got):
+        own = take_half(state, way.upper)
+        low_block = jnp.where(way.upper, other, own)
+        high_block = jnp.where(way.upper, own, other)
+        pair_total = way.gain(1, 2 * way.pair + 1, 2 * way.pair + 1) * low_block + high_block
+        pair_prefix = pair_scan(way, pair_total)
+        lifted = way.gain(1, 2 * way.pair, 2 * way.pair) * pair_prefix + low_block
+        lifted_parts.append(jnp.where(way.upper, pair_prefix, lifted))
+        keep_parts.append(jnp.where(way.upper, lifted, pair_prefix))
+    got = lax.ppermute(jnp.concatenate(lifted_parts, -1), "ctx", [(i, i ^ 1) for i in range(count)])
+    unit = jnp.exp(jnp.min(tables[-1]) * 0.0)
+    got = got * unit
+    half = got.shape[-1] // 2
+    results = []
+    for way, mine, other in zip(ways, keep_parts, [got[..., :half], got[..., half:]]):
+        results.append(join_halves(mine, other, way.upper))
+    return results
 
 
 def local(token_values, cotangent, write_coeffs, read_coeffs, decay_codes, skip_gain):
@@ -144,9 +195,10 @@
     grad_skip = jnp.sum(tables[-1][:, count], axis=0)
     for bit in range(lax.axis_size("dp").bit_length() - 1):
         grad_skip = grad_skip + lax.ppermute(grad_skip, "dp", xor_pairs(lax.axis_size("dp"), bit))
-    scan = jax.vmap(sweep_scan, (0, 0, None, None, None))
-    carried_state = scan(tables, fwd_state, position, count, False)
-    carried_adjoint = scan(tables, adj_state, position, count, True)
+    head_width = token_values.shape[2] // decay_codes.shape[2]
+    carried_state, carried_adjoint = jax.vmap(carried_pair, (0, 0, 0, None, None, None))(
+        tables, fwd_state, adj_state, position, count, head_width
+    )
     local_grads = jax.vmap(block_local_grads, (0, 0, 0, 0, 0, None))(
         token_values, cotangent, write_coeffs, read_coeffs, within, skip_gain
     )

time: 161 us -> 130 us (0.81)
  other arithmetic: 45.1 us -> 32.4 us
  waiting for transfers between devices: 51.4 us -> 41.2 us
  starting transfers between devices: 42.4 us -> 34.5 us
  matrix products: 12 us -> 8.49 us
    add x12 -> x9, other arithmetic: 37.5 us -> 12.1 us  [the longest x4 5.99 us: pair_scan(): prefix = lower_gain * prefix + lowers[level]]
    ppermute x14 -> x12, starting transfers between devices: 37.6 us -> 27.1 us  [the longest x4 11.7 us: pair_scan(): prefix = prefix + lax.ppermute(prefix, 'ctx', way.pair_pairs(pairs))]
    ppermute x14 -> x12, waiting for transfers between devices: 48.6 us -> 38.4 us  [the longest x6 31.5 us: pair_scan(): lower = lax.ppermute(total, 'ctx', way.pair_pairs(pairs))]
    concatenate x0 -> x4, other arithmetic: none -> 5 us  [the longest x2 2.69 us: join_halves(): jnp.concatenate([other, mine], -1)]
    select_n x6 -> x12, other arithmetic: 0.03 us -> 4.49 us  [the longest x5 1.54 us: take_half(): return jnp.where(upper, array[..., half:], array[..., :half])]
    and x8 -> x14, other arithmetic: 1.2 us -> 4.4 us  [range_gain(): inside = (virtual >= low) & (virtual <= high)]
    ppermute x4, starting transfers between devices: 3.65 us -> 6.21 us  [gather_totals(): table = table + lax.ppermute(table, 'ctx', xor_pairs(count, bit))]
    another operation x1 -> x0, other arithmetic: 2.51 us -> none
  transfers between devices with their start and end apart: 19 -> 17, of which waited for: 4 -> 10; matrix products, arithmetic and copies ran while one was open for 34% -> 26% of each run, Pallas kernels for 0% -> 0%
where the time goes in v4:
time: 130 us; the launch traced here: 128 us
  waiting for transfers between devices  41.2 us (32%)
  starting transfers between devices  34.5 us (27%)
  other arithmetic  32.4 us (25%)
  local copies, waits for them, and re-layouts  9.04 us (7%)
  matrix products  8.49 us (7%)
  between operations  1.94 us (1%)
    ppermute x6, waiting for transfers between devices, pair_scan(): lower = lax.ppermute(total, 'ctx', way.pair_pairs(pairs))  31.5 us
    ppermute x4, starting transfers between devices, pair_scan(): prefix = prefix + lax.ppermute(prefix, 'ctx', way.pair_pairs(pairs))  11.7 us
    ppermute x1, starting transfers between devices, carried_pair(): lax.ppermute(jnp.concatenate(lifted_parts, -1), 'ctx', [(i, i ^ 1) for i...  7.55 us
    ppermute x6, starting transfers between devices, pair_scan(): lower = lax.ppermute(total, 'ctx', way.pair_pairs(pairs))  7.49 us
    ppermute x4, waiting for transfers between devices, pair_scan(): prefix = prefix + lax.ppermute(prefix, 'ctx', way.pair_pairs(pairs))  6.93 us
    ppermute x4, starting transfers between devices, gather_totals(): table = table + lax.ppermute(table, 'ctx', xor_pairs(count, bit))  6.21 us
    add x4, other arithmetic, pair_scan(): prefix = lower_gain * prefix + lowers[level]  5.99 us
    unnamed x67, local copies, waits for them, and re-layouts  5.34 us
  transfers between devices with their start and end apart: 17, of which 10 were waited for; matrix products, arithmetic and copies ran while one was open for 26% of the time, Pallas kernels for 0%

profile of v4, /device:TPU:1, one launch (start us, length us, event | category | flops | bytes accessed | tf_op | source)
XLA Modules:
  0.0 127.6 jit_solution(642141628615511818)
XLA Ops:
  1.8 1.4 %copy.43 = bf16[1,128,2560]{1,2,0:T(8,128)(2,1)S(1)} copy(bf16[1,128,2560]{2,1,0:T(8,128)(2,1)} %param.7) | data formatting | bytes 1310720 | tf_op args[1]
  12.4 2.2 %convert_reduce_fusion = bf16[128,128]{1,0:T(8,128)(2,1)S(1)} fusion(f32[40,128]{1,0:T(8,128)S(1)} %copy.41, pred[128,128]{1,0:T(8,128)(4,1)S(1)} %iota_compare_fusion, bf16[128,40,64]{0,2,1:T(8,128)(2,1)S(1)} %bitcast.155, bf16[128,40,64]{0,2,1:T(8,128)(2,1)} %bitcast.158), kind=kOutput, calls=%fused_computation.7 | convolution fusion | flops 88457216 | bytes 1380352 | tf_op jit(solution)/shard_map/vmap(ihp,jhp->hij)/dot_general | solution.py:45
  14.9 2.4 %collective-permute-start.1 = (f32[1,17,40]{2,1,0:T(8,128)S(1)}, f32[1,17,40]{2,1,0:T(8,128)S(1)}, u32[]{:S(2)}, u32[]{:S(2)}) collective-permute-start(f32[1,17,40]{2,1,0:T(8,128)S(1)} %fusion.58), channel_id=1, source_target_pairs={{0,2},{1,3},{2,0},{3,1},{4,6},{5,7},{6,4},{7,5},{8,10},{9,11},{10,... | collective-permute-start | bytes 8168 | tf_op jit(solution)/shard_map/vmap()/ppermute | solution.py:87
  20.2 1.3 %collective-permute-start.2 = (f32[1,17,40]{2,1,0:T(8,128)S(1)}, f32[1,17,40]{2,1,0:T(8,128)S(1)}, u32[]{:S(2)}, u32[]{:S(2)}) collective-permute-start(f32[1,17,40]{2,1,0:T(8,128)S(1)} %add.194), channel_id=1, source_target_pairs={{0,4},{1,5},{2,6},{3,7},{4,0},{5,1},{6,2},{7,3},{8,12},{9,13},{10,... | collective-permute-start | bytes 8168 | tf_op jit(solution)/shard_map/vmap()/ppermute | solution.py:87
  22.8 2.3 %collective-permute-start.3 = (f32[1,17,40]{2,1,0:T(8,128)S(1)}, f32[1,17,40]{2,1,0:T(8,128)S(1)}, u32[]{:S(2)}, u32[]{:S(2)}) collective-permute-start(f32[1,17,40]{2,1,0:T(8,128)S(1)} %add.195), channel_id=1, source_target_pairs={{0,8},{1,9},{2,10},{3,11},{4,12},{5,13},{6,14},{7,15},{8,0},{9,1},... | collective-permute-start | bytes 8168 | tf_op jit(solution)/shard_map/vmap()/ppermute | solution.py:87
  26.8 1.4 %select_reduce_fusion.13 = (f32[40]{0:T(128)S(1)}, f32[40]{0:T(128)S(1)}, f32[40]{0:T(128)S(1)}, f32[40]{0:T(128)}, f32[40]{0:T(128)}, /*index=5*/f32[40]{0:T(128)}) fusion(f32[1,17,40]{2,1,0:T(8,128)S(1)} %get-tuple-element.37, pred[16]{0:T(512)(128)(4,1)} %compare_and_fusion.9, pred[16]{0:T(512)(128)(4,1)S(1)} %compare_and_fusion.8, ...), kind=kLoop, calls=%fused_computation.97 | loop fusion | flops 7440 | bytes 3616 | tf_op jit(solution)/shard_map/vmap()/reduce_sum | solution.py:96
  28.4 3.0 %select_add_fusion.1 = (f32[1,128,1280]{1,2,0:T(8,128)}, f32[1,128,1280]{1,2,0:T(8,128)}, f32[1,128,1280]{1,2,0:T(8,128)}, f32[1,128,1280]{1,2,0:T(8,128)S(1)}) fusion(f32[1,128,2560]{1,2,0:T(8,128)} %collective-permute-done.4, f32[1280]{0:T(1024)S(1)} %broadcast_in_dim.254, pred[]{:T(512)S(6)} %eq.44, f32[1,128,2560]{1,2,0:T(8,128)S(1)} %convolution_bitcast_fusion.2, ...), kind=kLoop, calls=%fused_computation.58 | loop fusion | flops 1638400 | bytes 6563842 | tf_op jit(solution)/shard_map/vmap()/add | solution.py:170
  31.4 2.2 %collective-permute-start.5 = (f32[1,128,1280]{1,2,0:T(8,128)}, f32[1,128,1280]{1,2,0:T(8,128)S(1)}, u32[]{:S(2)}, u32[]{:S(2)}) collective-permute-start(f32[1,128,1280]{1,2,0:T(8,128)} %get-tuple-element.38), channel_id=1, source_target_pairs={{0,2},{1,3},{4,6},{5,7},{8,10},{9,11},{12,14},{13,15},{16,18},{17,... | collective-permute-start | bytes 1966088 | tf_op jit(solution)/shard_map/vmap()/ppermute | solution.py:140
  36.0 1.3 %collective-permute-start.10 = (f32[1,128,1280]{1,2,0:T(8,128)}, f32[1,128,1280]{1,2,0:T(8,128)S(1)}, u32[]{:S(2)}, u32[]{:S(2)}) collective-permute-start(f32[1,128,1280]{1,2,0:T(8,128)} %get-tuple-element.44), channel_id=1, source_target_pairs={{15,13},{14,12},{11,9},{10,8},{7,5},{6,4},{3,1},{2,0},{31,29},{30,... | collective-permute-start | bytes 1966088 | tf_op jit(solution)/shard_map/vmap()/ppermute | solution.py:140
  37.2 7.4 %collective-permute-done.5 = f32[1,128,1280]{1,2,0:T(8,128)S(1)} collective-permute-done((f32[1,128,1280]{1,2,0:T(8,128)}, f32[1,128,1280]{1,2,0:T(8,128)S(1)}, u32[]{:S(2)}, u32[]{:S(2)}) %collective-permute-start.5) | collective-permute-done | bytes 655392 | tf_op jit(solution)/shard_map/vmap()/ppermute | solution.py:140
  44.6 1.6 %multiply_add_fusion.9 = f32[1,128,1280]{1,2,0:T(8,128)S(1)} fusion(f32[1,128,1280]{1,2,0:T(8,128)} %get-tuple-element.38, f32[1,128,1280]{1,2,0:T(8,128)S(1)} %collective-permute-done.5, f32[1280]{0:T(1024)S(1)} %broadcast_in_dim.251), kind=kLoop, calls=%fused_computation.57 | loop fusion | flops 327680 | bytes 1971200 | tf_op jit(solution)/shard_map/vmap()/add | solution.py:144
  47.5 3.2 %collective-permute-done.10 = f32[1,128,1280]{1,2,0:T(8,128)S(1)} collective-permute-done((f32[1,128,1280]{1,2,0:T(8,128)}, f32[1,128,1280]{1,2,0:T(8,128)S(1)}, u32[]{:S(2)}, u32[]{:S(2)}) %collective-permute-start.10) | collective-permute-done | bytes 655392 | tf_op jit(solution)/shard_map/vmap()/ppermute | solution.py:140
  50.9 1.3 %collective-permute-start.11 = (f32[1,128,1280]{1,2,0:T(8,128)S(1)}, f32[1,128,1280]{1,2,0:T(8,128)S(1)}, u32[]{:S(2)}, u32[]{:S(2)}) collective-permute-start(f32[1,128,1280]{1,2,0:T(8,128)S(1)} %multiply_add_fusion.4), channel_id=1, source_target_pairs={{13,9},{12,8},{5,1},{4,0},{29,25},{28,24},{21,17},{20,16}} | collective-permute-start | bytes 1966088 | tf_op jit(solution)/shard_map/vmap()/ppermute | solution.py:140
  53.2 11.3 %collective-permute-done.11 = f32[1,128,1280]{1,2,0:T(8,128)S(1)} collective-permute-done((f32[1,128,1280]{1,2,0:T(8,128)S(1)}, f32[1,128,1280]{1,2,0:T(8,128)S(1)}, u32[]{:S(2)}, u32[]{:S(2)}) %collective-permute-start.11) | collective-permute-done | bytes 655392 | tf_op jit(solution)/shard_map/vmap()/ppermute | solution.py:140
  65.6 1.3 %collective-permute-start.12 = (f32[1,128,1280]{1,2,0:T(8,128)}, f32[1,128,1280]{1,2,0:T(8,128)S(1)}, u32[]{:S(2)}, u32[]{:S(2)}) collective-permute-start(f32[1,128,1280]{1,2,0:T(8,128)} %multiply_add_fusion.3), channel_id=1, source_target_pairs={{9,1},{8,0},{25,17},{24,16}} | collective-permute-start | bytes 1966088 | tf_op jit(solution)/shard_map/vmap()/ppermute | solution.py:140
  68.0 1.5 %collective-permute-start.8 = (f32[1,128,1280]{1,2,0:T(8,128)}, f32[1,128,1280]{1,2,0:T(8,128)}, u32[]{:S(2)}, u32[]{:S(2)}) collective-permute-start(f32[1,128,1280]{1,2,0:T(8,128)} %broadcast_add_fusion.1), channel_id=1, source_target_pairs={{6,2},{7,3},{14,10},{15,11},{22,18},{23,19},{30,26},{31,27}} | collective-permute-start | bytes 1966088 | tf_op jit(solution)/shard_map/vmap()/ppermute | solution.py:150
  69.7 9.7 %collective-permute-done.12 = f32[1,128,1280]{1,2,0:T(8,128)S(1)} collective-permute-done((f32[1,128,1280]{1,2,0:T(8,128)}, f32[1,128,1280]{1,2,0:T(8,128)S(1)}, u32[]{:S(2)}, u32[]{:S(2)}) %collective-permute-start.12) | collective-permute-done | bytes 655392 | tf_op jit(solution)/shard_map/vmap()/ppermute | solution.py:140
  80.4 2.3 %collective-permute-start.13 = (f32[1,128,1280]{1,2,0:T(8,128)}, f32[1,128,1280]{1,2,0:T(8,128)}, u32[]{:S(2)}, u32[]{:S(2)}) collective-permute-start(f32[1,128,1280]{1,2,0:T(8,128)} %broadcast_add_fusion), channel_id=1, source_target_pairs={{9,13},{8,12},{1,5},{0,4},{25,29},{24,28},{17,21},{16,20}} | collective-permute-start | bytes 1966088 | tf_op jit(solution)/shard_map/vmap()/ppermute | solution.py:150
  82.7 2.3 %multiply_add_fusion.7 = f32[1,128,1280]{1,2,0:T(8,128)} fusion(f32[1,128,1280]{1,2,0:T(8,128)S(1)} %collective-permute-done.6, f32[1,128,1280]{1,2,0:T(8,128)} %collective-permute-done.8, f32[1280]{0:T(1024)S(1)} %select_n.395, f32[1,128,1280]{1,2,0:T(8,128)S(1)} %collective-permute-done.7, f32[1280]{0:T(1024)S(1)} %mul.268), kind=kLoop, calls=%fused_computation.55 | loop fusion | flops 655360 | bytes 2631680 | tf_op jit(solution)/shard_map/vmap()/add | solution.py:154
  85.1 1.3 %collective-permute-start.9 = (f32[1,128,1280]{1,2,0:T(8,128)}, f32[1,128,1280]{1,2,0:T(8,128)}, u32[]{:S(2)}, u32[]{:S(2)}) collective-permute-start(f32[1,128,1280]{1,2,0:T(8,128)} %multiply_add_fusion.7), channel_id=1, source_target_pairs={{2,0},{3,1},{6,4},{7,5},{10,8},{11,9},{14,12},{15,13},{18,16},{19,... | collective-permute-start | bytes 1966088 | tf_op jit(solution)/shard_map/vmap()/ppermute | solution.py:150
  87.9 2.2 %collective-permute-done.13 = f32[1,128,1280]{1,2,0:T(8,128)} collective-permute-done((f32[1,128,1280]{1,2,0:T(8,128)}, f32[1,128,1280]{1,2,0:T(8,128)}, u32[]{:S(2)}, u32[]{:S(2)}) %collective-permute-start.13) | collective-permute-done | bytes 655392 | tf_op jit(solution)/shard_map/vmap()/ppermute | solution.py:150
  90.1 1.5 %multiply_add_fusion.2 = f32[1,128,1280]{1,2,0:T(8,128)S(1)} fusion(f32[1,128,1280]{1,2,0:T(8,128)S(1)} %collective-permute-done.11, f32[1,128,1280]{1,2,0:T(8,128)} %collective-permute-done.13, f32[1280]{0:T(1024)S(1)} %select_n.437, f32[1,128,1280]{1,2,0:T(8,128)S(1)} %collective-permute-done.12, f32[1280]{0:T(1024)S(1)} %mul.292), kind=kLoop, calls=%fused_computation.48 | loop fusion | flops 655360 | bytes 2631680 | tf_op jit(solution)/shard_map/vmap()/add | solution.py:154
  91.6 6.6 %collective-permute-start.14 = (f32[1,128,1280]{1,2,0:T(8,128)S(1)}, f32[1,128,1280]{1,2,0:T(8,128)S(1)}, u32[]{:S(2)}, u32[]{:S(2)}) collective-permute-start(f32[1,128,1280]{1,2,0:T(8,128)S(1)} %multiply_add_fusion.2), channel_id=1, source_target_pairs={{13,15},{12,14},{9,11},{8,10},{5,7},{4,6},{1,3},{0,2},{29,31},{28,... | collective-permute-start | bytes 1966088 | tf_op jit(solution)/shard_map/vmap()/ppermute | solution.py:150
  98.2 2.7 %collective-permute-done.9 = f32[1,128,1280]{1,2,0:T(8,128)} collective-permute-done((f32[1,128,1280]{1,2,0:T(8,128)}, f32[1,128,1280]{1,2,0:T(8,128)}, u32[]{:S(2)}, u32[]{:S(2)}) %collective-permute-start.9) | collective-permute-done | bytes 655392 | tf_op jit(solution)/shard_map/vmap()/ppermute | solution.py:150
  100.8 2.5 %select_bitcast_fusion = (bf16[128,1280]{0,1:T(8,128)(2,1)}, f32[1,128,1280]{1,2,0:T(8,128)S(1)}) fusion(f32[1,128,1280]{1,2,0:T(8,128)S(1)} %copy-done.1, f32[1280]{0:T(1024)S(1)} %broadcast_in_dim.260, pred[]{:T(512)S(6)} %eq.44, f32[1,128,1280]{1,2,0:T(8,128)S(1)} %copy-done.14, f32[1,128,1280]{1,2,0:T(8,128)} %multiply_add_fusion.7, ...), kind=kLoop, calls=%fused_computation.42 | loop fusion | flops 983040 | bytes 3614721 | tf_op jit(solution)/shard_map/vmap()/concatenate | solution.py:105
  103.5 2.1 %collective-permute-done.14 = f32[1,128,1280]{1,2,0:T(8,128)S(1)} collective-permute-done((f32[1,128,1280]{1,2,0:T(8,128)S(1)}, f32[1,128,1280]{1,2,0:T(8,128)S(1)}, u32[]{:S(2)}, u32[]{:S(2)}) %collective-permute-start.14) | collective-permute-done | bytes 655392 | tf_op jit(solution)/shard_map/vmap()/ppermute | solution.py:150
  105.6 1.3 fusion.23
  108.1 7.6 %collective-permute-start.15 = (f32[1,128,2560]{1,2,0:T(8,128)}, f32[1,128,2560]{1,2,0:T(8,128)}, u32[]{:S(2)}, u32[]{:S(2)}) collective-permute-start(f32[1,128,2560]{1,2,0:T(8,128)} %pad_maximum_fusion.1), channel_id=1, source_target_pairs={{0,1},{1,0},{2,3},{3,2},{4,5},{5,4},{6,7},{7,6},{8,9},{9,8},{10,11... | collective-permute-start | bytes 3932168 | tf_op jit(solution)/shard_map/vmap()/ppermute | solution.py:175
  115.8 2.2 %fusion.4 = f32[1,128,40,64]{1,3,2,0:T(8,128)} fusion(bf16[128,40,64]{0,2,1:T(8,128)(2,1)S(1)} %bitcast.156, f32[40,128]{1,0:T(8,128)S(1)} %copy-done.22, f32[128,128]{1,0:T(8,128)S(1)} %fusion.31, pred[128,128]{1,0:T(8,128)(4,1)S(1)} %iota_compare_fusion, f32[40]{0:T(128)S(1)} %copy-done.31, bf16[1,128,40,64]{1,3,2,0:T(8,128)(2,1)S(1)} %bitcast.157), kind=kOutput, calls=%fused_computation.14 | convolution fusion | flops 88145920 | bytes 2724000 | tf_op jit(solution)/shard_map/vmap(hij,ihp->jhp)/dot_general | solution.py:51
  118.0 1.2 collective-permute-start.16
  121.2 1.5 %broadcast_multiply_fusion = bf16[1,128,2560]{1,2,0:T(8,128)(2,1)S(1)} fusion(f32[1,128,2560]{1,2,0:T(8,128)} %collective-permute-done.15, f32[]{:T(128)S(6)} %exp.249), kind=kLoop, calls=%fused_computation.44 | loop fusion | flops 655360 | bytes 1966084 | tf_op jit(solution)/shard_map/vmap()/mul | solution.py:177
  123.8 1.2 copy-done.16
  (184 shorter events, 32.6 us)
Async XLA Ops:
  4.7 10.2 %collective-permute-start = (f32[1,17,40]{2,1,0:T(8,128)S(1)}, f32[1,17,40]{2,1,0:T(8,128)S(1)}, u32[]{:S(2)}, u32[]{:S(2)}) collective-permute-start(f32[1,17,40]{2,1,0:T(8,128)S(1)} %pad_maximum_fusion.2), channel_id=1, source_target_pairs={{0,1},{1,0},{2,3},{3,2},{4,5},{5,4},{6,7},{7,6},{8,9},{9,8},{10,11... | collective-permute-start | bytes 8168 | tf_op jit(solution)/shard_map/vmap()/ppermute | solution.py:87
  5.7 6.6 %copy-start.7 = (bf16[1,128,2560]{1,2,0:T(8,128)(2,1)S(1)}, bf16[1,128,2560]{1,2,0:T(8,128)(2,1)}, u32[]{:S(2)}) copy-start(bf16[1,128,2560]{1,2,0:T(8,128)(2,1)} %copy-done.6) | copy-start | bytes 1966084
  6.9 21.5 %collective-permute-start.4 = (f32[1,128,2560]{1,2,0:T(8,128)}, f32[1,128,2560]{1,2,0:T(8,128)}, u32[]{:S(2)}, u32[]{:S(2)}) collective-permute-start(f32[1,128,2560]{1,2,0:T(8,128)} %pad_maximum_fusion), channel_id=1, source_target_pairs={{0,1},{1,0},{2,3},{3,2},{4,5},{5,4},{6,7},{7,6},{8,9},{9,8},{10,11... | collective-permute-start | bytes 3932168 | tf_op jit(solution)/shard_map/vmap()/ppermute | solution.py:162
  12.4 5.0 %copy-start.28 = (pred[16]{0:T(512)(128)(4,1)S(1)}, pred[16]{0:T(512)(128)(4,1)}, u32[]{:S(2)}) copy-start(pred[16]{0:T(512)(128)(4,1)} %compare_and_fusion.12) | copy-start | bytes 52
  12.4 5.0 %copy-start.29 = (pred[16]{0:T(512)(128)(4,1)S(1)}, pred[16]{0:T(512)(128)(4,1)}, u32[]{:S(2)}) copy-start(pred[16]{0:T(512)(128)(4,1)} %compare_and_fusion.1) | copy-start | bytes 52
  14.9 5.2 %collective-permute-start.1 = (f32[1,17,40]{2,1,0:T(8,128)S(1)}, f32[1,17,40]{2,1,0:T(8,128)S(1)}, u32[]{:S(2)}, u32[]{:S(2)}) collective-permute-start(f32[1,17,40]{2,1,0:T(8,128)S(1)} %fusion.58), channel_id=1, source_target_pairs={{0,2},{1,3},{2,0},{3,1},{4,6},{5,7},{6,4},{7,5},{8,10},{9,11},{10,... | collective-permute-start | bytes 8168 | tf_op jit(solution)/shard_map/vmap()/ppermute | solution.py:87
  20.2 2.6 %collective-permute-start.2 = (f32[1,17,40]{2,1,0:T(8,128)S(1)}, f32[1,17,40]{2,1,0:T(8,128)S(1)}, u32[]{:S(2)}, u32[]{:S(2)}) collective-permute-start(f32[1,17,40]{2,1,0:T(8,128)S(1)} %add.194), channel_id=1, source_target_pairs={{0,4},{1,5},{2,6},{3,7},{4,0},{5,1},{6,2},{7,3},{8,12},{9,13},{10,... | collective-permute-start | bytes 8168 | tf_op jit(solution)/shard_map/vmap()/ppermute | solution.py:87
  22.8 3.4 %collective-permute-start.3 = (f32[1,17,40]{2,1,0:T(8,128)S(1)}, f32[1,17,40]{2,1,0:T(8,128)S(1)}, u32[]{:S(2)}, u32[]{:S(2)}) collective-permute-start(f32[1,17,40]{2,1,0:T(8,128)S(1)} %add.195), channel_id=1, source_target_pairs={{0,8},{1,9},{2,10},{3,11},{4,12},{5,13},{6,14},{7,15},{8,0},{9,1},... | collective-permute-start | bytes 8168 | tf_op jit(solution)/shard_map/vmap()/ppermute | solution.py:87
  31.4 19.2 %copy-start.15 = (f32[1,128,1280]{1,2,0:T(8,128)S(1)}, f32[1,128,1280]{1,2,0:T(8,128)}, u32[]{:S(2)}) copy-start(f32[1,128,1280]{1,2,0:T(8,128)} %get-tuple-element.44) | copy-start | bytes 1966084
  31.4 13.2 %collective-permute-start.5 = (f32[1,128,1280]{1,2,0:T(8,128)}, f32[1,128,1280]{1,2,0:T(8,128)S(1)}, u32[]{:S(2)}, u32[]{:S(2)}) collective-permute-start(f32[1,128,1280]{1,2,0:T(8,128)} %get-tuple-element.38), channel_id=1, source_target_pairs={{0,2},{1,3},{4,6},{5,7},{8,10},{9,11},{12,14},{13,15},{16,18},{17,... | collective-permute-start | bytes 1966088 | tf_op jit(solution)/shard_map/vmap()/ppermute | solution.py:140
  36.0 14.7 %collective-permute-start.10 = (f32[1,128,1280]{1,2,0:T(8,128)}, f32[1,128,1280]{1,2,0:T(8,128)S(1)}, u32[]{:S(2)}, u32[]{:S(2)}) collective-permute-start(f32[1,128,1280]{1,2,0:T(8,128)} %get-tuple-element.44), channel_id=1, source_target_pairs={{15,13},{14,12},{11,9},{10,8},{7,5},{6,4},{3,1},{2,0},{31,29},{30,... | collective-permute-start | bytes 1966088 | tf_op jit(solution)/shard_map/vmap()/ppermute | solution.py:140
  44.6 6.0 %copy-start.13 = (f32[1,128,1280]{1,2,0:T(8,128)}, f32[1,128,1280]{1,2,0:T(8,128)S(1)}, u32[]{:S(2)}) copy-start(f32[1,128,1280]{1,2,0:T(8,128)S(1)} %collective-permute-done.5) | copy-start | bytes 1966084
  46.2 6.0 %collective-permute-start.6 = (f32[1,128,1280]{1,2,0:T(8,128)S(1)}, f32[1,128,1280]{1,2,0:T(8,128)S(1)}, u32[]{:S(2)}, u32[]{:S(2)}) collective-permute-start(f32[1,128,1280]{1,2,0:T(8,128)S(1)} %multiply_add_fusion.9), channel_id=1, source_target_pairs={{2,6},{3,7},{10,14},{11,15},{18,22},{19,23},{26,30},{27,31}} | collective-permute-start | bytes 1966088 | tf_op jit(solution)/shard_map/vmap()/ppermute | solution.py:140
  50.9 13.6 %collective-permute-start.11 = (f32[1,128,1280]{1,2,0:T(8,128)S(1)}, f32[1,128,1280]{1,2,0:T(8,128)S(1)}, u32[]{:S(2)}, u32[]{:S(2)}) collective-permute-start(f32[1,128,1280]{1,2,0:T(8,128)S(1)} %multiply_add_fusion.4), channel_id=1, source_target_pairs={{13,9},{12,8},{5,1},{4,0},{29,25},{28,24},{21,17},{20,16}} | collective-permute-start | bytes 1966088 | tf_op jit(solution)/shard_map/vmap()/ppermute | solution.py:140
  52.5 14.4 %collective-permute-start.7 = (f32[1,128,1280]{1,2,0:T(8,128)S(1)}, f32[1,128,1280]{1,2,0:T(8,128)S(1)}, u32[]{:S(2)}, u32[]{:S(2)}) collective-permute-start(f32[1,128,1280]{1,2,0:T(8,128)S(1)} %multiply_add_fusion.8), channel_id=1, source_target_pairs={{6,14},{7,15},{22,30},{23,31}} | collective-permute-start | bytes 1966088 | tf_op jit(solution)/shard_map/vmap()/ppermute | solution.py:140
  65.6 13.8 %collective-permute-start.12 = (f32[1,128,1280]{1,2,0:T(8,128)}, f32[1,128,1280]{1,2,0:T(8,128)S(1)}, u32[]{:S(2)}, u32[]{:S(2)}) collective-permute-start(f32[1,128,1280]{1,2,0:T(8,128)} %multiply_add_fusion.3), channel_id=1, source_target_pairs={{9,1},{8,0},{25,17},{24,16}} | collective-permute-start | bytes 1966088 | tf_op jit(solution)/shard_map/vmap()/ppermute | solution.py:140
  68.0 14.8 %collective-permute-start.8 = (f32[1,128,1280]{1,2,0:T(8,128)}, f32[1,128,1280]{1,2,0:T(8,128)}, u32[]{:S(2)}, u32[]{:S(2)}) collective-permute-start(f32[1,128,1280]{1,2,0:T(8,128)} %broadcast_add_fusion.1), channel_id=1, source_target_pairs={{6,2},{7,3},{14,10},{15,11},{22,18},{23,19},{30,26},{31,27}} | collective-permute-start | bytes 1966088 | tf_op jit(solution)/shard_map/vmap()/ppermute | solution.py:150
  80.4 6.8 %copy-start.23 = (f32[20]{0:T(128)S(1)}, f32[20]{0:T(128)}, u32[]{:S(2)}) copy-start(f32[20]{0:T(128)} %get-tuple-element.62) | copy-start | bytes 244
  80.4 6.9 %copy-start.24 = (f32[20]{0:T(128)S(1)}, f32[20]{0:T(128)}, u32[]{:S(2)}) copy-start(f32[20]{0:T(128)} %get-tuple-element.56) | copy-start | bytes 244
  80.4 7.0 %copy-start.25 = (f32[20]{0:T(128)S(1)}, f32[20]{0:T(128)}, u32[]{:S(2)}) copy-start(f32[20]{0:T(128)} %get-tuple-element.59) | copy-start | bytes 244
  80.4 7.3 %copy-start.26 = (f32[20]{0:T(128)S(1)}, f32[20]{0:T(128)}, u32[]{:S(2)}) copy-start(f32[20]{0:T(128)} %get-tuple-element.53) | copy-start | bytes 244
  80.4 9.6 %collective-permute-start.13 = (f32[1,128,1280]{1,2,0:T(8,128)}, f32[1,128,1280]{1,2,0:T(8,128)}, u32[]{:S(2)}, u32[]{:S(2)}) collective-permute-start(f32[1,128,1280]{1,2,0:T(8,128)} %broadcast_add_fusion), channel_id=1, source_target_pairs={{9,13},{8,12},{1,5},{0,4},{25,29},{24,28},{17,21},{16,20}} | collective-permute-start | bytes 1966088 | tf_op jit(solution)/shard_map/vmap()/ppermute | solution.py:150
  85.1 15.8 %collective-permute-start.9 = (f32[1,128,1280]{1,2,0:T(8,128)}, f32[1,128,1280]{1,2,0:T(8,128)}, u32[]{:S(2)}, u32[]{:S(2)}) collective-permute-start(f32[1,128,1280]{1,2,0:T(8,128)} %multiply_add_fusion.7), channel_id=1, source_target_pairs={{2,0},{3,1},{6,4},{7,5},{10,8},{11,9},{14,12},{15,13},{18,16},{19,... | collective-permute-start | bytes 1966088 | tf_op jit(solution)/shard_map/vmap()/ppermute | solution.py:150
  87.9 12.9 %copy-start.1 = (f32[1,128,1280]{1,2,0:T(8,128)S(1)}, f32[1,128,1280]{1,2,0:T(8,128)}, u32[]{:S(2)}) copy-start(f32[1,128,1280]{1,2,0:T(8,128)} %get-tuple-element.39) | copy-start | bytes 1966084
  87.9 12.9 %copy-start.14 = (f32[1,128,1280]{1,2,0:T(8,128)S(1)}, f32[1,128,1280]{1,2,0:T(8,128)}, u32[]{:S(2)}) copy-start(f32[1,128,1280]{1,2,0:T(8,128)} %copy-done.13) | copy-start | bytes 1966084
  91.6 14.1 %collective-permute-start.14 = (f32[1,128,1280]{1,2,0:T(8,128)S(1)}, f32[1,128,1280]{1,2,0:T(8,128)S(1)}, u32[]{:S(2)}, u32[]{:S(2)}) collective-permute-start(f32[1,128,1280]{1,2,0:T(8,128)S(1)} %multiply_add_fusion.2), channel_id=1, source_target_pairs={{13,15},{12,14},{9,11},{8,10},{5,7},{4,6},{1,3},{0,2},{29,31},{28,... | collective-permute-start | bytes 1966088 | tf_op jit(solution)/shard_map/vmap()/ppermute | solution.py:150
  106.9 8.8 %copy-start.8 = (bf16[1,128,2560]{1,2,0:T(8,128)(2,1)S(1)}, bf16[1,128,2560]{1,2,0:T(8,128)(2,1)}, u32[]{:S(2)}) copy-start(bf16[1,128,2560]{1,2,0:T(8,128)(2,1)} %copy-done.6) | copy-start | bytes 1966084
  106.9 8.9 %copy-start.22 = (f32[40,128]{1,0:T(8,128)S(1)}, f32[40,128]{1,0:T(8,128)}, u32[]{:S(2)}) copy-start(f32[40,128]{1,0:T(8,128)} %copy-done.21) | copy-start | bytes 61444
  106.9 8.9 %copy-start.31 = (f32[40]{0:T(128)S(1)}, f32[40]{0:T(128)}, u32[]{:S(2)}) copy-start(f32[40]{0:T(128)} %param.11) | copy-start | bytes 484
  108.1 13.1 %collective-permute-start.15 = (f32[1,128,2560]{1,2,0:T(8,128)}, f32[1,128,2560]{1,2,0:T(8,128)}, u32[]{:S(2)}, u32[]{:S(2)}) collective-permute-start(f32[1,128,2560]{1,2,0:T(8,128)} %pad_maximum_fusion.1), channel_id=1, source_target_pairs={{0,1},{1,0},{2,3},{3,2},{4,5},{5,4},{6,7},{7,6},{8,9},{9,8},{10,11... | collective-permute-start | bytes 3932168 | tf_op jit(solution)/shard_map/vmap()/ppermute | solution.py:175
  115.8 5.1 %copy-start.10 = (f32[1,128,1280]{1,2,0:T(8,128)S(1)}, f32[1,128,1280]{1,2,0:T(8,128)}, u32[]{:S(2)}) copy-start(f32[1,128,1280]{1,2,0:T(8,128)} %get-tuple-element.41) | copy-start | bytes 1966084
  118.0 2.4 %collective-permute-start.16 = (f32[40]{0:T(128)S(1)}, f32[40]{0:T(128)S(1)}, u32[]{:S(2)}, u32[]{:S(2)}) collective-permute-start(f32[40]{0:T(128)S(1)} %slice_bitcast_fusion.2), channel_id=1, source_target_pairs={{0,16},{16,0},{1,17},{17,1},{2,18},{18,2},{3,19},{19,3},{4,20},{20... | collective-permute-start | bytes 488 | tf_op jit(solution)/shard_map/ppermute | solution.py:197
  (17 other events, 30.6 us)

commit v5 on v4

--- a/solution.py
+++ b/solution.py
@@ -131,26 +131,56 @@
 def pair_scan(way, pair_total):
     pair_count = way.count // 2
     level_count = pair_count.bit_length() - 1
-    low_tables = lambda level: min(level + 1, len(way.tables) - 1)
+    flip = level_count >= 2
+    last_table = len(way.tables) - 1
+    table_at = lambda level: min(level + 2, last_table)
+    pair = way.pair
+    role = jnp.where(way.upper, pair ^ 1, pair) if flip else pair
+
+    def device_pairs(pairs, first_level):
+        lower = [(2 * a, 2 * b) for a, b in pairs]
+        if flip and first_level:
+            upper = [(2 * b + 1, 2 * a + 1) for a, b in pairs]
+        elif flip:
+            upper = [(2 * (a ^ 1) + 1, 2 * (b ^ 1) + 1) for a, b in pairs]
+        else:
+            upper = [(2 * a + 1, 2 * b + 1) for a, b in pairs]
+        return way.actual(lower + upper)
+
+    def pair_gain(level, low_pair, high_pair):
+        return way.gain(table_at(level), 2 * low_pair, 2 * high_pair + 1)
+
     total = pair_total
     lowers = []
     for level in range(level_count):
         span = 1 << level
         pairs = [(a, a + span) for a in range(pair_count) if a % (2 * span) == span - 1]
-        lower = lax.ppermute(total, "ctx", way.pair_pairs(pairs))
+        lower = lax.ppermute(total, "ctx", device_pairs(pairs, level == 0))
         lowers.append(lower)
         if level < level_count - 1:
-            first = 2 * (way.pair - span + 1)
-            total = way.gain(low_tables(level), first, 2 * way.pair + 1) * lower + total
+            if flip and level == 0:
+                kept_upper = pair_gain(0, pair ^ 1, pair ^ 1) * total + lower
+                kept_lower = pair_gain(0, pair, pair) * lower + total
+                total = jnp.where(way.upper, kept_upper, kept_lower)
+            else:
+                total = pair_gain(level, role - span + 1, role) * lower + total
     prefix = jnp.zeros_like(pair_total)
     for level in reversed(range(level_count)):
         span = 1 << level
+        if flip and level == 0:
+            sent = jnp.where(way.upper, pair_gain(0, pair, pair) * prefix + pair_total, prefix)
+            pairs = [(2 * (a + 1), 2 * a) for a in range(0, pair_count, 2)]
+            pairs += [(2 * a + 1, 2 * (a + 1) + 1) for a in range(0, pair_count, 2)]
+            got = lax.ppermute(sent, "ctx", way.actual(pairs))
+            grown = pair_gain(level_count, pair - 1, pair - 1) * prefix + lowers[0]
+            odd = pair % 2 == 1
+            prefix = jnp.where(way.upper, jnp.where(odd, got, prefix), jnp.where(odd, grown, got))
+            continue
         if level < level_count - 1:
             pairs = [(a, a - span) for a in range(pair_count) if a % (2 * span) == 2 * span - 1]
-            prefix = prefix + lax.ppermute(prefix, "ctx", way.pair_pairs(pairs))
-        first = 2 * (way.pair - 2 * span + 1)
-        lower_gain = way.gain(-1, first, 2 * (way.pair - span) + 1)
-        lower_gain = jnp.where(way.pair % (2 * span) == 2 * span - 1, lower_gain, 1.0)
+            prefix = prefix + lax.ppermute(prefix, "ctx", device_pairs(pairs, False))
+        lower_gain = pair_gain(level_count, role - 2 * span + 1, role - span)
+        lower_gain = jnp.where(role % (2 * span) == 2 * span - 1, lower_gain, 1.0)
         prefix = lower_gain * prefix + lowers[level]
     return prefix
 

time: 130 us -> 120 us (0.923)
  other arithmetic: 32.4 us -> 23.6 us
    select_n x4 -> x6, other arithmetic: 1.37 us -> 6.77 us  [the longest x2 4.72 us: pair_scan(): jnp.where(way.upper, pair_gain(0, pair, pair) * prefix + pair_total, prefix)]
    add x4 -> x2, other arithmetic: 5.99 us -> 1.32 us  [pair_scan(): prefix = lower_gain * prefix + lowers[level]]
    and x14 -> x16, other arithmetic: 4.4 us -> 0.64 us  [range_gain(): inside = (virtual >= low) & (virtual <= high)]
    ppermute x10, starting transfers between devices: 19.1 us -> 16.3 us  [the longest x6 9.28 us: pair_scan(): lower = lax.ppermute(total, 'ctx', device_pairs(pairs, level == 0))]
    add x4 -> x2, other arithmetic: 3.11 us -> 0.47 us  [pair_scan(): total = pair_gain(level, role - span + 1, role) * lower + total]
    ppermute x1, starting transfers between devices: 7.55 us -> 9.88 us  [carried_pair(): lax.ppermute(jnp.concatenate(lifted_parts, -1), 'ctx', [(i, i ^ 1) for i...]
    ppermute x10, waiting for transfers between devices: 38.4 us -> 40.1 us  [the longest x6 29.3 us: pair_scan(): lower = lax.ppermute(total, 'ctx', device_pairs(pairs, level == 0))]
    unnamed x67 -> x61, local copies, waits for them, and re-layouts: 5.34 us -> 5.34 us
  transfers between devices with their start and end apart: 17 -> 17, of which waited for: 10 -> 12; matrix products, arithmetic and copies ran while one was open for 26% -> 21% of each run, Pallas kernels for 0% -> 0%
where the time goes in v5:
time: 120 us; the launch traced here: 119 us
  waiting for transfers between devices  41.9 us (35%)
  starting transfers between devices  34.3 us (29%)
  other arithmetic  23.6 us (20%)
  matrix products  8.47 us (7%)
  local copies, waits for them, and re-layouts  8.12 us (7%)
  between operations  2.12 us (2%)
    ppermute x6, waiting for transfers between devices, pair_scan(): lower = lax.ppermute(total, 'ctx', device_pairs(pairs, level == 0))  29.3 us
    ppermute x1, starting transfers between devices, carried_pair(): lax.ppermute(jnp.concatenate(lifted_parts, -1), 'ctx', [(i, i ^ 1) for i...  9.88 us
    ppermute x6, starting transfers between devices, pair_scan(): lower = lax.ppermute(total, 'ctx', device_pairs(pairs, level == 0))  9.28 us
    ppermute x2, waiting for transfers between devices, pair_scan(): got = lax.ppermute(sent, 'ctx', way.actual(pairs))  7.1 us
    ppermute x4, starting transfers between devices, gather_totals(): table = table + lax.ppermute(table, 'ctx', xor_pairs(count, bit))  6.54 us
    unnamed x61, local copies, waits for them, and re-layouts  5.34 us
    select_n x2, other arithmetic, pair_scan(): jnp.where(way.upper, pair_gain(0, pair, pair) * prefix + pair_total, prefix)  4.72 us
    ppermute x2, waiting for transfers between devices, pair_scan(): prefix = prefix + lax.ppermute(prefix, 'ctx', device_pairs(pairs, False))  3.71 us
  transfers between devices with their start and end apart: 17, of which 12 were waited for; matrix products, arithmetic and copies ran while one was open for 21% of the time, Pallas kernels for 0%

profile of v5, /device:TPU:1, one launch (start us, length us, event | category | flops | bytes accessed | tf_op | source)
XLA Modules:
  0.0 118.6 jit_solution(6949163188492566053)
XLA Ops:
  1.8 1.4 %copy.43 = bf16[1,128,2560]{1,2,0:T(8,128)(2,1)S(1)} copy(bf16[1,128,2560]{2,1,0:T(8,128)(2,1)} %param.7) | data formatting | bytes 1310720 | tf_op args[1]
  8.6 2.2 %convert_reduce_fusion = bf16[128,128]{1,0:T(8,128)(2,1)S(1)} fusion(f32[40,128]{1,0:T(8,128)S(1)} %copy.41, pred[128,128]{1,0:T(8,128)(4,1)S(1)} %iota_compare_fusion, bf16[128,40,64]{0,2,1:T(8,128)(2,1)S(1)} %bitcast.163, bf16[128,40,64]{0,2,1:T(8,128)(2,1)} %bitcast.166), kind=kOutput, calls=%fused_computation.7 | convolution fusion | flops 88457216 | bytes 1380352 | tf_op jit(solution)/shard_map/vmap(ihp,jhp->hij)/dot_general | solution.py:45
  12.0 2.4 %collective-permute-start.1 = (f32[1,17,40]{2,1,0:T(8,128)S(1)}, f32[1,17,40]{2,1,0:T(8,128)S(1)}, u32[]{:S(2)}, u32[]{:S(2)}) collective-permute-start(f32[1,17,40]{2,1,0:T(8,128)S(1)} %fusion.59), channel_id=1, source_target_pairs={{0,2},{1,3},{2,0},{3,1},{4,6},{5,7},{6,4},{7,5},{8,10},{9,11},{10,... | collective-permute-start | bytes 8168 | tf_op jit(solution)/shard_map/vmap()/ppermute | solution.py:87
  15.6 1.5 %collective-permute-start.2 = (f32[1,17,40]{2,1,0:T(8,128)S(1)}, f32[1,17,40]{2,1,0:T(8,128)S(1)}, u32[]{:S(2)}, u32[]{:S(2)}) collective-permute-start(f32[1,17,40]{2,1,0:T(8,128)S(1)} %add.203), channel_id=1, source_target_pairs={{0,4},{1,5},{2,6},{3,7},{4,0},{5,1},{6,2},{7,3},{8,12},{9,13},{10,... | collective-permute-start | bytes 8168 | tf_op jit(solution)/shard_map/vmap()/ppermute | solution.py:87
  18.2 2.5 %collective-permute-start.3 = (f32[1,17,40]{2,1,0:T(8,128)S(1)}, f32[1,17,40]{2,1,0:T(8,128)S(1)}, u32[]{:S(2)}, u32[]{:S(2)}) collective-permute-start(f32[1,17,40]{2,1,0:T(8,128)S(1)} %add.207), channel_id=1, source_target_pairs={{0,8},{1,9},{2,10},{3,11},{4,12},{5,13},{6,14},{7,15},{8,0},{9,1},... | collective-permute-start | bytes 8168 | tf_op jit(solution)/shard_map/vmap()/ppermute | solution.py:87
  23.4 3.0 %select_add_fusion.1 = (f32[1,128,1280]{1,2,0:T(8,128)}, f32[1,128,1280]{1,2,0:T(8,128)}, f32[1,128,1280]{1,2,0:T(8,128)}, f32[1,128,1280]{1,2,0:T(8,128)S(1)}) fusion(f32[1,128,2560]{1,2,0:T(8,128)} %collective-permute-done.4, f32[1280]{0:T(1024)S(1)} %broadcast_in_dim.293, pred[]{:T(512)S(6)} %eq.44, f32[1,128,2560]{1,2,0:T(8,128)S(1)} %convolution_bitcast_fusion.2, ...), kind=kLoop, calls=%fused_computation.60 | loop fusion | flops 1638400 | bytes 6563842 | tf_op jit(solution)/shard_map/vmap()/add | solution.py:200
  26.4 1.4 %collective-permute-start.5 = (f32[1,128,1280]{1,2,0:T(8,128)}, f32[1,128,1280]{1,2,0:T(8,128)S(1)}, u32[]{:S(2)}, u32[]{:S(2)}) collective-permute-start(f32[1,128,1280]{1,2,0:T(8,128)} %get-tuple-element.42), channel_id=1, source_target_pairs={{0,2},{4,6},{8,10},{12,14},{3,1},{7,5},{11,9},{15,13},{16,18},{20,... | collective-permute-start | bytes 1966088 | tf_op jit(solution)/shard_map/vmap()/ppermute | solution.py:158
  28.1 1.3 %collective-permute-start.10 = (f32[1,128,1280]{1,2,0:T(8,128)}, f32[1,128,1280]{1,2,0:T(8,128)S(1)}, u32[]{:S(2)}, u32[]{:S(2)}) collective-permute-start(f32[1,128,1280]{1,2,0:T(8,128)} %get-tuple-element.50), channel_id=1, source_target_pairs={{15,13},{11,9},{7,5},{3,1},{12,14},{8,10},{4,6},{0,2},{31,29},{27,... | collective-permute-start | bytes 1966088 | tf_op jit(solution)/shard_map/vmap()/ppermute | solution.py:158
  29.4 8.7 %collective-permute-done.5 = f32[1,128,1280]{1,2,0:T(8,128)S(1)} collective-permute-done((f32[1,128,1280]{1,2,0:T(8,128)}, f32[1,128,1280]{1,2,0:T(8,128)S(1)}, u32[]{:S(2)}, u32[]{:S(2)}) %collective-permute-start.5) | collective-permute-done | bytes 655392 | tf_op jit(solution)/shard_map/vmap()/ppermute | solution.py:158
  38.1 1.5 %add_select_fusion.3 = f32[1,128,1280]{1,2,0:T(8,128)S(1)} fusion(f32[1,128,1280]{1,2,0:T(8,128)} %get-tuple-element.42, f32[1,128,1280]{1,2,0:T(8,128)S(1)} %collective-permute-done.5, f32[1280]{0:T(1024)S(1)} %broadcast_in_dim.290, f32[1280]{0:T(1024)S(1)} %broadcast_in_dim.279, pred[]{:T(512)S(6)} %eq.44), kind=kLoop, calls=%fused_computation.59 | loop fusion | flops 819200 | bytes 1976321 | tf_op jit(solution)/shard_map/vmap(jit(_where))/select_n | solution.py:164
  39.6 3.3 %collective-permute-start.6 = (f32[1,128,1280]{1,2,0:T(8,128)S(1)}, f32[1,128,1280]{1,2,0:T(8,128)S(1)}, u32[]{:S(2)}, u32[]{:S(2)}) collective-permute-start(f32[1,128,1280]{1,2,0:T(8,128)S(1)} %add_select_fusion.3), channel_id=1, source_target_pairs={{2,6},{10,14},{1,5},{9,13},{18,22},{26,30},{17,21},{25,29}} | collective-permute-start | bytes 1966088 | tf_op jit(solution)/shard_map/vmap()/ppermute | solution.py:158
  42.9 2.2 %collective-permute-done.10 = f32[1,128,1280]{1,2,0:T(8,128)S(1)} collective-permute-done((f32[1,128,1280]{1,2,0:T(8,128)}, f32[1,128,1280]{1,2,0:T(8,128)S(1)}, u32[]{:S(2)}, u32[]{:S(2)}) %collective-permute-start.10) | collective-permute-done | bytes 655392 | tf_op jit(solution)/shard_map/vmap()/ppermute | solution.py:158
  45.5 1.3 %collective-permute-start.11 = (f32[1,128,1280]{1,2,0:T(8,128)S(1)}, f32[1,128,1280]{1,2,0:T(8,128)S(1)}, u32[]{:S(2)}, u32[]{:S(2)}) collective-permute-start(f32[1,128,1280]{1,2,0:T(8,128)S(1)} %add_select_fusion.1), channel_id=1, source_target_pairs={{13,9},{5,1},{14,10},{6,2},{29,25},{21,17},{30,26},{22,18}} | collective-permute-start | bytes 1966088 | tf_op jit(solution)/shard_map/vmap()/ppermute | solution.py:158
  46.8 3.5 %collective-permute-done.6 = f32[1,128,1280]{1,2,0:T(8,128)S(1)} collective-permute-done((f32[1,128,1280]{1,2,0:T(8,128)S(1)}, f32[1,128,1280]{1,2,0:T(8,128)S(1)}, u32[]{:S(2)}, u32[]{:S(2)}) %collective-permute-start.6) | collective-permute-done | bytes 655392 | tf_op jit(solution)/shard_map/vmap()/ppermute | solution.py:158
  51.4 5.5 %collective-permute-done.11 = f32[1,128,1280]{1,2,0:T(8,128)S(1)} collective-permute-done((f32[1,128,1280]{1,2,0:T(8,128)S(1)}, f32[1,128,1280]{1,2,0:T(8,128)S(1)}, u32[]{:S(2)}, u32[]{:S(2)}) %collective-permute-start.11) | collective-permute-done | bytes 655392 | tf_op jit(solution)/shard_map/vmap()/ppermute | solution.py:158
  57.1 1.3 %collective-permute-start.12 = (f32[1,128,1280]{1,2,0:T(8,128)S(1)}, f32[1,128,1280]{1,2,0:T(8,128)S(1)}, u32[]{:S(2)}, u32[]{:S(2)}) collective-permute-start(f32[1,128,1280]{1,2,0:T(8,128)S(1)} %multiply_add_fusion.2), channel_id=1, source_target_pairs={{9,1},{10,2},{25,17},{26,18}} | collective-permute-start | bytes 1966088 | tf_op jit(solution)/shard_map/vmap()/ppermute | solution.py:158
  58.6 1.3 %collective-permute-start.8 = (f32[1,128,1280]{1,2,0:T(8,128)S(1)}, f32[1,128,1280]{1,2,0:T(8,128)S(1)}, u32[]{:S(2)}, u32[]{:S(2)}) collective-permute-start(f32[1,128,1280]{1,2,0:T(8,128)S(1)} %broadcast_add_fusion.1), channel_id=1, source_target_pairs={{6,2},{14,10},{5,1},{13,9},{22,18},{30,26},{21,17},{29,25}} | collective-permute-start | bytes 1966088 | tf_op jit(solution)/shard_map/vmap()/ppermute | solution.py:181
  59.9 9.5 %collective-permute-done.12 = f32[1,128,1280]{1,2,0:T(8,128)S(1)} collective-permute-done((f32[1,128,1280]{1,2,0:T(8,128)S(1)}, f32[1,128,1280]{1,2,0:T(8,128)S(1)}, u32[]{:S(2)}, u32[]{:S(2)}) %collective-permute-start.12) | collective-permute-done | bytes 655392 | tf_op jit(solution)/shard_map/vmap()/ppermute | solution.py:158
  70.5 2.1 %collective-permute-start.13 = (f32[1,128,1280]{1,2,0:T(8,128)}, f32[1,128,1280]{1,2,0:T(8,128)}, u32[]{:S(2)}, u32[]{:S(2)}) collective-permute-start(f32[1,128,1280]{1,2,0:T(8,128)} %broadcast_add_fusion), channel_id=1, source_target_pairs={{9,13},{1,5},{10,14},{2,6},{25,29},{17,21},{26,30},{18,22}} | collective-permute-start | bytes 1966088 | tf_op jit(solution)/shard_map/vmap()/ppermute | solution.py:181
  72.6 3.7 %collective-permute-done.8 = f32[1,128,1280]{1,2,0:T(8,128)S(1)} collective-permute-done((f32[1,128,1280]{1,2,0:T(8,128)S(1)}, f32[1,128,1280]{1,2,0:T(8,128)S(1)}, u32[]{:S(2)}, u32[]{:S(2)}) %collective-permute-start.8) | collective-permute-done | bytes 655392 | tf_op jit(solution)/shard_map/vmap()/ppermute | solution.py:181
  76.3 2.8 %add_select_fusion.2 = (f32[1,128,1280]{1,2,0:T(8,128)}, f32[1,128,1280]{1,2,0:T(8,128)}) fusion(f32[1,128,1280]{1,2,0:T(8,128)} %get-tuple-element.42, f32[1280]{0:T(1024)S(1)} %broadcast_in_dim.279, pred[]{:T(512)S(6)} %eq.44, f32[1,128,1280]{1,2,0:T(8,128)S(1)} %collective-permute-done.6, f32[1,128,1280]{1,2,0:T(8,128)S(1)} %collective-permute-done.8, ...), kind=kLoop, calls=%fused_computation.56 | loop fusion | flops 1146880 | bytes 3947521 | tf_op jit(solution)/shard_map/vmap(jit(_where))/select_n | solution.py:171
  79.1 2.1 %collective-permute-start.9 = (f32[1,128,1280]{1,2,0:T(8,128)}, f32[1,128,1280]{1,2,0:T(8,128)}, u32[]{:S(2)}, u32[]{:S(2)}) collective-permute-start(f32[1,128,1280]{1,2,0:T(8,128)} %get-tuple-element.40), channel_id=1, source_target_pairs={{2,0},{6,4},{10,8},{14,12},{1,3},{5,7},{9,11},{13,15},{18,16},{22,... | collective-permute-start | bytes 1966088 | tf_op jit(solution)/shard_map/vmap()/ppermute | solution.py:174
  82.0 2.0 %add_select_fusion = (f32[1,128,1280]{1,2,0:T(8,128)S(1)}, f32[1,128,1280]{1,2,0:T(8,128)S(1)}) fusion(f32[1,128,1280]{1,2,0:T(8,128)S(1)} %copy-done.2, f32[1280]{0:T(1024)S(1)} %broadcast_in_dim.305, pred[]{:T(512)S(6)} %eq.43, f32[1,128,1280]{1,2,0:T(8,128)} %copy-done.13, f32[1,128,1280]{1,2,0:T(8,128)} %collective-permute-done.13, ...), kind=kLoop, calls=%fused_computation.48 | loop fusion | flops 1146880 | bytes 3947521 | tf_op jit(solution)/shard_map/vmap(jit(_where))/select_n | solution.py:171
  84.0 1.5 %collective-permute-start.14 = (f32[1,128,1280]{1,2,0:T(8,128)S(1)}, f32[1,128,1280]{1,2,0:T(8,128)S(1)}, u32[]{:S(2)}, u32[]{:S(2)}) collective-permute-start(f32[1,128,1280]{1,2,0:T(8,128)S(1)} %get-tuple-element.46), channel_id=1, source_target_pairs={{13,15},{9,11},{5,7},{1,3},{14,12},{10,8},{6,4},{2,0},{29,31},{25,... | collective-permute-start | bytes 1966088 | tf_op jit(solution)/shard_map/vmap()/ppermute | solution.py:174
  85.5 2.7 %collective-permute-done.9 = f32[1,128,1280]{1,2,0:T(8,128)} collective-permute-done((f32[1,128,1280]{1,2,0:T(8,128)}, f32[1,128,1280]{1,2,0:T(8,128)}, u32[]{:S(2)}, u32[]{:S(2)}) %collective-permute-start.9) | collective-permute-done | bytes 655392 | tf_op jit(solution)/shard_map/vmap()/ppermute | solution.py:174
  88.2 2.3 %select_bitcast_fusion = (bf16[128,1280]{0,1:T(8,128)(2,1)}, f32[1,128,1280]{1,2,0:T(8,128)S(1)}) fusion(f32[1,128,1280]{1,2,0:T(8,128)S(1)} %copy-done.1, f32[1280]{0:T(1024)S(1)} %broadcast_in_dim.302, pred[]{:T(512)S(6)} %eq.44, f32[1,128,1280]{1,2,0:T(8,128)} %collective-permute-done.9, f32[1,128,1280]{1,2,0:T(8,128)S(1)} %collective-permute-done.5, ...), kind=kLoop, calls=%fused_computation.42 | loop fusion | flops 1310720 | bytes 3614722 | tf_op jit(solution)/shard_map/vmap()/concatenate | solution.py:105
  90.7 4.4 %collective-permute-done.14 = f32[1,128,1280]{1,2,0:T(8,128)S(1)} collective-permute-done((f32[1,128,1280]{1,2,0:T(8,128)S(1)}, f32[1,128,1280]{1,2,0:T(8,128)S(1)}, u32[]{:S(2)}, u32[]{:S(2)}) %collective-permute-start.14) | collective-permute-done | bytes 655392 | tf_op jit(solution)/shard_map/vmap()/ppermute | solution.py:174
  96.8 9.9 %collective-permute-start.15 = (f32[1,128,2560]{1,2,0:T(8,128)}, f32[1,128,2560]{1,2,0:T(8,128)}, u32[]{:S(2)}, u32[]{:S(2)}) collective-permute-start(f32[1,128,2560]{1,2,0:T(8,128)} %pad_maximum_fusion.1), channel_id=1, source_target_pairs={{0,1},{1,0},{2,3},{3,2},{4,5},{5,4},{6,7},{7,6},{8,9},{9,8},{10,11... | collective-permute-start | bytes 3932168 | tf_op jit(solution)/shard_map/vmap()/ppermute | solution.py:205
  106.8 2.1 %fusion.4 = f32[1,128,40,64]{1,3,2,0:T(8,128)} fusion(bf16[128,40,64]{0,2,1:T(8,128)(2,1)S(1)} %bitcast.164, f32[40,128]{1,0:T(8,128)S(1)} %copy-done.21, f32[128,128]{1,0:T(8,128)S(1)} %fusion.31, pred[128,128]{1,0:T(8,128)(4,1)S(1)} %copy-done.23, f32[40]{0:T(128)S(1)} %copy-done.28, bf16[1,128,40,64]{1,3,2,0:T(8,128)(2,1)S(1)} %bitcast.165), kind=kOutput, calls=%fused_computation.14 | convolution fusion | flops 88145920 | bytes 2724000 | tf_op jit(solution)/shard_map/vmap(hij,ihp->jhp)/dot_general | solution.py:51
  109.0 1.2 %collective-permute-start.16 = (f32[40]{0:T(128)S(1)}, f32[40]{0:T(128)S(1)}, u32[]{:S(2)}, u32[]{:S(2)}) collective-permute-start(f32[40]{0:T(128)S(1)} %slice_bitcast_fusion.2), channel_id=1, source_target_pairs={{0,16},{16,0},{1,17},{17,1},{2,18},{18,2},{3,19},{19,3},{4,20},{20... | collective-permute-start | bytes 488 | tf_op jit(solution)/shard_map/ppermute | solution.py:227
  112.2 1.5 %broadcast_multiply_fusion = bf16[1,128,2560]{1,2,0:T(8,128)(2,1)S(1)} fusion(f32[1,128,2560]{1,2,0:T(8,128)} %collective-permute-done.15, f32[]{:T(128)S(6)} %exp.283), kind=kLoop, calls=%fused_computation.44 | loop fusion | flops 655360 | bytes 1966084 | tf_op jit(solution)/shard_map/vmap()/mul | solution.py:207
  114.8 1.2 %copy-done.15 = f32[1,128,40,64]{1,3,2,0:T(8,128)S(1)} copy-done((f32[1,128,40,64]{1,3,2,0:T(8,128)S(1)}, f32[1,128,40,64]{1,3,2,0:T(8,128)}, u32[]{:S(2)}) %copy-start.15) | copy-done | bytes 1310744
  (188 shorter events, 23.3 us)
Async XLA Ops:
  0.6 4.6 %copy-start = (bf16[1,128,128]{2,1,0:T(8,128)(2,1)S(1)}, bf16[1,128,128]{2,1,0:T(8,128)(2,1)}, u32[]{:S(2)}) copy-start(bf16[1,128,128]{2,1,0:T(8,128)(2,1)} %param.8) | copy-start | bytes 98308
  4.7 7.3 %collective-permute-start = (f32[1,17,40]{2,1,0:T(8,128)S(1)}, f32[1,17,40]{2,1,0:T(8,128)S(1)}, u32[]{:S(2)}, u32[]{:S(2)}) collective-permute-start(f32[1,17,40]{2,1,0:T(8,128)S(1)} %pad_maximum_fusion.2), channel_id=1, source_target_pairs={{0,1},{1,0},{2,3},{3,2},{4,5},{5,4},{6,7},{7,6},{8,9},{9,8},{10,11... | collective-permute-start | bytes 8168 | tf_op jit(solution)/shard_map/vmap()/ppermute | solution.py:87
  5.7 2.8 %copy-start.8 = (bf16[1,128,2560]{1,2,0:T(8,128)(2,1)S(1)}, bf16[1,128,2560]{1,2,0:T(8,128)(2,1)}, u32[]{:S(2)}) copy-start(bf16[1,128,2560]{1,2,0:T(8,128)(2,1)} %copy-done.7) | copy-start | bytes 1966084
  6.9 16.5 %collective-permute-start.4 = (f32[1,128,2560]{1,2,0:T(8,128)}, f32[1,128,2560]{1,2,0:T(8,128)}, u32[]{:S(2)}, u32[]{:S(2)}) collective-permute-start(f32[1,128,2560]{1,2,0:T(8,128)} %pad_maximum_fusion), channel_id=1, source_target_pairs={{0,1},{1,0},{2,3},{3,2},{4,5},{5,4},{6,7},{7,6},{8,9},{9,8},{10,11... | collective-permute-start | bytes 3932168 | tf_op jit(solution)/shard_map/vmap()/ppermute | solution.py:192
  8.6 5.9 %copy-start.24 = (pred[16]{0:T(512)(128)(4,1)S(1)}, pred[16]{0:T(512)(128)(4,1)}, u32[]{:S(2)}) copy-start(pred[16]{0:T(512)(128)(4,1)} %compare_and_fusion.7) | copy-start | bytes 52
  12.0 3.5 %collective-permute-start.1 = (f32[1,17,40]{2,1,0:T(8,128)S(1)}, f32[1,17,40]{2,1,0:T(8,128)S(1)}, u32[]{:S(2)}, u32[]{:S(2)}) collective-permute-start(f32[1,17,40]{2,1,0:T(8,128)S(1)} %fusion.59), channel_id=1, source_target_pairs={{0,2},{1,3},{2,0},{3,1},{4,6},{5,7},{6,4},{7,5},{8,10},{9,11},{10,... | collective-permute-start | bytes 8168 | tf_op jit(solution)/shard_map/vmap()/ppermute | solution.py:87
  15.6 2.6 %collective-permute-start.2 = (f32[1,17,40]{2,1,0:T(8,128)S(1)}, f32[1,17,40]{2,1,0:T(8,128)S(1)}, u32[]{:S(2)}, u32[]{:S(2)}) collective-permute-start(f32[1,17,40]{2,1,0:T(8,128)S(1)} %add.203), channel_id=1, source_target_pairs={{0,4},{1,5},{2,6},{3,7},{4,0},{5,1},{6,2},{7,3},{8,12},{9,13},{10,... | collective-permute-start | bytes 8168 | tf_op jit(solution)/shard_map/vmap()/ppermute | solution.py:87
  18.2 3.6 %collective-permute-start.3 = (f32[1,17,40]{2,1,0:T(8,128)S(1)}, f32[1,17,40]{2,1,0:T(8,128)S(1)}, u32[]{:S(2)}, u32[]{:S(2)}) collective-permute-start(f32[1,17,40]{2,1,0:T(8,128)S(1)} %add.207), channel_id=1, source_target_pairs={{0,8},{1,9},{2,10},{3,11},{4,12},{5,13},{6,14},{7,15},{8,0},{9,1},... | collective-permute-start | bytes 8168 | tf_op jit(solution)/shard_map/vmap()/ppermute | solution.py:87
  23.4 4.5 %copy-start.27 = (f32[40]{0:T(128)S(1)}, f32[40]{0:T(128)}, u32[]{:S(2)}) copy-start(f32[40]{0:T(128)} %get-tuple-element.27) | copy-start | bytes 484
  23.4 4.5 %copy-start.26 = (f32[40]{0:T(128)S(1)}, f32[40]{0:T(128)}, u32[]{:S(2)}) copy-start(f32[40]{0:T(128)} %get-tuple-element.26) | copy-start | bytes 484
  26.4 16.5 %copy-start.25 = (f32[40]{0:T(128)S(1)}, f32[40]{0:T(128)}, u32[]{:S(2)}) copy-start(f32[40]{0:T(128)} %get-tuple-element.24) | copy-start | bytes 484
  26.4 18.7 %copy-start.2 = (f32[1,128,1280]{1,2,0:T(8,128)S(1)}, f32[1,128,1280]{1,2,0:T(8,128)}, u32[]{:S(2)}) copy-start(f32[1,128,1280]{1,2,0:T(8,128)} %get-tuple-element.50) | copy-start | bytes 1966084
  26.4 11.7 %collective-permute-start.5 = (f32[1,128,1280]{1,2,0:T(8,128)}, f32[1,128,1280]{1,2,0:T(8,128)S(1)}, u32[]{:S(2)}, u32[]{:S(2)}) collective-permute-start(f32[1,128,1280]{1,2,0:T(8,128)} %get-tuple-element.42), channel_id=1, source_target_pairs={{0,2},{4,6},{8,10},{12,14},{3,1},{7,5},{11,9},{15,13},{16,18},{20,... | collective-permute-start | bytes 1966088 | tf_op jit(solution)/shard_map/vmap()/ppermute | solution.py:158
  28.1 17.0 %collective-permute-start.10 = (f32[1,128,1280]{1,2,0:T(8,128)}, f32[1,128,1280]{1,2,0:T(8,128)S(1)}, u32[]{:S(2)}, u32[]{:S(2)}) collective-permute-start(f32[1,128,1280]{1,2,0:T(8,128)} %get-tuple-element.50), channel_id=1, source_target_pairs={{15,13},{11,9},{7,5},{3,1},{12,14},{8,10},{4,6},{0,2},{31,29},{27,... | collective-permute-start | bytes 1966088 | tf_op jit(solution)/shard_map/vmap()/ppermute | solution.py:158
  39.6 10.8 %collective-permute-start.6 = (f32[1,128,1280]{1,2,0:T(8,128)S(1)}, f32[1,128,1280]{1,2,0:T(8,128)S(1)}, u32[]{:S(2)}, u32[]{:S(2)}) collective-permute-start(f32[1,128,1280]{1,2,0:T(8,128)S(1)} %add_select_fusion.3), channel_id=1, source_target_pairs={{2,6},{10,14},{1,5},{9,13},{18,22},{26,30},{17,21},{25,29}} | collective-permute-start | bytes 1966088 | tf_op jit(solution)/shard_map/vmap()/ppermute | solution.py:158
  45.1 5.5 %copy-start.11 = (f32[1,128,1280]{1,2,0:T(8,128)}, f32[1,128,1280]{1,2,0:T(8,128)S(1)}, u32[]{:S(2)}) copy-start(f32[1,128,1280]{1,2,0:T(8,128)S(1)} %collective-permute-done.10) | copy-start | bytes 1966084
  45.5 11.3 %collective-permute-start.11 = (f32[1,128,1280]{1,2,0:T(8,128)S(1)}, f32[1,128,1280]{1,2,0:T(8,128)S(1)}, u32[]{:S(2)}, u32[]{:S(2)}) collective-permute-start(f32[1,128,1280]{1,2,0:T(8,128)S(1)} %add_select_fusion.1), channel_id=1, source_target_pairs={{13,9},{5,1},{14,10},{6,2},{29,25},{21,17},{30,26},{22,18}} | collective-permute-start | bytes 1966088 | tf_op jit(solution)/shard_map/vmap()/ppermute | solution.py:158
  50.6 7.8 %collective-permute-start.7 = (f32[1,128,1280]{1,2,0:T(8,128)S(1)}, f32[1,128,1280]{1,2,0:T(8,128)S(1)}, u32[]{:S(2)}, u32[]{:S(2)}) collective-permute-start(f32[1,128,1280]{1,2,0:T(8,128)S(1)} %multiply_add_fusion.5), channel_id=1, source_target_pairs={{6,14},{5,13},{22,30},{21,29}} | collective-permute-start | bytes 1966088 | tf_op jit(solution)/shard_map/vmap()/ppermute | solution.py:158
  57.1 12.3 %collective-permute-start.12 = (f32[1,128,1280]{1,2,0:T(8,128)S(1)}, f32[1,128,1280]{1,2,0:T(8,128)S(1)}, u32[]{:S(2)}, u32[]{:S(2)}) collective-permute-start(f32[1,128,1280]{1,2,0:T(8,128)S(1)} %multiply_add_fusion.2), channel_id=1, source_target_pairs={{9,1},{10,2},{25,17},{26,18}} | collective-permute-start | bytes 1966088 | tf_op jit(solution)/shard_map/vmap()/ppermute | solution.py:158
  58.6 17.7 %collective-permute-start.8 = (f32[1,128,1280]{1,2,0:T(8,128)S(1)}, f32[1,128,1280]{1,2,0:T(8,128)S(1)}, u32[]{:S(2)}, u32[]{:S(2)}) collective-permute-start(f32[1,128,1280]{1,2,0:T(8,128)S(1)} %broadcast_add_fusion.1), channel_id=1, source_target_pairs={{6,2},{14,10},{5,1},{13,9},{22,18},{30,26},{21,17},{29,25}} | collective-permute-start | bytes 1966088 | tf_op jit(solution)/shard_map/vmap()/ppermute | solution.py:181
  70.5 11.5 %collective-permute-start.13 = (f32[1,128,1280]{1,2,0:T(8,128)}, f32[1,128,1280]{1,2,0:T(8,128)}, u32[]{:S(2)}, u32[]{:S(2)}) collective-permute-start(f32[1,128,1280]{1,2,0:T(8,128)} %broadcast_add_fusion), channel_id=1, source_target_pairs={{9,13},{1,5},{10,14},{2,6},{25,29},{17,21},{26,30},{18,22}} | collective-permute-start | bytes 1966088 | tf_op jit(solution)/shard_map/vmap()/ppermute | solution.py:181
  79.1 9.1 %collective-permute-start.9 = (f32[1,128,1280]{1,2,0:T(8,128)}, f32[1,128,1280]{1,2,0:T(8,128)}, u32[]{:S(2)}, u32[]{:S(2)}) collective-permute-start(f32[1,128,1280]{1,2,0:T(8,128)} %get-tuple-element.40), channel_id=1, source_target_pairs={{2,0},{6,4},{10,8},{14,12},{1,3},{5,7},{9,11},{13,15},{18,16},{22,... | collective-permute-start | bytes 1966088 | tf_op jit(solution)/shard_map/vmap()/ppermute | solution.py:174
  82.0 6.2 %copy-start.1 = (f32[1,128,1280]{1,2,0:T(8,128)S(1)}, f32[1,128,1280]{1,2,0:T(8,128)}, u32[]{:S(2)}) copy-start(f32[1,128,1280]{1,2,0:T(8,128)} %get-tuple-element.43) | copy-start | bytes 1966084
  82.0 6.2 %copy-start.14 = (f32[1,128,1280]{1,2,0:T(8,128)S(1)}, f32[1,128,1280]{1,2,0:T(8,128)}, u32[]{:S(2)}) copy-start(f32[1,128,1280]{1,2,0:T(8,128)} %get-tuple-element.41) | copy-start | bytes 1966084
  84.0 11.1 %collective-permute-start.14 = (f32[1,128,1280]{1,2,0:T(8,128)S(1)}, f32[1,128,1280]{1,2,0:T(8,128)S(1)}, u32[]{:S(2)}, u32[]{:S(2)}) collective-permute-start(f32[1,128,1280]{1,2,0:T(8,128)S(1)} %get-tuple-element.46), channel_id=1, source_target_pairs={{13,15},{9,11},{5,7},{1,3},{14,12},{10,8},{6,4},{2,0},{29,31},{25,... | collective-permute-start | bytes 1966088 | tf_op jit(solution)/shard_map/vmap()/ppermute | solution.py:174
  90.5 4.7 %copy-start.12 = (f32[1,128,1280]{1,2,0:T(8,128)S(1)}, f32[1,128,1280]{1,2,0:T(8,128)}, u32[]{:S(2)}) copy-start(f32[1,128,1280]{1,2,0:T(8,128)} %copy-done.11) | copy-start | bytes 1966084
  95.6 11.2 %copy-start.9 = (bf16[1,128,2560]{1,2,0:T(8,128)(2,1)S(1)}, bf16[1,128,2560]{1,2,0:T(8,128)(2,1)}, u32[]{:S(2)}) copy-start(bf16[1,128,2560]{1,2,0:T(8,128)(2,1)} %copy-done.7) | copy-start | bytes 1966084
  95.6 11.2 %copy-start.21 = (f32[40,128]{1,0:T(8,128)S(1)}, f32[40,128]{1,0:T(8,128)}, u32[]{:S(2)}) copy-start(f32[40,128]{1,0:T(8,128)} %copy-done.20) | copy-start | bytes 61444
  95.6 11.2 %copy-start.23 = (pred[128,128]{1,0:T(8,128)(4,1)S(1)}, pred[128,128]{1,0:T(8,128)(4,1)}, u32[]{:S(2)}) copy-start(pred[128,128]{1,0:T(8,128)(4,1)} %copy-done.22) | copy-start | bytes 49156
  95.6 11.2 %copy-start.28 = (f32[40]{0:T(128)S(1)}, f32[40]{0:T(128)}, u32[]{:S(2)}) copy-start(f32[40]{0:T(128)} %param.11) | copy-start | bytes 484
  96.8 15.4 %collective-permute-start.15 = (f32[1,128,2560]{1,2,0:T(8,128)}, f32[1,128,2560]{1,2,0:T(8,128)}, u32[]{:S(2)}, u32[]{:S(2)}) collective-permute-start(f32[1,128,2560]{1,2,0:T(8,128)} %pad_maximum_fusion.1), channel_id=1, source_target_pairs={{0,1},{1,0},{2,3},{3,2},{4,5},{5,4},{6,7},{7,6},{8,9},{9,8},{10,11... | collective-permute-start | bytes 3932168 | tf_op jit(solution)/shard_map/vmap()/ppermute | solution.py:205
  109.0 2.4 %collective-permute-start.16 = (f32[40]{0:T(128)S(1)}, f32[40]{0:T(128)S(1)}, u32[]{:S(2)}, u32[]{:S(2)}) collective-permute-start(f32[40]{0:T(128)S(1)} %slice_bitcast_fusion.2), channel_id=1, source_target_pairs={{0,16},{16,0},{1,17},{17,1},{2,18},{18,2},{3,19},{19,3},{4,20},{20... | collective-permute-start | bytes 488 | tf_op jit(solution)/shard_map/ppermute | solution.py:227
  (14 other events, 17.2 us)

commit v6 on v4

--- a/solution.py
+++ b/solution.py
@@ -54,27 +54,6 @@
     return grad_values.reshape(token_count, head_count * head_width), grad_write, grad_read
 
 
-def block_carried_grads(
-    write_map, value_scale, decayed_vals, decayed_cot, carried_state, carried_adjoint, local_grads
-):
-    local_values, local_write, local_read = local_grads
-    state_rounded = carried_state.astype(jnp.bfloat16)
-    adjoint_rounded = carried_adjoint.astype(jnp.bfloat16)
-    grad_read = local_read + jnp.einsum(
-        "iq,nq->in", decayed_cot, state_rounded, preferred_element_type=jnp.float32
-    )
-    grad_write = local_write + jnp.einsum(
-        "jq,nq->jn", decayed_vals, adjoint_rounded, preferred_element_type=jnp.float32
-    )
-    carried_term = jnp.einsum("jn,nq->jq", write_map, adjoint_rounded, preferred_element_type=jnp.float32)
-    grad_values = local_values + value_scale * carried_term
-    return (
-        grad_values.astype(jnp.bfloat16),
-        grad_write.astype(jnp.bfloat16),
-        grad_read.astype(jnp.bfloat16),
-    )
-
-
 def xor_pairs(count, bit):
     return [(i, i ^ (1 << bit)) for i in range(count)]
 
@@ -128,31 +107,107 @@
         return spread_heads(take_half(full, self.upper), self.head_width)[..., None, :]
 
 
-def pair_scan(way, pair_total):
-    pair_count = way.count // 2
-    level_count = pair_count.bit_length() - 1
-    low_tables = lambda level: min(level + 1, len(way.tables) - 1)
-    total = pair_total
-    lowers = []
+def exchange(payloads, pair_lists):
+    results = [None] * len(payloads)
+    done = set()
+    for first in range(len(payloads)):
+        if first in done:
+            continue
+        group = [k for k in range(len(payloads)) if set(pair_lists[k]) == set(pair_lists[first])]
+        done.update(group)
+        widths = [payloads[k].shape[-1] for k in group]
+        moved = lax.ppermute(jnp.concatenate([payloads[k] for k in group], -1), "ctx", pair_lists[first])
+        offset = 0
+        for k, width in zip(group, widths):
+            results[k] = moved[..., offset : offset + width]
+            offset += width
+    return results
+
+
+class PairScan:
+    def __init__(self, way):
+        self.way = way
+        self.pair_count = way.count // 2
+        self.level_count = self.pair_count.bit_length() - 1
+        self.flip = self.level_count >= 2
+        pair = way.pair
+        self.role = jnp.where(way.upper, pair ^ 1, pair) if self.flip else pair
+
+    def device_pairs(self, pairs, first_level):
+        lower = [(2 * a, 2 * b) for a, b in pairs]
+        if self.flip and first_level:
+            upper = [(2 * b + 1, 2 * a + 1) for a, b in pairs]
+        elif self.flip:
+            upper = [(2 * (a ^ 1) + 1, 2 * (b ^ 1) + 1) for a, b in pairs]
+        else:
+            upper = [(2 * a + 1, 2 * b + 1) for a, b in pairs]
+        return self.way.actual(lower + upper)
+
+    def pair_gain(self, level, low_pair, high_pair):
+        table = min(level + 2, len(self.way.tables) - 1)
+        return self.way.gain(table, 2 * low_pair, 2 * high_pair + 1)
+
+    def up_send(self, level):
+        span = 1 << level
+        pairs = [(a, a + span) for a in range(self.pair_count) if a % (2 * span) == span - 1]
+        return self.device_pairs(pairs, level == 0)
+
+    def up_combine(self, level, total, lower):
+        span = 1 << level
+        if self.flip and level == 0:
+            pair = self.way.pair
+            kept_upper = self.pair_gain(0, pair ^ 1, pair ^ 1) * total + lower
+            kept_lower = self.pair_gain(0, pair, pair) * lower + total
+            return jnp.where(self.way.upper, kept_upper, kept_lower)
+        return self.pair_gain(level, self.role - span + 1, self.role) * lower + total
+
+    def down_send(self, level, prefix, pair_total):
+        span = 1 << level
+        if self.flip and level == 0:
+            pair = self.way.pair
+            sent = jnp.where(self.way.upper, self.pair_gain(0, pair, pair) * prefix + pair_total, prefix)
+            pairs = [(2 * (a + 1), 2 * a) for a in range(0, self.pair_count, 2)]
+            pairs += [(2 * a + 1, 2 * (a + 1) + 1) for a in range(0, self.pair_count, 2)]
+            return sent, self.way.actual(pairs)
+        pairs = [(a, a - span) for a in range(self.pair_count) if a % (2 * span) == 2 * span - 1]
+        return prefix, self.device_pairs(pairs, False)
+
+    def down_combine(self, level, prefix, got, lowers):
+        span = 1 << level
+        if self.flip and level == 0:
+            pair = self.way.pair
+            grown = self.pair_gain(self.level_count, pair - 1, pair - 1) * prefix + lowers[0]
+            odd = pair % 2 == 1
+            return jnp.where(self.way.upper, jnp.where(odd, got, prefix), jnp.where(odd, grown, got))
+        if got is not None:
+            prefix = prefix + got
+        lower_gain = self.pair_gain(self.level_count, self.role - 2 * span + 1, self.role - span)
+        lower_gain = jnp.where(self.role % (2 * span) == 2 * span - 1, lower_gain, 1.0)
+        return lower_gain * prefix + lowers[level]
+
+
+def pair_scans(ways, pair_totals):
+    scans = [PairScan(way) for way in ways]
+    level_count = scans[0].level_count
+    totals = list(pair_totals)
+    lowers = [[] for _ in scans]
     for level in range(level_count):
-        span = 1 << level
-        pairs = [(a, a + span) for a in range(pair_count) if a % (2 * span) == span - 1]
-        lower = lax.ppermute(total, "ctx", way.pair_pairs(pairs))
-        lowers.append(lower)
-        if level < level_count - 1:
-            first = 2 * (way.pair - span + 1)
-            total = way.gain(low_tables(level), first, 2 * way.pair + 1) * lower + total
-    prefix = jnp.zeros_like(pair_total)
+        got = exchange(totals, [scan.up_send(level) for scan in scans])
+        for k, scan in enumerate(scans):
+            lowers[k].append(got[k])
+            if level < level_count - 1:
+                totals[k] = scan.up_combine(level, totals[k], got[k])
+    prefixes = [jnp.zeros_like(total) for total in pair_totals]
     for level in reversed(range(level_count)):
-        span = 1 << level
-        if level < level_count - 1:
-            pairs = [(a, a - span) for a in range(pair_count) if a % (2 * span) == 2 * span - 1]
-            prefix = prefix + lax.ppermute(prefix, "ctx", way.pair_pairs(pairs))
-        first = 2 * (way.pair - 2 * span + 1)
-        lower_gain = way.gain(-1, first, 2 * (way.pair - span) + 1)
-        lower_gain = jnp.where(way.pair % (2 * span) == 2 * span - 1, lower_gain, 1.0)
-        prefix = lower_gain * prefix + lowers[level]
-    return prefix
+        if level < level_count - 1 or (scans[0].flip and level == 0):
+            sends = [scan.down_send(level, p, t) for scan, p, t in zip(scans, prefixes, pair_totals)]
+            got = exchange([s[0] for s in sends], [s[1] for s in sends])
+        else:
+            got = [None] * len(scans)
+        prefixes = [
+            scan.down_combine(level, p, g, low) for scan, p, g, low in zip(scans, prefixes, got, lowers)
+        ]
+    return prefixes
 
 
 def carried_pair(tables, fwd_state, adj_state, position, count, head_width):
@@ -161,14 +216,18 @@
     sent = jnp.concatenate([take_half(s, ~w.upper) for s, w in zip(states, ways)], -1)
     got = lax.ppermute(sent, "ctx", [(i, i ^ 1) for i in range(count)])
     got = [got[..., : got.shape[-1] // 2], got[..., got.shape[-1] // 2 :]]
-    lifted_parts = []
-    keep_parts = []
+    lows = []
+    totals = []
     for way, state, other in zip(ways, states, got):
         own = take_half(state, way.upper)
         low_block = jnp.where(way.upper, other, own)
         high_block = jnp.where(way.upper, own, other)
-        pair_total = way.gain(1, 2 * way.pair + 1, 2 * way.pair + 1) * low_block + high_block
-        pair_prefix = pair_scan(way, pair_total)
+        lows.append(low_block)
+        totals.append(way.gain(1, 2 * way.pair + 1, 2 * way.pair + 1) * low_block + high_block)
+    pair_prefixes = pair_scans(ways, totals)
+    lifted_parts = []
+    keep_parts = []
+    for way, pair_prefix, low_block in zip(ways, pair_prefixes, lows):
         lifted = way.gain(1, 2 * way.pair, 2 * way.pair) * pair_prefix + low_block
         lifted_parts.append(jnp.where(way.upper, pair_prefix, lifted))
         keep_parts.append(jnp.where(way.upper, lifted, pair_prefix))
@@ -176,10 +235,36 @@
     unit = jnp.exp(jnp.min(tables[-1]) * 0.0)
     got = got * unit
     half = got.shape[-1] // 2
-    results = []
-    for way, mine, other in zip(ways, keep_parts, [got[..., :half], got[..., half:]]):
-        results.append(join_halves(mine, other, way.upper))
-    return results
+    others = [got[..., :half], got[..., half:]]
+    return keep_parts, others, [way.upper for way in ways]
+
+
+def block_carried_grads(write_map, value_scale, decayed_vals, decayed_cot, carried, local_grads):
+    local_values, local_write, local_read = local_grads
+    (state_mine, adjoint_mine), (state_other, adjoint_other), (state_upper, adjoint_upper) = carried
+
+    def rows_times(coeffs, mine, other, upper):
+        return jnp.einsum(
+            "iq,nq->in", take_half(coeffs, upper), mine.astype(jnp.bfloat16), preferred_element_type=jnp.float32
+        ) + jnp.einsum(
+            "iq,nq->in", take_half(coeffs, ~upper), other.astype(jnp.bfloat16), preferred_element_type=jnp.float32
+        )
+
+    grad_read = local_read + rows_times(decayed_cot, state_mine, state_other, state_upper)
+    grad_write = local_write + rows_times(decayed_vals, adjoint_mine, adjoint_other, adjoint_upper)
+    term_mine = jnp.einsum(
+        "jn,nq->jq", write_map, adjoint_mine.astype(jnp.bfloat16), preferred_element_type=jnp.float32
+    )
+    term_other = jnp.einsum(
+        "jn,nq->jq", write_map, adjoint_other.astype(jnp.bfloat16), preferred_element_type=jnp.float32
+    )
+    carried_term = join_halves(term_mine, term_other, adjoint_upper)
+    grad_values = local_values + value_scale * carried_term
+    return (
+        grad_values.astype(jnp.bfloat16),
+        grad_write.astype(jnp.bfloat16),
+        grad_read.astype(jnp.bfloat16),
+    )
 
 
 def local(token_values, cotangent, write_coeffs, read_coeffs, decay_codes, skip_gain):
@@ -196,14 +281,14 @@
     for bit in range(lax.axis_size("dp").bit_length() - 1):
         grad_skip = grad_skip + lax.ppermute(grad_skip, "dp", xor_pairs(lax.axis_size("dp"), bit))
     head_width = token_values.shape[2] // decay_codes.shape[2]
-    carried_state, carried_adjoint = jax.vmap(carried_pair, (0, 0, 0, None, None, None))(
+    carried = jax.vmap(carried_pair, (0, 0, 0, None, None, None))(
         tables, fwd_state, adj_state, position, count, head_width
     )
     local_grads = jax.vmap(block_local_grads, (0, 0, 0, 0, 0, None))(
         token_values, cotangent, write_coeffs, read_coeffs, within, skip_gain
     )
     grad_values, grad_write, grad_read = jax.vmap(block_carried_grads)(
-        write_coeffs, value_scale, decayed_vals, decayed_cot, carried_state, carried_adjoint, local_grads
+        write_coeffs, value_scale, decayed_vals, decayed_cot, carried, local_grads
     )
     return (grad_values, grad_write, grad_read, grad_skip)
 

time: 130 us -> 124 us (0.954); the launches traced: 128 us -> 123 us
  other arithmetic: 32.4 us -> 23.8 us
  waiting for transfers between devices: 41.2 us -> 44.9 us
    select_n x4 -> x3, other arithmetic: 1.37 us -> 7.34 us  [the longest x2 5.42 us: down_send(): jnp.where(self.way.upper, self.pair_gain(0, pair, pair) * prefix + pair_t...]
    add x8 -> x4, other arithmetic: 9.1 us -> 3.71 us  [the longest x2 2.15 us: down_combine(): return lower_gain * prefix + lowers[level]]
    ppermute x10 -> x8, waiting for transfers between devices: 38.4 us -> 43 us  [exchange(): lax.ppermute(jnp.concatenate([payloads[k] for k in group], -1), 'ctx', pa...]
    and x14 -> x16, other arithmetic: 4.4 us -> 0.14 us  [range_gain(): inside = (virtual >= low) & (virtual <= high)]
    ppermute x10 -> x8, starting transfers between devices: 19.1 us -> 15.3 us  [exchange(): lax.ppermute(jnp.concatenate([payloads[k] for k in group], -1), 'ctx', pa...]
    ppermute x1, starting transfers between devices: 7.55 us -> 11.1 us  [carried_pair(): lax.ppermute(jnp.concatenate(lifted_parts, -1), 'ctx', [(i, i ^ 1) for i...]
    reduce_sum x3 -> x4, other arithmetic: 2.21 us -> 0.37 us  [range_gain(): jnp.sum(jnp.where(inside[:, None], table[:count], 0.0), axis=0)]
    concatenate x2, other arithmetic: 2.69 us -> 1.25 us  [exchange(): jnp.concatenate([payloads[k] for k in group], -1)]
  transfers between devices with their start and end apart: 17 -> 15, of which waited for: 10 -> 9; matrix products, arithmetic and copies ran while one was open for 26% -> 19% of each run, Pallas kernels for 0% -> 0%
where the time goes in v6:
time: 124 us; the launch traced here: 123 us
  waiting for transfers between devices  44.9 us (36%)
  starting transfers between devices  34.6 us (28%)
  other arithmetic  23.8 us (19%)
  matrix products  9.63 us (8%)
  local copies, waits for them, and re-layouts  8.13 us (7%)
  between operations  2.09 us (2%)
    ppermute x8, waiting for transfers between devices, exchange(): lax.ppermute(jnp.concatenate([payloads[k] for k in group], -1), 'ctx', pa...  43 us
    ppermute x8, starting transfers between devices, exchange(): lax.ppermute(jnp.concatenate([payloads[k] for k in group], -1), 'ctx', pa...  15.3 us
    ppermute x1, starting transfers between devices, carried_pair(): lax.ppermute(jnp.concatenate(lifted_parts, -1), 'ctx', [(i, i ^ 1) for i...  11.1 us
    ppermute x4, starting transfers between devices, gather_totals(): table = table + lax.ppermute(table, 'ctx', xor_pairs(count, bit))  6.55 us
    unnamed x47, local copies, waits for them, and re-layouts  5.47 us
    select_n x2, other arithmetic, down_send(): jnp.where(self.way.upper, self.pair_gain(0, pair, pair) * prefix + pair_t...  5.42 us
    dot_general x1, matrix products, block_local_grads(): jnp.einsum('hij,ihp->jhp', value_weights, cot_three, preferred_element_ty...  3.52 us
    add x1, other arithmetic, carried_pair(): way.gain(1, 2 * way.pair + 1, 2 * way.pair + 1) * low_block + high_block  2.85 us
  transfers between devices with their start and end apart: 15, of which 9 were waited for; matrix products, arithmetic and copies ran while one was open for 19% of the time, Pallas kernels for 0%

profile of v6, /device:TPU:1, one launch (start us, length us, event | category | flops | bytes accessed | tf_op | source)
XLA Modules:
  0.0 123.2 jit_solution(7550498841055749784)
XLA Ops:
  1.8 1.4 %copy.44 = bf16[1,128,2560]{1,2,0:T(8,128)(2,1)S(1)} copy(bf16[1,128,2560]{2,1,0:T(8,128)(2,1)} %param.7) | data formatting | bytes 1310720 | tf_op args[1]
  5.7 1.2 pad_maximum_fusion
  7.7 2.4 %collective-permute-start.1 = (f32[1,17,40]{2,1,0:T(8,128)S(1)}, f32[1,17,40]{2,1,0:T(8,128)S(1)}, u32[]{:S(2)}, u32[]{:S(2)}) collective-permute-start(f32[1,17,40]{2,1,0:T(8,128)S(1)} %fusion.79), channel_id=1, source_target_pairs={{0,2},{1,3},{2,0},{3,1},{4,6},{5,7},{6,4},{7,5},{8,10},{9,11},{10,... | collective-permute-start | bytes 8168 | tf_op jit(solution)/shard_map/vmap()/ppermute | solution.py:66
  11.3 1.5 %collective-permute-start.2 = (f32[1,17,40]{2,1,0:T(8,128)S(1)}, f32[1,17,40]{2,1,0:T(8,128)S(1)}, u32[]{:S(2)}, u32[]{:S(2)}) collective-permute-start(f32[1,17,40]{2,1,0:T(8,128)S(1)} %add.218), channel_id=1, source_target_pairs={{0,4},{1,5},{2,6},{3,7},{4,0},{5,1},{6,2},{7,3},{8,12},{9,13},{10,... | collective-permute-start | bytes 8168 | tf_op jit(solution)/shard_map/vmap()/ppermute | solution.py:66
  13.9 2.5 %collective-permute-start.3 = (f32[1,17,40]{2,1,0:T(8,128)S(1)}, f32[1,17,40]{2,1,0:T(8,128)S(1)}, u32[]{:S(2)}, u32[]{:S(2)}) collective-permute-start(f32[1,17,40]{2,1,0:T(8,128)S(1)} %add.222), channel_id=1, source_target_pairs={{0,8},{1,9},{2,10},{3,11},{4,12},{5,13},{6,14},{7,15},{8,0},{9,1},... | collective-permute-start | bytes 8168 | tf_op jit(solution)/shard_map/vmap()/ppermute | solution.py:66
  18.1 2.8 %select_add_fusion.1 = (f32[1,128,1280]{1,2,0:T(8,128)S(1)}, f32[1,128,1280]{1,2,0:T(8,128)}, f32[1,128,1280]{1,2,0:T(8,128)S(1)}, f32[1,128,1280]{1,2,0:T(8,128)}) fusion(f32[1,128,2560]{1,2,0:T(8,128)} %collective-permute-done.4, f32[1280]{0:T(1024)S(1)} %broadcast_in_dim.303, pred[]{:T(512)S(6)} %eq.44, f32[1,128,2560]{1,2,0:T(8,128)S(1)} %convolution_bitcast_fusion.1, ...), kind=kLoop, calls=%fused_computation.57 | loop fusion | flops 1638400 | bytes 6563842 | tf_op jit(solution)/shard_map/vmap()/add | solution.py:226
  21.8 1.3 %collective-permute-start.5 = (f32[1,128,2560]{1,2,0:T(8,128)S(1)}, f32[1,128,2560]{1,2,0:T(8,128)S(1)}, u32[]{:S(2)}, u32[]{:S(2)}) collective-permute-start(f32[1,128,2560]{1,2,0:T(8,128)S(1)} %pad_maximum_fusion.1), channel_id=1, source_target_pairs={{0,2},{4,6},{8,10},{12,14},{3,1},{7,5},{11,9},{15,13},{16,18},{20,... | collective-permute-start | bytes 3932168 | tf_op jit(solution)/shard_map/vmap()/ppermute | solution.py:119
  23.8 16.4 %collective-permute-done.5 = f32[1,128,2560]{1,2,0:T(8,128)S(1)} collective-permute-done((f32[1,128,2560]{1,2,0:T(8,128)S(1)}, f32[1,128,2560]{1,2,0:T(8,128)S(1)}, u32[]{:S(2)}, u32[]{:S(2)}) %collective-permute-start.5) | collective-permute-done | bytes 1310752 | tf_op jit(solution)/shard_map/vmap()/ppermute | solution.py:119
  40.2 1.9 %add_select_fusion.3 = (f32[1,128,1280]{1,2,0:T(8,128)S(1)}, f32[1,128,1280]{1,2,0:T(8,128)S(1)}) fusion(f32[1,128,1280]{1,2,0:T(8,128)S(1)} %get-tuple-element.46, f32[1,128,2560]{1,2,0:T(8,128)S(1)} %collective-permute-done.5, f32[1280]{0:T(1024)S(1)} %broadcast_in_dim.300, f32[1280]{0:T(1024)S(1)} %broadcast_in_dim.289, pred[]{:T(512)S(6)} %eq.44, ...), kind=kLoop, calls=%fused_computation.55 | loop fusion | flops 1638400 | bytes 3952642 | tf_op jit(solution)/shard_map/vmap(jit(_where))/select_n | solution.py:161
  42.1 1.3 %collective-permute-start.9 = (f32[1,128,1280]{1,2,0:T(8,128)S(1)}, f32[1,128,1280]{1,2,0:T(8,128)}, u32[]{:S(2)}, u32[]{:S(2)}) collective-permute-start(f32[1,128,1280]{1,2,0:T(8,128)S(1)} %get-tuple-element.53), channel_id=1, source_target_pairs={{13,9},{5,1},{14,10},{6,2},{29,25},{21,17},{30,26},{22,18}} | collective-permute-start | bytes 1966088 | tf_op jit(solution)/shard_map/vmap()/ppermute | solution.py:119
  43.6 4.9 %collective-permute-start.6 = (f32[1,128,1280]{1,2,0:T(8,128)S(1)}, f32[1,128,1280]{1,2,0:T(8,128)S(1)}, u32[]{:S(2)}, u32[]{:S(2)}) collective-permute-start(f32[1,128,1280]{1,2,0:T(8,128)S(1)} %get-tuple-element.52), channel_id=1, source_target_pairs={{2,6},{10,14},{1,5},{9,13},{18,22},{26,30},{17,21},{25,29}} | collective-permute-start | bytes 1966088 | tf_op jit(solution)/shard_map/vmap()/ppermute | solution.py:119
  48.6 4.9 %collective-permute-done.9 = f32[1,128,1280]{1,2,0:T(8,128)} collective-permute-done((f32[1,128,1280]{1,2,0:T(8,128)S(1)}, f32[1,128,1280]{1,2,0:T(8,128)}, u32[]{:S(2)}, u32[]{:S(2)}) %collective-permute-start.9) | collective-permute-done | bytes 655392 | tf_op jit(solution)/shard_map/vmap()/ppermute | solution.py:119
  53.5 1.3 %multiply_add_fusion.3 = f32[1,128,1280]{1,2,0:T(8,128)S(1)} fusion(f32[1,128,1280]{1,2,0:T(8,128)S(1)} %get-tuple-element.53, f32[1,128,1280]{1,2,0:T(8,128)} %collective-permute-done.9, f32[1280]{0:T(1024)S(1)} %broadcast_in_dim.318), kind=kLoop, calls=%fused_computation.50 | loop fusion | flops 327680 | bytes 1971200 | tf_op jit(solution)/shard_map/vmap()/add | solution.py:162
  54.9 1.3 %collective-permute-start.10 = (f32[1,128,1280]{1,2,0:T(8,128)S(1)}, f32[1,128,1280]{1,2,0:T(8,128)S(1)}, u32[]{:S(2)}, u32[]{:S(2)}) collective-permute-start(f32[1,128,1280]{1,2,0:T(8,128)S(1)} %multiply_add_fusion.3), channel_id=1, source_target_pairs={{9,1},{10,2},{25,17},{26,18}} | collective-permute-start | bytes 1966088 | tf_op jit(solution)/shard_map/vmap()/ppermute | solution.py:119
  57.2 9.9 %collective-permute-done.10 = f32[1,128,1280]{1,2,0:T(8,128)S(1)} collective-permute-done((f32[1,128,1280]{1,2,0:T(8,128)S(1)}, f32[1,128,1280]{1,2,0:T(8,128)S(1)}, u32[]{:S(2)}, u32[]{:S(2)}) %collective-permute-start.10) | collective-permute-done | bytes 655392 | tf_op jit(solution)/shard_map/vmap()/ppermute | solution.py:119
  67.1 1.1 broadcast_add_fusion
  68.2 2.2 %collective-permute-start.11 = (f32[1,128,1280]{1,2,0:T(8,128)}, f32[1,128,1280]{1,2,0:T(8,128)}, u32[]{:S(2)}, u32[]{:S(2)}) collective-permute-start(f32[1,128,1280]{1,2,0:T(8,128)} %broadcast_add_fusion), channel_id=1, source_target_pairs={{9,13},{1,5},{10,14},{2,6},{25,29},{17,21},{26,30},{18,22}} | collective-permute-start | bytes 1966088 | tf_op jit(solution)/shard_map/vmap()/ppermute | solution.py:119
  70.3 1.1 broadcast_add_fusion.1
  71.4 1.3 %collective-permute-start.8 = (f32[1,128,1280]{1,2,0:T(8,128)}, f32[1,128,1280]{1,2,0:T(8,128)}, u32[]{:S(2)}, u32[]{:S(2)}) collective-permute-start(f32[1,128,1280]{1,2,0:T(8,128)} %broadcast_add_fusion.1), channel_id=1, source_target_pairs={{6,2},{14,10},{5,1},{13,9},{22,18},{30,26},{21,17},{29,25}} | collective-permute-start | bytes 1966088 | tf_op jit(solution)/shard_map/vmap()/ppermute | solution.py:119
  73.6 3.7 %collective-permute-done.11 = f32[1,128,1280]{1,2,0:T(8,128)} collective-permute-done((f32[1,128,1280]{1,2,0:T(8,128)}, f32[1,128,1280]{1,2,0:T(8,128)}, u32[]{:S(2)}, u32[]{:S(2)}) %collective-permute-start.11) | collective-permute-done | bytes 655392 | tf_op jit(solution)/shard_map/vmap()/ppermute | solution.py:119
  77.3 2.9 %add_select_fusion = (f32[1,128,1280]{1,2,0:T(8,128)S(1)}, f32[1,128,1280]{1,2,0:T(8,128)}) fusion(f32[1,128,1280]{1,2,0:T(8,128)S(1)} %copy-done.2, f32[1280]{0:T(1024)S(1)} %broadcast_in_dim.311, pred[]{:T(512)S(6)} %eq.43, f32[1,128,1280]{1,2,0:T(8,128)} %collective-permute-done.9, f32[1,128,1280]{1,2,0:T(8,128)} %collective-permute-done.11, ...), kind=kLoop, calls=%fused_computation.48 | loop fusion | flops 1146880 | bytes 3947521 | tf_op jit(solution)/shard_map/vmap(jit(_where))/select_n | solution.py:168
  80.2 2.9 %collective-permute-done.8 = f32[1,128,1280]{1,2,0:T(8,128)} collective-permute-done((f32[1,128,1280]{1,2,0:T(8,128)}, f32[1,128,1280]{1,2,0:T(8,128)}, u32[]{:S(2)}, u32[]{:S(2)}) %collective-permute-start.8) | collective-permute-done | bytes 655392 | tf_op jit(solution)/shard_map/vmap()/ppermute | solution.py:119
  83.1 2.5 %add_select_fusion.2 = (f32[1,128,1280]{1,2,0:T(8,128)S(1)}, f32[1,128,1280]{1,2,0:T(8,128)}) fusion(f32[1,128,1280]{1,2,0:T(8,128)S(1)} %get-tuple-element.46, f32[1280]{0:T(1024)S(1)} %broadcast_in_dim.289, pred[]{:T(512)S(6)} %eq.44, f32[1,128,1280]{1,2,0:T(8,128)S(1)} %copy-done.16, f32[1,128,1280]{1,2,0:T(8,128)} %collective-permute-done.8, ...), kind=kLoop, calls=%fused_computation.52 | loop fusion | flops 1146880 | bytes 3947521 | tf_op jit(solution)/shard_map/vmap(jit(_where))/select_n | solution.py:168
  85.6 1.2 pad_maximum_fusion.2
  86.8 2.4 %collective-permute-start.12 = (f32[1,128,2560]{1,2,0:T(8,128)}, f32[1,128,2560]{1,2,0:T(8,128)}, u32[]{:S(2)}, u32[]{:S(2)}) collective-permute-start(f32[1,128,2560]{1,2,0:T(8,128)} %pad_maximum_fusion.2), channel_id=1, source_target_pairs={{2,0},{6,4},{10,8},{14,12},{1,3},{5,7},{9,11},{13,15},{18,16},{22,... | collective-permute-start | bytes 3932168 | tf_op jit(solution)/shard_map/vmap()/ppermute | solution.py:119
  89.1 1.3 %convert_reduce_fusion = bf16[128,128]{1,0:T(8,128)(2,1)S(1)} fusion(f32[40,128]{1,0:T(8,128)S(1)} %copy.42, pred[128,128]{1,0:T(8,128)(4,1)S(1)} %iota_compare_fusion, bf16[128,40,64]{0,2,1:T(8,128)(2,1)S(1)} %bitcast.183, bf16[128,40,64]{0,2,1:T(8,128)(2,1)S(1)} %bitcast.184), kind=kOutput, calls=%fused_computation.2 | convolution fusion | flops 88457216 | bytes 1380352 | tf_op jit(solution)/shard_map/vmap(ihp,jhp->hij)/dot_general | solution.py:45
  91.6 3.5 %fusion = f32[1,128,40,64]{1,3,2,0:T(8,128)} fusion(bf16[128,40,64]{0,2,1:T(8,128)(2,1)} %bitcast.181, f32[40,128]{1,0:T(8,128)S(1)} %copy.42, f32[128,128]{1,0:T(8,128)S(1)} %fusion.52, pred[128,128]{1,0:T(8,128)(4,1)S(1)} %iota_compare_fusion, f32[40]{0:T(128)} %param.11, bf16[1,128,40,64]{1,3,2,0:T(8,128)(2,1)} %bitcast.182), kind=kOutput, calls=%fused_computation.12 | convolution fusion | flops 88145920 | bytes 2724000 | tf_op jit(solution)/shard_map/vmap(hij,ihp->jhp)/dot_general | solution.py:51
  96.4 1.3 %collective-permute-start.14 = (f32[40]{0:T(128)S(1)}, f32[40]{0:T(128)S(1)}, u32[]{:S(2)}, u32[]{:S(2)}) collective-permute-start(f32[40]{0:T(128)S(1)} %slice_bitcast_fusion.5), channel_id=1, source_target_pairs={{0,16},{16,0},{1,17},{17,1},{2,18},{18,2},{3,19},{19,3},{4,20},{20... | collective-permute-start | bytes 488 | tf_op jit(solution)/shard_map/ppermute | solution.py:282
  97.8 5.2 %collective-permute-done.12 = f32[1,128,2560]{1,2,0:T(8,128)} collective-permute-done((f32[1,128,2560]{1,2,0:T(8,128)}, f32[1,128,2560]{1,2,0:T(8,128)}, u32[]{:S(2)}, u32[]{:S(2)}) %collective-permute-start.12) | collective-permute-done | bytes 1310752 | tf_op jit(solution)/shard_map/vmap()/ppermute | solution.py:119
  102.9 2.2 %fusion.20 = (f32[1,128,1280]{1,2,0:T(8,128)S(1)}, f32[1,128,1280]{1,2,0:T(8,128)S(1)}, f32[1,128,1280]{1,2,0:T(8,128)S(1)}, f32[1,128,1280]{1,2,0:T(8,128)S(1)}) fusion(f32[1,128,1280]{1,2,0:T(8,128)S(1)} %copy-done.3, f32[1280]{0:T(1024)S(1)} %broadcast_in_dim.327, pred[]{:T(512)S(6)} %eq.44, f32[1,128,2560]{1,2,0:T(8,128)S(1)} %collective-permute-done.5, ...), kind=kLoop, calls=%fused_computation.46 | loop fusion | flops 2621440 | bytes 7884804 | tf_op jit(solution)/shard_map/vmap(jit(_where))/select_n | solution.py:232
  105.2 11.1 %collective-permute-start.13 = (f32[1,128,2560]{1,2,0:T(8,128)S(1)}, f32[1,128,2560]{1,2,0:T(8,128)S(1)}, u32[]{:S(2)}, u32[]{:S(2)}) collective-permute-start(f32[1,128,2560]{1,2,0:T(8,128)S(1)} %pad_maximum_fusion.3), channel_id=1, source_target_pairs={{0,1},{1,0},{2,3},{3,2},{4,5},{5,4},{6,7},{7,6},{8,9},{9,8},{10,11... | collective-permute-start | bytes 3932168 | tf_op jit(solution)/shard_map/vmap()/ppermute | solution.py:234
  120.3 1.1 copy.49
  (172 shorter events, 19.2 us)
Async XLA Ops:
  0.6 4.6 %copy-start = (bf16[1,128,128]{2,1,0:T(8,128)(2,1)S(1)}, bf16[1,128,128]{2,1,0:T(8,128)(2,1)}, u32[]{:S(2)}) copy-start(bf16[1,128,128]{2,1,0:T(8,128)(2,1)} %param.8) | copy-start | bytes 98308
  0.6 2.6 %copy-start.18 = (bf16[1,128,2560]{2,1,0:T(8,128)(2,1)S(1)}, bf16[1,128,2560]{2,1,0:T(8,128)(2,1)}, u32[]{:S(2)}) copy-start(bf16[1,128,2560]{2,1,0:T(8,128)(2,1)} %param.6) | copy-start | bytes 1966084
  3.7 1.2 copy-start.19
  4.4 1.2 copy-start.9
  4.7 3.0 %collective-permute-start = (f32[1,17,40]{2,1,0:T(8,128)S(1)}, f32[1,17,40]{2,1,0:T(8,128)S(1)}, u32[]{:S(2)}, u32[]{:S(2)}) collective-permute-start(f32[1,17,40]{2,1,0:T(8,128)S(1)} %pad_maximum_fusion.4), channel_id=1, source_target_pairs={{0,1},{1,0},{2,3},{3,2},{4,5},{5,4},{6,7},{7,6},{8,9},{9,8},{10,11... | collective-permute-start | bytes 8168 | tf_op jit(solution)/shard_map/vmap()/ppermute | solution.py:66
  6.9 11.2 %collective-permute-start.4 = (f32[1,128,2560]{1,2,0:T(8,128)}, f32[1,128,2560]{1,2,0:T(8,128)}, u32[]{:S(2)}, u32[]{:S(2)}) collective-permute-start(f32[1,128,2560]{1,2,0:T(8,128)} %pad_maximum_fusion), channel_id=1, source_target_pairs={{0,1},{1,0},{2,3},{3,2},{4,5},{5,4},{6,7},{7,6},{8,9},{9,8},{10,11... | collective-permute-start | bytes 3932168 | tf_op jit(solution)/shard_map/vmap()/ppermute | solution.py:217
  7.7 3.5 %collective-permute-start.1 = (f32[1,17,40]{2,1,0:T(8,128)S(1)}, f32[1,17,40]{2,1,0:T(8,128)S(1)}, u32[]{:S(2)}, u32[]{:S(2)}) collective-permute-start(f32[1,17,40]{2,1,0:T(8,128)S(1)} %fusion.79), channel_id=1, source_target_pairs={{0,2},{1,3},{2,0},{3,1},{4,6},{5,7},{6,4},{7,5},{8,10},{9,11},{10,... | collective-permute-start | bytes 8168 | tf_op jit(solution)/shard_map/vmap()/ppermute | solution.py:66
  11.3 2.6 %collective-permute-start.2 = (f32[1,17,40]{2,1,0:T(8,128)S(1)}, f32[1,17,40]{2,1,0:T(8,128)S(1)}, u32[]{:S(2)}, u32[]{:S(2)}) collective-permute-start(f32[1,17,40]{2,1,0:T(8,128)S(1)} %add.218), channel_id=1, source_target_pairs={{0,4},{1,5},{2,6},{3,7},{4,0},{5,1},{6,2},{7,3},{8,12},{9,13},{10,... | collective-permute-start | bytes 8168 | tf_op jit(solution)/shard_map/vmap()/ppermute | solution.py:66
  13.9 3.6 %collective-permute-start.3 = (f32[1,17,40]{2,1,0:T(8,128)S(1)}, f32[1,17,40]{2,1,0:T(8,128)S(1)}, u32[]{:S(2)}, u32[]{:S(2)}) collective-permute-start(f32[1,17,40]{2,1,0:T(8,128)S(1)} %add.222), channel_id=1, source_target_pairs={{0,8},{1,9},{2,10},{3,11},{4,12},{5,13},{6,14},{7,15},{8,0},{9,1},... | collective-permute-start | bytes 8168 | tf_op jit(solution)/shard_map/vmap()/ppermute | solution.py:66
  21.8 18.3 %collective-permute-start.5 = (f32[1,128,2560]{1,2,0:T(8,128)S(1)}, f32[1,128,2560]{1,2,0:T(8,128)S(1)}, u32[]{:S(2)}, u32[]{:S(2)}) collective-permute-start(f32[1,128,2560]{1,2,0:T(8,128)S(1)} %pad_maximum_fusion.1), channel_id=1, source_target_pairs={{0,2},{4,6},{8,10},{12,14},{3,1},{7,5},{11,9},{15,13},{16,18},{20,... | collective-permute-start | bytes 3932168 | tf_op jit(solution)/shard_map/vmap()/ppermute | solution.py:119
  42.1 11.4 %collective-permute-start.9 = (f32[1,128,1280]{1,2,0:T(8,128)S(1)}, f32[1,128,1280]{1,2,0:T(8,128)}, u32[]{:S(2)}, u32[]{:S(2)}) collective-permute-start(f32[1,128,1280]{1,2,0:T(8,128)S(1)} %get-tuple-element.53), channel_id=1, source_target_pairs={{13,9},{5,1},{14,10},{6,2},{29,25},{21,17},{30,26},{22,18}} | collective-permute-start | bytes 1966088 | tf_op jit(solution)/shard_map/vmap()/ppermute | solution.py:119
  43.6 12.5 %collective-permute-start.6 = (f32[1,128,1280]{1,2,0:T(8,128)S(1)}, f32[1,128,1280]{1,2,0:T(8,128)S(1)}, u32[]{:S(2)}, u32[]{:S(2)}) collective-permute-start(f32[1,128,1280]{1,2,0:T(8,128)S(1)} %get-tuple-element.52), channel_id=1, source_target_pairs={{2,6},{10,14},{1,5},{9,13},{18,22},{26,30},{17,21},{25,29}} | collective-permute-start | bytes 1966088 | tf_op jit(solution)/shard_map/vmap()/ppermute | solution.py:119
  54.9 12.2 %collective-permute-start.10 = (f32[1,128,1280]{1,2,0:T(8,128)S(1)}, f32[1,128,1280]{1,2,0:T(8,128)S(1)}, u32[]{:S(2)}, u32[]{:S(2)}) collective-permute-start(f32[1,128,1280]{1,2,0:T(8,128)S(1)} %multiply_add_fusion.3), channel_id=1, source_target_pairs={{9,1},{10,2},{25,17},{26,18}} | collective-permute-start | bytes 1966088 | tf_op jit(solution)/shard_map/vmap()/ppermute | solution.py:119
  56.2 12.0 %copy-start.15 = (f32[1,128,1280]{1,2,0:T(8,128)}, f32[1,128,1280]{1,2,0:T(8,128)S(1)}, u32[]{:S(2)}) copy-start(f32[1,128,1280]{1,2,0:T(8,128)S(1)} %collective-permute-done.6) | copy-start | bytes 1966084
  56.4 13.9 %collective-permute-start.7 = (f32[1,128,1280]{1,2,0:T(8,128)S(1)}, f32[1,128,1280]{1,2,0:T(8,128)S(1)}, u32[]{:S(2)}, u32[]{:S(2)}) collective-permute-start(f32[1,128,1280]{1,2,0:T(8,128)S(1)} %multiply_add_fusion.5), channel_id=1, source_target_pairs={{6,14},{5,13},{22,30},{21,29}} | collective-permute-start | bytes 1966088 | tf_op jit(solution)/shard_map/vmap()/ppermute | solution.py:119
  57.1 20.1 %copy-start.2 = (f32[1,128,1280]{1,2,0:T(8,128)S(1)}, f32[1,128,1280]{1,2,0:T(8,128)}, u32[]{:S(2)}) copy-start(f32[1,128,1280]{1,2,0:T(8,128)} %copy-done.1) | copy-start | bytes 1966084
  67.1 4.3 %copy-start.8 = (f32[1,128,1280]{1,2,0:T(8,128)}, f32[1,128,1280]{1,2,0:T(8,128)S(1)}, u32[]{:S(2)}) copy-start(f32[1,128,1280]{1,2,0:T(8,128)S(1)} %collective-permute-done.10) | copy-start | bytes 1966084
  68.2 9.1 %collective-permute-start.11 = (f32[1,128,1280]{1,2,0:T(8,128)}, f32[1,128,1280]{1,2,0:T(8,128)}, u32[]{:S(2)}, u32[]{:S(2)}) collective-permute-start(f32[1,128,1280]{1,2,0:T(8,128)} %broadcast_add_fusion), channel_id=1, source_target_pairs={{9,13},{1,5},{10,14},{2,6},{25,29},{17,21},{26,30},{18,22}} | collective-permute-start | bytes 1966088 | tf_op jit(solution)/shard_map/vmap()/ppermute | solution.py:119
  71.4 11.6 %collective-permute-start.8 = (f32[1,128,1280]{1,2,0:T(8,128)}, f32[1,128,1280]{1,2,0:T(8,128)}, u32[]{:S(2)}, u32[]{:S(2)}) collective-permute-start(f32[1,128,1280]{1,2,0:T(8,128)} %broadcast_add_fusion.1), channel_id=1, source_target_pairs={{6,2},{14,10},{5,1},{13,9},{22,18},{30,26},{21,17},{29,25}} | collective-permute-start | bytes 1966088 | tf_op jit(solution)/shard_map/vmap()/ppermute | solution.py:119
  73.6 9.5 %copy-start.16 = (f32[1,128,1280]{1,2,0:T(8,128)S(1)}, f32[1,128,1280]{1,2,0:T(8,128)}, u32[]{:S(2)}) copy-start(f32[1,128,1280]{1,2,0:T(8,128)} %copy-done.15) | copy-start | bytes 1966084
  85.6 3.5 %copy-start.12 = (bf16[1,128,2560]{1,2,0:T(8,128)(2,1)S(1)}, bf16[1,128,2560]{1,2,0:T(8,128)(2,1)}, u32[]{:S(2)}) copy-start(bf16[1,128,2560]{1,2,0:T(8,128)(2,1)} %copy-done.11) | copy-start | bytes 1966084
  85.6 3.5 %copy-start.14 = (bf16[1,128,2560]{1,2,0:T(8,128)(2,1)S(1)}, bf16[1,128,2560]{1,2,0:T(8,128)(2,1)}, u32[]{:S(2)}) copy-start(bf16[1,128,2560]{1,2,0:T(8,128)(2,1)} %copy-done.13) | copy-start | bytes 1966084
  86.8 16.1 %collective-permute-start.12 = (f32[1,128,2560]{1,2,0:T(8,128)}, f32[1,128,2560]{1,2,0:T(8,128)}, u32[]{:S(2)}, u32[]{:S(2)}) collective-permute-start(f32[1,128,2560]{1,2,0:T(8,128)} %pad_maximum_fusion.2), channel_id=1, source_target_pairs={{2,0},{6,4},{10,8},{14,12},{1,3},{5,7},{9,11},{13,15},{18,16},{22,... | collective-permute-start | bytes 3932168 | tf_op jit(solution)/shard_map/vmap()/ppermute | solution.py:119
  91.5 4.0 %copy-start.21 = (f32[20]{0:T(128)S(1)}, f32[20]{0:T(128)}, u32[]{:S(2)}) copy-start(f32[20]{0:T(128)} %get-tuple-element.71) | copy-start | bytes 244
  91.5 11.4 %copy-start.3 = (f32[1,128,1280]{1,2,0:T(8,128)S(1)}, f32[1,128,1280]{1,2,0:T(8,128)}, u32[]{:S(2)}) copy-start(f32[1,128,1280]{1,2,0:T(8,128)} %get-tuple-element.47) | copy-start | bytes 1966084
  91.6 11.3 %copy-start.4 = (f32[1,128,1280]{1,2,0:T(8,128)S(1)}, f32[1,128,1280]{1,2,0:T(8,128)}, u32[]{:S(2)}) copy-start(f32[1,128,1280]{1,2,0:T(8,128)} %get-tuple-element.55) | copy-start | bytes 1966084
  91.6 11.3 %copy-start.7 = (f32[1,128,1280]{1,2,0:T(8,128)S(1)}, f32[1,128,1280]{1,2,0:T(8,128)}, u32[]{:S(2)}) copy-start(f32[1,128,1280]{1,2,0:T(8,128)} %get-tuple-element.45) | copy-start | bytes 1966084
  96.4 19.9 %collective-permute-start.14 = (f32[40]{0:T(128)S(1)}, f32[40]{0:T(128)S(1)}, u32[]{:S(2)}, u32[]{:S(2)}) collective-permute-start(f32[40]{0:T(128)S(1)} %slice_bitcast_fusion.5), channel_id=1, source_target_pairs={{0,16},{16,0},{1,17},{17,1},{2,18},{18,2},{3,19},{19,3},{4,20},{20... | collective-permute-start | bytes 488 | tf_op jit(solution)/shard_map/ppermute | solution.py:282
  105.2 13.8 %collective-permute-start.13 = (f32[1,128,2560]{1,2,0:T(8,128)S(1)}, f32[1,128,2560]{1,2,0:T(8,128)S(1)}, u32[]{:S(2)}, u32[]{:S(2)}) collective-permute-start(f32[1,128,2560]{1,2,0:T(8,128)S(1)} %pad_maximum_fusion.3), channel_id=1, source_target_pairs={{0,1},{1,0},{2,3},{3,2},{4,5},{5,4},{6,7},{7,6},{8,9},{9,8},{10,11... | collective-permute-start | bytes 3932168 | tf_op jit(solution)/shard_map/vmap()/ppermute | solution.py:234
  117.1 1.1 copy-start.6
  118.8 1.3 %copy-start.17 = (f32[1,128,40,64]{1,3,2,0:T(8,128)S(1)}, f32[1,128,40,64]{1,3,2,0:T(8,128)}, u32[]{:S(2)}) copy-start(f32[1,128,40,64]{1,3,2,0:T(8,128)} %fusion) | copy-start | bytes 3932164
  120.3 1.1 copy-start.20
  (5 other events, 4.5 us)

commit v7 on v6

--- a/solution.py
+++ b/solution.py
@@ -108,20 +108,7 @@
 
 
 def exchange(payloads, pair_lists):
-    results = [None] * len(payloads)
-    done = set()
-    for first in range(len(payloads)):
-        if first in done:
-            continue
-        group = [k for k in range(len(payloads)) if set(pair_lists[k]) == set(pair_lists[first])]
-        done.update(group)
-        widths = [payloads[k].shape[-1] for k in group]
-        moved = lax.ppermute(jnp.concatenate([payloads[k] for k in group], -1), "ctx", pair_lists[first])
-        offset = 0
-        for k, width in zip(group, widths):
-            results[k] = moved[..., offset : offset + width]
-            offset += width
-    return results
+    return [lax.ppermute(p, "ctx", pairs) for p, pairs in zip(payloads, pair_lists)]
 
 
 class PairScan:

time: 124 us -> 126 us (1.016)
  other arithmetic: 23.8 us -> 34.8 us
  waiting for transfers between devices: 44.9 us -> 37.5 us
    and x16, other arithmetic: 0.14 us -> 8.79 us  [range_gain(): inside = (virtual >= low) & (virtual <= high)]
    ppermute x8 -> x10, waiting for transfers between devices: 43 us -> 37.3 us  [exchange(): lax.ppermute(p, 'ctx', pairs)]
    reduce_sum x4, other arithmetic: 0.37 us -> 3.04 us  [range_gain(): jnp.sum(jnp.where(inside[:, None], table[:count], 0.0), axis=0)]
    ppermute x4, waiting for transfers between devices: 1.71 us -> 0.01 us  [gather_totals(): table = table + lax.ppermute(table, 'ctx', xor_pairs(count, bit))]
    ppermute x1, starting transfers between devices: 11.1 us -> 9.57 us  [carried_pair(): lax.ppermute(jnp.concatenate(lifted_parts, -1), 'ctx', [(i, i ^ 1) for i...]
    ppermute x8 -> x10, starting transfers between devices: 15.3 us -> 16.7 us  [exchange(): lax.ppermute(p, 'ctx', pairs)]
    select_n x1 -> x2, other arithmetic: 2.21 us -> 3.18 us  [carried_pair(): lifted_parts.append(jnp.where(way.upper, pair_prefix, lifted))]
    unnamed x47 -> x49, local copies, waits for them, and re-layouts: 5.47 us -> 4.64 us
  transfers between devices with their start and end apart: 15 -> 17, of which waited for: 9 -> 8; matrix products, arithmetic and copies ran while one was open for 19% -> 31% of each run, Pallas kernels for 0% -> 0%
where the time goes in v7:
time: 126 us; the launch traced here: 125 us
  waiting for transfers between devices  37.5 us (30%)
  other arithmetic  34.8 us (28%)
  starting transfers between devices  34.1 us (27%)
  matrix products  9.9 us (8%)
  local copies, waits for them, and re-layouts  7.29 us (6%)
  between operations  1.83 us (1%)
    ppermute x10, waiting for transfers between devices, exchange(): lax.ppermute(p, 'ctx', pairs)  37.3 us
    ppermute x10, starting transfers between devices, exchange(): lax.ppermute(p, 'ctx', pairs)  16.7 us
    ppermute x1, starting transfers between devices, carried_pair(): lax.ppermute(jnp.concatenate(lifted_parts, -1), 'ctx', [(i, i ^ 1) for i...  9.57 us
    and x16, other arithmetic, range_gain(): inside = (virtual >= low) & (virtual <= high)  8.79 us
    ppermute x4, starting transfers between devices, gather_totals(): table = table + lax.ppermute(table, 'ctx', xor_pairs(count, bit))  6.13 us
    select_n x2, other arithmetic, down_send(): jnp.where(self.way.upper, self.pair_gain(0, pair, pair) * prefix + pair_t...  5.85 us
    unnamed x49, local copies, waits for them, and re-layouts  4.64 us
    select_n x2, other arithmetic, carried_pair(): lifted_parts.append(jnp.where(way.upper, pair_prefix, lifted))  3.18 us
  transfers between devices with their start and end apart: 17, of which 8 were waited for; matrix products, arithmetic and copies ran while one was open for 31% of the time, Pallas kernels for 0%

profile of v7, /device:TPU:1, one launch (start us, length us, event | category | flops | bytes accessed | tf_op | source)
XLA Modules:
  0.0 125.4 jit_solution(11082442637383113567)
XLA Ops:
  1.8 1.4 %copy.44 = bf16[1,128,2560]{1,2,0:T(8,128)(2,1)S(1)} copy(bf16[1,128,2560]{2,1,0:T(8,128)(2,1)} %param.7) | data formatting | bytes 1310720 | tf_op args[1]
  6.3 1.2 pad_maximum_fusion
  11.4 2.3 %convert_reduce_fusion = bf16[128,128]{1,0:T(8,128)(2,1)S(1)} fusion(f32[40,128]{1,0:T(8,128)S(1)} %copy.42, pred[128,128]{1,0:T(8,128)(4,1)S(1)} %iota_compare_fusion, bf16[128,40,64]{0,2,1:T(8,128)(2,1)S(1)} %bitcast.181, bf16[128,40,64]{0,2,1:T(8,128)(2,1)} %bitcast.184), kind=kOutput, calls=%fused_computation.2 | convolution fusion | flops 88457216 | bytes 1380352 | tf_op jit(solution)/shard_map/vmap(ihp,jhp->hij)/dot_general | solution.py:45
  20.2 2.8 %fusion = f32[1,128,40,64]{1,3,2,0:T(8,128)} fusion(bf16[128,40,64]{0,2,1:T(8,128)(2,1)S(1)} %bitcast.182, f32[40,128]{1,0:T(8,128)S(1)} %copy.42, f32[128,128]{1,0:T(8,128)S(1)} %fusion.52, pred[128,128]{1,0:T(8,128)(4,1)S(1)} %iota_compare_fusion, f32[40]{0:T(128)} %param.11, bf16[1,128,40,64]{1,3,2,0:T(8,128)(2,1)S(1)} %bitcast.183), kind=kOutput, calls=%fused_computation.12 | convolution fusion | flops 88145920 | bytes 2724000 | tf_op jit(solution)/shard_map/vmap(hij,ihp->jhp)/dot_general | solution.py:51
  23.0 2.3 %collective-permute-start.1 = (f32[1,17,40]{2,1,0:T(8,128)S(1)}, f32[1,17,40]{2,1,0:T(8,128)S(1)}, u32[]{:S(2)}, u32[]{:S(2)}) collective-permute-start(f32[1,17,40]{2,1,0:T(8,128)S(1)} %fusion.79), channel_id=1, source_target_pairs={{0,2},{1,3},{2,0},{3,1},{4,6},{5,7},{6,4},{7,5},{8,10},{9,11},{10,... | collective-permute-start | bytes 8168 | tf_op jit(solution)/shard_map/vmap()/ppermute | solution.py:66
  26.5 1.4 %collective-permute-start.2 = (f32[1,17,40]{2,1,0:T(8,128)S(1)}, f32[1,17,40]{2,1,0:T(8,128)S(1)}, u32[]{:S(2)}, u32[]{:S(2)}) collective-permute-start(f32[1,17,40]{2,1,0:T(8,128)S(1)} %add.218), channel_id=1, source_target_pairs={{0,4},{1,5},{2,6},{3,7},{4,0},{5,1},{6,2},{7,3},{8,12},{9,13},{10,... | collective-permute-start | bytes 8168 | tf_op jit(solution)/shard_map/vmap()/ppermute | solution.py:66
  29.5 2.4 %collective-permute-start.3 = (f32[1,17,40]{2,1,0:T(8,128)S(1)}, f32[1,17,40]{2,1,0:T(8,128)S(1)}, u32[]{:S(2)}, u32[]{:S(2)}) collective-permute-start(f32[1,17,40]{2,1,0:T(8,128)S(1)} %add.222), channel_id=1, source_target_pairs={{0,8},{1,9},{2,10},{3,11},{4,12},{5,13},{6,14},{7,15},{8,0},{9,1},... | collective-permute-start | bytes 8168 | tf_op jit(solution)/shard_map/vmap()/ppermute | solution.py:66
  34.7 3.2 %select_add_fusion.1 = (f32[1,128,1280]{1,2,0:T(8,128)}, f32[1,128,1280]{1,2,0:T(8,128)S(1)}, f32[1,128,1280]{1,2,0:T(8,128)}, f32[1,128,1280]{1,2,0:T(8,128)}) fusion(f32[1,128,2560]{1,2,0:T(8,128)} %collective-permute-done.4, f32[1280]{0:T(1024)S(1)} %broadcast_in_dim.303, pred[]{:T(512)S(6)} %eq.44, f32[1,128,2560]{1,2,0:T(8,128)S(1)} %convolution_bitcast_fusion.1, ...), kind=kLoop, calls=%fused_computation.55 | loop fusion | flops 1638400 | bytes 6563842 | tf_op jit(solution)/shard_map/vmap()/add | solution.py:213
  37.8 1.4 %collective-permute-start.5 = (f32[1,128,1280]{1,2,0:T(8,128)}, f32[1,128,1280]{1,2,0:T(8,128)S(1)}, u32[]{:S(2)}, u32[]{:S(2)}) collective-permute-start(f32[1,128,1280]{1,2,0:T(8,128)} %get-tuple-element.42), channel_id=1, source_target_pairs={{0,2},{4,6},{8,10},{12,14},{3,1},{7,5},{11,9},{15,13},{16,18},{20,... | collective-permute-start | bytes 1966088 | tf_op jit(solution)/shard_map/vmap()/ppermute | solution.py:111
  39.5 1.3 %collective-permute-start.10 = (f32[1,128,1280]{1,2,0:T(8,128)}, f32[1,128,1280]{1,2,0:T(8,128)S(1)}, u32[]{:S(2)}, u32[]{:S(2)}) collective-permute-start(f32[1,128,1280]{1,2,0:T(8,128)} %get-tuple-element.50), channel_id=1, source_target_pairs={{15,13},{11,9},{7,5},{3,1},{12,14},{8,10},{4,6},{0,2},{31,29},{27,... | collective-permute-start | bytes 1966088 | tf_op jit(solution)/shard_map/vmap()/ppermute | solution.py:111
  40.8 8.7 %collective-permute-done.5 = f32[1,128,1280]{1,2,0:T(8,128)S(1)} collective-permute-done((f32[1,128,1280]{1,2,0:T(8,128)}, f32[1,128,1280]{1,2,0:T(8,128)S(1)}, u32[]{:S(2)}, u32[]{:S(2)}) %collective-permute-start.5) | collective-permute-done | bytes 655392 | tf_op jit(solution)/shard_map/vmap()/ppermute | solution.py:111
  49.5 1.5 %add_select_fusion.3 = f32[1,128,1280]{1,2,0:T(8,128)S(1)} fusion(f32[1,128,1280]{1,2,0:T(8,128)} %get-tuple-element.42, f32[1,128,1280]{1,2,0:T(8,128)S(1)} %collective-permute-done.5, f32[1280]{0:T(1024)S(1)} %broadcast_in_dim.300, f32[1280]{0:T(1024)S(1)} %broadcast_in_dim.289, pred[]{:T(512)S(6)} %eq.44), kind=kLoop, calls=%fused_computation.54 | loop fusion | flops 819200 | bytes 1976321 | tf_op jit(solution)/shard_map/vmap(jit(_where))/select_n | solution.py:148
  51.0 2.9 %collective-permute-start.6 = (f32[1,128,1280]{1,2,0:T(8,128)S(1)}, f32[1,128,1280]{1,2,0:T(8,128)S(1)}, u32[]{:S(2)}, u32[]{:S(2)}) collective-permute-start(f32[1,128,1280]{1,2,0:T(8,128)S(1)} %add_select_fusion.3), channel_id=1, source_target_pairs={{2,6},{10,14},{1,5},{9,13},{18,22},{26,30},{17,21},{25,29}} | collective-permute-start | bytes 1966088 | tf_op jit(solution)/shard_map/vmap()/ppermute | solution.py:111
  53.9 2.6 %collective-permute-done.10 = f32[1,128,1280]{1,2,0:T(8,128)S(1)} collective-permute-done((f32[1,128,1280]{1,2,0:T(8,128)}, f32[1,128,1280]{1,2,0:T(8,128)S(1)}, u32[]{:S(2)}, u32[]{:S(2)}) %collective-permute-start.10) | collective-permute-done | bytes 655392 | tf_op jit(solution)/shard_map/vmap()/ppermute | solution.py:111
  56.9 1.3 %collective-permute-start.11 = (f32[1,128,1280]{1,2,0:T(8,128)S(1)}, f32[1,128,1280]{1,2,0:T(8,128)S(1)}, u32[]{:S(2)}, u32[]{:S(2)}) collective-permute-start(f32[1,128,1280]{1,2,0:T(8,128)S(1)} %add_select_fusion.1), channel_id=1, source_target_pairs={{13,9},{5,1},{14,10},{6,2},{29,25},{21,17},{30,26},{22,18}} | collective-permute-start | bytes 1966088 | tf_op jit(solution)/shard_map/vmap()/ppermute | solution.py:111
  58.2 3.1 %collective-permute-done.6 = f32[1,128,1280]{1,2,0:T(8,128)S(1)} collective-permute-done((f32[1,128,1280]{1,2,0:T(8,128)S(1)}, f32[1,128,1280]{1,2,0:T(8,128)S(1)}, u32[]{:S(2)}, u32[]{:S(2)}) %collective-permute-start.6) | collective-permute-done | bytes 655392 | tf_op jit(solution)/shard_map/vmap()/ppermute | solution.py:111
  62.3 5.9 %collective-permute-done.11 = f32[1,128,1280]{1,2,0:T(8,128)S(1)} collective-permute-done((f32[1,128,1280]{1,2,0:T(8,128)S(1)}, f32[1,128,1280]{1,2,0:T(8,128)S(1)}, u32[]{:S(2)}, u32[]{:S(2)}) %collective-permute-start.11) | collective-permute-done | bytes 655392 | tf_op jit(solution)/shard_map/vmap()/ppermute | solution.py:111
  68.5 1.3 %collective-permute-start.12 = (f32[1,128,1280]{1,2,0:T(8,128)S(1)}, f32[1,128,1280]{1,2,0:T(8,128)S(1)}, u32[]{:S(2)}, u32[]{:S(2)}) collective-permute-start(f32[1,128,1280]{1,2,0:T(8,128)S(1)} %multiply_add_fusion.2), channel_id=1, source_target_pairs={{9,1},{10,2},{25,17},{26,18}} | collective-permute-start | bytes 1966088 | tf_op jit(solution)/shard_map/vmap()/ppermute | solution.py:111
  71.0 1.3 %collective-permute-start.8 = (f32[1,128,1280]{1,2,0:T(8,128)}, f32[1,128,1280]{1,2,0:T(8,128)}, u32[]{:S(2)}, u32[]{:S(2)}) collective-permute-start(f32[1,128,1280]{1,2,0:T(8,128)} %broadcast_add_fusion.1), channel_id=1, source_target_pairs={{6,2},{14,10},{5,1},{13,9},{22,18},{30,26},{21,17},{29,25}} | collective-permute-start | bytes 1966088 | tf_op jit(solution)/shard_map/vmap()/ppermute | solution.py:111
  72.3 8.6 %collective-permute-done.12 = f32[1,128,1280]{1,2,0:T(8,128)S(1)} collective-permute-done((f32[1,128,1280]{1,2,0:T(8,128)S(1)}, f32[1,128,1280]{1,2,0:T(8,128)S(1)}, u32[]{:S(2)}, u32[]{:S(2)}) %collective-permute-start.12) | collective-permute-done | bytes 655392 | tf_op jit(solution)/shard_map/vmap()/ppermute | solution.py:111
  81.9 2.1 %collective-permute-start.13 = (f32[1,128,1280]{1,2,0:T(8,128)}, f32[1,128,1280]{1,2,0:T(8,128)}, u32[]{:S(2)}, u32[]{:S(2)}) collective-permute-start(f32[1,128,1280]{1,2,0:T(8,128)} %broadcast_add_fusion), channel_id=1, source_target_pairs={{9,13},{1,5},{10,14},{2,6},{25,29},{17,21},{26,30},{18,22}} | collective-permute-start | bytes 1966088 | tf_op jit(solution)/shard_map/vmap()/ppermute | solution.py:111
  84.3 3.5 %collective-permute-done.8 = f32[1,128,1280]{1,2,0:T(8,128)} collective-permute-done((f32[1,128,1280]{1,2,0:T(8,128)}, f32[1,128,1280]{1,2,0:T(8,128)}, u32[]{:S(2)}, u32[]{:S(2)}) %collective-permute-start.8) | collective-permute-done | bytes 655392 | tf_op jit(solution)/shard_map/vmap()/ppermute | solution.py:111
  87.9 3.1 %add_select_fusion.2 = (f32[1,128,1280]{1,2,0:T(8,128)}, f32[1,128,1280]{1,2,0:T(8,128)}) fusion(f32[1,128,1280]{1,2,0:T(8,128)} %get-tuple-element.42, f32[1280]{0:T(1024)S(1)} %broadcast_in_dim.289, pred[]{:T(512)S(6)} %eq.44, f32[1,128,1280]{1,2,0:T(8,128)} %copy-done.14, f32[1,128,1280]{1,2,0:T(8,128)} %collective-permute-done.8, ...), kind=kLoop, calls=%fused_computation.51 | loop fusion | flops 1146880 | bytes 3947521 | tf_op jit(solution)/shard_map/vmap(jit(_where))/select_n | solution.py:155
  91.0 2.3 %collective-permute-start.9 = (f32[1,128,1280]{1,2,0:T(8,128)}, f32[1,128,1280]{1,2,0:T(8,128)}, u32[]{:S(2)}, u32[]{:S(2)}) collective-permute-start(f32[1,128,1280]{1,2,0:T(8,128)} %get-tuple-element.40), channel_id=1, source_target_pairs={{2,0},{6,4},{10,8},{14,12},{1,3},{5,7},{9,11},{13,15},{18,16},{22,... | collective-permute-start | bytes 1966088 | tf_op jit(solution)/shard_map/vmap()/ppermute | solution.py:111
  93.3 2.7 %add_select_fusion = (f32[1,128,1280]{1,2,0:T(8,128)}, f32[1,128,1280]{1,2,0:T(8,128)}) fusion(f32[1,128,1280]{1,2,0:T(8,128)S(1)} %copy-done.2, f32[1280]{0:T(1024)S(1)} %broadcast_in_dim.314, pred[]{:T(512)S(6)} %eq.43, f32[1,128,1280]{1,2,0:T(8,128)S(1)} %copy-done.13, f32[1,128,1280]{1,2,0:T(8,128)} %collective-permute-done.13, f32[1280]{0:T(1024)S(1)} %select_n.488, ...), kind=kLoop, calls=%fused_computation.43 | loop fusion | flops 1146880 | bytes 3947521 | tf_op jit(solution)/shard_map/vmap(jit(_where))/select_n | solution.py:155
  96.0 2.1 %collective-permute-start.14 = (f32[1,128,1280]{1,2,0:T(8,128)}, f32[1,128,1280]{1,2,0:T(8,128)}, u32[]{:S(2)}, u32[]{:S(2)}) collective-permute-start(f32[1,128,1280]{1,2,0:T(8,128)} %get-tuple-element.46), channel_id=1, source_target_pairs={{13,15},{9,11},{5,7},{1,3},{14,12},{10,8},{6,4},{2,0},{29,31},{25,... | collective-permute-start | bytes 1966088 | tf_op jit(solution)/shard_map/vmap()/ppermute | solution.py:111
  99.5 1.3 %collective-permute-start.16 = (f32[40]{0:T(128)S(1)}, f32[40]{0:T(128)S(1)}, u32[]{:S(2)}, u32[]{:S(2)}) collective-permute-start(f32[40]{0:T(128)S(1)} %slice_bitcast_fusion.5), channel_id=1, source_target_pairs={{0,16},{16,0},{1,17},{17,1},{2,18},{18,2},{3,19},{19,3},{4,20},{20... | collective-permute-start | bytes 488 | tf_op jit(solution)/shard_map/ppermute | solution.py:269
  100.8 1.7 %fusion.20 = (f32[1,128,1280]{1,2,0:T(8,128)S(1)}, f32[1,128,1280]{1,2,0:T(8,128)S(1)}) fusion(f32[1,128,1280]{1,2,0:T(8,128)S(1)} %get-tuple-element.43, f32[1280]{0:T(1024)S(1)} %broadcast_in_dim.311, pred[]{:T(512)S(6)} %eq.44, f32[1,128,1280]{1,2,0:T(8,128)} %collective-permute-done.9, f32[1,128,1280]{1,2,0:T(8,128)S(1)} %collective-permute-done.5, ...), kind=kLoop, calls=%fused_computation.49 | loop fusion | flops 1310720 | bytes 3942402 | tf_op jit(solution)/shard_map/vmap(jit(_where))/select_n | solution.py:219
  102.5 4.8 %collective-permute-done.14 = f32[1,128,1280]{1,2,0:T(8,128)} collective-permute-done((f32[1,128,1280]{1,2,0:T(8,128)}, f32[1,128,1280]{1,2,0:T(8,128)}, u32[]{:S(2)}, u32[]{:S(2)}) %collective-permute-start.14) | collective-permute-done | bytes 655392 | tf_op jit(solution)/shard_map/vmap()/ppermute | solution.py:111
  107.3 1.5 %fusion.19 = (f32[1,128,1280]{1,2,0:T(8,128)S(1)}, f32[1,128,1280]{1,2,0:T(8,128)S(1)}) fusion(f32[1,128,1280]{1,2,0:T(8,128)S(1)} %copy-done.1, f32[1280]{0:T(1024)S(1)} %broadcast_in_dim.333, pred[]{:T(512)S(6)} %eq.43, f32[1,128,1280]{1,2,0:T(8,128)} %collective-permute-done.14, f32[1,128,1280]{1,2,0:T(8,128)S(1)} %copy-done.11, ...), kind=kLoop, calls=%fused_computation.41 | loop fusion | flops 1310720 | bytes 3942402 | tf_op jit(solution)/shard_map/vmap(jit(_where))/select_n | solution.py:219
  108.9 9.6 %collective-permute-start.15 = (f32[1,128,2560]{1,2,0:T(8,128)S(1)}, f32[1,128,2560]{1,2,0:T(8,128)S(1)}, u32[]{:S(2)}, u32[]{:S(2)}) collective-permute-start(f32[1,128,2560]{1,2,0:T(8,128)S(1)} %pad_maximum_fusion.1), channel_id=1, source_target_pairs={{0,1},{1,0},{2,3},{3,2},{4,5},{5,4},{6,7},{7,6},{8,9},{9,8},{10,11... | collective-permute-start | bytes 3932168 | tf_op jit(solution)/shard_map/vmap()/ppermute | solution.py:221
  122.4 1.1 copy.49
  (177 shorter events, 30.9 us)
Async XLA Ops:
  0.6 5.2 %copy-start = (bf16[1,128,128]{2,1,0:T(8,128)(2,1)S(1)}, bf16[1,128,128]{2,1,0:T(8,128)(2,1)}, u32[]{:S(2)}) copy-start(bf16[1,128,128]{2,1,0:T(8,128)(2,1)} %param.8) | copy-start | bytes 98308
  0.6 2.6 %copy-start.18 = (bf16[1,128,2560]{2,1,0:T(8,128)(2,1)S(1)}, bf16[1,128,2560]{2,1,0:T(8,128)(2,1)}, u32[]{:S(2)}) copy-start(bf16[1,128,2560]{2,1,0:T(8,128)(2,1)} %param.6) | copy-start | bytes 1966084
  3.7 1.8 %copy-start.19 = (bf16[1,128,128]{2,1,0:T(8,128)(2,1)S(1)}, bf16[1,128,128]{2,1,0:T(8,128)(2,1)}, u32[]{:S(2)}) copy-start(bf16[1,128,128]{2,1,0:T(8,128)(2,1)} %param.9) | copy-start | bytes 98308
  5.5 17.5 %collective-permute-start = (f32[1,17,40]{2,1,0:T(8,128)}, f32[1,17,40]{2,1,0:T(8,128)S(1)}, u32[]{:S(2)}, u32[]{:S(2)}) collective-permute-start(f32[1,17,40]{2,1,0:T(8,128)} %pad_maximum_fusion.2), channel_id=1, source_target_pairs={{0,1},{1,0},{2,3},{3,2},{4,5},{5,4},{6,7},{7,6},{8,9},{9,8},{10,11... | collective-permute-start | bytes 8168 | tf_op jit(solution)/shard_map/vmap()/ppermute | solution.py:66
  6.3 5.0 %copy-start.8 = (bf16[1,128,2560]{1,2,0:T(8,128)(2,1)S(1)}, bf16[1,128,2560]{1,2,0:T(8,128)(2,1)}, u32[]{:S(2)}) copy-start(bf16[1,128,2560]{1,2,0:T(8,128)(2,1)} %copy-done.7) | copy-start | bytes 1966084
  7.5 27.2 %collective-permute-start.4 = (f32[1,128,2560]{1,2,0:T(8,128)}, f32[1,128,2560]{1,2,0:T(8,128)}, u32[]{:S(2)}, u32[]{:S(2)}) collective-permute-start(f32[1,128,2560]{1,2,0:T(8,128)} %pad_maximum_fusion), channel_id=1, source_target_pairs={{0,1},{1,0},{2,3},{3,2},{4,5},{5,4},{6,7},{7,6},{8,9},{9,8},{10,11... | collective-permute-start | bytes 3932168 | tf_op jit(solution)/shard_map/vmap()/ppermute | solution.py:204
  20.2 5.2 %copy-start.21 = (pred[16]{0:T(512)(128)(4,1)S(1)}, pred[16]{0:T(512)(128)(4,1)}, u32[]{:S(2)}) copy-start(pred[16]{0:T(512)(128)(4,1)} %compare_and_fusion.2) | copy-start | bytes 52
  20.2 5.2 %copy-start.22 = (pred[16]{0:T(512)(128)(4,1)S(1)}, pred[16]{0:T(512)(128)(4,1)}, u32[]{:S(2)}) copy-start(pred[16]{0:T(512)(128)(4,1)} %compare_and_fusion) | copy-start | bytes 52
  23.0 3.5 %collective-permute-start.1 = (f32[1,17,40]{2,1,0:T(8,128)S(1)}, f32[1,17,40]{2,1,0:T(8,128)S(1)}, u32[]{:S(2)}, u32[]{:S(2)}) collective-permute-start(f32[1,17,40]{2,1,0:T(8,128)S(1)} %fusion.79), channel_id=1, source_target_pairs={{0,2},{1,3},{2,0},{3,1},{4,6},{5,7},{6,4},{7,5},{8,10},{9,11},{10,... | collective-permute-start | bytes 8168 | tf_op jit(solution)/shard_map/vmap()/ppermute | solution.py:66
  26.5 2.9 %collective-permute-start.2 = (f32[1,17,40]{2,1,0:T(8,128)S(1)}, f32[1,17,40]{2,1,0:T(8,128)S(1)}, u32[]{:S(2)}, u32[]{:S(2)}) collective-permute-start(f32[1,17,40]{2,1,0:T(8,128)S(1)} %add.218), channel_id=1, source_target_pairs={{0,4},{1,5},{2,6},{3,7},{4,0},{5,1},{6,2},{7,3},{8,12},{9,13},{10,... | collective-permute-start | bytes 8168 | tf_op jit(solution)/shard_map/vmap()/ppermute | solution.py:66
  29.5 3.6 %collective-permute-start.3 = (f32[1,17,40]{2,1,0:T(8,128)S(1)}, f32[1,17,40]{2,1,0:T(8,128)S(1)}, u32[]{:S(2)}, u32[]{:S(2)}) collective-permute-start(f32[1,17,40]{2,1,0:T(8,128)S(1)} %add.222), channel_id=1, source_target_pairs={{0,8},{1,9},{2,10},{3,11},{4,12},{5,13},{6,14},{7,15},{8,0},{9,1},... | collective-permute-start | bytes 8168 | tf_op jit(solution)/shard_map/vmap()/ppermute | solution.py:66
  37.8 18.7 %copy-start.2 = (f32[1,128,1280]{1,2,0:T(8,128)S(1)}, f32[1,128,1280]{1,2,0:T(8,128)}, u32[]{:S(2)}) copy-start(f32[1,128,1280]{1,2,0:T(8,128)} %get-tuple-element.50) | copy-start | bytes 1966084
  37.8 11.7 %collective-permute-start.5 = (f32[1,128,1280]{1,2,0:T(8,128)}, f32[1,128,1280]{1,2,0:T(8,128)S(1)}, u32[]{:S(2)}, u32[]{:S(2)}) collective-permute-start(f32[1,128,1280]{1,2,0:T(8,128)} %get-tuple-element.42), channel_id=1, source_target_pairs={{0,2},{4,6},{8,10},{12,14},{3,1},{7,5},{11,9},{15,13},{16,18},{20,... | collective-permute-start | bytes 1966088 | tf_op jit(solution)/shard_map/vmap()/ppermute | solution.py:111
  39.5 17.0 %collective-permute-start.10 = (f32[1,128,1280]{1,2,0:T(8,128)}, f32[1,128,1280]{1,2,0:T(8,128)S(1)}, u32[]{:S(2)}, u32[]{:S(2)}) collective-permute-start(f32[1,128,1280]{1,2,0:T(8,128)} %get-tuple-element.50), channel_id=1, source_target_pairs={{15,13},{11,9},{7,5},{3,1},{12,14},{8,10},{4,6},{0,2},{31,29},{27,... | collective-permute-start | bytes 1966088 | tf_op jit(solution)/shard_map/vmap()/ppermute | solution.py:111
  51.0 10.4 %collective-permute-start.6 = (f32[1,128,1280]{1,2,0:T(8,128)S(1)}, f32[1,128,1280]{1,2,0:T(8,128)S(1)}, u32[]{:S(2)}, u32[]{:S(2)}) collective-permute-start(f32[1,128,1280]{1,2,0:T(8,128)S(1)} %add_select_fusion.3), channel_id=1, source_target_pairs={{2,6},{10,14},{1,5},{9,13},{18,22},{26,30},{17,21},{25,29}} | collective-permute-start | bytes 1966088 | tf_op jit(solution)/shard_map/vmap()/ppermute | solution.py:111
  56.5 5.1 %copy-start.10 = (f32[1,128,1280]{1,2,0:T(8,128)}, f32[1,128,1280]{1,2,0:T(8,128)S(1)}, u32[]{:S(2)}) copy-start(f32[1,128,1280]{1,2,0:T(8,128)S(1)} %collective-permute-done.10) | copy-start | bytes 1966084
  56.9 11.3 %collective-permute-start.11 = (f32[1,128,1280]{1,2,0:T(8,128)S(1)}, f32[1,128,1280]{1,2,0:T(8,128)S(1)}, u32[]{:S(2)}, u32[]{:S(2)}) collective-permute-start(f32[1,128,1280]{1,2,0:T(8,128)S(1)} %add_select_fusion.1), channel_id=1, source_target_pairs={{13,9},{5,1},{14,10},{6,2},{29,25},{21,17},{30,26},{22,18}} | collective-permute-start | bytes 1966088 | tf_op jit(solution)/shard_map/vmap()/ppermute | solution.py:111
  61.4 7.1 %copy-start.14 = (f32[1,128,1280]{1,2,0:T(8,128)}, f32[1,128,1280]{1,2,0:T(8,128)S(1)}, u32[]{:S(2)}) copy-start(f32[1,128,1280]{1,2,0:T(8,128)S(1)} %collective-permute-done.6) | copy-start | bytes 1966084
  61.6 8.3 %collective-permute-start.7 = (f32[1,128,1280]{1,2,0:T(8,128)S(1)}, f32[1,128,1280]{1,2,0:T(8,128)S(1)}, u32[]{:S(2)}, u32[]{:S(2)}) collective-permute-start(f32[1,128,1280]{1,2,0:T(8,128)S(1)} %multiply_add_fusion.5), channel_id=1, source_target_pairs={{6,14},{5,13},{22,30},{21,29}} | collective-permute-start | bytes 1966088 | tf_op jit(solution)/shard_map/vmap()/ppermute | solution.py:111
  68.3 2.7 %copy-start.12 = (f32[1,128,1280]{1,2,0:T(8,128)}, f32[1,128,1280]{1,2,0:T(8,128)S(1)}, u32[]{:S(2)}) copy-start(f32[1,128,1280]{1,2,0:T(8,128)S(1)} %collective-permute-done.11) | copy-start | bytes 1966084
  68.5 12.3 %collective-permute-start.12 = (f32[1,128,1280]{1,2,0:T(8,128)S(1)}, f32[1,128,1280]{1,2,0:T(8,128)S(1)}, u32[]{:S(2)}, u32[]{:S(2)}) collective-permute-start(f32[1,128,1280]{1,2,0:T(8,128)S(1)} %multiply_add_fusion.2), channel_id=1, source_target_pairs={{9,1},{10,2},{25,17},{26,18}} | collective-permute-start | bytes 1966088 | tf_op jit(solution)/shard_map/vmap()/ppermute | solution.py:111
  71.0 16.9 %collective-permute-start.8 = (f32[1,128,1280]{1,2,0:T(8,128)}, f32[1,128,1280]{1,2,0:T(8,128)}, u32[]{:S(2)}, u32[]{:S(2)}) collective-permute-start(f32[1,128,1280]{1,2,0:T(8,128)} %broadcast_add_fusion.1), channel_id=1, source_target_pairs={{6,2},{14,10},{5,1},{13,9},{22,18},{30,26},{21,17},{29,25}} | collective-permute-start | bytes 1966088 | tf_op jit(solution)/shard_map/vmap()/ppermute | solution.py:111
  81.9 11.4 %collective-permute-start.13 = (f32[1,128,1280]{1,2,0:T(8,128)}, f32[1,128,1280]{1,2,0:T(8,128)}, u32[]{:S(2)}, u32[]{:S(2)}) collective-permute-start(f32[1,128,1280]{1,2,0:T(8,128)} %broadcast_add_fusion), channel_id=1, source_target_pairs={{9,13},{1,5},{10,14},{2,6},{25,29},{17,21},{26,30},{18,22}} | collective-permute-start | bytes 1966088 | tf_op jit(solution)/shard_map/vmap()/ppermute | solution.py:111
  84.3 8.9 %copy-start.13 = (f32[1,128,1280]{1,2,0:T(8,128)S(1)}, f32[1,128,1280]{1,2,0:T(8,128)}, u32[]{:S(2)}) copy-start(f32[1,128,1280]{1,2,0:T(8,128)} %copy-done.12) | copy-start | bytes 1966084
  91.0 9.8 %copy-start.15 = (f32[1,128,1280]{1,2,0:T(8,128)S(1)}, f32[1,128,1280]{1,2,0:T(8,128)}, u32[]{:S(2)}) copy-start(f32[1,128,1280]{1,2,0:T(8,128)} %get-tuple-element.41) | copy-start | bytes 1966084
  91.0 9.8 %collective-permute-start.9 = (f32[1,128,1280]{1,2,0:T(8,128)}, f32[1,128,1280]{1,2,0:T(8,128)}, u32[]{:S(2)}, u32[]{:S(2)}) collective-permute-start(f32[1,128,1280]{1,2,0:T(8,128)} %get-tuple-element.40), channel_id=1, source_target_pairs={{2,0},{6,4},{10,8},{14,12},{1,3},{5,7},{9,11},{13,15},{18,16},{22,... | collective-permute-start | bytes 1966088 | tf_op jit(solution)/shard_map/vmap()/ppermute | solution.py:111
  96.0 11.3 %collective-permute-start.14 = (f32[1,128,1280]{1,2,0:T(8,128)}, f32[1,128,1280]{1,2,0:T(8,128)}, u32[]{:S(2)}, u32[]{:S(2)}) collective-permute-start(f32[1,128,1280]{1,2,0:T(8,128)} %get-tuple-element.46), channel_id=1, source_target_pairs={{13,15},{9,11},{5,7},{1,3},{14,12},{10,8},{6,4},{2,0},{29,31},{25,... | collective-permute-start | bytes 1966088 | tf_op jit(solution)/shard_map/vmap()/ppermute | solution.py:111
  99.5 19.0 %collective-permute-start.16 = (f32[40]{0:T(128)S(1)}, f32[40]{0:T(128)S(1)}, u32[]{:S(2)}, u32[]{:S(2)}) collective-permute-start(f32[40]{0:T(128)S(1)} %slice_bitcast_fusion.5), channel_id=1, source_target_pairs={{0,16},{16,0},{1,17},{17,1},{2,18},{18,2},{3,19},{19,3},{4,20},{20... | collective-permute-start | bytes 488 | tf_op jit(solution)/shard_map/ppermute | solution.py:269
  100.8 6.5 %copy-start.1 = (f32[1,128,1280]{1,2,0:T(8,128)S(1)}, f32[1,128,1280]{1,2,0:T(8,128)}, u32[]{:S(2)}) copy-start(f32[1,128,1280]{1,2,0:T(8,128)} %get-tuple-element.51) | copy-start | bytes 1966084
  100.8 6.5 %copy-start.11 = (f32[1,128,1280]{1,2,0:T(8,128)S(1)}, f32[1,128,1280]{1,2,0:T(8,128)}, u32[]{:S(2)}) copy-start(f32[1,128,1280]{1,2,0:T(8,128)} %copy-done.10) | copy-start | bytes 1966084
  100.8 6.5 %copy-start.16 = (f32[1,128,1280]{1,2,0:T(8,128)S(1)}, f32[1,128,1280]{1,2,0:T(8,128)}, u32[]{:S(2)}) copy-start(f32[1,128,1280]{1,2,0:T(8,128)} %get-tuple-element.47) | copy-start | bytes 1966084
  108.9 12.2 %collective-permute-start.15 = (f32[1,128,2560]{1,2,0:T(8,128)S(1)}, f32[1,128,2560]{1,2,0:T(8,128)S(1)}, u32[]{:S(2)}, u32[]{:S(2)}) collective-permute-start(f32[1,128,2560]{1,2,0:T(8,128)S(1)} %pad_maximum_fusion.1), channel_id=1, source_target_pairs={{0,1},{1,0},{2,3},{3,2},{4,5},{5,4},{6,7},{7,6},{8,9},{9,8},{10,11... | collective-permute-start | bytes 3932168 | tf_op jit(solution)/shard_map/vmap()/ppermute | solution.py:221
  (8 other events, 9.5 us)

commit v8 on v7

--- a/solution.py
+++ b/solution.py
@@ -68,13 +68,6 @@
     return tables
 
 
-def range_gain(table, count, low, high, reverse):
-    rows = jnp.arange(count)
-    virtual = count - 1 - rows if reverse else rows
-    inside = (virtual >= low) & (virtual <= high)
-    return jnp.exp(jnp.sum(jnp.where(inside[:, None], table[:count], 0.0), axis=0))
-
-
 def take_half(array, upper):
     half = array.shape[-1] // 2
     return jnp.where(upper, array[..., half:], array[..., :half])
@@ -93,6 +86,7 @@
         self.index = count - 1 - position if reverse else position
         self.upper = self.index % 2 == 1
         self.pair = self.index // 2
+        self.pyramids = {}
 
     def actual(self, pairs):
         if self.reverse:
@@ -102,8 +96,15 @@
     def pair_pairs(self, pairs):
         return self.actual([(2 * a + j, 2 * b + j) for a, b in pairs for j in (0, 1)])
 
-    def gain(self, table_index, low_block, high_block):
-        full = range_gain(self.tables[table_index], self.count, low_block, high_block, self.reverse)
+    def gain(self, table_index, low_block, size):
+        key = (table_index % len(self.tables), size)
+        if key not in self.pyramids:
+            rows = self.tables[key[0]][: self.count]
+            if self.reverse:
+                rows = rows[::-1]
+            grouped = rows.reshape(self.count // size, size, rows.shape[-1]).sum(axis=1)
+            self.pyramids[key] = jnp.exp(grouped)
+        full = lax.dynamic_index_in_dim(self.pyramids[key], low_block // size, keepdims=False)
         return spread_heads(take_half(full, self.upper), self.head_width)[..., None, :]
 
 
@@ -130,9 +131,9 @@
             upper = [(2 * a + 1, 2 * b + 1) for a, b in pairs]
         return self.way.actual(lower + upper)
 
-    def pair_gain(self, level, low_pair, high_pair):
+    def pair_gain(self, level, low_pair, pair_span):
         table = min(level + 2, len(self.way.tables) - 1)
-        return self.way.gain(table, 2 * low_pair, 2 * high_pair + 1)
+        return self.way.gain(table, 2 * low_pair, 2 * pair_span)
 
     def up_send(self, level):
         span = 1 << level
@@ -143,16 +144,16 @@
         span = 1 << level
         if self.flip and level == 0:
             pair = self.way.pair
-            kept_upper = self.pair_gain(0, pair ^ 1, pair ^ 1) * total + lower
-            kept_lower = self.pair_gain(0, pair, pair) * lower + total
+            kept_upper = self.pair_gain(0, pair ^ 1, 1) * total + lower
+            kept_lower = self.pair_gain(0, pair, 1) * lower + total
             return jnp.where(self.way.upper, kept_upper, kept_lower)
-        return self.pair_gain(level, self.role - span + 1, self.role) * lower + total
+        return self.pair_gain(level, self.role - span + 1, span) * lower + total
 
     def down_send(self, level, prefix, pair_total):
         span = 1 << level
         if self.flip and level == 0:
             pair = self.way.pair
-            sent = jnp.where(self.way.upper, self.pair_gain(0, pair, pair) * prefix + pair_total, prefix)
+            sent = jnp.where(self.way.upper, self.pair_gain(0, pair, 1) * prefix + pair_total, prefix)
             pairs = [(2 * (a + 1), 2 * a) for a in range(0, self.pair_count, 2)]
             pairs += [(2 * a + 1, 2 * (a + 1) + 1) for a in range(0, self.pair_count, 2)]
             return sent, self.way.actual(pairs)
@@ -163,12 +164,12 @@
         span = 1 << level
         if self.flip and level == 0:
             pair = self.way.pair
-            grown = self.pair_gain(self.level_count, pair - 1, pair - 1) * prefix + lowers[0]
+            grown = self.pair_gain(self.level_count, pair - 1, 1) * prefix + lowers[0]
             odd = pair % 2 == 1
             return jnp.where(self.way.upper, jnp.where(odd, got, prefix), jnp.where(odd, grown, got))
         if got is not None:
             prefix = prefix + got
-        lower_gain = self.pair_gain(self.level_count, self.role - 2 * span + 1, self.role - span)
+        lower_gain = self.pair_gain(self.level_count, self.role - 2 * span + 1, span)
         lower_gain = jnp.where(self.role % (2 * span) == 2 * span - 1, lower_gain, 1.0)
         return lower_gain * prefix + lowers[level]
 
@@ -210,12 +211,12 @@
         low_block = jnp.where(way.upper, other, own)
         high_block = jnp.where(way.upper, own, other)
         lows.append(low_block)
-        totals.append(way.gain(1, 2 * way.pair + 1, 2 * way.pair + 1) * low_block + high_block)
+        totals.append(way.gain(1, 2 * way.pair + 1, 1) * low_block + high_block)
     pair_prefixes = pair_scans(ways, totals)
     lifted_parts = []
     keep_parts = []
     for way, pair_prefix, low_block in zip(ways, pair_prefixes, lows):
-        lifted = way.gain(1, 2 * way.pair, 2 * way.pair) * pair_prefix + low_block
+        lifted = way.gain(1, 2 * way.pair, 1) * pair_prefix + low_block
         lifted_parts.append(jnp.where(way.upper, pair_prefix, lifted))
         keep_parts.append(jnp.where(way.upper, lifted, pair_prefix))
     got = lax.ppermute(jnp.concatenate(lifted_parts, -1), "ctx", [(i, i ^ 1) for i in range(count)])

time: 126 us -> 125 us (level)
  local copies, waits for them, and re-layouts: 7.29 us -> 14.5 us
  other arithmetic: 34.8 us -> 28 us
  starting transfers between devices: 34.1 us -> 31.7 us
    and x16 -> x0, other arithmetic: 8.79 us -> none  [range_gain(): inside = (virtual >= low) & (virtual <= high)]
    squeeze x0 -> x12, local copies, waits for them, and re-layouts: none -> 5.25 us  [gain(): lax.dynamic_index_in_dim(self.pyramids[key], low_block // size, keepdims=...]
    concatenate x0 -> x8, other arithmetic: none -> 3.9 us  [gain(): lax.dynamic_index_in_dim(self.pyramids[key], low_block // size, keepdims=...]
    reduce_sum x4 -> x10, other arithmetic: 3.04 us -> 0.19 us  [gain(): grouped = rows.reshape(self.count // size, size, rows.shape[-1]).sum(axis=1)]
    unnamed x49 -> x59, local copies, waits for them, and re-layouts: 4.64 us -> 6.54 us
    add x3, other arithmetic: 3.62 us -> 5.04 us  [the longest x1 2.63 us: carried_pair(): totals.append(way.gain(1, 2 * way.pair + 1, 1) * low_block + high_block)]
  transfers between devices with their start and end apart: 17 -> 17, of which waited for: 8 -> 9; matrix products, arithmetic and copies ran while one was open for 31% -> 31% of each run, Pallas kernels for 0% -> 0%
where the time goes in v8:
time: 125 us; the launch traced here: 124 us
  waiting for transfers between devices  37.3 us (30%)
  starting transfers between devices  31.7 us (25%)
  other arithmetic  28 us (22%)
  local copies, waits for them, and re-layouts  14.5 us (12%)
  matrix products  10.5 us (8%)
  between operations  1.95 us (2%)
    ppermute x10, waiting for transfers between devices, exchange(): lax.ppermute(p, 'ctx', pairs)  37.1 us
    ppermute x10, starting transfers between devices, exchange(): lax.ppermute(p, 'ctx', pairs)  15.6 us
    ppermute x1, starting transfers between devices, carried_pair(): lax.ppermute(jnp.concatenate(lifted_parts, -1), 'ctx', [(i, i ^ 1) for i...  8.33 us
    unnamed x59, local copies, waits for them, and re-layouts  6.54 us
    ppermute x4, starting transfers between devices, gather_totals(): table = table + lax.ppermute(table, 'ctx', xor_pairs(count, bit))  6.07 us
    select_n x2, other arithmetic, down_send(): jnp.where(self.way.upper, self.pair_gain(0, pair, 1) * prefix + pair_tota...  5.85 us
    squeeze x12, local copies, waits for them, and re-layouts, gain(): lax.dynamic_index_in_dim(self.pyramids[key], low_block // size, keepdims=...  5.25 us
    concatenate x8, other arithmetic, gain(): lax.dynamic_index_in_dim(self.pyramids[key], low_block // size, keepdims=...  3.9 us
  transfers between devices with their start and end apart: 17, of which 9 were waited for; matrix products, arithmetic and copies ran while one was open for 31% of the time, Pallas kernels for 0%

profile of v8, /device:TPU:1, one launch (start us, length us, event | category | flops | bytes accessed | tf_op | source)
XLA Modules:
  0.0 124.0 jit_solution(14138036418579617687)
XLA Ops:
  1.8 1.4 %copy.44 = bf16[1,128,2560]{1,2,0:T(8,128)(2,1)S(1)} copy(bf16[1,128,2560]{2,1,0:T(8,128)(2,1)} %param.7) | data formatting | bytes 1310720 | tf_op args[1]
  6.4 1.1 pad_maximum_fusion
  8.0 2.3 %convert_reduce_fusion = bf16[128,128]{1,0:T(8,128)(2,1)S(1)} fusion(f32[40,128]{1,0:T(8,128)S(1)} %copy.42, pred[128,128]{1,0:T(8,128)(4,1)S(1)} %iota_compare_fusion, bf16[128,40,64]{0,2,1:T(8,128)(2,1)S(1)} %bitcast.249, bf16[128,40,64]{0,2,1:T(8,128)(2,1)} %bitcast.252), kind=kOutput, calls=%fused_computation.2 | convolution fusion | flops 88457216 | bytes 1380352 | tf_op jit(solution)/shard_map/vmap(ihp,jhp->hij)/dot_general | solution.py:45
  15.3 2.8 %fusion = f32[1,128,40,64]{1,3,2,0:T(8,128)} fusion(bf16[128,40,64]{0,2,1:T(8,128)(2,1)S(1)} %bitcast.250, f32[40,128]{1,0:T(8,128)S(1)} %copy.42, f32[128,128]{1,0:T(8,128)S(1)} %fusion.52, pred[128,128]{1,0:T(8,128)(4,1)S(1)} %iota_compare_fusion, f32[40]{0:T(128)} %param.11, bf16[1,128,40,64]{1,3,2,0:T(8,128)(2,1)S(1)} %bitcast.251), kind=kOutput, calls=%fused_computation.12 | convolution fusion | flops 88145920 | bytes 2724000 | tf_op jit(solution)/shard_map/vmap(hij,ihp->jhp)/dot_general | solution.py:51
  18.1 2.4 %collective-permute-start.1 = (f32[1,17,40]{2,1,0:T(8,128)S(1)}, f32[1,17,40]{2,1,0:T(8,128)S(1)}, u32[]{:S(2)}, u32[]{:S(2)}) collective-permute-start(f32[1,17,40]{2,1,0:T(8,128)S(1)} %fusion.99), channel_id=1, source_target_pairs={{0,2},{1,3},{2,0},{3,1},{4,6},{5,7},{6,4},{7,5},{8,10},{9,11},{10,... | collective-permute-start | bytes 8168 | tf_op jit(solution)/shard_map/vmap()/ppermute | solution.py:66
  22.6 1.4 %collective-permute-start.2 = (f32[1,17,40]{2,1,0:T(8,128)S(1)}, f32[1,17,40]{2,1,0:T(8,128)S(1)}, u32[]{:S(2)}, u32[]{:S(2)}) collective-permute-start(f32[1,17,40]{2,1,0:T(8,128)S(1)} %add.259), channel_id=1, source_target_pairs={{0,4},{1,5},{2,6},{3,7},{4,0},{5,1},{6,2},{7,3},{8,12},{9,13},{10,... | collective-permute-start | bytes 8168 | tf_op jit(solution)/shard_map/vmap()/ppermute | solution.py:66
  25.2 2.3 %collective-permute-start.3 = (f32[1,17,40]{2,1,0:T(8,128)S(1)}, f32[1,17,40]{2,1,0:T(8,128)S(1)}, u32[]{:S(2)}, u32[]{:S(2)}) collective-permute-start(f32[1,17,40]{2,1,0:T(8,128)S(1)} %add.262), channel_id=1, source_target_pairs={{0,8},{1,9},{2,10},{3,11},{4,12},{5,13},{6,14},{7,15},{8,0},{9,1},... | collective-permute-start | bytes 8168 | tf_op jit(solution)/shard_map/vmap()/ppermute | solution.py:66
  32.7 2.6 %select_add_fusion.1 = (f32[1,128,1280]{1,2,0:T(8,128)S(1)}, f32[1,128,1280]{1,2,0:T(8,128)S(1)}, f32[1,128,1280]{1,2,0:T(8,128)S(1)}, f32[1,128,1280]{1,2,0:T(8,128)}) fusion(f32[1,128,2560]{1,2,0:T(8,128)} %collective-permute-done.4, f32[1280]{0:T(1024)S(1)} %broadcast_in_dim.231, pred[]{:T(512)S(6)} %eq.44, ...), kind=kLoop, calls=%fused_computation.55 | loop fusion | flops 1638400 | bytes 6563842 | tf_op jit(solution)/shard_map/vmap()/add | solution.py:214
  35.3 1.3 %collective-permute-start.5 = (f32[1,128,1280]{1,2,0:T(8,128)S(1)}, f32[1,128,1280]{1,2,0:T(8,128)S(1)}, u32[]{:S(2)}, u32[]{:S(2)}) collective-permute-start(f32[1,128,1280]{1,2,0:T(8,128)S(1)} %get-tuple-element.202), channel_id=1, source_target_pairs={{0,2},{4,6},{8,10},{12,14},{3,1},{7,5},{11,9},{15,13},{16,18},{20,... | collective-permute-start | bytes 1966088 | tf_op jit(solution)/shard_map/vmap()/ppermute | solution.py:112
  36.8 1.3 %collective-permute-start.10 = (f32[1,128,1280]{1,2,0:T(8,128)S(1)}, f32[1,128,1280]{1,2,0:T(8,128)S(1)}, u32[]{:S(2)}, u32[]{:S(2)}) collective-permute-start(f32[1,128,1280]{1,2,0:T(8,128)S(1)} %get-tuple-element.210), channel_id=1, source_target_pairs={{15,13},{11,9},{7,5},{3,1},{12,14},{8,10},{4,6},{0,2},{31,29},{27,... | collective-permute-start | bytes 1966088 | tf_op jit(solution)/shard_map/vmap()/ppermute | solution.py:112
  38.1 8.6 %collective-permute-done.5 = f32[1,128,1280]{1,2,0:T(8,128)S(1)} collective-permute-done((f32[1,128,1280]{1,2,0:T(8,128)S(1)}, f32[1,128,1280]{1,2,0:T(8,128)S(1)}, u32[]{:S(2)}, u32[]{:S(2)}) %collective-permute-start.5) | collective-permute-done | bytes 655392 | tf_op jit(solution)/shard_map/vmap()/ppermute | solution.py:112
  47.1 3.2 %collective-permute-start.6 = (f32[1,128,1280]{1,2,0:T(8,128)S(1)}, f32[1,128,1280]{1,2,0:T(8,128)S(1)}, u32[]{:S(2)}, u32[]{:S(2)}) collective-permute-start(f32[1,128,1280]{1,2,0:T(8,128)S(1)} %add_select_fusion.3), channel_id=1, source_target_pairs={{2,6},{10,14},{1,5},{9,13},{18,22},{26,30},{17,21},{25,29}} | collective-permute-start | bytes 1966088 | tf_op jit(solution)/shard_map/vmap()/ppermute | solution.py:112
  50.4 3.3 %collective-permute-done.10 = f32[1,128,1280]{1,2,0:T(8,128)S(1)} collective-permute-done((f32[1,128,1280]{1,2,0:T(8,128)S(1)}, f32[1,128,1280]{1,2,0:T(8,128)S(1)}, u32[]{:S(2)}, u32[]{:S(2)}) %collective-permute-start.10) | collective-permute-done | bytes 655392 | tf_op jit(solution)/shard_map/vmap()/ppermute | solution.py:112
  54.1 1.3 %collective-permute-start.11 = (f32[1,128,1280]{1,2,0:T(8,128)S(1)}, f32[1,128,1280]{1,2,0:T(8,128)}, u32[]{:S(2)}, u32[]{:S(2)}) collective-permute-start(f32[1,128,1280]{1,2,0:T(8,128)S(1)} %add_select_fusion.1), channel_id=1, source_target_pairs={{13,9},{5,1},{14,10},{6,2},{29,25},{21,17},{30,26},{22,18}} | collective-permute-start | bytes 1966088 | tf_op jit(solution)/shard_map/vmap()/ppermute | solution.py:112
  55.4 2.4 %collective-permute-done.6 = f32[1,128,1280]{1,2,0:T(8,128)S(1)} collective-permute-done((f32[1,128,1280]{1,2,0:T(8,128)S(1)}, f32[1,128,1280]{1,2,0:T(8,128)S(1)}, u32[]{:S(2)}, u32[]{:S(2)}) %collective-permute-start.6) | collective-permute-done | bytes 655392 | tf_op jit(solution)/shard_map/vmap()/ppermute | solution.py:112
  59.8 5.7 %collective-permute-done.11 = f32[1,128,1280]{1,2,0:T(8,128)} collective-permute-done((f32[1,128,1280]{1,2,0:T(8,128)S(1)}, f32[1,128,1280]{1,2,0:T(8,128)}, u32[]{:S(2)}, u32[]{:S(2)}) %collective-permute-start.11) | collective-permute-done | bytes 655392 | tf_op jit(solution)/shard_map/vmap()/ppermute | solution.py:112
  65.6 1.3 %multiply_add_fusion.2 = f32[1,128,1280]{1,2,0:T(8,128)S(1)} fusion(f32[1,128,1280]{1,2,0:T(8,128)S(1)} %add_select_fusion.1, f32[1,128,1280]{1,2,0:T(8,128)} %collective-permute-done.11, f32[1280]{0:T(1024)S(1)} %broadcast_in_dim.249), kind=kLoop, calls=%fused_computation.45 | loop fusion | flops 327680 | bytes 1971200 | tf_op jit(solution)/shard_map/vmap()/add | solution.py:150
  66.9 1.4 %collective-permute-start.12 = (f32[1,128,1280]{1,2,0:T(8,128)S(1)}, f32[1,128,1280]{1,2,0:T(8,128)S(1)}, u32[]{:S(2)}, u32[]{:S(2)}) collective-permute-start(f32[1,128,1280]{1,2,0:T(8,128)S(1)} %multiply_add_fusion.2), channel_id=1, source_target_pairs={{9,1},{10,2},{25,17},{26,18}} | collective-permute-start | bytes 1966088 | tf_op jit(solution)/shard_map/vmap()/ppermute | solution.py:112
  69.4 1.3 %collective-permute-start.8 = (f32[1,128,1280]{1,2,0:T(8,128)}, f32[1,128,1280]{1,2,0:T(8,128)}, u32[]{:S(2)}, u32[]{:S(2)}) collective-permute-start(f32[1,128,1280]{1,2,0:T(8,128)} %broadcast_add_fusion.1), channel_id=1, source_target_pairs={{6,2},{14,10},{5,1},{13,9},{22,18},{30,26},{21,17},{29,25}} | collective-permute-start | bytes 1966088 | tf_op jit(solution)/shard_map/vmap()/ppermute | solution.py:112
  71.0 8.4 %collective-permute-done.12 = f32[1,128,1280]{1,2,0:T(8,128)S(1)} collective-permute-done((f32[1,128,1280]{1,2,0:T(8,128)S(1)}, f32[1,128,1280]{1,2,0:T(8,128)S(1)}, u32[]{:S(2)}, u32[]{:S(2)}) %collective-permute-start.12) | collective-permute-done | bytes 655392 | tf_op jit(solution)/shard_map/vmap()/ppermute | solution.py:112
  79.4 1.1 broadcast_add_fusion
  80.5 2.1 %collective-permute-start.13 = (f32[1,128,1280]{1,2,0:T(8,128)}, f32[1,128,1280]{1,2,0:T(8,128)}, u32[]{:S(2)}, u32[]{:S(2)}) collective-permute-start(f32[1,128,1280]{1,2,0:T(8,128)} %broadcast_add_fusion), channel_id=1, source_target_pairs={{9,13},{1,5},{10,14},{2,6},{25,29},{17,21},{26,30},{18,22}} | collective-permute-start | bytes 1966088 | tf_op jit(solution)/shard_map/vmap()/ppermute | solution.py:112
  83.0 3.4 %collective-permute-done.8 = f32[1,128,1280]{1,2,0:T(8,128)} collective-permute-done((f32[1,128,1280]{1,2,0:T(8,128)}, f32[1,128,1280]{1,2,0:T(8,128)}, u32[]{:S(2)}, u32[]{:S(2)}) %collective-permute-start.8) | collective-permute-done | bytes 655392 | tf_op jit(solution)/shard_map/vmap()/ppermute | solution.py:112
  86.4 2.9 %add_select_fusion.2 = (f32[1,128,1280]{1,2,0:T(8,128)}, f32[1,128,1280]{1,2,0:T(8,128)}) fusion(f32[1,128,1280]{1,2,0:T(8,128)S(1)} %copy-done.5, f32[1280]{0:T(1024)S(1)} %broadcast_in_dim.217, pred[]{:T(512)S(6)} %eq.44, f32[1,128,1280]{1,2,0:T(8,128)} %copy-done.17, f32[1,128,1280]{1,2,0:T(8,128)} %collective-permute-done.8, f32[1280]{0:T(1024)S(1)} %select_n.486, ...), kind=kLoop, calls=%fused_computation.51 | loop fusion | flops 1146880 | bytes 3947521 | tf_op jit(solution)/shard_map/vmap(jit(_where))/select_n | solution.py:156
  89.3 1.4 %collective-permute-start.9 = (f32[1,128,1280]{1,2,0:T(8,128)}, f32[1,128,1280]{1,2,0:T(8,128)S(1)}, u32[]{:S(2)}, u32[]{:S(2)}) collective-permute-start(f32[1,128,1280]{1,2,0:T(8,128)} %get-tuple-element.200), channel_id=1, source_target_pairs={{2,0},{6,4},{10,8},{14,12},{1,3},{5,7},{9,11},{13,15},{18,16},{22,... | collective-permute-start | bytes 1966088 | tf_op jit(solution)/shard_map/vmap()/ppermute | solution.py:112
  90.8 2.9 %add_select_fusion = (f32[1,128,1280]{1,2,0:T(8,128)}, f32[1,128,1280]{1,2,0:T(8,128)}) fusion(f32[1,128,1280]{1,2,0:T(8,128)S(1)} %copy-done.3, f32[1280]{0:T(1024)S(1)} %broadcast_in_dim.242, pred[]{:T(512)S(6)} %eq.43, f32[1,128,1280]{1,2,0:T(8,128)} %collective-permute-done.11, f32[1,128,1280]{1,2,0:T(8,128)} %collective-permute-done.13, ...), kind=kLoop, calls=%fused_computation.43 | loop fusion | flops 1146880 | bytes 3947521 | tf_op jit(solution)/shard_map/vmap(jit(_where))/select_n | solution.py:156
  93.7 1.5 %collective-permute-start.14 = (f32[1,128,1280]{1,2,0:T(8,128)}, f32[1,128,1280]{1,2,0:T(8,128)S(1)}, u32[]{:S(2)}, u32[]{:S(2)}) collective-permute-start(f32[1,128,1280]{1,2,0:T(8,128)} %get-tuple-element.206), channel_id=1, source_target_pairs={{13,15},{9,11},{5,7},{1,3},{14,12},{10,8},{6,4},{2,0},{29,31},{25,... | collective-permute-start | bytes 1966088 | tf_op jit(solution)/shard_map/vmap()/ppermute | solution.py:112
  96.3 1.3 %collective-permute-start.16 = (f32[40]{0:T(128)S(1)}, f32[40]{0:T(128)S(1)}, u32[]{:S(2)}, u32[]{:S(2)}) collective-permute-start(f32[40]{0:T(128)S(1)} %slice_bitcast_fusion.5), channel_id=1, source_target_pairs={{0,16},{16,0},{1,17},{17,1},{2,18},{18,2},{3,19},{19,3},{4,20},{20... | collective-permute-start | bytes 488 | tf_op jit(solution)/shard_map/ppermute | solution.py:270
  99.4 1.8 %fusion.20 = (f32[1,128,1280]{1,2,0:T(8,128)S(1)}, f32[1,128,1280]{1,2,0:T(8,128)S(1)}) fusion(f32[1,128,1280]{1,2,0:T(8,128)S(1)} %get-tuple-element.203, f32[1280]{0:T(1024)S(1)} %broadcast_in_dim.239, pred[]{:T(512)S(6)} %eq.44, f32[1,128,1280]{1,2,0:T(8,128)} %copy-done.21, f32[1,128,1280]{1,2,0:T(8,128)S(1)} %copy-done.16, ...), kind=kLoop, calls=%fused_computation.49 | loop fusion | flops 1310720 | bytes 3942402 | tf_op jit(solution)/shard_map/vmap(jit(_where))/select_n | solution.py:220
  101.3 4.3 %collective-permute-done.14 = f32[1,128,1280]{1,2,0:T(8,128)S(1)} collective-permute-done((f32[1,128,1280]{1,2,0:T(8,128)}, f32[1,128,1280]{1,2,0:T(8,128)S(1)}, u32[]{:S(2)}, u32[]{:S(2)}) %collective-permute-start.14) | collective-permute-done | bytes 655392 | tf_op jit(solution)/shard_map/vmap()/ppermute | solution.py:112
  106.4 1.5 %fusion.19 = (f32[1,128,1280]{1,2,0:T(8,128)S(1)}, f32[1,128,1280]{1,2,0:T(8,128)S(1)}) fusion(f32[1,128,1280]{1,2,0:T(8,128)S(1)} %copy-done.1, f32[1280]{0:T(1024)S(1)} %broadcast_in_dim.261, pred[]{:T(512)S(6)} %eq.43, f32[1,128,1280]{1,2,0:T(8,128)} %copy-done.22, f32[1,128,1280]{1,2,0:T(8,128)S(1)} %copy-done.14, f32[1,128,1280]{1,2,0:T(8,128)S(1)} %copy-done.18, ...), kind=kLoop, calls=%fused_computation.41 | loop fusion | flops 1310720 | bytes 3942402 | tf_op jit(solution)/shard_map/vmap(jit(_where))/select_n | solution.py:220
  108.0 8.3 %collective-permute-start.15 = (f32[1,128,2560]{1,2,0:T(8,128)S(1)}, f32[1,128,2560]{1,2,0:T(8,128)S(1)}, u32[]{:S(2)}, u32[]{:S(2)}) collective-permute-start(f32[1,128,2560]{1,2,0:T(8,128)S(1)} %pad_maximum_fusion.1), channel_id=1, source_target_pairs={{0,1},{1,0},{2,3},{3,2},{4,5},{5,4},{6,7},{7,6},{8,9},{9,8},{10,11... | collective-permute-start | bytes 3932168 | tf_op jit(solution)/shard_map/vmap()/ppermute | solution.py:222
  (208 shorter events, 33.5 us)
Async XLA Ops:
  0.6 5.2 %copy-start = (bf16[1,128,128]{2,1,0:T(8,128)(2,1)S(1)}, bf16[1,128,128]{2,1,0:T(8,128)(2,1)}, u32[]{:S(2)}) copy-start(bf16[1,128,128]{2,1,0:T(8,128)(2,1)} %param.8) | copy-start | bytes 98308
  0.6 2.6 %copy-start.20 = (bf16[1,128,2560]{2,1,0:T(8,128)(2,1)S(1)}, bf16[1,128,2560]{2,1,0:T(8,128)(2,1)}, u32[]{:S(2)}) copy-start(bf16[1,128,2560]{2,1,0:T(8,128)(2,1)} %param.6) | copy-start | bytes 1966084
  5.5 12.6 %collective-permute-start = (f32[1,17,40]{2,1,0:T(8,128)}, f32[1,17,40]{2,1,0:T(8,128)S(1)}, u32[]{:S(2)}, u32[]{:S(2)}) collective-permute-start(f32[1,17,40]{2,1,0:T(8,128)} %pad_maximum_fusion.2), channel_id=1, source_target_pairs={{0,1},{1,0},{2,3},{3,2},{4,5},{5,4},{6,7},{7,6},{8,9},{9,8},{10,11... | collective-permute-start | bytes 8168 | tf_op jit(solution)/shard_map/vmap()/ppermute | solution.py:66
  7.5 25.2 %collective-permute-start.4 = (f32[1,128,2560]{1,2,0:T(8,128)}, f32[1,128,2560]{1,2,0:T(8,128)}, u32[]{:S(2)}, u32[]{:S(2)}) collective-permute-start(f32[1,128,2560]{1,2,0:T(8,128)} %pad_maximum_fusion), channel_id=1, source_target_pairs={{0,1},{1,0},{2,3},{3,2},{4,5},{5,4},{6,7},{7,6},{8,9},{9,8},{10,11... | collective-permute-start | bytes 3932168 | tf_op jit(solution)/shard_map/vmap()/ppermute | solution.py:205
  18.1 4.6 %collective-permute-start.1 = (f32[1,17,40]{2,1,0:T(8,128)S(1)}, f32[1,17,40]{2,1,0:T(8,128)S(1)}, u32[]{:S(2)}, u32[]{:S(2)}) collective-permute-start(f32[1,17,40]{2,1,0:T(8,128)S(1)} %fusion.99), channel_id=1, source_target_pairs={{0,2},{1,3},{2,0},{3,1},{4,6},{5,7},{6,4},{7,5},{8,10},{9,11},{10,... | collective-permute-start | bytes 8168 | tf_op jit(solution)/shard_map/vmap()/ppermute | solution.py:66
  22.6 2.6 %collective-permute-start.2 = (f32[1,17,40]{2,1,0:T(8,128)S(1)}, f32[1,17,40]{2,1,0:T(8,128)S(1)}, u32[]{:S(2)}, u32[]{:S(2)}) collective-permute-start(f32[1,17,40]{2,1,0:T(8,128)S(1)} %add.259), channel_id=1, source_target_pairs={{0,4},{1,5},{2,6},{3,7},{4,0},{5,1},{6,2},{7,3},{8,12},{9,13},{10,... | collective-permute-start | bytes 8168 | tf_op jit(solution)/shard_map/vmap()/ppermute | solution.py:66
  25.2 4.0 %collective-permute-start.3 = (f32[1,17,40]{2,1,0:T(8,128)S(1)}, f32[1,17,40]{2,1,0:T(8,128)S(1)}, u32[]{:S(2)}, u32[]{:S(2)}) collective-permute-start(f32[1,17,40]{2,1,0:T(8,128)S(1)} %add.262), channel_id=1, source_target_pairs={{0,8},{1,9},{2,10},{3,11},{4,12},{5,13},{6,14},{7,15},{8,0},{9,1},... | collective-permute-start | bytes 8168 | tf_op jit(solution)/shard_map/vmap()/ppermute | solution.py:66
  35.3 18.8 %copy-start.2 = (f32[1,128,1280]{1,2,0:T(8,128)}, f32[1,128,1280]{1,2,0:T(8,128)S(1)}, u32[]{:S(2)}) copy-start(f32[1,128,1280]{1,2,0:T(8,128)S(1)} %get-tuple-element.210) | copy-start | bytes 1966084
  35.3 18.8 %copy-start.4 = (f32[1,128,1280]{1,2,0:T(8,128)}, f32[1,128,1280]{1,2,0:T(8,128)S(1)}, u32[]{:S(2)}) copy-start(f32[1,128,1280]{1,2,0:T(8,128)S(1)} %get-tuple-element.202) | copy-start | bytes 1966084
  35.3 11.3 %collective-permute-start.5 = (f32[1,128,1280]{1,2,0:T(8,128)S(1)}, f32[1,128,1280]{1,2,0:T(8,128)S(1)}, u32[]{:S(2)}, u32[]{:S(2)}) collective-permute-start(f32[1,128,1280]{1,2,0:T(8,128)S(1)} %get-tuple-element.202), channel_id=1, source_target_pairs={{0,2},{4,6},{8,10},{12,14},{3,1},{7,5},{11,9},{15,13},{16,18},{20,... | collective-permute-start | bytes 1966088 | tf_op jit(solution)/shard_map/vmap()/ppermute | solution.py:112
  36.8 16.9 %collective-permute-start.10 = (f32[1,128,1280]{1,2,0:T(8,128)S(1)}, f32[1,128,1280]{1,2,0:T(8,128)S(1)}, u32[]{:S(2)}, u32[]{:S(2)}) collective-permute-start(f32[1,128,1280]{1,2,0:T(8,128)S(1)} %get-tuple-element.210), channel_id=1, source_target_pairs={{15,13},{11,9},{7,5},{3,1},{12,14},{8,10},{4,6},{0,2},{31,29},{27,... | collective-permute-start | bytes 1966088 | tf_op jit(solution)/shard_map/vmap()/ppermute | solution.py:112
  46.7 7.5 %copy-start.15 = (f32[1,128,1280]{1,2,0:T(8,128)}, f32[1,128,1280]{1,2,0:T(8,128)S(1)}, u32[]{:S(2)}) copy-start(f32[1,128,1280]{1,2,0:T(8,128)S(1)} %collective-permute-done.5) | copy-start | bytes 1966084
  47.1 10.7 %collective-permute-start.6 = (f32[1,128,1280]{1,2,0:T(8,128)S(1)}, f32[1,128,1280]{1,2,0:T(8,128)S(1)}, u32[]{:S(2)}, u32[]{:S(2)}) collective-permute-start(f32[1,128,1280]{1,2,0:T(8,128)S(1)} %add_select_fusion.3), channel_id=1, source_target_pairs={{2,6},{10,14},{1,5},{9,13},{18,22},{26,30},{17,21},{25,29}} | collective-permute-start | bytes 1966088 | tf_op jit(solution)/shard_map/vmap()/ppermute | solution.py:112
  53.7 4.1 %copy-start.13 = (f32[1,128,1280]{1,2,0:T(8,128)}, f32[1,128,1280]{1,2,0:T(8,128)S(1)}, u32[]{:S(2)}) copy-start(f32[1,128,1280]{1,2,0:T(8,128)S(1)} %collective-permute-done.10) | copy-start | bytes 1966084
  54.1 5.6 %copy-start.26 = (s32[1,2]{1,0:T(1,128)S(1)}, s32[1,2]{1,0:T(1,128)}, u32[]{:S(2)}) copy-start(s32[1,2]{1,0:T(1,128)} %get-tuple-element.237) | copy-start | bytes 28
  54.1 11.4 %collective-permute-start.11 = (f32[1,128,1280]{1,2,0:T(8,128)S(1)}, f32[1,128,1280]{1,2,0:T(8,128)}, u32[]{:S(2)}, u32[]{:S(2)}) collective-permute-start(f32[1,128,1280]{1,2,0:T(8,128)S(1)} %add_select_fusion.1), channel_id=1, source_target_pairs={{13,9},{5,1},{14,10},{6,2},{29,25},{21,17},{30,26},{22,18}} | collective-permute-start | bytes 1966088 | tf_op jit(solution)/shard_map/vmap()/ppermute | solution.py:112
  58.9 9.4 %collective-permute-start.7 = (f32[1,128,1280]{1,2,0:T(8,128)}, f32[1,128,1280]{1,2,0:T(8,128)S(1)}, u32[]{:S(2)}, u32[]{:S(2)}) collective-permute-start(f32[1,128,1280]{1,2,0:T(8,128)} %multiply_add_fusion.5), channel_id=1, source_target_pairs={{6,14},{5,13},{22,30},{21,29}} | collective-permute-start | bytes 1966088 | tf_op jit(solution)/shard_map/vmap()/ppermute | solution.py:112
  66.9 15.8 %copy-start.25 = (s32[1,2]{1,0:T(1,128)S(1)}, s32[1,2]{1,0:T(1,128)}, u32[]{:S(2)}) copy-start(s32[1,2]{1,0:T(1,128)} %get-tuple-element.241) | copy-start | bytes 28
  66.9 19.5 %copy-start.5 = (f32[1,128,1280]{1,2,0:T(8,128)S(1)}, f32[1,128,1280]{1,2,0:T(8,128)}, u32[]{:S(2)}) copy-start(f32[1,128,1280]{1,2,0:T(8,128)} %copy-done.4) | copy-start | bytes 1966084
  66.9 12.5 %collective-permute-start.12 = (f32[1,128,1280]{1,2,0:T(8,128)S(1)}, f32[1,128,1280]{1,2,0:T(8,128)S(1)}, u32[]{:S(2)}, u32[]{:S(2)}) collective-permute-start(f32[1,128,1280]{1,2,0:T(8,128)S(1)} %multiply_add_fusion.2), channel_id=1, source_target_pairs={{9,1},{10,2},{25,17},{26,18}} | collective-permute-start | bytes 1966088 | tf_op jit(solution)/shard_map/vmap()/ppermute | solution.py:112
  69.4 17.0 %collective-permute-start.8 = (f32[1,128,1280]{1,2,0:T(8,128)}, f32[1,128,1280]{1,2,0:T(8,128)}, u32[]{:S(2)}, u32[]{:S(2)}) collective-permute-start(f32[1,128,1280]{1,2,0:T(8,128)} %broadcast_add_fusion.1), channel_id=1, source_target_pairs={{6,2},{14,10},{5,1},{13,9},{22,18},{30,26},{21,17},{29,25}} | collective-permute-start | bytes 1966088 | tf_op jit(solution)/shard_map/vmap()/ppermute | solution.py:112
  80.5 10.3 %collective-permute-start.13 = (f32[1,128,1280]{1,2,0:T(8,128)}, f32[1,128,1280]{1,2,0:T(8,128)}, u32[]{:S(2)}, u32[]{:S(2)}) collective-permute-start(f32[1,128,1280]{1,2,0:T(8,128)} %broadcast_add_fusion), channel_id=1, source_target_pairs={{9,13},{1,5},{10,14},{2,6},{25,29},{17,21},{26,30},{18,22}} | collective-permute-start | bytes 1966088 | tf_op jit(solution)/shard_map/vmap()/ppermute | solution.py:112
  83.0 7.8 %copy-start.3 = (f32[1,128,1280]{1,2,0:T(8,128)S(1)}, f32[1,128,1280]{1,2,0:T(8,128)}, u32[]{:S(2)}) copy-start(f32[1,128,1280]{1,2,0:T(8,128)} %copy-done.2) | copy-start | bytes 1966084
  89.3 10.1 %copy-start.16 = (f32[1,128,1280]{1,2,0:T(8,128)S(1)}, f32[1,128,1280]{1,2,0:T(8,128)}, u32[]{:S(2)}) copy-start(f32[1,128,1280]{1,2,0:T(8,128)} %copy-done.15) | copy-start | bytes 1966084
  89.3 9.2 %collective-permute-start.9 = (f32[1,128,1280]{1,2,0:T(8,128)}, f32[1,128,1280]{1,2,0:T(8,128)S(1)}, u32[]{:S(2)}, u32[]{:S(2)}) collective-permute-start(f32[1,128,1280]{1,2,0:T(8,128)} %get-tuple-element.200), channel_id=1, source_target_pairs={{2,0},{6,4},{10,8},{14,12},{1,3},{5,7},{9,11},{13,15},{18,16},{22,... | collective-permute-start | bytes 1966088 | tf_op jit(solution)/shard_map/vmap()/ppermute | solution.py:112
  93.7 11.9 %collective-permute-start.14 = (f32[1,128,1280]{1,2,0:T(8,128)}, f32[1,128,1280]{1,2,0:T(8,128)S(1)}, u32[]{:S(2)}, u32[]{:S(2)}) collective-permute-start(f32[1,128,1280]{1,2,0:T(8,128)} %get-tuple-element.206), channel_id=1, source_target_pairs={{13,15},{9,11},{5,7},{1,3},{14,12},{10,8},{6,4},{2,0},{29,31},{25,... | collective-permute-start | bytes 1966088 | tf_op jit(solution)/shard_map/vmap()/ppermute | solution.py:112
  96.3 20.1 %collective-permute-start.16 = (f32[40]{0:T(128)S(1)}, f32[40]{0:T(128)S(1)}, u32[]{:S(2)}, u32[]{:S(2)}) collective-permute-start(f32[40]{0:T(128)S(1)} %slice_bitcast_fusion.5), channel_id=1, source_target_pairs={{0,16},{16,0},{1,17},{17,1},{2,18},{18,2},{3,19},{19,3},{4,20},{20... | collective-permute-start | bytes 488 | tf_op jit(solution)/shard_map/ppermute | solution.py:270
  99.4 7.0 %copy-start.1 = (f32[1,128,1280]{1,2,0:T(8,128)S(1)}, f32[1,128,1280]{1,2,0:T(8,128)}, u32[]{:S(2)}) copy-start(f32[1,128,1280]{1,2,0:T(8,128)} %get-tuple-element.211) | copy-start | bytes 1966084
  99.4 7.0 %copy-start.14 = (f32[1,128,1280]{1,2,0:T(8,128)S(1)}, f32[1,128,1280]{1,2,0:T(8,128)}, u32[]{:S(2)}) copy-start(f32[1,128,1280]{1,2,0:T(8,128)} %copy-done.13) | copy-start | bytes 1966084
  99.4 7.0 %copy-start.18 = (f32[1,128,1280]{1,2,0:T(8,128)S(1)}, f32[1,128,1280]{1,2,0:T(8,128)}, u32[]{:S(2)}) copy-start(f32[1,128,1280]{1,2,0:T(8,128)} %get-tuple-element.207) | copy-start | bytes 1966084
  108.0 11.4 %collective-permute-start.15 = (f32[1,128,2560]{1,2,0:T(8,128)S(1)}, f32[1,128,2560]{1,2,0:T(8,128)S(1)}, u32[]{:S(2)}, u32[]{:S(2)}) collective-permute-start(f32[1,128,2560]{1,2,0:T(8,128)S(1)} %pad_maximum_fusion.1), channel_id=1, source_target_pairs={{0,1},{1,0},{2,3},{3,2},{4,5},{5,4},{6,7},{7,6},{8,9},{9,8},{10,11... | collective-permute-start | bytes 3932168 | tf_op jit(solution)/shard_map/vmap()/ppermute | solution.py:222
  121.0 2.0 %copy-start.27 = (f32[128,128]{1,0:T(8,128)S(1)}, f32[128,128]{1,0:T(8,128)}, u32[]{:S(2)}) copy-start(f32[128,128]{1,0:T(8,128)} %fusion.28) | copy-start | bytes 196612
  (13 other events, 16.5 us)

commit v9 on v8

--- a/solution.py
+++ b/solution.py
@@ -195,7 +195,8 @@
         prefixes = [
             scan.down_combine(level, p, g, low) for scan, p, g, low in zip(scans, prefixes, got, lowers)
         ]
-    return prefixes
+    anchor = lowers[0][0] if level_count else pair_totals[0]
+    return prefixes, anchor
 
 
 def carried_pair(tables, fwd_state, adj_state, position, count, head_width):
@@ -212,7 +213,7 @@
         high_block = jnp.where(way.upper, own, other)
         lows.append(low_block)
         totals.append(way.gain(1, 2 * way.pair + 1, 1) * low_block + high_block)
-    pair_prefixes = pair_scans(ways, totals)
+    pair_prefixes, anchor = pair_scans(ways, totals)
     lifted_parts = []
     keep_parts = []
     for way, pair_prefix, low_block in zip(ways, pair_prefixes, lows):
@@ -224,7 +225,7 @@
     got = got * unit
     half = got.shape[-1] // 2
     others = [got[..., :half], got[..., half:]]
-    return keep_parts, others, [way.upper for way in ways]
+    return (keep_parts, others, [way.upper for way in ways]), anchor
 
 
 def block_carried_grads(write_map, value_scale, decayed_vals, decayed_cot, carried, local_grads):
@@ -269,12 +270,13 @@
     for bit in range(lax.axis_size("dp").bit_length() - 1):
         grad_skip = grad_skip + lax.ppermute(grad_skip, "dp", xor_pairs(lax.axis_size("dp"), bit))
     head_width = token_values.shape[2] // decay_codes.shape[2]
-    carried = jax.vmap(carried_pair, (0, 0, 0, None, None, None))(
+    carried, anchor = jax.vmap(carried_pair, (0, 0, 0, None, None, None))(
         tables, fwd_state, adj_state, position, count, head_width
     )
-    local_grads = jax.vmap(block_local_grads, (0, 0, 0, 0, 0, None))(
-        token_values, cotangent, write_coeffs, read_coeffs, within, skip_gain
-    )
+    local_inputs, _ = lax.optimization_barrier(
+        ((token_values, cotangent, write_coeffs, read_coeffs, within), anchor)
+    )
+    local_grads = jax.vmap(block_local_grads, (0, 0, 0, 0, 0, None))(*local_inputs, skip_gain)
     grad_values, grad_write, grad_read = jax.vmap(block_carried_grads)(
         write_coeffs, value_scale, decayed_vals, decayed_cot, carried, local_grads
     )

time: 125 us -> 121 us (0.968)
  waiting for transfers between devices: 37.3 us -> 29.6 us
  starting transfers between devices: 31.7 us -> 35.2 us
  matrix products: 10.5 us -> 7.65 us
  local copies, waits for them, and re-layouts: 14.5 us -> 16.9 us
    ppermute x10, waiting for transfers between devices: 37.1 us -> 29.5 us  [exchange(): lax.ppermute(p, 'ctx', pairs)]
    squeeze x12, local copies, waits for them, and re-layouts: 5.25 us -> 2.95 us  [gain(): lax.dynamic_index_in_dim(self.pyramids[key], low_block // size, keepdims=...]
    optimization_barrier x0 -> x2, local copies, waits for them, and re-layouts: none -> 2.27 us  [local(): lax.optimization_barrier(((token_values, cotangent, write_coeffs, read_co...]
    add x2, other arithmetic: 2.41 us -> 0.47 us  [up_combine(): return self.pair_gain(level, self.role - span + 1, span) * lower + total]
    unnamed x59 -> x63, local copies, waits for them, and re-layouts: 6.54 us -> 4.65 us
    ppermute x1, starting transfers between devices: 8.33 us -> 9.9 us  [carried_pair(): lax.ppermute(jnp.concatenate(lifted_parts, -1), 'ctx', [(i, i ^ 1) for i...]
    ppermute x10, starting transfers between devices: 15.6 us -> 17.1 us  [exchange(): lax.ppermute(p, 'ctx', pairs)]
    convert_element_type x0 -> x1, local copies, waits for them, and re-layouts: none -> 1.3 us  [block_local_grads(): cot_three.astype(jnp.float32)]
  transfers between devices with their start and end apart: 17 -> 17, of which waited for: 9 -> 8; matrix products, arithmetic and copies ran while one was open for 31% -> 31% of each run, Pallas kernels for 0% -> 0%
where the time goes in v9:
time: 121 us; the launch traced here: 119 us
  starting transfers between devices  35.2 us (29%)
  waiting for transfers between devices  29.6 us (24%)
  other arithmetic  27.8 us (23%)
  local copies, waits for them, and re-layouts  16.9 us (14%)
  matrix products  7.65 us (6%)
  between operations  1.97 us (2%)
    ppermute x10, waiting for transfers between devices, exchange(): lax.ppermute(p, 'ctx', pairs)  29.5 us
    ppermute x10, starting transfers between devices, exchange(): lax.ppermute(p, 'ctx', pairs)  17.1 us
    ppermute x1, starting transfers between devices, carried_pair(): lax.ppermute(jnp.concatenate(lifted_parts, -1), 'ctx', [(i, i ^ 1) for i...  9.9 us
    ppermute x4, starting transfers between devices, gather_totals(): table = table + lax.ppermute(table, 'ctx', xor_pairs(count, bit))  6.46 us
    select_n x2, other arithmetic, down_send(): jnp.where(self.way.upper, self.pair_gain(0, pair, 1) * prefix + pair_tota...  5.92 us
    unnamed x63, local copies, waits for them, and re-layouts  4.65 us
    concatenate x8, other arithmetic, gain(): lax.dynamic_index_in_dim(self.pyramids[key], low_block // size, keepdims=...  3.38 us
    add x1, other arithmetic, carried_pair(): totals.append(way.gain(1, 2 * way.pair + 1, 1) * low_block + high_block)  3.28 us
  transfers between devices with their start and end apart: 17, of which 8 were waited for; matrix products, arithmetic and copies ran while one was open for 31% of the time, Pallas kernels for 0%

profile of v9, /device:TPU:1, one launch (start us, length us, event | category | flops | bytes accessed | tf_op | source)
XLA Modules:
  0.0 119.1 jit_solution(5787620504635199097)
XLA Ops:
  1.8 1.4 %copy.45 = bf16[1,128,2560]{1,2,0:T(8,128)(2,1)S(1)} copy(bf16[1,128,2560]{2,1,0:T(8,128)(2,1)} %param.6) | data formatting | bytes 1310720 | tf_op args[0]
  3.7 1.2 fusion.1
  12.4 2.4 %collective-permute-start.3 = (f32[1,17,40]{2,1,0:T(8,128)S(1)}, f32[1,17,40]{2,1,0:T(8,128)S(1)}, u32[]{:S(2)}, u32[]{:S(2)}) collective-permute-start(f32[1,17,40]{2,1,0:T(8,128)S(1)} %fusion.95), channel_id=1, source_target_pairs={{0,2},{1,3},{2,0},{3,1},{4,6},{5,7},{6,4},{7,5},{8,10},{9,11},{10,... | collective-permute-start | bytes 8168 | tf_op jit(solution)/shard_map/vmap()/ppermute | solution.py:66
  15.9 1.5 %collective-permute-start.4 = (f32[1,17,40]{2,1,0:T(8,128)S(1)}, f32[1,17,40]{2,1,0:T(8,128)S(1)}, u32[]{:S(2)}, u32[]{:S(2)}) collective-permute-start(f32[1,17,40]{2,1,0:T(8,128)S(1)} %add.262), channel_id=1, source_target_pairs={{0,4},{1,5},{2,6},{3,7},{4,0},{5,1},{6,2},{7,3},{8,12},{9,13},{10,... | collective-permute-start | bytes 8168 | tf_op jit(solution)/shard_map/vmap()/ppermute | solution.py:66
  18.5 2.5 %collective-permute-start.5 = (f32[1,17,40]{2,1,0:T(8,128)S(1)}, f32[1,17,40]{2,1,0:T(8,128)S(1)}, u32[]{:S(2)}, u32[]{:S(2)}) collective-permute-start(f32[1,17,40]{2,1,0:T(8,128)S(1)} %add.265), channel_id=1, source_target_pairs={{0,8},{1,9},{2,10},{3,11},{4,12},{5,13},{6,14},{7,15},{8,0},{9,1},... | collective-permute-start | bytes 8168 | tf_op jit(solution)/shard_map/vmap()/ppermute | solution.py:66
  27.7 3.3 %select_add_fusion.1 = (f32[1,128,1280]{1,2,0:T(8,128)}, f32[1,128,1280]{1,2,0:T(8,128)}, f32[1,128,1280]{1,2,0:T(8,128)}, f32[1,128,1280]{1,2,0:T(8,128)}) fusion(f32[1,128,2560]{1,2,0:T(8,128)} %collective-permute-done.1, f32[1280]{0:T(1024)S(1)} %broadcast_in_dim.215, pred[]{:T(512)S(6)} %eq.43, f32[1,128,2560]{1,2,0:T(8,128)S(1)} %convolution_bitcast_fusion.1, ...), kind=kLoop, calls=%fused_computation.55 | loop fusion | flops 1638400 | bytes 6563842 | tf_op jit(solution)/shard_map/vmap()/add | solution.py:215
  31.0 1.4 %collective-permute-start.2 = (f32[1,128,1280]{1,2,0:T(8,128)}, f32[1,128,1280]{1,2,0:T(8,128)S(1)}, u32[]{:S(2)}, u32[]{:S(2)}) collective-permute-start(f32[1,128,1280]{1,2,0:T(8,128)} %get-tuple-element.212), channel_id=1, source_target_pairs={{0,2},{4,6},{8,10},{12,14},{3,1},{7,5},{11,9},{15,13},{16,18},{20,... | collective-permute-start | bytes 1966088 | tf_op jit(solution)/shard_map/vmap()/ppermute | solution.py:112
  33.3 1.3 %collective-permute-start.10 = (f32[1,128,1280]{1,2,0:T(8,128)}, f32[1,128,1280]{1,2,0:T(8,128)S(1)}, u32[]{:S(2)}, u32[]{:S(2)}) collective-permute-start(f32[1,128,1280]{1,2,0:T(8,128)} %get-tuple-element.220), channel_id=1, source_target_pairs={{15,13},{11,9},{7,5},{3,1},{12,14},{8,10},{4,6},{0,2},{31,29},{27,... | collective-permute-start | bytes 1966088 | tf_op jit(solution)/shard_map/vmap()/ppermute | solution.py:112
  35.5 7.1 %collective-permute-done.2 = f32[1,128,1280]{1,2,0:T(8,128)S(1)} collective-permute-done((f32[1,128,1280]{1,2,0:T(8,128)}, f32[1,128,1280]{1,2,0:T(8,128)S(1)}, u32[]{:S(2)}, u32[]{:S(2)}) %collective-permute-start.2) | collective-permute-done | bytes 655392 | tf_op jit(solution)/shard_map/vmap()/ppermute | solution.py:112
  42.6 1.5 %add_select_fusion.3 = f32[1,128,1280]{1,2,0:T(8,128)S(1)} fusion(f32[1,128,1280]{1,2,0:T(8,128)} %get-tuple-element.212, f32[1,128,1280]{1,2,0:T(8,128)S(1)} %collective-permute-done.2, f32[1280]{0:T(1024)S(1)} %broadcast_in_dim.236, f32[1280]{0:T(1024)S(1)} %broadcast_in_dim.225, pred[]{:T(512)S(6)} %eq.43), kind=kLoop, calls=%fused_computation.54 | loop fusion | flops 819200 | bytes 1976321 | tf_op jit(solution)/shard_map/vmap(jit(_where))/select_n | solution.py:149
  44.1 3.2 %collective-permute-start.6 = (f32[1,128,1280]{1,2,0:T(8,128)S(1)}, f32[1,128,1280]{1,2,0:T(8,128)S(1)}, u32[]{:S(2)}, u32[]{:S(2)}) collective-permute-start(f32[1,128,1280]{1,2,0:T(8,128)S(1)} %add_select_fusion.3), channel_id=1, source_target_pairs={{2,6},{10,14},{1,5},{9,13},{18,22},{26,30},{17,21},{25,29}} | collective-permute-start | bytes 1966088 | tf_op jit(solution)/shard_map/vmap()/ppermute | solution.py:112
  47.4 2.3 %collective-permute-done.10 = f32[1,128,1280]{1,2,0:T(8,128)S(1)} collective-permute-done((f32[1,128,1280]{1,2,0:T(8,128)}, f32[1,128,1280]{1,2,0:T(8,128)S(1)}, u32[]{:S(2)}, u32[]{:S(2)}) %collective-permute-start.10) | collective-permute-done | bytes 655392 | tf_op jit(solution)/shard_map/vmap()/ppermute | solution.py:112
  50.1 1.3 %collective-permute-start.11 = (f32[1,128,1280]{1,2,0:T(8,128)S(1)}, f32[1,128,1280]{1,2,0:T(8,128)S(1)}, u32[]{:S(2)}, u32[]{:S(2)}) collective-permute-start(f32[1,128,1280]{1,2,0:T(8,128)S(1)} %add_select_fusion.1), channel_id=1, source_target_pairs={{13,9},{5,1},{14,10},{6,2},{29,25},{21,17},{30,26},{22,18}} | collective-permute-start | bytes 1966088 | tf_op jit(solution)/shard_map/vmap()/ppermute | solution.py:112
  51.4 1.3 %collective-permute-start.16 = (f32[40]{0:T(128)S(1)}, f32[40]{0:T(128)S(1)}, u32[]{:S(2)}, u32[]{:S(2)}) collective-permute-start(f32[40]{0:T(128)S(1)} %slice_bitcast_fusion.5), channel_id=1, source_target_pairs={{0,16},{16,0},{1,17},{17,1},{2,18},{18,2},{3,19},{19,3},{4,20},{20... | collective-permute-start | bytes 488 | tf_op jit(solution)/shard_map/ppermute | solution.py:271
  52.7 2.2 %collective-permute-done.6 = f32[1,128,1280]{1,2,0:T(8,128)S(1)} collective-permute-done((f32[1,128,1280]{1,2,0:T(8,128)S(1)}, f32[1,128,1280]{1,2,0:T(8,128)S(1)}, u32[]{:S(2)}, u32[]{:S(2)}) %collective-permute-start.6) | collective-permute-done | bytes 655392 | tf_op jit(solution)/shard_map/vmap()/ppermute | solution.py:112
  55.8 5.6 %collective-permute-done.11 = f32[1,128,1280]{1,2,0:T(8,128)S(1)} collective-permute-done((f32[1,128,1280]{1,2,0:T(8,128)S(1)}, f32[1,128,1280]{1,2,0:T(8,128)S(1)}, u32[]{:S(2)}, u32[]{:S(2)}) %collective-permute-start.11) | collective-permute-done | bytes 655392 | tf_op jit(solution)/shard_map/vmap()/ppermute | solution.py:112
  61.7 1.3 %collective-permute-start.12 = (f32[1,128,1280]{1,2,0:T(8,128)S(1)}, f32[1,128,1280]{1,2,0:T(8,128)S(1)}, u32[]{:S(2)}, u32[]{:S(2)}) collective-permute-start(f32[1,128,1280]{1,2,0:T(8,128)S(1)} %multiply_add_fusion.2), channel_id=1, source_target_pairs={{9,1},{10,2},{25,17},{26,18}} | collective-permute-start | bytes 1966088 | tf_op jit(solution)/shard_map/vmap()/ppermute | solution.py:112
  64.6 1.3 %collective-permute-start.8 = (f32[1,128,1280]{1,2,0:T(8,128)}, f32[1,128,1280]{1,2,0:T(8,128)}, u32[]{:S(2)}, u32[]{:S(2)}) collective-permute-start(f32[1,128,1280]{1,2,0:T(8,128)} %broadcast_add_fusion.1), channel_id=1, source_target_pairs={{6,2},{14,10},{5,1},{13,9},{22,18},{30,26},{21,17},{29,25}} | collective-permute-start | bytes 1966088 | tf_op jit(solution)/shard_map/vmap()/ppermute | solution.py:112
  65.9 8.1 %collective-permute-done.12 = f32[1,128,1280]{1,2,0:T(8,128)S(1)} collective-permute-done((f32[1,128,1280]{1,2,0:T(8,128)S(1)}, f32[1,128,1280]{1,2,0:T(8,128)S(1)}, u32[]{:S(2)}, u32[]{:S(2)}) %collective-permute-start.12) | collective-permute-done | bytes 655392 | tf_op jit(solution)/shard_map/vmap()/ppermute | solution.py:112
  75.1 2.1 %collective-permute-start.13 = (f32[1,128,1280]{1,2,0:T(8,128)}, f32[1,128,1280]{1,2,0:T(8,128)}, u32[]{:S(2)}, u32[]{:S(2)}) collective-permute-start(f32[1,128,1280]{1,2,0:T(8,128)} %broadcast_add_fusion), channel_id=1, source_target_pairs={{9,13},{1,5},{10,14},{2,6},{25,29},{17,21},{26,30},{18,22}} | collective-permute-start | bytes 1966088 | tf_op jit(solution)/shard_map/vmap()/ppermute | solution.py:112
  78.5 1.3 %copy.51 = f32[1,128,2560]{1,2,0:T(8,128)} copy(bf16[1,128,2560]{2,1,0:T(8,128)(2,1)S(1)} %copy-done.1) | data formatting | bytes 1966080 | tf_op jit(solution)/shard_map/vmap()/convert_element_type | solution.py:53
  81.0 3.2 %add_select_fusion.2 = (f32[1,128,1280]{1,2,0:T(8,128)}, f32[1,128,1280]{1,2,0:T(8,128)}) fusion(f32[1,128,1280]{1,2,0:T(8,128)} %get-tuple-element.212, f32[1280]{0:T(1024)S(1)} %broadcast_in_dim.225, pred[]{:T(512)S(6)} %eq.43, f32[1,128,1280]{1,2,0:T(8,128)} %copy-done.14, f32[1,128,1280]{1,2,0:T(8,128)} %collective-permute-done.8, f32[1280]{0:T(1024)} %select_n.496, ...), kind=kLoop, calls=%fused_computation.51 | loop fusion | flops 1146880 | bytes 3947521 | tf_op jit(solution)/shard_map/vmap(jit(_where))/select_n | solution.py:156
  84.2 2.3 %collective-permute-start.9 = (f32[1,128,1280]{1,2,0:T(8,128)}, f32[1,128,1280]{1,2,0:T(8,128)}, u32[]{:S(2)}, u32[]{:S(2)}) collective-permute-start(f32[1,128,1280]{1,2,0:T(8,128)} %get-tuple-element.210), channel_id=1, source_target_pairs={{2,0},{6,4},{10,8},{14,12},{1,3},{5,7},{9,11},{13,15},{18,16},{22,... | collective-permute-start | bytes 1966088 | tf_op jit(solution)/shard_map/vmap()/ppermute | solution.py:112
  86.5 2.8 %add_select_fusion = (f32[1,128,1280]{1,2,0:T(8,128)}, f32[1,128,1280]{1,2,0:T(8,128)}) fusion(f32[1,128,1280]{1,2,0:T(8,128)S(1)} %copy-done.4, f32[1280]{0:T(1024)S(1)} %broadcast_in_dim.245, pred[]{:T(512)S(6)} %eq.46, f32[1,128,1280]{1,2,0:T(8,128)S(1)} %copy-done.13, f32[1,128,1280]{1,2,0:T(8,128)} %collective-permute-done.13, f32[1280]{0:T(1024)S(1)} %copy-done.25, ...), kind=kLoop, calls=%fused_computation.43 | loop fusion | flops 1146880 | bytes 3947521 | tf_op jit(solution)/shard_map/vmap(jit(_where))/select_n | solution.py:156
  89.3 2.1 %collective-permute-start.14 = (f32[1,128,1280]{1,2,0:T(8,128)}, f32[1,128,1280]{1,2,0:T(8,128)}, u32[]{:S(2)}, u32[]{:S(2)}) collective-permute-start(f32[1,128,1280]{1,2,0:T(8,128)} %get-tuple-element.216), channel_id=1, source_target_pairs={{13,15},{9,11},{5,7},{1,3},{14,12},{10,8},{6,4},{2,0},{29,31},{25,... | collective-permute-start | bytes 1966088 | tf_op jit(solution)/shard_map/vmap()/ppermute | solution.py:112
  91.5 2.2 %fusion = f32[1,128,40,64]{1,3,2,0:T(8,128)} fusion(bf16[128,40,64]{0,2,1:T(8,128)(2,1)S(1)} %bitcast.247, f32[1,128,40,64]{1,3,2,0:T(8,128)S(1)} %bitcast.246, f32[40,128]{1,0:T(8,128)S(1)} %copy-done.26, f32[128,128]{1,0:T(8,128)S(1)} %fusion.46, pred[128,128]{1,0:T(8,128)(4,1)S(1)} %copy-done.27, f32[40]{0:T(128)S(1)} %copy-done.29), kind=kOutput, calls=%fused_computation.13 | convolution fusion | flops 87818240 | bytes 3379360 | tf_op jit(solution)/shard_map/vmap(hij,ihp->jhp)/dot_general | solution.py:51
  93.6 1.2 copy.52
  95.2 1.6 %fusion.18 = (f32[1,128,1280]{1,2,0:T(8,128)S(1)}, f32[1,128,1280]{1,2,0:T(8,128)S(1)}) fusion(f32[1,128,1280]{1,2,0:T(8,128)S(1)} %copy-done.2, f32[1280]{0:T(1024)S(1)} %broadcast_in_dim.242, pred[]{:T(512)S(6)} %eq.43, f32[1,128,1280]{1,2,0:T(8,128)} %collective-permute-done.9, f32[1,128,1280]{1,2,0:T(8,128)S(1)} %collective-permute-done.2, ...), kind=kLoop, calls=%fused_computation.49 | loop fusion | flops 1310720 | bytes 3942402 | tf_op jit(solution)/shard_map/vmap(jit(_where))/select_n | solution.py:221
  96.8 3.7 %collective-permute-done.14 = f32[1,128,1280]{1,2,0:T(8,128)} collective-permute-done((f32[1,128,1280]{1,2,0:T(8,128)}, f32[1,128,1280]{1,2,0:T(8,128)}, u32[]{:S(2)}, u32[]{:S(2)}) %collective-permute-start.14) | collective-permute-done | bytes 655392 | tf_op jit(solution)/shard_map/vmap()/ppermute | solution.py:112
  100.5 1.5 %fusion.17 = (f32[1,128,1280]{1,2,0:T(8,128)S(1)}, f32[1,128,1280]{1,2,0:T(8,128)S(1)}) fusion(f32[1,128,1280]{1,2,0:T(8,128)S(1)} %copy-done.3, f32[1280]{0:T(1024)S(1)} %broadcast_in_dim.264, pred[]{:T(512)S(6)} %eq.46, f32[1,128,1280]{1,2,0:T(8,128)} %collective-permute-done.14, f32[1,128,1280]{1,2,0:T(8,128)S(1)} %copy-done.11, ...), kind=kLoop, calls=%fused_computation.41 | loop fusion | flops 1310720 | bytes 3942402 | tf_op jit(solution)/shard_map/vmap(jit(_where))/select_n | solution.py:221
  102.1 9.9 %collective-permute-start.15 = (f32[1,128,2560]{1,2,0:T(8,128)S(1)}, f32[1,128,2560]{1,2,0:T(8,128)S(1)}, u32[]{:S(2)}, u32[]{:S(2)}) collective-permute-start(f32[1,128,2560]{1,2,0:T(8,128)S(1)} %pad_maximum_fusion.1), channel_id=1, source_target_pairs={{0,1},{1,0},{2,3},{3,2},{4,5},{5,4},{6,7},{7,6},{8,9},{9,8},{10,11... | collective-permute-start | bytes 3932168 | tf_op jit(solution)/shard_map/vmap()/ppermute | solution.py:223
  112.0 1.3 %convert_reduce_fusion = bf16[128,128]{1,0:T(8,128)(2,1)S(1)} fusion(f32[40,128]{1,0:T(8,128)S(1)} %copy-done.26, pred[128,128]{1,0:T(8,128)(4,1)S(1)} %copy-done.27, bf16[128,40,64]{0,2,1:T(8,128)(2,1)S(1)} %bitcast.248, bf16[128,40,64]{0,2,1:T(8,128)(2,1)S(1)} %bitcast.249), kind=kOutput, calls=%fused_computation.2 | convolution fusion | flops 88457216 | bytes 1380352 | tf_op jit(solution)/shard_map/vmap(ihp,jhp->hij)/dot_general | solution.py:45
  (215 shorter events, 31.9 us)
Async XLA Ops:
  5.1 7.3 %collective-permute-start = (f32[1,17,40]{2,1,0:T(8,128)S(1)}, f32[1,17,40]{2,1,0:T(8,128)S(1)}, u32[]{:S(2)}, u32[]{:S(2)}) collective-permute-start(f32[1,17,40]{2,1,0:T(8,128)S(1)} %pad_maximum_fusion.2), channel_id=1, source_target_pairs={{0,1},{1,0},{2,3},{3,2},{4,5},{5,4},{6,7},{7,6},{8,9},{9,8},{10,11... | collective-permute-start | bytes 8168 | tf_op jit(solution)/shard_map/vmap()/ppermute | solution.py:66
  8.0 19.7 %collective-permute-start.1 = (f32[1,128,2560]{1,2,0:T(8,128)}, f32[1,128,2560]{1,2,0:T(8,128)}, u32[]{:S(2)}, u32[]{:S(2)}) collective-permute-start(f32[1,128,2560]{1,2,0:T(8,128)} %pad_maximum_fusion), channel_id=1, source_target_pairs={{0,1},{1,0},{2,3},{3,2},{4,5},{5,4},{6,7},{7,6},{8,9},{9,8},{10,11... | collective-permute-start | bytes 3932168 | tf_op jit(solution)/shard_map/vmap()/ppermute | solution.py:206
  12.4 3.4 %collective-permute-start.3 = (f32[1,17,40]{2,1,0:T(8,128)S(1)}, f32[1,17,40]{2,1,0:T(8,128)S(1)}, u32[]{:S(2)}, u32[]{:S(2)}) collective-permute-start(f32[1,17,40]{2,1,0:T(8,128)S(1)} %fusion.95), channel_id=1, source_target_pairs={{0,2},{1,3},{2,0},{3,1},{4,6},{5,7},{6,4},{7,5},{8,10},{9,11},{10,... | collective-permute-start | bytes 8168 | tf_op jit(solution)/shard_map/vmap()/ppermute | solution.py:66
  15.9 2.6 %collective-permute-start.4 = (f32[1,17,40]{2,1,0:T(8,128)S(1)}, f32[1,17,40]{2,1,0:T(8,128)S(1)}, u32[]{:S(2)}, u32[]{:S(2)}) collective-permute-start(f32[1,17,40]{2,1,0:T(8,128)S(1)} %add.262), channel_id=1, source_target_pairs={{0,4},{1,5},{2,6},{3,7},{4,0},{5,1},{6,2},{7,3},{8,12},{9,13},{10,... | collective-permute-start | bytes 8168 | tf_op jit(solution)/shard_map/vmap()/ppermute | solution.py:66
  18.5 3.7 %collective-permute-start.5 = (f32[1,17,40]{2,1,0:T(8,128)S(1)}, f32[1,17,40]{2,1,0:T(8,128)S(1)}, u32[]{:S(2)}, u32[]{:S(2)}) collective-permute-start(f32[1,17,40]{2,1,0:T(8,128)S(1)} %add.265), channel_id=1, source_target_pairs={{0,8},{1,9},{2,10},{3,11},{4,12},{5,13},{6,14},{7,15},{8,0},{9,1},... | collective-permute-start | bytes 8168 | tf_op jit(solution)/shard_map/vmap()/ppermute | solution.py:66
  27.7 5.6 %copy-start.28 = (s32[1,2]{1,0:T(1,128)S(1)}, s32[1,2]{1,0:T(1,128)}, u32[]{:S(2)}) copy-start(s32[1,2]{1,0:T(1,128)} %get-tuple-element.247) | copy-start | bytes 28
  31.0 18.7 %copy-start.4 = (f32[1,128,1280]{1,2,0:T(8,128)S(1)}, f32[1,128,1280]{1,2,0:T(8,128)}, u32[]{:S(2)}) copy-start(f32[1,128,1280]{1,2,0:T(8,128)} %get-tuple-element.220) | copy-start | bytes 1966084
  31.0 11.7 %collective-permute-start.2 = (f32[1,128,1280]{1,2,0:T(8,128)}, f32[1,128,1280]{1,2,0:T(8,128)S(1)}, u32[]{:S(2)}, u32[]{:S(2)}) collective-permute-start(f32[1,128,1280]{1,2,0:T(8,128)} %get-tuple-element.212), channel_id=1, source_target_pairs={{0,2},{4,6},{8,10},{12,14},{3,1},{7,5},{11,9},{15,13},{16,18},{20,... | collective-permute-start | bytes 1966088 | tf_op jit(solution)/shard_map/vmap()/ppermute | solution.py:112
  33.3 16.4 %collective-permute-start.10 = (f32[1,128,1280]{1,2,0:T(8,128)}, f32[1,128,1280]{1,2,0:T(8,128)S(1)}, u32[]{:S(2)}, u32[]{:S(2)}) collective-permute-start(f32[1,128,1280]{1,2,0:T(8,128)} %get-tuple-element.220), channel_id=1, source_target_pairs={{15,13},{11,9},{7,5},{3,1},{12,14},{8,10},{4,6},{0,2},{31,29},{27,... | collective-permute-start | bytes 1966088 | tf_op jit(solution)/shard_map/vmap()/ppermute | solution.py:112
  44.1 10.7 %copy-start.24 = (f32[1280]{0:T(1024)S(1)}, f32[1280]{0:T(1024)}, u32[]{:S(2)}) copy-start(f32[1280]{0:T(1024)} %broadcast_in_dim.233) | copy-start | bytes 15364
  44.1 10.7 %collective-permute-start.6 = (f32[1,128,1280]{1,2,0:T(8,128)S(1)}, f32[1,128,1280]{1,2,0:T(8,128)S(1)}, u32[]{:S(2)}, u32[]{:S(2)}) collective-permute-start(f32[1,128,1280]{1,2,0:T(8,128)S(1)} %add_select_fusion.3), channel_id=1, source_target_pairs={{2,6},{10,14},{1,5},{9,13},{18,22},{26,30},{17,21},{25,29}} | collective-permute-start | bytes 1966088 | tf_op jit(solution)/shard_map/vmap()/ppermute | solution.py:112
  49.7 5.5 %copy-start.10 = (f32[1,128,1280]{1,2,0:T(8,128)}, f32[1,128,1280]{1,2,0:T(8,128)S(1)}, u32[]{:S(2)}) copy-start(f32[1,128,1280]{1,2,0:T(8,128)S(1)} %collective-permute-done.10) | copy-start | bytes 1966084
  50.1 11.3 %collective-permute-start.11 = (f32[1,128,1280]{1,2,0:T(8,128)S(1)}, f32[1,128,1280]{1,2,0:T(8,128)S(1)}, u32[]{:S(2)}, u32[]{:S(2)}) collective-permute-start(f32[1,128,1280]{1,2,0:T(8,128)S(1)} %add_select_fusion.1), channel_id=1, source_target_pairs={{13,9},{5,1},{14,10},{6,2},{29,25},{21,17},{30,26},{22,18}} | collective-permute-start | bytes 1966088 | tf_op jit(solution)/shard_map/vmap()/ppermute | solution.py:112
  51.4 11.6 %collective-permute-start.16 = (f32[40]{0:T(128)S(1)}, f32[40]{0:T(128)S(1)}, u32[]{:S(2)}, u32[]{:S(2)}) collective-permute-start(f32[40]{0:T(128)S(1)} %slice_bitcast_fusion.5), channel_id=1, source_target_pairs={{0,16},{16,0},{1,17},{17,1},{2,18},{18,2},{3,19},{19,3},{4,20},{20... | collective-permute-start | bytes 488 | tf_op jit(solution)/shard_map/ppermute | solution.py:271
  54.9 6.8 %copy-start.14 = (f32[1,128,1280]{1,2,0:T(8,128)}, f32[1,128,1280]{1,2,0:T(8,128)S(1)}, u32[]{:S(2)}) copy-start(f32[1,128,1280]{1,2,0:T(8,128)S(1)} %collective-permute-done.6) | copy-start | bytes 1966084
  55.1 8.4 %collective-permute-start.7 = (f32[1,128,1280]{1,2,0:T(8,128)S(1)}, f32[1,128,1280]{1,2,0:T(8,128)S(1)}, u32[]{:S(2)}, u32[]{:S(2)}) collective-permute-start(f32[1,128,1280]{1,2,0:T(8,128)S(1)} %multiply_add_fusion.5), channel_id=1, source_target_pairs={{6,14},{5,13},{22,30},{21,29}} | collective-permute-start | bytes 1966088 | tf_op jit(solution)/shard_map/vmap()/ppermute | solution.py:112
  61.7 12.3 %collective-permute-start.12 = (f32[1,128,1280]{1,2,0:T(8,128)S(1)}, f32[1,128,1280]{1,2,0:T(8,128)S(1)}, u32[]{:S(2)}, u32[]{:S(2)}) collective-permute-start(f32[1,128,1280]{1,2,0:T(8,128)S(1)} %multiply_add_fusion.2), channel_id=1, source_target_pairs={{9,1},{10,2},{25,17},{26,18}} | collective-permute-start | bytes 1966088 | tf_op jit(solution)/shard_map/vmap()/ppermute | solution.py:112
  64.6 16.4 %collective-permute-start.8 = (f32[1,128,1280]{1,2,0:T(8,128)}, f32[1,128,1280]{1,2,0:T(8,128)}, u32[]{:S(2)}, u32[]{:S(2)}) collective-permute-start(f32[1,128,1280]{1,2,0:T(8,128)} %broadcast_add_fusion.1), channel_id=1, source_target_pairs={{6,2},{14,10},{5,1},{13,9},{22,18},{30,26},{21,17},{29,25}} | collective-permute-start | bytes 1966088 | tf_op jit(solution)/shard_map/vmap()/ppermute | solution.py:112
  75.1 11.4 %collective-permute-start.13 = (f32[1,128,1280]{1,2,0:T(8,128)}, f32[1,128,1280]{1,2,0:T(8,128)}, u32[]{:S(2)}, u32[]{:S(2)}) collective-permute-start(f32[1,128,1280]{1,2,0:T(8,128)} %broadcast_add_fusion), channel_id=1, source_target_pairs={{9,13},{1,5},{10,14},{2,6},{25,29},{17,21},{26,30},{18,22}} | collective-permute-start | bytes 1966088 | tf_op jit(solution)/shard_map/vmap()/ppermute | solution.py:112
  80.5 6.0 %copy-start.13 = (f32[1,128,1280]{1,2,0:T(8,128)S(1)}, f32[1,128,1280]{1,2,0:T(8,128)}, u32[]{:S(2)}) copy-start(f32[1,128,1280]{1,2,0:T(8,128)} %copy-done.12) | copy-start | bytes 1966084
  80.5 6.0 %copy-start.25 = (f32[1280]{0:T(1024)S(1)}, f32[1280]{0:T(1024)}, u32[]{:S(2)}) copy-start(f32[1280]{0:T(1024)} %select_n.541) | copy-start | bytes 15364
  84.2 7.2 %copy-start.18 = (f32[1,128,2560]{1,2,0:T(8,128)S(1)}, f32[1,128,2560]{1,2,0:T(8,128)}, u32[]{:S(2)}) copy-start(f32[1,128,2560]{1,2,0:T(8,128)} %copy.51) | copy-start | bytes 3932164
  84.2 7.2 %copy-start.19 = (bf16[1,128,2560]{1,2,0:T(8,128)(2,1)S(1)}, bf16[1,128,2560]{1,2,0:T(8,128)(2,1)}, u32[]{:S(2)}) copy-start(bf16[1,128,2560]{1,2,0:T(8,128)(2,1)} %copy.48) | copy-start | bytes 1966084
  84.2 7.2 %copy-start.26 = (f32[40,128]{1,0:T(8,128)S(1)}, f32[40,128]{1,0:T(8,128)}, u32[]{:S(2)}) copy-start(f32[40,128]{1,0:T(8,128)} %copy.49) | copy-start | bytes 61444
  84.2 7.2 %copy-start.27 = (pred[128,128]{1,0:T(8,128)(4,1)S(1)}, pred[128,128]{1,0:T(8,128)(4,1)}, u32[]{:S(2)}) copy-start(pred[128,128]{1,0:T(8,128)(4,1)} %iota_compare_fusion) | copy-start | bytes 49156
  84.2 7.2 %copy-start.29 = (f32[40]{0:T(128)S(1)}, f32[40]{0:T(128)}, u32[]{:S(2)}) copy-start(f32[40]{0:T(128)} %param.11) | copy-start | bytes 484
  84.2 10.6 %collective-permute-start.9 = (f32[1,128,1280]{1,2,0:T(8,128)}, f32[1,128,1280]{1,2,0:T(8,128)}, u32[]{:S(2)}, u32[]{:S(2)}) collective-permute-start(f32[1,128,1280]{1,2,0:T(8,128)} %get-tuple-element.210), channel_id=1, source_target_pairs={{2,0},{6,4},{10,8},{14,12},{1,3},{5,7},{9,11},{13,15},{18,16},{22,... | collective-permute-start | bytes 1966088 | tf_op jit(solution)/shard_map/vmap()/ppermute | solution.py:112
  89.3 11.2 %collective-permute-start.14 = (f32[1,128,1280]{1,2,0:T(8,128)}, f32[1,128,1280]{1,2,0:T(8,128)}, u32[]{:S(2)}, u32[]{:S(2)}) collective-permute-start(f32[1,128,1280]{1,2,0:T(8,128)} %get-tuple-element.216), channel_id=1, source_target_pairs={{13,15},{9,11},{5,7},{1,3},{14,12},{10,8},{6,4},{2,0},{29,31},{25,... | collective-permute-start | bytes 1966088 | tf_op jit(solution)/shard_map/vmap()/ppermute | solution.py:112
  95.1 5.3 %copy-start.16 = (f32[1,128,1280]{1,2,0:T(8,128)S(1)}, f32[1,128,1280]{1,2,0:T(8,128)}, u32[]{:S(2)}) copy-start(f32[1,128,1280]{1,2,0:T(8,128)} %get-tuple-element.217) | copy-start | bytes 1966084
  102.0 10.0 %copy-start.20 = (bf16[1,128,2560]{1,2,0:T(8,128)(2,1)S(1)}, bf16[1,128,2560]{1,2,0:T(8,128)(2,1)}, u32[]{:S(2)}) copy-start(bf16[1,128,2560]{1,2,0:T(8,128)(2,1)} %copy.48) | copy-start | bytes 1966084
  102.0 10.0 %copy-start.21 = (bf16[1,128,2560]{1,2,0:T(8,128)(2,1)S(1)}, bf16[1,128,2560]{1,2,0:T(8,128)(2,1)}, u32[]{:S(2)}) copy-start(bf16[1,128,2560]{1,2,0:T(8,128)(2,1)} %copy.52) | copy-start | bytes 1966084
  102.1 13.1 %collective-permute-start.15 = (f32[1,128,2560]{1,2,0:T(8,128)S(1)}, f32[1,128,2560]{1,2,0:T(8,128)S(1)}, u32[]{:S(2)}, u32[]{:S(2)}) collective-permute-start(f32[1,128,2560]{1,2,0:T(8,128)S(1)} %pad_maximum_fusion.1), channel_id=1, source_target_pairs={{0,1},{1,0},{2,3},{3,2},{4,5},{5,4},{6,7},{7,6},{8,9},{9,8},{10,11... | collective-permute-start | bytes 3932168 | tf_op jit(solution)/shard_map/vmap()/ppermute | solution.py:223
  (15 other events, 37.7 us)

commit v10 on v9

--- a/solution.py
+++ b/solution.py
@@ -58,14 +58,11 @@
     return [(i, i ^ (1 << bit)) for i in range(count)]
 
 
-def gather_totals(totals, skip_part, position, count):
-    rows = jnp.arange(count)[:, None]
-    table = jnp.concatenate([jnp.where(rows == position, totals[None, :], 0.0), skip_part[None, :]], 0)
-    tables = [table]
-    for bit in range(count.bit_length() - 1):
-        table = table + lax.ppermute(table, "ctx", xor_pairs(count, bit))
-        tables.append(table)
-    return tables
+def all_sum(value, axis):
+    size = lax.axis_size(axis)
+    for bit in range(size.bit_length() - 1):
+        value = value + lax.ppermute(value, axis, xor_pairs(size, bit))
+    return value
 
 
 def take_half(array, upper):
@@ -78,38 +75,31 @@
 
 
 class Direction:
-    def __init__(self, tables, position, count, reverse, head_width):
-        self.tables = tables
+    def __init__(self, position, count, reverse):
         self.count = count
         self.reverse = reverse
-        self.head_width = head_width
         self.index = count - 1 - position if reverse else position
         self.upper = self.index % 2 == 1
         self.pair = self.index // 2
-        self.pyramids = {}
 
     def actual(self, pairs):
         if self.reverse:
             return [(self.count - 1 - a, self.count - 1 - b) for a, b in pairs]
         return pairs
 
-    def pair_pairs(self, pairs):
-        return self.actual([(2 * a + j, 2 * b + j) for a, b in pairs for j in (0, 1)])
-
-    def gain(self, table_index, low_block, size):
-        key = (table_index % len(self.tables), size)
-        if key not in self.pyramids:
-            rows = self.tables[key[0]][: self.count]
-            if self.reverse:
-                rows = rows[::-1]
-            grouped = rows.reshape(self.count // size, size, rows.shape[-1]).sum(axis=1)
-            self.pyramids[key] = jnp.exp(grouped)
-        full = lax.dynamic_index_in_dim(self.pyramids[key], low_block // size, keepdims=False)
-        return spread_heads(take_half(full, self.upper), self.head_width)[..., None, :]
-
 
 def exchange(payloads, pair_lists):
     return [lax.ppermute(p, "ctx", pairs) for p, pairs in zip(payloads, pair_lists)]
+
+
+def chain(earlier, later):
+    rows = lax.broadcasted_iota(jnp.int32, earlier.shape, earlier.ndim - 2)
+    gain = jnp.exp(later[..., -1:, :])
+    return jnp.where(rows < earlier.shape[-2] - 1, gain * earlier + later, earlier + later)
+
+
+def lift(summary, prefix):
+    return jnp.exp(summary[..., -1:, :]) * prefix + summary[..., :-1, :]
 
 
 class PairScan:
@@ -118,8 +108,6 @@
         self.pair_count = way.count // 2
         self.level_count = self.pair_count.bit_length() - 1
         self.flip = self.level_count >= 2
-        pair = way.pair
-        self.role = jnp.where(way.upper, pair ^ 1, pair) if self.flip else pair
 
     def device_pairs(self, pairs, first_level):
         lower = [(2 * a, 2 * b) for a, b in pairs]
@@ -131,29 +119,20 @@
             upper = [(2 * a + 1, 2 * b + 1) for a, b in pairs]
         return self.way.actual(lower + upper)
 
-    def pair_gain(self, level, low_pair, pair_span):
-        table = min(level + 2, len(self.way.tables) - 1)
-        return self.way.gain(table, 2 * low_pair, 2 * pair_span)
-
     def up_send(self, level):
         span = 1 << level
         pairs = [(a, a + span) for a in range(self.pair_count) if a % (2 * span) == span - 1]
         return self.device_pairs(pairs, level == 0)
 
     def up_combine(self, level, total, lower):
-        span = 1 << level
         if self.flip and level == 0:
-            pair = self.way.pair
-            kept_upper = self.pair_gain(0, pair ^ 1, 1) * total + lower
-            kept_lower = self.pair_gain(0, pair, 1) * lower + total
-            return jnp.where(self.way.upper, kept_upper, kept_lower)
-        return self.pair_gain(level, self.role - span + 1, span) * lower + total
+            return jnp.where(self.way.upper, chain(total, lower), chain(lower, total))
+        return chain(lower, total)
 
     def down_send(self, level, prefix, pair_total):
         span = 1 << level
         if self.flip and level == 0:
-            pair = self.way.pair
-            sent = jnp.where(self.way.upper, self.pair_gain(0, pair, 1) * prefix + pair_total, prefix)
+            sent = jnp.where(self.way.upper, lift(pair_total, prefix), prefix)
             pairs = [(2 * (a + 1), 2 * a) for a in range(0, self.pair_count, 2)]
             pairs += [(2 * a + 1, 2 * (a + 1) + 1) for a in range(0, self.pair_count, 2)]
             return sent, self.way.actual(pairs)
@@ -161,17 +140,13 @@
         return prefix, self.device_pairs(pairs, False)
 
     def down_combine(self, level, prefix, got, lowers):
-        span = 1 << level
         if self.flip and level == 0:
-            pair = self.way.pair
-            grown = self.pair_gain(self.level_count, pair - 1, 1) * prefix + lowers[0]
-            odd = pair % 2 == 1
+            odd = self.way.pair % 2 == 1
+            grown = lift(lowers[0], prefix)
             return jnp.where(self.way.upper, jnp.where(odd, got, prefix), jnp.where(odd, grown, got))
         if got is not None:
             prefix = prefix + got
-        lower_gain = self.pair_gain(self.level_count, self.role - 2 * span + 1, span)
-        lower_gain = jnp.where(self.role % (2 * span) == 2 * span - 1, lower_gain, 1.0)
-        return lower_gain * prefix + lowers[level]
+        return lift(lowers[level], prefix)
 
 
 def pair_scans(ways, pair_totals):
@@ -185,7 +160,7 @@
             lowers[k].append(got[k])
             if level < level_count - 1:
                 totals[k] = scan.up_combine(level, totals[k], got[k])
-    prefixes = [jnp.zeros_like(total) for total in pair_totals]
+    prefixes = [jnp.zeros_like(total[..., :-1, :]) for total in pair_totals]
     for level in reversed(range(level_count)):
         if level < level_count - 1 or (scans[0].flip and level == 0):
             sends = [scan.down_send(level, p, t) for scan, p, t in zip(scans, prefixes, pair_totals)]
@@ -199,29 +174,29 @@
     return prefixes, anchor
 
 
-def carried_pair(tables, fwd_state, adj_state, position, count, head_width):
-    ways = [Direction(tables, position, count, reverse, head_width) for reverse in (False, True)]
-    states = [fwd_state, adj_state]
-    sent = jnp.concatenate([take_half(s, ~w.upper) for s, w in zip(states, ways)], -1)
+def carried_pair(log_totals, fwd_state, adj_state, position, count):
+    ways = [Direction(position, count, reverse) for reverse in (False, True)]
+    summaries = [jnp.concatenate([s, log_totals[None, :]], 0) for s in (fwd_state, adj_state)]
+    sent = jnp.concatenate([take_half(s, ~w.upper) for s, w in zip(summaries, ways)], -1)
     got = lax.ppermute(sent, "ctx", [(i, i ^ 1) for i in range(count)])
     got = [got[..., : got.shape[-1] // 2], got[..., got.shape[-1] // 2 :]]
     lows = []
     totals = []
-    for way, state, other in zip(ways, states, got):
-        own = take_half(state, way.upper)
+    for way, summary, other in zip(ways, summaries, got):
+        own = take_half(summary, way.upper)
         low_block = jnp.where(way.upper, other, own)
         high_block = jnp.where(way.upper, own, other)
         lows.append(low_block)
-        totals.append(way.gain(1, 2 * way.pair + 1, 1) * low_block + high_block)
+        totals.append(chain(low_block, high_block))
     pair_prefixes, anchor = pair_scans(ways, totals)
     lifted_parts = []
     keep_parts = []
     for way, pair_prefix, low_block in zip(ways, pair_prefixes, lows):
-        lifted = way.gain(1, 2 * way.pair, 1) * pair_prefix + low_block
+        lifted = lift(low_block, pair_prefix)
         lifted_parts.append(jnp.where(way.upper, pair_prefix, lifted))
         keep_parts.append(jnp.where(way.upper, lifted, pair_prefix))
     got = lax.ppermute(jnp.concatenate(lifted_parts, -1), "ctx", [(i, i ^ 1) for i in range(count)])
-    unit = jnp.exp(jnp.min(tables[-1]) * 0.0)
+    unit = jnp.exp(jnp.min(log_totals) * 0.0)
     got = got * unit
     half = got.shape[-1] // 2
     others = [got[..., :half], got[..., half:]]
@@ -265,13 +240,10 @@
     )
     position = lax.axis_index("ctx")
     count = lax.axis_size("ctx")
-    tables = jax.vmap(gather_totals, (0, 0, None, None))(totals, skip_parts, position, count)
-    grad_skip = jnp.sum(tables[-1][:, count], axis=0)
-    for bit in range(lax.axis_size("dp").bit_length() - 1):
-        grad_skip = grad_skip + lax.ppermute(grad_skip, "dp", xor_pairs(lax.axis_size("dp"), bit))
+    grad_skip = all_sum(all_sum(jnp.sum(skip_parts, axis=0), "ctx"), "dp")
     head_width = token_values.shape[2] // decay_codes.shape[2]
-    carried, anchor = jax.vmap(carried_pair, (0, 0, 0, None, None, None))(
-        tables, fwd_state, adj_state, position, count, head_width
+    carried, anchor = jax.vmap(carried_pair, (0, 0, 0, None, None))(
+        spread_heads(totals, head_width), fwd_state, adj_state, position, count
     )
     local_inputs, _ = lax.optimization_barrier(
         ((token_values, cotangent, write_coeffs, read_coeffs, within), anchor)

time: 121 us -> 135 us (1.12)
  waiting for transfers between devices: 29.6 us -> 39.9 us
  local copies, waits for them, and re-layouts: 16.9 us -> 23.1 us
  other arithmetic: 27.8 us -> 25 us
    ppermute x5, waiting for transfers between devices: 0.13 us -> 6.46 us  [all_sum(): value = value + lax.ppermute(value, axis, xor_pairs(size, bit))]
    select_n x2 -> x6, local copies, waits for them, and re-layouts: 1.34 us -> 6.9 us  [the longest x4 4.69 us: chain(): jnp.where(rows < earlier.shape[-2] - 1, gain * earlier + later, earlier +...]
    concatenate x10 -> x1, other arithmetic: 4.54 us -> 0.13 us  [carried_pair(): jnp.concatenate([take_half(s, ~w.upper) for s, w in zip(summaries, ways)]...]
    exp x12 -> x11, local copies, waits for them, and re-layouts: 0.08 us -> 4.33 us  [the longest x6 3.5 us: lift(): return jnp.exp(summary[..., -1:, :]) * prefix + summary[..., :-1, :]]
    ppermute x0 -> x2, other arithmetic: none -> 3.87 us  [exchange(): lax.ppermute(p, 'ctx', pairs)]
    ppermute x1, waiting for transfers between devices: 0.01 us -> 2.98 us  [carried_pair(): got = lax.ppermute(sent, 'ctx', [(i, i ^ 1) for i in range(count)])]
    squeeze x12 -> x0, local copies, waits for them, and re-layouts: 2.95 us -> none  [gain(): lax.dynamic_index_in_dim(self.pyramids[key], low_block // size, keepdims=...]
    select_n x7 -> x5, other arithmetic: 8.04 us -> 5.39 us  [the longest x2 2.85 us: chain(): jnp.where(rows < earlier.shape[-2] - 1, gain * earlier + later, earlier +...]
  transfers between devices with their start and end apart: 17 -> 17, of which waited for: 8 -> 11; matrix products, arithmetic and copies ran while one was open for 31% -> 28% of each run, Pallas kernels for 0% -> 0%
where the time goes in v10:
time: 135 us; the launch traced here: 134 us
  waiting for transfers between devices  39.9 us (30%)
  starting transfers between devices  35.3 us (26%)
  other arithmetic  25 us (19%)
  local copies, waits for them, and re-layouts  23.1 us (17%)
  matrix products  8.26 us (6%)
  between operations  1.96 us (1%)
    ppermute x10, waiting for transfers between devices, exchange(): lax.ppermute(p, 'ctx', pairs)  30.5 us
    ppermute x10, starting transfers between devices, exchange(): lax.ppermute(p, 'ctx', pairs)  18 us
    ppermute x1, starting transfers between devices, carried_pair(): lax.ppermute(jnp.concatenate(lifted_parts, -1), 'ctx', [(i, i ^ 1) for i...  10.7 us
    ppermute x5, waiting for transfers between devices, all_sum(): value = value + lax.ppermute(value, axis, xor_pairs(size, bit))  6.46 us
    ppermute x5, starting transfers between devices, all_sum(): value = value + lax.ppermute(value, axis, xor_pairs(size, bit))  6.45 us
    add x5, other arithmetic, all_sum(): value = value + lax.ppermute(value, axis, xor_pairs(size, bit))  6.02 us
    select_n x4, local copies, waits for them, and re-layouts, chain(): jnp.where(rows < earlier.shape[-2] - 1, gain * earlier + later, earlier +...  4.69 us
    ppermute x2, other arithmetic, exchange(): lax.ppermute(p, 'ctx', pairs)  3.87 us
  transfers between devices with their start and end apart: 17, of which 11 were waited for; matrix products, arithmetic and copies ran while one was open for 28% of the time, Pallas kernels for 0%

profile of v10, /device:TPU:1, one launch (start us, length us, event | category | flops | bytes accessed | tf_op | source)
XLA Modules:
  0.0 133.6 jit_solution(12218154236537351590)
XLA Ops:
  3.0 1.5 %copy.106 = f32[1,128,2560]{2,1,0:T(8,128)} copy(f32[1,128,2560]{1,2,0:T(8,128)S(1)} %bitcast.101) | data formatting | bytes 2621440 | tf_op jit(solution)/shard_map/vmap()/broadcast_in_dim | solution.py:10
  4.6 2.4 %fusion.3 = (f32[2560]{0:T(1024)}, bf16[1,128,2560]{2,1,0:T(8,128)(2,1)S(1)}, bf16[1,128,2560]{2,1,0:T(8,128)(2,1)S(1)}) fusion(bf16[1,128,2560]{2,1,0:T(8,128)(2,1)S(1)} %copy-done.1, bf16[1,128,2560]{2,1,0:T(8,128)(2,1)} %param.6, f32[1,128,2560]{2,1,0:T(8,128)S(1)} %copy.105, f32[1,128,2560]{2,1,0:T(8,128)} %copy.106), kind=kLoop, calls=%fused_computation.19 | loop fusion | flops 2618880 | bytes 5253120 | tf_op jit(solution)/shard_map/vmap()/reduce_sum | solution.py:25
  8.4 1.4 %copy.107 = f32[1,129,2560]{2,0,1:T(1,128)S(1)} copy(f32[1,129,2560]{2,1,0:T(8,128)S(1)} %pad_maximum_fusion) | data formatting | bytes 2641920 | tf_op jit(solution)/shard_map/vmap()/concatenate | solution.py:180
  9.9 3.0 %collective-permute-done = f32[1,129,2560]{2,0,1:T(1,128)S(1)} collective-permute-done((f32[1,129,2560]{2,0,1:T(1,128)S(1)}, f32[1,129,2560]{2,0,1:T(1,128)S(1)}, u32[]{:S(2)}, u32[]{:S(2)}) %collective-permute-start) | collective-permute-done | bytes 1320992 | tf_op jit(solution)/shard_map/vmap()/ppermute | solution.py:181
  14.1 1.6 %add_select_fusion.3 = (f32[1,129,1280]{2,1,0:T(8,128)S(1)}, f32[1,129,1280]{2,1,0:T(8,128)}, f32[1,129,1280]{2,1,0:T(8,128)S(1)}, f32[1,129,1280]{2,1,0:T(8,128)}) fusion(f32[1,129,1280]{2,1,0:T(8,128)S(1)} %get-tuple-element.59, f32[1280]{0:T(1024)S(1)} %get-tuple-element.66, pred[129]{0:T(512)(128)(4,1)S(1)} %iota_compare_fusion.1, ...), kind=kLoop, calls=%fused_computation.48 | loop fusion | flops 2641920 | bytes 7925891 | tf_op jit(solution)/shard_map/vmap(jit(_where))/select_n | solution.py:98
  16.4 1.3 collective-permute-start.1
  17.7 1.5 %copy.125 = f32[1,129,1280]{2,0,1:T(1,128)} copy(f32[1,129,1280]{2,1,0:T(8,128)S(1)} %get-tuple-element.57) | data formatting | bytes 1320960 | tf_op jit(solution)/shard_map/vmap(jit(_where))/select_n | solution.py:98
  20.5 7.5 %collective-permute-done.1 = f32[1,129,1280]{2,0,1:T(1,128)S(1)} collective-permute-done((f32[1,129,1280]{2,0,1:T(1,128)S(1)}, f32[1,129,1280]{2,0,1:T(1,128)S(1)}, u32[]{:S(2)}, u32[]{:S(2)}) %collective-permute-start.1) | collective-permute-done | bytes 660512 | tf_op jit(solution)/shard_map/vmap()/ppermute | solution.py:92
  29.9 4.9 %collective-permute-start.2 = (f32[1,129,1280]{2,0,1:T(1,128)S(1)}, f32[1,129,1280]{2,0,1:T(1,128)}, u32[]{:S(2)}, u32[]{:S(2)}) collective-permute-start(f32[1,129,1280]{2,0,1:T(1,128)S(1)} %copy.117), channel_id=1, source_target_pairs={{2,6},{10,14},{1,5},{9,13},{18,22},{26,30},{17,21},{25,29}} | collective-permute-start | bytes 1981448 | tf_op jit(solution)/shard_map/vmap()/ppermute | solution.py:92
  35.6 1.3 broadcast_reduce_fusion
  37.8 3.8 %collective-permute-done.2 = f32[1,129,1280]{2,0,1:T(1,128)} collective-permute-done((f32[1,129,1280]{2,0,1:T(1,128)S(1)}, f32[1,129,1280]{2,0,1:T(1,128)}, u32[]{:S(2)}, u32[]{:S(2)}) %collective-permute-start.2) | collective-permute-done | bytes 660512 | tf_op jit(solution)/shard_map/vmap()/ppermute | solution.py:92
  41.5 2.8 %fusion.85 = (f32[1,129,1280]{2,1,0:T(8,128)}, f32[1,129,1280]{2,1,0:T(8,128)S(1)}, f32[1,129,1280]{2,1,0:T(8,128)}, f32[1,129,1280]{2,1,0:T(8,128)}) fusion(f32[1,129,1280]{2,0,1:T(1,128)} %collective-permute-done.6, f32[1,129,1280]{2,1,0:T(8,128)S(1)} %get-tuple-element.57, f32[1280]{0:T(1024)S(1)} %fusion.70, f32[1280]{0:T(1024)S(1)} %fusion.69, ...), kind=kLoop, calls=%fused_computation.156 | loop fusion | flops 1981440 | bytes 5299330 | tf_op jit(solution)/shard_map/vmap()/ppermute | solution.py:92
  44.3 1.5 %copy.129 = f32[1,129,1280]{2,0,1:T(1,128)} copy(f32[1,129,1280]{2,1,0:T(8,128)S(1)} %get-tuple-element.49) | data formatting | bytes 1320960 | tf_op jit(solution)/shard_map/vmap(jit(_where))/select_n | solution.py:129
  48.9 2.6 %collective-permute-done.13 = f32[40]{0:T(128)} collective-permute-done((f32[40]{0:T(128)}, f32[40]{0:T(128)}, u32[]{:S(2)}, u32[]{:S(2)}) %collective-permute-start.13) | collective-permute-done | bytes 192 | tf_op jit(solution)/shard_map/ppermute | solution.py:64
  52.8 2.9 %collective-permute-start.14 = (f32[40]{0:T(128)}, f32[40]{0:T(128)}, u32[]{:S(2)}, u32[]{:S(2)}) collective-permute-start(f32[40]{0:T(128)} %add.177), channel_id=1, source_target_pairs={{0,4},{1,5},{2,6},{3,7},{4,0},{5,1},{6,2},{7,3},{8,12},{9,13},{10,... | collective-permute-start | bytes 488 | tf_op jit(solution)/shard_map/ppermute | solution.py:64
  55.7 1.9 %collective-permute-done.14 = f32[40]{0:T(128)} collective-permute-done((f32[40]{0:T(128)}, f32[40]{0:T(128)}, u32[]{:S(2)}, u32[]{:S(2)}) %collective-permute-start.14) | collective-permute-done | bytes 192 | tf_op jit(solution)/shard_map/ppermute | solution.py:64
  58.8 2.3 %collective-permute-start.15 = (f32[40]{0:T(128)}, f32[40]{0:T(128)}, u32[]{:S(2)}, u32[]{:S(2)}) collective-permute-start(f32[40]{0:T(128)} %add.178), channel_id=1, source_target_pairs={{0,8},{1,9},{2,10},{3,11},{4,12},{5,13},{6,14},{7,15},{8,0},{9,1},... | collective-permute-start | bytes 488 | tf_op jit(solution)/shard_map/ppermute | solution.py:64
  67.4 1.4 %fusion.72 = f32[1280]{0:T(1024)} fusion(f32[1,129,1280]{2,1,0:T(8,128)} %get-tuple-element.35), kind=kLoop, calls=%fused_computation.137 | loop fusion | bytes 10240 | tf_op jit(solution)/shard_map/vmap()/exp | solution.py:102
  70.5 1.3 copy.113
  73.4 1.8 %copy.120 = f32[1,129,1280]{2,0,1:T(1,128)S(1)} copy(f32[1,129,1280]{2,1,0:T(8,128)} %get-tuple-element.64) | data formatting | bytes 1320960 | tf_op jit(solution)/shard_map/vmap(jit(_where))/select_n | solution.py:98
  78.2 1.3 collective-permute-start.8
  81.7 8.8 %collective-permute-done.8 = f32[1,129,1280]{2,0,1:T(1,128)S(1)} collective-permute-done((f32[1,129,1280]{2,0,1:T(1,128)S(1)}, f32[1,129,1280]{2,0,1:T(1,128)S(1)}, u32[]{:S(2)}, u32[]{:S(2)}) %collective-permute-start.8) | collective-permute-done | bytes 660512 | tf_op jit(solution)/shard_map/vmap()/ppermute | solution.py:92
  90.6 1.5 %collective-permute-start.9 = (f32[1,128,1280]{2,1,0:T(8,128)S(1)}, f32[1,128,1280]{2,1,0:T(8,128)S(1)}, u32[]{:S(2)}, u32[]{:S(2)}) collective-permute-start(f32[1,128,1280]{2,1,0:T(8,128)S(1)} %copy_add_fusion), channel_id=1, source_target_pairs={{9,13},{1,5},{10,14},{2,6},{25,29},{17,21},{26,30},{18,22}} | collective-permute-start | bytes 1966088 | tf_op jit(solution)/shard_map/vmap()/ppermute | solution.py:92
  92.8 4.6 %collective-permute-done.4 = f32[1,128,1280]{2,1,0:T(8,128)S(1)} collective-permute-done((f32[1,128,1280]{2,1,0:T(8,128)S(1)}, f32[1,128,1280]{2,1,0:T(8,128)S(1)}, u32[]{:S(2)}, u32[]{:S(2)}) %collective-permute-start.4) | collective-permute-done | bytes 655392 | tf_op jit(solution)/shard_map/vmap()/ppermute | solution.py:92
  98.5 2.1 %collective-permute-start.5 = (f32[1,128,1280]{2,1,0:T(8,128)}, f32[1,128,1280]{2,1,0:T(8,128)}, u32[]{:S(2)}, u32[]{:S(2)}) collective-permute-start(f32[1,128,1280]{2,1,0:T(8,128)} %get-tuple-element.32), channel_id=1, source_target_pairs={{2,0},{6,4},{10,8},{14,12},{1,3},{5,7},{9,11},{13,15},{18,16},{22,... | collective-permute-start | bytes 1966088 | tf_op jit(solution)/shard_map/vmap()/ppermute | solution.py:92
  101.9 2.1 %collective-permute-start.10 = (f32[1,128,1280]{2,1,0:T(8,128)}, f32[1,128,1280]{2,1,0:T(8,128)}, u32[]{:S(2)}, u32[]{:S(2)}) collective-permute-start(f32[1,128,1280]{2,1,0:T(8,128)} %get-tuple-element.38), channel_id=1, source_target_pairs={{13,15},{9,11},{5,7},{1,3},{14,12},{10,8},{6,4},{2,0},{29,31},{25,... | collective-permute-start | bytes 1966088 | tf_op jit(solution)/shard_map/vmap()/ppermute | solution.py:92
  104.1 2.2 %fusion = f32[1,128,40,64]{1,3,2,0:T(8,128)} fusion(bf16[128,40,64]{0,2,1:T(8,128)(2,1)S(1)} %bitcast.104, f32[1,128,40,64]{1,3,2,0:T(8,128)S(1)} %bitcast.103, f32[40,128]{1,0:T(8,128)S(1)} %copy-done.29, f32[128,128]{1,0:T(8,128)S(1)} %fusion.55, pred[128,128]{1,0:T(8,128)(4,1)S(1)} %copy-done.30, f32[40]{0:T(128)S(1)} %copy-done.35), kind=kOutput, calls=%fused_computation.12 | convolution fusion | flops 87818240 | bytes 3379360 | tf_op jit(solution)/shard_map/vmap(hij,ihp->jhp)/dot_general | solution.py:51
  107.6 1.4 %fusion.27 = (f32[1,128,1280]{2,1,0:T(8,128)S(1)}, f32[1,128,1280]{2,1,0:T(8,128)S(1)}) fusion(f32[1,129,1280]{2,1,0:T(8,128)S(1)} %copy-done.3, f32[1280]{0:T(1024)S(1)} %copy-done.28, pred[]{:T(512)S(6)} %eq.17, f32[1,128,1280]{2,1,0:T(8,128)} %collective-permute-done.5, f32[1,129,1280]{2,1,0:T(8,128)S(1)} %copy-done.4, ...), kind=kLoop, calls=%fused_computation.74 | loop fusion | flops 1310720 | bytes 3942402 | tf_op jit(solution)/shard_map/vmap(jit(_where))/select_n | solution.py:196
  109.1 5.5 %collective-permute-done.10 = f32[1,128,1280]{2,1,0:T(8,128)} collective-permute-done((f32[1,128,1280]{2,1,0:T(8,128)}, f32[1,128,1280]{2,1,0:T(8,128)}, u32[]{:S(2)}, u32[]{:S(2)}) %collective-permute-start.10) | collective-permute-done | bytes 655392 | tf_op jit(solution)/shard_map/vmap()/ppermute | solution.py:92
  114.6 1.3 fusion.26
  116.1 10.7 %collective-permute-start.11 = (f32[1,128,2560]{2,1,0:T(8,128)S(1)}, f32[1,128,2560]{2,1,0:T(8,128)S(1)}, u32[]{:S(2)}, u32[]{:S(2)}) collective-permute-start(f32[1,128,2560]{2,1,0:T(8,128)S(1)} %pad_maximum_fusion.1), channel_id=1, source_target_pairs={{0,1},{1,0},{2,3},{3,2},{4,5},{5,4},{6,7},{7,6},{8,9},{9,8},{10,11... | collective-permute-start | bytes 3932168 | tf_op jit(solution)/shard_map/vmap()/ppermute | solution.py:198
  126.8 1.3 convert_reduce_fusion
  (155 shorter events, 39.9 us)
Async XLA Ops:
  0.6 6.8 %copy-start = (bf16[1,128,128]{2,1,0:T(8,128)(2,1)S(1)}, bf16[1,128,128]{2,1,0:T(8,128)(2,1)}, u32[]{:S(2)}) copy-start(bf16[1,128,128]{2,1,0:T(8,128)(2,1)} %param.8) | copy-start | bytes 98308
  9.8 3.1 %collective-permute-start = (f32[1,129,2560]{2,0,1:T(1,128)S(1)}, f32[1,129,2560]{2,0,1:T(1,128)S(1)}, u32[]{:S(2)}, u32[]{:S(2)}) collective-permute-start(f32[1,129,2560]{2,0,1:T(1,128)S(1)} %copy.107), channel_id=1, source_target_pairs={{0,1},{1,0},{2,3},{3,2},{4,5},{5,4},{6,7},{7,6},{8,9},{9,8},{10,11... | collective-permute-start | bytes 3962888 | tf_op jit(solution)/shard_map/vmap()/ppermute | solution.py:181
  9.9 18.2 %copy-start.32 = (pred[129]{0:T(512)(128)(4,1)}, pred[129]{0:T(512)(128)(4,1)S(1)}, u32[]{:S(2)}) copy-start(pred[129]{0:T(512)(128)(4,1)S(1)} %iota_compare_fusion.1) | copy-start | bytes 391
  16.4 11.7 %collective-permute-start.1 = (f32[1,129,1280]{2,0,1:T(1,128)S(1)}, f32[1,129,1280]{2,0,1:T(1,128)S(1)}, u32[]{:S(2)}, u32[]{:S(2)}) collective-permute-start(f32[1,129,1280]{2,0,1:T(1,128)S(1)} %copy.109), channel_id=1, source_target_pairs={{0,2},{4,6},{8,10},{12,14},{3,1},{7,5},{11,9},{15,13},{16,18},{20,... | collective-permute-start | bytes 1981448 | tf_op jit(solution)/shard_map/vmap()/ppermute | solution.py:92
  19.2 17.8 %collective-permute-start.6 = (f32[1,129,1280]{2,0,1:T(1,128)}, f32[1,129,1280]{2,0,1:T(1,128)}, u32[]{:S(2)}, u32[]{:S(2)}) collective-permute-start(f32[1,129,1280]{2,0,1:T(1,128)} %copy.125), channel_id=1, source_target_pairs={{15,13},{11,9},{7,5},{3,1},{12,14},{8,10},{4,6},{0,2},{31,29},{27,... | collective-permute-start | bytes 1981448 | tf_op jit(solution)/shard_map/vmap()/ppermute | solution.py:92
  29.2 5.6 %copy-start.27 = (f32[2560]{0:T(1024)S(1)}, f32[2560]{0:T(1024)}, u32[]{:S(2)}) copy-start(f32[2560]{0:T(1024)} %get-tuple-element.52) | copy-start | bytes 30724
  29.9 11.6 %collective-permute-start.2 = (f32[1,129,1280]{2,0,1:T(1,128)S(1)}, f32[1,129,1280]{2,0,1:T(1,128)}, u32[]{:S(2)}, u32[]{:S(2)}) collective-permute-start(f32[1,129,1280]{2,0,1:T(1,128)S(1)} %copy.117), channel_id=1, source_target_pairs={{2,6},{10,14},{1,5},{9,13},{18,22},{26,30},{17,21},{25,29}} | collective-permute-start | bytes 1981448 | tf_op jit(solution)/shard_map/vmap()/ppermute | solution.py:92
  35.6 12.1 %collective-permute-start.12 = (f32[40]{0:T(128)}, f32[40]{0:T(128)}, u32[]{:S(2)}, u32[]{:S(2)}) collective-permute-start(f32[40]{0:T(128)} %reduce_sum.36), channel_id=1, source_target_pairs={{0,1},{1,0},{2,3},{3,2},{4,5},{5,4},{6,7},{7,6},{8,9},{9,8},{10,11... | collective-permute-start | bytes 488 | tf_op jit(solution)/shard_map/ppermute | solution.py:64
  37.0 7.3 %copy-start.24 = (f32[1280]{0:T(1024)}, f32[1280]{0:T(1024)S(1)}, u32[]{:S(2)}) copy-start(f32[1280]{0:T(1024)S(1)} %fusion.70) | copy-start | bytes 15364
  37.7 6.6 %copy-start.22 = (f32[1280]{0:T(1024)}, f32[1280]{0:T(1024)S(1)}, u32[]{:S(2)}) copy-start(f32[1280]{0:T(1024)S(1)} %fusion.69) | copy-start | bytes 15364
  44.3 24.5 %copy-start.2 = (f32[1,129,1280]{2,1,0:T(8,128)S(1)}, f32[1,129,1280]{2,1,0:T(8,128)}, u32[]{:S(2)}) copy-start(f32[1,129,1280]{2,1,0:T(8,128)} %get-tuple-element.58) | copy-start | bytes 1981444
  45.8 30.3 %collective-permute-start.7 = (f32[1,129,1280]{2,0,1:T(1,128)}, f32[1,129,1280]{2,0,1:T(1,128)}, u32[]{:S(2)}, u32[]{:S(2)}) collective-permute-start(f32[1,129,1280]{2,0,1:T(1,128)} %copy.129), channel_id=1, source_target_pairs={{13,9},{5,1},{14,10},{6,2},{29,25},{21,17},{30,26},{22,18}} | collective-permute-start | bytes 1981448 | tf_op jit(solution)/shard_map/vmap()/ppermute | solution.py:92
  48.9 2.6 %collective-permute-start.13 = (f32[40]{0:T(128)}, f32[40]{0:T(128)}, u32[]{:S(2)}, u32[]{:S(2)}) collective-permute-start(f32[40]{0:T(128)} %add.176), channel_id=1, source_target_pairs={{0,2},{1,3},{2,0},{3,1},{4,6},{5,7},{6,4},{7,5},{8,10},{9,11},{10,... | collective-permute-start | bytes 488 | tf_op jit(solution)/shard_map/ppermute | solution.py:64
  52.8 4.8 %collective-permute-start.14 = (f32[40]{0:T(128)}, f32[40]{0:T(128)}, u32[]{:S(2)}, u32[]{:S(2)}) collective-permute-start(f32[40]{0:T(128)} %add.177), channel_id=1, source_target_pairs={{0,4},{1,5},{2,6},{3,7},{4,0},{5,1},{6,2},{7,3},{8,12},{9,13},{10,... | collective-permute-start | bytes 488 | tf_op jit(solution)/shard_map/ppermute | solution.py:64
  58.8 3.5 %collective-permute-start.15 = (f32[40]{0:T(128)}, f32[40]{0:T(128)}, u32[]{:S(2)}, u32[]{:S(2)}) collective-permute-start(f32[40]{0:T(128)} %add.178), channel_id=1, source_target_pairs={{0,8},{1,9},{2,10},{3,11},{4,12},{5,13},{6,14},{7,15},{8,0},{9,1},... | collective-permute-start | bytes 488 | tf_op jit(solution)/shard_map/ppermute | solution.py:64
  63.5 2.6 %collective-permute-start.16 = (f32[40]{0:T(128)}, f32[40]{0:T(128)}, u32[]{:S(2)}, u32[]{:S(2)}) collective-permute-start(f32[40]{0:T(128)} %add.179), channel_id=1, source_target_pairs={{0,16},{16,0},{1,17},{17,1},{2,18},{18,2},{3,19},{19,3},{4,20},{20... | collective-permute-start | bytes 488 | tf_op jit(solution)/shard_map/ppermute | solution.py:64
  71.8 4.3 %copy-start.33 = (pred[129]{0:T(512)(128)(4,1)S(1)}, pred[129]{0:T(512)(128)(4,1)}, u32[]{:S(2)}) copy-start(pred[129]{0:T(512)(128)(4,1)} %copy-done.32) | copy-start | bytes 391
  75.2 4.9 %collective-permute-start.3 = (f32[1,129,1280]{2,0,1:T(1,128)S(1)}, f32[1,129,1280]{2,0,1:T(1,128)S(1)}, u32[]{:S(2)}, u32[]{:S(2)}) collective-permute-start(f32[1,129,1280]{2,0,1:T(1,128)S(1)} %copy.120), channel_id=1, source_target_pairs={{6,14},{5,13},{22,30},{21,29}} | collective-permute-start | bytes 1981448 | tf_op jit(solution)/shard_map/vmap()/ppermute | solution.py:92
  78.2 12.3 %collective-permute-start.8 = (f32[1,129,1280]{2,0,1:T(1,128)S(1)}, f32[1,129,1280]{2,0,1:T(1,128)S(1)}, u32[]{:S(2)}, u32[]{:S(2)}) collective-permute-start(f32[1,129,1280]{2,0,1:T(1,128)S(1)} %copy.132), channel_id=1, source_target_pairs={{9,1},{10,2},{25,17},{26,18}} | collective-permute-start | bytes 1981448 | tf_op jit(solution)/shard_map/vmap()/ppermute | solution.py:92
  80.4 17.1 %collective-permute-start.4 = (f32[1,128,1280]{2,1,0:T(8,128)S(1)}, f32[1,128,1280]{2,1,0:T(8,128)S(1)}, u32[]{:S(2)}, u32[]{:S(2)}) collective-permute-start(f32[1,128,1280]{2,1,0:T(8,128)S(1)} %copy_add_fusion.1), channel_id=1, source_target_pairs={{6,2},{14,10},{5,1},{13,9},{22,18},{30,26},{21,17},{29,25}} | collective-permute-start | bytes 1966088 | tf_op jit(solution)/shard_map/vmap()/ppermute | solution.py:92
  90.5 7.0 %copy-start.6 = (f32[1,129,1280]{2,1,0:T(8,128)S(1)}, f32[1,129,1280]{2,1,0:T(8,128)}, u32[]{:S(2)}) copy-start(f32[1,129,1280]{2,1,0:T(8,128)} %get-tuple-element.63) | copy-start | bytes 1981444
  90.6 10.0 %collective-permute-start.9 = (f32[1,128,1280]{2,1,0:T(8,128)S(1)}, f32[1,128,1280]{2,1,0:T(8,128)S(1)}, u32[]{:S(2)}, u32[]{:S(2)}) collective-permute-start(f32[1,128,1280]{2,1,0:T(8,128)S(1)} %copy_add_fusion), channel_id=1, source_target_pairs={{9,13},{1,5},{10,14},{2,6},{25,29},{17,21},{26,30},{18,22}} | collective-permute-start | bytes 1966088 | tf_op jit(solution)/shard_map/vmap()/ppermute | solution.py:92
  98.5 9.1 %collective-permute-start.5 = (f32[1,128,1280]{2,1,0:T(8,128)}, f32[1,128,1280]{2,1,0:T(8,128)}, u32[]{:S(2)}, u32[]{:S(2)}) collective-permute-start(f32[1,128,1280]{2,1,0:T(8,128)} %get-tuple-element.32), channel_id=1, source_target_pairs={{2,0},{6,4},{10,8},{14,12},{1,3},{5,7},{9,11},{13,15},{18,16},{22,... | collective-permute-start | bytes 1966088 | tf_op jit(solution)/shard_map/vmap()/ppermute | solution.py:92
  101.9 12.7 %collective-permute-start.10 = (f32[1,128,1280]{2,1,0:T(8,128)}, f32[1,128,1280]{2,1,0:T(8,128)}, u32[]{:S(2)}, u32[]{:S(2)}) collective-permute-start(f32[1,128,1280]{2,1,0:T(8,128)} %get-tuple-element.38), channel_id=1, source_target_pairs={{13,15},{9,11},{5,7},{1,3},{14,12},{10,8},{6,4},{2,0},{29,31},{25,... | collective-permute-start | bytes 1966088 | tf_op jit(solution)/shard_map/vmap()/ppermute | solution.py:92
  107.6 7.0 %copy-start.5 = (f32[1,129,1280]{2,1,0:T(8,128)S(1)}, f32[1,129,1280]{2,1,0:T(8,128)}, u32[]{:S(2)}) copy-start(f32[1,129,1280]{2,1,0:T(8,128)} %get-tuple-element.48) | copy-start | bytes 1981444
  107.6 7.0 %copy-start.12 = (f32[1,128,1280]{2,1,0:T(8,128)S(1)}, f32[1,128,1280]{2,1,0:T(8,128)}, u32[]{:S(2)}) copy-start(f32[1,128,1280]{2,1,0:T(8,128)} %get-tuple-element.39) | copy-start | bytes 1966084
  107.6 7.0 %copy-start.23 = (f32[1280]{0:T(1024)S(1)}, f32[1280]{0:T(1024)}, u32[]{:S(2)}) copy-start(f32[1280]{0:T(1024)} %copy-done.22) | copy-start | bytes 15364
  107.6 7.0 %copy-start.26 = (f32[1280]{0:T(1024)S(1)}, f32[1280]{0:T(1024)}, u32[]{:S(2)}) copy-start(f32[1280]{0:T(1024)} %fusion.64) | copy-start | bytes 15364
  116.0 10.9 %copy-start.16 = (bf16[1,128,2560]{1,2,0:T(8,128)(2,1)S(1)}, bf16[1,128,2560]{1,2,0:T(8,128)(2,1)}, u32[]{:S(2)}) copy-start(bf16[1,128,2560]{1,2,0:T(8,128)(2,1)} %copy.110) | copy-start | bytes 1966084
  116.0 10.9 %copy-start.17 = (bf16[1,128,2560]{1,2,0:T(8,128)(2,1)S(1)}, bf16[1,128,2560]{1,2,0:T(8,128)(2,1)}, u32[]{:S(2)}) copy-start(bf16[1,128,2560]{1,2,0:T(8,128)(2,1)} %copy.136) | copy-start | bytes 1966084
  116.0 10.9 %copy-start.31 = (pred[128,128]{1,0:T(8,128)(4,1)S(1)}, pred[128,128]{1,0:T(8,128)(4,1)}, u32[]{:S(2)}) copy-start(pred[128,128]{1,0:T(8,128)(4,1)} %iota_compare_fusion) | copy-start | bytes 49156
  116.1 13.7 %collective-permute-start.11 = (f32[1,128,2560]{2,1,0:T(8,128)S(1)}, f32[1,128,2560]{2,1,0:T(8,128)S(1)}, u32[]{:S(2)}, u32[]{:S(2)}) collective-permute-start(f32[1,128,2560]{2,1,0:T(8,128)S(1)} %pad_maximum_fusion.1), channel_id=1, source_target_pairs={{0,1},{1,0},{2,3},{3,2},{4,5},{5,4},{6,7},{7,6},{8,9},{9,8},{10,11... | collective-permute-start | bytes 3932168 | tf_op jit(solution)/shard_map/vmap()/ppermute | solution.py:198
  (21 other events, 46.0 us)

commit v11 on v9

--- a/solution.py
+++ b/solution.py
@@ -61,11 +61,12 @@
 def gather_totals(totals, skip_part, position, count):
     rows = jnp.arange(count)[:, None]
     table = jnp.concatenate([jnp.where(rows == position, totals[None, :], 0.0), skip_part[None, :]], 0)
-    tables = [table]
-    for bit in range(count.bit_length() - 1):
-        table = table + lax.ppermute(table, "ctx", xor_pairs(count, bit))
-        tables.append(table)
-    return tables
+    return [table]
+
+
+def extend_totals(tables, count, start_bit, stop_bit):
+    for bit in range(start_bit, min(stop_bit, count.bit_length() - 1)):
+        tables.append(tables[-1] + lax.ppermute(tables[-1], "ctx", xor_pairs(count, bit)))
 
 
 def take_half(array, upper):
@@ -207,12 +208,15 @@
     got = [got[..., : got.shape[-1] // 2], got[..., got.shape[-1] // 2 :]]
     lows = []
     totals = []
+    extend_totals(tables, count, 0, 1)
     for way, state, other in zip(ways, states, got):
         own = take_half(state, way.upper)
         low_block = jnp.where(way.upper, other, own)
         high_block = jnp.where(way.upper, own, other)
         lows.append(low_block)
         totals.append(way.gain(1, 2 * way.pair + 1, 1) * low_block + high_block)
+    tables[-1], _ = lax.optimization_barrier((tables[-1], totals))
+    extend_totals(tables, count, 1, count.bit_length())
     pair_prefixes, anchor = pair_scans(ways, totals)
     lifted_parts = []
     keep_parts = []
@@ -225,7 +229,7 @@
     got = got * unit
     half = got.shape[-1] // 2
     others = [got[..., :half], got[..., half:]]
-    return (keep_parts, others, [way.upper for way in ways]), anchor
+    return (keep_parts, others, [way.upper for way in ways]), anchor, tables[-1]
 
 
 def block_carried_grads(write_map, value_scale, decayed_vals, decayed_cot, carried, local_grads):
@@ -266,13 +270,13 @@
     position = lax.axis_index("ctx")
     count = lax.axis_size("ctx")
     tables = jax.vmap(gather_totals, (0, 0, None, None))(totals, skip_parts, position, count)
-    grad_skip = jnp.sum(tables[-1][:, count], axis=0)
+    head_width = token_values.shape[2] // decay_codes.shape[2]
+    carried, anchor, final_table = jax.vmap(carried_pair, (0, 0, 0, None, None, None))(
+        tables, fwd_state, adj_state, position, count, head_width
+    )
+    grad_skip = jnp.sum(final_table[:, count], axis=0)
     for bit in range(lax.axis_size("dp").bit_length() - 1):
         grad_skip = grad_skip + lax.ppermute(grad_skip, "dp", xor_pairs(lax.axis_size("dp"), bit))
-    head_width = token_values.shape[2] // decay_codes.shape[2]
-    carried, anchor = jax.vmap(carried_pair, (0, 0, 0, None, None, None))(
-        tables, fwd_state, adj_state, position, count, head_width
-    )
     local_inputs, _ = lax.optimization_barrier(
         ((token_values, cotangent, write_coeffs, read_coeffs, within), anchor)
     )

time: 121 us -> 106 us (0.88)
  waiting for transfers between devices: 29.6 us -> 20.2 us
  other arithmetic: 27.8 us -> 25.5 us
  starting transfers between devices: 35.2 us -> 33.5 us
  local copies, waits for them, and re-layouts: 16.9 us -> 15.5 us
    ppermute x10, waiting for transfers between devices: 29.5 us -> 19.5 us  [exchange(): lax.ppermute(p, 'ctx', pairs)]
    ppermute x1, starting transfers between devices: 9.9 us -> 7.66 us  [carried_pair(): lax.ppermute(jnp.concatenate(lifted_parts, -1), 'ctx', [(i, i ^ 1) for i...]
  transfers between devices with their start and end apart: 17 -> 17, of which waited for: 8 -> 7; matrix products, arithmetic and copies ran while one was open for 31% -> 32% of each run, Pallas kernels for 0% -> 0%
where the time goes in v11:
time: 106 us; the launch traced here: 104 us
  starting transfers between devices  33.5 us (32%)
  other arithmetic  25.5 us (24%)
  waiting for transfers between devices  20.2 us (19%)
  local copies, waits for them, and re-layouts  15.5 us (15%)
  matrix products  7.65 us (7%)
  between operations  2.04 us (2%)
    ppermute x10, waiting for transfers between devices, exchange(): lax.ppermute(p, 'ctx', pairs)  19.5 us
    ppermute x10, starting transfers between devices, exchange(): lax.ppermute(p, 'ctx', pairs)  18 us
    ppermute x1, starting transfers between devices, carried_pair(): lax.ppermute(jnp.concatenate(lifted_parts, -1), 'ctx', [(i, i ^ 1) for i...  7.66 us
    ppermute x4, starting transfers between devices, extend_totals(): lax.ppermute(tables[-1], 'ctx', xor_pairs(count, bit))  6.09 us
    select_n x2, other arithmetic, down_send(): jnp.where(self.way.upper, self.pair_gain(0, pair, 1) * prefix + pair_tota...  5.74 us
    unnamed x63, local copies, waits for them, and re-layouts  4.71 us
    select_n x2, other arithmetic, carried_pair(): lifted_parts.append(jnp.where(way.upper, pair_prefix, lifted))  3.33 us
    add x1, other arithmetic, carried_pair(): totals.append(way.gain(1, 2 * way.pair + 1, 1) * low_block + high_block)  3.25 us
  transfers between devices with their start and end apart: 17, of which 7 were waited for; matrix products, arithmetic and copies ran while one was open for 32% of the time, Pallas kernels for 0%

profile of v11, /device:TPU:1, one launch (start us, length us, event | category | flops | bytes accessed | tf_op | source)
XLA Modules:
  0.0 104.4 jit_solution(3945430541708249867)
XLA Ops:
  1.8 1.4 %copy.45 = bf16[1,128,2560]{1,2,0:T(8,128)(2,1)S(1)} copy(bf16[1,128,2560]{2,1,0:T(8,128)(2,1)} %param.6) | data formatting | bytes 1310720 | tf_op args[0]
  3.7 1.2 %fusion.1 = (f32[2560]{0:T(1024)S(1)}, bf16[1,128,2560]{1,2,0:T(8,128)(2,1)}, bf16[1,128,2560]{1,2,0:T(8,128)(2,1)S(1)}) fusion(bf16[1,128,2560]{1,2,0:T(8,128)(2,1)S(1)} %copy.46, bf16[1,128,2560]{1,2,0:T(8,128)(2,1)S(1)} %copy.45, f32[128,40]{0,1:T(8,128)S(1)} %get-tuple-element.227, f32[128,40]{0,1:T(8,128)S(1)} %get-tuple-element.228), kind=kLoop, calls=%fused_computation.14 | loop fusion | flops 2618880 | bytes 2672640 | tf_op jit(solution)/shard_map/vmap()/reduce_sum | solution.py:25
  6.8 1.2 %pad_maximum_fusion = f32[1,128,2560]{1,2,0:T(8,128)} fusion(f32[1,128,1280]{1,2,0:T(8,128)S(1)} %get-tuple-element.255, f32[1,128,1280]{1,2,0:T(8,128)S(1)} %get-tuple-element.256), kind=kLoop, calls=%fused_computation.19 | loop fusion | flops 327680 | bytes 2621440 | tf_op jit(solution)/shard_map/vmap()/concatenate | solution.py:206
  11.9 3.2 %select_add_fusion.1 = (f32[1,128,1280]{1,2,0:T(8,128)}, f32[1,128,1280]{1,2,0:T(8,128)}, f32[1,128,1280]{1,2,0:T(8,128)}, f32[1,128,1280]{1,2,0:T(8,128)}) fusion(f32[1,128,2560]{1,2,0:T(8,128)} %collective-permute-done.1, f32[1280]{0:T(1024)S(1)} %broadcast_in_dim.215, pred[]{:T(512)S(6)} %eq.43, f32[1,128,2560]{1,2,0:T(8,128)S(1)} %convolution_bitcast_fusion.1, ...), kind=kLoop, calls=%fused_computation.55 | loop fusion | flops 1638400 | bytes 6563842 | tf_op jit(solution)/shard_map/vmap()/add | solution.py:217
  15.1 2.3 %collective-permute-start.3 = (f32[1,17,40]{2,1,0:T(8,128)S(1)}, f32[1,17,40]{2,1,0:T(8,128)S(1)}, u32[]{:S(2)}, u32[]{:S(2)}) collective-permute-start(f32[1,17,40]{2,1,0:T(8,128)S(1)} %fusion.95), channel_id=1, source_target_pairs={{0,2},{1,3},{2,0},{3,1},{4,6},{5,7},{6,4},{7,5},{8,10},{9,11},{10,... | collective-permute-start | bytes 8168 | tf_op jit(solution)/shard_map/vmap()/ppermute | solution.py:69
  17.8 1.3 %collective-permute-start.2 = (f32[1,128,1280]{1,2,0:T(8,128)}, f32[1,128,1280]{1,2,0:T(8,128)S(1)}, u32[]{:S(2)}, u32[]{:S(2)}) collective-permute-start(f32[1,128,1280]{1,2,0:T(8,128)} %get-tuple-element.218), channel_id=1, source_target_pairs={{0,2},{4,6},{8,10},{12,14},{3,1},{7,5},{11,9},{15,13},{16,18},{20,... | collective-permute-start | bytes 1966088 | tf_op jit(solution)/shard_map/vmap()/ppermute | solution.py:113
  19.1 1.3 %collective-permute-start.10 = (f32[1,128,1280]{1,2,0:T(8,128)}, f32[1,128,1280]{1,2,0:T(8,128)S(1)}, u32[]{:S(2)}, u32[]{:S(2)}) collective-permute-start(f32[1,128,1280]{1,2,0:T(8,128)} %get-tuple-element.222), channel_id=1, source_target_pairs={{15,13},{11,9},{7,5},{3,1},{12,14},{8,10},{4,6},{0,2},{31,29},{27,... | collective-permute-start | bytes 1966088 | tf_op jit(solution)/shard_map/vmap()/ppermute | solution.py:113
  20.4 1.4 %collective-permute-start.4 = (f32[1,17,40]{2,1,0:T(8,128)S(1)}, f32[1,17,40]{2,1,0:T(8,128)S(1)}, u32[]{:S(2)}, u32[]{:S(2)}) collective-permute-start(f32[1,17,40]{2,1,0:T(8,128)S(1)} %add.265), channel_id=1, source_target_pairs={{0,4},{1,5},{2,6},{3,7},{4,0},{5,1},{6,2},{7,3},{8,12},{9,13},{10,... | collective-permute-start | bytes 8168 | tf_op jit(solution)/shard_map/vmap()/ppermute | solution.py:69
  23.0 2.3 %collective-permute-start.5 = (f32[1,17,40]{2,1,0:T(8,128)S(1)}, f32[1,17,40]{2,1,0:T(8,128)S(1)}, u32[]{:S(2)}, u32[]{:S(2)}) collective-permute-start(f32[1,17,40]{2,1,0:T(8,128)S(1)} %add.268), channel_id=1, source_target_pairs={{0,8},{1,9},{2,10},{3,11},{4,12},{5,13},{6,14},{7,15},{8,0},{9,1},... | collective-permute-start | bytes 8168 | tf_op jit(solution)/shard_map/vmap()/ppermute | solution.py:69
  33.5 3.3 %collective-permute-start.6 = (f32[1,128,1280]{1,2,0:T(8,128)S(1)}, f32[1,128,1280]{1,2,0:T(8,128)S(1)}, u32[]{:S(2)}, u32[]{:S(2)}) collective-permute-start(f32[1,128,1280]{1,2,0:T(8,128)S(1)} %add_select_fusion.3), channel_id=1, source_target_pairs={{2,6},{10,14},{1,5},{9,13},{18,22},{26,30},{17,21},{25,29}} | collective-permute-start | bytes 1966088 | tf_op jit(solution)/shard_map/vmap()/ppermute | solution.py:113
  37.3 1.3 %collective-permute-start.11 = (f32[1,128,1280]{1,2,0:T(8,128)S(1)}, f32[1,128,1280]{1,2,0:T(8,128)S(1)}, u32[]{:S(2)}, u32[]{:S(2)}) collective-permute-start(f32[1,128,1280]{1,2,0:T(8,128)S(1)} %add_select_fusion.1), channel_id=1, source_target_pairs={{13,9},{5,1},{14,10},{6,2},{29,25},{21,17},{30,26},{22,18}} | collective-permute-start | bytes 1966088 | tf_op jit(solution)/shard_map/vmap()/ppermute | solution.py:113
  38.6 1.3 %collective-permute-start.16 = (f32[40]{0:T(128)S(1)}, f32[40]{0:T(128)S(1)}, u32[]{:S(2)}, u32[]{:S(2)}) collective-permute-start(f32[40]{0:T(128)S(1)} %slice_bitcast_fusion.5), channel_id=1, source_target_pairs={{0,16},{16,0},{1,17},{17,1},{2,18},{18,2},{3,19},{19,3},{4,20},{20... | collective-permute-start | bytes 488 | tf_op jit(solution)/shard_map/ppermute | solution.py:279
  39.9 4.4 %collective-permute-done.6 = f32[1,128,1280]{1,2,0:T(8,128)S(1)} collective-permute-done((f32[1,128,1280]{1,2,0:T(8,128)S(1)}, f32[1,128,1280]{1,2,0:T(8,128)S(1)}, u32[]{:S(2)}, u32[]{:S(2)}) %collective-permute-start.6) | collective-permute-done | bytes 655392 | tf_op jit(solution)/shard_map/vmap()/ppermute | solution.py:113
  45.2 3.4 %collective-permute-done.11 = f32[1,128,1280]{1,2,0:T(8,128)S(1)} collective-permute-done((f32[1,128,1280]{1,2,0:T(8,128)S(1)}, f32[1,128,1280]{1,2,0:T(8,128)S(1)}, u32[]{:S(2)}, u32[]{:S(2)}) %collective-permute-start.11) | collective-permute-done | bytes 655392 | tf_op jit(solution)/shard_map/vmap()/ppermute | solution.py:113
  48.8 1.3 %collective-permute-start.12 = (f32[1,128,1280]{1,2,0:T(8,128)S(1)}, f32[1,128,1280]{1,2,0:T(8,128)S(1)}, u32[]{:S(2)}, u32[]{:S(2)}) collective-permute-start(f32[1,128,1280]{1,2,0:T(8,128)S(1)} %multiply_add_fusion.2), channel_id=1, source_target_pairs={{9,1},{10,2},{25,17},{26,18}} | collective-permute-start | bytes 1966088 | tf_op jit(solution)/shard_map/vmap()/ppermute | solution.py:113
  50.7 1.1 %broadcast_add_fusion.1 = f32[1,128,1280]{1,2,0:T(8,128)} fusion(f32[1,128,1280]{1,2,0:T(8,128)S(1)} %collective-permute-done.7, f32[1280]{0:T(1024)S(1)} %mul.298), kind=kLoop, calls=%fused_computation.78 | loop fusion | flops 163840 | bytes 1315840 | tf_op jit(solution)/shard_map/vmap()/add | solution.py:175
  51.8 1.3 %collective-permute-start.8 = (f32[1,128,1280]{1,2,0:T(8,128)}, f32[1,128,1280]{1,2,0:T(8,128)}, u32[]{:S(2)}, u32[]{:S(2)}) collective-permute-start(f32[1,128,1280]{1,2,0:T(8,128)} %broadcast_add_fusion.1), channel_id=1, source_target_pairs={{6,2},{14,10},{5,1},{13,9},{22,18},{30,26},{21,17},{29,25}} | collective-permute-start | bytes 1966088 | tf_op jit(solution)/shard_map/vmap()/ppermute | solution.py:113
  53.1 8.0 %collective-permute-done.12 = f32[1,128,1280]{1,2,0:T(8,128)S(1)} collective-permute-done((f32[1,128,1280]{1,2,0:T(8,128)S(1)}, f32[1,128,1280]{1,2,0:T(8,128)S(1)}, u32[]{:S(2)}, u32[]{:S(2)}) %collective-permute-start.12) | collective-permute-done | bytes 655392 | tf_op jit(solution)/shard_map/vmap()/ppermute | solution.py:113
  61.1 1.2 %broadcast_add_fusion = f32[1,128,1280]{1,2,0:T(8,128)} fusion(f32[1,128,1280]{1,2,0:T(8,128)S(1)} %collective-permute-done.12, f32[1280]{0:T(1024)S(1)} %mul.320), kind=kLoop, calls=%fused_computation.76 | loop fusion | flops 163840 | bytes 1315840 | tf_op jit(solution)/shard_map/vmap()/add | solution.py:175
  62.2 3.1 %collective-permute-start.13 = (f32[1,128,1280]{1,2,0:T(8,128)}, f32[1,128,1280]{1,2,0:T(8,128)}, u32[]{:S(2)}, u32[]{:S(2)}) collective-permute-start(f32[1,128,1280]{1,2,0:T(8,128)} %broadcast_add_fusion), channel_id=1, source_target_pairs={{9,13},{1,5},{10,14},{2,6},{25,29},{17,21},{26,30},{18,22}} | collective-permute-start | bytes 1966088 | tf_op jit(solution)/shard_map/vmap()/ppermute | solution.py:113
  65.4 1.1 %copy.48 = bf16[1,128,2560]{1,2,0:T(8,128)(2,1)} copy(bf16[1,128,2560]{2,1,0:T(8,128)(2,1)S(1)} %copy-done.1) | data formatting | bytes 1310720 | tf_op jit(solution)/shard_map/optimization_barrier | solution.py:280
  66.6 1.3 %copy.51 = f32[1,128,2560]{1,2,0:T(8,128)} copy(bf16[1,128,2560]{2,1,0:T(8,128)(2,1)S(1)} %copy-done.1) | data formatting | bytes 1966080 | tf_op jit(solution)/shard_map/vmap()/convert_element_type | solution.py:53
  68.8 3.0 %add_select_fusion.2 = (f32[1,128,1280]{1,2,0:T(8,128)}, f32[1,128,1280]{1,2,0:T(8,128)}) fusion(f32[1,128,1280]{1,2,0:T(8,128)S(1)} %copy-done.5, f32[1280]{0:T(1024)S(1)} %broadcast_in_dim.228, pred[]{:T(512)S(6)} %eq.43, f32[1,128,1280]{1,2,0:T(8,128)} %copy-done.17, f32[1,128,1280]{1,2,0:T(8,128)} %collective-permute-done.8, f32[1280]{0:T(1024)} %select_n.505, ...), kind=kLoop, calls=%fused_computation.50 | loop fusion | flops 1146880 | bytes 3947521 | tf_op jit(solution)/shard_map/vmap(jit(_where))/select_n | solution.py:157
  71.7 2.3 %collective-permute-start.9 = (f32[1,128,1280]{1,2,0:T(8,128)}, f32[1,128,1280]{1,2,0:T(8,128)}, u32[]{:S(2)}, u32[]{:S(2)}) collective-permute-start(f32[1,128,1280]{1,2,0:T(8,128)} %get-tuple-element.212), channel_id=1, source_target_pairs={{2,0},{6,4},{10,8},{14,12},{1,3},{5,7},{9,11},{13,15},{18,16},{22,... | collective-permute-start | bytes 1966088 | tf_op jit(solution)/shard_map/vmap()/ppermute | solution.py:113
  74.0 2.8 %add_select_fusion = (f32[1,128,1280]{1,2,0:T(8,128)}, f32[1,128,1280]{1,2,0:T(8,128)}) fusion(f32[1,128,1280]{1,2,0:T(8,128)S(1)} %copy-done.4, f32[1280]{0:T(1024)S(1)} %broadcast_in_dim.248, pred[]{:T(512)S(6)} %eq.46, f32[1,128,1280]{1,2,0:T(8,128)S(1)} %copy-done.16, f32[1,128,1280]{1,2,0:T(8,128)} %collective-permute-done.13, f32[1280]{0:T(1024)S(1)} %copy-done.26, ...), kind=kLoop, calls=%fused_computation.43 | loop fusion | flops 1146880 | bytes 3947521 | tf_op jit(solution)/shard_map/vmap(jit(_where))/select_n | solution.py:157
  76.8 2.2 %collective-permute-start.14 = (f32[1,128,1280]{1,2,0:T(8,128)}, f32[1,128,1280]{1,2,0:T(8,128)}, u32[]{:S(2)}, u32[]{:S(2)}) collective-permute-start(f32[1,128,1280]{1,2,0:T(8,128)} %get-tuple-element.216), channel_id=1, source_target_pairs={{13,15},{9,11},{5,7},{1,3},{14,12},{10,8},{6,4},{2,0},{29,31},{25,... | collective-permute-start | bytes 1966088 | tf_op jit(solution)/shard_map/vmap()/ppermute | solution.py:113
  79.0 2.2 %fusion = f32[1,128,40,64]{1,3,2,0:T(8,128)} fusion(bf16[128,40,64]{0,2,1:T(8,128)(2,1)S(1)} %bitcast.247, f32[1,128,40,64]{1,3,2,0:T(8,128)S(1)} %bitcast.246, f32[40,128]{1,0:T(8,128)S(1)} %copy-done.27, f32[128,128]{1,0:T(8,128)S(1)} %fusion.46, pred[128,128]{1,0:T(8,128)(4,1)S(1)} %copy-done.28, f32[40]{0:T(128)S(1)} %copy-done.29), kind=kOutput, calls=%fused_computation.13 | convolution fusion | flops 87818240 | bytes 3379360 | tf_op jit(solution)/shard_map/vmap(hij,ihp->jhp)/dot_general | solution.py:51
  82.7 1.8 %fusion.18 = (f32[1,128,1280]{1,2,0:T(8,128)S(1)}, f32[1,128,1280]{1,2,0:T(8,128)S(1)}) fusion(f32[1,128,1280]{1,2,0:T(8,128)S(1)} %copy-done.2, f32[1280]{0:T(1024)S(1)} %broadcast_in_dim.245, pred[]{:T(512)S(6)} %eq.43, f32[1,128,1280]{1,2,0:T(8,128)} %collective-permute-done.9, f32[1,128,1280]{1,2,0:T(8,128)S(1)} %copy-done.14, ...), kind=kLoop, calls=%fused_computation.48 | loop fusion | flops 1310720 | bytes 3942402 | tf_op jit(solution)/shard_map/vmap(jit(_where))/select_n | solution.py:225
  84.6 3.5 %collective-permute-done.14 = f32[1,128,1280]{1,2,0:T(8,128)} collective-permute-done((f32[1,128,1280]{1,2,0:T(8,128)}, f32[1,128,1280]{1,2,0:T(8,128)}, u32[]{:S(2)}, u32[]{:S(2)}) %collective-permute-start.14) | collective-permute-done | bytes 655392 | tf_op jit(solution)/shard_map/vmap()/ppermute | solution.py:113
  88.0 1.5 %fusion.17 = (f32[1,128,1280]{1,2,0:T(8,128)S(1)}, f32[1,128,1280]{1,2,0:T(8,128)S(1)}) fusion(f32[1,128,1280]{1,2,0:T(8,128)S(1)} %copy-done.3, f32[1280]{0:T(1024)S(1)} %broadcast_in_dim.264, pred[]{:T(512)S(6)} %eq.46, f32[1,128,1280]{1,2,0:T(8,128)} %collective-permute-done.14, f32[1,128,1280]{1,2,0:T(8,128)S(1)} %copy-done.12, ...), kind=kLoop, calls=%fused_computation.41 | loop fusion | flops 1310720 | bytes 3942402 | tf_op jit(solution)/shard_map/vmap(jit(_where))/select_n | solution.py:225
  89.7 7.7 %collective-permute-start.15 = (f32[1,128,2560]{1,2,0:T(8,128)S(1)}, f32[1,128,2560]{1,2,0:T(8,128)S(1)}, u32[]{:S(2)}, u32[]{:S(2)}) collective-permute-start(f32[1,128,2560]{1,2,0:T(8,128)S(1)} %pad_maximum_fusion.1), channel_id=1, source_target_pairs={{0,1},{1,0},{2,3},{3,2},{4,5},{5,4},{6,7},{7,6},{8,9},{9,8},{10,11... | collective-permute-start | bytes 3932168 | tf_op jit(solution)/shard_map/vmap()/ppermute | solution.py:227
  97.3 1.3 %convert_reduce_fusion = bf16[128,128]{1,0:T(8,128)(2,1)S(1)} fusion(f32[40,128]{1,0:T(8,128)S(1)} %copy-done.27, pred[128,128]{1,0:T(8,128)(4,1)S(1)} %copy-done.28, bf16[128,40,64]{0,2,1:T(8,128)(2,1)S(1)} %bitcast.248, bf16[128,40,64]{0,2,1:T(8,128)(2,1)S(1)} %bitcast.249), kind=kOutput, calls=%fused_computation.2 | convolution fusion | flops 88457216 | bytes 1380352 | tf_op jit(solution)/shard_map/vmap(ihp,jhp->hij)/dot_general | solution.py:45
  (215 shorter events, 26.7 us)
Async XLA Ops:
  5.1 6.1 %collective-permute-start = (f32[1,17,40]{2,1,0:T(8,128)S(1)}, f32[1,17,40]{2,1,0:T(8,128)S(1)}, u32[]{:S(2)}, u32[]{:S(2)}) collective-permute-start(f32[1,17,40]{2,1,0:T(8,128)S(1)} %pad_maximum_fusion.2), channel_id=1, source_target_pairs={{0,1},{1,0},{2,3},{3,2},{4,5},{5,4},{6,7},{7,6},{8,9},{9,8},{10,11... | collective-permute-start | bytes 8168 | tf_op jit(solution)/shard_map/vmap()/ppermute | solution.py:69
  8.0 3.9 %collective-permute-start.1 = (f32[1,128,2560]{1,2,0:T(8,128)}, f32[1,128,2560]{1,2,0:T(8,128)}, u32[]{:S(2)}, u32[]{:S(2)}) collective-permute-start(f32[1,128,2560]{1,2,0:T(8,128)} %pad_maximum_fusion), channel_id=1, source_target_pairs={{0,1},{1,0},{2,3},{3,2},{4,5},{5,4},{6,7},{7,6},{8,9},{9,8},{10,11... | collective-permute-start | bytes 3932168 | tf_op jit(solution)/shard_map/vmap()/ppermute | solution.py:207
  15.1 17.9 %copy-start.5 = (f32[1,128,1280]{1,2,0:T(8,128)S(1)}, f32[1,128,1280]{1,2,0:T(8,128)}, u32[]{:S(2)}) copy-start(f32[1,128,1280]{1,2,0:T(8,128)} %get-tuple-element.218) | copy-start | bytes 1966084
  15.1 5.2 %collective-permute-start.3 = (f32[1,17,40]{2,1,0:T(8,128)S(1)}, f32[1,17,40]{2,1,0:T(8,128)S(1)}, u32[]{:S(2)}, u32[]{:S(2)}) collective-permute-start(f32[1,17,40]{2,1,0:T(8,128)S(1)} %fusion.95), channel_id=1, source_target_pairs={{0,2},{1,3},{2,0},{3,1},{4,6},{5,7},{6,4},{7,5},{8,10},{9,11},{10,... | collective-permute-start | bytes 8168 | tf_op jit(solution)/shard_map/vmap()/ppermute | solution.py:69
  17.8 15.2 %collective-permute-start.2 = (f32[1,128,1280]{1,2,0:T(8,128)}, f32[1,128,1280]{1,2,0:T(8,128)S(1)}, u32[]{:S(2)}, u32[]{:S(2)}) collective-permute-start(f32[1,128,1280]{1,2,0:T(8,128)} %get-tuple-element.218), channel_id=1, source_target_pairs={{0,2},{4,6},{8,10},{12,14},{3,1},{7,5},{11,9},{15,13},{16,18},{20,... | collective-permute-start | bytes 1966088 | tf_op jit(solution)/shard_map/vmap()/ppermute | solution.py:113
  19.1 17.7 %collective-permute-start.10 = (f32[1,128,1280]{1,2,0:T(8,128)}, f32[1,128,1280]{1,2,0:T(8,128)S(1)}, u32[]{:S(2)}, u32[]{:S(2)}) collective-permute-start(f32[1,128,1280]{1,2,0:T(8,128)} %get-tuple-element.222), channel_id=1, source_target_pairs={{15,13},{11,9},{7,5},{3,1},{12,14},{8,10},{4,6},{0,2},{31,29},{27,... | collective-permute-start | bytes 1966088 | tf_op jit(solution)/shard_map/vmap()/ppermute | solution.py:113
  20.4 2.6 %collective-permute-start.4 = (f32[1,17,40]{2,1,0:T(8,128)S(1)}, f32[1,17,40]{2,1,0:T(8,128)S(1)}, u32[]{:S(2)}, u32[]{:S(2)}) collective-permute-start(f32[1,17,40]{2,1,0:T(8,128)S(1)} %add.265), channel_id=1, source_target_pairs={{0,4},{1,5},{2,6},{3,7},{4,0},{5,1},{6,2},{7,3},{8,12},{9,13},{10,... | collective-permute-start | bytes 8168 | tf_op jit(solution)/shard_map/vmap()/ppermute | solution.py:69
  22.8 14.0 %copy-start.4 = (f32[1,128,1280]{1,2,0:T(8,128)S(1)}, f32[1,128,1280]{1,2,0:T(8,128)}, u32[]{:S(2)}) copy-start(f32[1,128,1280]{1,2,0:T(8,128)} %get-tuple-element.222) | copy-start | bytes 1966084
  23.0 3.4 %collective-permute-start.5 = (f32[1,17,40]{2,1,0:T(8,128)S(1)}, f32[1,17,40]{2,1,0:T(8,128)S(1)}, u32[]{:S(2)}, u32[]{:S(2)}) collective-permute-start(f32[1,17,40]{2,1,0:T(8,128)S(1)} %add.268), channel_id=1, source_target_pairs={{0,8},{1,9},{2,10},{3,11},{4,12},{5,13},{6,14},{7,15},{8,0},{9,1},... | collective-permute-start | bytes 8168 | tf_op jit(solution)/shard_map/vmap()/ppermute | solution.py:69
  33.5 10.8 %collective-permute-start.6 = (f32[1,128,1280]{1,2,0:T(8,128)S(1)}, f32[1,128,1280]{1,2,0:T(8,128)S(1)}, u32[]{:S(2)}, u32[]{:S(2)}) collective-permute-start(f32[1,128,1280]{1,2,0:T(8,128)S(1)} %add_select_fusion.3), channel_id=1, source_target_pairs={{2,6},{10,14},{1,5},{9,13},{18,22},{26,30},{17,21},{25,29}} | collective-permute-start | bytes 1966088 | tf_op jit(solution)/shard_map/vmap()/ppermute | solution.py:113
  36.8 7.7 %copy-start.11 = (f32[1,128,1280]{1,2,0:T(8,128)}, f32[1,128,1280]{1,2,0:T(8,128)S(1)}, u32[]{:S(2)}) copy-start(f32[1,128,1280]{1,2,0:T(8,128)S(1)} %collective-permute-done.10) | copy-start | bytes 1966084
  37.3 11.3 %collective-permute-start.11 = (f32[1,128,1280]{1,2,0:T(8,128)S(1)}, f32[1,128,1280]{1,2,0:T(8,128)S(1)}, u32[]{:S(2)}, u32[]{:S(2)}) collective-permute-start(f32[1,128,1280]{1,2,0:T(8,128)S(1)} %add_select_fusion.1), channel_id=1, source_target_pairs={{13,9},{5,1},{14,10},{6,2},{29,25},{21,17},{30,26},{22,18}} | collective-permute-start | bytes 1966088 | tf_op jit(solution)/shard_map/vmap()/ppermute | solution.py:113
  38.6 11.6 %collective-permute-start.16 = (f32[40]{0:T(128)S(1)}, f32[40]{0:T(128)S(1)}, u32[]{:S(2)}, u32[]{:S(2)}) collective-permute-start(f32[40]{0:T(128)S(1)} %slice_bitcast_fusion.5), channel_id=1, source_target_pairs={{0,16},{16,0},{1,17},{17,1},{2,18},{18,2},{3,19},{19,3},{4,20},{20... | collective-permute-start | bytes 488 | tf_op jit(solution)/shard_map/ppermute | solution.py:279
  44.5 6.1 %collective-permute-start.7 = (f32[1,128,1280]{1,2,0:T(8,128)S(1)}, f32[1,128,1280]{1,2,0:T(8,128)S(1)}, u32[]{:S(2)}, u32[]{:S(2)}) collective-permute-start(f32[1,128,1280]{1,2,0:T(8,128)S(1)} %multiply_add_fusion.5), channel_id=1, source_target_pairs={{6,14},{5,13},{22,30},{21,29}} | collective-permute-start | bytes 1966088 | tf_op jit(solution)/shard_map/vmap()/ppermute | solution.py:113
  48.8 12.2 %collective-permute-start.12 = (f32[1,128,1280]{1,2,0:T(8,128)S(1)}, f32[1,128,1280]{1,2,0:T(8,128)S(1)}, u32[]{:S(2)}, u32[]{:S(2)}) collective-permute-start(f32[1,128,1280]{1,2,0:T(8,128)S(1)} %multiply_add_fusion.2), channel_id=1, source_target_pairs={{9,1},{10,2},{25,17},{26,18}} | collective-permute-start | bytes 1966088 | tf_op jit(solution)/shard_map/vmap()/ppermute | solution.py:113
  51.8 17.0 %collective-permute-start.8 = (f32[1,128,1280]{1,2,0:T(8,128)}, f32[1,128,1280]{1,2,0:T(8,128)}, u32[]{:S(2)}, u32[]{:S(2)}) collective-permute-start(f32[1,128,1280]{1,2,0:T(8,128)} %broadcast_add_fusion.1), channel_id=1, source_target_pairs={{6,2},{14,10},{5,1},{13,9},{22,18},{30,26},{21,17},{29,25}} | collective-permute-start | bytes 1966088 | tf_op jit(solution)/shard_map/vmap()/ppermute | solution.py:113
  62.2 11.8 %collective-permute-start.13 = (f32[1,128,1280]{1,2,0:T(8,128)}, f32[1,128,1280]{1,2,0:T(8,128)}, u32[]{:S(2)}, u32[]{:S(2)}) collective-permute-start(f32[1,128,1280]{1,2,0:T(8,128)} %broadcast_add_fusion), channel_id=1, source_target_pairs={{9,13},{1,5},{10,14},{2,6},{25,29},{17,21},{26,30},{18,22}} | collective-permute-start | bytes 1966088 | tf_op jit(solution)/shard_map/vmap()/ppermute | solution.py:113
  68.5 5.5 %copy-start.16 = (f32[1,128,1280]{1,2,0:T(8,128)S(1)}, f32[1,128,1280]{1,2,0:T(8,128)}, u32[]{:S(2)}) copy-start(f32[1,128,1280]{1,2,0:T(8,128)} %copy-done.15) | copy-start | bytes 1966084
  68.5 5.5 %copy-start.26 = (f32[1280]{0:T(1024)S(1)}, f32[1280]{0:T(1024)}, u32[]{:S(2)}) copy-start(f32[1280]{0:T(1024)} %select_n.547) | copy-start | bytes 15364
  71.7 7.3 %copy-start.20 = (f32[1,128,2560]{1,2,0:T(8,128)S(1)}, f32[1,128,2560]{1,2,0:T(8,128)}, u32[]{:S(2)}) copy-start(f32[1,128,2560]{1,2,0:T(8,128)} %copy.51) | copy-start | bytes 3932164
  71.7 7.3 %copy-start.21 = (bf16[1,128,2560]{1,2,0:T(8,128)(2,1)S(1)}, bf16[1,128,2560]{1,2,0:T(8,128)(2,1)}, u32[]{:S(2)}) copy-start(bf16[1,128,2560]{1,2,0:T(8,128)(2,1)} %copy.48) | copy-start | bytes 1966084
  71.7 7.3 %copy-start.27 = (f32[40,128]{1,0:T(8,128)S(1)}, f32[40,128]{1,0:T(8,128)}, u32[]{:S(2)}) copy-start(f32[40,128]{1,0:T(8,128)} %copy.49) | copy-start | bytes 61444
  71.7 7.3 %copy-start.28 = (pred[128,128]{1,0:T(8,128)(4,1)S(1)}, pred[128,128]{1,0:T(8,128)(4,1)}, u32[]{:S(2)}) copy-start(pred[128,128]{1,0:T(8,128)(4,1)} %iota_compare_fusion) | copy-start | bytes 49156
  71.7 7.3 %copy-start.29 = (f32[40]{0:T(128)S(1)}, f32[40]{0:T(128)}, u32[]{:S(2)}) copy-start(f32[40]{0:T(128)} %param.11) | copy-start | bytes 484
  71.7 10.6 %collective-permute-start.9 = (f32[1,128,1280]{1,2,0:T(8,128)}, f32[1,128,1280]{1,2,0:T(8,128)}, u32[]{:S(2)}, u32[]{:S(2)}) collective-permute-start(f32[1,128,1280]{1,2,0:T(8,128)} %get-tuple-element.212), channel_id=1, source_target_pairs={{2,0},{6,4},{10,8},{14,12},{1,3},{5,7},{9,11},{13,15},{18,16},{22,... | collective-permute-start | bytes 1966088 | tf_op jit(solution)/shard_map/vmap()/ppermute | solution.py:113
  76.8 11.2 %collective-permute-start.14 = (f32[1,128,1280]{1,2,0:T(8,128)}, f32[1,128,1280]{1,2,0:T(8,128)}, u32[]{:S(2)}, u32[]{:S(2)}) collective-permute-start(f32[1,128,1280]{1,2,0:T(8,128)} %get-tuple-element.216), channel_id=1, source_target_pairs={{13,15},{9,11},{5,7},{1,3},{14,12},{10,8},{6,4},{2,0},{29,31},{25,... | collective-permute-start | bytes 1966088 | tf_op jit(solution)/shard_map/vmap()/ppermute | solution.py:113
  82.7 5.3 %copy-start.3 = (f32[1,128,1280]{1,2,0:T(8,128)S(1)}, f32[1,128,1280]{1,2,0:T(8,128)}, u32[]{:S(2)}) copy-start(f32[1,128,1280]{1,2,0:T(8,128)} %get-tuple-element.223) | copy-start | bytes 1966084
  82.7 5.3 %copy-start.12 = (f32[1,128,1280]{1,2,0:T(8,128)S(1)}, f32[1,128,1280]{1,2,0:T(8,128)}, u32[]{:S(2)}) copy-start(f32[1,128,1280]{1,2,0:T(8,128)} %copy-done.11) | copy-start | bytes 1966084
  82.7 5.3 %copy-start.18 = (f32[1,128,1280]{1,2,0:T(8,128)S(1)}, f32[1,128,1280]{1,2,0:T(8,128)}, u32[]{:S(2)}) copy-start(f32[1,128,1280]{1,2,0:T(8,128)} %get-tuple-element.217) | copy-start | bytes 1966084
  89.5 7.8 %copy-start.22 = (bf16[1,128,2560]{1,2,0:T(8,128)(2,1)S(1)}, bf16[1,128,2560]{1,2,0:T(8,128)(2,1)}, u32[]{:S(2)}) copy-start(bf16[1,128,2560]{1,2,0:T(8,128)(2,1)} %copy.48) | copy-start | bytes 1966084
  89.5 7.8 %copy-start.23 = (bf16[1,128,2560]{1,2,0:T(8,128)(2,1)S(1)}, bf16[1,128,2560]{1,2,0:T(8,128)(2,1)}, u32[]{:S(2)}) copy-start(bf16[1,128,2560]{1,2,0:T(8,128)(2,1)} %copy.52) | copy-start | bytes 1966084
  89.7 10.9 %collective-permute-start.15 = (f32[1,128,2560]{1,2,0:T(8,128)S(1)}, f32[1,128,2560]{1,2,0:T(8,128)S(1)}, u32[]{:S(2)}, u32[]{:S(2)}) collective-permute-start(f32[1,128,2560]{1,2,0:T(8,128)S(1)} %pad_maximum_fusion.1), channel_id=1, source_target_pairs={{0,1},{1,0},{2,3},{3,2},{4,5},{5,4},{6,7},{7,6},{8,9},{9,8},{10,11... | collective-permute-start | bytes 3932168 | tf_op jit(solution)/shard_map/vmap()/ppermute | solution.py:227
  (15 other events, 35.6 us)

commit v12 on v11

--- a/solution.py
+++ b/solution.py
@@ -110,7 +110,9 @@
 
 
 def exchange(payloads, pair_lists):
-    return [lax.ppermute(p, "ctx", pairs) for p, pairs in zip(payloads, pair_lists)]
+    return [
+        lax.ppermute(p, "ctx", pairs) if pairs else jnp.zeros_like(p) for p, pairs in zip(payloads, pair_lists)
+    ]
 
 
 class PairScan:
@@ -155,10 +157,10 @@
         if self.flip and level == 0:
             pair = self.way.pair
             sent = jnp.where(self.way.upper, self.pair_gain(0, pair, 1) * prefix + pair_total, prefix)
-            pairs = [(2 * (a + 1), 2 * a) for a in range(0, self.pair_count, 2)]
+            pairs = [(2 * (a + 1), 2 * a) for a in range(2, self.pair_count, 2)]
             pairs += [(2 * a + 1, 2 * (a + 1) + 1) for a in range(0, self.pair_count, 2)]
             return sent, self.way.actual(pairs)
-        pairs = [(a, a - span) for a in range(self.pair_count) if a % (2 * span) == 2 * span - 1]
+        pairs = [(a, a - span) for a in range(2 * span, self.pair_count) if a % (2 * span) == 2 * span - 1]
         return prefix, self.device_pairs(pairs, False)
 
     def down_combine(self, level, prefix, got, lowers):

time: 106 us -> 105 us (level)
  the two profiles are of different devices: /device:TPU:1 before, /device:TPU:18 now
where the time goes in v12:
time: 105 us
  waiting for transfers between devices  36.1 us (34%)
  other arithmetic  25.6 us (24%)
  starting transfers between devices  17.1 us (16%)
  local copies, waits for them, and re-layouts  16.2 us (15%)
  matrix products  7.63 us (7%)
  between operations  2.18 us (2%)
    ppermute x10, waiting for transfers between devices, exchange(): lax.ppermute(p, 'ctx', pairs)  30 us
    ppermute x10, starting transfers between devices, exchange(): lax.ppermute(p, 'ctx', pairs)  12.5 us
    select_n x2, other arithmetic, down_send(): jnp.where(self.way.upper, self.pair_gain(0, pair, 1) * prefix + pair_tota...  5.81 us
    unnamed x63, local copies, waits for them, and re-layouts  5.4 us
    ppermute x4, waiting for transfers between devices, extend_totals(): lax.ppermute(tables[-1], 'ctx', xor_pairs(count, bit))  4.94 us
    ppermute x4, starting transfers between devices, extend_totals(): lax.ppermute(tables[-1], 'ctx', xor_pairs(count, bit))  3.46 us
    select_n x2, other arithmetic, carried_pair(): lifted_parts.append(jnp.where(way.upper, pair_prefix, lifted))  3.34 us
    add x1, other arithmetic, carried_pair(): totals.append(way.gain(1, 2 * way.pair + 1, 1) * low_block + high_block)  3.25 us
  transfers between devices with their start and end apart: 17, of which 5 were waited for; matrix products, arithmetic and copies ran while one was open for 32% of the time, Pallas kernels for 0%

profile of v12, /device:TPU:18, one launch (start us, length us, event | category | flops | bytes accessed | tf_op | source)
XLA Modules:
  0.0 104.8 jit_solution(15340464115263147226)
XLA Ops:
  0.7 0.8 negate_multiply_fusion
  1.8 1.4 %copy.45 = bf16[1,128,2560]{1,2,0:T(8,128)(2,1)S(1)} copy(bf16[1,128,2560]{2,1,0:T(8,128)(2,1)} %param.6) | data formatting | bytes 1310720 | tf_op args[0]
  3.7 1.2 %fusion.1 = (f32[2560]{0:T(1024)S(1)}, bf16[1,128,2560]{1,2,0:T(8,128)(2,1)}, bf16[1,128,2560]{1,2,0:T(8,128)(2,1)S(1)}) fusion(bf16[1,128,2560]{1,2,0:T(8,128)(2,1)S(1)} %copy.46, bf16[1,128,2560]{1,2,0:T(8,128)(2,1)S(1)} %copy.45, f32[128,40]{0,1:T(8,128)S(1)} %get-tuple-element.227, f32[128,40]{0,1:T(8,128)S(1)} %get-tuple-element.228), kind=kLoop, calls=%fused_computation.14 | loop fusion | flops 2618880 | bytes 2672640 | tf_op jit(solution)/shard_map/vmap()/reduce_sum | solution.py:25
  6.8 1.2 %pad_maximum_fusion = f32[1,128,2560]{1,2,0:T(8,128)} fusion(f32[1,128,1280]{1,2,0:T(8,128)S(1)} %get-tuple-element.255, f32[1,128,1280]{1,2,0:T(8,128)S(1)} %get-tuple-element.256), kind=kLoop, calls=%fused_computation.19 | loop fusion | flops 327680 | bytes 2621440 | tf_op jit(solution)/shard_map/vmap()/concatenate | solution.py:208
  11.9 3.2 %select_add_fusion.1 = (f32[1,128,1280]{1,2,0:T(8,128)}, f32[1,128,1280]{1,2,0:T(8,128)}, f32[1,128,1280]{1,2,0:T(8,128)}, f32[1,128,1280]{1,2,0:T(8,128)}) fusion(f32[1,128,2560]{1,2,0:T(8,128)} %collective-permute-done.1, f32[1280]{0:T(1024)S(1)} %broadcast_in_dim.215, pred[]{:T(512)S(6)} %eq.43, f32[1,128,2560]{1,2,0:T(8,128)S(1)} %convolution_bitcast_fusion.1, ...), kind=kLoop, calls=%fused_computation.55 | loop fusion | flops 1638400 | bytes 6563842 | tf_op jit(solution)/shard_map/vmap()/add | solution.py:219
  15.2 1.5 %collective-permute-start.3 = (f32[1,17,40]{2,1,0:T(8,128)S(1)}, f32[1,17,40]{2,1,0:T(8,128)S(1)}, u32[]{:S(2)}, u32[]{:S(2)}) collective-permute-start(f32[1,17,40]{2,1,0:T(8,128)S(1)} %fusion.95), channel_id=1, source_target_pairs={{0,2},{1,3},{2,0},{3,1},{4,6},{5,7},{6,4},{7,5},{8,10},{9,11},{10,... | collective-permute-start | bytes 8168 | tf_op jit(solution)/shard_map/vmap()/ppermute | solution.py:69
  17.0 2.4 %collective-permute-start.2 = (f32[1,128,1280]{1,2,0:T(8,128)}, f32[1,128,1280]{1,2,0:T(8,128)S(1)}, u32[]{:S(2)}, u32[]{:S(2)}) collective-permute-start(f32[1,128,1280]{1,2,0:T(8,128)} %get-tuple-element.218), channel_id=1, source_target_pairs={{0,2},{4,6},{8,10},{12,14},{3,1},{7,5},{11,9},{15,13},{16,18},{20,... | collective-permute-start | bytes 1966088 | tf_op jit(solution)/shard_map/vmap()/ppermute | solution.py:114
  19.5 1.3 %collective-permute-start.10 = (f32[1,128,1280]{1,2,0:T(8,128)}, f32[1,128,1280]{1,2,0:T(8,128)S(1)}, u32[]{:S(2)}, u32[]{:S(2)}) collective-permute-start(f32[1,128,1280]{1,2,0:T(8,128)} %get-tuple-element.222), channel_id=1, source_target_pairs={{15,13},{11,9},{7,5},{3,1},{12,14},{8,10},{4,6},{0,2},{31,29},{27,... | collective-permute-start | bytes 1966088 | tf_op jit(solution)/shard_map/vmap()/ppermute | solution.py:114
  20.8 1.6 %collective-permute-start.4 = (f32[1,17,40]{2,1,0:T(8,128)S(1)}, f32[1,17,40]{2,1,0:T(8,128)S(1)}, u32[]{:S(2)}, u32[]{:S(2)}) collective-permute-start(f32[1,17,40]{2,1,0:T(8,128)S(1)} %add.265), channel_id=1, source_target_pairs={{0,4},{1,5},{2,6},{3,7},{4,0},{5,1},{6,2},{7,3},{8,12},{9,13},{10,... | collective-permute-start | bytes 8168 | tf_op jit(solution)/shard_map/vmap()/ppermute | solution.py:69
  23.5 1.2 %collective-permute-done.4 = f32[1,17,40]{2,1,0:T(8,128)S(1)} collective-permute-done((f32[1,17,40]{2,1,0:T(8,128)S(1)}, f32[1,17,40]{2,1,0:T(8,128)S(1)}, u32[]{:S(2)}, u32[]{:S(2)}) %collective-permute-start.4) | collective-permute-done | bytes 2752 | tf_op jit(solution)/shard_map/vmap()/ppermute | solution.py:69
  25.6 3.8 %collective-permute-done.5 = f32[1,17,40]{2,1,0:T(8,128)S(1)} collective-permute-done((f32[1,17,40]{2,1,0:T(8,128)S(1)}, f32[1,17,40]{2,1,0:T(8,128)S(1)}, u32[]{:S(2)}, u32[]{:S(2)}) %collective-permute-start.5) | collective-permute-done | bytes 2752 | tf_op jit(solution)/shard_map/vmap()/ppermute | solution.py:69
  40.7 1.1 %collective-permute-done.16 = f32[40]{0:T(128)S(1)} collective-permute-done((f32[40]{0:T(128)S(1)}, f32[40]{0:T(128)S(1)}, u32[]{:S(2)}, u32[]{:S(2)}) %collective-permute-start.16) | collective-permute-done | bytes 192 | tf_op jit(solution)/shard_map/ppermute | solution.py:281
  42.3 1.1 %broadcast_add_fusion.1 = f32[1,128,1280]{1,2,0:T(8,128)} fusion(f32[1,128,1280]{1,2,0:T(8,128)S(1)} %collective-permute-done.7, f32[1280]{0:T(1024)S(1)} %mul.298), kind=kLoop, calls=%fused_computation.78 | loop fusion | flops 163840 | bytes 1315840 | tf_op jit(solution)/shard_map/vmap()/add | solution.py:177
  43.4 1.5 %collective-permute-start.8 = (f32[1,128,1280]{1,2,0:T(8,128)}, f32[1,128,1280]{1,2,0:T(8,128)}, u32[]{:S(2)}, u32[]{:S(2)}) collective-permute-start(f32[1,128,1280]{1,2,0:T(8,128)} %broadcast_add_fusion.1), channel_id=1, source_target_pairs={{14,10},{13,9},{30,26},{29,25}} | collective-permute-start | bytes 1966088 | tf_op jit(solution)/shard_map/vmap()/ppermute | solution.py:114
  44.9 1.2 %broadcast_add_fusion = f32[1,128,1280]{1,2,0:T(8,128)} fusion(f32[1,128,1280]{1,2,0:T(8,128)S(1)} %collective-permute-done.12, f32[1280]{0:T(1024)S(1)} %mul.320), kind=kLoop, calls=%fused_computation.76 | loop fusion | flops 163840 | bytes 1315840 | tf_op jit(solution)/shard_map/vmap()/add | solution.py:177
  46.1 1.6 %collective-permute-start.13 = (f32[1,128,1280]{1,2,0:T(8,128)}, f32[1,128,1280]{1,2,0:T(8,128)}, u32[]{:S(2)}, u32[]{:S(2)}) collective-permute-start(f32[1,128,1280]{1,2,0:T(8,128)} %broadcast_add_fusion), channel_id=1, source_target_pairs={{1,5},{2,6},{17,21},{18,22}} | collective-permute-start | bytes 1966088 | tf_op jit(solution)/shard_map/vmap()/ppermute | solution.py:114
  47.8 1.1 %copy.48 = bf16[1,128,2560]{1,2,0:T(8,128)(2,1)} copy(bf16[1,128,2560]{2,1,0:T(8,128)(2,1)S(1)} %copy-done.1) | data formatting | bytes 1310720 | tf_op jit(solution)/shard_map/optimization_barrier | solution.py:282
  48.9 1.3 %copy.51 = f32[1,128,2560]{1,2,0:T(8,128)} copy(bf16[1,128,2560]{2,1,0:T(8,128)(2,1)S(1)} %copy-done.1) | data formatting | bytes 1966080 | tf_op jit(solution)/shard_map/vmap()/convert_element_type | solution.py:53
  50.9 3.0 %add_select_fusion.2 = (f32[1,128,1280]{1,2,0:T(8,128)}, f32[1,128,1280]{1,2,0:T(8,128)}) fusion(f32[1,128,1280]{1,2,0:T(8,128)S(1)} %copy-done.5, f32[1280]{0:T(1024)S(1)} %broadcast_in_dim.228, pred[]{:T(512)S(6)} %eq.43, f32[1,128,1280]{1,2,0:T(8,128)} %copy-done.17, f32[1,128,1280]{1,2,0:T(8,128)} %collective-permute-done.8, f32[1280]{0:T(1024)} %select_n.505, ...), kind=kLoop, calls=%fused_computation.50 | loop fusion | flops 1146880 | bytes 3947521 | tf_op jit(solution)/shard_map/vmap(jit(_where))/select_n | solution.py:159
  53.9 1.4 %collective-permute-start.9 = (f32[1,128,1280]{1,2,0:T(8,128)}, f32[1,128,1280]{1,2,0:T(8,128)}, u32[]{:S(2)}, u32[]{:S(2)}) collective-permute-start(f32[1,128,1280]{1,2,0:T(8,128)} %get-tuple-element.212), channel_id=1, source_target_pairs={{6,4},{10,8},{14,12},{1,3},{5,7},{9,11},{13,15},{22,20},{26,24},{3... | collective-permute-start | bytes 1966088 | tf_op jit(solution)/shard_map/vmap()/ppermute | solution.py:114
  55.4 2.8 %add_select_fusion = (f32[1,128,1280]{1,2,0:T(8,128)}, f32[1,128,1280]{1,2,0:T(8,128)}) fusion(f32[1,128,1280]{1,2,0:T(8,128)S(1)} %copy-done.4, f32[1280]{0:T(1024)S(1)} %broadcast_in_dim.248, pred[]{:T(512)S(6)} %eq.46, f32[1,128,1280]{1,2,0:T(8,128)S(1)} %copy-done.16, f32[1,128,1280]{1,2,0:T(8,128)} %collective-permute-done.13, f32[1280]{0:T(1024)S(1)} %copy-done.26, ...), kind=kLoop, calls=%fused_computation.43 | loop fusion | flops 1146880 | bytes 3947521 | tf_op jit(solution)/shard_map/vmap(jit(_where))/select_n | solution.py:159
  58.2 1.5 %collective-permute-start.14 = (f32[1,128,1280]{1,2,0:T(8,128)}, f32[1,128,1280]{1,2,0:T(8,128)}, u32[]{:S(2)}, u32[]{:S(2)}) collective-permute-start(f32[1,128,1280]{1,2,0:T(8,128)} %get-tuple-element.216), channel_id=1, source_target_pairs={{9,11},{5,7},{1,3},{14,12},{10,8},{6,4},{2,0},{25,27},{21,23},{17,... | collective-permute-start | bytes 1966088 | tf_op jit(solution)/shard_map/vmap()/ppermute | solution.py:114
  59.7 2.2 %fusion = f32[1,128,40,64]{1,3,2,0:T(8,128)} fusion(bf16[128,40,64]{0,2,1:T(8,128)(2,1)S(1)} %bitcast.247, f32[1,128,40,64]{1,3,2,0:T(8,128)S(1)} %bitcast.246, f32[40,128]{1,0:T(8,128)S(1)} %copy-done.27, f32[128,128]{1,0:T(8,128)S(1)} %fusion.46, pred[128,128]{1,0:T(8,128)(4,1)S(1)} %copy-done.28, f32[40]{0:T(128)S(1)} %copy-done.29), kind=kOutput, calls=%fused_computation.13 | convolution fusion | flops 87818240 | bytes 3379360 | tf_op jit(solution)/shard_map/vmap(hij,ihp->jhp)/dot_general | solution.py:51
  61.9 1.1 %copy.52 = bf16[1,128,2560]{1,2,0:T(8,128)(2,1)} copy(bf16[1,128,2560]{2,1,0:T(8,128)(2,1)S(1)} %copy-done.8) | data formatting | bytes 1310720 | tf_op jit(solution)/shard_map/optimization_barrier | solution.py:282
  63.0 24.9 %collective-permute-done.9 = f32[1,128,1280]{1,2,0:T(8,128)} collective-permute-done((f32[1,128,1280]{1,2,0:T(8,128)}, f32[1,128,1280]{1,2,0:T(8,128)}, u32[]{:S(2)}, u32[]{:S(2)}) %collective-permute-start.9) | collective-permute-done | bytes 655392 | tf_op jit(solution)/shard_map/vmap()/ppermute | solution.py:114
  87.9 1.8 %fusion.18 = (f32[1,128,1280]{1,2,0:T(8,128)S(1)}, f32[1,128,1280]{1,2,0:T(8,128)S(1)}) fusion(f32[1,128,1280]{1,2,0:T(8,128)S(1)} %copy-done.2, f32[1280]{0:T(1024)S(1)} %broadcast_in_dim.245, pred[]{:T(512)S(6)} %eq.43, f32[1,128,1280]{1,2,0:T(8,128)} %collective-permute-done.9, f32[1,128,1280]{1,2,0:T(8,128)S(1)} %copy-done.14, ...), kind=kLoop, calls=%fused_computation.48 | loop fusion | flops 1310720 | bytes 3942402 | tf_op jit(solution)/shard_map/vmap(jit(_where))/select_n | solution.py:227
  89.8 5.1 %collective-permute-done.14 = f32[1,128,1280]{1,2,0:T(8,128)} collective-permute-done((f32[1,128,1280]{1,2,0:T(8,128)}, f32[1,128,1280]{1,2,0:T(8,128)}, u32[]{:S(2)}, u32[]{:S(2)}) %collective-permute-start.14) | collective-permute-done | bytes 655392 | tf_op jit(solution)/shard_map/vmap()/ppermute | solution.py:114
  94.9 1.5 %fusion.17 = (f32[1,128,1280]{1,2,0:T(8,128)S(1)}, f32[1,128,1280]{1,2,0:T(8,128)S(1)}) fusion(f32[1,128,1280]{1,2,0:T(8,128)S(1)} %copy-done.3, f32[1280]{0:T(1024)S(1)} %broadcast_in_dim.264, pred[]{:T(512)S(6)} %eq.46, f32[1,128,1280]{1,2,0:T(8,128)} %collective-permute-done.14, f32[1,128,1280]{1,2,0:T(8,128)S(1)} %copy-done.12, ...), kind=kLoop, calls=%fused_computation.41 | loop fusion | flops 1310720 | bytes 3942402 | tf_op jit(solution)/shard_map/vmap(jit(_where))/select_n | solution.py:227
  96.6 0.9 copy-done.22
  97.7 1.3 %convert_reduce_fusion = bf16[128,128]{1,0:T(8,128)(2,1)S(1)} fusion(f32[40,128]{1,0:T(8,128)S(1)} %copy-done.27, pred[128,128]{1,0:T(8,128)(4,1)S(1)} %copy-done.28, bf16[128,40,64]{0,2,1:T(8,128)(2,1)S(1)} %bitcast.248, bf16[128,40,64]{0,2,1:T(8,128)(2,1)S(1)} %bitcast.249), kind=kOutput, calls=%fused_computation.2 | convolution fusion | flops 88457216 | bytes 1380352 | tf_op jit(solution)/shard_map/vmap(ihp,jhp->hij)/dot_general | solution.py:45
  102.6 0.8 fusion.14
  103.7 1.1 %copy.53 = bf16[1,128,2560]{2,1,0:T(8,128)(2,1)} copy(bf16[1,128,2560]{1,2,0:T(8,128)(2,1)S(1)} %fusion.5) | data formatting | bytes 1310720
  (215 shorter events, 24.7 us)
Async XLA Ops:
  0.6 5.1 %copy-start = (bf16[1,128,128]{2,1,0:T(8,128)(2,1)S(1)}, bf16[1,128,128]{2,1,0:T(8,128)(2,1)}, u32[]{:S(2)}) copy-start(bf16[1,128,128]{2,1,0:T(8,128)(2,1)} %param.8) | copy-start | bytes 98308
  5.1 6.1 %collective-permute-start = (f32[1,17,40]{2,1,0:T(8,128)S(1)}, f32[1,17,40]{2,1,0:T(8,128)S(1)}, u32[]{:S(2)}, u32[]{:S(2)}) collective-permute-start(f32[1,17,40]{2,1,0:T(8,128)S(1)} %pad_maximum_fusion.2), channel_id=1, source_target_pairs={{0,1},{1,0},{2,3},{3,2},{4,5},{5,4},{6,7},{7,6},{8,9},{9,8},{10,11... | collective-permute-start | bytes 8168 | tf_op jit(solution)/shard_map/vmap()/ppermute | solution.py:69
  8.0 3.9 %collective-permute-start.1 = (f32[1,128,2560]{1,2,0:T(8,128)}, f32[1,128,2560]{1,2,0:T(8,128)}, u32[]{:S(2)}, u32[]{:S(2)}) collective-permute-start(f32[1,128,2560]{1,2,0:T(8,128)} %pad_maximum_fusion), channel_id=1, source_target_pairs={{0,1},{1,0},{2,3},{3,2},{4,5},{5,4},{6,7},{7,6},{8,9},{9,8},{10,11... | collective-permute-start | bytes 3932168 | tf_op jit(solution)/shard_map/vmap()/ppermute | solution.py:209
  15.2 20.7 %copy-start.5 = (f32[1,128,1280]{1,2,0:T(8,128)S(1)}, f32[1,128,1280]{1,2,0:T(8,128)}, u32[]{:S(2)}) copy-start(f32[1,128,1280]{1,2,0:T(8,128)} %get-tuple-element.218) | copy-start | bytes 1966084
  15.2 5.7 %collective-permute-start.3 = (f32[1,17,40]{2,1,0:T(8,128)S(1)}, f32[1,17,40]{2,1,0:T(8,128)S(1)}, u32[]{:S(2)}, u32[]{:S(2)}) collective-permute-start(f32[1,17,40]{2,1,0:T(8,128)S(1)} %fusion.95), channel_id=1, source_target_pairs={{0,2},{1,3},{2,0},{3,1},{4,6},{5,7},{6,4},{7,5},{8,10},{9,11},{10,... | collective-permute-start | bytes 8168 | tf_op jit(solution)/shard_map/vmap()/ppermute | solution.py:69
  17.0 18.8 %collective-permute-start.2 = (f32[1,128,1280]{1,2,0:T(8,128)}, f32[1,128,1280]{1,2,0:T(8,128)S(1)}, u32[]{:S(2)}, u32[]{:S(2)}) collective-permute-start(f32[1,128,1280]{1,2,0:T(8,128)} %get-tuple-element.218), channel_id=1, source_target_pairs={{0,2},{4,6},{8,10},{12,14},{3,1},{7,5},{11,9},{15,13},{16,18},{20,... | collective-permute-start | bytes 1966088 | tf_op jit(solution)/shard_map/vmap()/ppermute | solution.py:114
  19.5 17.5 %collective-permute-start.10 = (f32[1,128,1280]{1,2,0:T(8,128)}, f32[1,128,1280]{1,2,0:T(8,128)S(1)}, u32[]{:S(2)}, u32[]{:S(2)}) collective-permute-start(f32[1,128,1280]{1,2,0:T(8,128)} %get-tuple-element.222), channel_id=1, source_target_pairs={{15,13},{11,9},{7,5},{3,1},{12,14},{8,10},{4,6},{0,2},{31,29},{27,... | collective-permute-start | bytes 1966088 | tf_op jit(solution)/shard_map/vmap()/ppermute | solution.py:114
  20.8 3.9 %collective-permute-start.4 = (f32[1,17,40]{2,1,0:T(8,128)S(1)}, f32[1,17,40]{2,1,0:T(8,128)S(1)}, u32[]{:S(2)}, u32[]{:S(2)}) collective-permute-start(f32[1,17,40]{2,1,0:T(8,128)S(1)} %add.265), channel_id=1, source_target_pairs={{0,4},{1,5},{2,6},{3,7},{4,0},{5,1},{6,2},{7,3},{8,12},{9,13},{10,... | collective-permute-start | bytes 8168 | tf_op jit(solution)/shard_map/vmap()/ppermute | solution.py:69
  23.5 13.5 %copy-start.4 = (f32[1,128,1280]{1,2,0:T(8,128)S(1)}, f32[1,128,1280]{1,2,0:T(8,128)}, u32[]{:S(2)}) copy-start(f32[1,128,1280]{1,2,0:T(8,128)} %get-tuple-element.222) | copy-start | bytes 1966084
  24.7 4.6 %collective-permute-start.5 = (f32[1,17,40]{2,1,0:T(8,128)S(1)}, f32[1,17,40]{2,1,0:T(8,128)S(1)}, u32[]{:S(2)}, u32[]{:S(2)}) collective-permute-start(f32[1,17,40]{2,1,0:T(8,128)S(1)} %add.268), channel_id=1, source_target_pairs={{0,8},{1,9},{2,10},{3,11},{4,12},{5,13},{6,14},{7,15},{8,0},{9,1},... | collective-permute-start | bytes 8168 | tf_op jit(solution)/shard_map/vmap()/ppermute | solution.py:69
  36.3 2.5 %collective-permute-start.6 = (f32[1,128,1280]{1,2,0:T(8,128)S(1)}, f32[1,128,1280]{1,2,0:T(8,128)S(1)}, u32[]{:S(2)}, u32[]{:S(2)}) collective-permute-start(f32[1,128,1280]{1,2,0:T(8,128)S(1)} %add_select_fusion.3), channel_id=1, source_target_pairs={{2,6},{10,14},{1,5},{9,13},{18,22},{26,30},{17,21},{25,29}} | collective-permute-start | bytes 1966088 | tf_op jit(solution)/shard_map/vmap()/ppermute | solution.py:114
  37.5 2.3 %collective-permute-start.11 = (f32[1,128,1280]{1,2,0:T(8,128)S(1)}, f32[1,128,1280]{1,2,0:T(8,128)S(1)}, u32[]{:S(2)}, u32[]{:S(2)}) collective-permute-start(f32[1,128,1280]{1,2,0:T(8,128)S(1)} %add_select_fusion.1), channel_id=1, source_target_pairs={{13,9},{5,1},{14,10},{6,2},{29,25},{21,17},{30,26},{22,18}} | collective-permute-start | bytes 1966088 | tf_op jit(solution)/shard_map/vmap()/ppermute | solution.py:114
  38.2 3.6 %collective-permute-start.16 = (f32[40]{0:T(128)S(1)}, f32[40]{0:T(128)S(1)}, u32[]{:S(2)}, u32[]{:S(2)}) collective-permute-start(f32[40]{0:T(128)S(1)} %slice_bitcast_fusion.5), channel_id=1, source_target_pairs={{0,16},{16,0},{1,17},{17,1},{2,18},{18,2},{3,19},{19,3},{4,20},{20... | collective-permute-start | bytes 488 | tf_op jit(solution)/shard_map/ppermute | solution.py:281
  39.0 3.3 %collective-permute-start.7 = (f32[1,128,1280]{1,2,0:T(8,128)S(1)}, f32[1,128,1280]{1,2,0:T(8,128)S(1)}, u32[]{:S(2)}, u32[]{:S(2)}) collective-permute-start(f32[1,128,1280]{1,2,0:T(8,128)S(1)} %multiply_add_fusion.5), channel_id=1, source_target_pairs={{6,14},{5,13},{22,30},{21,29}} | collective-permute-start | bytes 1966088 | tf_op jit(solution)/shard_map/vmap()/ppermute | solution.py:114
  40.0 4.9 %collective-permute-start.12 = (f32[1,128,1280]{1,2,0:T(8,128)S(1)}, f32[1,128,1280]{1,2,0:T(8,128)S(1)}, u32[]{:S(2)}, u32[]{:S(2)}) collective-permute-start(f32[1,128,1280]{1,2,0:T(8,128)S(1)} %multiply_add_fusion.2), channel_id=1, source_target_pairs={{9,1},{10,2},{25,17},{26,18}} | collective-permute-start | bytes 1966088 | tf_op jit(solution)/shard_map/vmap()/ppermute | solution.py:114
  43.4 7.5 %collective-permute-start.8 = (f32[1,128,1280]{1,2,0:T(8,128)}, f32[1,128,1280]{1,2,0:T(8,128)}, u32[]{:S(2)}, u32[]{:S(2)}) collective-permute-start(f32[1,128,1280]{1,2,0:T(8,128)} %broadcast_add_fusion.1), channel_id=1, source_target_pairs={{14,10},{13,9},{30,26},{29,25}} | collective-permute-start | bytes 1966088 | tf_op jit(solution)/shard_map/vmap()/ppermute | solution.py:114
  46.1 9.3 %collective-permute-start.13 = (f32[1,128,1280]{1,2,0:T(8,128)}, f32[1,128,1280]{1,2,0:T(8,128)}, u32[]{:S(2)}, u32[]{:S(2)}) collective-permute-start(f32[1,128,1280]{1,2,0:T(8,128)} %broadcast_add_fusion), channel_id=1, source_target_pairs={{1,5},{2,6},{17,21},{18,22}} | collective-permute-start | bytes 1966088 | tf_op jit(solution)/shard_map/vmap()/ppermute | solution.py:114
  50.9 4.5 %copy-start.26 = (f32[1280]{0:T(1024)S(1)}, f32[1280]{0:T(1024)}, u32[]{:S(2)}) copy-start(f32[1280]{0:T(1024)} %select_n.547) | copy-start | bytes 15364
  53.9 5.7 %copy-start.20 = (f32[1,128,2560]{1,2,0:T(8,128)S(1)}, f32[1,128,2560]{1,2,0:T(8,128)}, u32[]{:S(2)}) copy-start(f32[1,128,2560]{1,2,0:T(8,128)} %copy.51) | copy-start | bytes 3932164
  53.9 5.8 %copy-start.21 = (bf16[1,128,2560]{1,2,0:T(8,128)(2,1)S(1)}, bf16[1,128,2560]{1,2,0:T(8,128)(2,1)}, u32[]{:S(2)}) copy-start(bf16[1,128,2560]{1,2,0:T(8,128)(2,1)} %copy.48) | copy-start | bytes 1966084
  53.9 5.8 %copy-start.27 = (f32[40,128]{1,0:T(8,128)S(1)}, f32[40,128]{1,0:T(8,128)}, u32[]{:S(2)}) copy-start(f32[40,128]{1,0:T(8,128)} %copy.49) | copy-start | bytes 61444
  53.9 5.8 %copy-start.28 = (pred[128,128]{1,0:T(8,128)(4,1)S(1)}, pred[128,128]{1,0:T(8,128)(4,1)}, u32[]{:S(2)}) copy-start(pred[128,128]{1,0:T(8,128)(4,1)} %iota_compare_fusion) | copy-start | bytes 49156
  53.9 5.8 %copy-start.29 = (f32[40]{0:T(128)S(1)}, f32[40]{0:T(128)}, u32[]{:S(2)}) copy-start(f32[40]{0:T(128)} %param.11) | copy-start | bytes 484
  53.9 33.9 %collective-permute-start.9 = (f32[1,128,1280]{1,2,0:T(8,128)}, f32[1,128,1280]{1,2,0:T(8,128)}, u32[]{:S(2)}, u32[]{:S(2)}) collective-permute-start(f32[1,128,1280]{1,2,0:T(8,128)} %get-tuple-element.212), channel_id=1, source_target_pairs={{6,4},{10,8},{14,12},{1,3},{5,7},{9,11},{13,15},{22,20},{26,24},{3... | collective-permute-start | bytes 1966088 | tf_op jit(solution)/shard_map/vmap()/ppermute | solution.py:114
  58.2 36.7 %collective-permute-start.14 = (f32[1,128,1280]{1,2,0:T(8,128)}, f32[1,128,1280]{1,2,0:T(8,128)}, u32[]{:S(2)}, u32[]{:S(2)}) collective-permute-start(f32[1,128,1280]{1,2,0:T(8,128)} %get-tuple-element.216), channel_id=1, source_target_pairs={{9,11},{5,7},{1,3},{14,12},{10,8},{6,4},{2,0},{25,27},{21,23},{17,... | collective-permute-start | bytes 1966088 | tf_op jit(solution)/shard_map/vmap()/ppermute | solution.py:114
  59.7 28.2 %copy-start.25 = (f32[1280]{0:T(1024)S(1)}, f32[1280]{0:T(1024)}, u32[]{:S(2)}) copy-start(f32[1280]{0:T(1024)} %broadcast_in_dim.242) | copy-start | bytes 15364
  61.9 26.0 %copy-start.2 = (f32[1,128,1280]{1,2,0:T(8,128)S(1)}, f32[1,128,1280]{1,2,0:T(8,128)}, u32[]{:S(2)}) copy-start(f32[1,128,1280]{1,2,0:T(8,128)} %get-tuple-element.219) | copy-start | bytes 1966084
  61.9 26.0 %copy-start.14 = (f32[1,128,1280]{1,2,0:T(8,128)S(1)}, f32[1,128,1280]{1,2,0:T(8,128)}, u32[]{:S(2)}) copy-start(f32[1,128,1280]{1,2,0:T(8,128)} %copy-done.13) | copy-start | bytes 1966084
  87.9 7.0 %copy-start.3 = (f32[1,128,1280]{1,2,0:T(8,128)S(1)}, f32[1,128,1280]{1,2,0:T(8,128)}, u32[]{:S(2)}) copy-start(f32[1,128,1280]{1,2,0:T(8,128)} %get-tuple-element.223) | copy-start | bytes 1966084
  87.9 7.0 %copy-start.12 = (f32[1,128,1280]{1,2,0:T(8,128)S(1)}, f32[1,128,1280]{1,2,0:T(8,128)}, u32[]{:S(2)}) copy-start(f32[1,128,1280]{1,2,0:T(8,128)} %copy-done.11) | copy-start | bytes 1966084
  87.9 7.0 %copy-start.18 = (f32[1,128,1280]{1,2,0:T(8,128)S(1)}, f32[1,128,1280]{1,2,0:T(8,128)}, u32[]{:S(2)}) copy-start(f32[1,128,1280]{1,2,0:T(8,128)} %get-tuple-element.217) | copy-start | bytes 1966084
  96.5 4.4 %collective-permute-start.15 = (f32[1,128,2560]{1,2,0:T(8,128)S(1)}, f32[1,128,2560]{1,2,0:T(8,128)S(1)}, u32[]{:S(2)}, u32[]{:S(2)}) collective-permute-start(f32[1,128,2560]{1,2,0:T(8,128)S(1)} %pad_maximum_fusion.1), channel_id=1, source_target_pairs={{0,1},{1,0},{2,3},{3,2},{4,5},{5,4},{6,7},{7,6},{8,9},{9,8},{10,11... | collective-permute-start | bytes 3932168 | tf_op jit(solution)/shard_map/vmap()/ppermute | solution.py:229
  (15 other events, 28.1 us)

commit v13 on v12

--- a/solution.py
+++ b/solution.py
@@ -180,6 +180,8 @@
 def pair_scans(ways, pair_totals):
     scans = [PairScan(way) for way in ways]
     level_count = scans[0].level_count
+    if scans[0].flip:
+        return shift_scans(scans, pair_totals)
     totals = list(pair_totals)
     lowers = [[] for _ in scans]
     for level in range(level_count):
@@ -190,7 +192,7 @@
                 totals[k] = scan.up_combine(level, totals[k], got[k])
     prefixes = [jnp.zeros_like(total) for total in pair_totals]
     for level in reversed(range(level_count)):
-        if level < level_count - 1 or (scans[0].flip and level == 0):
+        if level < level_count - 1:
             sends = [scan.down_send(level, p, t) for scan, p, t in zip(scans, prefixes, pair_totals)]
             got = exchange([s[0] for s in sends], [s[1] for s in sends])
         else:
@@ -200,6 +202,35 @@
         ]
     anchor = lowers[0][0] if level_count else pair_totals[0]
     return prefixes, anchor
+
+
+def shift_scans(scans, pair_totals):
+    group_count = scans[0].pair_count // 2
+    got = exchange(list(pair_totals), [scan.up_send(0) for scan in scans])
+    lowers = [[g] for g in got]
+    through = [scan.up_combine(0, t, g) for scan, t, g in zip(scans, pair_totals, got)]
+    before = [jnp.zeros_like(t) for t in pair_totals]
+
+    def group_gain(scan, group):
+        return scan.way.gain(-1, 4 * group, 4)
+
+    span = 1
+    while span < group_count:
+        pairs = [(2 * g + 1, 2 * (g + span) + 1) for g in range(group_count - span)]
+        got = exchange(through, [scan.device_pairs(pairs, False) for scan in scans])
+        for k, scan in enumerate(scans):
+            group = scan.way.pair // 2
+            before_gain = 1.0
+            for back in range(1, span):
+                before_gain = before_gain * group_gain(scan, group - back)
+            if span < group_count // 2:
+                through[k] = before_gain * group_gain(scan, group) * got[k] + through[k]
+            before[k] = before_gain * got[k] + before[k]
+        span *= 2
+    sends = [scan.down_send(0, p, t) for scan, p, t in zip(scans, before, pair_totals)]
+    got = exchange([s[0] for s in sends], [s[1] for s in sends])
+    prefixes = [scan.down_combine(0, p, g, low) for scan, p, g, low in zip(scans, before, got, lowers)]
+    return prefixes, lowers[0][0]
 
 
 def carried_pair(tables, fwd_state, adj_state, position, count, head_width):

time: 105 us -> 101 us (0.962)
  the two profiles are of different devices: /device:TPU:18 before, /device:TPU:1 now
where the time goes in v13:
time: 101 us; the launch traced here: 99.8 us
  starting transfers between devices  33.2 us (33%)
  other arithmetic  24 us (24%)
  waiting for transfers between devices  18.7 us (19%)
  local copies, waits for them, and re-layouts  14.4 us (14%)
  matrix products  7.66 us (8%)
  between operations  1.91 us (2%)
    ppermute x8, starting transfers between devices, exchange(): lax.ppermute(p, 'ctx', pairs)  17.7 us
    ppermute x8, waiting for transfers between devices, exchange(): lax.ppermute(p, 'ctx', pairs)  16.1 us
    ppermute x1, starting transfers between devices, carried_pair(): lax.ppermute(jnp.concatenate(lifted_parts, -1), 'ctx', [(i, i ^ 1) for i...  7.44 us
    unnamed x53, local copies, waits for them, and re-layouts  6.85 us
    ppermute x4, starting transfers between devices, extend_totals(): lax.ppermute(tables[-1], 'ctx', xor_pairs(count, bit))  6.4 us
    select_n x2, other arithmetic, down_send(): jnp.where(self.way.upper, self.pair_gain(0, pair, 1) * prefix + pair_tota...  4.77 us
    select_n x2, other arithmetic, carried_pair(): lifted_parts.append(jnp.where(way.upper, pair_prefix, lifted))  4.03 us
    add x1, other arithmetic, carried_pair(): totals.append(way.gain(1, 2 * way.pair + 1, 1) * low_block + high_block)  3.23 us
  transfers between devices with their start and end apart: 15, of which 7 were waited for; matrix products, arithmetic and copies ran while one was open for 29% of the time, Pallas kernels for 0%

profile of v13, /device:TPU:1, one launch (start us, length us, event | category | flops | bytes accessed | tf_op | source)
XLA Modules:
  0.0 99.8 jit_solution(16003682926775306639)
XLA Ops:
  1.8 1.4 %copy.45 = bf16[1,128,2560]{1,2,0:T(8,128)(2,1)S(1)} copy(bf16[1,128,2560]{2,1,0:T(8,128)(2,1)} %param.6) | data formatting | bytes 1310720 | tf_op args[0]
  3.7 1.2 %fusion.1 = (f32[2560]{0:T(1024)S(1)}, bf16[1,128,2560]{1,2,0:T(8,128)(2,1)}, bf16[1,128,2560]{1,2,0:T(8,128)(2,1)S(1)}) fusion(bf16[1,128,2560]{1,2,0:T(8,128)(2,1)S(1)} %copy.46, bf16[1,128,2560]{1,2,0:T(8,128)(2,1)S(1)} %copy.45, f32[128,40]{0,1:T(8,128)S(1)} %get-tuple-element.201, f32[128,40]{0,1:T(8,128)S(1)} %get-tuple-element.202), kind=kLoop, calls=%fused_computation.14 | loop fusion | flops 2618880 | bytes 2672640 | tf_op jit(solution)/shard_map/vmap()/reduce_sum | solution.py:25
  6.8 1.1 %pad_maximum_fusion = f32[1,128,2560]{1,2,0:T(8,128)} fusion(f32[1,128,1280]{1,2,0:T(8,128)S(1)} %get-tuple-element.231, f32[1,128,1280]{1,2,0:T(8,128)S(1)} %get-tuple-element.232), kind=kLoop, calls=%fused_computation.19 | loop fusion | flops 327680 | bytes 2621440 | tf_op jit(solution)/shard_map/vmap()/concatenate | solution.py:239
  10.2 1.2 %collective-permute-done.1 = f32[1,128,2560]{1,2,0:T(8,128)} collective-permute-done((f32[1,128,2560]{1,2,0:T(8,128)}, f32[1,128,2560]{1,2,0:T(8,128)}, u32[]{:S(2)}, u32[]{:S(2)}) %collective-permute-start.1) | collective-permute-done | bytes 1310752 | tf_op jit(solution)/shard_map/vmap()/ppermute | solution.py:240
  11.4 3.2 %select_add_fusion.1 = (f32[1,128,1280]{1,2,0:T(8,128)}, f32[1,128,1280]{1,2,0:T(8,128)}, f32[1,128,1280]{1,2,0:T(8,128)}, f32[1,128,1280]{1,2,0:T(8,128)}) fusion(f32[1,128,2560]{1,2,0:T(8,128)} %collective-permute-done.1, f32[1280]{0:T(1024)S(1)} %broadcast_in_dim.199, pred[]{:T(512)S(6)} %eq.27, f32[1,128,2560]{1,2,0:T(8,128)S(1)} %convolution_bitcast_fusion.1, ...), kind=kLoop, calls=%fused_computation.55 | loop fusion | flops 1638400 | bytes 6563842 | tf_op jit(solution)/shard_map/vmap()/add | solution.py:250
  14.6 2.6 %collective-permute-start.3 = (f32[1,17,40]{2,1,0:T(8,128)S(1)}, f32[1,17,40]{2,1,0:T(8,128)S(1)}, u32[]{:S(2)}, u32[]{:S(2)}) collective-permute-start(f32[1,17,40]{2,1,0:T(8,128)S(1)} %fusion.89), channel_id=1, source_target_pairs={{0,2},{1,3},{2,0},{3,1},{4,6},{5,7},{6,4},{7,5},{8,10},{9,11},{10,... | collective-permute-start | bytes 8168 | tf_op jit(solution)/shard_map/vmap()/ppermute | solution.py:69
  17.6 1.3 %collective-permute-start.2 = (f32[1,128,1280]{1,2,0:T(8,128)}, f32[1,128,1280]{1,2,0:T(8,128)S(1)}, u32[]{:S(2)}, u32[]{:S(2)}) collective-permute-start(f32[1,128,1280]{1,2,0:T(8,128)} %get-tuple-element.192), channel_id=1, source_target_pairs={{0,2},{4,6},{8,10},{12,14},{3,1},{7,5},{11,9},{15,13},{16,18},{20,... | collective-permute-start | bytes 1966088 | tf_op jit(solution)/shard_map/vmap()/ppermute | solution.py:114
  18.9 1.3 %collective-permute-start.9 = (f32[1,128,1280]{1,2,0:T(8,128)}, f32[1,128,1280]{1,2,0:T(8,128)S(1)}, u32[]{:S(2)}, u32[]{:S(2)}) collective-permute-start(f32[1,128,1280]{1,2,0:T(8,128)} %get-tuple-element.196), channel_id=1, source_target_pairs={{15,13},{11,9},{7,5},{3,1},{12,14},{8,10},{4,6},{0,2},{31,29},{27,... | collective-permute-start | bytes 1966088 | tf_op jit(solution)/shard_map/vmap()/ppermute | solution.py:114
  20.2 1.4 %collective-permute-start.4 = (f32[1,17,40]{2,1,0:T(8,128)S(1)}, f32[1,17,40]{2,1,0:T(8,128)S(1)}, u32[]{:S(2)}, u32[]{:S(2)}) collective-permute-start(f32[1,17,40]{2,1,0:T(8,128)S(1)} %add.200), channel_id=1, source_target_pairs={{0,4},{1,5},{2,6},{3,7},{4,0},{5,1},{6,2},{7,3},{8,12},{9,13},{10,... | collective-permute-start | bytes 8168 | tf_op jit(solution)/shard_map/vmap()/ppermute | solution.py:69
  22.8 2.3 %collective-permute-start.5 = (f32[1,17,40]{2,1,0:T(8,128)S(1)}, f32[1,17,40]{2,1,0:T(8,128)S(1)}, u32[]{:S(2)}, u32[]{:S(2)}) collective-permute-start(f32[1,17,40]{2,1,0:T(8,128)S(1)} %add.202), channel_id=1, source_target_pairs={{0,8},{1,9},{2,10},{3,11},{4,12},{5,13},{6,14},{7,15},{8,0},{9,1},... | collective-permute-start | bytes 8168 | tf_op jit(solution)/shard_map/vmap()/ppermute | solution.py:69
  29.9 1.3 %collective-permute-start.14 = (f32[40]{0:T(128)S(1)}, f32[40]{0:T(128)S(1)}, u32[]{:S(2)}, u32[]{:S(2)}) collective-permute-start(f32[40]{0:T(128)S(1)} %slice_bitcast_fusion.5), channel_id=1, source_target_pairs={{0,16},{16,0},{1,17},{17,1},{2,18},{18,2},{3,19},{19,3},{4,20},{20... | collective-permute-start | bytes 488 | tf_op jit(solution)/shard_map/ppermute | solution.py:312
  32.0 1.5 %add_select_fusion.3 = f32[1,128,1280]{1,2,0:T(8,128)S(1)} fusion(f32[1,128,1280]{1,2,0:T(8,128)} %get-tuple-element.192, f32[1,128,1280]{1,2,0:T(8,128)S(1)} %collective-permute-done.2, f32[1280]{0:T(1024)S(1)} %broadcast_in_dim.221, f32[1280]{0:T(1024)S(1)} %broadcast_in_dim.212, pred[]{:T(512)S(6)} %eq.27), kind=kLoop, calls=%fused_computation.53 | loop fusion | flops 819200 | bytes 1976321 | tf_op jit(solution)/shard_map/vmap(jit(_where))/select_n | solution.py:152
  33.5 3.2 %collective-permute-start.6 = (f32[1,128,1280]{1,2,0:T(8,128)S(1)}, f32[1,128,1280]{1,2,0:T(8,128)S(1)}, u32[]{:S(2)}, u32[]{:S(2)}) collective-permute-start(f32[1,128,1280]{1,2,0:T(8,128)S(1)} %add_select_fusion.3), channel_id=1, source_target_pairs={{2,6},{6,10},{10,14},{1,5},{5,9},{9,13},{18,22},{22,26},{26,30},{1... | collective-permute-start | bytes 1966088 | tf_op jit(solution)/shard_map/vmap()/ppermute | solution.py:114
  38.0 1.3 %collective-permute-start.10 = (f32[1,128,1280]{1,2,0:T(8,128)S(1)}, f32[1,128,1280]{1,2,0:T(8,128)S(1)}, u32[]{:S(2)}, u32[]{:S(2)}) collective-permute-start(f32[1,128,1280]{1,2,0:T(8,128)S(1)} %add_select_fusion.1), channel_id=1, source_target_pairs={{13,9},{9,5},{5,1},{14,10},{10,6},{6,2},{29,25},{25,21},{21,17},{3... | collective-permute-start | bytes 1966088 | tf_op jit(solution)/shard_map/vmap()/ppermute | solution.py:114
  39.8 4.4 %collective-permute-done.6 = f32[1,128,1280]{1,2,0:T(8,128)S(1)} collective-permute-done((f32[1,128,1280]{1,2,0:T(8,128)S(1)}, f32[1,128,1280]{1,2,0:T(8,128)S(1)}, u32[]{:S(2)}, u32[]{:S(2)}) %collective-permute-start.6) | collective-permute-done | bytes 655392 | tf_op jit(solution)/shard_map/vmap()/ppermute | solution.py:114
  44.2 1.1 %multiply_add_fusion.5 = f32[1,128,1280]{1,2,0:T(8,128)} fusion(f32[1,128,1280]{1,2,0:T(8,128)S(1)} %add_select_fusion.3, f32[1,128,1280]{1,2,0:T(8,128)S(1)} %collective-permute-done.6, f32[1280]{0:T(1024)S(1)} %broadcast_in_dim.218), kind=kLoop, calls=%fused_computation.52 | loop fusion | flops 327680 | bytes 1971200 | tf_op jit(solution)/shard_map/vmap()/add | solution.py:227
  45.4 5.7 %collective-permute-start.7 = (f32[1,128,1280]{1,2,0:T(8,128)}, f32[1,128,1280]{1,2,0:T(8,128)}, u32[]{:S(2)}, u32[]{:S(2)}) collective-permute-start(f32[1,128,1280]{1,2,0:T(8,128)} %multiply_add_fusion.5), channel_id=1, source_target_pairs={{2,10},{6,14},{1,9},{5,13},{18,26},{22,30},{17,25},{21,29}} | collective-permute-start | bytes 1966088 | tf_op jit(solution)/shard_map/vmap()/ppermute | solution.py:114
  52.1 1.3 %collective-permute-start.11 = (f32[1,128,1280]{1,2,0:T(8,128)}, f32[1,128,1280]{1,2,0:T(8,128)}, u32[]{:S(2)}, u32[]{:S(2)}) collective-permute-start(f32[1,128,1280]{1,2,0:T(8,128)} %multiply_add_fusion.2), channel_id=1, source_target_pairs={{13,5},{9,1},{14,6},{10,2},{29,21},{25,17},{30,22},{26,18}} | collective-permute-start | bytes 1966088 | tf_op jit(solution)/shard_map/vmap()/ppermute | solution.py:114
  53.5 1.1 %copy.48 = bf16[1,128,2560]{1,2,0:T(8,128)(2,1)} copy(bf16[1,128,2560]{2,1,0:T(8,128)(2,1)S(1)} %copy-done.1) | data formatting | bytes 1310720 | tf_op jit(solution)/shard_map/optimization_barrier | solution.py:313
  54.7 1.3 %copy.51 = f32[1,128,2560]{1,2,0:T(8,128)} copy(bf16[1,128,2560]{2,1,0:T(8,128)(2,1)S(1)} %copy-done.1) | data formatting | bytes 1966080 | tf_op jit(solution)/shard_map/vmap()/convert_element_type | solution.py:53
  56.7 1.4 %collective-permute-done.7 = f32[1,128,1280]{1,2,0:T(8,128)} collective-permute-done((f32[1,128,1280]{1,2,0:T(8,128)}, f32[1,128,1280]{1,2,0:T(8,128)}, u32[]{:S(2)}, u32[]{:S(2)}) %collective-permute-start.7) | collective-permute-done | bytes 655392 | tf_op jit(solution)/shard_map/vmap()/ppermute | solution.py:114
  58.0 2.4 %add_select_fusion.2 = f32[1,128,1280]{1,2,0:T(8,128)} fusion(f32[1,128,1280]{1,2,0:T(8,128)S(1)} %copy-done.5, f32[1280]{0:T(1024)S(1)} %broadcast_in_dim.212, pred[]{:T(512)S(6)} %eq.27, f32[1,128,1280]{1,2,0:T(8,128)S(1)} %collective-permute-done.6, f32[1,128,1280]{1,2,0:T(8,128)} %collective-permute-done.7, f32[1280]{0:T(1024)S(1)} %broadcast_in_dim.215), kind=kLoop, calls=%fused_computation.50 | loop fusion | flops 819200 | bytes 2631681 | tf_op jit(solution)/shard_map/vmap(jit(_where))/select_n | solution.py:159
  60.5 1.5 %collective-permute-start.8 = (f32[1,128,1280]{1,2,0:T(8,128)}, f32[1,128,1280]{1,2,0:T(8,128)S(1)}, u32[]{:S(2)}, u32[]{:S(2)}) collective-permute-start(f32[1,128,1280]{1,2,0:T(8,128)} %add_select_fusion.2), channel_id=1, source_target_pairs={{6,4},{10,8},{14,12},{1,3},{5,7},{9,11},{13,15},{22,20},{26,24},{3... | collective-permute-start | bytes 1966088 | tf_op jit(solution)/shard_map/vmap()/ppermute | solution.py:114
  61.9 9.8 %collective-permute-done.11 = f32[1,128,1280]{1,2,0:T(8,128)} collective-permute-done((f32[1,128,1280]{1,2,0:T(8,128)}, f32[1,128,1280]{1,2,0:T(8,128)}, u32[]{:S(2)}, u32[]{:S(2)}) %collective-permute-start.11) | collective-permute-done | bytes 655392 | tf_op jit(solution)/shard_map/vmap()/ppermute | solution.py:114
  71.7 2.4 %add_select_fusion = f32[1,128,1280]{1,2,0:T(8,128)} fusion(f32[1,128,1280]{1,2,0:T(8,128)S(1)} %copy-done.4, f32[1280]{0:T(1024)S(1)} %broadcast_in_dim.230, pred[]{:T(512)S(6)} %eq.30, f32[1,128,1280]{1,2,0:T(8,128)S(1)} %collective-permute-done.10, f32[1,128,1280]{1,2,0:T(8,128)} %collective-permute-done.11, f32[1280]{0:T(1024)S(1)} %broadcast_in_dim.233), kind=kLoop, calls=%fused_computation.43 | loop fusion | flops 819200 | bytes 2631681 | tf_op jit(solution)/shard_map/vmap(jit(_where))/select_n | solution.py:159
  74.1 2.1 %collective-permute-start.12 = (f32[1,128,1280]{1,2,0:T(8,128)}, f32[1,128,1280]{1,2,0:T(8,128)}, u32[]{:S(2)}, u32[]{:S(2)}) collective-permute-start(f32[1,128,1280]{1,2,0:T(8,128)} %add_select_fusion), channel_id=1, source_target_pairs={{9,11},{5,7},{1,3},{14,12},{10,8},{6,4},{2,0},{25,27},{21,23},{17,... | collective-permute-start | bytes 1966088 | tf_op jit(solution)/shard_map/vmap()/ppermute | solution.py:114
  76.2 2.2 %fusion = f32[1,128,40,64]{1,3,2,0:T(8,128)} fusion(bf16[128,40,64]{0,2,1:T(8,128)(2,1)S(1)} %bitcast.227, f32[1,128,40,64]{1,3,2,0:T(8,128)S(1)} %bitcast.226, f32[40,128]{1,0:T(8,128)S(1)} %copy-done.22, f32[128,128]{1,0:T(8,128)S(1)} %fusion.46, pred[128,128]{1,0:T(8,128)(4,1)S(1)} %copy-done.23, f32[40]{0:T(128)S(1)} %copy-done.24), kind=kOutput, calls=%fused_computation.13 | convolution fusion | flops 87818240 | bytes 3379360 | tf_op jit(solution)/shard_map/vmap(hij,ihp->jhp)/dot_general | solution.py:51
  78.4 1.1 %copy.52 = bf16[1,128,2560]{1,2,0:T(8,128)(2,1)} copy(bf16[1,128,2560]{2,1,0:T(8,128)(2,1)S(1)} %copy-done.11) | data formatting | bytes 1310720 | tf_op jit(solution)/shard_map/optimization_barrier | solution.py:313
  80.4 2.2 %fusion.18 = (f32[1,128,1280]{1,2,0:T(8,128)S(1)}, f32[1,128,1280]{1,2,0:T(8,128)S(1)}) fusion(f32[1,128,1280]{1,2,0:T(8,128)S(1)} %copy-done.2, f32[1280]{0:T(1024)S(1)} %broadcast_in_dim.227, pred[]{:T(512)S(6)} %eq.27, f32[1,128,1280]{1,2,0:T(8,128)} %copy-done.16, f32[1,128,1280]{1,2,0:T(8,128)} %copy-done.10, f32[1280]{0:T(1024)S(1)} %copy-done.21, ...), kind=kLoop, calls=%fused_computation.48 | loop fusion | flops 1638400 | bytes 4602882 | tf_op jit(solution)/shard_map/vmap(jit(_where))/select_n | solution.py:258
  83.2 1.9 %fusion.17 = (f32[1,128,1280]{1,2,0:T(8,128)S(1)}, f32[1,128,1280]{1,2,0:T(8,128)S(1)}) fusion(f32[1,128,1280]{1,2,0:T(8,128)S(1)} %copy-done.3, f32[1280]{0:T(1024)S(1)} %broadcast_in_dim.245, pred[]{:T(512)S(6)} %eq.30, f32[1,128,1280]{1,2,0:T(8,128)} %collective-permute-done.12, f32[1,128,1280]{1,2,0:T(8,128)S(1)} %copy-done.9, ...), kind=kLoop, calls=%fused_computation.41 | loop fusion | flops 1638400 | bytes 4602882 | tf_op jit(solution)/shard_map/vmap(jit(_where))/select_n | solution.py:258
  85.2 7.4 %collective-permute-start.13 = (f32[1,128,2560]{1,2,0:T(8,128)S(1)}, f32[1,128,2560]{1,2,0:T(8,128)S(1)}, u32[]{:S(2)}, u32[]{:S(2)}) collective-permute-start(f32[1,128,2560]{1,2,0:T(8,128)S(1)} %pad_maximum_fusion.1), channel_id=1, source_target_pairs={{0,1},{1,0},{2,3},{3,2},{4,5},{5,4},{6,7},{7,6},{8,9},{9,8},{10,11... | collective-permute-start | bytes 3932168 | tf_op jit(solution)/shard_map/vmap()/ppermute | solution.py:260
  92.6 1.3 %convert_reduce_fusion = bf16[128,128]{1,0:T(8,128)(2,1)S(1)} fusion(f32[40,128]{1,0:T(8,128)S(1)} %copy-done.22, pred[128,128]{1,0:T(8,128)(4,1)S(1)} %copy-done.23, bf16[128,40,64]{0,2,1:T(8,128)(2,1)S(1)} %bitcast.228, bf16[128,40,64]{0,2,1:T(8,128)(2,1)S(1)} %bitcast.229), kind=kOutput, calls=%fused_computation.2 | convolution fusion | flops 88457216 | bytes 1380352 | tf_op jit(solution)/shard_map/vmap(ihp,jhp->hij)/dot_general | solution.py:45
  (178 shorter events, 23.1 us)
Async XLA Ops:
  0.6 5.1 %copy-start = (bf16[1,128,128]{2,1,0:T(8,128)(2,1)S(1)}, bf16[1,128,128]{2,1,0:T(8,128)(2,1)}, u32[]{:S(2)}) copy-start(bf16[1,128,128]{2,1,0:T(8,128)(2,1)} %param.8) | copy-start | bytes 98308
  0.6 2.6 %copy-start.1 = (bf16[1,128,2560]{2,1,0:T(8,128)(2,1)S(1)}, bf16[1,128,2560]{2,1,0:T(8,128)(2,1)}, u32[]{:S(2)}) copy-start(bf16[1,128,2560]{2,1,0:T(8,128)(2,1)} %param.7) | copy-start | bytes 1966084
  5.1 4.4 %collective-permute-start = (f32[1,17,40]{2,1,0:T(8,128)S(1)}, f32[1,17,40]{2,1,0:T(8,128)S(1)}, u32[]{:S(2)}, u32[]{:S(2)}) collective-permute-start(f32[1,17,40]{2,1,0:T(8,128)S(1)} %pad_maximum_fusion.2), channel_id=1, source_target_pairs={{0,1},{1,0},{2,3},{3,2},{4,5},{5,4},{6,7},{7,6},{8,9},{9,8},{10,11... | collective-permute-start | bytes 8168 | tf_op jit(solution)/shard_map/vmap()/ppermute | solution.py:69
  8.0 3.5 %collective-permute-start.1 = (f32[1,128,2560]{1,2,0:T(8,128)}, f32[1,128,2560]{1,2,0:T(8,128)}, u32[]{:S(2)}, u32[]{:S(2)}) collective-permute-start(f32[1,128,2560]{1,2,0:T(8,128)} %pad_maximum_fusion), channel_id=1, source_target_pairs={{0,1},{1,0},{2,3},{3,2},{4,5},{5,4},{6,7},{7,6},{8,9},{9,8},{10,11... | collective-permute-start | bytes 3932168 | tf_op jit(solution)/shard_map/vmap()/ppermute | solution.py:240
  14.6 5.6 %collective-permute-start.3 = (f32[1,17,40]{2,1,0:T(8,128)S(1)}, f32[1,17,40]{2,1,0:T(8,128)S(1)}, u32[]{:S(2)}, u32[]{:S(2)}) collective-permute-start(f32[1,17,40]{2,1,0:T(8,128)S(1)} %fusion.89), channel_id=1, source_target_pairs={{0,2},{1,3},{2,0},{3,1},{4,6},{5,7},{6,4},{7,5},{8,10},{9,11},{10,... | collective-permute-start | bytes 8168 | tf_op jit(solution)/shard_map/vmap()/ppermute | solution.py:69
  17.6 13.5 %collective-permute-start.2 = (f32[1,128,1280]{1,2,0:T(8,128)}, f32[1,128,1280]{1,2,0:T(8,128)S(1)}, u32[]{:S(2)}, u32[]{:S(2)}) collective-permute-start(f32[1,128,1280]{1,2,0:T(8,128)} %get-tuple-element.192), channel_id=1, source_target_pairs={{0,2},{4,6},{8,10},{12,14},{3,1},{7,5},{11,9},{15,13},{16,18},{20,... | collective-permute-start | bytes 1966088 | tf_op jit(solution)/shard_map/vmap()/ppermute | solution.py:114
  18.9 17.8 %collective-permute-start.9 = (f32[1,128,1280]{1,2,0:T(8,128)}, f32[1,128,1280]{1,2,0:T(8,128)S(1)}, u32[]{:S(2)}, u32[]{:S(2)}) collective-permute-start(f32[1,128,1280]{1,2,0:T(8,128)} %get-tuple-element.196), channel_id=1, source_target_pairs={{15,13},{11,9},{7,5},{3,1},{12,14},{8,10},{4,6},{0,2},{31,29},{27,... | collective-permute-start | bytes 1966088 | tf_op jit(solution)/shard_map/vmap()/ppermute | solution.py:114
  20.2 2.6 %collective-permute-start.4 = (f32[1,17,40]{2,1,0:T(8,128)S(1)}, f32[1,17,40]{2,1,0:T(8,128)S(1)}, u32[]{:S(2)}, u32[]{:S(2)}) collective-permute-start(f32[1,17,40]{2,1,0:T(8,128)S(1)} %add.200), channel_id=1, source_target_pairs={{0,4},{1,5},{2,6},{3,7},{4,0},{5,1},{6,2},{7,3},{8,12},{9,13},{10,... | collective-permute-start | bytes 8168 | tf_op jit(solution)/shard_map/vmap()/ppermute | solution.py:69
  21.8 15.8 %copy-start.4 = (f32[1,128,1280]{1,2,0:T(8,128)S(1)}, f32[1,128,1280]{1,2,0:T(8,128)}, u32[]{:S(2)}) copy-start(f32[1,128,1280]{1,2,0:T(8,128)} %get-tuple-element.196) | copy-start | bytes 1966084
  22.8 3.4 %collective-permute-start.5 = (f32[1,17,40]{2,1,0:T(8,128)S(1)}, f32[1,17,40]{2,1,0:T(8,128)S(1)}, u32[]{:S(2)}, u32[]{:S(2)}) collective-permute-start(f32[1,17,40]{2,1,0:T(8,128)S(1)} %add.202), channel_id=1, source_target_pairs={{0,8},{1,9},{2,10},{3,11},{4,12},{5,13},{6,14},{7,15},{8,0},{9,1},... | collective-permute-start | bytes 8168 | tf_op jit(solution)/shard_map/vmap()/ppermute | solution.py:69
  29.9 9.5 %collective-permute-start.14 = (f32[40]{0:T(128)S(1)}, f32[40]{0:T(128)S(1)}, u32[]{:S(2)}, u32[]{:S(2)}) collective-permute-start(f32[40]{0:T(128)S(1)} %slice_bitcast_fusion.5), channel_id=1, source_target_pairs={{0,16},{16,0},{1,17},{17,1},{2,18},{18,2},{3,19},{19,3},{4,20},{20... | collective-permute-start | bytes 488 | tf_op jit(solution)/shard_map/ppermute | solution.py:312
  33.5 10.7 %collective-permute-start.6 = (f32[1,128,1280]{1,2,0:T(8,128)S(1)}, f32[1,128,1280]{1,2,0:T(8,128)S(1)}, u32[]{:S(2)}, u32[]{:S(2)}) collective-permute-start(f32[1,128,1280]{1,2,0:T(8,128)S(1)} %add_select_fusion.3), channel_id=1, source_target_pairs={{2,6},{6,10},{10,14},{1,5},{5,9},{9,13},{18,22},{22,26},{26,30},{1... | collective-permute-start | bytes 1966088 | tf_op jit(solution)/shard_map/vmap()/ppermute | solution.py:114
  38.0 13.0 %collective-permute-start.10 = (f32[1,128,1280]{1,2,0:T(8,128)S(1)}, f32[1,128,1280]{1,2,0:T(8,128)S(1)}, u32[]{:S(2)}, u32[]{:S(2)}) collective-permute-start(f32[1,128,1280]{1,2,0:T(8,128)S(1)} %add_select_fusion.1), channel_id=1, source_target_pairs={{13,9},{9,5},{5,1},{14,10},{10,6},{6,2},{29,25},{25,21},{21,17},{3... | collective-permute-start | bytes 1966088 | tf_op jit(solution)/shard_map/vmap()/ppermute | solution.py:114
  45.4 12.7 %collective-permute-start.7 = (f32[1,128,1280]{1,2,0:T(8,128)}, f32[1,128,1280]{1,2,0:T(8,128)}, u32[]{:S(2)}, u32[]{:S(2)}) collective-permute-start(f32[1,128,1280]{1,2,0:T(8,128)} %multiply_add_fusion.5), channel_id=1, source_target_pairs={{2,10},{6,14},{1,9},{5,13},{18,26},{22,30},{17,25},{21,29}} | collective-permute-start | bytes 1966088 | tf_op jit(solution)/shard_map/vmap()/ppermute | solution.py:114
  52.1 19.6 %collective-permute-start.11 = (f32[1,128,1280]{1,2,0:T(8,128)}, f32[1,128,1280]{1,2,0:T(8,128)}, u32[]{:S(2)}, u32[]{:S(2)}) collective-permute-start(f32[1,128,1280]{1,2,0:T(8,128)} %multiply_add_fusion.2), channel_id=1, source_target_pairs={{13,5},{9,1},{14,6},{10,2},{29,21},{25,17},{30,22},{26,18}} | collective-permute-start | bytes 1966088 | tf_op jit(solution)/shard_map/vmap()/ppermute | solution.py:114
  54.7 3.4 %copy-start.5 = (f32[1,128,1280]{1,2,0:T(8,128)S(1)}, f32[1,128,1280]{1,2,0:T(8,128)}, u32[]{:S(2)}) copy-start(f32[1,128,1280]{1,2,0:T(8,128)} %get-tuple-element.192) | copy-start | bytes 1966084
  60.4 15.8 %copy-start.15 = (f32[1,128,2560]{1,2,0:T(8,128)S(1)}, f32[1,128,2560]{1,2,0:T(8,128)}, u32[]{:S(2)}) copy-start(f32[1,128,2560]{1,2,0:T(8,128)} %copy.51) | copy-start | bytes 3932164
  60.4 15.8 %copy-start.17 = (bf16[1,128,2560]{1,2,0:T(8,128)(2,1)S(1)}, bf16[1,128,2560]{1,2,0:T(8,128)(2,1)}, u32[]{:S(2)}) copy-start(bf16[1,128,2560]{1,2,0:T(8,128)(2,1)} %copy.48) | copy-start | bytes 1966084
  60.4 15.8 %copy-start.22 = (f32[40,128]{1,0:T(8,128)S(1)}, f32[40,128]{1,0:T(8,128)}, u32[]{:S(2)}) copy-start(f32[40,128]{1,0:T(8,128)} %copy.49) | copy-start | bytes 61444
  60.4 15.8 %copy-start.23 = (pred[128,128]{1,0:T(8,128)(4,1)S(1)}, pred[128,128]{1,0:T(8,128)(4,1)}, u32[]{:S(2)}) copy-start(pred[128,128]{1,0:T(8,128)(4,1)} %iota_compare_fusion) | copy-start | bytes 49156
  60.4 15.8 %copy-start.24 = (f32[40]{0:T(128)S(1)}, f32[40]{0:T(128)}, u32[]{:S(2)}) copy-start(f32[40]{0:T(128)} %param.11) | copy-start | bytes 484
  60.5 19.1 %collective-permute-start.8 = (f32[1,128,1280]{1,2,0:T(8,128)}, f32[1,128,1280]{1,2,0:T(8,128)S(1)}, u32[]{:S(2)}, u32[]{:S(2)}) collective-permute-start(f32[1,128,1280]{1,2,0:T(8,128)} %add_select_fusion.2), channel_id=1, source_target_pairs={{6,4},{10,8},{14,12},{1,3},{5,7},{9,11},{13,15},{22,20},{26,24},{3... | collective-permute-start | bytes 1966088 | tf_op jit(solution)/shard_map/vmap()/ppermute | solution.py:114
  74.1 9.1 %collective-permute-start.12 = (f32[1,128,1280]{1,2,0:T(8,128)}, f32[1,128,1280]{1,2,0:T(8,128)}, u32[]{:S(2)}, u32[]{:S(2)}) collective-permute-start(f32[1,128,1280]{1,2,0:T(8,128)} %add_select_fusion), channel_id=1, source_target_pairs={{9,11},{5,7},{1,3},{14,12},{10,8},{6,4},{2,0},{25,27},{21,23},{17,... | collective-permute-start | bytes 1966088 | tf_op jit(solution)/shard_map/vmap()/ppermute | solution.py:114
  76.2 2.2 %copy-start.11 = (bf16[1,128,2560]{2,1,0:T(8,128)(2,1)S(1)}, bf16[1,128,2560]{2,1,0:T(8,128)(2,1)}, u32[]{:S(2)}) copy-start(bf16[1,128,2560]{2,1,0:T(8,128)(2,1)} %param.6) | copy-start | bytes 1966084
  78.4 2.0 %copy-start.2 = (f32[1,128,1280]{1,2,0:T(8,128)S(1)}, f32[1,128,1280]{1,2,0:T(8,128)}, u32[]{:S(2)}) copy-start(f32[1,128,1280]{1,2,0:T(8,128)} %get-tuple-element.193) | copy-start | bytes 1966084
  78.4 2.0 %copy-start.21 = (f32[1280]{0:T(1024)S(1)}, f32[1280]{0:T(1024)}, u32[]{:S(2)}) copy-start(f32[1280]{0:T(1024)} %broadcast_in_dim.224) | copy-start | bytes 15364
  80.4 2.8 %copy-start.3 = (f32[1,128,1280]{1,2,0:T(8,128)S(1)}, f32[1,128,1280]{1,2,0:T(8,128)}, u32[]{:S(2)}) copy-start(f32[1,128,1280]{1,2,0:T(8,128)} %get-tuple-element.197) | copy-start | bytes 1966084
  80.4 2.8 %copy-start.9 = (f32[1,128,1280]{1,2,0:T(8,128)S(1)}, f32[1,128,1280]{1,2,0:T(8,128)}, u32[]{:S(2)}) copy-start(f32[1,128,1280]{1,2,0:T(8,128)} %copy-done.8) | copy-start | bytes 1966084
  85.1 7.6 %copy-start.18 = (bf16[1,128,2560]{1,2,0:T(8,128)(2,1)S(1)}, bf16[1,128,2560]{1,2,0:T(8,128)(2,1)}, u32[]{:S(2)}) copy-start(bf16[1,128,2560]{1,2,0:T(8,128)(2,1)} %copy.48) | copy-start | bytes 1966084
  85.1 7.6 %copy-start.19 = (bf16[1,128,2560]{1,2,0:T(8,128)(2,1)S(1)}, bf16[1,128,2560]{1,2,0:T(8,128)(2,1)}, u32[]{:S(2)}) copy-start(bf16[1,128,2560]{1,2,0:T(8,128)(2,1)} %copy.52) | copy-start | bytes 1966084
  85.2 10.7 %collective-permute-start.13 = (f32[1,128,2560]{1,2,0:T(8,128)S(1)}, f32[1,128,2560]{1,2,0:T(8,128)S(1)}, u32[]{:S(2)}, u32[]{:S(2)}) collective-permute-start(f32[1,128,2560]{1,2,0:T(8,128)S(1)} %pad_maximum_fusion.1), channel_id=1, source_target_pairs={{0,1},{1,0},{2,3},{3,2},{4,5},{5,4},{6,7},{7,6},{8,9},{9,8},{10,11... | collective-permute-start | bytes 3932168 | tf_op jit(solution)/shard_map/vmap()/ppermute | solution.py:260
  96.2 2.2 %copy-start.14 = (f32[1,128,40,64]{1,3,2,0:T(8,128)S(1)}, f32[1,128,40,64]{1,3,2,0:T(8,128)}, u32[]{:S(2)}) copy-start(f32[1,128,40,64]{1,3,2,0:T(8,128)} %fusion) | copy-start | bytes 3932164
  (8 other events, 8.4 us)

commit v14 on v13

--- a/solution.py
+++ b/solution.py
@@ -177,11 +177,11 @@
         return lower_gain * prefix + lowers[level]
 
 
-def pair_scans(ways, pair_totals):
+def pair_scans(ways, pair_totals, local_terms):
     scans = [PairScan(way) for way in ways]
     level_count = scans[0].level_count
     if scans[0].flip:
-        return shift_scans(scans, pair_totals)
+        return shift_scans(scans, pair_totals, local_terms)
     totals = list(pair_totals)
     lowers = [[] for _ in scans]
     for level in range(level_count):
@@ -201,10 +201,10 @@
             scan.down_combine(level, p, g, low) for scan, p, g, low in zip(scans, prefixes, got, lowers)
         ]
     anchor = lowers[0][0] if level_count else pair_totals[0]
-    return prefixes, anchor
-
-
-def shift_scans(scans, pair_totals):
+    return prefixes, local_terms(anchor)
+
+
+def shift_scans(scans, pair_totals, local_terms):
     group_count = scans[0].pair_count // 2
     got = exchange(list(pair_totals), [scan.up_send(0) for scan in scans])
     lowers = [[g] for g in got]
@@ -227,13 +227,14 @@
                 through[k] = before_gain * group_gain(scan, group) * got[k] + through[k]
             before[k] = before_gain * got[k] + before[k]
         span *= 2
+    before, local = lax.optimization_barrier((before, local_terms(lowers[0][0])))
     sends = [scan.down_send(0, p, t) for scan, p, t in zip(scans, before, pair_totals)]
     got = exchange([s[0] for s in sends], [s[1] for s in sends])
     prefixes = [scan.down_combine(0, p, g, low) for scan, p, g, low in zip(scans, before, got, lowers)]
-    return prefixes, lowers[0][0]
-
-
-def carried_pair(tables, fwd_state, adj_state, position, count, head_width):
+    return prefixes, local
+
+
+def carried_pair(tables, fwd_state, adj_state, position, count, head_width, local_inputs, skip_gain):
     ways = [Direction(tables, position, count, reverse, head_width) for reverse in (False, True)]
     states = [fwd_state, adj_state]
     sent = jnp.concatenate([take_half(s, ~w.upper) for s, w in zip(states, ways)], -1)
@@ -250,7 +251,12 @@
         totals.append(way.gain(1, 2 * way.pair + 1, 1) * low_block + high_block)
     tables[-1], _ = lax.optimization_barrier((tables[-1], totals))
     extend_totals(tables, count, 1, count.bit_length())
-    pair_prefixes, anchor = pair_scans(ways, totals)
+
+    def local_terms(anchor):
+        held, _ = lax.optimization_barrier((local_inputs, anchor))
+        return block_local_grads(*held, skip_gain)
+
+    pair_prefixes, local_grads = pair_scans(ways, totals, local_terms)
     lifted_parts = []
     keep_parts = []
     for way, pair_prefix, low_block in zip(ways, pair_prefixes, lows):
@@ -262,7 +268,7 @@
     got = got * unit
     half = got.shape[-1] // 2
     others = [got[..., :half], got[..., half:]]
-    return (keep_parts, others, [way.upper for way in ways]), anchor, tables[-1]
+    return (keep_parts, others, [way.upper for way in ways]), local_grads, tables[-1]
 
 
 def block_carried_grads(write_map, value_scale, decayed_vals, decayed_cot, carried, local_grads):
@@ -304,16 +310,13 @@
     count = lax.axis_size("ctx")
     tables = jax.vmap(gather_totals, (0, 0, None, None))(totals, skip_parts, position, count)
     head_width = token_values.shape[2] // decay_codes.shape[2]
-    carried, anchor, final_table = jax.vmap(carried_pair, (0, 0, 0, None, None, None))(
-        tables, fwd_state, adj_state, position, count, head_width
+    local_inputs = (token_values, cotangent, write_coeffs, read_coeffs, within)
+    carried, local_grads, final_table = jax.vmap(carried_pair, (0, 0, 0, None, None, None, 0, None))(
+        tables, fwd_state, adj_state, position, count, head_width, local_inputs, skip_gain
     )
     grad_skip = jnp.sum(final_table[:, count], axis=0)
     for bit in range(lax.axis_size("dp").bit_length() - 1):
         grad_skip = grad_skip + lax.ppermute(grad_skip, "dp", xor_pairs(lax.axis_size("dp"), bit))
-    local_inputs, _ = lax.optimization_barrier(
-        ((token_values, cotangent, write_coeffs, read_coeffs, within), anchor)
-    )
-    local_grads = jax.vmap(block_local_grads, (0, 0, 0, 0, 0, None))(*local_inputs, skip_gain)
     grad_values, grad_write, grad_read = jax.vmap(block_carried_grads)(
         write_coeffs, value_scale, decayed_vals, decayed_cot, carried, local_grads
     )

time: 101 us -> 107 us (1.059)
  the two profiles are of different devices: /device:TPU:1 before, /device:TPU:27 now
where the time goes in v14:
time: 107 us; the launch traced here: 106 us
  waiting for transfers between devices  28.3 us (26%)
  other arithmetic  27.7 us (26%)
  starting transfers between devices  26.2 us (24%)
  local copies, waits for them, and re-layouts  14.2 us (13%)
  matrix products  8.17 us (8%)
  between operations  1.9 us (2%)
    ppermute x8, waiting for transfers between devices, exchange(): lax.ppermute(p, 'ctx', pairs)  22.9 us
    ppermute x8, starting transfers between devices, exchange(): lax.ppermute(p, 'ctx', pairs)  14.1 us
    ppermute x1, starting transfers between devices, carried_pair(): lax.ppermute(jnp.concatenate(lifted_parts, -1), 'ctx', [(i, i ^ 1) for i...  9.43 us
    unnamed x51, local copies, waits for them, and re-layouts  5.23 us
    ppermute x4, waiting for transfers between devices, extend_totals(): lax.ppermute(tables[-1], 'ctx', xor_pairs(count, bit))  4.74 us
    dot_general x1, matrix products, block_local_grads(): jnp.einsum('hij,ihp->jhp', value_weights, cot_three, preferred_element_ty...  3.3 us
    select_n x2, other arithmetic, carried_pair(): lifted_parts.append(jnp.where(way.upper, pair_prefix, lifted))  3.29 us
    add x1, other arithmetic, carried_pair(): totals.append(way.gain(1, 2 * way.pair + 1, 1) * low_block + high_block)  3.28 us
  transfers between devices with their start and end apart: 15, of which 8 were waited for; matrix products, arithmetic and copies ran while one was open for 30% of the time, Pallas kernels for 0%

profile of v14, /device:TPU:27, one launch (start us, length us, event | category | flops | bytes accessed | tf_op | source)
XLA Modules:
  0.0 106.4 jit_solution(15286497221647619505)
XLA Ops:
  1.8 1.4 %copy.45 = bf16[1,128,2560]{1,2,0:T(8,128)(2,1)S(1)} copy(bf16[1,128,2560]{2,1,0:T(8,128)(2,1)} %param.6) | data formatting | bytes 1310720 | tf_op args[0]
  3.7 1.2 %fusion.1 = (f32[2560]{0:T(1024)S(1)}, bf16[1,128,2560]{1,2,0:T(8,128)(2,1)}, bf16[1,128,2560]{1,2,0:T(8,128)(2,1)S(1)}) fusion(bf16[1,128,2560]{1,2,0:T(8,128)(2,1)S(1)} %copy.46, bf16[1,128,2560]{1,2,0:T(8,128)(2,1)S(1)} %copy.45, f32[128,40]{0,1:T(8,128)S(1)} %get-tuple-element.211, f32[128,40]{0,1:T(8,128)S(1)} %get-tuple-element.212), kind=kLoop, calls=%fused_computation.14 | loop fusion | flops 2618880 | bytes 2672640 | tf_op jit(solution)/shard_map/vmap()/reduce_sum | solution.py:25
  7.4 1.1 %pad_maximum_fusion = f32[1,128,2560]{1,2,0:T(8,128)} fusion(f32[1,128,1280]{1,2,0:T(8,128)S(1)} %get-tuple-element.241, f32[1,128,1280]{1,2,0:T(8,128)S(1)} %get-tuple-element.242), kind=kLoop, calls=%fused_computation.19 | loop fusion | flops 327680 | bytes 2621440 | tf_op jit(solution)/shard_map/vmap()/concatenate | solution.py:240
  11.9 3.3 %select_add_fusion = (f32[1,128,1280]{1,2,0:T(8,128)}, f32[1,128,1280]{1,2,0:T(8,128)}, f32[1,128,1280]{1,2,0:T(8,128)}, f32[1,128,1280]{1,2,0:T(8,128)}) fusion(f32[1,128,2560]{1,2,0:T(8,128)} %collective-permute-done.1, f32[1280]{0:T(1024)S(1)} %broadcast_in_dim.206, pred[]{:T(512)S(6)} %eq.30, f32[1,128,2560]{1,2,0:T(8,128)S(1)} %convolution_bitcast_fusion, ...), kind=kLoop, calls=%fused_computation.52 | loop fusion | flops 1638400 | bytes 6563842 | tf_op jit(solution)/shard_map/vmap()/add | solution.py:251
  15.2 1.2 %collective-permute-start.2 = (f32[1,17,40]{2,1,0:T(8,128)S(1)}, f32[1,17,40]{2,1,0:T(8,128)S(1)}, u32[]{:S(2)}, u32[]{:S(2)}) collective-permute-start(f32[1,17,40]{2,1,0:T(8,128)S(1)} %fusion.87), channel_id=1, source_target_pairs={{0,2},{1,3},{2,0},{3,1},{4,6},{5,7},{6,4},{7,5},{8,10},{9,11},{10,... | collective-permute-start | bytes 8168 | tf_op jit(solution)/shard_map/vmap()/ppermute | solution.py:69
  16.8 1.3 %collective-permute-start.5 = (f32[1,128,1280]{1,2,0:T(8,128)}, f32[1,128,1280]{1,2,0:T(8,128)S(1)}, u32[]{:S(2)}, u32[]{:S(2)}) collective-permute-start(f32[1,128,1280]{1,2,0:T(8,128)} %get-tuple-element.206), channel_id=1, source_target_pairs={{0,2},{4,6},{8,10},{12,14},{3,1},{7,5},{11,9},{15,13},{16,18},{20,... | collective-permute-start | bytes 1966088 | tf_op jit(solution)/shard_map/vmap()/ppermute | solution.py:114
  18.1 1.3 %collective-permute-start.8 = (f32[1,128,1280]{1,2,0:T(8,128)}, f32[1,128,1280]{1,2,0:T(8,128)S(1)}, u32[]{:S(2)}, u32[]{:S(2)}) collective-permute-start(f32[1,128,1280]{1,2,0:T(8,128)} %get-tuple-element.202), channel_id=1, source_target_pairs={{15,13},{11,9},{7,5},{3,1},{12,14},{8,10},{4,6},{0,2},{31,29},{27,... | collective-permute-start | bytes 1966088 | tf_op jit(solution)/shard_map/vmap()/ppermute | solution.py:114
  20.1 2.0 %collective-permute-done.3 = f32[1,17,40]{2,1,0:T(8,128)S(1)} collective-permute-done((f32[1,17,40]{2,1,0:T(8,128)S(1)}, f32[1,17,40]{2,1,0:T(8,128)S(1)}, u32[]{:S(2)}, u32[]{:S(2)}) %collective-permute-start.3) | collective-permute-done | bytes 2752 | tf_op jit(solution)/shard_map/vmap()/ppermute | solution.py:69
  22.8 2.8 %collective-permute-done.4 = f32[1,17,40]{2,1,0:T(8,128)S(1)} collective-permute-done((f32[1,17,40]{2,1,0:T(8,128)S(1)}, f32[1,17,40]{2,1,0:T(8,128)S(1)}, u32[]{:S(2)}, u32[]{:S(2)}) %collective-permute-start.4) | collective-permute-done | bytes 2752 | tf_op jit(solution)/shard_map/vmap()/ppermute | solution.py:69
  30.1 2.4 %copy.52 = bf16[1,128,2560]{1,2,0:T(8,128)(2,1)} copy(bf16[1,128,2560]{2,1,0:T(8,128)(2,1)} %param.6) | data formatting | bytes 1310720 | tf_op jit(solution)/shard_map/vmap()/optimization_barrier | solution.py:256
  32.6 2.8 %collective-permute-done.8 = f32[1,128,1280]{1,2,0:T(8,128)S(1)} collective-permute-done((f32[1,128,1280]{1,2,0:T(8,128)}, f32[1,128,1280]{1,2,0:T(8,128)S(1)}, u32[]{:S(2)}, u32[]{:S(2)}) %collective-permute-start.8) | collective-permute-done | bytes 655392 | tf_op jit(solution)/shard_map/vmap()/ppermute | solution.py:114
  35.4 1.3 %add_select_fusion.2 = f32[1,128,1280]{1,2,0:T(8,128)} fusion(f32[1,128,1280]{1,2,0:T(8,128)S(1)} %copy-done.2, f32[1,128,1280]{1,2,0:T(8,128)S(1)} %collective-permute-done.8, f32[1280]{0:T(1024)S(1)} %broadcast_in_dim.230, f32[1280]{0:T(1024)S(1)} %broadcast_in_dim.227, pred[]{:T(512)S(6)} %eq.30), kind=kLoop, calls=%fused_computation.48 | loop fusion | flops 819200 | bytes 1976321 | tf_op jit(solution)/shard_map/vmap(jit(_where))/select_n | solution.py:152
  36.7 2.9 %collective-permute-start.9 = (f32[1,128,1280]{1,2,0:T(8,128)}, f32[1,128,1280]{1,2,0:T(8,128)}, u32[]{:S(2)}, u32[]{:S(2)}) collective-permute-start(f32[1,128,1280]{1,2,0:T(8,128)} %add_select_fusion.2), channel_id=1, source_target_pairs={{13,9},{9,5},{5,1},{14,10},{10,6},{6,2},{29,25},{25,21},{21,17},{3... | collective-permute-start | bytes 1966088 | tf_op jit(solution)/shard_map/vmap()/ppermute | solution.py:114
  39.6 1.3 %add_select_fusion.3 = f32[1,128,1280]{1,2,0:T(8,128)} fusion(f32[1,128,1280]{1,2,0:T(8,128)S(1)} %copy-done.3, f32[1,128,1280]{1,2,0:T(8,128)S(1)} %collective-permute-done.5, f32[1280]{0:T(1024)S(1)} %broadcast_in_dim.218, f32[1280]{0:T(1024)S(1)} %broadcast_in_dim.215, pred[]{:T(512)S(6)} %eq.27), kind=kLoop, calls=%fused_computation.51 | loop fusion | flops 819200 | bytes 1976321 | tf_op jit(solution)/shard_map/vmap(jit(_where))/select_n | solution.py:152
  40.9 1.3 %collective-permute-start.6 = (f32[1,128,1280]{1,2,0:T(8,128)}, f32[1,128,1280]{1,2,0:T(8,128)S(1)}, u32[]{:S(2)}, u32[]{:S(2)}) collective-permute-start(f32[1,128,1280]{1,2,0:T(8,128)} %add_select_fusion.3), channel_id=1, source_target_pairs={{2,6},{6,10},{10,14},{1,5},{5,9},{9,13},{18,22},{22,26},{26,30},{1... | collective-permute-start | bytes 1966088 | tf_op jit(solution)/shard_map/vmap()/ppermute | solution.py:114
  42.7 1.3 %copy.51 = f32[1,128,2560]{1,2,0:T(8,128)} copy(bf16[1,128,2560]{2,1,0:T(8,128)(2,1)S(1)} %copy-done.1) | data formatting | bytes 1966080 | tf_op jit(solution)/shard_map/vmap()/convert_element_type | solution.py:53
  44.0 3.3 %fusion = f32[1,128,40,64]{1,3,2,0:T(8,128)} fusion(bf16[128,40,64]{0,2,1:T(8,128)(2,1)S(1)} %bitcast.232, f32[1,128,40,64]{1,3,2,0:T(8,128)} %bitcast.230, f32[40,128]{1,0:T(8,128)S(1)} %copy.49, f32[128,128]{1,0:T(8,128)S(1)} %fusion.44, pred[128,128]{1,0:T(8,128)(4,1)S(1)} %copy-done.19, f32[40]{0:T(128)S(1)} %copy-done.22), kind=kOutput, calls=%fused_computation.13 | convolution fusion | flops 87818240 | bytes 3379360 | tf_op jit(solution)/shard_map/vmap(hij,ihp->jhp)/dot_general | solution.py:51
  47.3 1.3 %convert_reduce_fusion = bf16[128,128]{1,0:T(8,128)(2,1)S(1)} fusion(f32[40,128]{1,0:T(8,128)S(1)} %copy.49, pred[128,128]{1,0:T(8,128)(4,1)S(1)} %copy-done.19, bf16[128,40,64]{0,2,1:T(8,128)(2,1)S(1)} %bitcast.233, bf16[128,40,64]{0,2,1:T(8,128)(2,1)S(1)} %bitcast.231), kind=kOutput, calls=%fused_computation.2 | convolution fusion | flops 88457216 | bytes 1380352 | tf_op jit(solution)/shard_map/vmap(ihp,jhp->hij)/dot_general | solution.py:45
  48.6 1.5 %multiply_add_fusion.3 = f32[1,128,1280]{1,2,0:T(8,128)S(1)} fusion(f32[1,128,1280]{1,2,0:T(8,128)} %add_select_fusion.2, f32[1,128,1280]{1,2,0:T(8,128)} %collective-permute-done.9, f32[1280]{0:T(1024)S(1)} %broadcast_in_dim.224), kind=kLoop, calls=%fused_computation.47 | loop fusion | flops 327680 | bytes 1971200 | tf_op jit(solution)/shard_map/vmap()/add | solution.py:227
  50.1 3.1 %collective-permute-start.10 = (f32[1,128,1280]{1,2,0:T(8,128)S(1)}, f32[1,128,1280]{1,2,0:T(8,128)S(1)}, u32[]{:S(2)}, u32[]{:S(2)}) collective-permute-start(f32[1,128,1280]{1,2,0:T(8,128)S(1)} %multiply_add_fusion.3), channel_id=1, source_target_pairs={{13,5},{9,1},{14,6},{10,2},{29,21},{25,17},{30,22},{26,18}} | collective-permute-start | bytes 1966088 | tf_op jit(solution)/shard_map/vmap()/ppermute | solution.py:114
  53.2 1.6 %multiply_add_fusion.5 = f32[1,128,1280]{1,2,0:T(8,128)S(1)} fusion(f32[1,128,1280]{1,2,0:T(8,128)} %add_select_fusion.3, f32[1,128,1280]{1,2,0:T(8,128)S(1)} %collective-permute-done.6, f32[1280]{0:T(1024)S(1)} %broadcast_in_dim.212), kind=kLoop, calls=%fused_computation.50 | loop fusion | flops 327680 | bytes 1971200 | tf_op jit(solution)/shard_map/vmap()/add | solution.py:227
  54.8 1.3 %collective-permute-start.7 = (f32[1,128,1280]{1,2,0:T(8,128)S(1)}, f32[1,128,1280]{1,2,0:T(8,128)S(1)}, u32[]{:S(2)}, u32[]{:S(2)}) collective-permute-start(f32[1,128,1280]{1,2,0:T(8,128)S(1)} %multiply_add_fusion.5), channel_id=1, source_target_pairs={{2,10},{6,14},{1,9},{5,13},{18,26},{22,30},{17,25},{21,29}} | collective-permute-start | bytes 1966088 | tf_op jit(solution)/shard_map/vmap()/ppermute | solution.py:114
  56.4 4.3 %collective-permute-done.10 = f32[1,128,1280]{1,2,0:T(8,128)S(1)} collective-permute-done((f32[1,128,1280]{1,2,0:T(8,128)S(1)}, f32[1,128,1280]{1,2,0:T(8,128)S(1)}, u32[]{:S(2)}, u32[]{:S(2)}) %collective-permute-start.10) | collective-permute-done | bytes 655392 | tf_op jit(solution)/shard_map/vmap()/ppermute | solution.py:114
  60.7 1.3 %multiply_add_fusion.2 = f32[1,128,1280]{1,2,0:T(8,128)S(1)} fusion(f32[1,128,1280]{1,2,0:T(8,128)} %collective-permute-done.9, f32[1,128,1280]{1,2,0:T(8,128)S(1)} %collective-permute-done.10, f32[1280]{0:T(1024)S(1)} %broadcast_in_dim.221), kind=kLoop, calls=%fused_computation.46 | loop fusion | flops 327680 | bytes 1971200 | tf_op jit(solution)/shard_map/vmap()/add | solution.py:228
  62.1 12.0 %collective-permute-done.7 = f32[1,128,1280]{1,2,0:T(8,128)S(1)} collective-permute-done((f32[1,128,1280]{1,2,0:T(8,128)S(1)}, f32[1,128,1280]{1,2,0:T(8,128)S(1)}, u32[]{:S(2)}, u32[]{:S(2)}) %collective-permute-start.7) | collective-permute-done | bytes 655392 | tf_op jit(solution)/shard_map/vmap()/ppermute | solution.py:114
  74.1 1.3 %multiply_add_fusion.4 = f32[1,128,1280]{1,2,0:T(8,128)S(1)} fusion(f32[1,128,1280]{1,2,0:T(8,128)} %copy-done.13, f32[1,128,1280]{1,2,0:T(8,128)S(1)} %collective-permute-done.7, f32[1280]{0:T(1024)S(1)} %broadcast_in_dim.209), kind=kLoop, calls=%fused_computation.49 | loop fusion | flops 327680 | bytes 1971200 | tf_op jit(solution)/shard_map/vmap()/add | solution.py:228
  76.5 1.5 %collective-permute-start.11 = (f32[1,128,1280]{1,2,0:T(8,128)}, f32[1,128,1280]{1,2,0:T(8,128)S(1)}, u32[]{:S(2)}, u32[]{:S(2)}) collective-permute-start(f32[1,128,1280]{1,2,0:T(8,128)} %add_select_fusion.1), channel_id=1, source_target_pairs={{6,4},{10,8},{14,12},{1,3},{5,7},{9,11},{13,15},{22,20},{26,24},{3... | collective-permute-start | bytes 1966088 | tf_op jit(solution)/shard_map/vmap()/ppermute | solution.py:114
  79.0 1.5 %collective-permute-start.12 = (f32[1,128,1280]{1,2,0:T(8,128)}, f32[1,128,1280]{1,2,0:T(8,128)}, u32[]{:S(2)}, u32[]{:S(2)}) collective-permute-start(f32[1,128,1280]{1,2,0:T(8,128)} %add_select_fusion), channel_id=1, source_target_pairs={{9,11},{5,7},{1,3},{14,12},{10,8},{6,4},{2,0},{25,27},{21,23},{17,... | collective-permute-start | bytes 1966088 | tf_op jit(solution)/shard_map/vmap()/ppermute | solution.py:114
  82.0 3.8 %collective-permute-done.11 = f32[1,128,1280]{1,2,0:T(8,128)S(1)} collective-permute-done((f32[1,128,1280]{1,2,0:T(8,128)}, f32[1,128,1280]{1,2,0:T(8,128)S(1)}, u32[]{:S(2)}, u32[]{:S(2)}) %collective-permute-start.11) | collective-permute-done | bytes 655392 | tf_op jit(solution)/shard_map/vmap()/ppermute | solution.py:114
  86.6 1.8 %fusion.16 = (f32[1,128,1280]{1,2,0:T(8,128)S(1)}, f32[1,128,1280]{1,2,0:T(8,128)S(1)}) fusion(f32[1,128,1280]{1,2,0:T(8,128)S(1)} %copy-done.4, f32[1280]{0:T(1024)S(1)} %broadcast_in_dim.239, pred[]{:T(512)S(6)} %eq.27, f32[1,128,1280]{1,2,0:T(8,128)} %copy-done.16, f32[1,128,1280]{1,2,0:T(8,128)} %copy-done.12, ...), kind=kLoop, calls=%fused_computation.43 | loop fusion | flops 1310720 | bytes 3942402 | tf_op jit(solution)/shard_map/vmap(jit(_where))/select_n | solution.py:264
  88.4 1.5 %fusion.15 = (f32[1,128,1280]{1,2,0:T(8,128)S(1)}, f32[1,128,1280]{1,2,0:T(8,128)S(1)}) fusion(f32[1,128,1280]{1,2,0:T(8,128)S(1)} %copy-done.5, f32[1280]{0:T(1024)S(1)} %broadcast_in_dim.245, pred[]{:T(512)S(6)} %eq.30, f32[1,128,1280]{1,2,0:T(8,128)} %collective-permute-done.12, f32[1,128,1280]{1,2,0:T(8,128)S(1)} %copy-done.11, ...), kind=kLoop, calls=%fused_computation.39 | loop fusion | flops 1310720 | bytes 3942402 | tf_op jit(solution)/shard_map/vmap(jit(_where))/select_n | solution.py:264
  90.0 9.4 %collective-permute-start.13 = (f32[1,128,2560]{1,2,0:T(8,128)S(1)}, f32[1,128,2560]{1,2,0:T(8,128)S(1)}, u32[]{:S(2)}, u32[]{:S(2)}) collective-permute-start(f32[1,128,2560]{1,2,0:T(8,128)S(1)} %pad_maximum_fusion.1), channel_id=1, source_target_pairs={{0,1},{1,0},{2,3},{3,2},{4,5},{5,4},{6,7},{7,6},{8,9},{9,8},{10,11... | collective-permute-start | bytes 3932168 | tf_op jit(solution)/shard_map/vmap()/ppermute | solution.py:266
  (180 shorter events, 25.2 us)
Async XLA Ops:
  0.6 5.6 %copy-start = (bf16[1,128,128]{2,1,0:T(8,128)(2,1)S(1)}, bf16[1,128,128]{2,1,0:T(8,128)(2,1)}, u32[]{:S(2)}) copy-start(bf16[1,128,128]{2,1,0:T(8,128)(2,1)} %param.8) | copy-start | bytes 98308
  0.6 2.6 %copy-start.1 = (bf16[1,128,2560]{2,1,0:T(8,128)(2,1)S(1)}, bf16[1,128,2560]{2,1,0:T(8,128)(2,1)}, u32[]{:S(2)}) copy-start(bf16[1,128,2560]{2,1,0:T(8,128)(2,1)} %param.7) | copy-start | bytes 1966084
  3.7 2.2 %copy-start.17 = (bf16[1,128,128]{2,1,0:T(8,128)(2,1)S(1)}, bf16[1,128,128]{2,1,0:T(8,128)(2,1)}, u32[]{:S(2)}) copy-start(bf16[1,128,128]{2,1,0:T(8,128)(2,1)} %param.9) | copy-start | bytes 98308
  4.9 1.3 %copy-start.6 = (bf16[1,128,2560]{1,2,0:T(8,128)(2,1)}, bf16[1,128,2560]{1,2,0:T(8,128)(2,1)S(1)}, u32[]{:S(2)}) copy-start(bf16[1,128,2560]{1,2,0:T(8,128)(2,1)S(1)} %get-tuple-element.210) | copy-start | bytes 1966084
  5.1 5.7 %collective-permute-start = (f32[1,17,40]{2,1,0:T(8,128)S(1)}, f32[1,17,40]{2,1,0:T(8,128)S(1)}, u32[]{:S(2)}, u32[]{:S(2)}) collective-permute-start(f32[1,17,40]{2,1,0:T(8,128)S(1)} %pad_maximum_fusion.2), channel_id=1, source_target_pairs={{0,1},{1,0},{2,3},{3,2},{4,5},{5,4},{6,7},{7,6},{8,9},{9,8},{10,11... | collective-permute-start | bytes 8168 | tf_op jit(solution)/shard_map/vmap()/ppermute | solution.py:69
  8.6 3.4 %collective-permute-start.1 = (f32[1,128,2560]{1,2,0:T(8,128)}, f32[1,128,2560]{1,2,0:T(8,128)}, u32[]{:S(2)}, u32[]{:S(2)}) collective-permute-start(f32[1,128,2560]{1,2,0:T(8,128)} %pad_maximum_fusion), channel_id=1, source_target_pairs={{0,1},{1,0},{2,3},{3,2},{4,5},{5,4},{6,7},{7,6},{8,9},{9,8},{10,11... | collective-permute-start | bytes 3932168 | tf_op jit(solution)/shard_map/vmap()/ppermute | solution.py:241
  15.2 20.2 %copy-start.2 = (f32[1,128,1280]{1,2,0:T(8,128)S(1)}, f32[1,128,1280]{1,2,0:T(8,128)}, u32[]{:S(2)}) copy-start(f32[1,128,1280]{1,2,0:T(8,128)} %get-tuple-element.202) | copy-start | bytes 1966084
  15.2 4.2 %collective-permute-start.2 = (f32[1,17,40]{2,1,0:T(8,128)S(1)}, f32[1,17,40]{2,1,0:T(8,128)S(1)}, u32[]{:S(2)}, u32[]{:S(2)}) collective-permute-start(f32[1,17,40]{2,1,0:T(8,128)S(1)} %fusion.87), channel_id=1, source_target_pairs={{0,2},{1,3},{2,0},{3,1},{4,6},{5,7},{6,4},{7,5},{8,10},{9,11},{10,... | collective-permute-start | bytes 8168 | tf_op jit(solution)/shard_map/vmap()/ppermute | solution.py:69
  16.8 13.3 %collective-permute-start.5 = (f32[1,128,1280]{1,2,0:T(8,128)}, f32[1,128,1280]{1,2,0:T(8,128)S(1)}, u32[]{:S(2)}, u32[]{:S(2)}) collective-permute-start(f32[1,128,1280]{1,2,0:T(8,128)} %get-tuple-element.206), channel_id=1, source_target_pairs={{0,2},{4,6},{8,10},{12,14},{3,1},{7,5},{11,9},{15,13},{16,18},{20,... | collective-permute-start | bytes 1966088 | tf_op jit(solution)/shard_map/vmap()/ppermute | solution.py:114
  18.1 17.3 %collective-permute-start.8 = (f32[1,128,1280]{1,2,0:T(8,128)}, f32[1,128,1280]{1,2,0:T(8,128)S(1)}, u32[]{:S(2)}, u32[]{:S(2)}) collective-permute-start(f32[1,128,1280]{1,2,0:T(8,128)} %get-tuple-element.202), channel_id=1, source_target_pairs={{15,13},{11,9},{7,5},{3,1},{12,14},{8,10},{4,6},{0,2},{31,29},{27,... | collective-permute-start | bytes 1966088 | tf_op jit(solution)/shard_map/vmap()/ppermute | solution.py:114
  19.5 2.6 %collective-permute-start.3 = (f32[1,17,40]{2,1,0:T(8,128)S(1)}, f32[1,17,40]{2,1,0:T(8,128)S(1)}, u32[]{:S(2)}, u32[]{:S(2)}) collective-permute-start(f32[1,17,40]{2,1,0:T(8,128)S(1)} %add.192), channel_id=1, source_target_pairs={{0,4},{1,5},{2,6},{3,7},{4,0},{5,1},{6,2},{7,3},{8,12},{9,13},{10,... | collective-permute-start | bytes 8168 | tf_op jit(solution)/shard_map/vmap()/ppermute | solution.py:69
  22.1 3.5 %collective-permute-start.4 = (f32[1,17,40]{2,1,0:T(8,128)S(1)}, f32[1,17,40]{2,1,0:T(8,128)S(1)}, u32[]{:S(2)}, u32[]{:S(2)}) collective-permute-start(f32[1,17,40]{2,1,0:T(8,128)S(1)} %add.193), channel_id=1, source_target_pairs={{0,8},{1,9},{2,10},{3,11},{4,12},{5,13},{6,14},{7,15},{8,0},{9,1},... | collective-permute-start | bytes 8168 | tf_op jit(solution)/shard_map/vmap()/ppermute | solution.py:69
  30.1 9.4 %copy-start.12 = (f32[1,128,1280]{1,2,0:T(8,128)}, f32[1,128,1280]{1,2,0:T(8,128)S(1)}, u32[]{:S(2)}) copy-start(f32[1,128,1280]{1,2,0:T(8,128)S(1)} %collective-permute-done.5) | copy-start | bytes 1966084
  32.5 7.0 %copy-start.3 = (f32[1,128,1280]{1,2,0:T(8,128)S(1)}, f32[1,128,1280]{1,2,0:T(8,128)}, u32[]{:S(2)}) copy-start(f32[1,128,1280]{1,2,0:T(8,128)} %get-tuple-element.206) | copy-start | bytes 1966084
  35.4 5.5 %copy-start.10 = (f32[1,128,1280]{1,2,0:T(8,128)}, f32[1,128,1280]{1,2,0:T(8,128)S(1)}, u32[]{:S(2)}) copy-start(f32[1,128,1280]{1,2,0:T(8,128)S(1)} %collective-permute-done.8) | copy-start | bytes 1966084
  36.7 11.9 %collective-permute-start.9 = (f32[1,128,1280]{1,2,0:T(8,128)}, f32[1,128,1280]{1,2,0:T(8,128)}, u32[]{:S(2)}, u32[]{:S(2)}) collective-permute-start(f32[1,128,1280]{1,2,0:T(8,128)} %add_select_fusion.2), channel_id=1, source_target_pairs={{13,9},{9,5},{5,1},{14,10},{10,6},{6,2},{29,25},{25,21},{21,17},{3... | collective-permute-start | bytes 1966088 | tf_op jit(solution)/shard_map/vmap()/ppermute | solution.py:114
  40.9 12.3 %collective-permute-start.6 = (f32[1,128,1280]{1,2,0:T(8,128)}, f32[1,128,1280]{1,2,0:T(8,128)S(1)}, u32[]{:S(2)}, u32[]{:S(2)}) collective-permute-start(f32[1,128,1280]{1,2,0:T(8,128)} %add_select_fusion.3), channel_id=1, source_target_pairs={{2,6},{6,10},{10,14},{1,5},{5,9},{9,13},{18,22},{22,26},{26,30},{1... | collective-permute-start | bytes 1966088 | tf_op jit(solution)/shard_map/vmap()/ppermute | solution.py:114
  44.0 3.3 %copy-start.15 = (bf16[1,128,2560]{1,2,0:T(8,128)(2,1)S(1)}, bf16[1,128,2560]{1,2,0:T(8,128)(2,1)}, u32[]{:S(2)}) copy-start(bf16[1,128,2560]{1,2,0:T(8,128)(2,1)} %copy.52) | copy-start | bytes 1966084
  50.1 10.6 %collective-permute-start.10 = (f32[1,128,1280]{1,2,0:T(8,128)S(1)}, f32[1,128,1280]{1,2,0:T(8,128)S(1)}, u32[]{:S(2)}, u32[]{:S(2)}) collective-permute-start(f32[1,128,1280]{1,2,0:T(8,128)S(1)} %multiply_add_fusion.3), channel_id=1, source_target_pairs={{13,5},{9,1},{14,6},{10,2},{29,21},{25,17},{30,22},{26,18}} | collective-permute-start | bytes 1966088 | tf_op jit(solution)/shard_map/vmap()/ppermute | solution.py:114
  53.2 8.8 %copy-start.13 = (f32[1,128,1280]{1,2,0:T(8,128)}, f32[1,128,1280]{1,2,0:T(8,128)S(1)}, u32[]{:S(2)}) copy-start(f32[1,128,1280]{1,2,0:T(8,128)S(1)} %collective-permute-done.6) | copy-start | bytes 1966084
  54.8 19.3 %collective-permute-start.7 = (f32[1,128,1280]{1,2,0:T(8,128)S(1)}, f32[1,128,1280]{1,2,0:T(8,128)S(1)}, u32[]{:S(2)}, u32[]{:S(2)}) collective-permute-start(f32[1,128,1280]{1,2,0:T(8,128)S(1)} %multiply_add_fusion.5), channel_id=1, source_target_pairs={{2,10},{6,14},{1,9},{5,13},{18,26},{22,30},{17,25},{21,29}} | collective-permute-start | bytes 1966088 | tf_op jit(solution)/shard_map/vmap()/ppermute | solution.py:114
  76.5 4.1 %copy-start.20 = (f32[1,40]{1,0:T(1,128)S(1)}, f32[1,40]{1,0:T(1,128)}, u32[]{:S(2)}) copy-start(f32[1,40]{1,0:T(1,128)} %constant_dynamic-slice_fusion.1) | copy-start | bytes 484
  76.5 4.2 %copy-start.21 = (f32[20]{0:T(128)S(1)}, f32[20]{0:T(128)}, u32[]{:S(2)}) copy-start(f32[20]{0:T(128)} %fusion.72) | copy-start | bytes 244
  76.5 5.2 %copy-start.23 = (f32[40]{0:T(128)S(1)}, f32[40]{0:T(128)}, u32[]{:S(2)}) copy-start(f32[40]{0:T(128)} %slice_bitcast_fusion.5) | copy-start | bytes 484
  76.5 10.1 %copy-start.4 = (f32[1,128,1280]{1,2,0:T(8,128)S(1)}, f32[1,128,1280]{1,2,0:T(8,128)}, u32[]{:S(2)}) copy-start(f32[1,128,1280]{1,2,0:T(8,128)} %get-tuple-element.207) | copy-start | bytes 1966084
  76.5 9.3 %collective-permute-start.11 = (f32[1,128,1280]{1,2,0:T(8,128)}, f32[1,128,1280]{1,2,0:T(8,128)S(1)}, u32[]{:S(2)}, u32[]{:S(2)}) collective-permute-start(f32[1,128,1280]{1,2,0:T(8,128)} %add_select_fusion.1), channel_id=1, source_target_pairs={{6,4},{10,8},{14,12},{1,3},{5,7},{9,11},{13,15},{22,20},{26,24},{3... | collective-permute-start | bytes 1966088 | tf_op jit(solution)/shard_map/vmap()/ppermute | solution.py:114
  79.0 9.4 %collective-permute-start.12 = (f32[1,128,1280]{1,2,0:T(8,128)}, f32[1,128,1280]{1,2,0:T(8,128)}, u32[]{:S(2)}, u32[]{:S(2)}) collective-permute-start(f32[1,128,1280]{1,2,0:T(8,128)} %add_select_fusion), channel_id=1, source_target_pairs={{9,11},{5,7},{1,3},{14,12},{10,8},{6,4},{2,0},{25,27},{21,23},{17,... | collective-permute-start | bytes 1966088 | tf_op jit(solution)/shard_map/vmap()/ppermute | solution.py:114
  81.6 17.8 %collective-permute-start.14 = (f32[40]{0:T(128)S(1)}, f32[40]{0:T(128)S(1)}, u32[]{:S(2)}, u32[]{:S(2)}) collective-permute-start(f32[40]{0:T(128)S(1)} %copy-done.23), channel_id=1, source_target_pairs={{0,16},{16,0},{1,17},{17,1},{2,18},{18,2},{3,19},{19,3},{4,20},{20... | collective-permute-start | bytes 488 | tf_op jit(solution)/shard_map/ppermute | solution.py:319
  86.6 1.8 %copy-start.5 = (f32[1,128,1280]{1,2,0:T(8,128)S(1)}, f32[1,128,1280]{1,2,0:T(8,128)}, u32[]{:S(2)}) copy-start(f32[1,128,1280]{1,2,0:T(8,128)} %get-tuple-element.203) | copy-start | bytes 1966084
  86.6 1.8 %copy-start.11 = (f32[1,128,1280]{1,2,0:T(8,128)S(1)}, f32[1,128,1280]{1,2,0:T(8,128)}, u32[]{:S(2)}) copy-start(f32[1,128,1280]{1,2,0:T(8,128)} %copy-done.10) | copy-start | bytes 1966084
  90.0 12.1 %collective-permute-start.13 = (f32[1,128,2560]{1,2,0:T(8,128)S(1)}, f32[1,128,2560]{1,2,0:T(8,128)S(1)}, u32[]{:S(2)}, u32[]{:S(2)}) collective-permute-start(f32[1,128,2560]{1,2,0:T(8,128)S(1)} %pad_maximum_fusion.1), channel_id=1, source_target_pairs={{0,1},{1,0},{2,3},{3,2},{4,5},{5,4},{6,7},{7,6},{8,9},{9,8},{10,11... | collective-permute-start | bytes 3932168 | tf_op jit(solution)/shard_map/vmap()/ppermute | solution.py:266
  102.4 1.3 %copy-start.14 = (f32[1,128,40,64]{1,3,2,0:T(8,128)S(1)}, f32[1,128,40,64]{1,3,2,0:T(8,128)}, u32[]{:S(2)}) copy-start(f32[1,128,40,64]{1,3,2,0:T(8,128)} %fusion) | copy-start | bytes 3932164
  (7 other events, 7.9 us)

commit v15 on v13

--- a/solution.py
+++ b/solution.py
@@ -236,9 +236,8 @@
 def carried_pair(tables, fwd_state, adj_state, position, count, head_width):
     ways = [Direction(tables, position, count, reverse, head_width) for reverse in (False, True)]
     states = [fwd_state, adj_state]
-    sent = jnp.concatenate([take_half(s, ~w.upper) for s, w in zip(states, ways)], -1)
-    got = lax.ppermute(sent, "ctx", [(i, i ^ 1) for i in range(count)])
-    got = [got[..., : got.shape[-1] // 2], got[..., got.shape[-1] // 2 :]]
+    swap = [(i, i ^ 1) for i in range(count)]
+    got = [lax.ppermute(take_half(s, ~w.upper), "ctx", swap) for s, w in zip(states, ways)]
     lows = []
     totals = []
     extend_totals(tables, count, 0, 1)
@@ -257,11 +256,8 @@
         lifted = way.gain(1, 2 * way.pair, 1) * pair_prefix + low_block
         lifted_parts.append(jnp.where(way.upper, pair_prefix, lifted))
         keep_parts.append(jnp.where(way.upper, lifted, pair_prefix))
-    got = lax.ppermute(jnp.concatenate(lifted_parts, -1), "ctx", [(i, i ^ 1) for i in range(count)])
     unit = jnp.exp(jnp.min(tables[-1]) * 0.0)
-    got = got * unit
-    half = got.shape[-1] // 2
-    others = [got[..., :half], got[..., half:]]
+    others = [lax.ppermute(part, "ctx", swap) * unit for part in lifted_parts]
     return (keep_parts, others, [way.upper for way in ways]), anchor, tables[-1]
 
 

time: 101 us -> 114 us (1.13)
  other arithmetic: 24 us -> 29.9 us
  waiting for transfers between devices: 18.7 us -> 22.2 us
  matrix products: 7.66 us -> 9.9 us
  starting transfers between devices: 33.2 us -> 34.8 us
    ppermute x8, waiting for transfers between devices: 16.1 us -> 20.8 us  [exchange(): lax.ppermute(p, 'ctx', pairs)]
    select_n x2, other arithmetic: 1.89 us -> 5.02 us  [up_combine(): return jnp.where(self.way.upper, kept_upper, kept_lower)]
    select_n x2, other arithmetic: 4.77 us -> 2.12 us  [down_send(): jnp.where(self.way.upper, self.pair_gain(0, pair, 1) * prefix + pair_tota...]
    unnamed x53 -> x37, local copies, waits for them, and re-layouts: 6.85 us -> 4.26 us
    squeeze x8, local copies, waits for them, and re-layouts: 0.35 us -> 2.19 us  [gain(): lax.dynamic_index_in_dim(self.pyramids[key], low_block // size, keepdims=...]
    select_n x15 -> x16, other arithmetic: 1.15 us -> 2.86 us  [take_half(): return jnp.where(upper, array[..., half:], array[..., :half])]
    concatenate x7, other arithmetic: 0.52 us -> 2.14 us  [gain(): lax.dynamic_index_in_dim(self.pyramids[key], low_block // size, keepdims=...]
    add x2, other arithmetic: 2.23 us -> 3.76 us  [shift_scans(): through[k] = before_gain * group_gain(scan, group) * got[k] + through[k]]
  transfers between devices with their start and end apart: 15 -> 17, of which waited for: 7 -> 6; matrix products, arithmetic and copies ran while one was open for 29% -> 39% of each run, Pallas kernels for 0% -> 0%
where the time goes in v15:
time: 114 us; the launch traced here: 113 us
  starting transfers between devices  34.8 us (31%)
  other arithmetic  29.9 us (26%)
  waiting for transfers between devices  22.2 us (19%)
  local copies, waits for them, and re-layouts  14.6 us (13%)
  matrix products  9.9 us (9%)
  between operations  1.86 us (2%)
    ppermute x8, waiting for transfers between devices, exchange(): lax.ppermute(p, 'ctx', pairs)  20.8 us
    ppermute x8, starting transfers between devices, exchange(): lax.ppermute(p, 'ctx', pairs)  18.1 us
    ppermute x2, starting transfers between devices, carried_pair(): others = [lax.ppermute(part, 'ctx', swap) * unit for part in lifted_parts]  8.5 us
    ppermute x4, starting transfers between devices, extend_totals(): lax.ppermute(tables[-1], 'ctx', xor_pairs(count, bit))  6.46 us
    select_n x2, other arithmetic, up_combine(): return jnp.where(self.way.upper, kept_upper, kept_lower)  5.02 us
    add x2, other arithmetic, carried_pair(): totals.append(way.gain(1, 2 * way.pair + 1, 1) * low_block + high_block)  4.37 us
    unnamed x37, local copies, waits for them, and re-layouts  4.26 us
    select_n x2, other arithmetic, carried_pair(): lifted_parts.append(jnp.where(way.upper, pair_prefix, lifted))  4.21 us
  transfers between devices with their start and end apart: 17, of which 6 were waited for; matrix products, arithmetic and copies ran while one was open for 39% of the time, Pallas kernels for 0%

profile of v15, /device:TPU:1, one launch (start us, length us, event | category | flops | bytes accessed | tf_op | source)
XLA Modules:
  0.0 113.4 jit_solution(17991492229489305556)
XLA Ops:
  1.8 1.4 %copy.45 = bf16[1,128,2560]{1,2,0:T(8,128)(2,1)S(1)} copy(bf16[1,128,2560]{2,1,0:T(8,128)(2,1)} %param.6) | data formatting | bytes 1310720 | tf_op args[0]
  7.0 1.4 %convolution_bitcast_fusion = f32[1,128,2560]{1,2,0:T(8,128)S(1)} fusion(bf16[1,128,2560]{1,2,0:T(8,128)(2,1)} %get-tuple-element.194, bf16[1,128,128]{2,1,0:T(8,128)(2,1)S(1)} %copy-done.13), kind=kOutput, calls=%fused_computation | convolution fusion | flops 83886080 | bytes 1998848 | tf_op jit(solution)/shard_map/vmap(in,iq->nq)/dot_general | solution.py:24
  12.8 2.2 %select_add_fusion.1 = f32[1,128,1280]{1,2,0:T(8,128)} fusion(f32[1,128,1280]{1,2,0:T(8,128)} %collective-permute-done.1, f32[1280]{0:T(1024)S(1)} %broadcast_in_dim.200, pred[]{:T(512)S(6)} %eq.27, f32[1,128,2560]{1,2,0:T(8,128)S(1)} %convolution_bitcast_fusion.1), kind=kLoop, calls=%fused_computation.54 | loop fusion | flops 819200 | bytes 2626561 | tf_op jit(solution)/shard_map/vmap()/add | solution.py:249
  15.0 2.2 %select_add_fusion = f32[1,128,1280]{1,2,0:T(8,128)} fusion(f32[1,128,1280]{1,2,0:T(8,128)} %collective-permute-done.3, f32[1280]{0:T(1024)S(1)} %broadcast_in_dim.208, pred[]{:T(512)S(6)} %eq.30, f32[1,128,2560]{1,2,0:T(8,128)S(1)} %convolution_bitcast_fusion), kind=kLoop, calls=%fused_computation.53 | loop fusion | flops 819200 | bytes 2626561 | tf_op jit(solution)/shard_map/vmap()/add | solution.py:249
  17.1 2.7 %collective-permute-start.4 = (f32[1,17,40]{2,1,0:T(8,128)S(1)}, f32[1,17,40]{2,1,0:T(8,128)S(1)}, u32[]{:S(2)}, u32[]{:S(2)}) collective-permute-start(f32[1,17,40]{2,1,0:T(8,128)S(1)} %fusion.95), channel_id=1, source_target_pairs={{0,2},{1,3},{2,0},{3,1},{4,6},{5,7},{6,4},{7,5},{8,10},{9,11},{10,... | collective-permute-start | bytes 8168 | tf_op jit(solution)/shard_map/vmap()/ppermute | solution.py:69
  20.2 1.3 %collective-permute-start.2 = (f32[1,128,1280]{1,2,0:T(8,128)}, f32[1,128,1280]{1,2,0:T(8,128)}, u32[]{:S(2)}, u32[]{:S(2)}) collective-permute-start(f32[1,128,1280]{1,2,0:T(8,128)} %select_add_fusion.1), channel_id=1, source_target_pairs={{0,2},{4,6},{8,10},{12,14},{3,1},{7,5},{11,9},{15,13},{16,18},{20,... | collective-permute-start | bytes 1966088 | tf_op jit(solution)/shard_map/vmap()/ppermute | solution.py:114
  21.5 1.3 %collective-permute-start.7 = (f32[1,128,1280]{1,2,0:T(8,128)}, f32[1,128,1280]{1,2,0:T(8,128)}, u32[]{:S(2)}, u32[]{:S(2)}) collective-permute-start(f32[1,128,1280]{1,2,0:T(8,128)} %select_add_fusion), channel_id=1, source_target_pairs={{15,13},{11,9},{7,5},{3,1},{12,14},{8,10},{4,6},{0,2},{31,29},{27,... | collective-permute-start | bytes 1966088 | tf_op jit(solution)/shard_map/vmap()/ppermute | solution.py:114
  22.8 1.4 %collective-permute-start.5 = (f32[1,17,40]{2,1,0:T(8,128)S(1)}, f32[1,17,40]{2,1,0:T(8,128)S(1)}, u32[]{:S(2)}, u32[]{:S(2)}) collective-permute-start(f32[1,17,40]{2,1,0:T(8,128)S(1)} %add.200), channel_id=1, source_target_pairs={{0,4},{1,5},{2,6},{3,7},{4,0},{5,1},{6,2},{7,3},{8,12},{9,13},{10,... | collective-permute-start | bytes 8168 | tf_op jit(solution)/shard_map/vmap()/ppermute | solution.py:69
  25.4 2.3 %collective-permute-start.6 = (f32[1,17,40]{2,1,0:T(8,128)S(1)}, f32[1,17,40]{2,1,0:T(8,128)S(1)}, u32[]{:S(2)}, u32[]{:S(2)}) collective-permute-start(f32[1,17,40]{2,1,0:T(8,128)S(1)} %add.202), channel_id=1, source_target_pairs={{0,8},{1,9},{2,10},{3,11},{4,12},{5,13},{6,14},{7,15},{8,0},{9,1},... | collective-permute-start | bytes 8168 | tf_op jit(solution)/shard_map/vmap()/ppermute | solution.py:69
  33.1 1.3 %collective-permute-start.16 = (f32[40]{0:T(128)}, f32[40]{0:T(128)}, u32[]{:S(2)}, u32[]{:S(2)}) collective-permute-start(f32[40]{0:T(128)} %slice_bitcast_fusion), channel_id=1, source_target_pairs={{0,16},{16,0},{1,17},{17,1},{2,18},{18,2},{3,19},{19,3},{4,20},{20... | collective-permute-start | bytes 488 | tf_op jit(solution)/shard_map/ppermute | solution.py:308
  37.8 1.3 %copy.51 = f32[1,128,2560]{1,2,0:T(8,128)} copy(bf16[1,128,2560]{2,1,0:T(8,128)(2,1)S(1)} %copy-done.1) | data formatting | bytes 1966080 | tf_op jit(solution)/shard_map/vmap()/convert_element_type | solution.py:53
  39.1 2.6 %add_select_fusion.1 = f32[1,128,1280]{1,2,0:T(8,128)} fusion(f32[1,128,1280]{1,2,0:T(8,128)} %select_add_fusion.1, f32[1,128,1280]{1,2,0:T(8,128)} %collective-permute-done.2, f32[1280]{0:T(1024)S(1)} %broadcast_in_dim.243, f32[1280]{0:T(1024)S(1)} %broadcast_in_dim.234, pred[]{:T(512)S(6)} %eq.27), kind=kLoop, calls=%fused_computation.43 | loop fusion | flops 819200 | bytes 1976321 | tf_op jit(solution)/shard_map/vmap(jit(_where))/select_n | solution.py:152
  41.7 4.0 %collective-permute-start.12 = (f32[1,128,1280]{1,2,0:T(8,128)}, f32[1,128,1280]{1,2,0:T(8,128)}, u32[]{:S(2)}, u32[]{:S(2)}) collective-permute-start(f32[1,128,1280]{1,2,0:T(8,128)} %add_select_fusion.1), channel_id=1, source_target_pairs={{2,6},{6,10},{10,14},{1,5},{5,9},{9,13},{18,22},{22,26},{26,30},{1... | collective-permute-start | bytes 1966088 | tf_op jit(solution)/shard_map/vmap()/ppermute | solution.py:114
  46.4 2.4 %add_select_fusion.3 = f32[1,128,1280]{1,2,0:T(8,128)} fusion(f32[1,128,1280]{1,2,0:T(8,128)S(1)} %copy-done.2, f32[1,128,1280]{1,2,0:T(8,128)} %collective-permute-done.7, f32[1280]{0:T(1024)S(1)} %broadcast_in_dim.222, f32[1280]{0:T(1024)S(1)} %broadcast_in_dim.213, pred[]{:T(512)S(6)} %eq.30), kind=kLoop, calls=%fused_computation.52 | loop fusion | flops 819200 | bytes 1976321 | tf_op jit(solution)/shard_map/vmap(jit(_where))/select_n | solution.py:152
  48.9 1.4 %collective-permute-start.8 = (f32[1,128,1280]{1,2,0:T(8,128)}, f32[1,128,1280]{1,2,0:T(8,128)S(1)}, u32[]{:S(2)}, u32[]{:S(2)}) collective-permute-start(f32[1,128,1280]{1,2,0:T(8,128)} %add_select_fusion.3), channel_id=1, source_target_pairs={{13,9},{9,5},{5,1},{14,10},{10,6},{6,2},{29,25},{25,21},{21,17},{3... | collective-permute-start | bytes 1966088 | tf_op jit(solution)/shard_map/vmap()/ppermute | solution.py:114
  50.4 2.3 %collective-permute-done.12 = f32[1,128,1280]{1,2,0:T(8,128)} collective-permute-done((f32[1,128,1280]{1,2,0:T(8,128)}, f32[1,128,1280]{1,2,0:T(8,128)}, u32[]{:S(2)}, u32[]{:S(2)}) %collective-permute-start.12) | collective-permute-done | bytes 655392 | tf_op jit(solution)/shard_map/vmap()/ppermute | solution.py:114
  52.7 2.4 %multiply_add_fusion.2 = f32[1,128,1280]{1,2,0:T(8,128)} fusion(f32[1,128,1280]{1,2,0:T(8,128)} %add_select_fusion.1, f32[1,128,1280]{1,2,0:T(8,128)} %collective-permute-done.12, f32[1280]{0:T(1024)S(1)} %broadcast_in_dim.240), kind=kLoop, calls=%fused_computation.42 | loop fusion | flops 327680 | bytes 1971200 | tf_op jit(solution)/shard_map/vmap()/add | solution.py:227
  55.1 5.8 %collective-permute-start.13 = (f32[1,128,1280]{1,2,0:T(8,128)}, f32[1,128,1280]{1,2,0:T(8,128)}, u32[]{:S(2)}, u32[]{:S(2)}) collective-permute-start(f32[1,128,1280]{1,2,0:T(8,128)} %multiply_add_fusion.2), channel_id=1, source_target_pairs={{2,10},{6,14},{1,9},{5,13},{18,26},{22,30},{17,25},{21,29}} | collective-permute-start | bytes 1966088 | tf_op jit(solution)/shard_map/vmap()/ppermute | solution.py:114
  60.9 2.2 %fusion = f32[1,128,40,64]{1,3,2,0:T(8,128)} fusion(bf16[128,40,64]{0,2,1:T(8,128)(2,1)S(1)} %bitcast.227, f32[1,128,40,64]{1,3,2,0:T(8,128)S(1)} %bitcast.226, f32[40,128]{1,0:T(8,128)S(1)} %copy-done.14, f32[128,128]{1,0:T(8,128)S(1)} %fusion.53, pred[128,128]{1,0:T(8,128)(4,1)S(1)} %copy-done.15, f32[40]{0:T(128)S(1)} %copy-done.16), kind=kOutput, calls=%fused_computation.13 | convolution fusion | flops 87818240 | bytes 3379360 | tf_op jit(solution)/shard_map/vmap(hij,ihp->jhp)/dot_general | solution.py:51
  63.0 2.2 %copy.52 = bf16[1,128,2560]{1,2,0:T(8,128)(2,1)} copy(bf16[1,128,2560]{2,1,0:T(8,128)(2,1)} %param.6) | data formatting | bytes 1310720 | tf_op jit(solution)/shard_map/optimization_barrier | solution.py:309
  65.3 1.4 %multiply_add_fusion.5 = f32[1,128,1280]{1,2,0:T(8,128)S(1)} fusion(f32[1,128,1280]{1,2,0:T(8,128)} %add_select_fusion.3, f32[1,128,1280]{1,2,0:T(8,128)S(1)} %collective-permute-done.8, f32[1280]{0:T(1024)S(1)} %broadcast_in_dim.219), kind=kLoop, calls=%fused_computation.51 | loop fusion | flops 327680 | bytes 1971200 | tf_op jit(solution)/shard_map/vmap()/add | solution.py:227
  66.7 1.4 %collective-permute-start.9 = (f32[1,128,1280]{1,2,0:T(8,128)S(1)}, f32[1,128,1280]{1,2,0:T(8,128)S(1)}, u32[]{:S(2)}, u32[]{:S(2)}) collective-permute-start(f32[1,128,1280]{1,2,0:T(8,128)S(1)} %multiply_add_fusion.5), channel_id=1, source_target_pairs={{13,5},{9,1},{14,6},{10,2},{29,21},{25,17},{30,22},{26,18}} | collective-permute-start | bytes 1966088 | tf_op jit(solution)/shard_map/vmap()/ppermute | solution.py:114
  68.2 1.7 %add_select_fusion = f32[1,128,1280]{1,2,0:T(8,128)S(1)} fusion(f32[1,128,1280]{1,2,0:T(8,128)S(1)} %copy-done.4, f32[1280]{0:T(1024)S(1)} %broadcast_in_dim.234, pred[]{:T(512)S(6)} %eq.27, f32[1,128,1280]{1,2,0:T(8,128)} %collective-permute-done.12, f32[1,128,1280]{1,2,0:T(8,128)} %collective-permute-done.13, f32[1280]{0:T(1024)S(1)} %broadcast_in_dim.237), kind=kLoop, calls=%fused_computation.40 | loop fusion | flops 819200 | bytes 2631681 | tf_op jit(solution)/shard_map/vmap(jit(_where))/select_n | solution.py:159
  69.9 1.3 %collective-permute-start.14 = (f32[1,128,1280]{1,2,0:T(8,128)S(1)}, f32[1,128,1280]{1,2,0:T(8,128)S(1)}, u32[]{:S(2)}, u32[]{:S(2)}) collective-permute-start(f32[1,128,1280]{1,2,0:T(8,128)S(1)} %add_select_fusion), channel_id=1, source_target_pairs={{6,4},{10,8},{14,12},{1,3},{5,7},{9,11},{13,15},{22,20},{26,24},{3... | collective-permute-start | bytes 1966088 | tf_op jit(solution)/shard_map/vmap()/ppermute | solution.py:114
  71.2 1.3 %convert_reduce_fusion = bf16[128,128]{1,0:T(8,128)(2,1)S(1)} fusion(f32[40,128]{1,0:T(8,128)S(1)} %copy-done.14, pred[128,128]{1,0:T(8,128)(4,1)S(1)} %copy-done.15, bf16[128,40,64]{0,2,1:T(8,128)(2,1)S(1)} %bitcast.228, bf16[128,40,64]{0,2,1:T(8,128)(2,1)S(1)} %bitcast.229), kind=kOutput, calls=%fused_computation.2 | convolution fusion | flops 88457216 | bytes 1380352 | tf_op jit(solution)/shard_map/vmap(ihp,jhp->hij)/dot_general | solution.py:45
  72.5 13.5 %collective-permute-done.9 = f32[1,128,1280]{1,2,0:T(8,128)S(1)} collective-permute-done((f32[1,128,1280]{1,2,0:T(8,128)S(1)}, f32[1,128,1280]{1,2,0:T(8,128)S(1)}, u32[]{:S(2)}, u32[]{:S(2)}) %collective-permute-start.9) | collective-permute-done | bytes 655392 | tf_op jit(solution)/shard_map/vmap()/ppermute | solution.py:114
  86.5 1.5 %collective-permute-start.10 = (f32[1,128,1280]{1,2,0:T(8,128)S(1)}, f32[1,128,1280]{1,2,0:T(8,128)S(1)}, u32[]{:S(2)}, u32[]{:S(2)}) collective-permute-start(f32[1,128,1280]{1,2,0:T(8,128)S(1)} %add_select_fusion.2), channel_id=1, source_target_pairs={{9,11},{5,7},{1,3},{14,12},{10,8},{6,4},{2,0},{25,27},{21,23},{17,... | collective-permute-start | bytes 1966088 | tf_op jit(solution)/shard_map/vmap()/ppermute | solution.py:114
  88.0 2.3 %fusion.17 = (f32[1,128,1280]{1,2,0:T(8,128)S(1)}, f32[1,128,1280]{1,2,0:T(8,128)S(1)}) fusion(f32[1280]{0:T(1024)S(1)} %broadcast_in_dim.231, pred[]{:T(512)S(6)} %eq.27, f32[1,128,1280]{1,2,0:T(8,128)} %collective-permute-done.1, f32[1,128,2560]{1,2,0:T(8,128)S(1)} %convolution_bitcast_fusion.1, f32[1,128,1280]{1,2,0:T(8,128)S(1)} %collective-permute-done.14, ...), kind=kLoop, calls=%fused_computation.38 | loop fusion | flops 1966080 | bytes 5913602 | tf_op jit(solution)/shard_map/vmap(jit(_where))/select_n | solution.py:257
  90.4 4.9 %collective-permute-done.10 = f32[1,128,1280]{1,2,0:T(8,128)S(1)} collective-permute-done((f32[1,128,1280]{1,2,0:T(8,128)S(1)}, f32[1,128,1280]{1,2,0:T(8,128)S(1)}, u32[]{:S(2)}, u32[]{:S(2)}) %collective-permute-start.10) | collective-permute-done | bytes 655392 | tf_op jit(solution)/shard_map/vmap()/ppermute | solution.py:114
  95.3 1.9 %fusion.18 = (f32[1,128,1280]{1,2,0:T(8,128)S(1)}, f32[1,128,1280]{1,2,0:T(8,128)S(1)}) fusion(f32[1280]{0:T(1024)S(1)} %broadcast_in_dim.228, pred[]{:T(512)S(6)} %eq.30, f32[1,128,1280]{1,2,0:T(8,128)} %collective-permute-done.3, f32[1,128,2560]{1,2,0:T(8,128)S(1)} %convolution_bitcast_fusion, f32[1,128,1280]{1,2,0:T(8,128)S(1)} %collective-permute-done.10, ...), kind=kLoop, calls=%fused_computation.47 | loop fusion | flops 1966080 | bytes 5913602 | tf_op jit(solution)/shard_map/vmap(jit(_where))/select_n | solution.py:257
  97.3 8.4 %collective-permute-start.11 = (f32[1,128,1280]{1,2,0:T(8,128)S(1)}, f32[1,128,1280]{1,2,0:T(8,128)S(1)}, u32[]{:S(2)}, u32[]{:S(2)}) collective-permute-start(f32[1,128,1280]{1,2,0:T(8,128)S(1)} %get-tuple-element.190), channel_id=1, source_target_pairs={{0,1},{1,0},{2,3},{3,2},{4,5},{5,4},{6,7},{7,6},{8,9},{9,8},{10,11... | collective-permute-start | bytes 1966088 | tf_op jit(solution)/shard_map/vmap()/ppermute | solution.py:260
  107.9 1.6 %fusion.22 = f32[128,128]{1,0:T(8,128)S(1)} fusion(f32[1,128,1280]{1,2,0:T(8,128)S(1)} %get-tuple-element.187, f32[1280]{0:T(1024)S(1)} %broadcast_in_dim.231, pred[]{:T(512)S(6)} %eq.27, f32[1,128,1280]{1,2,0:T(8,128)} %collective-permute-done.1, bf16[1,128,2560]{1,2,0:T(8,128)(2,1)S(1)} %copy-done.7, f32[1,128,2560]{1,2,0:T(8,128)S(1)} %convolution_bitcast_fusion.1), kind=kOutput, calls=%fused_computation.62 | convolution fusion | flops 43089920 | bytes 3348480 | tf_op jit(solution)/shard_map/vmap(iq,nq->in)/dot_general | solution.py:269
  (165 shorter events, 26.1 us)
Async XLA Ops:
  0.6 4.6 %copy-start = (bf16[1,128,128]{2,1,0:T(8,128)(2,1)S(1)}, bf16[1,128,128]{2,1,0:T(8,128)(2,1)}, u32[]{:S(2)}) copy-start(bf16[1,128,128]{2,1,0:T(8,128)(2,1)} %param.8) | copy-start | bytes 98308
  0.6 2.6 %copy-start.1 = (bf16[1,128,2560]{2,1,0:T(8,128)(2,1)S(1)}, bf16[1,128,2560]{2,1,0:T(8,128)(2,1)}, u32[]{:S(2)}) copy-start(bf16[1,128,2560]{2,1,0:T(8,128)(2,1)} %param.7) | copy-start | bytes 1966084
  4.8 1.7 %copy-start.5 = (bf16[1,128,2560]{1,2,0:T(8,128)(2,1)}, bf16[1,128,2560]{1,2,0:T(8,128)(2,1)S(1)}, u32[]{:S(2)}) copy-start(bf16[1,128,2560]{1,2,0:T(8,128)(2,1)S(1)} %get-tuple-element.192) | copy-start | bytes 1966084
  5.1 7.0 %collective-permute-start = (f32[1,17,40]{2,1,0:T(8,128)S(1)}, f32[1,17,40]{2,1,0:T(8,128)S(1)}, u32[]{:S(2)}, u32[]{:S(2)}) collective-permute-start(f32[1,17,40]{2,1,0:T(8,128)S(1)} %pad_maximum_fusion), channel_id=1, source_target_pairs={{0,1},{1,0},{2,3},{3,2},{4,5},{5,4},{6,7},{7,6},{8,9},{9,8},{10,11... | collective-permute-start | bytes 8168 | tf_op jit(solution)/shard_map/vmap()/ppermute | solution.py:69
  5.6 1.4 %copy-start.13 = (bf16[1,128,128]{2,1,0:T(8,128)(2,1)S(1)}, bf16[1,128,128]{2,1,0:T(8,128)(2,1)}, u32[]{:S(2)}) copy-start(bf16[1,128,128]{2,1,0:T(8,128)(2,1)} %param.9) | copy-start | bytes 98308
  6.5 6.3 %collective-permute-start.1 = (f32[1,128,1280]{1,2,0:T(8,128)}, f32[1,128,1280]{1,2,0:T(8,128)}, u32[]{:S(2)}, u32[]{:S(2)}) collective-permute-start(f32[1,128,1280]{1,2,0:T(8,128)} %slice_select_fusion.3), channel_id=1, source_target_pairs={{0,1},{1,0},{2,3},{3,2},{4,5},{5,4},{6,7},{7,6},{8,9},{9,8},{10,11... | collective-permute-start | bytes 1966088 | tf_op jit(solution)/shard_map/vmap()/ppermute | solution.py:240
  9.3 5.7 %collective-permute-start.3 = (f32[1,128,1280]{1,2,0:T(8,128)}, f32[1,128,1280]{1,2,0:T(8,128)}, u32[]{:S(2)}, u32[]{:S(2)}) collective-permute-start(f32[1,128,1280]{1,2,0:T(8,128)} %slice_select_fusion.1), channel_id=1, source_target_pairs={{0,1},{1,0},{2,3},{3,2},{4,5},{5,4},{6,7},{7,6},{8,9},{9,8},{10,11... | collective-permute-start | bytes 1966088 | tf_op jit(solution)/shard_map/vmap()/ppermute | solution.py:240
  17.1 5.6 %collective-permute-start.4 = (f32[1,17,40]{2,1,0:T(8,128)S(1)}, f32[1,17,40]{2,1,0:T(8,128)S(1)}, u32[]{:S(2)}, u32[]{:S(2)}) collective-permute-start(f32[1,17,40]{2,1,0:T(8,128)S(1)} %fusion.95), channel_id=1, source_target_pairs={{0,2},{1,3},{2,0},{3,1},{4,6},{5,7},{6,4},{7,5},{8,10},{9,11},{10,... | collective-permute-start | bytes 8168 | tf_op jit(solution)/shard_map/vmap()/ppermute | solution.py:69
  20.2 16.5 %collective-permute-start.2 = (f32[1,128,1280]{1,2,0:T(8,128)}, f32[1,128,1280]{1,2,0:T(8,128)}, u32[]{:S(2)}, u32[]{:S(2)}) collective-permute-start(f32[1,128,1280]{1,2,0:T(8,128)} %select_add_fusion.1), channel_id=1, source_target_pairs={{0,2},{4,6},{8,10},{12,14},{3,1},{7,5},{11,9},{15,13},{16,18},{20,... | collective-permute-start | bytes 1966088 | tf_op jit(solution)/shard_map/vmap()/ppermute | solution.py:114
  21.5 24.9 %collective-permute-start.7 = (f32[1,128,1280]{1,2,0:T(8,128)}, f32[1,128,1280]{1,2,0:T(8,128)}, u32[]{:S(2)}, u32[]{:S(2)}) collective-permute-start(f32[1,128,1280]{1,2,0:T(8,128)} %select_add_fusion), channel_id=1, source_target_pairs={{15,13},{11,9},{7,5},{3,1},{12,14},{8,10},{4,6},{0,2},{31,29},{27,... | collective-permute-start | bytes 1966088 | tf_op jit(solution)/shard_map/vmap()/ppermute | solution.py:114
  22.8 2.6 %collective-permute-start.5 = (f32[1,17,40]{2,1,0:T(8,128)S(1)}, f32[1,17,40]{2,1,0:T(8,128)S(1)}, u32[]{:S(2)}, u32[]{:S(2)}) collective-permute-start(f32[1,17,40]{2,1,0:T(8,128)S(1)} %add.200), channel_id=1, source_target_pairs={{0,4},{1,5},{2,6},{3,7},{4,0},{5,1},{6,2},{7,3},{8,12},{9,13},{10,... | collective-permute-start | bytes 8168 | tf_op jit(solution)/shard_map/vmap()/ppermute | solution.py:69
  25.4 3.4 %collective-permute-start.6 = (f32[1,17,40]{2,1,0:T(8,128)S(1)}, f32[1,17,40]{2,1,0:T(8,128)S(1)}, u32[]{:S(2)}, u32[]{:S(2)}) collective-permute-start(f32[1,17,40]{2,1,0:T(8,128)S(1)} %add.202), channel_id=1, source_target_pairs={{0,8},{1,9},{2,10},{3,11},{4,12},{5,13},{6,14},{7,15},{8,0},{9,1},... | collective-permute-start | bytes 8168 | tf_op jit(solution)/shard_map/vmap()/ppermute | solution.py:69
  33.1 2.5 %collective-permute-start.16 = (f32[40]{0:T(128)}, f32[40]{0:T(128)}, u32[]{:S(2)}, u32[]{:S(2)}) collective-permute-start(f32[40]{0:T(128)} %slice_bitcast_fusion), channel_id=1, source_target_pairs={{0,16},{16,0},{1,17},{17,1},{2,18},{18,2},{3,19},{19,3},{4,20},{20... | collective-permute-start | bytes 488 | tf_op jit(solution)/shard_map/ppermute | solution.py:308
  39.1 7.3 %copy-start.2 = (f32[1,128,1280]{1,2,0:T(8,128)S(1)}, f32[1,128,1280]{1,2,0:T(8,128)}, u32[]{:S(2)}) copy-start(f32[1,128,1280]{1,2,0:T(8,128)} %select_add_fusion) | copy-start | bytes 1966084
  41.7 11.0 %collective-permute-start.12 = (f32[1,128,1280]{1,2,0:T(8,128)}, f32[1,128,1280]{1,2,0:T(8,128)}, u32[]{:S(2)}, u32[]{:S(2)}) collective-permute-start(f32[1,128,1280]{1,2,0:T(8,128)} %add_select_fusion.1), channel_id=1, source_target_pairs={{2,6},{6,10},{10,14},{1,5},{5,9},{9,13},{18,22},{22,26},{26,30},{1... | collective-permute-start | bytes 1966088 | tf_op jit(solution)/shard_map/vmap()/ppermute | solution.py:114
  48.9 12.0 %copy-start.9 = (f32[1,128,2560]{1,2,0:T(8,128)S(1)}, f32[1,128,2560]{1,2,0:T(8,128)}, u32[]{:S(2)}) copy-start(f32[1,128,2560]{1,2,0:T(8,128)} %copy.51) | copy-start | bytes 3932164
  48.9 12.0 %copy-start.10 = (bf16[1,128,2560]{1,2,0:T(8,128)(2,1)S(1)}, bf16[1,128,2560]{1,2,0:T(8,128)(2,1)}, u32[]{:S(2)}) copy-start(bf16[1,128,2560]{1,2,0:T(8,128)(2,1)} %copy.48) | copy-start | bytes 1966084
  48.9 12.0 %copy-start.14 = (f32[40,128]{1,0:T(8,128)S(1)}, f32[40,128]{1,0:T(8,128)}, u32[]{:S(2)}) copy-start(f32[40,128]{1,0:T(8,128)} %copy.49) | copy-start | bytes 61444
  48.9 12.0 %copy-start.15 = (pred[128,128]{1,0:T(8,128)(4,1)S(1)}, pred[128,128]{1,0:T(8,128)(4,1)}, u32[]{:S(2)}) copy-start(pred[128,128]{1,0:T(8,128)(4,1)} %iota_compare_fusion) | copy-start | bytes 49156
  48.9 12.0 %copy-start.16 = (f32[40]{0:T(128)S(1)}, f32[40]{0:T(128)}, u32[]{:S(2)}) copy-start(f32[40]{0:T(128)} %param.11) | copy-start | bytes 484
  48.9 16.4 %collective-permute-start.8 = (f32[1,128,1280]{1,2,0:T(8,128)}, f32[1,128,1280]{1,2,0:T(8,128)S(1)}, u32[]{:S(2)}, u32[]{:S(2)}) collective-permute-start(f32[1,128,1280]{1,2,0:T(8,128)} %add_select_fusion.3), channel_id=1, source_target_pairs={{13,9},{9,5},{5,1},{14,10},{10,6},{6,2},{29,25},{25,21},{21,17},{3... | collective-permute-start | bytes 1966088 | tf_op jit(solution)/shard_map/vmap()/ppermute | solution.py:114
  55.1 13.0 %collective-permute-start.13 = (f32[1,128,1280]{1,2,0:T(8,128)}, f32[1,128,1280]{1,2,0:T(8,128)}, u32[]{:S(2)}, u32[]{:S(2)}) collective-permute-start(f32[1,128,1280]{1,2,0:T(8,128)} %multiply_add_fusion.2), channel_id=1, source_target_pairs={{2,10},{6,14},{1,9},{5,13},{18,26},{22,30},{17,25},{21,29}} | collective-permute-start | bytes 1966088 | tf_op jit(solution)/shard_map/vmap()/ppermute | solution.py:114
  65.3 2.9 %copy-start.4 = (f32[1,128,1280]{1,2,0:T(8,128)S(1)}, f32[1,128,1280]{1,2,0:T(8,128)}, u32[]{:S(2)}) copy-start(f32[1,128,1280]{1,2,0:T(8,128)} %select_add_fusion.1) | copy-start | bytes 1966084
  66.7 4.5 %copy-start.11 = (bf16[1,128,2560]{1,2,0:T(8,128)(2,1)S(1)}, bf16[1,128,2560]{1,2,0:T(8,128)(2,1)}, u32[]{:S(2)}) copy-start(bf16[1,128,2560]{1,2,0:T(8,128)(2,1)} %copy.48) | copy-start | bytes 1966084
  66.7 4.5 %copy-start.12 = (bf16[1,128,2560]{1,2,0:T(8,128)(2,1)S(1)}, bf16[1,128,2560]{1,2,0:T(8,128)(2,1)}, u32[]{:S(2)}) copy-start(bf16[1,128,2560]{1,2,0:T(8,128)(2,1)} %copy.52) | copy-start | bytes 1966084
  66.7 19.4 %collective-permute-start.9 = (f32[1,128,1280]{1,2,0:T(8,128)S(1)}, f32[1,128,1280]{1,2,0:T(8,128)S(1)}, u32[]{:S(2)}, u32[]{:S(2)}) collective-permute-start(f32[1,128,1280]{1,2,0:T(8,128)S(1)} %multiply_add_fusion.5), channel_id=1, source_target_pairs={{13,5},{9,1},{14,6},{10,2},{29,21},{25,17},{30,22},{26,18}} | collective-permute-start | bytes 1966088 | tf_op jit(solution)/shard_map/vmap()/ppermute | solution.py:114
  69.9 18.2 %collective-permute-start.14 = (f32[1,128,1280]{1,2,0:T(8,128)S(1)}, f32[1,128,1280]{1,2,0:T(8,128)S(1)}, u32[]{:S(2)}, u32[]{:S(2)}) collective-permute-start(f32[1,128,1280]{1,2,0:T(8,128)S(1)} %add_select_fusion), channel_id=1, source_target_pairs={{6,4},{10,8},{14,12},{1,3},{5,7},{9,11},{13,15},{22,20},{26,24},{3... | collective-permute-start | bytes 1966088 | tf_op jit(solution)/shard_map/vmap()/ppermute | solution.py:114
  71.2 14.9 %copy-start.3 = (f32[1,128,1280]{1,2,0:T(8,128)S(1)}, f32[1,128,1280]{1,2,0:T(8,128)}, u32[]{:S(2)}) copy-start(f32[1,128,1280]{1,2,0:T(8,128)} %select_add_fusion) | copy-start | bytes 1966084
  86.5 8.8 %collective-permute-start.10 = (f32[1,128,1280]{1,2,0:T(8,128)S(1)}, f32[1,128,1280]{1,2,0:T(8,128)S(1)}, u32[]{:S(2)}, u32[]{:S(2)}) collective-permute-start(f32[1,128,1280]{1,2,0:T(8,128)S(1)} %add_select_fusion.2), channel_id=1, source_target_pairs={{9,11},{5,7},{1,3},{14,12},{10,8},{6,4},{2,0},{25,27},{21,23},{17,... | collective-permute-start | bytes 1966088 | tf_op jit(solution)/shard_map/vmap()/ppermute | solution.py:114
  90.3 19.2 %collective-permute-start.15 = (f32[1,128,1280]{1,2,0:T(8,128)S(1)}, f32[1,128,1280]{1,2,0:T(8,128)S(1)}, u32[]{:S(2)}, u32[]{:S(2)}) collective-permute-start(f32[1,128,1280]{1,2,0:T(8,128)S(1)} %get-tuple-element.186), channel_id=1, source_target_pairs={{0,1},{1,0},{2,3},{3,2},{4,5},{5,4},{6,7},{7,6},{8,9},{9,8},{10,11... | collective-permute-start | bytes 1966088 | tf_op jit(solution)/shard_map/vmap()/ppermute | solution.py:260
  97.3 13.3 %collective-permute-start.11 = (f32[1,128,1280]{1,2,0:T(8,128)S(1)}, f32[1,128,1280]{1,2,0:T(8,128)S(1)}, u32[]{:S(2)}, u32[]{:S(2)}) collective-permute-start(f32[1,128,1280]{1,2,0:T(8,128)S(1)} %get-tuple-element.190), channel_id=1, source_target_pairs={{0,1},{1,0},{2,3},{3,2},{4,5},{5,4},{6,7},{7,6},{8,9},{9,8},{10,11... | collective-permute-start | bytes 1966088 | tf_op jit(solution)/shard_map/vmap()/ppermute | solution.py:260
  110.6 1.4 %copy-start.8 = (f32[1,128,40,64]{1,3,2,0:T(8,128)S(1)}, f32[1,128,40,64]{1,3,2,0:T(8,128)}, u32[]{:S(2)}) copy-start(f32[1,128,40,64]{1,3,2,0:T(8,128)} %fusion) | copy-start | bytes 3932164
  (2 other events, 2.2 us)

commit v16 on v13

--- a/solution.py
+++ b/solution.py
@@ -110,9 +110,15 @@
 
 
 def exchange(payloads, pair_lists):
-    return [
-        lax.ppermute(p, "ctx", pairs) if pairs else jnp.zeros_like(p) for p, pairs in zip(payloads, pair_lists)
-    ]
+    results = []
+    for p, pairs in zip(payloads, pair_lists):
+        got = jnp.zeros_like(p)
+        for parity in (0, 1):
+            part = [(s, t) for s, t in pairs if s % 2 == parity]
+            if part:
+                got = got + lax.ppermute(p, "ctx", part)
+        results.append(got)
+    return results
 
 
 class PairScan:

time: 101 us -> 111 us (1.099)
  starting transfers between devices: 33.2 us -> 39.3 us
  waiting for transfers between devices: 18.7 us -> 24.4 us
  other arithmetic: 24 us -> 19.6 us
  matrix products: 7.66 us -> 10.4 us
    ppermute x8 -> x16, starting transfers between devices: 17.7 us -> 23.8 us  [exchange(): got = got + lax.ppermute(p, 'ctx', part)]
    ppermute x8 -> x16, waiting for transfers between devices: 16.1 us -> 20.8 us  [exchange(): got = got + lax.ppermute(p, 'ctx', part)]
    select_n x2, other arithmetic: 4.77 us -> 0.83 us  [down_send(): jnp.where(self.way.upper, self.pair_gain(0, pair, 1) * prefix + pair_tota...]
    select_n x2, other arithmetic: 4.03 us -> 0.89 us  [carried_pair(): lifted_parts.append(jnp.where(way.upper, pair_prefix, lifted))]
    select_n x2, other arithmetic: 1.89 us -> 4.36 us  [up_combine(): return jnp.where(self.way.upper, kept_upper, kept_lower)]
    dot_general x1, matrix products: 2.18 us -> 3.7 us  [block_local_grads(): jnp.einsum('hij,ihp->jhp', value_weights, cot_three, preferred_element_ty...]
    dot_general x2, matrix products: 0.6 us -> 1.83 us  [rows_times(): jnp.einsum('iq,nq->in', take_half(coeffs, ~upper), other.astype(jnp.bfloa...]
    unnamed x53 -> x51, local copies, waits for them, and re-layouts: 6.85 us -> 7.2 us
  transfers between devices with their start and end apart: 15 -> 23, of which waited for: 7 -> 7; matrix products, arithmetic and copies ran while one was open for 29% -> 25% of each run, Pallas kernels for 0% -> 0%
where the time goes in v16:
time: 111 us; the launch traced here: 110 us
  starting transfers between devices  39.3 us (35%)
  waiting for transfers between devices  24.4 us (22%)
  other arithmetic  19.6 us (18%)
  local copies, waits for them, and re-layouts  14.1 us (13%)
  matrix products  10.4 us (9%)
  between operations  2.2 us (2%)
    ppermute x16, starting transfers between devices, exchange(): got = got + lax.ppermute(p, 'ctx', part)  23.8 us
    ppermute x16, waiting for transfers between devices, exchange(): got = got + lax.ppermute(p, 'ctx', part)  20.8 us
    ppermute x1, starting transfers between devices, carried_pair(): lax.ppermute(jnp.concatenate(lifted_parts, -1), 'ctx', [(i, i ^ 1) for i...  7.37 us
    unnamed x51, local copies, waits for them, and re-layouts  7.2 us
    ppermute x4, starting transfers between devices, extend_totals(): lax.ppermute(tables[-1], 'ctx', xor_pairs(count, bit))  6.4 us
    select_n x2, other arithmetic, up_combine(): return jnp.where(self.way.upper, kept_upper, kept_lower)  4.36 us
    dot_general x1, matrix products, block_local_grads(): jnp.einsum('hij,ihp->jhp', value_weights, cot_three, preferred_element_ty...  3.7 us
    add x1, other arithmetic, carried_pair(): totals.append(way.gain(1, 2 * way.pair + 1, 1) * low_block + high_block)  3.27 us
  transfers between devices with their start and end apart: 23, of which 7 were waited for; matrix products, arithmetic and copies ran while one was open for 25% of the time, Pallas kernels for 0%

profile of v16, /device:TPU:1, one launch (start us, length us, event | category | flops | bytes accessed | tf_op | source)
XLA Modules:
  0.0 109.9 jit_solution(5251551823281495598)
XLA Ops:
  1.8 1.4 %copy.45 = bf16[1,128,2560]{1,2,0:T(8,128)(2,1)S(1)} copy(bf16[1,128,2560]{2,1,0:T(8,128)(2,1)} %param.6) | data formatting | bytes 1310720 | tf_op args[0]
  3.7 1.2 %fusion.1 = (f32[2560]{0:T(1024)S(1)}, bf16[1,128,2560]{1,2,0:T(8,128)(2,1)}, bf16[1,128,2560]{1,2,0:T(8,128)(2,1)S(1)}) fusion(bf16[1,128,2560]{1,2,0:T(8,128)(2,1)S(1)} %copy.46, bf16[1,128,2560]{1,2,0:T(8,128)(2,1)S(1)} %copy.45, f32[128,40]{0,1:T(8,128)S(1)} %get-tuple-element.213, f32[128,40]{0,1:T(8,128)S(1)} %get-tuple-element.214), kind=kLoop, calls=%fused_computation.14 | loop fusion | flops 2618880 | bytes 2672640 | tf_op jit(solution)/shard_map/vmap()/reduce_sum | solution.py:25
  6.8 1.2 %pad_maximum_fusion = f32[1,128,2560]{1,2,0:T(8,128)} fusion(f32[1,128,1280]{1,2,0:T(8,128)S(1)} %get-tuple-element.243, f32[1,128,1280]{1,2,0:T(8,128)S(1)} %get-tuple-element.244), kind=kLoop, calls=%fused_computation.19 | loop fusion | flops 327680 | bytes 2621440 | tf_op jit(solution)/shard_map/vmap()/concatenate | solution.py:245
  9.8 1.6 %collective-permute-done.1 = f32[1,128,2560]{1,2,0:T(8,128)} collective-permute-done((f32[1,128,2560]{1,2,0:T(8,128)}, f32[1,128,2560]{1,2,0:T(8,128)}, u32[]{:S(2)}, u32[]{:S(2)}) %collective-permute-start.1) | collective-permute-done | bytes 1310752 | tf_op jit(solution)/shard_map/vmap()/ppermute | solution.py:246
  11.4 3.3 %select_add_fusion.1 = (f32[1,128,1280]{1,2,0:T(8,128)}, f32[1,128,1280]{1,2,0:T(8,128)}, f32[1,128,1280]{1,2,0:T(8,128)}, f32[1,128,1280]{1,2,0:T(8,128)}) fusion(f32[1,128,2560]{1,2,0:T(8,128)} %collective-permute-done.1, f32[1280]{0:T(1024)S(1)} %broadcast_in_dim.199, pred[]{:T(512)S(6)} %eq.27, f32[1,128,2560]{1,2,0:T(8,128)S(1)} %convolution_bitcast_fusion.1, ...), kind=kLoop, calls=%fused_computation.55 | loop fusion | flops 1638400 | bytes 6563842 | tf_op jit(solution)/shard_map/vmap()/add | solution.py:256
  14.7 2.6 %collective-permute-start.4 = (f32[1,17,40]{2,1,0:T(8,128)S(1)}, f32[1,17,40]{2,1,0:T(8,128)S(1)}, u32[]{:S(2)}, u32[]{:S(2)}) collective-permute-start(f32[1,17,40]{2,1,0:T(8,128)S(1)} %fusion.93), channel_id=1, source_target_pairs={{0,2},{1,3},{2,0},{3,1},{4,6},{5,7},{6,4},{7,5},{8,10},{9,11},{10,... | collective-permute-start | bytes 8168 | tf_op jit(solution)/shard_map/vmap()/ppermute | solution.py:69
  18.4 1.3 %collective-permute-start.3 = (f32[1,128,1280]{1,2,0:T(8,128)}, f32[1,128,1280]{1,2,0:T(8,128)}, u32[]{:S(2)}, u32[]{:S(2)}) collective-permute-start(f32[1,128,1280]{1,2,0:T(8,128)} %get-tuple-element.204), channel_id=1, source_target_pairs={{3,1},{7,5},{11,9},{15,13},{19,17},{23,21},{27,25},{31,29}} | collective-permute-start | bytes 1966088 | tf_op jit(solution)/shard_map/vmap()/ppermute | solution.py:119
  20.4 1.3 %collective-permute-start.14 = (f32[1,128,1280]{1,2,0:T(8,128)}, f32[1,128,1280]{1,2,0:T(8,128)}, u32[]{:S(2)}, u32[]{:S(2)}) collective-permute-start(f32[1,128,1280]{1,2,0:T(8,128)} %get-tuple-element.208), channel_id=1, source_target_pairs={{15,13},{11,9},{7,5},{3,1},{31,29},{27,25},{23,21},{19,17}} | collective-permute-start | bytes 1966088 | tf_op jit(solution)/shard_map/vmap()/ppermute | solution.py:119
  21.7 1.4 %collective-permute-start.5 = (f32[1,17,40]{2,1,0:T(8,128)S(1)}, f32[1,17,40]{2,1,0:T(8,128)S(1)}, u32[]{:S(2)}, u32[]{:S(2)}) collective-permute-start(f32[1,17,40]{2,1,0:T(8,128)S(1)} %add.225), channel_id=1, source_target_pairs={{0,4},{1,5},{2,6},{3,7},{4,0},{5,1},{6,2},{7,3},{8,12},{9,13},{10,... | collective-permute-start | bytes 8168 | tf_op jit(solution)/shard_map/vmap()/ppermute | solution.py:69
  24.3 2.3 %collective-permute-start.6 = (f32[1,17,40]{2,1,0:T(8,128)S(1)}, f32[1,17,40]{2,1,0:T(8,128)S(1)}, u32[]{:S(2)}, u32[]{:S(2)}) collective-permute-start(f32[1,17,40]{2,1,0:T(8,128)S(1)} %add.227), channel_id=1, source_target_pairs={{0,8},{1,9},{2,10},{3,11},{4,12},{5,13},{6,14},{7,15},{8,0},{9,1},... | collective-permute-start | bytes 8168 | tf_op jit(solution)/shard_map/vmap()/ppermute | solution.py:69
  30.1 1.2 %collective-permute-start.22 = (f32[40]{0:T(128)S(1)}, f32[40]{0:T(128)S(1)}, u32[]{:S(2)}, u32[]{:S(2)}) collective-permute-start(f32[40]{0:T(128)S(1)} %slice_bitcast_fusion.5), channel_id=1, source_target_pairs={{0,16},{16,0},{1,17},{17,1},{2,18},{18,2},{3,19},{19,3},{4,20},{20... | collective-permute-start | bytes 488 | tf_op jit(solution)/shard_map/ppermute | solution.py:318
  33.9 1.9 %add_select_fusion.3 = (f32[1,128,1280]{1,2,0:T(8,128)S(1)}, f32[1,128,1280]{1,2,0:T(8,128)S(1)}) fusion(f32[1,128,1280]{1,2,0:T(8,128)} %get-tuple-element.204, f32[1280]{0:T(1024)S(1)} %broadcast_in_dim.221, f32[1280]{0:T(1024)S(1)} %broadcast_in_dim.212, pred[]{:T(512)S(6)} %eq.27, f32[1,128,1280]{1,2,0:T(8,128)} %copy-done.18, ...), kind=kLoop, calls=%fused_computation.53 | loop fusion | flops 983040 | bytes 3287041 | tf_op jit(solution)/shard_map/vmap(jit(_where))/select_n | solution.py:158
  35.8 1.5 %collective-permute-start.7 = (f32[1,128,1280]{1,2,0:T(8,128)S(1)}, f32[1,128,1280]{1,2,0:T(8,128)}, u32[]{:S(2)}, u32[]{:S(2)}) collective-permute-start(f32[1,128,1280]{1,2,0:T(8,128)S(1)} %get-tuple-element.194), channel_id=1, source_target_pairs={{2,6},{6,10},{10,14},{18,22},{22,26},{26,30}} | collective-permute-start | bytes 1966088 | tf_op jit(solution)/shard_map/vmap()/ppermute | solution.py:119
  37.3 4.2 %collective-permute-start.8 = (f32[1,128,1280]{1,2,0:T(8,128)S(1)}, f32[1,128,1280]{1,2,0:T(8,128)}, u32[]{:S(2)}, u32[]{:S(2)}) collective-permute-start(f32[1,128,1280]{1,2,0:T(8,128)S(1)} %get-tuple-element.194), channel_id=1, source_target_pairs={{1,5},{5,9},{9,13},{17,21},{21,25},{25,29}} | collective-permute-start | bytes 1966088 | tf_op jit(solution)/shard_map/vmap()/ppermute | solution.py:119
  42.4 2.5 %add_select_fusion.1 = (f32[1,128,1280]{1,2,0:T(8,128)S(1)}, f32[1,128,1280]{1,2,0:T(8,128)}) fusion(f32[1,128,1280]{1,2,0:T(8,128)S(1)} %copy-done.4, f32[1280]{0:T(1024)S(1)} %broadcast_in_dim.239, f32[1280]{0:T(1024)S(1)} %broadcast_in_dim.230, pred[]{:T(512)S(6)} %eq.30, f32[1,128,1280]{1,2,0:T(8,128)} %copy-done.17, ...), kind=kLoop, calls=%fused_computation.46 | loop fusion | flops 983040 | bytes 3287041 | tf_op jit(solution)/shard_map/vmap(jit(_where))/select_n | solution.py:158
  44.9 1.5 %collective-permute-start.15 = (f32[1,128,1280]{1,2,0:T(8,128)S(1)}, f32[1,128,1280]{1,2,0:T(8,128)}, u32[]{:S(2)}, u32[]{:S(2)}) collective-permute-start(f32[1,128,1280]{1,2,0:T(8,128)S(1)} %get-tuple-element.202), channel_id=1, source_target_pairs={{14,10},{10,6},{6,2},{30,26},{26,22},{22,18}} | collective-permute-start | bytes 1966088 | tf_op jit(solution)/shard_map/vmap()/ppermute | solution.py:119
  46.5 1.3 %collective-permute-start.16 = (f32[1,128,1280]{1,2,0:T(8,128)S(1)}, f32[1,128,1280]{1,2,0:T(8,128)}, u32[]{:S(2)}, u32[]{:S(2)}) collective-permute-start(f32[1,128,1280]{1,2,0:T(8,128)S(1)} %get-tuple-element.202), channel_id=1, source_target_pairs={{13,9},{9,5},{5,1},{29,25},{25,21},{21,17}} | collective-permute-start | bytes 1966088 | tf_op jit(solution)/shard_map/vmap()/ppermute | solution.py:119
  47.7 1.1 %copy.48 = bf16[1,128,2560]{1,2,0:T(8,128)(2,1)} copy(bf16[1,128,2560]{2,1,0:T(8,128)(2,1)S(1)} %copy-done.1) | data formatting | bytes 1310720 | tf_op jit(solution)/shard_map/optimization_barrier | solution.py:319
  48.9 1.3 %copy.51 = f32[1,128,2560]{1,2,0:T(8,128)} copy(bf16[1,128,2560]{2,1,0:T(8,128)(2,1)S(1)} %copy-done.1) | data formatting | bytes 1966080 | tf_op jit(solution)/shard_map/vmap()/convert_element_type | solution.py:53
  51.0 3.7 %fusion = f32[1,128,40,64]{1,3,2,0:T(8,128)} fusion(bf16[128,40,64]{0,2,1:T(8,128)(2,1)} %bitcast.227, f32[1,128,40,64]{1,3,2,0:T(8,128)} %bitcast.226, f32[40,128]{1,0:T(8,128)} %copy.49, f32[128,128]{1,0:T(8,128)S(1)} %fusion.49, pred[128,128]{1,0:T(8,128)(4,1)S(1)} %iota_compare_fusion, f32[40]{0:T(128)S(1)} %copy-done.22), kind=kOutput, calls=%fused_computation.13 | convolution fusion | flops 87818240 | bytes 3379360 | tf_op jit(solution)/shard_map/vmap(hij,ihp->jhp)/dot_general | solution.py:51
  55.8 1.5 %multiply_add_fusion.5 = (f32[1,128,1280]{1,2,0:T(8,128)S(1)}, f32[1,128,1280]{1,2,0:T(8,128)S(1)}) fusion(f32[1,128,1280]{1,2,0:T(8,128)S(1)} %get-tuple-element.194, f32[1280]{0:T(1024)S(1)} %broadcast_in_dim.218, f32[1,128,1280]{1,2,0:T(8,128)} %collective-permute-done.7, f32[1,128,1280]{1,2,0:T(8,128)} %collective-permute-done.8), kind=kLoop, calls=%fused_computation.52 | loop fusion | flops 491520 | bytes 3281920 | tf_op jit(solution)/shard_map/vmap()/add | solution.py:233
  57.3 4.3 %collective-permute-start.10 = (f32[1,128,1280]{1,2,0:T(8,128)S(1)}, f32[1,128,1280]{1,2,0:T(8,128)S(1)}, u32[]{:S(2)}, u32[]{:S(2)}) collective-permute-start(f32[1,128,1280]{1,2,0:T(8,128)S(1)} %get-tuple-element.192), channel_id=1, source_target_pairs={{1,9},{5,13},{17,25},{21,29}} | collective-permute-start | bytes 1966088 | tf_op jit(solution)/shard_map/vmap()/ppermute | solution.py:119
  62.4 1.5 %multiply_add_fusion.2 = (f32[1,128,1280]{1,2,0:T(8,128)S(1)}, f32[1,128,1280]{1,2,0:T(8,128)S(1)}) fusion(f32[1,128,1280]{1,2,0:T(8,128)S(1)} %get-tuple-element.202, f32[1280]{0:T(1024)S(1)} %broadcast_in_dim.236, f32[1,128,1280]{1,2,0:T(8,128)} %collective-permute-done.15, f32[1,128,1280]{1,2,0:T(8,128)} %collective-permute-done.16), kind=kLoop, calls=%fused_computation.45 | loop fusion | flops 491520 | bytes 3281920 | tf_op jit(solution)/shard_map/vmap()/add | solution.py:233
  64.7 1.3 %collective-permute-start.18 = (f32[1,128,1280]{1,2,0:T(8,128)S(1)}, f32[1,128,1280]{1,2,0:T(8,128)S(1)}, u32[]{:S(2)}, u32[]{:S(2)}) collective-permute-start(f32[1,128,1280]{1,2,0:T(8,128)S(1)} %get-tuple-element.200), channel_id=1, source_target_pairs={{13,5},{9,1},{29,21},{25,17}} | collective-permute-start | bytes 1966088 | tf_op jit(solution)/shard_map/vmap()/ppermute | solution.py:119
  66.0 1.3 %convert_reduce_fusion = bf16[128,128]{1,0:T(8,128)(2,1)S(1)} fusion(f32[40,128]{1,0:T(8,128)S(1)} %copy-done.21, pred[128,128]{1,0:T(8,128)(4,1)S(1)} %iota_compare_fusion, bf16[128,40,64]{0,2,1:T(8,128)(2,1)S(1)} %bitcast.228, bf16[128,40,64]{0,2,1:T(8,128)(2,1)S(1)} %bitcast.229), kind=kOutput, calls=%fused_computation.2 | convolution fusion | flops 88457216 | bytes 1380352 | tf_op jit(solution)/shard_map/vmap(ihp,jhp->hij)/dot_general | solution.py:45
  67.3 1.9 %collective-permute-done.10 = f32[1,128,1280]{1,2,0:T(8,128)S(1)} collective-permute-done((f32[1,128,1280]{1,2,0:T(8,128)S(1)}, f32[1,128,1280]{1,2,0:T(8,128)S(1)}, u32[]{:S(2)}, u32[]{:S(2)}) %collective-permute-start.10) | collective-permute-done | bytes 655392 | tf_op jit(solution)/shard_map/vmap()/ppermute | solution.py:119
  70.4 1.3 %collective-permute-start.12 = (f32[1,128,1280]{1,2,0:T(8,128)S(1)}, f32[1,128,1280]{1,2,0:T(8,128)S(1)}, u32[]{:S(2)}, u32[]{:S(2)}) collective-permute-start(f32[1,128,1280]{1,2,0:T(8,128)S(1)} %get-tuple-element.190), channel_id=1, source_target_pairs={{1,3},{5,7},{9,11},{13,15},{17,19},{21,23},{25,27},{29,31}} | collective-permute-start | bytes 1966088 | tf_op jit(solution)/shard_map/vmap()/ppermute | solution.py:119
  71.7 12.2 %collective-permute-done.18 = f32[1,128,1280]{1,2,0:T(8,128)S(1)} collective-permute-done((f32[1,128,1280]{1,2,0:T(8,128)S(1)}, f32[1,128,1280]{1,2,0:T(8,128)S(1)}, u32[]{:S(2)}, u32[]{:S(2)}) %collective-permute-start.18) | collective-permute-done | bytes 655392 | tf_op jit(solution)/shard_map/vmap()/ppermute | solution.py:119
  85.0 1.5 %collective-permute-start.20 = (f32[1,128,1280]{1,2,0:T(8,128)S(1)}, f32[1,128,1280]{1,2,0:T(8,128)S(1)}, u32[]{:S(2)}, u32[]{:S(2)}) collective-permute-start(f32[1,128,1280]{1,2,0:T(8,128)S(1)} %get-tuple-element.198), channel_id=1, source_target_pairs={{9,11},{5,7},{1,3},{25,27},{21,23},{17,19}} | collective-permute-start | bytes 1966088 | tf_op jit(solution)/shard_map/vmap()/ppermute | solution.py:119
  87.2 6.7 %collective-permute-done.20 = f32[1,128,1280]{1,2,0:T(8,128)S(1)} collective-permute-done((f32[1,128,1280]{1,2,0:T(8,128)S(1)}, f32[1,128,1280]{1,2,0:T(8,128)S(1)}, u32[]{:S(2)}, u32[]{:S(2)}) %collective-permute-start.20) | collective-permute-done | bytes 655392 | tf_op jit(solution)/shard_map/vmap()/ppermute | solution.py:119
  94.4 7.4 %collective-permute-start.21 = (f32[1,128,2560]{1,2,0:T(8,128)S(1)}, f32[1,128,2560]{1,2,0:T(8,128)S(1)}, u32[]{:S(2)}, u32[]{:S(2)}) collective-permute-start(f32[1,128,2560]{1,2,0:T(8,128)S(1)} %pad_maximum_fusion.1), channel_id=1, source_target_pairs={{0,1},{1,0},{2,3},{3,2},{4,5},{5,4},{6,7},{7,6},{8,9},{9,8},{10,11... | collective-permute-start | bytes 3932168 | tf_op jit(solution)/shard_map/vmap()/ppermute | solution.py:266
  107.0 1.1 copy.53
  (192 shorter events, 27.9 us)
Async XLA Ops:
  0.6 5.1 %copy-start = (bf16[1,128,128]{2,1,0:T(8,128)(2,1)S(1)}, bf16[1,128,128]{2,1,0:T(8,128)(2,1)}, u32[]{:S(2)}) copy-start(bf16[1,128,128]{2,1,0:T(8,128)(2,1)} %param.8) | copy-start | bytes 98308
  5.1 4.0 %collective-permute-start = (f32[1,17,40]{2,1,0:T(8,128)S(1)}, f32[1,17,40]{2,1,0:T(8,128)S(1)}, u32[]{:S(2)}, u32[]{:S(2)}) collective-permute-start(f32[1,17,40]{2,1,0:T(8,128)S(1)} %pad_maximum_fusion.2), channel_id=1, source_target_pairs={{0,1},{1,0},{2,3},{3,2},{4,5},{5,4},{6,7},{7,6},{8,9},{9,8},{10,11... | collective-permute-start | bytes 8168 | tf_op jit(solution)/shard_map/vmap()/ppermute | solution.py:69
  8.0 3.5 %collective-permute-start.1 = (f32[1,128,2560]{1,2,0:T(8,128)}, f32[1,128,2560]{1,2,0:T(8,128)}, u32[]{:S(2)}, u32[]{:S(2)}) collective-permute-start(f32[1,128,2560]{1,2,0:T(8,128)} %pad_maximum_fusion), channel_id=1, source_target_pairs={{0,1},{1,0},{2,3},{3,2},{4,5},{5,4},{6,7},{7,6},{8,9},{9,8},{10,11... | collective-permute-start | bytes 3932168 | tf_op jit(solution)/shard_map/vmap()/ppermute | solution.py:246
  14.7 7.0 %collective-permute-start.4 = (f32[1,17,40]{2,1,0:T(8,128)S(1)}, f32[1,17,40]{2,1,0:T(8,128)S(1)}, u32[]{:S(2)}, u32[]{:S(2)}) collective-permute-start(f32[1,17,40]{2,1,0:T(8,128)S(1)} %fusion.93), channel_id=1, source_target_pairs={{0,2},{1,3},{2,0},{3,1},{4,6},{5,7},{6,4},{7,5},{8,10},{9,11},{10,... | collective-permute-start | bytes 8168 | tf_op jit(solution)/shard_map/vmap()/ppermute | solution.py:69
  17.7 15.4 %collective-permute-start.2 = (f32[1,128,1280]{1,2,0:T(8,128)}, f32[1,128,1280]{1,2,0:T(8,128)S(1)}, u32[]{:S(2)}, u32[]{:S(2)}) collective-permute-start(f32[1,128,1280]{1,2,0:T(8,128)} %get-tuple-element.204), channel_id=1, source_target_pairs={{0,2},{4,6},{8,10},{12,14},{16,18},{20,22},{24,26},{28,30}} | collective-permute-start | bytes 1966088 | tf_op jit(solution)/shard_map/vmap()/ppermute | solution.py:119
  18.4 15.6 %collective-permute-start.3 = (f32[1,128,1280]{1,2,0:T(8,128)}, f32[1,128,1280]{1,2,0:T(8,128)}, u32[]{:S(2)}, u32[]{:S(2)}) collective-permute-start(f32[1,128,1280]{1,2,0:T(8,128)} %get-tuple-element.204), channel_id=1, source_target_pairs={{3,1},{7,5},{11,9},{15,13},{19,17},{23,21},{27,25},{31,29}} | collective-permute-start | bytes 1966088 | tf_op jit(solution)/shard_map/vmap()/ppermute | solution.py:119
  19.7 21.9 %collective-permute-start.13 = (f32[1,128,1280]{1,2,0:T(8,128)}, f32[1,128,1280]{1,2,0:T(8,128)S(1)}, u32[]{:S(2)}, u32[]{:S(2)}) collective-permute-start(f32[1,128,1280]{1,2,0:T(8,128)} %get-tuple-element.208), channel_id=1, source_target_pairs={{12,14},{8,10},{4,6},{0,2},{28,30},{24,26},{20,22},{16,18}} | collective-permute-start | bytes 1966088 | tf_op jit(solution)/shard_map/vmap()/ppermute | solution.py:119
  20.4 22.1 %collective-permute-start.14 = (f32[1,128,1280]{1,2,0:T(8,128)}, f32[1,128,1280]{1,2,0:T(8,128)}, u32[]{:S(2)}, u32[]{:S(2)}) collective-permute-start(f32[1,128,1280]{1,2,0:T(8,128)} %get-tuple-element.208), channel_id=1, source_target_pairs={{15,13},{11,9},{7,5},{3,1},{31,29},{27,25},{23,21},{19,17}} | collective-permute-start | bytes 1966088 | tf_op jit(solution)/shard_map/vmap()/ppermute | solution.py:119
  21.7 2.6 %collective-permute-start.5 = (f32[1,17,40]{2,1,0:T(8,128)S(1)}, f32[1,17,40]{2,1,0:T(8,128)S(1)}, u32[]{:S(2)}, u32[]{:S(2)}) collective-permute-start(f32[1,17,40]{2,1,0:T(8,128)S(1)} %add.225), channel_id=1, source_target_pairs={{0,4},{1,5},{2,6},{3,7},{4,0},{5,1},{6,2},{7,3},{8,12},{9,13},{10,... | collective-permute-start | bytes 8168 | tf_op jit(solution)/shard_map/vmap()/ppermute | solution.py:69
  24.3 3.4 %collective-permute-start.6 = (f32[1,17,40]{2,1,0:T(8,128)S(1)}, f32[1,17,40]{2,1,0:T(8,128)S(1)}, u32[]{:S(2)}, u32[]{:S(2)}) collective-permute-start(f32[1,17,40]{2,1,0:T(8,128)S(1)} %add.227), channel_id=1, source_target_pairs={{0,8},{1,9},{2,10},{3,11},{4,12},{5,13},{6,14},{7,15},{8,0},{9,1},... | collective-permute-start | bytes 8168 | tf_op jit(solution)/shard_map/vmap()/ppermute | solution.py:69
  30.1 2.5 %collective-permute-start.22 = (f32[40]{0:T(128)S(1)}, f32[40]{0:T(128)S(1)}, u32[]{:S(2)}, u32[]{:S(2)}) collective-permute-start(f32[40]{0:T(128)S(1)} %slice_bitcast_fusion.5), channel_id=1, source_target_pairs={{0,16},{16,0},{1,17},{17,1},{2,18},{18,2},{3,19},{19,3},{4,20},{20... | collective-permute-start | bytes 488 | tf_op jit(solution)/shard_map/ppermute | solution.py:318
  33.1 9.3 %copy-start.4 = (f32[1,128,1280]{1,2,0:T(8,128)S(1)}, f32[1,128,1280]{1,2,0:T(8,128)}, u32[]{:S(2)}) copy-start(f32[1,128,1280]{1,2,0:T(8,128)} %get-tuple-element.208) | copy-start | bytes 1966084
  35.8 20.0 %collective-permute-start.7 = (f32[1,128,1280]{1,2,0:T(8,128)S(1)}, f32[1,128,1280]{1,2,0:T(8,128)}, u32[]{:S(2)}, u32[]{:S(2)}) collective-permute-start(f32[1,128,1280]{1,2,0:T(8,128)S(1)} %get-tuple-element.194), channel_id=1, source_target_pairs={{2,6},{6,10},{10,14},{18,22},{22,26},{26,30}} | collective-permute-start | bytes 1966088 | tf_op jit(solution)/shard_map/vmap()/ppermute | solution.py:119
  37.3 18.4 %collective-permute-start.8 = (f32[1,128,1280]{1,2,0:T(8,128)S(1)}, f32[1,128,1280]{1,2,0:T(8,128)}, u32[]{:S(2)}, u32[]{:S(2)}) collective-permute-start(f32[1,128,1280]{1,2,0:T(8,128)S(1)} %get-tuple-element.194), channel_id=1, source_target_pairs={{1,5},{5,9},{9,13},{17,21},{21,25},{25,29}} | collective-permute-start | bytes 1966088 | tf_op jit(solution)/shard_map/vmap()/ppermute | solution.py:119
  44.9 17.5 %collective-permute-start.15 = (f32[1,128,1280]{1,2,0:T(8,128)S(1)}, f32[1,128,1280]{1,2,0:T(8,128)}, u32[]{:S(2)}, u32[]{:S(2)}) collective-permute-start(f32[1,128,1280]{1,2,0:T(8,128)S(1)} %get-tuple-element.202), channel_id=1, source_target_pairs={{14,10},{10,6},{6,2},{30,26},{26,22},{22,18}} | collective-permute-start | bytes 1966088 | tf_op jit(solution)/shard_map/vmap()/ppermute | solution.py:119
  46.5 16.0 %collective-permute-start.16 = (f32[1,128,1280]{1,2,0:T(8,128)S(1)}, f32[1,128,1280]{1,2,0:T(8,128)}, u32[]{:S(2)}, u32[]{:S(2)}) collective-permute-start(f32[1,128,1280]{1,2,0:T(8,128)S(1)} %get-tuple-element.202), channel_id=1, source_target_pairs={{13,9},{9,5},{5,1},{29,25},{25,21},{21,17}} | collective-permute-start | bytes 1966088 | tf_op jit(solution)/shard_map/vmap()/ppermute | solution.py:119
  51.0 3.7 %copy-start.8 = (bf16[1,128,2560]{2,1,0:T(8,128)(2,1)S(1)}, bf16[1,128,2560]{2,1,0:T(8,128)(2,1)}, u32[]{:S(2)}) copy-start(bf16[1,128,2560]{2,1,0:T(8,128)(2,1)} %param.6) | copy-start | bytes 1966084
  57.3 8.7 %copy-start.15 = (bf16[1,128,2560]{1,2,0:T(8,128)(2,1)S(1)}, bf16[1,128,2560]{1,2,0:T(8,128)(2,1)}, u32[]{:S(2)}) copy-start(bf16[1,128,2560]{1,2,0:T(8,128)(2,1)} %copy.48) | copy-start | bytes 1966084
  57.3 8.7 %copy-start.16 = (bf16[1,128,2560]{1,2,0:T(8,128)(2,1)S(1)}, bf16[1,128,2560]{1,2,0:T(8,128)(2,1)}, u32[]{:S(2)}) copy-start(bf16[1,128,2560]{1,2,0:T(8,128)(2,1)} %copy.52) | copy-start | bytes 1966084
  57.3 8.7 %copy-start.21 = (f32[40,128]{1,0:T(8,128)S(1)}, f32[40,128]{1,0:T(8,128)}, u32[]{:S(2)}) copy-start(f32[40,128]{1,0:T(8,128)} %copy.49) | copy-start | bytes 61444
  57.3 11.9 %collective-permute-start.10 = (f32[1,128,1280]{1,2,0:T(8,128)S(1)}, f32[1,128,1280]{1,2,0:T(8,128)S(1)}, u32[]{:S(2)}, u32[]{:S(2)}) collective-permute-start(f32[1,128,1280]{1,2,0:T(8,128)S(1)} %get-tuple-element.192), channel_id=1, source_target_pairs={{1,9},{5,13},{17,25},{21,29}} | collective-permute-start | bytes 1966088 | tf_op jit(solution)/shard_map/vmap()/ppermute | solution.py:119
  61.7 7.5 %collective-permute-start.9 = (f32[1,128,1280]{1,2,0:T(8,128)S(1)}, f32[1,128,1280]{1,2,0:T(8,128)S(1)}, u32[]{:S(2)}, u32[]{:S(2)}) collective-permute-start(f32[1,128,1280]{1,2,0:T(8,128)S(1)} %get-tuple-element.192), channel_id=1, source_target_pairs={{2,10},{6,14},{18,26},{22,30}} | collective-permute-start | bytes 1966088 | tf_op jit(solution)/shard_map/vmap()/ppermute | solution.py:119
  64.0 7.7 %collective-permute-start.17 = (f32[1,128,1280]{1,2,0:T(8,128)S(1)}, f32[1,128,1280]{1,2,0:T(8,128)S(1)}, u32[]{:S(2)}, u32[]{:S(2)}) collective-permute-start(f32[1,128,1280]{1,2,0:T(8,128)S(1)} %get-tuple-element.200), channel_id=1, source_target_pairs={{14,6},{10,2},{30,22},{26,18}} | collective-permute-start | bytes 1966088 | tf_op jit(solution)/shard_map/vmap()/ppermute | solution.py:119
  64.7 19.3 %collective-permute-start.18 = (f32[1,128,1280]{1,2,0:T(8,128)S(1)}, f32[1,128,1280]{1,2,0:T(8,128)S(1)}, u32[]{:S(2)}, u32[]{:S(2)}) collective-permute-start(f32[1,128,1280]{1,2,0:T(8,128)S(1)} %get-tuple-element.200), channel_id=1, source_target_pairs={{13,5},{9,1},{29,21},{25,17}} | collective-permute-start | bytes 1966088 | tf_op jit(solution)/shard_map/vmap()/ppermute | solution.py:119
  66.0 3.2 %copy-start.5 = (f32[1,128,1280]{1,2,0:T(8,128)S(1)}, f32[1,128,1280]{1,2,0:T(8,128)}, u32[]{:S(2)}) copy-start(f32[1,128,1280]{1,2,0:T(8,128)} %get-tuple-element.204) | copy-start | bytes 1966084
  69.6 17.0 %collective-permute-start.11 = (f32[1,128,1280]{1,2,0:T(8,128)S(1)}, f32[1,128,1280]{1,2,0:T(8,128)S(1)}, u32[]{:S(2)}, u32[]{:S(2)}) collective-permute-start(f32[1,128,1280]{1,2,0:T(8,128)S(1)} %get-tuple-element.190), channel_id=1, source_target_pairs={{6,4},{10,8},{14,12},{22,20},{26,24},{30,28}} | collective-permute-start | bytes 1966088 | tf_op jit(solution)/shard_map/vmap()/ppermute | solution.py:119
  70.4 16.3 %collective-permute-start.12 = (f32[1,128,1280]{1,2,0:T(8,128)S(1)}, f32[1,128,1280]{1,2,0:T(8,128)S(1)}, u32[]{:S(2)}, u32[]{:S(2)}) collective-permute-start(f32[1,128,1280]{1,2,0:T(8,128)S(1)} %get-tuple-element.190), channel_id=1, source_target_pairs={{1,3},{5,7},{9,11},{13,15},{17,19},{21,23},{25,27},{29,31}} | collective-permute-start | bytes 1966088 | tf_op jit(solution)/shard_map/vmap()/ppermute | solution.py:119
  84.3 2.9 %collective-permute-start.19 = (f32[1,128,1280]{1,2,0:T(8,128)S(1)}, f32[1,128,1280]{1,2,0:T(8,128)S(1)}, u32[]{:S(2)}, u32[]{:S(2)}) collective-permute-start(f32[1,128,1280]{1,2,0:T(8,128)S(1)} %get-tuple-element.198), channel_id=1, source_target_pairs={{14,12},{10,8},{6,4},{2,0},{30,28},{26,24},{22,20},{18,16}} | collective-permute-start | bytes 1966088 | tf_op jit(solution)/shard_map/vmap()/ppermute | solution.py:119
  85.0 8.8 %collective-permute-start.20 = (f32[1,128,1280]{1,2,0:T(8,128)S(1)}, f32[1,128,1280]{1,2,0:T(8,128)S(1)}, u32[]{:S(2)}, u32[]{:S(2)}) collective-permute-start(f32[1,128,1280]{1,2,0:T(8,128)S(1)} %get-tuple-element.198), channel_id=1, source_target_pairs={{9,11},{5,7},{1,3},{25,27},{21,23},{17,19}} | collective-permute-start | bytes 1966088 | tf_op jit(solution)/shard_map/vmap()/ppermute | solution.py:119
  86.7 7.1 %copy-start.3 = (f32[1,128,1280]{1,2,0:T(8,128)S(1)}, f32[1,128,1280]{1,2,0:T(8,128)}, u32[]{:S(2)}) copy-start(f32[1,128,1280]{1,2,0:T(8,128)} %get-tuple-element.209) | copy-start | bytes 1966084
  86.7 7.1 %copy-start.9 = (f32[1,128,1280]{1,2,0:T(8,128)S(1)}, f32[1,128,1280]{1,2,0:T(8,128)}, u32[]{:S(2)}) copy-start(f32[1,128,1280]{1,2,0:T(8,128)} %get-tuple-element.203) | copy-start | bytes 1966084
  94.4 10.7 %collective-permute-start.21 = (f32[1,128,2560]{1,2,0:T(8,128)S(1)}, f32[1,128,2560]{1,2,0:T(8,128)S(1)}, u32[]{:S(2)}, u32[]{:S(2)}) collective-permute-start(f32[1,128,2560]{1,2,0:T(8,128)S(1)} %pad_maximum_fusion.1), channel_id=1, source_target_pairs={{0,1},{1,0},{2,3},{3,2},{4,5},{5,4},{6,7},{7,6},{8,9},{9,8},{10,11... | collective-permute-start | bytes 3932168 | tf_op jit(solution)/shard_map/vmap()/ppermute | solution.py:266
  (15 other events, 23.1 us)

commit v17 on v13

--- a/solution.py
+++ b/solution.py
@@ -3,6 +3,7 @@
 import jax
 import jax.numpy as jnp
 from jax import lax
+from jax.experimental.layout import Layout, with_layout_constraint
 from jax.sharding import PartitionSpec as P
 
 
@@ -317,6 +318,7 @@
     grad_values, grad_write, grad_read = jax.vmap(block_carried_grads)(
         write_coeffs, value_scale, decayed_vals, decayed_cot, carried, local_grads
     )
+    grad_values = with_layout_constraint(grad_values, Layout(major_to_minor=tuple(range(grad_values.ndim))))
     return (grad_values, grad_write, grad_read, grad_skip)
 
 

time: 101 us -> 102 us (level)
  local copies, waits for them, and re-layouts: 14.4 us -> 18.4 us
  starting transfers between devices: 33.2 us -> 31 us
  waiting for transfers between devices: 18.7 us -> 17.2 us
    broadcast_in_dim x28 -> x30, local copies, waits for them, and re-layouts: 2.63 us -> 5.97 us  [spread_heads(): return jnp.repeat(per_head, width, axis=-1)]
    reshape x0 -> x1, local copies, waits for them, and re-layouts: none -> 2.78 us  [block_local_grads(): grad_values.reshape(token_count, head_count * head_width)]
    ppermute x1, starting transfers between devices: 7.44 us -> 5.4 us  [carried_pair(): lax.ppermute(jnp.concatenate(lifted_parts, -1), 'ctx', [(i, i ^ 1) for i...]
    unnamed x53 -> x50, local copies, waits for them, and re-layouts: 6.85 us -> 5.06 us
    convert_element_type x1 -> x0, local copies, waits for them, and re-layouts: 1.32 us -> none  [block_local_grads(): cot_three.astype(jnp.float32)]
    ppermute x1, waiting for transfers between devices: 1.18 us -> 0.01 us  [carried_pair(): got = lax.ppermute(sent, 'ctx', [(i, i ^ 1) for i in range(count)])]
    optimization_barrier x2, local copies, waits for them, and re-layouts: 2.21 us -> 3.27 us  [local(): lax.optimization_barrier(((token_values, cotangent, write_coeffs, read_co...]
  transfers between devices with their start and end apart: 15 -> 15, of which waited for: 7 -> 6; matrix products, arithmetic and copies ran while one was open for 29% -> 34% of each run, Pallas kernels for 0% -> 0%
where the time goes in v17:
time: 102 us; the launch traced here: 100 us
  starting transfers between devices  31 us (30%)
  other arithmetic  23.8 us (23%)
  local copies, waits for them, and re-layouts  18.4 us (18%)
  waiting for transfers between devices  17.2 us (17%)
  matrix products  7.68 us (8%)
  between operations  1.92 us (2%)
    ppermute x8, starting transfers between devices, exchange(): lax.ppermute(p, 'ctx', pairs)  17.9 us
    ppermute x8, waiting for transfers between devices, exchange(): lax.ppermute(p, 'ctx', pairs)  15.8 us
    ppermute x4, starting transfers between devices, extend_totals(): lax.ppermute(tables[-1], 'ctx', xor_pairs(count, bit))  6.16 us
    broadcast_in_dim x30, local copies, waits for them, and re-layouts, spread_heads(): return jnp.repeat(per_head, width, axis=-1)  5.97 us
    ppermute x1, starting transfers between devices, carried_pair(): lax.ppermute(jnp.concatenate(lifted_parts, -1), 'ctx', [(i, i ^ 1) for i...  5.4 us
    unnamed x50, local copies, waits for them, and re-layouts  5.06 us
    select_n x2, other arithmetic, down_send(): jnp.where(self.way.upper, self.pair_gain(0, pair, 1) * prefix + pair_tota...  4.7 us
    select_n x2, other arithmetic, carried_pair(): lifted_parts.append(jnp.where(way.upper, pair_prefix, lifted))  4.03 us
  transfers between devices with their start and end apart: 15, of which 6 were waited for; matrix products, arithmetic and copies ran while one was open for 34% of the time, Pallas kernels for 0%

profile of v17, /device:TPU:1, one launch (start us, length us, event | category | flops | bytes accessed | tf_op | source)
XLA Modules:
  0.0 100.0 jit_solution(1953996202131814155)
XLA Ops:
  1.8 1.4 %copy.57 = bf16[1,128,2560]{1,2,0:T(8,128)(2,1)S(1)} copy(bf16[1,128,2560]{2,1,0:T(8,128)(2,1)} %param.6) | data formatting | bytes 1310720 | tf_op args[0]
  5.4 1.2 %pad_maximum_fusion = f32[1,128,2560]{1,2,0:T(8,128)} fusion(f32[1,128,1280]{1,2,0:T(8,128)S(1)} %get-tuple-element.215, f32[1,128,1280]{1,2,0:T(8,128)S(1)} %get-tuple-element.216), kind=kLoop, calls=%fused_computation.16 | loop fusion | flops 327680 | bytes 2621440 | tf_op jit(solution)/shard_map/vmap()/concatenate | solution.py:240
  8.1 1.2 %broadcast_in_dim.200 = f32[128,40,64]{0,2,1:T(8,128)} broadcast(f32[128,40]{0,1:T(8,128)S(1)} %get-tuple-element.185), dimensions={0,1} | broadcast | bytes 1331200 | tf_op jit(solution)/shard_map/vmap()/broadcast_in_dim | solution.py:11
  9.3 2.8 %copy.68 = f32[1,128,2560]{2,1,0:T(8,128)} copy(f32[1,128,2560]{1,2,0:T(8,128)} %bitcast.219) | data formatting | bytes 2621440 | tf_op jit(solution)/shard_map/vmap()/broadcast_in_dim | solution.py:11
  12.7 3.0 %select_add_fusion = (f32[1,128,1280]{1,2,0:T(8,128)}, f32[1,128,1280]{1,2,0:T(8,128)}, f32[1,128,1280]{1,2,0:T(8,128)}, f32[1,128,1280]{1,2,0:T(8,128)S(1)}) fusion(f32[1,128,2560]{1,2,0:T(8,128)} %collective-permute-done.1, f32[1280]{0:T(1024)S(1)} %broadcast_in_dim.209, pred[]{:T(512)S(6)} %eq.30, f32[1,128,2560]{1,2,0:T(8,128)S(1)} %convolution_bitcast_fusion, ...), kind=kLoop, calls=%fused_computation.55 | loop fusion | flops 1638400 | bytes 6563842 | tf_op jit(solution)/shard_map/vmap()/add | solution.py:251
  15.7 2.4 %collective-permute-start.3 = (f32[1,17,40]{2,1,0:T(8,128)S(1)}, f32[1,17,40]{2,1,0:T(8,128)S(1)}, u32[]{:S(2)}, u32[]{:S(2)}) collective-permute-start(f32[1,17,40]{2,1,0:T(8,128)S(1)} %fusion.90), channel_id=1, source_target_pairs={{0,2},{1,3},{2,0},{3,1},{4,6},{5,7},{6,4},{7,5},{8,10},{9,11},{10,... | collective-permute-start | bytes 8168 | tf_op jit(solution)/shard_map/vmap()/ppermute | solution.py:70
  18.5 1.3 %collective-permute-start.2 = (f32[1,128,1280]{1,2,0:T(8,128)}, f32[1,128,1280]{1,2,0:T(8,128)S(1)}, u32[]{:S(2)}, u32[]{:S(2)}) collective-permute-start(f32[1,128,1280]{1,2,0:T(8,128)} %get-tuple-element.180), channel_id=1, source_target_pairs={{0,2},{4,6},{8,10},{12,14},{3,1},{7,5},{11,9},{15,13},{16,18},{20,... | collective-permute-start | bytes 1966088 | tf_op jit(solution)/shard_map/vmap()/ppermute | solution.py:115
  19.8 1.3 %collective-permute-start.9 = (f32[1,128,1280]{1,2,0:T(8,128)}, f32[1,128,1280]{1,2,0:T(8,128)S(1)}, u32[]{:S(2)}, u32[]{:S(2)}) collective-permute-start(f32[1,128,1280]{1,2,0:T(8,128)} %get-tuple-element.176), channel_id=1, source_target_pairs={{15,13},{11,9},{7,5},{3,1},{12,14},{8,10},{4,6},{0,2},{31,29},{27,... | collective-permute-start | bytes 1966088 | tf_op jit(solution)/shard_map/vmap()/ppermute | solution.py:115
  21.1 1.4 %collective-permute-start.4 = (f32[1,17,40]{2,1,0:T(8,128)S(1)}, f32[1,17,40]{2,1,0:T(8,128)S(1)}, u32[]{:S(2)}, u32[]{:S(2)}) collective-permute-start(f32[1,17,40]{2,1,0:T(8,128)S(1)} %add.200), channel_id=1, source_target_pairs={{0,4},{1,5},{2,6},{3,7},{4,0},{5,1},{6,2},{7,3},{8,12},{9,13},{10,... | collective-permute-start | bytes 8168 | tf_op jit(solution)/shard_map/vmap()/ppermute | solution.py:70
  23.7 2.3 %collective-permute-start.5 = (f32[1,17,40]{2,1,0:T(8,128)S(1)}, f32[1,17,40]{2,1,0:T(8,128)S(1)}, u32[]{:S(2)}, u32[]{:S(2)}) collective-permute-start(f32[1,17,40]{2,1,0:T(8,128)S(1)} %add.202), channel_id=1, source_target_pairs={{0,8},{1,9},{2,10},{3,11},{4,12},{5,13},{6,14},{7,15},{8,0},{9,1},... | collective-permute-start | bytes 8168 | tf_op jit(solution)/shard_map/vmap()/ppermute | solution.py:70
  27.8 1.2 %collective-permute-start.14 = (f32[40]{0:T(128)S(1)}, f32[40]{0:T(128)S(1)}, u32[]{:S(2)}, u32[]{:S(2)}) collective-permute-start(f32[40]{0:T(128)S(1)} %slice_bitcast_fusion.5), channel_id=1, source_target_pairs={{0,16},{16,0},{1,17},{17,1},{2,18},{18,2},{3,19},{19,3},{4,20},{20... | collective-permute-start | bytes 488 | tf_op jit(solution)/shard_map/ppermute | solution.py:313
  32.2 1.5 %add_select_fusion.3 = f32[1,128,1280]{1,2,0:T(8,128)S(1)} fusion(f32[1,128,1280]{1,2,0:T(8,128)} %get-tuple-element.180, f32[1,128,1280]{1,2,0:T(8,128)S(1)} %collective-permute-done.2, f32[1280]{0:T(1024)S(1)} %broadcast_in_dim.221, f32[1280]{0:T(1024)S(1)} %broadcast_in_dim.212, pred[]{:T(512)S(6)} %eq.27), kind=kLoop, calls=%fused_computation.54 | loop fusion | flops 819200 | bytes 1976321 | tf_op jit(solution)/shard_map/vmap(jit(_where))/select_n | solution.py:153
  33.7 3.3 %collective-permute-start.6 = (f32[1,128,1280]{1,2,0:T(8,128)S(1)}, f32[1,128,1280]{1,2,0:T(8,128)S(1)}, u32[]{:S(2)}, u32[]{:S(2)}) collective-permute-start(f32[1,128,1280]{1,2,0:T(8,128)S(1)} %add_select_fusion.3), channel_id=1, source_target_pairs={{2,6},{6,10},{10,14},{1,5},{5,9},{9,13},{18,22},{22,26},{26,30},{1... | collective-permute-start | bytes 1966088 | tf_op jit(solution)/shard_map/vmap()/ppermute | solution.py:115
  38.3 1.3 %collective-permute-start.10 = (f32[1,128,1280]{1,2,0:T(8,128)S(1)}, f32[1,128,1280]{1,2,0:T(8,128)S(1)}, u32[]{:S(2)}, u32[]{:S(2)}) collective-permute-start(f32[1,128,1280]{1,2,0:T(8,128)S(1)} %add_select_fusion.1), channel_id=1, source_target_pairs={{13,9},{9,5},{5,1},{14,10},{10,6},{6,2},{29,25},{25,21},{21,17},{3... | collective-permute-start | bytes 1966088 | tf_op jit(solution)/shard_map/vmap()/ppermute | solution.py:115
  40.1 4.3 %collective-permute-done.6 = f32[1,128,1280]{1,2,0:T(8,128)S(1)} collective-permute-done((f32[1,128,1280]{1,2,0:T(8,128)S(1)}, f32[1,128,1280]{1,2,0:T(8,128)S(1)}, u32[]{:S(2)}, u32[]{:S(2)}) %collective-permute-start.6) | collective-permute-done | bytes 655392 | tf_op jit(solution)/shard_map/vmap()/ppermute | solution.py:115
  44.4 1.1 %multiply_add_fusion.5 = f32[1,128,1280]{1,2,0:T(8,128)} fusion(f32[1,128,1280]{1,2,0:T(8,128)S(1)} %add_select_fusion.3, f32[1,128,1280]{1,2,0:T(8,128)S(1)} %collective-permute-done.6, f32[1280]{0:T(1024)S(1)} %broadcast_in_dim.218), kind=kLoop, calls=%fused_computation.53 | loop fusion | flops 327680 | bytes 1971200 | tf_op jit(solution)/shard_map/vmap()/add | solution.py:228
  45.5 5.8 %collective-permute-start.7 = (f32[1,128,1280]{1,2,0:T(8,128)}, f32[1,128,1280]{1,2,0:T(8,128)}, u32[]{:S(2)}, u32[]{:S(2)}) collective-permute-start(f32[1,128,1280]{1,2,0:T(8,128)} %multiply_add_fusion.5), channel_id=1, source_target_pairs={{2,10},{6,14},{1,9},{5,13},{18,26},{22,30},{17,25},{21,29}} | collective-permute-start | bytes 1966088 | tf_op jit(solution)/shard_map/vmap()/ppermute | solution.py:115
  52.4 1.3 %collective-permute-start.11 = (f32[1,128,1280]{1,2,0:T(8,128)}, f32[1,128,1280]{1,2,0:T(8,128)}, u32[]{:S(2)}, u32[]{:S(2)}) collective-permute-start(f32[1,128,1280]{1,2,0:T(8,128)} %multiply_add_fusion.2), channel_id=1, source_target_pairs={{13,5},{9,1},{14,6},{10,2},{29,21},{25,17},{30,22},{26,18}} | collective-permute-start | bytes 1966088 | tf_op jit(solution)/shard_map/vmap()/ppermute | solution.py:115
  53.8 2.2 %copy.60 = bf16[1,128,2560]{1,2,0:T(8,128)(2,1)} copy(bf16[1,128,2560]{2,1,0:T(8,128)(2,1)} %param.7) | data formatting | bytes 1310720 | tf_op jit(solution)/shard_map/optimization_barrier | solution.py:314
  56.7 1.6 %collective-permute-done.7 = f32[1,128,1280]{1,2,0:T(8,128)} collective-permute-done((f32[1,128,1280]{1,2,0:T(8,128)}, f32[1,128,1280]{1,2,0:T(8,128)}, u32[]{:S(2)}, u32[]{:S(2)}) %collective-permute-start.7) | collective-permute-done | bytes 655392 | tf_op jit(solution)/shard_map/vmap()/ppermute | solution.py:115
  58.3 2.3 %add_select_fusion.2 = f32[1,128,1280]{1,2,0:T(8,128)} fusion(f32[1,128,1280]{1,2,0:T(8,128)S(1)} %copy-done.3, f32[1280]{0:T(1024)S(1)} %broadcast_in_dim.212, pred[]{:T(512)S(6)} %eq.27, f32[1,128,1280]{1,2,0:T(8,128)S(1)} %collective-permute-done.6, f32[1,128,1280]{1,2,0:T(8,128)} %collective-permute-done.7, f32[1280]{0:T(1024)S(1)} %broadcast_in_dim.215), kind=kLoop, calls=%fused_computation.51 | loop fusion | flops 819200 | bytes 2631681 | tf_op jit(solution)/shard_map/vmap(jit(_where))/select_n | solution.py:160
  60.7 1.5 %collective-permute-start.8 = (f32[1,128,1280]{1,2,0:T(8,128)}, f32[1,128,1280]{1,2,0:T(8,128)S(1)}, u32[]{:S(2)}, u32[]{:S(2)}) collective-permute-start(f32[1,128,1280]{1,2,0:T(8,128)} %add_select_fusion.2), channel_id=1, source_target_pairs={{6,4},{10,8},{14,12},{1,3},{5,7},{9,11},{13,15},{22,20},{26,24},{3... | collective-permute-start | bytes 1966088 | tf_op jit(solution)/shard_map/vmap()/ppermute | solution.py:115
  62.1 9.8 %collective-permute-done.11 = f32[1,128,1280]{1,2,0:T(8,128)} collective-permute-done((f32[1,128,1280]{1,2,0:T(8,128)}, f32[1,128,1280]{1,2,0:T(8,128)}, u32[]{:S(2)}, u32[]{:S(2)}) %collective-permute-start.11) | collective-permute-done | bytes 655392 | tf_op jit(solution)/shard_map/vmap()/ppermute | solution.py:115
  72.0 2.4 %add_select_fusion = f32[1,128,1280]{1,2,0:T(8,128)} fusion(f32[1,128,1280]{1,2,0:T(8,128)S(1)} %copy-done.2, f32[1280]{0:T(1024)S(1)} %broadcast_in_dim.230, pred[]{:T(512)S(6)} %eq.30, f32[1,128,1280]{1,2,0:T(8,128)S(1)} %collective-permute-done.10, f32[1,128,1280]{1,2,0:T(8,128)} %collective-permute-done.11, f32[1280]{0:T(1024)S(1)} %broadcast_in_dim.233), kind=kLoop, calls=%fused_computation.44 | loop fusion | flops 819200 | bytes 2631681 | tf_op jit(solution)/shard_map/vmap(jit(_where))/select_n | solution.py:160
  74.3 2.2 %collective-permute-start.12 = (f32[1,128,1280]{1,2,0:T(8,128)}, f32[1,128,1280]{1,2,0:T(8,128)}, u32[]{:S(2)}, u32[]{:S(2)}) collective-permute-start(f32[1,128,1280]{1,2,0:T(8,128)} %add_select_fusion), channel_id=1, source_target_pairs={{9,11},{5,7},{1,3},{14,12},{10,8},{6,4},{2,0},{25,27},{21,23},{17,... | collective-permute-start | bytes 1966088 | tf_op jit(solution)/shard_map/vmap()/ppermute | solution.py:115
  76.6 2.2 %fusion = f32[1,128,40,64]{1,3,2,0:T(8,128)} fusion(bf16[128,40,64]{0,2,1:T(8,128)(2,1)S(1)} %bitcast.221, bf16[1,128,40,64]{1,3,2,0:T(8,128)(2,1)S(1)} %bitcast.222, f32[40,128]{1,0:T(8,128)S(1)} %copy-done.20, f32[128,128]{1,0:T(8,128)S(1)} %fusion.47, pred[128,128]{1,0:T(8,128)(4,1)S(1)} %copy-done.21, f32[40]{0:T(128)S(1)} %copy-done.23), kind=kOutput, calls=%fused_computation.12 | convolution fusion | flops 88145920 | bytes 2724000 | tf_op jit(solution)/shard_map/vmap(hij,ihp->jhp)/dot_general | solution.py:52
  79.8 2.8 %copy.69 = f32[1,128,2560]{2,1,0:T(8,128)} copy(f32[1,128,2560]{1,2,0:T(8,128)} %bitcast.220) | data formatting | bytes 2621440 | tf_op jit(solution)/shard_map/vmap()/reshape | solution.py:55
  83.4 2.2 %fusion.19 = (f32[1,128,1280]{1,2,0:T(8,128)S(1)}, f32[1,128,1280]{1,2,0:T(8,128)S(1)}) fusion(f32[1,128,1280]{1,2,0:T(8,128)S(1)} %get-tuple-element.181, f32[1280]{0:T(1024)S(1)} %broadcast_in_dim.227, pred[]{:T(512)S(6)} %eq.27, f32[1,128,1280]{1,2,0:T(8,128)} %copy-done.15, f32[1,128,1280]{1,2,0:T(8,128)} %copy-done.10, f32[1280]{0:T(1024)S(1)} %broadcast_in_dim.224, ...), kind=kLoop, calls=%fused_computation.49 | loop fusion | flops 1638400 | bytes 4602882 | tf_op jit(solution)/shard_map/vmap(jit(_where))/select_n | solution.py:259
  85.6 1.9 %fusion.18 = (f32[1,128,1280]{1,2,0:T(8,128)S(1)}, f32[1,128,1280]{1,2,0:T(8,128)S(1)}) fusion(f32[1,128,1280]{1,2,0:T(8,128)S(1)} %copy-done.1, f32[1280]{0:T(1024)S(1)} %broadcast_in_dim.245, pred[]{:T(512)S(6)} %eq.30, f32[1,128,1280]{1,2,0:T(8,128)} %collective-permute-done.12, f32[1,128,1280]{1,2,0:T(8,128)S(1)} %copy-done.9, ...), kind=kLoop, calls=%fused_computation.42 | loop fusion | flops 1638400 | bytes 4602882 | tf_op jit(solution)/shard_map/vmap(jit(_where))/select_n | solution.py:259
  87.6 5.4 %collective-permute-start.13 = (f32[1,128,2560]{1,2,0:T(8,128)S(1)}, f32[1,128,2560]{1,2,0:T(8,128)S(1)}, u32[]{:S(2)}, u32[]{:S(2)}) collective-permute-start(f32[1,128,2560]{1,2,0:T(8,128)S(1)} %pad_maximum_fusion.1), channel_id=1, source_target_pairs={{0,1},{1,0},{2,3},{3,2},{4,5},{5,4},{6,7},{7,6},{8,9},{9,8},{10,11... | collective-permute-start | bytes 3932168 | tf_op jit(solution)/shard_map/vmap()/ppermute | solution.py:261
  93.0 1.3 %convert_reduce_fusion = bf16[128,128]{1,0:T(8,128)(2,1)S(1)} fusion(f32[40,128]{1,0:T(8,128)S(1)} %copy-done.20, pred[128,128]{1,0:T(8,128)(4,1)S(1)} %copy-done.22, bf16[128,40,64]{0,2,1:T(8,128)(2,1)S(1)} %bitcast.223, bf16[128,40,64]{0,2,1:T(8,128)(2,1)S(1)} %bitcast.224), kind=kOutput, calls=%fused_computation.2 | convolution fusion | flops 88457216 | bytes 1380352 | tf_op jit(solution)/shard_map/vmap(ihp,jhp->hij)/dot_general | solution.py:46
  98.8 1.2 %fusion.6 = bf16[1,128,2560]{2,1,0:T(8,128)(2,1)} fusion(f32[1,128,2560]{2,1,0:T(8,128)S(1)} %copy-done.5, f32[1,128,2560]{2,1,0:T(8,128)S(1)} %copy-done.4, f32[1,128,1280]{2,1,0:T(8,128)S(1)} %convolution_bitcast_fusion.2, f32[1,128,1280]{2,1,0:T(8,128)S(1)} %convolution_bitcast_fusion.3, pred[]{:T(512)S(6)} %eq.30), kind=kLoop, calls=%fused_computation.21 | loop fusion | flops 1966080 | bytes 4587521 | tf_op jit(solution)/shard_map/vmap()/convert_element_type | solution.py:291
  (177 shorter events, 21.3 us)
Async XLA Ops:
  0.6 4.3 %copy-start = (bf16[1,128,128]{2,1,0:T(8,128)(2,1)S(1)}, bf16[1,128,128]{2,1,0:T(8,128)(2,1)}, u32[]{:S(2)}) copy-start(bf16[1,128,128]{2,1,0:T(8,128)(2,1)} %param.8) | copy-start | bytes 98308
  0.6 2.6 %copy-start.11 = (bf16[1,128,2560]{2,1,0:T(8,128)(2,1)S(1)}, bf16[1,128,2560]{2,1,0:T(8,128)(2,1)}, u32[]{:S(2)}) copy-start(bf16[1,128,2560]{2,1,0:T(8,128)(2,1)} %param.7) | copy-start | bytes 1966084
  4.1 1.1 %copy-start.13 = (bf16[1,128,2560]{1,2,0:T(8,128)(2,1)}, bf16[1,128,2560]{1,2,0:T(8,128)(2,1)S(1)}, u32[]{:S(2)}) copy-start(bf16[1,128,2560]{1,2,0:T(8,128)(2,1)S(1)} %get-tuple-element.183) | copy-start | bytes 1966084
  4.4 7.7 %collective-permute-start = (f32[1,17,40]{2,1,0:T(8,128)S(1)}, f32[1,17,40]{2,1,0:T(8,128)S(1)}, u32[]{:S(2)}, u32[]{:S(2)}) collective-permute-start(f32[1,17,40]{2,1,0:T(8,128)S(1)} %pad_maximum_fusion.2), channel_id=1, source_target_pairs={{0,1},{1,0},{2,3},{3,2},{4,5},{5,4},{6,7},{7,6},{8,9},{9,8},{10,11... | collective-permute-start | bytes 8168 | tf_op jit(solution)/shard_map/vmap()/ppermute | solution.py:70
  6.6 6.2 %collective-permute-start.1 = (f32[1,128,2560]{1,2,0:T(8,128)}, f32[1,128,2560]{1,2,0:T(8,128)}, u32[]{:S(2)}, u32[]{:S(2)}) collective-permute-start(f32[1,128,2560]{1,2,0:T(8,128)} %pad_maximum_fusion), channel_id=1, source_target_pairs={{0,1},{1,0},{2,3},{3,2},{4,5},{5,4},{6,7},{7,6},{8,9},{9,8},{10,11... | collective-permute-start | bytes 3932168 | tf_op jit(solution)/shard_map/vmap()/ppermute | solution.py:241
  15.7 5.3 %collective-permute-start.3 = (f32[1,17,40]{2,1,0:T(8,128)S(1)}, f32[1,17,40]{2,1,0:T(8,128)S(1)}, u32[]{:S(2)}, u32[]{:S(2)}) collective-permute-start(f32[1,17,40]{2,1,0:T(8,128)S(1)} %fusion.90), channel_id=1, source_target_pairs={{0,2},{1,3},{2,0},{3,1},{4,6},{5,7},{6,4},{7,5},{8,10},{9,11},{10,... | collective-permute-start | bytes 8168 | tf_op jit(solution)/shard_map/vmap()/ppermute | solution.py:70
  18.5 12.9 %collective-permute-start.2 = (f32[1,128,1280]{1,2,0:T(8,128)}, f32[1,128,1280]{1,2,0:T(8,128)S(1)}, u32[]{:S(2)}, u32[]{:S(2)}) collective-permute-start(f32[1,128,1280]{1,2,0:T(8,128)} %get-tuple-element.180), channel_id=1, source_target_pairs={{0,2},{4,6},{8,10},{12,14},{3,1},{7,5},{11,9},{15,13},{16,18},{20,... | collective-permute-start | bytes 1966088 | tf_op jit(solution)/shard_map/vmap()/ppermute | solution.py:115
  19.8 17.3 %collective-permute-start.9 = (f32[1,128,1280]{1,2,0:T(8,128)}, f32[1,128,1280]{1,2,0:T(8,128)S(1)}, u32[]{:S(2)}, u32[]{:S(2)}) collective-permute-start(f32[1,128,1280]{1,2,0:T(8,128)} %get-tuple-element.176), channel_id=1, source_target_pairs={{15,13},{11,9},{7,5},{3,1},{12,14},{8,10},{4,6},{0,2},{31,29},{27,... | collective-permute-start | bytes 1966088 | tf_op jit(solution)/shard_map/vmap()/ppermute | solution.py:115
  21.1 2.6 %collective-permute-start.4 = (f32[1,17,40]{2,1,0:T(8,128)S(1)}, f32[1,17,40]{2,1,0:T(8,128)S(1)}, u32[]{:S(2)}, u32[]{:S(2)}) collective-permute-start(f32[1,17,40]{2,1,0:T(8,128)S(1)} %add.200), channel_id=1, source_target_pairs={{0,4},{1,5},{2,6},{3,7},{4,0},{5,1},{6,2},{7,3},{8,12},{9,13},{10,... | collective-permute-start | bytes 8168 | tf_op jit(solution)/shard_map/vmap()/ppermute | solution.py:70
  22.7 15.2 %copy-start.2 = (f32[1,128,1280]{1,2,0:T(8,128)S(1)}, f32[1,128,1280]{1,2,0:T(8,128)}, u32[]{:S(2)}) copy-start(f32[1,128,1280]{1,2,0:T(8,128)} %get-tuple-element.176) | copy-start | bytes 1966084
  23.7 3.4 %collective-permute-start.5 = (f32[1,17,40]{2,1,0:T(8,128)S(1)}, f32[1,17,40]{2,1,0:T(8,128)S(1)}, u32[]{:S(2)}, u32[]{:S(2)}) collective-permute-start(f32[1,17,40]{2,1,0:T(8,128)S(1)} %add.202), channel_id=1, source_target_pairs={{0,8},{1,9},{2,10},{3,11},{4,12},{5,13},{6,14},{7,15},{8,0},{9,1},... | collective-permute-start | bytes 8168 | tf_op jit(solution)/shard_map/vmap()/ppermute | solution.py:70
  27.8 11.8 %collective-permute-start.14 = (f32[40]{0:T(128)S(1)}, f32[40]{0:T(128)S(1)}, u32[]{:S(2)}, u32[]{:S(2)}) collective-permute-start(f32[40]{0:T(128)S(1)} %slice_bitcast_fusion.5), channel_id=1, source_target_pairs={{0,16},{16,0},{1,17},{17,1},{2,18},{18,2},{3,19},{19,3},{4,20},{20... | collective-permute-start | bytes 488 | tf_op jit(solution)/shard_map/ppermute | solution.py:313
  33.7 10.7 %collective-permute-start.6 = (f32[1,128,1280]{1,2,0:T(8,128)S(1)}, f32[1,128,1280]{1,2,0:T(8,128)S(1)}, u32[]{:S(2)}, u32[]{:S(2)}) collective-permute-start(f32[1,128,1280]{1,2,0:T(8,128)S(1)} %add_select_fusion.3), channel_id=1, source_target_pairs={{2,6},{6,10},{10,14},{1,5},{5,9},{9,13},{18,22},{22,26},{26,30},{1... | collective-permute-start | bytes 1966088 | tf_op jit(solution)/shard_map/vmap()/ppermute | solution.py:115
  38.3 13.1 %collective-permute-start.10 = (f32[1,128,1280]{1,2,0:T(8,128)S(1)}, f32[1,128,1280]{1,2,0:T(8,128)S(1)}, u32[]{:S(2)}, u32[]{:S(2)}) collective-permute-start(f32[1,128,1280]{1,2,0:T(8,128)S(1)} %add_select_fusion.1), channel_id=1, source_target_pairs={{13,9},{9,5},{5,1},{14,10},{10,6},{6,2},{29,25},{25,21},{21,17},{3... | collective-permute-start | bytes 1966088 | tf_op jit(solution)/shard_map/vmap()/ppermute | solution.py:115
  45.5 12.8 %copy-start.3 = (f32[1,128,1280]{1,2,0:T(8,128)S(1)}, f32[1,128,1280]{1,2,0:T(8,128)}, u32[]{:S(2)}) copy-start(f32[1,128,1280]{1,2,0:T(8,128)} %get-tuple-element.180) | copy-start | bytes 1966084
  45.5 12.8 %collective-permute-start.7 = (f32[1,128,1280]{1,2,0:T(8,128)}, f32[1,128,1280]{1,2,0:T(8,128)}, u32[]{:S(2)}, u32[]{:S(2)}) collective-permute-start(f32[1,128,1280]{1,2,0:T(8,128)} %multiply_add_fusion.5), channel_id=1, source_target_pairs={{2,10},{6,14},{1,9},{5,13},{18,26},{22,30},{17,25},{21,29}} | collective-permute-start | bytes 1966088 | tf_op jit(solution)/shard_map/vmap()/ppermute | solution.py:115
  52.4 19.6 %collective-permute-start.11 = (f32[1,128,1280]{1,2,0:T(8,128)}, f32[1,128,1280]{1,2,0:T(8,128)}, u32[]{:S(2)}, u32[]{:S(2)}) collective-permute-start(f32[1,128,1280]{1,2,0:T(8,128)} %multiply_add_fusion.2), channel_id=1, source_target_pairs={{13,5},{9,1},{14,6},{10,2},{29,21},{25,17},{30,22},{26,18}} | collective-permute-start | bytes 1966088 | tf_op jit(solution)/shard_map/vmap()/ppermute | solution.py:115
  60.7 15.9 %copy-start.16 = (bf16[1,128,2560]{1,2,0:T(8,128)(2,1)S(1)}, bf16[1,128,2560]{1,2,0:T(8,128)(2,1)}, u32[]{:S(2)}) copy-start(bf16[1,128,2560]{1,2,0:T(8,128)(2,1)} %copy.60) | copy-start | bytes 1966084
  60.7 15.9 %copy-start.20 = (f32[40,128]{1,0:T(8,128)S(1)}, f32[40,128]{1,0:T(8,128)}, u32[]{:S(2)}) copy-start(f32[40,128]{1,0:T(8,128)} %copy.61) | copy-start | bytes 61444
  60.7 15.9 %copy-start.21 = (pred[128,128]{1,0:T(8,128)(4,1)S(1)}, pred[128,128]{1,0:T(8,128)(4,1)}, u32[]{:S(2)}) copy-start(pred[128,128]{1,0:T(8,128)(4,1)} %iota_compare_fusion) | copy-start | bytes 49156
  60.7 15.9 %copy-start.23 = (f32[40]{0:T(128)S(1)}, f32[40]{0:T(128)}, u32[]{:S(2)}) copy-start(f32[40]{0:T(128)} %param.11) | copy-start | bytes 484
  60.7 21.9 %collective-permute-start.8 = (f32[1,128,1280]{1,2,0:T(8,128)}, f32[1,128,1280]{1,2,0:T(8,128)S(1)}, u32[]{:S(2)}, u32[]{:S(2)}) collective-permute-start(f32[1,128,1280]{1,2,0:T(8,128)} %add_select_fusion.2), channel_id=1, source_target_pairs={{6,4},{10,8},{14,12},{1,3},{5,7},{9,11},{13,15},{22,20},{26,24},{3... | collective-permute-start | bytes 1966088 | tf_op jit(solution)/shard_map/vmap()/ppermute | solution.py:115
  74.3 11.3 %collective-permute-start.12 = (f32[1,128,1280]{1,2,0:T(8,128)}, f32[1,128,1280]{1,2,0:T(8,128)}, u32[]{:S(2)}, u32[]{:S(2)}) collective-permute-start(f32[1,128,1280]{1,2,0:T(8,128)} %add_select_fusion), channel_id=1, source_target_pairs={{9,11},{5,7},{1,3},{14,12},{10,8},{6,4},{2,0},{25,27},{21,23},{17,... | collective-permute-start | bytes 1966088 | tf_op jit(solution)/shard_map/vmap()/ppermute | solution.py:115
  76.5 2.2 %copy-start.12 = (bf16[1,128,2560]{2,1,0:T(8,128)(2,1)S(1)}, bf16[1,128,2560]{2,1,0:T(8,128)(2,1)}, u32[]{:S(2)}) copy-start(bf16[1,128,2560]{2,1,0:T(8,128)(2,1)} %param.6) | copy-start | bytes 1966084
  83.4 2.2 %copy-start.1 = (f32[1,128,1280]{1,2,0:T(8,128)S(1)}, f32[1,128,1280]{1,2,0:T(8,128)}, u32[]{:S(2)}) copy-start(f32[1,128,1280]{1,2,0:T(8,128)} %get-tuple-element.177) | copy-start | bytes 1966084
  83.4 2.2 %copy-start.9 = (f32[1,128,1280]{1,2,0:T(8,128)S(1)}, f32[1,128,1280]{1,2,0:T(8,128)}, u32[]{:S(2)}) copy-start(f32[1,128,1280]{1,2,0:T(8,128)} %copy-done.8) | copy-start | bytes 1966084
  87.5 5.5 %copy-start.17 = (bf16[1,128,2560]{1,2,0:T(8,128)(2,1)S(1)}, bf16[1,128,2560]{1,2,0:T(8,128)(2,1)}, u32[]{:S(2)}) copy-start(bf16[1,128,2560]{1,2,0:T(8,128)(2,1)} %copy.60) | copy-start | bytes 1966084
  87.5 5.5 %copy-start.18 = (bf16[1,128,2560]{1,2,0:T(8,128)(2,1)S(1)}, bf16[1,128,2560]{1,2,0:T(8,128)(2,1)}, u32[]{:S(2)}) copy-start(bf16[1,128,2560]{1,2,0:T(8,128)(2,1)} %copy.70) | copy-start | bytes 1966084
  87.5 5.5 %copy-start.22 = (pred[128,128]{1,0:T(8,128)(4,1)S(1)}, pred[128,128]{1,0:T(8,128)(4,1)}, u32[]{:S(2)}) copy-start(pred[128,128]{1,0:T(8,128)(4,1)} %iota_compare_fusion) | copy-start | bytes 49156
  87.6 8.6 %collective-permute-start.13 = (f32[1,128,2560]{1,2,0:T(8,128)S(1)}, f32[1,128,2560]{1,2,0:T(8,128)S(1)}, u32[]{:S(2)}, u32[]{:S(2)}) collective-permute-start(f32[1,128,2560]{1,2,0:T(8,128)S(1)} %pad_maximum_fusion.1), channel_id=1, source_target_pairs={{0,1},{1,0},{2,3},{3,2},{4,5},{5,4},{6,7},{7,6},{8,9},{9,8},{10,11... | collective-permute-start | bytes 3932168 | tf_op jit(solution)/shard_map/vmap()/ppermute | solution.py:261
  96.6 2.2 %copy-start.4 = (f32[1,128,2560]{2,1,0:T(8,128)S(1)}, f32[1,128,2560]{2,1,0:T(8,128)}, u32[]{:S(2)}) copy-start(f32[1,128,2560]{2,1,0:T(8,128)} %copy.68) | copy-start | bytes 3932164
  96.6 2.2 %copy-start.5 = (f32[1,128,2560]{2,1,0:T(8,128)S(1)}, f32[1,128,2560]{2,1,0:T(8,128)}, u32[]{:S(2)}) copy-start(f32[1,128,2560]{2,1,0:T(8,128)} %copy.69) | copy-start | bytes 3932164
  (7 other events, 6.5 us)

commit v18 on v17

--- a/solution.py
+++ b/solution.py
@@ -301,6 +301,9 @@
     within, totals, value_scale, decayed_vals, decayed_cot, fwd_state, adj_state, skip_parts = prepare(
         token_values, cotangent, write_coeffs, read_coeffs, decay_codes
     )
+    row_major = Layout(major_to_minor=tuple(range(decayed_vals.ndim)))
+    decayed_vals = with_layout_constraint(decayed_vals, row_major)
+    decayed_cot = with_layout_constraint(decayed_cot, row_major)
     position = lax.axis_index("ctx")
     count = lax.axis_size("ctx")
     tables = jax.vmap(gather_totals, (0, 0, None, None))(totals, skip_parts, position, count)

time: 102 us -> 104 us (1.020)
  other arithmetic: 23.8 us -> 26.7 us
    reduce_sum x2, other arithmetic: 0.53 us -> 3 us  [block_states(): jnp.sum((values.astype(jnp.float32) * cotan.astype(jnp.float32)).reshape(...]
    broadcast_in_dim x30 -> x32, local copies, waits for them, and re-layouts: 5.97 us -> 4.08 us  [spread_heads(): return jnp.repeat(per_head, width, axis=-1)]
    unnamed x50 -> x34, local copies, waits for them, and re-layouts: 5.06 us -> 3.24 us
    ppermute x8, waiting for transfers between devices: 15.8 us -> 14.5 us  [exchange(): lax.ppermute(p, 'ctx', pairs)]
    squeeze x8, local copies, waits for them, and re-layouts: 0.35 us -> 1.61 us  [gain(): lax.dynamic_index_in_dim(self.pyramids[key], low_block // size, keepdims=...]
    optimization_barrier x2, local copies, waits for them, and re-layouts: 3.27 us -> 4.44 us  [local(): lax.optimization_barrier(((token_values, cotangent, write_coeffs, read_co...]
  transfers between devices with their start and end apart: 15 -> 15, of which waited for: 6 -> 6; matrix products, arithmetic and copies ran while one was open for 34% -> 33% of each run, Pallas kernels for 0% -> 0%
where the time goes in v18:
time: 104 us; the launch traced here: 102 us
  starting transfers between devices  31.9 us (31%)
  other arithmetic  26.7 us (26%)
  local copies, waits for them, and re-layouts  17.7 us (17%)
  waiting for transfers between devices  16.6 us (16%)
  matrix products  7.38 us (7%)
  between operations  1.89 us (2%)
    ppermute x8, starting transfers between devices, exchange(): lax.ppermute(p, 'ctx', pairs)  18.5 us
    ppermute x8, waiting for transfers between devices, exchange(): lax.ppermute(p, 'ctx', pairs)  14.5 us
    ppermute x4, starting transfers between devices, extend_totals(): lax.ppermute(tables[-1], 'ctx', xor_pairs(count, bit))  6.4 us
    ppermute x1, starting transfers between devices, carried_pair(): lax.ppermute(jnp.concatenate(lifted_parts, -1), 'ctx', [(i, i ^ 1) for i...  5.3 us
    optimization_barrier x2, local copies, waits for them, and re-layouts, local(): lax.optimization_barrier(((token_values, cotangent, write_coeffs, read_co...  4.44 us
    select_n x2, other arithmetic, down_send(): jnp.where(self.way.upper, self.pair_gain(0, pair, 1) * prefix + pair_tota...  4.31 us
    broadcast_in_dim x32, local copies, waits for them, and re-layouts, spread_heads(): return jnp.repeat(per_head, width, axis=-1)  4.08 us
    select_n x2, other arithmetic, carried_pair(): lifted_parts.append(jnp.where(way.upper, pair_prefix, lifted))  3.51 us
  transfers between devices with their start and end apart: 15, of which 6 were waited for; matrix products, arithmetic and copies ran while one was open for 33% of the time, Pallas kernels for 0%

profile of v18, /device:TPU:1, one launch (start us, length us, event | category | flops | bytes accessed | tf_op | source)
XLA Modules:
  0.0 102.1 jit_solution(15133000187788166837)
XLA Ops:
  2.4 1.5 %copy.64 = f32[1,128,2560]{2,1,0:T(8,128)} copy(f32[1,128,2560]{1,2,0:T(8,128)S(1)} %bitcast.218) | data formatting | bytes 2621440 | tf_op jit(solution)/shard_map/vmap()/broadcast_in_dim | solution.py:11
  3.9 2.9 %fusion.2 = (f32[2560]{0:T(1024)S(1)}, bf16[1,128,2560]{2,1,0:T(8,128)(2,1)}, bf16[1,128,2560]{2,1,0:T(8,128)(2,1)S(1)}) fusion(bf16[1,128,2560]{2,1,0:T(8,128)(2,1)} %param.7, bf16[1,128,2560]{2,1,0:T(8,128)(2,1)} %param.6, f32[1,128,2560]{2,1,0:T(8,128)S(1)} %copy.62, f32[1,128,2560]{2,1,0:T(8,128)} %copy.64), kind=kLoop, calls=%fused_computation.14 | loop fusion | flops 2618880 | bytes 5253120 | tf_op jit(solution)/shard_map/vmap()/reduce_sum | solution.py:26
  14.4 3.1 %select_add_fusion = (f32[1,128,1280]{2,1,0:T(8,128)}, f32[1,128,1280]{2,1,0:T(8,128)}, f32[1,128,1280]{2,1,0:T(8,128)}, f32[1,128,1280]{2,1,0:T(8,128)S(1)}) fusion(f32[1,128,2560]{2,1,0:T(8,128)} %collective-permute-done.1, f32[1280]{0:T(1024)S(1)} %broadcast_in_dim.209, pred[]{:T(512)S(6)} %eq.30, f32[1,128,2560]{2,1,0:T(8,128)S(1)} %convolution_bitcast_fusion, ...), kind=kLoop, calls=%fused_computation.55 | loop fusion | flops 1638400 | bytes 6563842 | tf_op jit(solution)/shard_map/vmap()/add | solution.py:251
  17.6 2.6 %collective-permute-start.3 = (f32[1,17,40]{2,1,0:T(8,128)S(1)}, f32[1,17,40]{2,1,0:T(8,128)S(1)}, u32[]{:S(2)}, u32[]{:S(2)}) collective-permute-start(f32[1,17,40]{2,1,0:T(8,128)S(1)} %fusion.90), channel_id=1, source_target_pairs={{0,2},{1,3},{2,0},{3,1},{4,6},{5,7},{6,4},{7,5},{8,10},{9,11},{10,... | collective-permute-start | bytes 8168 | tf_op jit(solution)/shard_map/vmap()/ppermute | solution.py:70
  20.5 1.3 %collective-permute-start.2 = (f32[1,128,1280]{2,1,0:T(8,128)}, f32[1,128,1280]{2,1,0:T(8,128)S(1)}, u32[]{:S(2)}, u32[]{:S(2)}) collective-permute-start(f32[1,128,1280]{2,1,0:T(8,128)} %get-tuple-element.180), channel_id=1, source_target_pairs={{0,2},{4,6},{8,10},{12,14},{3,1},{7,5},{11,9},{15,13},{16,18},{20,... | collective-permute-start | bytes 1966088 | tf_op jit(solution)/shard_map/vmap()/ppermute | solution.py:115
  21.8 1.3 %collective-permute-start.9 = (f32[1,128,1280]{2,1,0:T(8,128)}, f32[1,128,1280]{2,1,0:T(8,128)}, u32[]{:S(2)}, u32[]{:S(2)}) collective-permute-start(f32[1,128,1280]{2,1,0:T(8,128)} %get-tuple-element.176), channel_id=1, source_target_pairs={{15,13},{11,9},{7,5},{3,1},{12,14},{8,10},{4,6},{0,2},{31,29},{27,... | collective-permute-start | bytes 1966088 | tf_op jit(solution)/shard_map/vmap()/ppermute | solution.py:115
  23.1 1.4 %collective-permute-start.4 = (f32[1,17,40]{2,1,0:T(8,128)S(1)}, f32[1,17,40]{2,1,0:T(8,128)S(1)}, u32[]{:S(2)}, u32[]{:S(2)}) collective-permute-start(f32[1,17,40]{2,1,0:T(8,128)S(1)} %add.200), channel_id=1, source_target_pairs={{0,4},{1,5},{2,6},{3,7},{4,0},{5,1},{6,2},{7,3},{8,12},{9,13},{10,... | collective-permute-start | bytes 8168 | tf_op jit(solution)/shard_map/vmap()/ppermute | solution.py:70
  25.8 2.3 %collective-permute-start.5 = (f32[1,17,40]{2,1,0:T(8,128)S(1)}, f32[1,17,40]{2,1,0:T(8,128)S(1)}, u32[]{:S(2)}, u32[]{:S(2)}) collective-permute-start(f32[1,17,40]{2,1,0:T(8,128)S(1)} %add.202), channel_id=1, source_target_pairs={{0,8},{1,9},{2,10},{3,11},{4,12},{5,13},{6,14},{7,15},{8,0},{9,1},... | collective-permute-start | bytes 8168 | tf_op jit(solution)/shard_map/vmap()/ppermute | solution.py:70
  30.3 1.2 %collective-permute-start.14 = (f32[40]{0:T(128)}, f32[40]{0:T(128)}, u32[]{:S(2)}, u32[]{:S(2)}) collective-permute-start(f32[40]{0:T(128)} %slice_bitcast_fusion.5), channel_id=1, source_target_pairs={{0,16},{16,0},{1,17},{17,1},{2,18},{18,2},{3,19},{19,3},{4,20},{20... | collective-permute-start | bytes 488 | tf_op jit(solution)/shard_map/ppermute | solution.py:316
  32.7 1.3 %constant_dynamic-slice_fusion.4 = (f32[1,40]{1,0:T(1,128)S(1)}, f32[1,40]{1,0:T(1,128)S(1)}) fusion(f32[4,40]{1,0:T(4,128)S(1)} %exp.129, s32[]{:T(128)} %bitcast.233, s32[]{:T(128)} %bitcast.234), kind=kLoop, calls=%fused_computation.110 | loop fusion | bytes 648 | tf_op jit(solution)/shard_map/vmap(jit(dynamic_index_in_dim))/squeeze | solution.py:109
  36.0 1.2 %add_select_fusion.3 = f32[1,128,1280]{2,1,0:T(8,128)S(1)} fusion(f32[1,128,1280]{2,1,0:T(8,128)} %get-tuple-element.180, f32[1,128,1280]{2,1,0:T(8,128)S(1)} %collective-permute-done.2, f32[1280]{0:T(1024)S(1)} %broadcast_in_dim.221, f32[1280]{0:T(1024)S(1)} %broadcast_in_dim.212, pred[]{:T(512)S(6)} %eq.27), kind=kLoop, calls=%fused_computation.54 | loop fusion | flops 819200 | bytes 1976321 | tf_op jit(solution)/shard_map/vmap(jit(_where))/select_n | solution.py:153
  37.2 3.2 %collective-permute-start.6 = (f32[1,128,1280]{2,1,0:T(8,128)S(1)}, f32[1,128,1280]{2,1,0:T(8,128)S(1)}, u32[]{:S(2)}, u32[]{:S(2)}) collective-permute-start(f32[1,128,1280]{2,1,0:T(8,128)S(1)} %add_select_fusion.3), channel_id=1, source_target_pairs={{2,6},{6,10},{10,14},{1,5},{5,9},{9,13},{18,22},{22,26},{26,30},{1... | collective-permute-start | bytes 1966088 | tf_op jit(solution)/shard_map/vmap()/ppermute | solution.py:115
  40.5 1.2 %add_select_fusion.1 = f32[1,128,1280]{2,1,0:T(8,128)S(1)} fusion(f32[1,128,1280]{2,1,0:T(8,128)S(1)} %copy-done.3, f32[1,128,1280]{2,1,0:T(8,128)} %collective-permute-done.9, f32[1280]{0:T(1024)S(1)} %broadcast_in_dim.239, f32[1280]{0:T(1024)S(1)} %broadcast_in_dim.230, pred[]{:T(512)S(6)} %eq.30), kind=kLoop, calls=%fused_computation.47 | loop fusion | flops 819200 | bytes 1976321 | tf_op jit(solution)/shard_map/vmap(jit(_where))/select_n | solution.py:153
  41.7 1.3 %collective-permute-start.10 = (f32[1,128,1280]{2,1,0:T(8,128)S(1)}, f32[1,128,1280]{2,1,0:T(8,128)S(1)}, u32[]{:S(2)}, u32[]{:S(2)}) collective-permute-start(f32[1,128,1280]{2,1,0:T(8,128)S(1)} %add_select_fusion.1), channel_id=1, source_target_pairs={{13,9},{9,5},{5,1},{14,10},{10,6},{6,2},{29,25},{25,21},{21,17},{3... | collective-permute-start | bytes 1966088 | tf_op jit(solution)/shard_map/vmap()/ppermute | solution.py:115
  44.1 3.8 %collective-permute-done.6 = f32[1,128,1280]{2,1,0:T(8,128)S(1)} collective-permute-done((f32[1,128,1280]{2,1,0:T(8,128)S(1)}, f32[1,128,1280]{2,1,0:T(8,128)S(1)}, u32[]{:S(2)}, u32[]{:S(2)}) %collective-permute-start.6) | collective-permute-done | bytes 655392 | tf_op jit(solution)/shard_map/vmap()/ppermute | solution.py:115
  48.8 5.7 %collective-permute-start.7 = (f32[1,128,1280]{2,1,0:T(8,128)}, f32[1,128,1280]{2,1,0:T(8,128)}, u32[]{:S(2)}, u32[]{:S(2)}) collective-permute-start(f32[1,128,1280]{2,1,0:T(8,128)} %multiply_add_fusion.5), channel_id=1, source_target_pairs={{2,10},{6,14},{1,9},{5,13},{18,26},{22,30},{17,25},{21,29}} | collective-permute-start | bytes 1966088 | tf_op jit(solution)/shard_map/vmap()/ppermute | solution.py:115
  55.5 1.3 %collective-permute-start.11 = (f32[1,128,1280]{2,1,0:T(8,128)}, f32[1,128,1280]{2,1,0:T(8,128)}, u32[]{:S(2)}, u32[]{:S(2)}) collective-permute-start(f32[1,128,1280]{2,1,0:T(8,128)} %multiply_add_fusion.2), channel_id=1, source_target_pairs={{13,5},{9,1},{14,6},{10,2},{29,21},{25,17},{30,22},{26,18}} | collective-permute-start | bytes 1966088 | tf_op jit(solution)/shard_map/vmap()/ppermute | solution.py:115
  56.9 2.2 %copy.66 = bf16[1,128,2560]{1,2,0:T(8,128)(2,1)} copy(bf16[1,128,2560]{2,1,0:T(8,128)(2,1)} %param.7) | data formatting | bytes 1310720 | tf_op jit(solution)/shard_map/optimization_barrier | solution.py:317
  59.8 1.7 %collective-permute-done.7 = f32[1,128,1280]{2,1,0:T(8,128)} collective-permute-done((f32[1,128,1280]{2,1,0:T(8,128)}, f32[1,128,1280]{2,1,0:T(8,128)}, u32[]{:S(2)}, u32[]{:S(2)}) %collective-permute-start.7) | collective-permute-done | bytes 655392 | tf_op jit(solution)/shard_map/vmap()/ppermute | solution.py:115
  61.5 2.2 %add_select_fusion.2 = f32[1,128,1280]{2,1,0:T(8,128)} fusion(f32[1,128,1280]{2,1,0:T(8,128)} %get-tuple-element.180, f32[1280]{0:T(1024)S(1)} %broadcast_in_dim.212, pred[]{:T(512)S(6)} %eq.27, f32[1,128,1280]{2,1,0:T(8,128)S(1)} %collective-permute-done.6, f32[1,128,1280]{2,1,0:T(8,128)} %collective-permute-done.7, f32[1280]{0:T(1024)S(1)} %broadcast_in_dim.215), kind=kLoop, calls=%fused_computation.51 | loop fusion | flops 819200 | bytes 2631681 | tf_op jit(solution)/shard_map/vmap(jit(_where))/select_n | solution.py:160
  63.8 2.3 %collective-permute-start.8 = (f32[1,128,1280]{2,1,0:T(8,128)}, f32[1,128,1280]{2,1,0:T(8,128)}, u32[]{:S(2)}, u32[]{:S(2)}) collective-permute-start(f32[1,128,1280]{2,1,0:T(8,128)} %add_select_fusion.2), channel_id=1, source_target_pairs={{6,4},{10,8},{14,12},{1,3},{5,7},{9,11},{13,15},{22,20},{26,24},{3... | collective-permute-start | bytes 1966088 | tf_op jit(solution)/shard_map/vmap()/ppermute | solution.py:115
  66.1 8.9 %collective-permute-done.11 = f32[1,128,1280]{2,1,0:T(8,128)} collective-permute-done((f32[1,128,1280]{2,1,0:T(8,128)}, f32[1,128,1280]{2,1,0:T(8,128)}, u32[]{:S(2)}, u32[]{:S(2)}) %collective-permute-start.11) | collective-permute-done | bytes 655392 | tf_op jit(solution)/shard_map/vmap()/ppermute | solution.py:115
  75.1 2.1 %add_select_fusion = f32[1,128,1280]{2,1,0:T(8,128)} fusion(f32[1,128,1280]{2,1,0:T(8,128)S(1)} %copy-done.4, f32[1280]{0:T(1024)S(1)} %broadcast_in_dim.230, pred[]{:T(512)S(6)} %eq.30, f32[1,128,1280]{2,1,0:T(8,128)S(1)} %collective-permute-done.10, f32[1,128,1280]{2,1,0:T(8,128)} %collective-permute-done.11, f32[1280]{0:T(1024)S(1)} %broadcast_in_dim.233), kind=kLoop, calls=%fused_computation.44 | loop fusion | flops 819200 | bytes 2631681 | tf_op jit(solution)/shard_map/vmap(jit(_where))/select_n | solution.py:160
  77.1 2.1 %collective-permute-start.12 = (f32[1,128,1280]{2,1,0:T(8,128)}, f32[1,128,1280]{2,1,0:T(8,128)}, u32[]{:S(2)}, u32[]{:S(2)}) collective-permute-start(f32[1,128,1280]{2,1,0:T(8,128)} %add_select_fusion), channel_id=1, source_target_pairs={{9,11},{5,7},{1,3},{14,12},{10,8},{6,4},{2,0},{25,27},{21,23},{17,... | collective-permute-start | bytes 1966088 | tf_op jit(solution)/shard_map/vmap()/ppermute | solution.py:115
  79.3 2.2 %fusion = f32[1,128,40,64]{1,3,2,0:T(8,128)} fusion(bf16[128,40,64]{0,2,1:T(8,128)(2,1)S(1)} %bitcast.220, bf16[1,128,40,64]{1,3,2,0:T(8,128)(2,1)S(1)} %bitcast.221, f32[40,128]{1,0:T(8,128)S(1)} %copy-done.15, f32[128,128]{1,0:T(8,128)S(1)} %fusion.47, pred[128,128]{1,0:T(8,128)(4,1)S(1)} %iota_compare_fusion, f32[40]{0:T(128)S(1)} %copy-done.16), kind=kOutput, calls=%fused_computation.12 | convolution fusion | flops 88145920 | bytes 2724000 | tf_op jit(solution)/shard_map/vmap(hij,ihp->jhp)/dot_general | solution.py:52
  81.4 2.2 %copy.76 = bf16[1,128,2560]{1,2,0:T(8,128)(2,1)} copy(bf16[1,128,2560]{2,1,0:T(8,128)(2,1)} %param.6) | data formatting | bytes 1310720 | tf_op jit(solution)/shard_map/optimization_barrier | solution.py:317
  83.7 2.8 %copy.75 = f32[1,128,2560]{2,1,0:T(8,128)} copy(f32[1,128,2560]{1,2,0:T(8,128)} %bitcast.219) | data formatting | bytes 2621440 | tf_op jit(solution)/shard_map/vmap()/reshape | solution.py:55
  86.5 1.8 %fusion.19 = (f32[1,128,1280]{2,1,0:T(8,128)S(1)}, f32[1,128,1280]{2,1,0:T(8,128)S(1)}) fusion(f32[1,128,1280]{2,1,0:T(8,128)S(1)} %get-tuple-element.181, f32[1280]{0:T(1024)S(1)} %broadcast_in_dim.227, pred[]{:T(512)S(6)} %eq.27, f32[1,128,1280]{2,1,0:T(8,128)} %collective-permute-done.8, f32[1,128,1280]{2,1,0:T(8,128)} %copy-done.10, ...), kind=kLoop, calls=%fused_computation.49 | loop fusion | flops 1638400 | bytes 4602882 | tf_op jit(solution)/shard_map/vmap(jit(_where))/select_n | solution.py:259
  88.3 1.7 %fusion.18 = (f32[1,128,1280]{2,1,0:T(8,128)S(1)}, f32[1,128,1280]{2,1,0:T(8,128)S(1)}) fusion(f32[1,128,1280]{2,1,0:T(8,128)S(1)} %copy-done.2, f32[1280]{0:T(1024)S(1)} %broadcast_in_dim.245, pred[]{:T(512)S(6)} %eq.30, f32[1,128,1280]{2,1,0:T(8,128)} %collective-permute-done.12, f32[1,128,1280]{2,1,0:T(8,128)} %collective-permute-done.9, ...), kind=kLoop, calls=%fused_computation.42 | loop fusion | flops 1638400 | bytes 4602882 | tf_op jit(solution)/shard_map/vmap(jit(_where))/select_n | solution.py:259
  90.2 5.3 %collective-permute-start.13 = (f32[1,128,2560]{2,1,0:T(8,128)S(1)}, f32[1,128,2560]{2,1,0:T(8,128)S(1)}, u32[]{:S(2)}, u32[]{:S(2)}) collective-permute-start(f32[1,128,2560]{2,1,0:T(8,128)S(1)} %pad_maximum_fusion.1), channel_id=1, source_target_pairs={{0,1},{1,0},{2,3},{3,2},{4,5},{5,4},{6,7},{7,6},{8,9},{9,8},{10,11... | collective-permute-start | bytes 3932168 | tf_op jit(solution)/shard_map/vmap()/ppermute | solution.py:261
  95.5 1.3 %convert_reduce_fusion = bf16[128,128]{1,0:T(8,128)(2,1)S(1)} fusion(f32[40,128]{1,0:T(8,128)S(1)} %copy-done.15, pred[128,128]{1,0:T(8,128)(4,1)S(1)} %iota_compare_fusion, bf16[128,40,64]{0,2,1:T(8,128)(2,1)S(1)} %bitcast.222, bf16[128,40,64]{0,2,1:T(8,128)(2,1)S(1)} %bitcast.223), kind=kOutput, calls=%fused_computation.2 | convolution fusion | flops 88457216 | bytes 1380352 | tf_op jit(solution)/shard_map/vmap(ihp,jhp->hij)/dot_general | solution.py:46
  100.9 1.2 %fusion.6 = bf16[1,128,2560]{2,1,0:T(8,128)(2,1)} fusion(f32[1,128,2560]{2,1,0:T(8,128)S(1)} %copy-done.5, f32[1,128,2560]{2,1,0:T(8,128)S(1)} %copy.62, f32[1,128,1280]{2,1,0:T(8,128)S(1)} %convolution_bitcast_fusion.2, f32[1,128,1280]{2,1,0:T(8,128)S(1)} %convolution_bitcast_fusion.3, pred[]{:T(512)S(6)} %eq.30), kind=kLoop, calls=%fused_computation.21 | loop fusion | flops 1966080 | bytes 4587521 | tf_op jit(solution)/shard_map/vmap()/convert_element_type | solution.py:291
  (163 shorter events, 23.4 us)
Async XLA Ops:
  0.6 7.0 %copy-start = (bf16[1,128,128]{2,1,0:T(8,128)(2,1)S(1)}, bf16[1,128,128]{2,1,0:T(8,128)(2,1)}, u32[]{:S(2)}) copy-start(bf16[1,128,128]{2,1,0:T(8,128)(2,1)} %param.8) | copy-start | bytes 98308
  3.9 3.3 %copy-start.14 = (bf16[1,128,128]{2,1,0:T(8,128)(2,1)S(1)}, bf16[1,128,128]{2,1,0:T(8,128)(2,1)}, u32[]{:S(2)}) copy-start(bf16[1,128,128]{2,1,0:T(8,128)(2,1)} %param.9) | copy-start | bytes 98308
  6.8 1.9 %copy-start.6 = (bf16[1,128,2560]{2,1,0:T(8,128)(2,1)}, bf16[1,128,2560]{2,1,0:T(8,128)(2,1)S(1)}, u32[]{:S(2)}) copy-start(bf16[1,128,2560]{2,1,0:T(8,128)(2,1)S(1)} %get-tuple-element.184) | copy-start | bytes 1966084
  7.1 5.9 %collective-permute-start = (f32[1,17,40]{2,1,0:T(8,128)S(1)}, f32[1,17,40]{2,1,0:T(8,128)S(1)}, u32[]{:S(2)}, u32[]{:S(2)}) collective-permute-start(f32[1,17,40]{2,1,0:T(8,128)S(1)} %pad_maximum_fusion.2), channel_id=1, source_target_pairs={{0,1},{1,0},{2,3},{3,2},{4,5},{5,4},{6,7},{7,6},{8,9},{9,8},{10,11... | collective-permute-start | bytes 8168 | tf_op jit(solution)/shard_map/vmap()/ppermute | solution.py:70
  7.2 1.1 %copy-start.8 = (bf16[1,128,2560]{2,1,0:T(8,128)(2,1)S(1)}, bf16[1,128,2560]{2,1,0:T(8,128)(2,1)}, u32[]{:S(2)}) copy-start(bf16[1,128,2560]{2,1,0:T(8,128)(2,1)} %get-tuple-element.183) | copy-start | bytes 1966084
  8.7 1.1 %copy-start.1 = (f32[1,128,2560]{2,1,0:T(8,128)}, f32[1,128,2560]{2,1,0:T(8,128)S(1)}, u32[]{:S(2)}) copy-start(f32[1,128,2560]{2,1,0:T(8,128)S(1)} %convolution_bitcast_fusion.1) | copy-start | bytes 3932164
  11.0 3.5 %collective-permute-start.1 = (f32[1,128,2560]{2,1,0:T(8,128)}, f32[1,128,2560]{2,1,0:T(8,128)}, u32[]{:S(2)}, u32[]{:S(2)}) collective-permute-start(f32[1,128,2560]{2,1,0:T(8,128)} %pad_maximum_fusion), channel_id=1, source_target_pairs={{0,1},{1,0},{2,3},{3,2},{4,5},{5,4},{6,7},{7,6},{8,9},{9,8},{10,11... | collective-permute-start | bytes 3932168 | tf_op jit(solution)/shard_map/vmap()/ppermute | solution.py:241
  17.6 5.6 %collective-permute-start.3 = (f32[1,17,40]{2,1,0:T(8,128)S(1)}, f32[1,17,40]{2,1,0:T(8,128)S(1)}, u32[]{:S(2)}, u32[]{:S(2)}) collective-permute-start(f32[1,17,40]{2,1,0:T(8,128)S(1)} %fusion.90), channel_id=1, source_target_pairs={{0,2},{1,3},{2,0},{3,1},{4,6},{5,7},{6,4},{7,5},{8,10},{9,11},{10,... | collective-permute-start | bytes 8168 | tf_op jit(solution)/shard_map/vmap()/ppermute | solution.py:70
  20.5 14.6 %collective-permute-start.2 = (f32[1,128,1280]{2,1,0:T(8,128)}, f32[1,128,1280]{2,1,0:T(8,128)S(1)}, u32[]{:S(2)}, u32[]{:S(2)}) collective-permute-start(f32[1,128,1280]{2,1,0:T(8,128)} %get-tuple-element.180), channel_id=1, source_target_pairs={{0,2},{4,6},{8,10},{12,14},{3,1},{7,5},{11,9},{15,13},{16,18},{20,... | collective-permute-start | bytes 1966088 | tf_op jit(solution)/shard_map/vmap()/ppermute | solution.py:115
  21.8 18.6 %collective-permute-start.9 = (f32[1,128,1280]{2,1,0:T(8,128)}, f32[1,128,1280]{2,1,0:T(8,128)}, u32[]{:S(2)}, u32[]{:S(2)}) collective-permute-start(f32[1,128,1280]{2,1,0:T(8,128)} %get-tuple-element.176), channel_id=1, source_target_pairs={{15,13},{11,9},{7,5},{3,1},{12,14},{8,10},{4,6},{0,2},{31,29},{27,... | collective-permute-start | bytes 1966088 | tf_op jit(solution)/shard_map/vmap()/ppermute | solution.py:115
  23.1 2.6 %collective-permute-start.4 = (f32[1,17,40]{2,1,0:T(8,128)S(1)}, f32[1,17,40]{2,1,0:T(8,128)S(1)}, u32[]{:S(2)}, u32[]{:S(2)}) collective-permute-start(f32[1,17,40]{2,1,0:T(8,128)S(1)} %add.200), channel_id=1, source_target_pairs={{0,4},{1,5},{2,6},{3,7},{4,0},{5,1},{6,2},{7,3},{8,12},{9,13},{10,... | collective-permute-start | bytes 8168 | tf_op jit(solution)/shard_map/vmap()/ppermute | solution.py:70
  24.7 15.7 %copy-start.3 = (f32[1,128,1280]{2,1,0:T(8,128)S(1)}, f32[1,128,1280]{2,1,0:T(8,128)}, u32[]{:S(2)}) copy-start(f32[1,128,1280]{2,1,0:T(8,128)} %get-tuple-element.176) | copy-start | bytes 1966084
  25.8 3.4 %collective-permute-start.5 = (f32[1,17,40]{2,1,0:T(8,128)S(1)}, f32[1,17,40]{2,1,0:T(8,128)S(1)}, u32[]{:S(2)}, u32[]{:S(2)}) collective-permute-start(f32[1,17,40]{2,1,0:T(8,128)S(1)} %add.202), channel_id=1, source_target_pairs={{0,8},{1,9},{2,10},{3,11},{4,12},{5,13},{6,14},{7,15},{8,0},{9,1},... | collective-permute-start | bytes 8168 | tf_op jit(solution)/shard_map/vmap()/ppermute | solution.py:70
  30.3 12.7 %collective-permute-start.14 = (f32[40]{0:T(128)}, f32[40]{0:T(128)}, u32[]{:S(2)}, u32[]{:S(2)}) collective-permute-start(f32[40]{0:T(128)} %slice_bitcast_fusion.5), channel_id=1, source_target_pairs={{0,16},{16,0},{1,17},{17,1},{2,18},{18,2},{3,19},{19,3},{4,20},{20... | collective-permute-start | bytes 488 | tf_op jit(solution)/shard_map/ppermute | solution.py:316
  35.2 0.9 copy-start.10
  37.2 10.7 %collective-permute-start.6 = (f32[1,128,1280]{2,1,0:T(8,128)S(1)}, f32[1,128,1280]{2,1,0:T(8,128)S(1)}, u32[]{:S(2)}, u32[]{:S(2)}) collective-permute-start(f32[1,128,1280]{2,1,0:T(8,128)S(1)} %add_select_fusion.3), channel_id=1, source_target_pairs={{2,6},{6,10},{10,14},{1,5},{5,9},{9,13},{18,22},{22,26},{26,30},{1... | collective-permute-start | bytes 1966088 | tf_op jit(solution)/shard_map/vmap()/ppermute | solution.py:115
  41.7 12.8 %collective-permute-start.10 = (f32[1,128,1280]{2,1,0:T(8,128)S(1)}, f32[1,128,1280]{2,1,0:T(8,128)S(1)}, u32[]{:S(2)}, u32[]{:S(2)}) collective-permute-start(f32[1,128,1280]{2,1,0:T(8,128)S(1)} %add_select_fusion.1), channel_id=1, source_target_pairs={{13,9},{9,5},{5,1},{14,10},{10,6},{6,2},{29,25},{25,21},{21,17},{3... | collective-permute-start | bytes 1966088 | tf_op jit(solution)/shard_map/vmap()/ppermute | solution.py:115
  48.8 12.7 %collective-permute-start.7 = (f32[1,128,1280]{2,1,0:T(8,128)}, f32[1,128,1280]{2,1,0:T(8,128)}, u32[]{:S(2)}, u32[]{:S(2)}) collective-permute-start(f32[1,128,1280]{2,1,0:T(8,128)} %multiply_add_fusion.5), channel_id=1, source_target_pairs={{2,10},{6,14},{1,9},{5,13},{18,26},{22,30},{17,25},{21,29}} | collective-permute-start | bytes 1966088 | tf_op jit(solution)/shard_map/vmap()/ppermute | solution.py:115
  55.5 19.6 %collective-permute-start.11 = (f32[1,128,1280]{2,1,0:T(8,128)}, f32[1,128,1280]{2,1,0:T(8,128)}, u32[]{:S(2)}, u32[]{:S(2)}) collective-permute-start(f32[1,128,1280]{2,1,0:T(8,128)} %multiply_add_fusion.2), channel_id=1, source_target_pairs={{13,5},{9,1},{14,6},{10,2},{29,21},{25,17},{30,22},{26,18}} | collective-permute-start | bytes 1966088 | tf_op jit(solution)/shard_map/vmap()/ppermute | solution.py:115
  59.8 15.3 %copy-start.4 = (f32[1,128,1280]{2,1,0:T(8,128)S(1)}, f32[1,128,1280]{2,1,0:T(8,128)}, u32[]{:S(2)}) copy-start(f32[1,128,1280]{2,1,0:T(8,128)} %get-tuple-element.176) | copy-start | bytes 1966084
  63.8 15.5 %copy-start.11 = (bf16[1,128,2560]{1,2,0:T(8,128)(2,1)S(1)}, bf16[1,128,2560]{1,2,0:T(8,128)(2,1)}, u32[]{:S(2)}) copy-start(bf16[1,128,2560]{1,2,0:T(8,128)(2,1)} %copy.66) | copy-start | bytes 1966084
  63.8 15.5 %copy-start.15 = (f32[40,128]{1,0:T(8,128)S(1)}, f32[40,128]{1,0:T(8,128)}, u32[]{:S(2)}) copy-start(f32[40,128]{1,0:T(8,128)} %copy.67) | copy-start | bytes 61444
  63.8 15.5 %copy-start.16 = (f32[40]{0:T(128)S(1)}, f32[40]{0:T(128)}, u32[]{:S(2)}) copy-start(f32[40]{0:T(128)} %param.11) | copy-start | bytes 484
  63.8 22.7 %collective-permute-start.8 = (f32[1,128,1280]{2,1,0:T(8,128)}, f32[1,128,1280]{2,1,0:T(8,128)}, u32[]{:S(2)}, u32[]{:S(2)}) collective-permute-start(f32[1,128,1280]{2,1,0:T(8,128)} %add_select_fusion.2), channel_id=1, source_target_pairs={{6,4},{10,8},{14,12},{1,3},{5,7},{9,11},{13,15},{22,20},{26,24},{3... | collective-permute-start | bytes 1966088 | tf_op jit(solution)/shard_map/vmap()/ppermute | solution.py:115
  77.1 11.1 %collective-permute-start.12 = (f32[1,128,1280]{2,1,0:T(8,128)}, f32[1,128,1280]{2,1,0:T(8,128)}, u32[]{:S(2)}, u32[]{:S(2)}) collective-permute-start(f32[1,128,1280]{2,1,0:T(8,128)} %add_select_fusion), channel_id=1, source_target_pairs={{9,11},{5,7},{1,3},{14,12},{10,8},{6,4},{2,0},{25,27},{21,23},{17,... | collective-permute-start | bytes 1966088 | tf_op jit(solution)/shard_map/vmap()/ppermute | solution.py:115
  86.5 1.8 %copy-start.2 = (f32[1,128,1280]{2,1,0:T(8,128)S(1)}, f32[1,128,1280]{2,1,0:T(8,128)}, u32[]{:S(2)}) copy-start(f32[1,128,1280]{2,1,0:T(8,128)} %get-tuple-element.177) | copy-start | bytes 1966084
  90.0 5.5 %copy-start.12 = (bf16[1,128,2560]{1,2,0:T(8,128)(2,1)S(1)}, bf16[1,128,2560]{1,2,0:T(8,128)(2,1)}, u32[]{:S(2)}) copy-start(bf16[1,128,2560]{1,2,0:T(8,128)(2,1)} %copy.66) | copy-start | bytes 1966084
  90.0 5.4 %copy-start.13 = (bf16[1,128,2560]{1,2,0:T(8,128)(2,1)S(1)}, bf16[1,128,2560]{1,2,0:T(8,128)(2,1)}, u32[]{:S(2)}) copy-start(bf16[1,128,2560]{1,2,0:T(8,128)(2,1)} %copy.76) | copy-start | bytes 1966084
  90.2 8.3 %collective-permute-start.13 = (f32[1,128,2560]{2,1,0:T(8,128)S(1)}, f32[1,128,2560]{2,1,0:T(8,128)S(1)}, u32[]{:S(2)}, u32[]{:S(2)}) collective-permute-start(f32[1,128,2560]{2,1,0:T(8,128)S(1)} %pad_maximum_fusion.1), channel_id=1, source_target_pairs={{0,1},{1,0},{2,3},{3,2},{4,5},{5,4},{6,7},{7,6},{8,9},{9,8},{10,11... | collective-permute-start | bytes 3932168 | tf_op jit(solution)/shard_map/vmap()/ppermute | solution.py:261
  96.8 1.1 %copy-start.9 = (bf16[1,128,2560]{2,1,0:T(8,128)(2,1)S(1)}, bf16[1,128,2560]{2,1,0:T(8,128)(2,1)}, u32[]{:S(2)}) copy-start(bf16[1,128,2560]{2,1,0:T(8,128)(2,1)} %get-tuple-element.183) | copy-start | bytes 1966084
  96.9 1.2 %copy-start.7 = (bf16[1,128,2560]{2,1,0:T(8,128)(2,1)S(1)}, bf16[1,128,2560]{2,1,0:T(8,128)(2,1)}, u32[]{:S(2)}) copy-start(bf16[1,128,2560]{2,1,0:T(8,128)(2,1)} %copy-done.6) | copy-start | bytes 1966084
  98.8 2.1 %copy-start.5 = (f32[1,128,2560]{2,1,0:T(8,128)S(1)}, f32[1,128,2560]{2,1,0:T(8,128)}, u32[]{:S(2)}) copy-start(f32[1,128,2560]{2,1,0:T(8,128)} %copy.75) | copy-start | bytes 3932164

commit v19 on v13

--- a/solution.py
+++ b/solution.py
@@ -246,14 +246,15 @@
         own = take_half(state, way.upper)
         low_block = jnp.where(way.upper, other, own)
         high_block = jnp.where(way.upper, own, other)
-        lows.append(low_block)
+        lows.append((way.upper, other, state))
         totals.append(way.gain(1, 2 * way.pair + 1, 1) * low_block + high_block)
     tables[-1], _ = lax.optimization_barrier((tables[-1], totals))
     extend_totals(tables, count, 1, count.bit_length())
     pair_prefixes, anchor = pair_scans(ways, totals)
     lifted_parts = []
     keep_parts = []
-    for way, pair_prefix, low_block in zip(ways, pair_prefixes, lows):
+    for way, pair_prefix, (upper, other, state) in zip(ways, pair_prefixes, lows):
+        low_block = jnp.where(upper, other, take_half(state, upper))
         lifted = way.gain(1, 2 * way.pair, 1) * pair_prefix + low_block
         lifted_parts.append(jnp.where(way.upper, pair_prefix, lifted))
         keep_parts.append(jnp.where(way.upper, lifted, pair_prefix))

time: 101 us -> 101 us (level)
  no operation moved by 1% of the time
where the time goes in v19:
time: 101 us; the launch traced here: 99.8 us
  starting transfers between devices  33.2 us (33%)
  other arithmetic  24 us (24%)
  waiting for transfers between devices  18.7 us (19%)
  local copies, waits for them, and re-layouts  14.4 us (14%)
  matrix products  7.66 us (8%)
  between operations  1.91 us (2%)
    ppermute x8, starting transfers between devices, exchange(): lax.ppermute(p, 'ctx', pairs)  17.7 us
    ppermute x8, waiting for transfers between devices, exchange(): lax.ppermute(p, 'ctx', pairs)  16.1 us
    ppermute x1, starting transfers between devices, carried_pair(): lax.ppermute(jnp.concatenate(lifted_parts, -1), 'ctx', [(i, i ^ 1) for i...  7.44 us
    unnamed x53, local copies, waits for them, and re-layouts  6.85 us
    ppermute x4, starting transfers between devices, extend_totals(): lax.ppermute(tables[-1], 'ctx', xor_pairs(count, bit))  6.4 us
    select_n x2, other arithmetic, down_send(): jnp.where(self.way.upper, self.pair_gain(0, pair, 1) * prefix + pair_tota...  4.77 us
    select_n x2, other arithmetic, carried_pair(): lifted_parts.append(jnp.where(way.upper, pair_prefix, lifted))  4.03 us
    add x1, other arithmetic, carried_pair(): totals.append(way.gain(1, 2 * way.pair + 1, 1) * low_block + high_block)  3.23 us
  transfers between devices with their start and end apart: 15, of which 7 were waited for; matrix products, arithmetic and copies ran while one was open for 29% of the time, Pallas kernels for 0%

profile of v19, /device:TPU:1, one launch (start us, length us, event | category | flops | bytes accessed | tf_op | source)
XLA Modules:
  0.0 99.8 jit_solution(16003682926775306639)
XLA Ops:
  1.8 1.4 %copy.45 = bf16[1,128,2560]{1,2,0:T(8,128)(2,1)S(1)} copy(bf16[1,128,2560]{2,1,0:T(8,128)(2,1)} %param.6) | data formatting | bytes 1310720 | tf_op args[0]
  3.7 1.2 %fusion.1 = (f32[2560]{0:T(1024)S(1)}, bf16[1,128,2560]{1,2,0:T(8,128)(2,1)}, bf16[1,128,2560]{1,2,0:T(8,128)(2,1)S(1)}) fusion(bf16[1,128,2560]{1,2,0:T(8,128)(2,1)S(1)} %copy.46, bf16[1,128,2560]{1,2,0:T(8,128)(2,1)S(1)} %copy.45, f32[128,40]{0,1:T(8,128)S(1)} %get-tuple-element.201, f32[128,40]{0,1:T(8,128)S(1)} %get-tuple-element.202), kind=kLoop, calls=%fused_computation.14 | loop fusion | flops 2618880 | bytes 2672640 | tf_op jit(solution)/shard_map/vmap()/reduce_sum | solution.py:25
  6.8 1.1 %pad_maximum_fusion = f32[1,128,2560]{1,2,0:T(8,128)} fusion(f32[1,128,1280]{1,2,0:T(8,128)S(1)} %get-tuple-element.231, f32[1,128,1280]{1,2,0:T(8,128)S(1)} %get-tuple-element.232), kind=kLoop, calls=%fused_computation.19 | loop fusion | flops 327680 | bytes 2621440 | tf_op jit(solution)/shard_map/vmap()/concatenate | solution.py:239
  10.2 1.2 %collective-permute-done.1 = f32[1,128,2560]{1,2,0:T(8,128)} collective-permute-done((f32[1,128,2560]{1,2,0:T(8,128)}, f32[1,128,2560]{1,2,0:T(8,128)}, u32[]{:S(2)}, u32[]{:S(2)}) %collective-permute-start.1) | collective-permute-done | bytes 1310752 | tf_op jit(solution)/shard_map/vmap()/ppermute | solution.py:240
  11.4 3.2 %select_add_fusion.1 = (f32[1,128,1280]{1,2,0:T(8,128)}, f32[1,128,1280]{1,2,0:T(8,128)}, f32[1,128,1280]{1,2,0:T(8,128)}, f32[1,128,1280]{1,2,0:T(8,128)}) fusion(f32[1,128,2560]{1,2,0:T(8,128)} %collective-permute-done.1, f32[1280]{0:T(1024)S(1)} %broadcast_in_dim.199, pred[]{:T(512)S(6)} %eq.27, f32[1,128,2560]{1,2,0:T(8,128)S(1)} %convolution_bitcast_fusion.1, ...), kind=kLoop, calls=%fused_computation.55 | loop fusion | flops 1638400 | bytes 6563842 | tf_op jit(solution)/shard_map/vmap()/add | solution.py:250
  14.6 2.6 %collective-permute-start.3 = (f32[1,17,40]{2,1,0:T(8,128)S(1)}, f32[1,17,40]{2,1,0:T(8,128)S(1)}, u32[]{:S(2)}, u32[]{:S(2)}) collective-permute-start(f32[1,17,40]{2,1,0:T(8,128)S(1)} %fusion.89), channel_id=1, source_target_pairs={{0,2},{1,3},{2,0},{3,1},{4,6},{5,7},{6,4},{7,5},{8,10},{9,11},{10,... | collective-permute-start | bytes 8168 | tf_op jit(solution)/shard_map/vmap()/ppermute | solution.py:69
  17.6 1.3 %collective-permute-start.2 = (f32[1,128,1280]{1,2,0:T(8,128)}, f32[1,128,1280]{1,2,0:T(8,128)S(1)}, u32[]{:S(2)}, u32[]{:S(2)}) collective-permute-start(f32[1,128,1280]{1,2,0:T(8,128)} %get-tuple-element.192), channel_id=1, source_target_pairs={{0,2},{4,6},{8,10},{12,14},{3,1},{7,5},{11,9},{15,13},{16,18},{20,... | collective-permute-start | bytes 1966088 | tf_op jit(solution)/shard_map/vmap()/ppermute | solution.py:114
  18.9 1.3 %collective-permute-start.9 = (f32[1,128,1280]{1,2,0:T(8,128)}, f32[1,128,1280]{1,2,0:T(8,128)S(1)}, u32[]{:S(2)}, u32[]{:S(2)}) collective-permute-start(f32[1,128,1280]{1,2,0:T(8,128)} %get-tuple-element.196), channel_id=1, source_target_pairs={{15,13},{11,9},{7,5},{3,1},{12,14},{8,10},{4,6},{0,2},{31,29},{27,... | collective-permute-start | bytes 1966088 | tf_op jit(solution)/shard_map/vmap()/ppermute | solution.py:114
  20.2 1.4 %collective-permute-start.4 = (f32[1,17,40]{2,1,0:T(8,128)S(1)}, f32[1,17,40]{2,1,0:T(8,128)S(1)}, u32[]{:S(2)}, u32[]{:S(2)}) collective-permute-start(f32[1,17,40]{2,1,0:T(8,128)S(1)} %add.200), channel_id=1, source_target_pairs={{0,4},{1,5},{2,6},{3,7},{4,0},{5,1},{6,2},{7,3},{8,12},{9,13},{10,... | collective-permute-start | bytes 8168 | tf_op jit(solution)/shard_map/vmap()/ppermute | solution.py:69
  22.8 2.3 %collective-permute-start.5 = (f32[1,17,40]{2,1,0:T(8,128)S(1)}, f32[1,17,40]{2,1,0:T(8,128)S(1)}, u32[]{:S(2)}, u32[]{:S(2)}) collective-permute-start(f32[1,17,40]{2,1,0:T(8,128)S(1)} %add.202), channel_id=1, source_target_pairs={{0,8},{1,9},{2,10},{3,11},{4,12},{5,13},{6,14},{7,15},{8,0},{9,1},... | collective-permute-start | bytes 8168 | tf_op jit(solution)/shard_map/vmap()/ppermute | solution.py:69
  29.9 1.3 %collective-permute-start.14 = (f32[40]{0:T(128)S(1)}, f32[40]{0:T(128)S(1)}, u32[]{:S(2)}, u32[]{:S(2)}) collective-permute-start(f32[40]{0:T(128)S(1)} %slice_bitcast_fusion.5), channel_id=1, source_target_pairs={{0,16},{16,0},{1,17},{17,1},{2,18},{18,2},{3,19},{19,3},{4,20},{20... | collective-permute-start | bytes 488 | tf_op jit(solution)/shard_map/ppermute | solution.py:313
  32.0 1.5 %add_select_fusion.3 = f32[1,128,1280]{1,2,0:T(8,128)S(1)} fusion(f32[1,128,1280]{1,2,0:T(8,128)} %get-tuple-element.192, f32[1,128,1280]{1,2,0:T(8,128)S(1)} %collective-permute-done.2, f32[1280]{0:T(1024)S(1)} %broadcast_in_dim.221, f32[1280]{0:T(1024)S(1)} %broadcast_in_dim.212, pred[]{:T(512)S(6)} %eq.27), kind=kLoop, calls=%fused_computation.53 | loop fusion | flops 819200 | bytes 1976321 | tf_op jit(solution)/shard_map/vmap(jit(_where))/select_n | solution.py:152
  33.5 3.2 %collective-permute-start.6 = (f32[1,128,1280]{1,2,0:T(8,128)S(1)}, f32[1,128,1280]{1,2,0:T(8,128)S(1)}, u32[]{:S(2)}, u32[]{:S(2)}) collective-permute-start(f32[1,128,1280]{1,2,0:T(8,128)S(1)} %add_select_fusion.3), channel_id=1, source_target_pairs={{2,6},{6,10},{10,14},{1,5},{5,9},{9,13},{18,22},{22,26},{26,30},{1... | collective-permute-start | bytes 1966088 | tf_op jit(solution)/shard_map/vmap()/ppermute | solution.py:114
  38.0 1.3 %collective-permute-start.10 = (f32[1,128,1280]{1,2,0:T(8,128)S(1)}, f32[1,128,1280]{1,2,0:T(8,128)S(1)}, u32[]{:S(2)}, u32[]{:S(2)}) collective-permute-start(f32[1,128,1280]{1,2,0:T(8,128)S(1)} %add_select_fusion.1), channel_id=1, source_target_pairs={{13,9},{9,5},{5,1},{14,10},{10,6},{6,2},{29,25},{25,21},{21,17},{3... | collective-permute-start | bytes 1966088 | tf_op jit(solution)/shard_map/vmap()/ppermute | solution.py:114
  39.8 4.4 %collective-permute-done.6 = f32[1,128,1280]{1,2,0:T(8,128)S(1)} collective-permute-done((f32[1,128,1280]{1,2,0:T(8,128)S(1)}, f32[1,128,1280]{1,2,0:T(8,128)S(1)}, u32[]{:S(2)}, u32[]{:S(2)}) %collective-permute-start.6) | collective-permute-done | bytes 655392 | tf_op jit(solution)/shard_map/vmap()/ppermute | solution.py:114
  44.2 1.1 %multiply_add_fusion.5 = f32[1,128,1280]{1,2,0:T(8,128)} fusion(f32[1,128,1280]{1,2,0:T(8,128)S(1)} %add_select_fusion.3, f32[1,128,1280]{1,2,0:T(8,128)S(1)} %collective-permute-done.6, f32[1280]{0:T(1024)S(1)} %broadcast_in_dim.218), kind=kLoop, calls=%fused_computation.52 | loop fusion | flops 327680 | bytes 1971200 | tf_op jit(solution)/shard_map/vmap()/add | solution.py:227
  45.4 5.7 %collective-permute-start.7 = (f32[1,128,1280]{1,2,0:T(8,128)}, f32[1,128,1280]{1,2,0:T(8,128)}, u32[]{:S(2)}, u32[]{:S(2)}) collective-permute-start(f32[1,128,1280]{1,2,0:T(8,128)} %multiply_add_fusion.5), channel_id=1, source_target_pairs={{2,10},{6,14},{1,9},{5,13},{18,26},{22,30},{17,25},{21,29}} | collective-permute-start | bytes 1966088 | tf_op jit(solution)/shard_map/vmap()/ppermute | solution.py:114
  52.1 1.3 %collective-permute-start.11 = (f32[1,128,1280]{1,2,0:T(8,128)}, f32[1,128,1280]{1,2,0:T(8,128)}, u32[]{:S(2)}, u32[]{:S(2)}) collective-permute-start(f32[1,128,1280]{1,2,0:T(8,128)} %multiply_add_fusion.2), channel_id=1, source_target_pairs={{13,5},{9,1},{14,6},{10,2},{29,21},{25,17},{30,22},{26,18}} | collective-permute-start | bytes 1966088 | tf_op jit(solution)/shard_map/vmap()/ppermute | solution.py:114
  53.5 1.1 %copy.48 = bf16[1,128,2560]{1,2,0:T(8,128)(2,1)} copy(bf16[1,128,2560]{2,1,0:T(8,128)(2,1)S(1)} %copy-done.1) | data formatting | bytes 1310720 | tf_op jit(solution)/shard_map/optimization_barrier | solution.py:314
  54.7 1.3 %copy.51 = f32[1,128,2560]{1,2,0:T(8,128)} copy(bf16[1,128,2560]{2,1,0:T(8,128)(2,1)S(1)} %copy-done.1) | data formatting | bytes 1966080 | tf_op jit(solution)/shard_map/vmap()/convert_element_type | solution.py:53
  56.7 1.4 %collective-permute-done.7 = f32[1,128,1280]{1,2,0:T(8,128)} collective-permute-done((f32[1,128,1280]{1,2,0:T(8,128)}, f32[1,128,1280]{1,2,0:T(8,128)}, u32[]{:S(2)}, u32[]{:S(2)}) %collective-permute-start.7) | collective-permute-done | bytes 655392 | tf_op jit(solution)/shard_map/vmap()/ppermute | solution.py:114
  58.0 2.4 %add_select_fusion.2 = f32[1,128,1280]{1,2,0:T(8,128)} fusion(f32[1,128,1280]{1,2,0:T(8,128)S(1)} %copy-done.5, f32[1280]{0:T(1024)S(1)} %broadcast_in_dim.212, pred[]{:T(512)S(6)} %eq.27, f32[1,128,1280]{1,2,0:T(8,128)S(1)} %collective-permute-done.6, f32[1,128,1280]{1,2,0:T(8,128)} %collective-permute-done.7, f32[1280]{0:T(1024)S(1)} %broadcast_in_dim.215), kind=kLoop, calls=%fused_computation.50 | loop fusion | flops 819200 | bytes 2631681 | tf_op jit(solution)/shard_map/vmap(jit(_where))/select_n | solution.py:159
  60.5 1.5 %collective-permute-start.8 = (f32[1,128,1280]{1,2,0:T(8,128)}, f32[1,128,1280]{1,2,0:T(8,128)S(1)}, u32[]{:S(2)}, u32[]{:S(2)}) collective-permute-start(f32[1,128,1280]{1,2,0:T(8,128)} %add_select_fusion.2), channel_id=1, source_target_pairs={{6,4},{10,8},{14,12},{1,3},{5,7},{9,11},{13,15},{22,20},{26,24},{3... | collective-permute-start | bytes 1966088 | tf_op jit(solution)/shard_map/vmap()/ppermute | solution.py:114
  61.9 9.8 %collective-permute-done.11 = f32[1,128,1280]{1,2,0:T(8,128)} collective-permute-done((f32[1,128,1280]{1,2,0:T(8,128)}, f32[1,128,1280]{1,2,0:T(8,128)}, u32[]{:S(2)}, u32[]{:S(2)}) %collective-permute-start.11) | collective-permute-done | bytes 655392 | tf_op jit(solution)/shard_map/vmap()/ppermute | solution.py:114
  71.7 2.4 %add_select_fusion = f32[1,128,1280]{1,2,0:T(8,128)} fusion(f32[1,128,1280]{1,2,0:T(8,128)S(1)} %copy-done.4, f32[1280]{0:T(1024)S(1)} %broadcast_in_dim.230, pred[]{:T(512)S(6)} %eq.30, f32[1,128,1280]{1,2,0:T(8,128)S(1)} %collective-permute-done.10, f32[1,128,1280]{1,2,0:T(8,128)} %collective-permute-done.11, f32[1280]{0:T(1024)S(1)} %broadcast_in_dim.233), kind=kLoop, calls=%fused_computation.43 | loop fusion | flops 819200 | bytes 2631681 | tf_op jit(solution)/shard_map/vmap(jit(_where))/select_n | solution.py:159
  74.1 2.1 %collective-permute-start.12 = (f32[1,128,1280]{1,2,0:T(8,128)}, f32[1,128,1280]{1,2,0:T(8,128)}, u32[]{:S(2)}, u32[]{:S(2)}) collective-permute-start(f32[1,128,1280]{1,2,0:T(8,128)} %add_select_fusion), channel_id=1, source_target_pairs={{9,11},{5,7},{1,3},{14,12},{10,8},{6,4},{2,0},{25,27},{21,23},{17,... | collective-permute-start | bytes 1966088 | tf_op jit(solution)/shard_map/vmap()/ppermute | solution.py:114
  76.2 2.2 %fusion = f32[1,128,40,64]{1,3,2,0:T(8,128)} fusion(bf16[128,40,64]{0,2,1:T(8,128)(2,1)S(1)} %bitcast.227, f32[1,128,40,64]{1,3,2,0:T(8,128)S(1)} %bitcast.226, f32[40,128]{1,0:T(8,128)S(1)} %copy-done.22, f32[128,128]{1,0:T(8,128)S(1)} %fusion.46, pred[128,128]{1,0:T(8,128)(4,1)S(1)} %copy-done.23, f32[40]{0:T(128)S(1)} %copy-done.24), kind=kOutput, calls=%fused_computation.13 | convolution fusion | flops 87818240 | bytes 3379360 | tf_op jit(solution)/shard_map/vmap(hij,ihp->jhp)/dot_general | solution.py:51
  78.4 1.1 %copy.52 = bf16[1,128,2560]{1,2,0:T(8,128)(2,1)} copy(bf16[1,128,2560]{2,1,0:T(8,128)(2,1)S(1)} %copy-done.11) | data formatting | bytes 1310720 | tf_op jit(solution)/shard_map/optimization_barrier | solution.py:314
  80.4 2.2 %fusion.18 = (f32[1,128,1280]{1,2,0:T(8,128)S(1)}, f32[1,128,1280]{1,2,0:T(8,128)S(1)}) fusion(f32[1,128,1280]{1,2,0:T(8,128)S(1)} %copy-done.2, f32[1280]{0:T(1024)S(1)} %broadcast_in_dim.227, pred[]{:T(512)S(6)} %eq.27, f32[1,128,1280]{1,2,0:T(8,128)} %copy-done.16, f32[1,128,1280]{1,2,0:T(8,128)} %copy-done.10, f32[1280]{0:T(1024)S(1)} %copy-done.21, ...), kind=kLoop, calls=%fused_computation.48 | loop fusion | flops 1638400 | bytes 4602882 | tf_op jit(solution)/shard_map/vmap(jit(_where))/select_n | solution.py:259
  83.2 1.9 %fusion.17 = (f32[1,128,1280]{1,2,0:T(8,128)S(1)}, f32[1,128,1280]{1,2,0:T(8,128)S(1)}) fusion(f32[1,128,1280]{1,2,0:T(8,128)S(1)} %copy-done.3, f32[1280]{0:T(1024)S(1)} %broadcast_in_dim.245, pred[]{:T(512)S(6)} %eq.30, f32[1,128,1280]{1,2,0:T(8,128)} %collective-permute-done.12, f32[1,128,1280]{1,2,0:T(8,128)S(1)} %copy-done.9, ...), kind=kLoop, calls=%fused_computation.41 | loop fusion | flops 1638400 | bytes 4602882 | tf_op jit(solution)/shard_map/vmap(jit(_where))/select_n | solution.py:259
  85.2 7.4 %collective-permute-start.13 = (f32[1,128,2560]{1,2,0:T(8,128)S(1)}, f32[1,128,2560]{1,2,0:T(8,128)S(1)}, u32[]{:S(2)}, u32[]{:S(2)}) collective-permute-start(f32[1,128,2560]{1,2,0:T(8,128)S(1)} %pad_maximum_fusion.1), channel_id=1, source_target_pairs={{0,1},{1,0},{2,3},{3,2},{4,5},{5,4},{6,7},{7,6},{8,9},{9,8},{10,11... | collective-permute-start | bytes 3932168 | tf_op jit(solution)/shard_map/vmap()/ppermute | solution.py:261
  92.6 1.3 %convert_reduce_fusion = bf16[128,128]{1,0:T(8,128)(2,1)S(1)} fusion(f32[40,128]{1,0:T(8,128)S(1)} %copy-done.22, pred[128,128]{1,0:T(8,128)(4,1)S(1)} %copy-done.23, bf16[128,40,64]{0,2,1:T(8,128)(2,1)S(1)} %bitcast.228, bf16[128,40,64]{0,2,1:T(8,128)(2,1)S(1)} %bitcast.229), kind=kOutput, calls=%fused_computation.2 | convolution fusion | flops 88457216 | bytes 1380352 | tf_op jit(solution)/shard_map/vmap(ihp,jhp->hij)/dot_general | solution.py:45
  (178 shorter events, 23.1 us)
Async XLA Ops:
  0.6 5.1 %copy-start = (bf16[1,128,128]{2,1,0:T(8,128)(2,1)S(1)}, bf16[1,128,128]{2,1,0:T(8,128)(2,1)}, u32[]{:S(2)}) copy-start(bf16[1,128,128]{2,1,0:T(8,128)(2,1)} %param.8) | copy-start | bytes 98308
  0.6 2.6 %copy-start.1 = (bf16[1,128,2560]{2,1,0:T(8,128)(2,1)S(1)}, bf16[1,128,2560]{2,1,0:T(8,128)(2,1)}, u32[]{:S(2)}) copy-start(bf16[1,128,2560]{2,1,0:T(8,128)(2,1)} %param.7) | copy-start | bytes 1966084
  5.1 4.4 %collective-permute-start = (f32[1,17,40]{2,1,0:T(8,128)S(1)}, f32[1,17,40]{2,1,0:T(8,128)S(1)}, u32[]{:S(2)}, u32[]{:S(2)}) collective-permute-start(f32[1,17,40]{2,1,0:T(8,128)S(1)} %pad_maximum_fusion.2), channel_id=1, source_target_pairs={{0,1},{1,0},{2,3},{3,2},{4,5},{5,4},{6,7},{7,6},{8,9},{9,8},{10,11... | collective-permute-start | bytes 8168 | tf_op jit(solution)/shard_map/vmap()/ppermute | solution.py:69
  8.0 3.5 %collective-permute-start.1 = (f32[1,128,2560]{1,2,0:T(8,128)}, f32[1,128,2560]{1,2,0:T(8,128)}, u32[]{:S(2)}, u32[]{:S(2)}) collective-permute-start(f32[1,128,2560]{1,2,0:T(8,128)} %pad_maximum_fusion), channel_id=1, source_target_pairs={{0,1},{1,0},{2,3},{3,2},{4,5},{5,4},{6,7},{7,6},{8,9},{9,8},{10,11... | collective-permute-start | bytes 3932168 | tf_op jit(solution)/shard_map/vmap()/ppermute | solution.py:240
  14.6 5.6 %collective-permute-start.3 = (f32[1,17,40]{2,1,0:T(8,128)S(1)}, f32[1,17,40]{2,1,0:T(8,128)S(1)}, u32[]{:S(2)}, u32[]{:S(2)}) collective-permute-start(f32[1,17,40]{2,1,0:T(8,128)S(1)} %fusion.89), channel_id=1, source_target_pairs={{0,2},{1,3},{2,0},{3,1},{4,6},{5,7},{6,4},{7,5},{8,10},{9,11},{10,... | collective-permute-start | bytes 8168 | tf_op jit(solution)/shard_map/vmap()/ppermute | solution.py:69
  17.6 13.5 %collective-permute-start.2 = (f32[1,128,1280]{1,2,0:T(8,128)}, f32[1,128,1280]{1,2,0:T(8,128)S(1)}, u32[]{:S(2)}, u32[]{:S(2)}) collective-permute-start(f32[1,128,1280]{1,2,0:T(8,128)} %get-tuple-element.192), channel_id=1, source_target_pairs={{0,2},{4,6},{8,10},{12,14},{3,1},{7,5},{11,9},{15,13},{16,18},{20,... | collective-permute-start | bytes 1966088 | tf_op jit(solution)/shard_map/vmap()/ppermute | solution.py:114
  18.9 17.8 %collective-permute-start.9 = (f32[1,128,1280]{1,2,0:T(8,128)}, f32[1,128,1280]{1,2,0:T(8,128)S(1)}, u32[]{:S(2)}, u32[]{:S(2)}) collective-permute-start(f32[1,128,1280]{1,2,0:T(8,128)} %get-tuple-element.196), channel_id=1, source_target_pairs={{15,13},{11,9},{7,5},{3,1},{12,14},{8,10},{4,6},{0,2},{31,29},{27,... | collective-permute-start | bytes 1966088 | tf_op jit(solution)/shard_map/vmap()/ppermute | solution.py:114
  20.2 2.6 %collective-permute-start.4 = (f32[1,17,40]{2,1,0:T(8,128)S(1)}, f32[1,17,40]{2,1,0:T(8,128)S(1)}, u32[]{:S(2)}, u32[]{:S(2)}) collective-permute-start(f32[1,17,40]{2,1,0:T(8,128)S(1)} %add.200), channel_id=1, source_target_pairs={{0,4},{1,5},{2,6},{3,7},{4,0},{5,1},{6,2},{7,3},{8,12},{9,13},{10,... | collective-permute-start | bytes 8168 | tf_op jit(solution)/shard_map/vmap()/ppermute | solution.py:69
  21.8 15.8 %copy-start.4 = (f32[1,128,1280]{1,2,0:T(8,128)S(1)}, f32[1,128,1280]{1,2,0:T(8,128)}, u32[]{:S(2)}) copy-start(f32[1,128,1280]{1,2,0:T(8,128)} %get-tuple-element.196) | copy-start | bytes 1966084
  22.8 3.4 %collective-permute-start.5 = (f32[1,17,40]{2,1,0:T(8,128)S(1)}, f32[1,17,40]{2,1,0:T(8,128)S(1)}, u32[]{:S(2)}, u32[]{:S(2)}) collective-permute-start(f32[1,17,40]{2,1,0:T(8,128)S(1)} %add.202), channel_id=1, source_target_pairs={{0,8},{1,9},{2,10},{3,11},{4,12},{5,13},{6,14},{7,15},{8,0},{9,1},... | collective-permute-start | bytes 8168 | tf_op jit(solution)/shard_map/vmap()/ppermute | solution.py:69
  29.9 9.5 %collective-permute-start.14 = (f32[40]{0:T(128)S(1)}, f32[40]{0:T(128)S(1)}, u32[]{:S(2)}, u32[]{:S(2)}) collective-permute-start(f32[40]{0:T(128)S(1)} %slice_bitcast_fusion.5), channel_id=1, source_target_pairs={{0,16},{16,0},{1,17},{17,1},{2,18},{18,2},{3,19},{19,3},{4,20},{20... | collective-permute-start | bytes 488 | tf_op jit(solution)/shard_map/ppermute | solution.py:313
  33.5 10.7 %collective-permute-start.6 = (f32[1,128,1280]{1,2,0:T(8,128)S(1)}, f32[1,128,1280]{1,2,0:T(8,128)S(1)}, u32[]{:S(2)}, u32[]{:S(2)}) collective-permute-start(f32[1,128,1280]{1,2,0:T(8,128)S(1)} %add_select_fusion.3), channel_id=1, source_target_pairs={{2,6},{6,10},{10,14},{1,5},{5,9},{9,13},{18,22},{22,26},{26,30},{1... | collective-permute-start | bytes 1966088 | tf_op jit(solution)/shard_map/vmap()/ppermute | solution.py:114
  38.0 13.0 %collective-permute-start.10 = (f32[1,128,1280]{1,2,0:T(8,128)S(1)}, f32[1,128,1280]{1,2,0:T(8,128)S(1)}, u32[]{:S(2)}, u32[]{:S(2)}) collective-permute-start(f32[1,128,1280]{1,2,0:T(8,128)S(1)} %add_select_fusion.1), channel_id=1, source_target_pairs={{13,9},{9,5},{5,1},{14,10},{10,6},{6,2},{29,25},{25,21},{21,17},{3... | collective-permute-start | bytes 1966088 | tf_op jit(solution)/shard_map/vmap()/ppermute | solution.py:114
  45.4 12.7 %collective-permute-start.7 = (f32[1,128,1280]{1,2,0:T(8,128)}, f32[1,128,1280]{1,2,0:T(8,128)}, u32[]{:S(2)}, u32[]{:S(2)}) collective-permute-start(f32[1,128,1280]{1,2,0:T(8,128)} %multiply_add_fusion.5), channel_id=1, source_target_pairs={{2,10},{6,14},{1,9},{5,13},{18,26},{22,30},{17,25},{21,29}} | collective-permute-start | bytes 1966088 | tf_op jit(solution)/shard_map/vmap()/ppermute | solution.py:114
  52.1 19.6 %collective-permute-start.11 = (f32[1,128,1280]{1,2,0:T(8,128)}, f32[1,128,1280]{1,2,0:T(8,128)}, u32[]{:S(2)}, u32[]{:S(2)}) collective-permute-start(f32[1,128,1280]{1,2,0:T(8,128)} %multiply_add_fusion.2), channel_id=1, source_target_pairs={{13,5},{9,1},{14,6},{10,2},{29,21},{25,17},{30,22},{26,18}} | collective-permute-start | bytes 1966088 | tf_op jit(solution)/shard_map/vmap()/ppermute | solution.py:114
  54.7 3.4 %copy-start.5 = (f32[1,128,1280]{1,2,0:T(8,128)S(1)}, f32[1,128,1280]{1,2,0:T(8,128)}, u32[]{:S(2)}) copy-start(f32[1,128,1280]{1,2,0:T(8,128)} %get-tuple-element.192) | copy-start | bytes 1966084
  60.4 15.8 %copy-start.15 = (f32[1,128,2560]{1,2,0:T(8,128)S(1)}, f32[1,128,2560]{1,2,0:T(8,128)}, u32[]{:S(2)}) copy-start(f32[1,128,2560]{1,2,0:T(8,128)} %copy.51) | copy-start | bytes 3932164
  60.4 15.8 %copy-start.17 = (bf16[1,128,2560]{1,2,0:T(8,128)(2,1)S(1)}, bf16[1,128,2560]{1,2,0:T(8,128)(2,1)}, u32[]{:S(2)}) copy-start(bf16[1,128,2560]{1,2,0:T(8,128)(2,1)} %copy.48) | copy-start | bytes 1966084
  60.4 15.8 %copy-start.22 = (f32[40,128]{1,0:T(8,128)S(1)}, f32[40,128]{1,0:T(8,128)}, u32[]{:S(2)}) copy-start(f32[40,128]{1,0:T(8,128)} %copy.49) | copy-start | bytes 61444
  60.4 15.8 %copy-start.23 = (pred[128,128]{1,0:T(8,128)(4,1)S(1)}, pred[128,128]{1,0:T(8,128)(4,1)}, u32[]{:S(2)}) copy-start(pred[128,128]{1,0:T(8,128)(4,1)} %iota_compare_fusion) | copy-start | bytes 49156
  60.4 15.8 %copy-start.24 = (f32[40]{0:T(128)S(1)}, f32[40]{0:T(128)}, u32[]{:S(2)}) copy-start(f32[40]{0:T(128)} %param.11) | copy-start | bytes 484
  60.5 19.1 %collective-permute-start.8 = (f32[1,128,1280]{1,2,0:T(8,128)}, f32[1,128,1280]{1,2,0:T(8,128)S(1)}, u32[]{:S(2)}, u32[]{:S(2)}) collective-permute-start(f32[1,128,1280]{1,2,0:T(8,128)} %add_select_fusion.2), channel_id=1, source_target_pairs={{6,4},{10,8},{14,12},{1,3},{5,7},{9,11},{13,15},{22,20},{26,24},{3... | collective-permute-start | bytes 1966088 | tf_op jit(solution)/shard_map/vmap()/ppermute | solution.py:114
  74.1 9.1 %collective-permute-start.12 = (f32[1,128,1280]{1,2,0:T(8,128)}, f32[1,128,1280]{1,2,0:T(8,128)}, u32[]{:S(2)}, u32[]{:S(2)}) collective-permute-start(f32[1,128,1280]{1,2,0:T(8,128)} %add_select_fusion), channel_id=1, source_target_pairs={{9,11},{5,7},{1,3},{14,12},{10,8},{6,4},{2,0},{25,27},{21,23},{17,... | collective-permute-start | bytes 1966088 | tf_op jit(solution)/shard_map/vmap()/ppermute | solution.py:114
  76.2 2.2 %copy-start.11 = (bf16[1,128,2560]{2,1,0:T(8,128)(2,1)S(1)}, bf16[1,128,2560]{2,1,0:T(8,128)(2,1)}, u32[]{:S(2)}) copy-start(bf16[1,128,2560]{2,1,0:T(8,128)(2,1)} %param.6) | copy-start | bytes 1966084
  78.4 2.0 %copy-start.2 = (f32[1,128,1280]{1,2,0:T(8,128)S(1)}, f32[1,128,1280]{1,2,0:T(8,128)}, u32[]{:S(2)}) copy-start(f32[1,128,1280]{1,2,0:T(8,128)} %get-tuple-element.193) | copy-start | bytes 1966084
  78.4 2.0 %copy-start.21 = (f32[1280]{0:T(1024)S(1)}, f32[1280]{0:T(1024)}, u32[]{:S(2)}) copy-start(f32[1280]{0:T(1024)} %broadcast_in_dim.224) | copy-start | bytes 15364
  80.4 2.8 %copy-start.3 = (f32[1,128,1280]{1,2,0:T(8,128)S(1)}, f32[1,128,1280]{1,2,0:T(8,128)}, u32[]{:S(2)}) copy-start(f32[1,128,1280]{1,2,0:T(8,128)} %get-tuple-element.197) | copy-start | bytes 1966084
  80.4 2.8 %copy-start.9 = (f32[1,128,1280]{1,2,0:T(8,128)S(1)}, f32[1,128,1280]{1,2,0:T(8,128)}, u32[]{:S(2)}) copy-start(f32[1,128,1280]{1,2,0:T(8,128)} %copy-done.8) | copy-start | bytes 1966084
  85.1 7.6 %copy-start.18 = (bf16[1,128,2560]{1,2,0:T(8,128)(2,1)S(1)}, bf16[1,128,2560]{1,2,0:T(8,128)(2,1)}, u32[]{:S(2)}) copy-start(bf16[1,128,2560]{1,2,0:T(8,128)(2,1)} %copy.48) | copy-start | bytes 1966084
  85.1 7.6 %copy-start.19 = (bf16[1,128,2560]{1,2,0:T(8,128)(2,1)S(1)}, bf16[1,128,2560]{1,2,0:T(8,128)(2,1)}, u32[]{:S(2)}) copy-start(bf16[1,128,2560]{1,2,0:T(8,128)(2,1)} %copy.52) | copy-start | bytes 1966084
  85.2 10.7 %collective-permute-start.13 = (f32[1,128,2560]{1,2,0:T(8,128)S(1)}, f32[1,128,2560]{1,2,0:T(8,128)S(1)}, u32[]{:S(2)}, u32[]{:S(2)}) collective-permute-start(f32[1,128,2560]{1,2,0:T(8,128)S(1)} %pad_maximum_fusion.1), channel_id=1, source_target_pairs={{0,1},{1,0},{2,3},{3,2},{4,5},{5,4},{6,7},{7,6},{8,9},{9,8},{10,11... | collective-permute-start | bytes 3932168 | tf_op jit(solution)/shard_map/vmap()/ppermute | solution.py:261
  96.2 2.2 %copy-start.14 = (f32[1,128,40,64]{1,3,2,0:T(8,128)S(1)}, f32[1,128,40,64]{1,3,2,0:T(8,128)}, u32[]{:S(2)}) copy-start(f32[1,128,40,64]{1,3,2,0:T(8,128)} %fusion) | copy-start | bytes 3932164
  (8 other events, 8.4 us)

commit v20 on v19

--- a/solution.py
+++ b/solution.py
@@ -71,7 +71,7 @@
 
 def take_half(array, upper):
     half = array.shape[-1] // 2
-    return jnp.where(upper, array[..., half:], array[..., :half])
+    return lax.dynamic_slice_in_dim(array, upper.astype(jnp.int32) * half, half, axis=array.ndim - 1)
 
 
 def join_halves(mine, other, upper):

time: 101 us -> 108 us (1.069)
  the two profiles are of different devices: /device:TPU:1 before, /device:TPU:25 now
where the time goes in v20:
time: 108 us; the launch traced here: 107 us
  other arithmetic  32 us (30%)
  waiting for transfers between devices  27.8 us (26%)
  starting transfers between devices  24 us (22%)
  local copies, waits for them, and re-layouts  12.6 us (12%)
  matrix products  8.22 us (8%)
  between operations  2.78 us (3%)
    ppermute x8, waiting for transfers between devices, exchange(): lax.ppermute(p, 'ctx', pairs)  22.6 us
    ppermute x8, starting transfers between devices, exchange(): lax.ppermute(p, 'ctx', pairs)  14.8 us
    select_n x2, other arithmetic, carried_pair(): lifted_parts.append(jnp.where(way.upper, pair_prefix, lifted))  7.17 us
    ppermute x1, starting transfers between devices, carried_pair(): lax.ppermute(jnp.concatenate(lifted_parts, -1), 'ctx', [(i, i ^ 1) for i...  5.64 us
    ppermute x4, waiting for transfers between devices, extend_totals(): lax.ppermute(tables[-1], 'ctx', xor_pairs(count, bit))  5.16 us
    select_n x2, other arithmetic, up_combine(): return jnp.where(self.way.upper, kept_upper, kept_lower)  4.87 us
    add x2, other arithmetic, shift_scans(): through[k] = before_gain * group_gain(scan, group) * got[k] + through[k]  4.53 us
    unnamed x33, local copies, waits for them, and re-layouts  3.93 us
  transfers between devices with their start and end apart: 15, of which 9 were waited for; matrix products, arithmetic and copies ran while one was open for 28% of the time, Pallas kernels for 0%

profile of v20, /device:TPU:25, one launch (start us, length us, event | category | flops | bytes accessed | tf_op | source)
XLA Modules:
  0.0 107.4 jit_solution(13264834159805622120)
XLA Ops:
  2.5 1.4 %copy.45 = bf16[1,128,2560]{1,2,0:T(8,128)(2,1)S(1)} copy(bf16[1,128,2560]{2,1,0:T(8,128)(2,1)} %param.6) | data formatting | bytes 1310720 | tf_op args[0]
  12.8 3.7 %fusion.16 = (f32[1,128,1280]{1,2,0:T(8,128)S(1)}, f32[1,128,1280]{1,2,0:T(8,128)}) fusion(f32[1,128,2560]{1,2,0:T(8,128)} %collective-permute-done.1, f32[2560,128]{1,0:T(8,128)S(1)} %fusion.19, s32[]{:T(128)} %bitcast.25, f32[1280]{0:T(1024)S(1)} %broadcast_in_dim.241, pred[]{:T(512)S(6)} %eq.29, f32[2560,128]{1,0:T(8,128)S(1)} %fusion.17, s32[]{:T(128)} %bitcast.45, ...), kind=kLoop, calls=%fused_computation.39 | loop fusion | flops 1310720 | bytes 3942410 | tf_op jit(solution)/shard_map/vmap()/add | solution.py:250
  16.5 1.3 %collective-permute-start.3 = (f32[1,17,40]{2,1,0:T(8,128)S(1)}, f32[1,17,40]{2,1,0:T(8,128)S(1)}, u32[]{:S(2)}, u32[]{:S(2)}) collective-permute-start(f32[1,17,40]{2,1,0:T(8,128)S(1)} %fusion.76), channel_id=1, source_target_pairs={{0,2},{1,3},{2,0},{3,1},{4,6},{5,7},{6,4},{7,5},{8,10},{9,11},{10,... | collective-permute-start | bytes 8168 | tf_op jit(solution)/shard_map/vmap()/ppermute | solution.py:69
  18.5 1.3 %collective-permute-start.9 = (f32[1,128,1280]{1,2,0:T(8,128)}, f32[1,128,1280]{1,2,0:T(8,128)}, u32[]{:S(2)}, u32[]{:S(2)}) collective-permute-start(f32[1,128,1280]{1,2,0:T(8,128)} %get-tuple-element.436), channel_id=1, source_target_pairs={{15,13},{11,9},{7,5},{3,1},{12,14},{8,10},{4,6},{0,2},{31,29},{27,... | collective-permute-start | bytes 1966088 | tf_op jit(solution)/shard_map/vmap()/ppermute | solution.py:114
  19.8 1.3 %collective-permute-start.2 = (f32[1,128,1280]{1,2,0:T(8,128)S(1)}, f32[1,128,1280]{1,2,0:T(8,128)}, u32[]{:S(2)}, u32[]{:S(2)}) collective-permute-start(f32[1,128,1280]{1,2,0:T(8,128)S(1)} %get-tuple-element.435), channel_id=1, source_target_pairs={{0,2},{4,6},{8,10},{12,14},{3,1},{7,5},{11,9},{15,13},{16,18},{20,... | collective-permute-start | bytes 1966088 | tf_op jit(solution)/shard_map/vmap()/ppermute | solution.py:114
  21.5 2.2 %collective-permute-done.4 = f32[1,17,40]{2,1,0:T(8,128)S(1)} collective-permute-done((f32[1,17,40]{2,1,0:T(8,128)S(1)}, f32[1,17,40]{2,1,0:T(8,128)S(1)}, u32[]{:S(2)}, u32[]{:S(2)}) %collective-permute-start.4) | collective-permute-done | bytes 2752 | tf_op jit(solution)/shard_map/vmap()/ppermute | solution.py:69
  24.4 2.9 %collective-permute-done.5 = f32[1,17,40]{2,1,0:T(8,128)} collective-permute-done((f32[1,17,40]{2,1,0:T(8,128)S(1)}, f32[1,17,40]{2,1,0:T(8,128)}, u32[]{:S(2)}, u32[]{:S(2)}) %collective-permute-start.5) | collective-permute-done | bytes 2752 | tf_op jit(solution)/shard_map/vmap()/ppermute | solution.py:69
  27.3 1.3 %fusion.77 = (f32[]{:T(128)}, f32[1,17,40]{2,1,0:T(8,128)S(1)}) fusion(f32[1,17,40]{2,1,0:T(8,128)S(1)} %add.228, f32[1,17,40]{2,1,0:T(8,128)} %collective-permute-done.5), kind=kLoop, calls=%fused_computation.159 | loop fusion | flops 1359 | bytes 8164 | tf_op jit(solution)/shard_map/vmap()/reduce_min | solution.py:262
  28.7 1.5 %collective-permute-done.9 = f32[1,128,1280]{1,2,0:T(8,128)} collective-permute-done((f32[1,128,1280]{1,2,0:T(8,128)}, f32[1,128,1280]{1,2,0:T(8,128)}, u32[]{:S(2)}, u32[]{:S(2)}) %collective-permute-start.9) | collective-permute-done | bytes 655392 | tf_op jit(solution)/shard_map/vmap()/ppermute | solution.py:114
  30.1 2.5 %add_select_fusion.1 = f32[1,128,1280]{1,2,0:T(8,128)} fusion(f32[1,128,1280]{1,2,0:T(8,128)} %get-tuple-element.436, f32[1,128,1280]{1,2,0:T(8,128)} %collective-permute-done.9, f32[1280]{0:T(1024)S(1)} %broadcast_in_dim.286, f32[1280]{0:T(1024)S(1)} %broadcast_in_dim.277, pred[]{:T(512)S(6)} %eq.30), kind=kLoop, calls=%fused_computation.54 | loop fusion | flops 819200 | bytes 1976321 | tf_op jit(solution)/shard_map/vmap(jit(_where))/select_n | solution.py:152
  32.7 2.9 %collective-permute-start.10 = (f32[1,128,1280]{1,2,0:T(8,128)}, f32[1,128,1280]{1,2,0:T(8,128)}, u32[]{:S(2)}, u32[]{:S(2)}) collective-permute-start(f32[1,128,1280]{1,2,0:T(8,128)} %add_select_fusion.1), channel_id=1, source_target_pairs={{13,9},{9,5},{5,1},{14,10},{10,6},{6,2},{29,25},{25,21},{21,17},{3... | collective-permute-start | bytes 1966088 | tf_op jit(solution)/shard_map/vmap()/ppermute | solution.py:114
  35.7 1.5 %collective-permute-done.2 = f32[1,128,1280]{1,2,0:T(8,128)} collective-permute-done((f32[1,128,1280]{1,2,0:T(8,128)S(1)}, f32[1,128,1280]{1,2,0:T(8,128)}, u32[]{:S(2)}, u32[]{:S(2)}) %collective-permute-start.2) | collective-permute-done | bytes 655392 | tf_op jit(solution)/shard_map/vmap()/ppermute | solution.py:114
  37.2 2.3 %add_select_fusion.3 = f32[1,128,1280]{1,2,0:T(8,128)} fusion(f32[1,128,1280]{1,2,0:T(8,128)S(1)} %get-tuple-element.435, f32[1,128,1280]{1,2,0:T(8,128)} %collective-permute-done.2, f32[1280]{0:T(1024)S(1)} %broadcast_in_dim.268, f32[1280]{0:T(1024)S(1)} %broadcast_in_dim.259, pred[]{:T(512)S(6)} %eq.29), kind=kLoop, calls=%fused_computation.61 | loop fusion | flops 819200 | bytes 1976321 | tf_op jit(solution)/shard_map/vmap(jit(_where))/select_n | solution.py:152
  39.5 1.3 %collective-permute-start.6 = (f32[1,128,1280]{1,2,0:T(8,128)}, f32[1,128,1280]{1,2,0:T(8,128)S(1)}, u32[]{:S(2)}, u32[]{:S(2)}) collective-permute-start(f32[1,128,1280]{1,2,0:T(8,128)} %add_select_fusion.3), channel_id=1, source_target_pairs={{2,6},{6,10},{10,14},{1,5},{5,9},{9,13},{18,22},{22,26},{26,30},{1... | collective-permute-start | bytes 1966088 | tf_op jit(solution)/shard_map/vmap()/ppermute | solution.py:114
  41.0 1.5 %collective-permute-done.10 = f32[1,128,1280]{1,2,0:T(8,128)} collective-permute-done((f32[1,128,1280]{1,2,0:T(8,128)}, f32[1,128,1280]{1,2,0:T(8,128)}, u32[]{:S(2)}, u32[]{:S(2)}) %collective-permute-start.10) | collective-permute-done | bytes 655392 | tf_op jit(solution)/shard_map/vmap()/ppermute | solution.py:114
  42.6 2.4 %multiply_add_fusion.2 = f32[1,128,1280]{1,2,0:T(8,128)} fusion(f32[1,128,1280]{1,2,0:T(8,128)} %add_select_fusion.1, f32[1,128,1280]{1,2,0:T(8,128)} %collective-permute-done.10, f32[1280]{0:T(1024)S(1)} %broadcast_in_dim.283), kind=kLoop, calls=%fused_computation.53 | loop fusion | flops 327680 | bytes 1971200 | tf_op jit(solution)/shard_map/vmap()/add | solution.py:227
  44.9 4.5 %collective-permute-start.11 = (f32[1,128,1280]{1,2,0:T(8,128)}, f32[1,128,1280]{1,2,0:T(8,128)}, u32[]{:S(2)}, u32[]{:S(2)}) collective-permute-start(f32[1,128,1280]{1,2,0:T(8,128)} %multiply_add_fusion.2), channel_id=1, source_target_pairs={{13,5},{9,1},{14,6},{10,2},{29,21},{25,17},{30,22},{26,18}} | collective-permute-start | bytes 1966088 | tf_op jit(solution)/shard_map/vmap()/ppermute | solution.py:114
  51.0 2.2 %multiply_add_fusion.5 = f32[1,128,1280]{1,2,0:T(8,128)} fusion(f32[1,128,1280]{1,2,0:T(8,128)} %add_select_fusion.3, f32[1,128,1280]{1,2,0:T(8,128)S(1)} %collective-permute-done.6, f32[1280]{0:T(1024)S(1)} %broadcast_in_dim.265), kind=kLoop, calls=%fused_computation.60 | loop fusion | flops 327680 | bytes 1971200 | tf_op jit(solution)/shard_map/vmap()/add | solution.py:227
  53.2 1.3 %collective-permute-start.7 = (f32[1,128,1280]{1,2,0:T(8,128)}, f32[1,128,1280]{1,2,0:T(8,128)}, u32[]{:S(2)}, u32[]{:S(2)}) collective-permute-start(f32[1,128,1280]{1,2,0:T(8,128)} %multiply_add_fusion.5), channel_id=1, source_target_pairs={{2,10},{6,14},{1,9},{5,13},{18,26},{22,30},{17,25},{21,29}} | collective-permute-start | bytes 1966088 | tf_op jit(solution)/shard_map/vmap()/ppermute | solution.py:114
  55.6 1.3 %collective-permute-start.14 = (f32[40]{0:T(128)S(1)}, f32[40]{0:T(128)S(1)}, u32[]{:S(2)}, u32[]{:S(2)}) collective-permute-start(f32[40]{0:T(128)S(1)} %slice_bitcast_fusion.5), channel_id=1, source_target_pairs={{0,16},{16,0},{1,17},{17,1},{2,18},{18,2},{3,19},{19,3},{4,20},{20... | collective-permute-start | bytes 488 | tf_op jit(solution)/shard_map/ppermute | solution.py:313
  56.8 1.9 %add_select_fusion = f32[1,128,1280]{1,2,0:T(8,128)S(1)} fusion(f32[1,128,1280]{1,2,0:T(8,128)} %get-tuple-element.436, f32[1280]{0:T(1024)S(1)} %broadcast_in_dim.277, pred[]{:T(512)S(6)} %eq.30, f32[1,128,1280]{1,2,0:T(8,128)} %collective-permute-done.10, f32[1,128,1280]{1,2,0:T(8,128)} %collective-permute-done.11, f32[1280]{0:T(1024)S(1)} %broadcast_in_dim.280), kind=kLoop, calls=%fused_computation.51 | loop fusion | flops 819200 | bytes 2631681 | tf_op jit(solution)/shard_map/vmap(jit(_where))/select_n | solution.py:159
  59.4 13.2 %collective-permute-done.7 = f32[1,128,1280]{1,2,0:T(8,128)} collective-permute-done((f32[1,128,1280]{1,2,0:T(8,128)}, f32[1,128,1280]{1,2,0:T(8,128)}, u32[]{:S(2)}, u32[]{:S(2)}) %collective-permute-start.7) | collective-permute-done | bytes 655392 | tf_op jit(solution)/shard_map/vmap()/ppermute | solution.py:114
  72.6 1.5 %add_select_fusion.2 = f32[1,128,1280]{1,2,0:T(8,128)S(1)} fusion(f32[1,128,1280]{1,2,0:T(8,128)S(1)} %copy-done.2, f32[1280]{0:T(1024)S(1)} %broadcast_in_dim.259, pred[]{:T(512)S(6)} %eq.29, f32[1,128,1280]{1,2,0:T(8,128)S(1)} %collective-permute-done.6, f32[1,128,1280]{1,2,0:T(8,128)} %collective-permute-done.7, f32[1280]{0:T(1024)S(1)} %broadcast_in_dim.262), kind=kLoop, calls=%fused_computation.58 | loop fusion | flops 819200 | bytes 2631681 | tf_op jit(solution)/shard_map/vmap(jit(_where))/select_n | solution.py:159
  74.1 1.5 %collective-permute-start.8 = (f32[1,128,1280]{1,2,0:T(8,128)S(1)}, f32[1,128,1280]{1,2,0:T(8,128)S(1)}, u32[]{:S(2)}, u32[]{:S(2)}) collective-permute-start(f32[1,128,1280]{1,2,0:T(8,128)S(1)} %add_select_fusion.2), channel_id=1, source_target_pairs={{6,4},{10,8},{14,12},{1,3},{5,7},{9,11},{13,15},{22,20},{26,24},{3... | collective-permute-start | bytes 1966088 | tf_op jit(solution)/shard_map/vmap()/ppermute | solution.py:114
  76.2 2.8 %fusion.21 = (f32[1,128,1280]{1,2,0:T(8,128)S(1)}, f32[1,128,1280]{1,2,0:T(8,128)S(1)}) fusion(f32[1280]{0:T(1024)S(1)} %broadcast_in_dim.292, pred[]{:T(512)S(6)} %eq.30, f32[2560,128]{1,0:T(8,128)S(1)} %fusion.17, s32[]{:T(128)} %bitcast.45, f32[1,128,2560]{1,2,0:T(8,128)} %collective-permute-done.1, f32[1,128,1280]{1,2,0:T(8,128)S(1)} %collective-permute-done.12, ...), kind=kLoop, calls=%fused_computation.49 | loop fusion | flops 1802240 | bytes 5258246 | tf_op jit(solution)/shard_map/vmap(jit(_where))/select_n | solution.py:259
  79.0 3.9 %collective-permute-done.8 = f32[1,128,1280]{1,2,0:T(8,128)S(1)} collective-permute-done((f32[1,128,1280]{1,2,0:T(8,128)S(1)}, f32[1,128,1280]{1,2,0:T(8,128)S(1)}, u32[]{:S(2)}, u32[]{:S(2)}) %collective-permute-start.8) | collective-permute-done | bytes 655392 | tf_op jit(solution)/shard_map/vmap()/ppermute | solution.py:114
  82.9 4.3 %fusion.22 = (f32[1,128,1280]{1,2,0:T(8,128)S(1)}, f32[1,128,1280]{1,2,0:T(8,128)}, bf16[128,1280]{0,1:T(8,128)(2,1)}) fusion(f32[1280]{0:T(1024)S(1)} %broadcast_in_dim.274, pred[]{:T(512)S(6)} %eq.29, f32[2560,128]{1,0:T(8,128)S(1)} %fusion.19, s32[]{:T(128)} %bitcast.25, f32[1,128,2560]{1,2,0:T(8,128)} %collective-permute-done.1, ...), kind=kLoop, calls=%fused_computation.56 | loop fusion | flops 2621440 | bytes 7557131 | tf_op jit(solution)/shard_map/vmap(jit(_where))/select_n | solution.py:259
  88.4 5.6 %collective-permute-start.13 = (f32[1,128,2560]{1,2,0:T(8,128)}, f32[1,128,2560]{1,2,0:T(8,128)}, u32[]{:S(2)}, u32[]{:S(2)}) collective-permute-start(f32[1,128,2560]{1,2,0:T(8,128)} %pad_maximum_fusion.1), channel_id=1, source_target_pairs={{0,1},{1,0},{2,3},{3,2},{4,5},{5,4},{6,7},{7,6},{8,9},{9,8},{10,11... | collective-permute-start | bytes 3932168 | tf_op jit(solution)/shard_map/vmap()/ppermute | solution.py:261
  94.6 1.3 %copy.51 = f32[1,128,2560]{1,2,0:T(8,128)} copy(bf16[1,128,2560]{2,1,0:T(8,128)(2,1)S(1)} %copy-done.4) | data formatting | bytes 1966080 | tf_op jit(solution)/shard_map/vmap()/convert_element_type | solution.py:53
  96.3 1.3 %convert_reduce_fusion = bf16[128,128]{1,0:T(8,128)(2,1)S(1)} fusion(f32[40,128]{1,0:T(8,128)S(1)} %copy.49, pred[128,128]{1,0:T(8,128)(4,1)S(1)} %iota_compare_fusion, bf16[128,40,64]{0,2,1:T(8,128)(2,1)S(1)} %bitcast.262, bf16[128,40,64]{0,2,1:T(8,128)(2,1)S(1)} %bitcast.264), kind=kOutput, calls=%fused_computation | convolution fusion | flops 88457216 | bytes 1380352 | tf_op jit(solution)/shard_map/vmap(ihp,jhp->hij)/dot_general | solution.py:45
  100.0 2.2 %fusion.25 = f32[128,128]{1,0:T(8,128)S(1)} fusion(f32[1,128,1280]{1,2,0:T(8,128)S(1)} %copy-done.10, bf16[1,128,2560]{1,2,0:T(8,128)(2,1)S(1)} %copy-done.8, s32[]{:T(128)} %mul.277, f32[1280]{0:T(1024)S(1)} %broadcast_in_dim.274, pred[]{:T(512)S(6)} %eq.29, f32[1,128,2560]{1,2,0:T(8,128)} %collective-permute-done.1, f32[2560,128]{1,0:T(8,128)S(1)} %fusion.19, ...), kind=kOutput, calls=%fused_computation.64 | convolution fusion | flops 42762240 | bytes 2368513 | tf_op jit(solution)/shard_map/vmap(iq,nq->in)/dot_general | solution.py:274
  102.2 1.4 %multiply_convert_fusion.3 = bf16[1,128,2560]{1,2,0:T(8,128)(2,1)S(1)} fusion(f32[1,128,2560]{1,2,0:T(8,128)} %collective-permute-done.13, f32[]{:T(128)S(6)} %exp.133), kind=kLoop, calls=%fused_computation.20 | loop fusion | flops 655360 | bytes 1966084 | tf_op jit(solution)/shard_map/convert.2
  (150 shorter events, 23.1 us)
Async XLA Ops:
  0.6 6.1 %copy-start = (bf16[1,128,128]{2,1,0:T(8,128)(2,1)S(1)}, bf16[1,128,128]{2,1,0:T(8,128)(2,1)}, u32[]{:S(2)}) copy-start(bf16[1,128,128]{2,1,0:T(8,128)(2,1)} %param.8) | copy-start | bytes 98308
  0.6 3.3 %copy-start.3 = (bf16[1,128,2560]{2,1,0:T(8,128)(2,1)S(1)}, bf16[1,128,2560]{2,1,0:T(8,128)(2,1)}, u32[]{:S(2)}) copy-start(bf16[1,128,2560]{2,1,0:T(8,128)(2,1)} %param.7) | copy-start | bytes 1966084
  4.9 0.8 copy-start.13
  5.3 1.3 %copy-start.7 = (bf16[1,128,2560]{1,2,0:T(8,128)(2,1)}, bf16[1,128,2560]{1,2,0:T(8,128)(2,1)S(1)}, u32[]{:S(2)}) copy-start(bf16[1,128,2560]{1,2,0:T(8,128)(2,1)S(1)} %get-tuple-element.439) | copy-start | bytes 1966084
  5.4 1.3 %copy-start.5 = (bf16[1,128,2560]{1,2,0:T(8,128)(2,1)}, bf16[1,128,2560]{1,2,0:T(8,128)(2,1)S(1)}, u32[]{:S(2)}) copy-start(bf16[1,128,2560]{1,2,0:T(8,128)(2,1)S(1)} %get-tuple-element.437) | copy-start | bytes 1966084
  8.9 3.8 %collective-permute-start.1 = (f32[1,128,2560]{1,2,0:T(8,128)}, f32[1,128,2560]{1,2,0:T(8,128)}, u32[]{:S(2)}, u32[]{:S(2)}) collective-permute-start(f32[1,128,2560]{1,2,0:T(8,128)} %pad_maximum_fusion), channel_id=1, source_target_pairs={{0,1},{1,0},{2,3},{3,2},{4,5},{5,4},{6,7},{7,6},{8,9},{9,8},{10,11... | collective-permute-start | bytes 3932168 | tf_op jit(solution)/shard_map/vmap()/ppermute | solution.py:240
  9.9 2.4 %collective-permute-start = (f32[1,17,40]{2,1,0:T(8,128)S(1)}, f32[1,17,40]{2,1,0:T(8,128)S(1)}, u32[]{:S(2)}, u32[]{:S(2)}) collective-permute-start(f32[1,17,40]{2,1,0:T(8,128)S(1)} %pad_maximum_fusion.2), channel_id=1, source_target_pairs={{0,1},{1,0},{2,3},{3,2},{4,5},{5,4},{6,7},{7,6},{8,9},{9,8},{10,11... | collective-permute-start | bytes 8168 | tf_op jit(solution)/shard_map/vmap()/ppermute | solution.py:69
  16.5 20.7 %copy-start.1 = (f32[1,128,1280]{1,2,0:T(8,128)}, f32[1,128,1280]{1,2,0:T(8,128)S(1)}, u32[]{:S(2)}) copy-start(f32[1,128,1280]{1,2,0:T(8,128)S(1)} %get-tuple-element.435) | copy-start | bytes 1966084
  16.5 4.6 %collective-permute-start.3 = (f32[1,17,40]{2,1,0:T(8,128)S(1)}, f32[1,17,40]{2,1,0:T(8,128)S(1)}, u32[]{:S(2)}, u32[]{:S(2)}) collective-permute-start(f32[1,17,40]{2,1,0:T(8,128)S(1)} %fusion.76), channel_id=1, source_target_pairs={{0,2},{1,3},{2,0},{3,1},{4,6},{5,7},{6,4},{7,5},{8,10},{9,11},{10,... | collective-permute-start | bytes 8168 | tf_op jit(solution)/shard_map/vmap()/ppermute | solution.py:69
  18.5 11.6 %collective-permute-start.9 = (f32[1,128,1280]{1,2,0:T(8,128)}, f32[1,128,1280]{1,2,0:T(8,128)}, u32[]{:S(2)}, u32[]{:S(2)}) collective-permute-start(f32[1,128,1280]{1,2,0:T(8,128)} %get-tuple-element.436), channel_id=1, source_target_pairs={{15,13},{11,9},{7,5},{3,1},{12,14},{8,10},{4,6},{0,2},{31,29},{27,... | collective-permute-start | bytes 1966088 | tf_op jit(solution)/shard_map/vmap()/ppermute | solution.py:114
  19.8 17.4 %collective-permute-start.2 = (f32[1,128,1280]{1,2,0:T(8,128)S(1)}, f32[1,128,1280]{1,2,0:T(8,128)}, u32[]{:S(2)}, u32[]{:S(2)}) collective-permute-start(f32[1,128,1280]{1,2,0:T(8,128)S(1)} %get-tuple-element.435), channel_id=1, source_target_pairs={{0,2},{4,6},{8,10},{12,14},{3,1},{7,5},{11,9},{15,13},{16,18},{20,... | collective-permute-start | bytes 1966088 | tf_op jit(solution)/shard_map/vmap()/ppermute | solution.py:114
  21.1 2.6 %collective-permute-start.4 = (f32[1,17,40]{2,1,0:T(8,128)S(1)}, f32[1,17,40]{2,1,0:T(8,128)S(1)}, u32[]{:S(2)}, u32[]{:S(2)}) collective-permute-start(f32[1,17,40]{2,1,0:T(8,128)S(1)} %add.226), channel_id=1, source_target_pairs={{0,4},{1,5},{2,6},{3,7},{4,0},{5,1},{6,2},{7,3},{8,12},{9,13},{10,... | collective-permute-start | bytes 8168 | tf_op jit(solution)/shard_map/vmap()/ppermute | solution.py:69
  23.7 3.6 %collective-permute-start.5 = (f32[1,17,40]{2,1,0:T(8,128)S(1)}, f32[1,17,40]{2,1,0:T(8,128)}, u32[]{:S(2)}, u32[]{:S(2)}) collective-permute-start(f32[1,17,40]{2,1,0:T(8,128)S(1)} %add.228), channel_id=1, source_target_pairs={{0,8},{1,9},{2,10},{3,11},{4,12},{5,13},{6,14},{7,15},{8,0},{9,1},... | collective-permute-start | bytes 8168 | tf_op jit(solution)/shard_map/vmap()/ppermute | solution.py:69
  32.7 9.9 %collective-permute-start.10 = (f32[1,128,1280]{1,2,0:T(8,128)}, f32[1,128,1280]{1,2,0:T(8,128)}, u32[]{:S(2)}, u32[]{:S(2)}) collective-permute-start(f32[1,128,1280]{1,2,0:T(8,128)} %add_select_fusion.1), channel_id=1, source_target_pairs={{13,9},{9,5},{5,1},{14,10},{10,6},{6,2},{29,25},{25,21},{21,17},{3... | collective-permute-start | bytes 1966088 | tf_op jit(solution)/shard_map/vmap()/ppermute | solution.py:114
  39.5 11.5 %collective-permute-start.6 = (f32[1,128,1280]{1,2,0:T(8,128)}, f32[1,128,1280]{1,2,0:T(8,128)S(1)}, u32[]{:S(2)}, u32[]{:S(2)}) collective-permute-start(f32[1,128,1280]{1,2,0:T(8,128)} %add_select_fusion.3), channel_id=1, source_target_pairs={{2,6},{6,10},{10,14},{1,5},{5,9},{9,13},{18,22},{22,26},{26,30},{1... | collective-permute-start | bytes 1966088 | tf_op jit(solution)/shard_map/vmap()/ppermute | solution.py:114
  44.9 11.9 %collective-permute-start.11 = (f32[1,128,1280]{1,2,0:T(8,128)}, f32[1,128,1280]{1,2,0:T(8,128)}, u32[]{:S(2)}, u32[]{:S(2)}) collective-permute-start(f32[1,128,1280]{1,2,0:T(8,128)} %multiply_add_fusion.2), channel_id=1, source_target_pairs={{13,5},{9,1},{14,6},{10,2},{29,21},{25,17},{30,22},{26,18}} | collective-permute-start | bytes 1966088 | tf_op jit(solution)/shard_map/vmap()/ppermute | solution.py:114
  53.2 19.4 %collective-permute-start.7 = (f32[1,128,1280]{1,2,0:T(8,128)}, f32[1,128,1280]{1,2,0:T(8,128)}, u32[]{:S(2)}, u32[]{:S(2)}) collective-permute-start(f32[1,128,1280]{1,2,0:T(8,128)} %multiply_add_fusion.5), channel_id=1, source_target_pairs={{2,10},{6,14},{1,9},{5,13},{18,26},{22,30},{17,25},{21,29}} | collective-permute-start | bytes 1966088 | tf_op jit(solution)/shard_map/vmap()/ppermute | solution.py:114
  55.5 17.1 %copy-start.2 = (f32[1,128,1280]{1,2,0:T(8,128)S(1)}, f32[1,128,1280]{1,2,0:T(8,128)}, u32[]{:S(2)}) copy-start(f32[1,128,1280]{1,2,0:T(8,128)} %copy-done.1) | copy-start | bytes 1966084
  55.6 20.1 %collective-permute-start.14 = (f32[40]{0:T(128)S(1)}, f32[40]{0:T(128)S(1)}, u32[]{:S(2)}, u32[]{:S(2)}) collective-permute-start(f32[40]{0:T(128)S(1)} %slice_bitcast_fusion.5), channel_id=1, source_target_pairs={{0,16},{16,0},{1,17},{17,1},{2,18},{18,2},{3,19},{19,3},{4,20},{20... | collective-permute-start | bytes 488 | tf_op jit(solution)/shard_map/ppermute | solution.py:313
  58.7 17.5 %collective-permute-start.12 = (f32[1,128,1280]{1,2,0:T(8,128)S(1)}, f32[1,128,1280]{1,2,0:T(8,128)S(1)}, u32[]{:S(2)}, u32[]{:S(2)}) collective-permute-start(f32[1,128,1280]{1,2,0:T(8,128)S(1)} %add_select_fusion), channel_id=1, source_target_pairs={{9,11},{5,7},{1,3},{14,12},{10,8},{6,4},{2,0},{25,27},{21,23},{17,... | collective-permute-start | bytes 1966088 | tf_op jit(solution)/shard_map/vmap()/ppermute | solution.py:114
  74.1 8.8 %collective-permute-start.8 = (f32[1,128,1280]{1,2,0:T(8,128)S(1)}, f32[1,128,1280]{1,2,0:T(8,128)S(1)}, u32[]{:S(2)}, u32[]{:S(2)}) collective-permute-start(f32[1,128,1280]{1,2,0:T(8,128)S(1)} %add_select_fusion.2), channel_id=1, source_target_pairs={{6,4},{10,8},{14,12},{1,3},{5,7},{9,11},{13,15},{22,20},{26,24},{3... | collective-permute-start | bytes 1966088 | tf_op jit(solution)/shard_map/vmap()/ppermute | solution.py:114
  87.3 6.9 %copy-start.4 = (bf16[1,128,2560]{2,1,0:T(8,128)(2,1)S(1)}, bf16[1,128,2560]{2,1,0:T(8,128)(2,1)}, u32[]{:S(2)}) copy-start(bf16[1,128,2560]{2,1,0:T(8,128)(2,1)} %param.7) | copy-start | bytes 1966084
  88.4 13.8 %collective-permute-start.13 = (f32[1,128,2560]{1,2,0:T(8,128)}, f32[1,128,2560]{1,2,0:T(8,128)}, u32[]{:S(2)}, u32[]{:S(2)}) collective-permute-start(f32[1,128,2560]{1,2,0:T(8,128)} %pad_maximum_fusion.1), channel_id=1, source_target_pairs={{0,1},{1,0},{2,3},{3,2},{4,5},{5,4},{6,7},{7,6},{8,9},{9,8},{10,11... | collective-permute-start | bytes 3932168 | tf_op jit(solution)/shard_map/vmap()/ppermute | solution.py:261
  94.6 1.3 %copy-start.11 = (bf16[1,128,2560]{2,1,0:T(8,128)(2,1)S(1)}, bf16[1,128,2560]{2,1,0:T(8,128)(2,1)}, u32[]{:S(2)}) copy-start(bf16[1,128,2560]{2,1,0:T(8,128)(2,1)} %param.6) | copy-start | bytes 1966084
  96.3 1.3 %copy-start.12 = (f32[1,128,2560]{1,2,0:T(8,128)S(1)}, f32[1,128,2560]{1,2,0:T(8,128)}, u32[]{:S(2)}) copy-start(f32[1,128,2560]{1,2,0:T(8,128)} %copy.51) | copy-start | bytes 3932164
  96.3 1.3 %copy-start.14 = (f32[40]{0:T(128)S(1)}, f32[40]{0:T(128)}, u32[]{:S(2)}) copy-start(f32[40]{0:T(128)} %param.11) | copy-start | bytes 484
  97.6 1.0 copy-start.9
  97.6 1.3 %copy-start.6 = (bf16[1,128,2560]{1,2,0:T(8,128)(2,1)S(1)}, bf16[1,128,2560]{1,2,0:T(8,128)(2,1)}, u32[]{:S(2)}) copy-start(bf16[1,128,2560]{1,2,0:T(8,128)(2,1)} %copy-done.5) | copy-start | bytes 1966084
  98.6 1.1 %copy-start.8 = (bf16[1,128,2560]{1,2,0:T(8,128)(2,1)S(1)}, bf16[1,128,2560]{1,2,0:T(8,128)(2,1)}, u32[]{:S(2)}) copy-start(bf16[1,128,2560]{1,2,0:T(8,128)(2,1)} %copy-done.7) | copy-start | bytes 1966084
  98.6 1.3 %copy-start.10 = (f32[1,128,1280]{1,2,0:T(8,128)S(1)}, f32[1,128,1280]{1,2,0:T(8,128)}, u32[]{:S(2)}) copy-start(f32[1,128,1280]{1,2,0:T(8,128)} %get-tuple-element.431) | copy-start | bytes 1966084

commit v21 on v19

--- a/solution.py
+++ b/solution.py
@@ -211,8 +211,8 @@
     through = [scan.up_combine(0, t, g) for scan, t, g in zip(scans, pair_totals, got)]
     before = [jnp.zeros_like(t) for t in pair_totals]
 
-    def group_gain(scan, group):
-        return scan.way.gain(-1, 4 * group, 4)
+    def group_gain(scan, group, table=-1):
+        return scan.way.gain(table, 4 * group, 4)
 
     span = 1
     while span < group_count:
@@ -224,7 +224,8 @@
             for back in range(1, span):
                 before_gain = before_gain * group_gain(scan, group - back)
             if span < group_count // 2:
-                through[k] = before_gain * group_gain(scan, group) * got[k] + through[k]
+                own_table = min(2, len(scan.way.tables) - 1) if span == 1 else -1
+                through[k] = before_gain * group_gain(scan, group, own_table) * got[k] + through[k]
             before[k] = before_gain * got[k] + before[k]
         span *= 2
     sends = [scan.down_send(0, p, t) for scan, p, t in zip(scans, before, pair_totals)]

time: 101 us -> 101 us (level)
    unnamed x53 -> x51, local copies, waits for them, and re-layouts: 6.85 us -> 5.97 us
where the time goes in v21:
time: 101 us; the launch traced here: 99.4 us
  starting transfers between devices  34.1 us (34%)
  other arithmetic  24 us (24%)
  waiting for transfers between devices  18.1 us (18%)
  local copies, waits for them, and re-layouts  13.5 us (13%)
  matrix products  7.65 us (8%)
  between operations  1.92 us (2%)
    ppermute x8, starting transfers between devices, exchange(): lax.ppermute(p, 'ctx', pairs)  18.5 us
    ppermute x8, waiting for transfers between devices, exchange(): lax.ppermute(p, 'ctx', pairs)  16.2 us
    ppermute x1, starting transfers between devices, carried_pair(): lax.ppermute(jnp.concatenate(lifted_parts, -1), 'ctx', [(i, i ^ 1) for i...  7.44 us
    ppermute x4, starting transfers between devices, extend_totals(): lax.ppermute(tables[-1], 'ctx', xor_pairs(count, bit))  6.4 us
    unnamed x51, local copies, waits for them, and re-layouts  5.97 us
    select_n x2, other arithmetic, down_send(): jnp.where(self.way.upper, self.pair_gain(0, pair, 1) * prefix + pair_tota...  4.76 us
    select_n x2, other arithmetic, carried_pair(): lifted_parts.append(jnp.where(way.upper, pair_prefix, lifted))  4.03 us
    add x1, other arithmetic, carried_pair(): totals.append(way.gain(1, 2 * way.pair + 1, 1) * low_block + high_block)  3.28 us
  transfers between devices with their start and end apart: 15, of which 7 were waited for; matrix products, arithmetic and copies ran while one was open for 29% of the time, Pallas kernels for 0%

profile of v21, /device:TPU:1, one launch (start us, length us, event | category | flops | bytes accessed | tf_op | source)
XLA Modules:
  0.0 99.4 jit_solution(15706141186575753461)
XLA Ops:
  1.8 1.4 %copy.45 = bf16[1,128,2560]{1,2,0:T(8,128)(2,1)S(1)} copy(bf16[1,128,2560]{2,1,0:T(8,128)(2,1)} %param.6) | data formatting | bytes 1310720 | tf_op args[0]
  3.7 1.2 %fusion.1 = (f32[2560]{0:T(1024)S(1)}, bf16[1,128,2560]{1,2,0:T(8,128)(2,1)}, bf16[1,128,2560]{1,2,0:T(8,128)(2,1)S(1)}) fusion(bf16[1,128,2560]{1,2,0:T(8,128)(2,1)S(1)} %copy.46, bf16[1,128,2560]{1,2,0:T(8,128)(2,1)S(1)} %copy.45, f32[128,40]{0,1:T(8,128)S(1)} %get-tuple-element.201, f32[128,40]{0,1:T(8,128)S(1)} %get-tuple-element.202), kind=kLoop, calls=%fused_computation.14 | loop fusion | flops 2618880 | bytes 2672640 | tf_op jit(solution)/shard_map/vmap()/reduce_sum | solution.py:25
  6.8 1.2 %pad_maximum_fusion = f32[1,128,2560]{1,2,0:T(8,128)} fusion(f32[1,128,1280]{1,2,0:T(8,128)S(1)} %get-tuple-element.227, f32[1,128,1280]{1,2,0:T(8,128)S(1)} %get-tuple-element.228), kind=kLoop, calls=%fused_computation.19 | loop fusion | flops 327680 | bytes 2621440 | tf_op jit(solution)/shard_map/vmap()/concatenate | solution.py:240
  10.2 1.2 %collective-permute-done.1 = f32[1,128,2560]{1,2,0:T(8,128)} collective-permute-done((f32[1,128,2560]{1,2,0:T(8,128)}, f32[1,128,2560]{1,2,0:T(8,128)}, u32[]{:S(2)}, u32[]{:S(2)}) %collective-permute-start.1) | collective-permute-done | bytes 1310752 | tf_op jit(solution)/shard_map/vmap()/ppermute | solution.py:241
  11.4 3.3 %select_add_fusion.1 = (f32[1,128,1280]{1,2,0:T(8,128)}, f32[1,128,1280]{1,2,0:T(8,128)}, f32[1,128,1280]{1,2,0:T(8,128)}, f32[1,128,1280]{1,2,0:T(8,128)}) fusion(f32[1,128,2560]{1,2,0:T(8,128)} %collective-permute-done.1, f32[1280]{0:T(1024)S(1)} %broadcast_in_dim.199, pred[]{:T(512)S(6)} %eq.27, f32[1,128,2560]{1,2,0:T(8,128)S(1)} %convolution_bitcast_fusion.1, ...), kind=kLoop, calls=%fused_computation.55 | loop fusion | flops 1638400 | bytes 6563842 | tf_op jit(solution)/shard_map/vmap()/add | solution.py:251
  14.7 2.6 %collective-permute-start.3 = (f32[1,17,40]{2,1,0:T(8,128)S(1)}, f32[1,17,40]{2,1,0:T(8,128)S(1)}, u32[]{:S(2)}, u32[]{:S(2)}) collective-permute-start(f32[1,17,40]{2,1,0:T(8,128)S(1)} %fusion.89), channel_id=1, source_target_pairs={{0,2},{1,3},{2,0},{3,1},{4,6},{5,7},{6,4},{7,5},{8,10},{9,11},{10,... | collective-permute-start | bytes 8168 | tf_op jit(solution)/shard_map/vmap()/ppermute | solution.py:69
  17.7 1.3 %collective-permute-start.2 = (f32[1,128,1280]{1,2,0:T(8,128)}, f32[1,128,1280]{1,2,0:T(8,128)S(1)}, u32[]{:S(2)}, u32[]{:S(2)}) collective-permute-start(f32[1,128,1280]{1,2,0:T(8,128)} %get-tuple-element.192), channel_id=1, source_target_pairs={{0,2},{4,6},{8,10},{12,14},{3,1},{7,5},{11,9},{15,13},{16,18},{20,... | collective-permute-start | bytes 1966088 | tf_op jit(solution)/shard_map/vmap()/ppermute | solution.py:114
  19.0 1.3 %collective-permute-start.9 = (f32[1,128,1280]{1,2,0:T(8,128)}, f32[1,128,1280]{1,2,0:T(8,128)S(1)}, u32[]{:S(2)}, u32[]{:S(2)}) collective-permute-start(f32[1,128,1280]{1,2,0:T(8,128)} %get-tuple-element.196), channel_id=1, source_target_pairs={{15,13},{11,9},{7,5},{3,1},{12,14},{8,10},{4,6},{0,2},{31,29},{27,... | collective-permute-start | bytes 1966088 | tf_op jit(solution)/shard_map/vmap()/ppermute | solution.py:114
  20.3 1.4 %collective-permute-start.4 = (f32[1,17,40]{2,1,0:T(8,128)S(1)}, f32[1,17,40]{2,1,0:T(8,128)S(1)}, u32[]{:S(2)}, u32[]{:S(2)}) collective-permute-start(f32[1,17,40]{2,1,0:T(8,128)S(1)} %add.200), channel_id=1, source_target_pairs={{0,4},{1,5},{2,6},{3,7},{4,0},{5,1},{6,2},{7,3},{8,12},{9,13},{10,... | collective-permute-start | bytes 8168 | tf_op jit(solution)/shard_map/vmap()/ppermute | solution.py:69
  22.9 2.3 %collective-permute-start.5 = (f32[1,17,40]{2,1,0:T(8,128)S(1)}, f32[1,17,40]{2,1,0:T(8,128)S(1)}, u32[]{:S(2)}, u32[]{:S(2)}) collective-permute-start(f32[1,17,40]{2,1,0:T(8,128)S(1)} %add.202), channel_id=1, source_target_pairs={{0,8},{1,9},{2,10},{3,11},{4,12},{5,13},{6,14},{7,15},{8,0},{9,1},... | collective-permute-start | bytes 8168 | tf_op jit(solution)/shard_map/vmap()/ppermute | solution.py:69
  29.5 1.3 %collective-permute-start.14 = (f32[40]{0:T(128)S(1)}, f32[40]{0:T(128)S(1)}, u32[]{:S(2)}, u32[]{:S(2)}) collective-permute-start(f32[40]{0:T(128)S(1)} %slice_bitcast_fusion.5), channel_id=1, source_target_pairs={{0,16},{16,0},{1,17},{17,1},{2,18},{18,2},{3,19},{19,3},{4,20},{20... | collective-permute-start | bytes 488 | tf_op jit(solution)/shard_map/ppermute | solution.py:314
  31.6 1.5 %add_select_fusion.3 = f32[1,128,1280]{1,2,0:T(8,128)S(1)} fusion(f32[1,128,1280]{1,2,0:T(8,128)} %get-tuple-element.192, f32[1,128,1280]{1,2,0:T(8,128)S(1)} %collective-permute-done.2, f32[1280]{0:T(1024)S(1)} %broadcast_in_dim.221, f32[1280]{0:T(1024)S(1)} %broadcast_in_dim.212, pred[]{:T(512)S(6)} %eq.27), kind=kLoop, calls=%fused_computation.53 | loop fusion | flops 819200 | bytes 1976321 | tf_op jit(solution)/shard_map/vmap(jit(_where))/select_n | solution.py:152
  33.1 3.2 %collective-permute-start.6 = (f32[1,128,1280]{1,2,0:T(8,128)S(1)}, f32[1,128,1280]{1,2,0:T(8,128)S(1)}, u32[]{:S(2)}, u32[]{:S(2)}) collective-permute-start(f32[1,128,1280]{1,2,0:T(8,128)S(1)} %add_select_fusion.3), channel_id=1, source_target_pairs={{2,6},{6,10},{10,14},{1,5},{5,9},{9,13},{18,22},{22,26},{26,30},{1... | collective-permute-start | bytes 1966088 | tf_op jit(solution)/shard_map/vmap()/ppermute | solution.py:114
  37.6 1.3 %collective-permute-start.10 = (f32[1,128,1280]{1,2,0:T(8,128)S(1)}, f32[1,128,1280]{1,2,0:T(8,128)S(1)}, u32[]{:S(2)}, u32[]{:S(2)}) collective-permute-start(f32[1,128,1280]{1,2,0:T(8,128)S(1)} %add_select_fusion.1), channel_id=1, source_target_pairs={{13,9},{9,5},{5,1},{14,10},{10,6},{6,2},{29,25},{25,21},{21,17},{3... | collective-permute-start | bytes 1966088 | tf_op jit(solution)/shard_map/vmap()/ppermute | solution.py:114
  39.4 4.4 %collective-permute-done.6 = f32[1,128,1280]{1,2,0:T(8,128)S(1)} collective-permute-done((f32[1,128,1280]{1,2,0:T(8,128)S(1)}, f32[1,128,1280]{1,2,0:T(8,128)S(1)}, u32[]{:S(2)}, u32[]{:S(2)}) %collective-permute-start.6) | collective-permute-done | bytes 655392 | tf_op jit(solution)/shard_map/vmap()/ppermute | solution.py:114
  43.8 1.1 %multiply_add_fusion.5 = f32[1,128,1280]{1,2,0:T(8,128)} fusion(f32[1,128,1280]{1,2,0:T(8,128)S(1)} %add_select_fusion.3, f32[1,128,1280]{1,2,0:T(8,128)S(1)} %collective-permute-done.6, f32[1280]{0:T(1024)S(1)} %broadcast_in_dim.218), kind=kLoop, calls=%fused_computation.52 | loop fusion | flops 327680 | bytes 1971200 | tf_op jit(solution)/shard_map/vmap()/add | solution.py:228
  45.0 5.7 %collective-permute-start.7 = (f32[1,128,1280]{1,2,0:T(8,128)}, f32[1,128,1280]{1,2,0:T(8,128)}, u32[]{:S(2)}, u32[]{:S(2)}) collective-permute-start(f32[1,128,1280]{1,2,0:T(8,128)} %multiply_add_fusion.5), channel_id=1, source_target_pairs={{2,10},{6,14},{1,9},{5,13},{18,26},{22,30},{17,25},{21,29}} | collective-permute-start | bytes 1966088 | tf_op jit(solution)/shard_map/vmap()/ppermute | solution.py:114
  51.7 1.3 %collective-permute-start.11 = (f32[1,128,1280]{1,2,0:T(8,128)}, f32[1,128,1280]{1,2,0:T(8,128)}, u32[]{:S(2)}, u32[]{:S(2)}) collective-permute-start(f32[1,128,1280]{1,2,0:T(8,128)} %multiply_add_fusion.2), channel_id=1, source_target_pairs={{13,5},{9,1},{14,6},{10,2},{29,21},{25,17},{30,22},{26,18}} | collective-permute-start | bytes 1966088 | tf_op jit(solution)/shard_map/vmap()/ppermute | solution.py:114
  53.1 1.1 %copy.48 = bf16[1,128,2560]{1,2,0:T(8,128)(2,1)} copy(bf16[1,128,2560]{2,1,0:T(8,128)(2,1)S(1)} %copy-done.1) | data formatting | bytes 1310720 | tf_op jit(solution)/shard_map/optimization_barrier | solution.py:315
  54.2 1.3 %copy.51 = f32[1,128,2560]{1,2,0:T(8,128)} copy(bf16[1,128,2560]{2,1,0:T(8,128)(2,1)S(1)} %copy-done.1) | data formatting | bytes 1966080 | tf_op jit(solution)/shard_map/vmap()/convert_element_type | solution.py:53
  56.2 1.4 %collective-permute-done.7 = f32[1,128,1280]{1,2,0:T(8,128)} collective-permute-done((f32[1,128,1280]{1,2,0:T(8,128)}, f32[1,128,1280]{1,2,0:T(8,128)}, u32[]{:S(2)}, u32[]{:S(2)}) %collective-permute-start.7) | collective-permute-done | bytes 655392 | tf_op jit(solution)/shard_map/vmap()/ppermute | solution.py:114
  57.7 2.3 %add_select_fusion.2 = f32[1,128,1280]{1,2,0:T(8,128)} fusion(f32[1,128,1280]{1,2,0:T(8,128)S(1)} %copy-done.5, f32[1280]{0:T(1024)S(1)} %broadcast_in_dim.212, pred[]{:T(512)S(6)} %eq.27, f32[1,128,1280]{1,2,0:T(8,128)S(1)} %collective-permute-done.6, f32[1,128,1280]{1,2,0:T(8,128)} %collective-permute-done.7, f32[1280]{0:T(1024)S(1)} %broadcast_in_dim.215), kind=kLoop, calls=%fused_computation.50 | loop fusion | flops 819200 | bytes 2631681 | tf_op jit(solution)/shard_map/vmap(jit(_where))/select_n | solution.py:159
  60.0 2.3 %collective-permute-start.8 = (f32[1,128,1280]{1,2,0:T(8,128)}, f32[1,128,1280]{1,2,0:T(8,128)}, u32[]{:S(2)}, u32[]{:S(2)}) collective-permute-start(f32[1,128,1280]{1,2,0:T(8,128)} %add_select_fusion.2), channel_id=1, source_target_pairs={{6,4},{10,8},{14,12},{1,3},{5,7},{9,11},{13,15},{22,20},{26,24},{3... | collective-permute-start | bytes 1966088 | tf_op jit(solution)/shard_map/vmap()/ppermute | solution.py:114
  62.4 8.9 %collective-permute-done.11 = f32[1,128,1280]{1,2,0:T(8,128)} collective-permute-done((f32[1,128,1280]{1,2,0:T(8,128)}, f32[1,128,1280]{1,2,0:T(8,128)}, u32[]{:S(2)}, u32[]{:S(2)}) %collective-permute-start.11) | collective-permute-done | bytes 655392 | tf_op jit(solution)/shard_map/vmap()/ppermute | solution.py:114
  71.3 2.4 %add_select_fusion = f32[1,128,1280]{1,2,0:T(8,128)} fusion(f32[1,128,1280]{1,2,0:T(8,128)S(1)} %copy-done.4, f32[1280]{0:T(1024)S(1)} %broadcast_in_dim.230, pred[]{:T(512)S(6)} %eq.30, f32[1,128,1280]{1,2,0:T(8,128)S(1)} %collective-permute-done.10, f32[1,128,1280]{1,2,0:T(8,128)} %collective-permute-done.11, f32[1280]{0:T(1024)S(1)} %broadcast_in_dim.233), kind=kLoop, calls=%fused_computation.43 | loop fusion | flops 819200 | bytes 2631681 | tf_op jit(solution)/shard_map/vmap(jit(_where))/select_n | solution.py:159
  73.7 2.1 %collective-permute-start.12 = (f32[1,128,1280]{1,2,0:T(8,128)}, f32[1,128,1280]{1,2,0:T(8,128)}, u32[]{:S(2)}, u32[]{:S(2)}) collective-permute-start(f32[1,128,1280]{1,2,0:T(8,128)} %add_select_fusion), channel_id=1, source_target_pairs={{9,11},{5,7},{1,3},{14,12},{10,8},{6,4},{2,0},{25,27},{21,23},{17,... | collective-permute-start | bytes 1966088 | tf_op jit(solution)/shard_map/vmap()/ppermute | solution.py:114
  75.8 2.2 %fusion = f32[1,128,40,64]{1,3,2,0:T(8,128)} fusion(bf16[128,40,64]{0,2,1:T(8,128)(2,1)S(1)} %bitcast.229, f32[1,128,40,64]{1,3,2,0:T(8,128)S(1)} %bitcast.228, f32[40,128]{1,0:T(8,128)S(1)} %copy-done.21, f32[128,128]{1,0:T(8,128)S(1)} %fusion.46, pred[128,128]{1,0:T(8,128)(4,1)S(1)} %copy-done.22, f32[40]{0:T(128)S(1)} %copy-done.23), kind=kOutput, calls=%fused_computation.13 | convolution fusion | flops 87818240 | bytes 3379360 | tf_op jit(solution)/shard_map/vmap(hij,ihp->jhp)/dot_general | solution.py:51
  79.1 2.2 %fusion.18 = (f32[1,128,1280]{1,2,0:T(8,128)S(1)}, f32[1,128,1280]{1,2,0:T(8,128)S(1)}) fusion(f32[1,128,1280]{1,2,0:T(8,128)S(1)} %copy-done.2, f32[1280]{0:T(1024)S(1)} %broadcast_in_dim.227, pred[]{:T(512)S(6)} %eq.27, f32[1,128,1280]{1,2,0:T(8,128)} %collective-permute-done.8, f32[1,128,1280]{1,2,0:T(8,128)} %copy-done.10, f32[1280]{0:T(1024)S(1)} %copy-done.20, ...), kind=kLoop, calls=%fused_computation.48 | loop fusion | flops 1638400 | bytes 4602882 | tf_op jit(solution)/shard_map/vmap(jit(_where))/select_n | solution.py:260
  81.3 1.5 %collective-permute-done.12 = f32[1,128,1280]{1,2,0:T(8,128)} collective-permute-done((f32[1,128,1280]{1,2,0:T(8,128)}, f32[1,128,1280]{1,2,0:T(8,128)}, u32[]{:S(2)}, u32[]{:S(2)}) %collective-permute-start.12) | collective-permute-done | bytes 655392 | tf_op jit(solution)/shard_map/vmap()/ppermute | solution.py:114
  82.8 1.9 %fusion.17 = (f32[1,128,1280]{1,2,0:T(8,128)S(1)}, f32[1,128,1280]{1,2,0:T(8,128)S(1)}) fusion(f32[1,128,1280]{1,2,0:T(8,128)S(1)} %copy-done.3, f32[1280]{0:T(1024)S(1)} %broadcast_in_dim.245, pred[]{:T(512)S(6)} %eq.30, f32[1,128,1280]{1,2,0:T(8,128)} %collective-permute-done.12, f32[1,128,1280]{1,2,0:T(8,128)S(1)} %copy-done.9, ...), kind=kLoop, calls=%fused_computation.41 | loop fusion | flops 1638400 | bytes 4602882 | tf_op jit(solution)/shard_map/vmap(jit(_where))/select_n | solution.py:260
  84.8 7.4 %collective-permute-start.13 = (f32[1,128,2560]{1,2,0:T(8,128)S(1)}, f32[1,128,2560]{1,2,0:T(8,128)S(1)}, u32[]{:S(2)}, u32[]{:S(2)}) collective-permute-start(f32[1,128,2560]{1,2,0:T(8,128)S(1)} %pad_maximum_fusion.1), channel_id=1, source_target_pairs={{0,1},{1,0},{2,3},{3,2},{4,5},{5,4},{6,7},{7,6},{8,9},{9,8},{10,11... | collective-permute-start | bytes 3932168 | tf_op jit(solution)/shard_map/vmap()/ppermute | solution.py:262
  92.2 1.3 %convert_reduce_fusion = bf16[128,128]{1,0:T(8,128)(2,1)S(1)} fusion(f32[40,128]{1,0:T(8,128)S(1)} %copy-done.21, pred[128,128]{1,0:T(8,128)(4,1)S(1)} %copy-done.22, bf16[128,40,64]{0,2,1:T(8,128)(2,1)S(1)} %bitcast.230, bf16[128,40,64]{0,2,1:T(8,128)(2,1)S(1)} %bitcast.231), kind=kOutput, calls=%fused_computation.2 | convolution fusion | flops 88457216 | bytes 1380352 | tf_op jit(solution)/shard_map/vmap(ihp,jhp->hij)/dot_general | solution.py:45
  (182 shorter events, 22.2 us)
Async XLA Ops:
  0.6 5.1 %copy-start = (bf16[1,128,128]{2,1,0:T(8,128)(2,1)S(1)}, bf16[1,128,128]{2,1,0:T(8,128)(2,1)}, u32[]{:S(2)}) copy-start(bf16[1,128,128]{2,1,0:T(8,128)(2,1)} %param.8) | copy-start | bytes 98308
  0.6 2.6 %copy-start.1 = (bf16[1,128,2560]{2,1,0:T(8,128)(2,1)S(1)}, bf16[1,128,2560]{2,1,0:T(8,128)(2,1)}, u32[]{:S(2)}) copy-start(bf16[1,128,2560]{2,1,0:T(8,128)(2,1)} %param.7) | copy-start | bytes 1966084
  3.7 1.6 %copy-start.19 = (bf16[1,128,128]{2,1,0:T(8,128)(2,1)S(1)}, bf16[1,128,128]{2,1,0:T(8,128)(2,1)}, u32[]{:S(2)}) copy-start(bf16[1,128,128]{2,1,0:T(8,128)(2,1)} %param.9) | copy-start | bytes 98308
  5.1 4.4 %collective-permute-start = (f32[1,17,40]{2,1,0:T(8,128)S(1)}, f32[1,17,40]{2,1,0:T(8,128)S(1)}, u32[]{:S(2)}, u32[]{:S(2)}) collective-permute-start(f32[1,17,40]{2,1,0:T(8,128)S(1)} %pad_maximum_fusion.2), channel_id=1, source_target_pairs={{0,1},{1,0},{2,3},{3,2},{4,5},{5,4},{6,7},{7,6},{8,9},{9,8},{10,11... | collective-permute-start | bytes 8168 | tf_op jit(solution)/shard_map/vmap()/ppermute | solution.py:69
  8.0 3.5 %collective-permute-start.1 = (f32[1,128,2560]{1,2,0:T(8,128)}, f32[1,128,2560]{1,2,0:T(8,128)}, u32[]{:S(2)}, u32[]{:S(2)}) collective-permute-start(f32[1,128,2560]{1,2,0:T(8,128)} %pad_maximum_fusion), channel_id=1, source_target_pairs={{0,1},{1,0},{2,3},{3,2},{4,5},{5,4},{6,7},{7,6},{8,9},{9,8},{10,11... | collective-permute-start | bytes 3932168 | tf_op jit(solution)/shard_map/vmap()/ppermute | solution.py:241
  14.7 5.6 %collective-permute-start.3 = (f32[1,17,40]{2,1,0:T(8,128)S(1)}, f32[1,17,40]{2,1,0:T(8,128)S(1)}, u32[]{:S(2)}, u32[]{:S(2)}) collective-permute-start(f32[1,17,40]{2,1,0:T(8,128)S(1)} %fusion.89), channel_id=1, source_target_pairs={{0,2},{1,3},{2,0},{3,1},{4,6},{5,7},{6,4},{7,5},{8,10},{9,11},{10,... | collective-permute-start | bytes 8168 | tf_op jit(solution)/shard_map/vmap()/ppermute | solution.py:69
  17.7 13.1 %collective-permute-start.2 = (f32[1,128,1280]{1,2,0:T(8,128)}, f32[1,128,1280]{1,2,0:T(8,128)S(1)}, u32[]{:S(2)}, u32[]{:S(2)}) collective-permute-start(f32[1,128,1280]{1,2,0:T(8,128)} %get-tuple-element.192), channel_id=1, source_target_pairs={{0,2},{4,6},{8,10},{12,14},{3,1},{7,5},{11,9},{15,13},{16,18},{20,... | collective-permute-start | bytes 1966088 | tf_op jit(solution)/shard_map/vmap()/ppermute | solution.py:114
  19.0 17.4 %collective-permute-start.9 = (f32[1,128,1280]{1,2,0:T(8,128)}, f32[1,128,1280]{1,2,0:T(8,128)S(1)}, u32[]{:S(2)}, u32[]{:S(2)}) collective-permute-start(f32[1,128,1280]{1,2,0:T(8,128)} %get-tuple-element.196), channel_id=1, source_target_pairs={{15,13},{11,9},{7,5},{3,1},{12,14},{8,10},{4,6},{0,2},{31,29},{27,... | collective-permute-start | bytes 1966088 | tf_op jit(solution)/shard_map/vmap()/ppermute | solution.py:114
  20.3 2.6 %collective-permute-start.4 = (f32[1,17,40]{2,1,0:T(8,128)S(1)}, f32[1,17,40]{2,1,0:T(8,128)S(1)}, u32[]{:S(2)}, u32[]{:S(2)}) collective-permute-start(f32[1,17,40]{2,1,0:T(8,128)S(1)} %add.200), channel_id=1, source_target_pairs={{0,4},{1,5},{2,6},{3,7},{4,0},{5,1},{6,2},{7,3},{8,12},{9,13},{10,... | collective-permute-start | bytes 8168 | tf_op jit(solution)/shard_map/vmap()/ppermute | solution.py:69
  22.0 15.2 %copy-start.4 = (f32[1,128,1280]{1,2,0:T(8,128)S(1)}, f32[1,128,1280]{1,2,0:T(8,128)}, u32[]{:S(2)}) copy-start(f32[1,128,1280]{1,2,0:T(8,128)} %get-tuple-element.196) | copy-start | bytes 1966084
  22.9 3.4 %collective-permute-start.5 = (f32[1,17,40]{2,1,0:T(8,128)S(1)}, f32[1,17,40]{2,1,0:T(8,128)S(1)}, u32[]{:S(2)}, u32[]{:S(2)}) collective-permute-start(f32[1,17,40]{2,1,0:T(8,128)S(1)} %add.202), channel_id=1, source_target_pairs={{0,8},{1,9},{2,10},{3,11},{4,12},{5,13},{6,14},{7,15},{8,0},{9,1},... | collective-permute-start | bytes 8168 | tf_op jit(solution)/shard_map/vmap()/ppermute | solution.py:69
  29.5 9.5 %collective-permute-start.14 = (f32[40]{0:T(128)S(1)}, f32[40]{0:T(128)S(1)}, u32[]{:S(2)}, u32[]{:S(2)}) collective-permute-start(f32[40]{0:T(128)S(1)} %slice_bitcast_fusion.5), channel_id=1, source_target_pairs={{0,16},{16,0},{1,17},{17,1},{2,18},{18,2},{3,19},{19,3},{4,20},{20... | collective-permute-start | bytes 488 | tf_op jit(solution)/shard_map/ppermute | solution.py:314
  33.1 10.7 %collective-permute-start.6 = (f32[1,128,1280]{1,2,0:T(8,128)S(1)}, f32[1,128,1280]{1,2,0:T(8,128)S(1)}, u32[]{:S(2)}, u32[]{:S(2)}) collective-permute-start(f32[1,128,1280]{1,2,0:T(8,128)S(1)} %add_select_fusion.3), channel_id=1, source_target_pairs={{2,6},{6,10},{10,14},{1,5},{5,9},{9,13},{18,22},{22,26},{26,30},{1... | collective-permute-start | bytes 1966088 | tf_op jit(solution)/shard_map/vmap()/ppermute | solution.py:114
  37.6 13.0 %collective-permute-start.10 = (f32[1,128,1280]{1,2,0:T(8,128)S(1)}, f32[1,128,1280]{1,2,0:T(8,128)S(1)}, u32[]{:S(2)}, u32[]{:S(2)}) collective-permute-start(f32[1,128,1280]{1,2,0:T(8,128)S(1)} %add_select_fusion.1), channel_id=1, source_target_pairs={{13,9},{9,5},{5,1},{14,10},{10,6},{6,2},{29,25},{25,21},{21,17},{3... | collective-permute-start | bytes 1966088 | tf_op jit(solution)/shard_map/vmap()/ppermute | solution.py:114
  45.0 12.7 %collective-permute-start.7 = (f32[1,128,1280]{1,2,0:T(8,128)}, f32[1,128,1280]{1,2,0:T(8,128)}, u32[]{:S(2)}, u32[]{:S(2)}) collective-permute-start(f32[1,128,1280]{1,2,0:T(8,128)} %multiply_add_fusion.5), channel_id=1, source_target_pairs={{2,10},{6,14},{1,9},{5,13},{18,26},{22,30},{17,25},{21,29}} | collective-permute-start | bytes 1966088 | tf_op jit(solution)/shard_map/vmap()/ppermute | solution.py:114
  51.7 19.6 %collective-permute-start.11 = (f32[1,128,1280]{1,2,0:T(8,128)}, f32[1,128,1280]{1,2,0:T(8,128)}, u32[]{:S(2)}, u32[]{:S(2)}) collective-permute-start(f32[1,128,1280]{1,2,0:T(8,128)} %multiply_add_fusion.2), channel_id=1, source_target_pairs={{13,5},{9,1},{14,6},{10,2},{29,21},{25,17},{30,22},{26,18}} | collective-permute-start | bytes 1966088 | tf_op jit(solution)/shard_map/vmap()/ppermute | solution.py:114
  54.2 3.4 %copy-start.5 = (f32[1,128,1280]{1,2,0:T(8,128)S(1)}, f32[1,128,1280]{1,2,0:T(8,128)}, u32[]{:S(2)}) copy-start(f32[1,128,1280]{1,2,0:T(8,128)} %get-tuple-element.192) | copy-start | bytes 1966084
  60.0 15.8 %copy-start.15 = (f32[1,128,2560]{1,2,0:T(8,128)S(1)}, f32[1,128,2560]{1,2,0:T(8,128)}, u32[]{:S(2)}) copy-start(f32[1,128,2560]{1,2,0:T(8,128)} %copy.51) | copy-start | bytes 3932164
  60.0 15.8 %copy-start.16 = (bf16[1,128,2560]{1,2,0:T(8,128)(2,1)S(1)}, bf16[1,128,2560]{1,2,0:T(8,128)(2,1)}, u32[]{:S(2)}) copy-start(bf16[1,128,2560]{1,2,0:T(8,128)(2,1)} %copy.48) | copy-start | bytes 1966084
  60.0 15.8 %copy-start.21 = (f32[40,128]{1,0:T(8,128)S(1)}, f32[40,128]{1,0:T(8,128)}, u32[]{:S(2)}) copy-start(f32[40,128]{1,0:T(8,128)} %copy.49) | copy-start | bytes 61444
  60.0 15.8 %copy-start.22 = (pred[128,128]{1,0:T(8,128)(4,1)S(1)}, pred[128,128]{1,0:T(8,128)(4,1)}, u32[]{:S(2)}) copy-start(pred[128,128]{1,0:T(8,128)(4,1)} %iota_compare_fusion) | copy-start | bytes 49156
  60.0 15.8 %copy-start.23 = (f32[40]{0:T(128)S(1)}, f32[40]{0:T(128)}, u32[]{:S(2)}) copy-start(f32[40]{0:T(128)} %param.11) | copy-start | bytes 484
  60.0 19.1 %collective-permute-start.8 = (f32[1,128,1280]{1,2,0:T(8,128)}, f32[1,128,1280]{1,2,0:T(8,128)}, u32[]{:S(2)}, u32[]{:S(2)}) collective-permute-start(f32[1,128,1280]{1,2,0:T(8,128)} %add_select_fusion.2), channel_id=1, source_target_pairs={{6,4},{10,8},{14,12},{1,3},{5,7},{9,11},{13,15},{22,20},{26,24},{3... | collective-permute-start | bytes 1966088 | tf_op jit(solution)/shard_map/vmap()/ppermute | solution.py:114
  73.7 9.1 %collective-permute-start.12 = (f32[1,128,1280]{1,2,0:T(8,128)}, f32[1,128,1280]{1,2,0:T(8,128)}, u32[]{:S(2)}, u32[]{:S(2)}) collective-permute-start(f32[1,128,1280]{1,2,0:T(8,128)} %add_select_fusion), channel_id=1, source_target_pairs={{9,11},{5,7},{1,3},{14,12},{10,8},{6,4},{2,0},{25,27},{21,23},{17,... | collective-permute-start | bytes 1966088 | tf_op jit(solution)/shard_map/vmap()/ppermute | solution.py:114
  75.8 2.2 %copy-start.11 = (bf16[1,128,2560]{2,1,0:T(8,128)(2,1)S(1)}, bf16[1,128,2560]{2,1,0:T(8,128)(2,1)}, u32[]{:S(2)}) copy-start(bf16[1,128,2560]{2,1,0:T(8,128)(2,1)} %param.6) | copy-start | bytes 1966084
  79.1 3.7 %copy-start.3 = (f32[1,128,1280]{1,2,0:T(8,128)S(1)}, f32[1,128,1280]{1,2,0:T(8,128)}, u32[]{:S(2)}) copy-start(f32[1,128,1280]{1,2,0:T(8,128)} %get-tuple-element.197) | copy-start | bytes 1966084
  79.1 3.7 %copy-start.9 = (f32[1,128,1280]{1,2,0:T(8,128)S(1)}, f32[1,128,1280]{1,2,0:T(8,128)}, u32[]{:S(2)}) copy-start(f32[1,128,1280]{1,2,0:T(8,128)} %copy-done.8) | copy-start | bytes 1966084
  84.7 7.6 %copy-start.17 = (bf16[1,128,2560]{1,2,0:T(8,128)(2,1)S(1)}, bf16[1,128,2560]{1,2,0:T(8,128)(2,1)}, u32[]{:S(2)}) copy-start(bf16[1,128,2560]{1,2,0:T(8,128)(2,1)} %copy.48) | copy-start | bytes 1966084
  84.7 7.6 %copy-start.18 = (bf16[1,128,2560]{1,2,0:T(8,128)(2,1)S(1)}, bf16[1,128,2560]{1,2,0:T(8,128)(2,1)}, u32[]{:S(2)}) copy-start(bf16[1,128,2560]{1,2,0:T(8,128)(2,1)} %copy.52) | copy-start | bytes 1966084
  84.8 10.7 %collective-permute-start.13 = (f32[1,128,2560]{1,2,0:T(8,128)S(1)}, f32[1,128,2560]{1,2,0:T(8,128)S(1)}, u32[]{:S(2)}, u32[]{:S(2)}) collective-permute-start(f32[1,128,2560]{1,2,0:T(8,128)S(1)} %pad_maximum_fusion.1), channel_id=1, source_target_pairs={{0,1},{1,0},{2,3},{3,2},{4,5},{5,4},{6,7},{7,6},{8,9},{9,8},{10,11... | collective-permute-start | bytes 3932168 | tf_op jit(solution)/shard_map/vmap()/ppermute | solution.py:262
  93.8 1.1 %copy-start.7 = (bf16[1,128,2560]{1,2,0:T(8,128)(2,1)S(1)}, bf16[1,128,2560]{1,2,0:T(8,128)(2,1)}, u32[]{:S(2)}) copy-start(bf16[1,128,2560]{1,2,0:T(8,128)(2,1)} %copy-done.6) | copy-start | bytes 1966084
  95.8 2.2 %copy-start.14 = (f32[1,128,40,64]{1,3,2,0:T(8,128)S(1)}, f32[1,128,40,64]{1,3,2,0:T(8,128)}, u32[]{:S(2)}) copy-start(f32[1,128,40,64]{1,3,2,0:T(8,128)} %fusion) | copy-start | bytes 3932164
  (7 other events, 6.9 us)
